TPU v7x, 32 devices: a whole 2x2x4 slice. The times are simulated.
32 devices in a mesh: groups: 2 (over y), section: 4 (over z), seq: 4 (over x, core).
Axes of the slice: x: 2, y: 2, z: 4, core: 2. Of those that a mesh axis runs over, the one named last changes fastest.
Arguments:
- incoming_states: bfloat16 [1536, 3072], P('groups', 'seq'), parts along dimension 0, may hold values from -6 to 6
- transit_states: bfloat16 [4, 512, 3072], P('section', 'groups', 'seq'), parts along dimension 1, may hold values from -6 to 6
- patch_sizes_list: int32 [8], P('groups'), parts along dimension 0, may hold values from 1 to 256, 768 in all
- outdated_lookups: bfloat16 [4, 16, 1536, 128], P('section', 'seq', 'groups'), parts along dimension 2, may hold values from -6 to 6
- outdated_contents: bfloat16 [4, 16, 1536, 128], P('section', 'seq', 'groups'), parts along dimension 2, may hold values from -6 to 6
- attention_projection: bfloat16 [4, 3072, 6144], P('section', None, 'seq'), may hold values from -0.109375 to 0.109375
- exit_projection: bfloat16 [4, 2048, 3072], P('section', None, 'seq'), may hold values from -0.125 to 0.125
- shift_and_scale: float32 [4, 2, 3072], P('section'), may hold values from -3 to 3
- branch_gates: float32 [4, 3072], P('section', 'seq'), may hold values from -4 to 4
Outputs:
- section_out: bfloat16 [4, 4, 512, 3072], P(None, 'section', 'groups', 'seq'), parts along dimension 2
There are 2 independent parts, one for each index of `groups`. A program takes and returns all parts, laid end to end along the dimension named above; an argument that names none is the same for every part. Nothing has to cross between parts.
Inputs may be any that keep to these rules, and one draw needn't show every extreme that they name: `patch_sizes_list`: the 4 counts sum to 768; the largest equals 256.
All inputs are finite; a program needn't handle non-finite values.
Results may differ from a plain program's by a relative error of at most 0.005.
Values may be sent and summed in bfloat16 or wider, within the bound.
No kernel may reach another device: no remote copies, remote signals or barrier semaphores. Data moves between devices by JAX's collectives and lax.ppermute only.
A program may use at most 128 MiB of HBM per device.

v0:
```python
import jax
import jax.numpy as jnp
from jax import lax
from jax.sharding import PartitionSpec as P

epsilon = 1e-06


def passed_along(value, axis, steps):
    count = lax.axis_size(axis)
    leading, last = (max(0, -steps), min(count, count - steps))
    return lax.ppermute(value, axis, [(source, source + steps) for source in range(leading, last)])


def layer_norm(values):
    row_mean = jnp.mean(values, axis=-1, keepdims=True)
    centred = values - row_mean
    spread = jnp.mean(centred * centred, axis=-1, keepdims=True)
    return centred * lax.rsqrt(spread + epsilon)


def rms_norm(values):
    return values * lax.rsqrt(jnp.mean(values * values, axis=-1, keepdims=True) + epsilon)


def pick_entry(vector, position):
    return jnp.sum(jnp.where(jnp.arange(vector.shape[0]) == position, vector, 0))


def run_block(
    full_rows,
    own_rows,
    live_rows,
    patch_start,
    key_cache,
    value_cache,
    qkv_weights,
    shift_scale,
    gating_here,
    project,
):
    biggest_patch_span = full_rows.shape[0]
    heads_here = key_cache.shape[0]
    head_dim = key_cache.shape[2]
    seq_len = key_cache.shape[1] - biggest_patch_span
    shaped = (
        layer_norm(full_rows.astype(jnp.float32)) * (1.0 + shift_scale[1]) + shift_scale[0]
    ).astype(jnp.bfloat16)
    mixed = jnp.dot(shaped, qkv_weights, preferred_element_type=jnp.float32).reshape(
        biggest_patch_span, heads_here, 3, head_dim
    )
    queries = rms_norm(mixed[:, :, 0]).astype(jnp.bfloat16)
    fresh_keys = jnp.transpose(rms_norm(mixed[:, :, 1]).astype(jnp.bfloat16), (1, 0, 2))
    fresh_values = jnp.transpose(mixed[:, :, 2].astype(jnp.bfloat16), (1, 0, 2))
    mask = live_rows[None, :, None]
    window = lax.dynamic_slice_in_dim(key_cache, patch_start, biggest_patch_span, 1)
    key_cache = lax.dynamic_update_slice_in_dim(
        key_cache, jnp.where(mask, fresh_keys, window), patch_start, 1
    )
    window = lax.dynamic_slice_in_dim(value_cache, patch_start, biggest_patch_span, 1)
    value_cache = lax.dynamic_update_slice_in_dim(
        value_cache, jnp.where(mask, fresh_values, window), patch_start, 1
    )
    scores = jnp.einsum(
        "qhd,hkd->hqk", queries, key_cache[:, :seq_len], preferred_element_type=jnp.float32
    ) * head_dim ** (-0.5)
    expos = jnp.exp(scores)
    weights = (expos / jnp.sum(expos, axis=-1, keepdims=True)).astype(jnp.bfloat16)
    attended = jnp.einsum(
        "hqk,hkd->qhd", weights, value_cache[:, :seq_len], preferred_element_type=jnp.float32
    ).astype(jnp.bfloat16)
    head_rows = attended.reshape(biggest_patch_span, heads_here * head_dim)
    projected = project(head_rows)
    updated = own_rows.astype(jnp.float32) + gating_here * projected
    updated = jnp.where(live_rows[:, None], updated, 0.0).astype(jnp.bfloat16)
    return (updated, key_cache, value_cache)


def shards(
    incoming_states,
    transit_states,
    patch_sizes_list,
    outdated_lookups,
    outdated_contents,
    attention_projection,
    exit_projection,
    shift_and_scale,
    branch_gates,
):
    section_index = lax.axis_index("section")
    patches = patch_sizes_list.shape[0]
    biggest_patch_span = transit_states.shape[1]
    columns = incoming_states.shape[1]
    heads_here = outdated_lookups.shape[1]
    head_dim = outdated_lookups.shape[3]
    starts = jnp.cumsum(patch_sizes_list) - patch_sizes_list
    padding = jnp.zeros((heads_here, biggest_patch_span, head_dim), jnp.bfloat16)
    key_cache = jnp.concatenate([outdated_lookups[0], padding], axis=1)
    value_cache = jnp.concatenate([outdated_contents[0], padding], axis=1)
    qkv_weights = attention_projection[0]
    out_weights = exit_projection[0]
    shift_scale = shift_and_scale[0]
    gating_here = branch_gates[0]
    row_numbers = jnp.arange(biggest_patch_span)

    def gather_heads(head_rows):
        every_head = lax.all_gather(head_rows, "seq", axis=1, tiled=True)
        return jnp.dot(every_head, out_weights, preferred_element_type=jnp.float32)

    results = []
    entering_ext = jnp.concatenate(
        [incoming_states, jnp.zeros((biggest_patch_span, columns), jnp.bfloat16)], axis=0
    )
    earlier_result = transit_states[0]
    for turn_number in range(patches):
        patch_index = jnp.remainder(turn_number - section_index, patches)
        patch_count = pick_entry(patch_sizes_list, patch_index)
        patch_start = pick_entry(starts, patch_index)
        live_rows = row_numbers < patch_count
        entry_patch = lax.dynamic_slice_in_dim(
            entering_ext, starts[turn_number], biggest_patch_span, 0
        )
        own_rows = jnp.where(section_index == 0, entry_patch, earlier_result)
        own_rows = jnp.where(live_rows[:, None], own_rows, jnp.zeros_like(own_rows))
        full_rows = lax.all_gather(own_rows, "seq", axis=1, tiled=True)
        updated, key_cache, value_cache = run_block(
            full_rows,
            own_rows,
            live_rows,
            patch_start,
            key_cache,
            value_cache,
            qkv_weights,
            shift_scale,
            gating_here,
            gather_heads,
        )
        results.append(updated)
        if turn_number + 1 < patches:
            earlier_result = passed_along(updated, "section", 1)
    return jnp.stack(results)[:, None]


def solution(mesh):
    return jax.shard_map(
        shards,
        mesh=mesh,
        in_specs=(
            P("groups", "seq"),
            P("section", "groups", "seq"),
            P("groups"),
            P("section", "seq", "groups", None),
            P("section", "seq", "groups", None),
            P("section", None, "seq"),
            P("section", None, "seq"),
            P("section", None, None),
            P("section", "seq"),
        ),
        out_specs=P(None, "section", "groups", "seq"),
        check_vma=False,
    )
```

profile of v0, /device:TPU:0, one launch (start us, length us, event | category | flops | bytes accessed | tf_op | source)
XLA Modules:
  0.0 327.5 jit_solution(2446914256059857910)
XLA Ops:
  12.3 2.1 fusion.107
  15.7 2.3 copy.35
  18.1 2.3 copy.32
  20.4 2.3 concatenate.10
  22.6 2.3 concatenate.11
  24.9 12.7 %copy.33 = bf16[1,3072,1536]{1,2,0:T(8,128)(2,1)} copy(bf16[1,3072,1536]{2,1,0:T(8,128)(2,1)} %param.14) | data formatting | bytes 18874368 | tf_op args[5]
  40.2 2.0 fusion.20
  42.2 5.7 %fusion.37 = f32[256,4,3,128]{0,3,2,1:T(8,128)S(1)} fusion(bf16[4,3,128,3072]{3,2,1,0:T(8,128)(2,1)} %bitcast.213, bf16[256,3072]{1,0:T(8,128)(2,1)S(1)} %copy-done.3, f32[3072]{0:T(1024)S(1)} %bitcast.229, f32[3072]{0:T(1024)S(1)} %bitcast.225, f32[256]{0:T(256)S(1)} %add_rsqrt_fusion.11, f32[256]{0:T(256)S(1)} %broadcast_multiply_fusion.3), kind=kOutput, calls=%fused_computation.57 | convolution fusion | flops 2420637696 | bytes 12609536 | tf_op jit(solution)/shard_map/dot_general | solution.py:49
  49.1 3.5 %dynamic_update_slice.24 = bf16[4,1024,128]{1,2,0:T(8,128)(2,1)} dynamic-update-slice(bf16[4,1024,128]{1,2,0:T(8,128)(2,1)} %concatenate.10, bf16[4,256,128]{1,2,0:T(8,128)(2,1)} %get-tuple-element.28, s32[]{:T(128)} %constant.58.clone.1, s32[]{:T(128)S(6)} %select_n.158, s32[]{:T(128)} %constant.58.clone.1) | dynamic-update-slice | bytes 524292 | tf_op jit(solution)/shard_map/dynamic_update_slice | solution.py:61
  52.6 3.4 %dynamic_update_slice.25 = bf16[4,1024,128]{1,2,0:T(8,128)(2,1)} dynamic-update-slice(bf16[4,1024,128]{1,2,0:T(8,128)(2,1)} %concatenate.11, bf16[4,256,128]{1,2,0:T(8,128)(2,1)S(1)} %get-tuple-element.29, s32[]{:T(128)} %constant.58.clone.1, s32[]{:T(128)S(6)} %select_n.158, s32[]{:T(128)} %constant.58.clone.1) | dynamic-update-slice | bytes 524292 | tf_op jit(solution)/shard_map/dynamic_update_slice | solution.py:57
  56.0 2.2 fusion.32
  60.5 18.8 %all-gather.11.cloned.1.call-done = bf16[256,2048]{0,1:T(8,128)(2,1)} async-done(((bf16[256,512]{0,1:T(8,128)(2,1)}), bf16[256,2048]{0,1:T(8,128)(2,1)}) %all-gather.11.cloned.1.call-update) | async-done | bytes 1048592 | tf_op jit(solution)/shard_map/all_gather | solution.py:107
  79.3 3.0 fusion.86
  82.3 3.4 %collective-permute-start = (bf16[256,768]{1,0:T(8,128)(2,1)}, bf16[256,768]{1,0:T(8,128)(2,1)S(1)}, u32[]{:S(2)}, u32[]{:S(2)}) collective-permute-start(bf16[256,768]{1,0:T(8,128)(2,1)} %fusion.86), channel_id=1, source_target_pairs={{0,4},{4,8},{8,12},{1,5},{5,9},{9,13},{2,6},{6,10},{10,14},{3,7},{... | collective-permute-start | bytes 1179656 | tf_op jit(solution)/shard_map/ppermute | solution.py:12
  88.4 6.4 %collective-permute-done = bf16[256,768]{1,0:T(8,128)(2,1)S(1)} collective-permute-done((bf16[256,768]{1,0:T(8,128)(2,1)}, bf16[256,768]{1,0:T(8,128)(2,1)S(1)}, u32[]{:S(2)}, u32[]{:S(2)}) %collective-permute-start) | collective-permute-done | bytes 393248 | tf_op jit(solution)/shard_map/ppermute | solution.py:12
  98.8 18.7 %all-gather.13.cloned.1.call-done = bf16[256,3072]{1,0:T(8,128)(2,1)} async-done(((bf16[256,768]{1,0:T(8,128)(2,1)}), bf16[256,3072]{1,0:T(8,128)(2,1)}) %all-gather.13.cloned.1.call-update) | async-done | bytes 1572880 | tf_op jit(solution)/shard_map/all_gather | solution.py:125
  119.3 2.0 fusion.16
  121.3 5.6 %fusion.40 = f32[256,4,3,128]{0,3,2,1:T(8,128)S(1)} fusion(bf16[4,3,128,3072]{3,2,1,0:T(8,128)(2,1)} %bitcast.214, bf16[256,3072]{1,0:T(8,128)(2,1)S(1)} %copy-done.5, f32[256]{0:T(256)S(1)} %add_rsqrt_fusion.10, f32[256]{0:T(256)S(1)} %broadcast_multiply_fusion.2, f32[3072]{0:T(1024)S(1)} %bitcast.230, f32[3072]{0:T(1024)S(1)} %bitcast.226), kind=kOutput, calls=%fused_computation.59 | convolution fusion | flops 2420637696 | bytes 12609536 | tf_op jit(solution)/shard_map/dot_general | solution.py:49
  128.0 2.1 fusion.131
  130.1 3.9 %dynamic_update_slice.26 = bf16[4,1024,128]{1,2,0:T(8,128)(2,1)} dynamic-update-slice(bf16[4,1024,128]{1,2,0:T(8,128)(2,1)} %dynamic_update_slice.24, bf16[4,256,128]{1,2,0:T(8,128)(2,1)} %get-tuple-element.26, s32[]{:T(128)} %constant.58.clone.1, s32[]{:T(128)S(6)} %select_n.168, s32[]{:T(128)} %constant.58.clone.1) | dynamic-update-slice | bytes 524292 | tf_op jit(solution)/shard_map/dynamic_update_slice | solution.py:61
  134.1 3.9 %dynamic_update_slice.27 = bf16[4,1024,128]{1,2,0:T(8,128)(2,1)} dynamic-update-slice(bf16[4,1024,128]{1,2,0:T(8,128)(2,1)} %dynamic_update_slice.25, bf16[4,256,128]{1,2,0:T(8,128)(2,1)S(1)} %get-tuple-element.27, s32[]{:T(128)} %constant.58.clone.1, s32[]{:T(128)S(6)} %select_n.168, s32[]{:T(128)} %constant.58.clone.1) | dynamic-update-slice | bytes 524292 | tf_op jit(solution)/shard_map/dynamic_update_slice | solution.py:57
  138.0 2.2 fusion.33
  141.7 16.8 %all-gather.15.cloned.1.call-done = bf16[256,2048]{0,1:T(8,128)(2,1)} async-done(((bf16[256,512]{0,1:T(8,128)(2,1)}), bf16[256,2048]{0,1:T(8,128)(2,1)}) %all-gather.15.cloned.1.call-update) | async-done | bytes 1048592 | tf_op jit(solution)/shard_map/all_gather | solution.py:107
  158.5 3.0 select_convert_fusion.2
  161.5 3.4 %collective-permute-start.1 = (bf16[256,768]{1,0:T(8,128)(2,1)}, bf16[256,768]{1,0:T(8,128)(2,1)S(1)}, u32[]{:S(2)}, u32[]{:S(2)}) collective-permute-start(bf16[256,768]{1,0:T(8,128)(2,1)} %select_convert_fusion.2), channel_id=1, source_target_pairs={{0,4},{4,8},{8,12},{1,5},{5,9},{9,13},{2,6},{6,10},{10,14},{3,7},{... | collective-permute-start | bytes 1179656 | tf_op jit(solution)/shard_map/ppermute | solution.py:12
  167.7 6.3 %collective-permute-done.1 = bf16[256,768]{1,0:T(8,128)(2,1)S(1)} collective-permute-done((bf16[256,768]{1,0:T(8,128)(2,1)}, bf16[256,768]{1,0:T(8,128)(2,1)S(1)}, u32[]{:S(2)}, u32[]{:S(2)}) %collective-permute-start.1) | collective-permute-done | bytes 393248 | tf_op jit(solution)/shard_map/ppermute | solution.py:12
  174.0 2.0 fusion.111
  178.1 18.6 %all-gather.17.cloned.1.call-done = bf16[256,3072]{1,0:T(8,128)(2,1)} async-done(((bf16[256,768]{1,0:T(8,128)(2,1)}), bf16[256,3072]{1,0:T(8,128)(2,1)}) %all-gather.17.cloned.1.call-update) | async-done | bytes 1572880 | tf_op jit(solution)/shard_map/all_gather | solution.py:125
  198.5 2.0 fusion.12
  200.5 5.6 %fusion.43 = f32[256,4,3,128]{0,3,2,1:T(8,128)S(1)} fusion(bf16[4,3,128,3072]{3,2,1,0:T(8,128)(2,1)} %bitcast.215, bf16[256,3072]{1,0:T(8,128)(2,1)S(1)} %copy-done.6, f32[256]{0:T(256)S(1)} %add_rsqrt_fusion.9, f32[256]{0:T(256)S(1)} %broadcast_multiply_fusion.1, f32[3072]{0:T(1024)S(1)} %bitcast.231, f32[3072]{0:T(1024)S(1)} %bitcast.227), kind=kOutput, calls=%fused_computation.61 | convolution fusion | flops 2420637696 | bytes 12609536 | tf_op jit(solution)/shard_map/dot_general | solution.py:49
  207.2 2.1 fusion.133
  209.3 3.9 %dynamic_update_slice.28 = bf16[4,1024,128]{1,2,0:T(8,128)(2,1)} dynamic-update-slice(bf16[4,1024,128]{1,2,0:T(8,128)(2,1)} %dynamic_update_slice.26, bf16[4,256,128]{1,2,0:T(8,128)(2,1)} %get-tuple-element.24, s32[]{:T(128)} %constant.58.clone.1, s32[]{:T(128)S(6)} %select_n.178, s32[]{:T(128)} %constant.58.clone.1) | dynamic-update-slice | bytes 524292 | tf_op jit(solution)/shard_map/dynamic_update_slice | solution.py:61
  213.3 3.8 %dynamic_update_slice.29 = bf16[4,1024,128]{1,2,0:T(8,128)(2,1)} dynamic-update-slice(bf16[4,1024,128]{1,2,0:T(8,128)(2,1)} %dynamic_update_slice.27, bf16[4,256,128]{1,2,0:T(8,128)(2,1)S(1)} %get-tuple-element.25, s32[]{:T(128)} %constant.58.clone.1, s32[]{:T(128)S(6)} %select_n.178, s32[]{:T(128)} %constant.58.clone.1) | dynamic-update-slice | bytes 524292 | tf_op jit(solution)/shard_map/dynamic_update_slice | solution.py:57
  217.1 2.2 fusion.34
  220.9 16.7 %all-gather.19.cloned.1.call-done = bf16[256,2048]{0,1:T(8,128)(2,1)} async-done(((bf16[256,512]{0,1:T(8,128)(2,1)}), bf16[256,2048]{0,1:T(8,128)(2,1)}) %all-gather.19.cloned.1.call-update) | async-done | bytes 1048592 | tf_op jit(solution)/shard_map/all_gather | solution.py:107
  237.6 3.0 select_convert_fusion.1
  240.6 3.6 %collective-permute-start.2 = (bf16[256,768]{1,0:T(8,128)(2,1)}, bf16[256,768]{1,0:T(8,128)(2,1)S(1)}, u32[]{:S(2)}, u32[]{:S(2)}) collective-permute-start(bf16[256,768]{1,0:T(8,128)(2,1)} %select_convert_fusion.1), channel_id=1, source_target_pairs={{0,4},{4,8},{8,12},{1,5},{5,9},{9,13},{2,6},{6,10},{10,14},{3,7},{... | collective-permute-start | bytes 1179656 | tf_op jit(solution)/shard_map/ppermute | solution.py:12
  246.7 6.3 %collective-permute-done.2 = bf16[256,768]{1,0:T(8,128)(2,1)S(1)} collective-permute-done((bf16[256,768]{1,0:T(8,128)(2,1)}, bf16[256,768]{1,0:T(8,128)(2,1)S(1)}, u32[]{:S(2)}, u32[]{:S(2)}) %collective-permute-start.2) | collective-permute-done | bytes 393248 | tf_op jit(solution)/shard_map/ppermute | solution.py:12
  253.1 2.0 fusion.113
  257.0 18.7 %all-gather.21.cloned.1.call-done = bf16[256,3072]{1,0:T(8,128)(2,1)} async-done(((bf16[256,768]{1,0:T(8,128)(2,1)}), bf16[256,3072]{1,0:T(8,128)(2,1)}) %all-gather.21.cloned.1.call-update) | async-done | bytes 1572880 | tf_op jit(solution)/shard_map/all_gather | solution.py:125
  279.5 5.6 %fusion.46 = f32[256,4,3,128]{0,3,2,1:T(8,128)S(1)} fusion(bf16[4,3,128,3072]{3,2,1,0:T(8,128)(2,1)} %bitcast.216, bf16[256,3072]{1,0:T(8,128)(2,1)S(1)} %copy-done.4, f32[256]{0:T(256)S(1)} %add_rsqrt_fusion.8, f32[256]{0:T(256)S(1)} %broadcast_multiply_fusion, f32[3072]{0:T(1024)S(1)} %bitcast.232, f32[3072]{0:T(1024)S(1)} %bitcast.228), kind=kOutput, calls=%fused_computation.63 | convolution fusion | flops 2420637696 | bytes 12609536 | tf_op jit(solution)/shard_map/dot_general | solution.py:49
  286.2 2.1 fusion.135
  288.3 3.9 %dynamic_update_slice.30 = bf16[4,1024,128]{1,2,0:T(8,128)(2,1)} dynamic-update-slice(bf16[4,1024,128]{1,2,0:T(8,128)(2,1)} %dynamic_update_slice.28, bf16[4,256,128]{1,2,0:T(8,128)(2,1)} %get-tuple-element.18, s32[]{:T(128)} %constant.58.clone.1, s32[]{:T(128)S(6)} %select_n.188, s32[]{:T(128)} %constant.58.clone.1) | dynamic-update-slice | bytes 524292 | tf_op jit(solution)/shard_map/dynamic_update_slice | solution.py:61
  292.3 3.9 %dynamic_update_slice.31 = bf16[4,1024,128]{1,2,0:T(8,128)(2,1)} dynamic-update-slice(bf16[4,1024,128]{1,2,0:T(8,128)(2,1)} %dynamic_update_slice.29, bf16[4,256,128]{1,2,0:T(8,128)(2,1)S(1)} %get-tuple-element.19, s32[]{:T(128)} %constant.58.clone.1, s32[]{:T(128)S(6)} %select_n.188, s32[]{:T(128)} %constant.58.clone.1) | dynamic-update-slice | bytes 524292 | tf_op jit(solution)/shard_map/dynamic_update_slice | solution.py:57
  296.1 2.2 fusion.35
  299.8 16.0 %all-gather.23.cloned.1.call-done = bf16[256,2048]{0,1:T(8,128)(2,1)} async-done(((bf16[256,512]{0,1:T(8,128)(2,1)}), bf16[256,2048]{0,1:T(8,128)(2,1)}) %all-gather.23.cloned.1.call-update) | async-done | bytes 1048592 | tf_op jit(solution)/shard_map/all_gather | solution.py:107
  315.8 2.2 fusion.105
  318.1 2.6 maximum_bitcast_fusion
  (123 shorter events, 28.9 us)
Async XLA Ops:
  6.5 72.7 %copy-start = (bf16[1,2048,768]{2,1,0:T(8,128)(2,1)S(1)}, bf16[1,2048,768]{2,1,0:T(8,128)(2,1)}, u32[]{:S(2)}) copy-start(bf16[1,2048,768]{2,1,0:T(8,128)(2,1)} %param.15) | copy-start | bytes 9437188
  6.5 31.8 %all-gather.9.cloned.1.call-start = ((), (), s32[]{:S(2)}) async-start(), calls=%async_computation | async-start | bytes 1966080 | tf_op jit(solution)/shard_map/all_gather | solution.py:125
  9.7 38.4 %copy-start.31 = (pred[256]{0:T(512)(128)(4,1)}, pred[256]{0:T(512)(128)(4,1)S(1)}, u32[]{:S(2)}) copy-start(pred[256]{0:T(512)(128)(4,1)S(1)} %iota_compare_fusion.3) | copy-start | bytes 772
  14.4 64.9 %all-gather.11.cloned.1.call-start = ((), (), s32[]{:S(2)}) async-start(), calls=%async_computation.1 | async-start | bytes 1310720 | tf_op jit(solution)/shard_map/all_gather | solution.py:107
  24.9 13.4 %copy-start.19 = (f32[1,2,3072]{2,1,0:T(2,128)S(1)}, f32[1,2,3072]{2,1,0:T(2,128)}, u32[]{:S(2)}) copy-start(f32[1,2,3072]{2,1,0:T(2,128)} %param.16) | copy-start | bytes 73732
  38.3 9.6 %copy-start.20 = (f32[1,1,3072]{2,1,0:T(1,128)}, f32[1,1,3072]{2,1,0:T(1,128)S(1)}, u32[]{:S(2)}) copy-start(f32[1,1,3072]{2,1,0:T(1,128)S(1)} %get-tuple-element.17) | copy-start | bytes 36868
  38.3 3.8 %copy-start.3 = (bf16[256,3072]{1,0:T(8,128)(2,1)S(1)}, bf16[256,3072]{1,0:T(8,128)(2,1)}, u32[]{:S(2)}) copy-start(bf16[256,3072]{1,0:T(8,128)(2,1)} %all-gather.9.cloned.1.call-done) | copy-start | bytes 4718596
  42.2 5.9 %copy-start.1 = (bf16[1,4,768,128]{2,3,1,0:T(8,128)(2,1)S(1)}, bf16[1,4,768,128]{2,3,1,0:T(8,128)(2,1)}, u32[]{:S(2)}) copy-start(bf16[1,4,768,128]{2,3,1,0:T(8,128)(2,1)} %copy.35) | copy-start | bytes 2359300
  42.2 5.9 %copy-start.2 = (bf16[1,4,768,128]{2,3,1,0:T(8,128)(2,1)S(1)}, bf16[1,4,768,128]{2,3,1,0:T(8,128)(2,1)}, u32[]{:S(2)}) copy-start(bf16[1,4,768,128]{2,3,1,0:T(8,128)(2,1)} %copy.32) | copy-start | bytes 2359300
  47.9 1.2 copy-start.7
  56.0 2.2 copy-start.11
  58.2 21.1 %copy-start.15 = (bf16[256,768]{1,0:T(8,128)(2,1)S(1)}, bf16[256,768]{1,0:T(8,128)(2,1)}, u32[]{:S(2)}) copy-start(bf16[256,768]{1,0:T(8,128)(2,1)} %fusion.107) | copy-start | bytes 1179652
  59.7 57.8 %all-gather.13.cloned.1.call-start = ((), (), s32[]{:S(2)}) async-start(), calls=%async_computation.2 | async-start | bytes 1966080 | tf_op jit(solution)/shard_map/all_gather | solution.py:125
  82.3 12.5 %collective-permute-start = (bf16[256,768]{1,0:T(8,128)(2,1)}, bf16[256,768]{1,0:T(8,128)(2,1)S(1)}, u32[]{:S(2)}, u32[]{:S(2)}) collective-permute-start(bf16[256,768]{1,0:T(8,128)(2,1)} %fusion.86), channel_id=1, source_target_pairs={{0,4},{4,8},{8,12},{1,5},{5,9},{9,13},{2,6},{6,10},{10,14},{3,7},{... | collective-permute-start | bytes 1179656 | tf_op jit(solution)/shard_map/ppermute | solution.py:12
  88.4 6.4 %copy-start.27 = (pred[256]{0:T(512)(128)(4,1)}, pred[256]{0:T(512)(128)(4,1)S(1)}, u32[]{:S(2)}) copy-start(pred[256]{0:T(512)(128)(4,1)S(1)} %iota_compare_fusion.2) | copy-start | bytes 772
  96.7 24.5 %copy-start.21 = (f32[1,1,3072]{2,1,0:T(1,128)S(1)}, f32[1,1,3072]{2,1,0:T(1,128)}, u32[]{:S(2)}) copy-start(f32[1,1,3072]{2,1,0:T(1,128)} %copy-done.20) | copy-start | bytes 36868
  96.8 61.7 %all-gather.15.cloned.1.call-start = ((), (), s32[]{:S(2)}) async-start(), calls=%async_computation.3 | async-start | bytes 1310720 | tf_op jit(solution)/shard_map/all_gather | solution.py:107
  117.5 3.8 %copy-start.5 = (bf16[256,3072]{1,0:T(8,128)(2,1)S(1)}, bf16[256,3072]{1,0:T(8,128)(2,1)}, u32[]{:S(2)}) copy-start(bf16[256,3072]{1,0:T(8,128)(2,1)} %all-gather.13.cloned.1.call-done) | copy-start | bytes 4718596
  121.3 6.7 %copy-start.28 = (pred[256]{0:T(512)(128)(4,1)S(1)}, pred[256]{0:T(512)(128)(4,1)}, u32[]{:S(2)}) copy-start(pred[256]{0:T(512)(128)(4,1)} %copy-done.27) | copy-start | bytes 772
  126.9 1.1 copy-start.9
  138.0 2.2 copy-start.12
  140.1 18.4 %copy-start.17 = (bf16[256,768]{1,0:T(8,128)(2,1)S(1)}, bf16[256,768]{1,0:T(8,128)(2,1)}, u32[]{:S(2)}) copy-start(bf16[256,768]{1,0:T(8,128)(2,1)} %fusion.109) | copy-start | bytes 1179652
  141.7 55.0 %all-gather.17.cloned.1.call-start = ((), (), s32[]{:S(2)}) async-start(), calls=%async_computation.4 | async-start | bytes 1966080 | tf_op jit(solution)/shard_map/all_gather | solution.py:125
  161.5 12.5 %collective-permute-start.1 = (bf16[256,768]{1,0:T(8,128)(2,1)}, bf16[256,768]{1,0:T(8,128)(2,1)S(1)}, u32[]{:S(2)}, u32[]{:S(2)}) collective-permute-start(bf16[256,768]{1,0:T(8,128)(2,1)} %select_convert_fusion.2), channel_id=1, source_target_pairs={{0,4},{4,8},{8,12},{1,5},{5,9},{9,13},{2,6},{6,10},{10,14},{3,7},{... | collective-permute-start | bytes 1179656 | tf_op jit(solution)/shard_map/ppermute | solution.py:12
  167.6 6.3 %copy-start.29 = (pred[256]{0:T(512)(128)(4,1)}, pred[256]{0:T(512)(128)(4,1)S(1)}, u32[]{:S(2)}) copy-start(pred[256]{0:T(512)(128)(4,1)S(1)} %iota_compare_fusion.1) | copy-start | bytes 772
  175.9 24.5 %copy-start.22 = (f32[1,1,3072]{2,1,0:T(1,128)S(1)}, f32[1,1,3072]{2,1,0:T(1,128)}, u32[]{:S(2)}) copy-start(f32[1,1,3072]{2,1,0:T(1,128)} %copy-done.20) | copy-start | bytes 36868
  176.0 61.6 %all-gather.19.cloned.1.call-start = ((), (), s32[]{:S(2)}) async-start(), calls=%async_computation.5 | async-start | bytes 1310720 | tf_op jit(solution)/shard_map/all_gather | solution.py:107
  196.7 3.8 %copy-start.6 = (bf16[256,3072]{1,0:T(8,128)(2,1)S(1)}, bf16[256,3072]{1,0:T(8,128)(2,1)}, u32[]{:S(2)}) copy-start(bf16[256,3072]{1,0:T(8,128)(2,1)} %all-gather.17.cloned.1.call-done) | copy-start | bytes 4718596
  200.5 6.7 %copy-start.30 = (pred[256]{0:T(512)(128)(4,1)S(1)}, pred[256]{0:T(512)(128)(4,1)}, u32[]{:S(2)}) copy-start(pred[256]{0:T(512)(128)(4,1)} %copy-done.29) | copy-start | bytes 772
  206.1 1.1 copy-start.10
  217.1 2.2 copy-start.13
  219.3 18.3 %copy-start.18 = (bf16[256,768]{1,0:T(8,128)(2,1)S(1)}, bf16[256,768]{1,0:T(8,128)(2,1)}, u32[]{:S(2)}) copy-start(bf16[256,768]{1,0:T(8,128)(2,1)} %fusion.111) | copy-start | bytes 1179652
  220.8 54.9 %all-gather.21.cloned.1.call-start = ((), (), s32[]{:S(2)}) async-start(), calls=%async_computation.6 | async-start | bytes 1966080 | tf_op jit(solution)/shard_map/all_gather | solution.py:125
  240.6 12.5 %collective-permute-start.2 = (bf16[256,768]{1,0:T(8,128)(2,1)}, bf16[256,768]{1,0:T(8,128)(2,1)S(1)}, u32[]{:S(2)}, u32[]{:S(2)}) collective-permute-start(bf16[256,768]{1,0:T(8,128)(2,1)} %select_convert_fusion.1), channel_id=1, source_target_pairs={{0,4},{4,8},{8,12},{1,5},{5,9},{9,13},{2,6},{6,10},{10,14},{3,7},{... | collective-permute-start | bytes 1179656 | tf_op jit(solution)/shard_map/ppermute | solution.py:12
  246.7 6.4 %copy-start.24 = (pred[256]{0:T(512)(128)(4,1)}, pred[256]{0:T(512)(128)(4,1)S(1)}, u32[]{:S(2)}) copy-start(pred[256]{0:T(512)(128)(4,1)S(1)} %iota_compare_fusion) | copy-start | bytes 772
  255.0 24.5 %copy-start.23 = (f32[1,1,3072]{2,1,0:T(1,128)S(1)}, f32[1,1,3072]{2,1,0:T(1,128)}, u32[]{:S(2)}) copy-start(f32[1,1,3072]{2,1,0:T(1,128)} %copy-done.20) | copy-start | bytes 36868
  255.0 60.8 %all-gather.23.cloned.1.call-start = ((), (), s32[]{:S(2)}) async-start(), calls=%async_computation.7 | async-start | bytes 1310720 | tf_op jit(solution)/shard_map/all_gather | solution.py:107
  275.7 3.8 %copy-start.4 = (bf16[256,3072]{1,0:T(8,128)(2,1)S(1)}, bf16[256,3072]{1,0:T(8,128)(2,1)}, u32[]{:S(2)}) copy-start(bf16[256,3072]{1,0:T(8,128)(2,1)} %all-gather.21.cloned.1.call-done) | copy-start | bytes 4718596
  279.5 6.7 %copy-start.25 = (pred[256]{0:T(512)(128)(4,1)S(1)}, pred[256]{0:T(512)(128)(4,1)}, u32[]{:S(2)}) copy-start(pred[256]{0:T(512)(128)(4,1)} %copy-done.24) | copy-start | bytes 772
  285.1 1.1 copy-start.8
  296.1 2.2 copy-start.14
  298.3 17.5 %copy-start.16 = (bf16[256,768]{1,0:T(8,128)(2,1)S(1)}, bf16[256,768]{1,0:T(8,128)(2,1)}, u32[]{:S(2)}) copy-start(bf16[256,768]{1,0:T(8,128)(2,1)} %fusion.113) | copy-start | bytes 1179652
  298.3 17.5 %copy-start.26 = (pred[256]{0:T(512)(128)(4,1)S(1)}, pred[256]{0:T(512)(128)(4,1)}, u32[]{:S(2)}) copy-start(pred[256]{0:T(512)(128)(4,1)} %copy-done.24) | copy-start | bytes 772
Sparse Core Ops, SparseCore 0:
  14.5 22.3 all-gather.8
  59.8 19.3 all-gather.10
  96.9 20.5 all-gather.12
  141.8 16.6 all-gather.14
  176.1 20.5 all-gather.16
  220.9 16.5 all-gather.18
  255.2 20.4 all-gather.20
  300.0 15.8 all-gather.22
where the time goes:
time: 330 us; the launch traced here: 328 us
  waiting for transfers between devices  143 us (43%)
  local copies, waits for them, and re-layouts  55.9 us (17%)
  matrix products  48.4 us (15%)
  other arithmetic  39.2 us (12%)
  between operations  29.6 us (9%)
  starting transfers between devices  10.9 us (3%)
    all_gather x4, waiting for transfers between devices, gather_heads(): every_head = lax.all_gather(head_rows, 'seq', axis=1, tiled=True)  68.3 us
    all_gather x4, waiting for transfers between devices, shards(): full_rows = lax.all_gather(own_rows, 'seq', axis=1, tiled=True)  56 us
    dot_general x4, matrix products, run_block(): jnp.dot(shaped, qkv_weights, preferred_element_type=jnp.float32)  22.4 us
    unnamed x67, local copies, waits for them, and re-layouts  20.5 us
    ppermute x3, waiting for transfers between devices, passed_along(): lax.ppermute(value, axis, [(source, source + steps) for source in range(l...  19 us
    dynamic_update_slice x4, local copies, waits for them, and re-layouts, run_block(): lax.dynamic_update_slice_in_dim(value_cache, jnp.where(mask, fresh_values...  15.3 us
    dynamic_update_slice x4, local copies, waits for them, and re-layouts, run_block(): lax.dynamic_update_slice_in_dim(key_cache, jnp.where(mask, fresh_keys, wi...  15 us
    dot_general x4, matrix products, gather_heads(): return jnp.dot(every_head, out_weights, preferred_element_type=jnp.float32)  11.3 us
  transfers between devices with their start and end apart: 11, of which 10 were waited for; matrix products, arithmetic and copies ran while one was open for 7% of the time, Pallas kernels for 0%

commit v1 on v0

--- a/solution.py
+++ b/solution.py
@@ -21,6 +21,13 @@
 
 def rms_norm(values):
     return values * lax.rsqrt(jnp.mean(values * values, axis=-1, keepdims=True) + epsilon)
+
+
+def gather_features(rows):
+    across_chips = lax.all_gather(rows, "seq_chip", axis=0)
+    both_cores = lax.all_gather(across_chips, "seq_core", axis=1)
+    count, width = rows.shape
+    return jnp.transpose(both_cores, (2, 0, 1, 3)).reshape(count, -1)
 
 
 def pick_entry(vector, position):
@@ -104,7 +111,7 @@
     row_numbers = jnp.arange(biggest_patch_span)
 
     def gather_heads(head_rows):
-        every_head = lax.all_gather(head_rows, "seq", axis=1, tiled=True)
+        every_head = gather_features(head_rows)
         return jnp.dot(every_head, out_weights, preferred_element_type=jnp.float32)
 
     results = []
@@ -122,7 +129,7 @@
         )
         own_rows = jnp.where(section_index == 0, entry_patch, earlier_result)
         own_rows = jnp.where(live_rows[:, None], own_rows, jnp.zeros_like(own_rows))
-        full_rows = lax.all_gather(own_rows, "seq", axis=1, tiled=True)
+        full_rows = gather_features(own_rows)
         updated, key_cache, value_cache = run_block(
             full_rows,
             own_rows,
@@ -141,21 +148,31 @@
     return jnp.stack(results)[:, None]
 
 
+def chip_mesh(mesh):
+    devices = mesh.devices
+    groups, section, seq = devices.shape
+    return jax.sharding.Mesh(
+        devices.reshape(groups, section, seq // 2, 2), ("groups", "section", "seq_chip", "seq_core")
+    )
+
+
 def solution(mesh):
+    mesh = chip_mesh(mesh)
+    seq = ("seq_chip", "seq_core")
     return jax.shard_map(
         shards,
         mesh=mesh,
         in_specs=(
-            P("groups", "seq"),
-            P("section", "groups", "seq"),
+            P("groups", seq),
+            P("section", "groups", seq),
             P("groups"),
-            P("section", "seq", "groups", None),
-            P("section", "seq", "groups", None),
-            P("section", None, "seq"),
-            P("section", None, "seq"),
+            P("section", seq, "groups", None),
+            P("section", seq, "groups", None),
+            P("section", None, seq),
+            P("section", None, seq),
             P("section", None, None),
-            P("section", "seq"),
+            P("section", seq),
         ),
-        out_specs=P(None, "section", "groups", "seq"),
+        out_specs=P(None, "section", "groups", seq),
         check_vma=False,
     )

time: 330 us -> 409 us (1.24)
  blocking collectives: 0 us -> 94.7 us
  waiting for transfers between devices: 143 us -> 83.7 us
  local copies, waits for them, and re-layouts: 55.9 us -> 87.4 us
  other arithmetic: 39.2 us -> 49.1 us
    all_gather x0 -> x8, blocking collectives: none -> 94.7 us  [gather_features(): across_chips = lax.all_gather(rows, 'seq_chip', axis=0)]
    all_gather x8, waiting for transfers between devices: 124 us -> 65.7 us  [gather_features(): both_cores = lax.all_gather(across_chips, 'seq_core', axis=1)]
    convert_element_type x0 -> x8, other arithmetic: none -> 14.6 us  [the longest x4 7.6 us: run_block(): shaped = (layer_norm(full_rows.astype(jnp.float32)) * (1.0 + shift_scale[...]
    convert_element_type x0 -> x4, local copies, waits for them, and re-layouts: none -> 10.4 us  [run_block(): shaped = (layer_norm(full_rows.astype(jnp.float32)) * (1.0 + shift_scale[...]
    transpose x0 -> x4, local copies, waits for them, and re-layouts: none -> 9.03 us  [gather_features(): return jnp.transpose(both_cores, (2, 0, 1, 3)).reshape(count, -1)]
    another operation x0 -> x4, local copies, waits for them, and re-layouts: none -> 7.21 us  [gather_features(): across_chips = lax.all_gather(rows, 'seq_chip', axis=0)]
    reduce_sum x4, other arithmetic: 7.84 us -> 1.83 us  [layer_norm(): spread = jnp.mean(centred * centred, axis=-1, keepdims=True)]
    reduce_sum x4 -> x8, other arithmetic: 7.26 us -> 9.55 us  [layer_norm(): row_mean = jnp.mean(values, axis=-1, keepdims=True)]
where the time goes in v1:
time: 409 us; the launch traced here: 406 us
  blocking collectives  94.7 us (23%)
  local copies, waits for them, and re-layouts  87.4 us (21%)
  waiting for transfers between devices  83.7 us (20%)
  other arithmetic  49.1 us (12%)
  matrix products  48.7 us (12%)
  between operations  28.5 us (7%)
  starting transfers between devices  14.3 us (3%)
    all_gather x8, blocking collectives, gather_features(): across_chips = lax.all_gather(rows, 'seq_chip', axis=0)  94.7 us
    all_gather x8, waiting for transfers between devices, gather_features(): both_cores = lax.all_gather(across_chips, 'seq_core', axis=1)  65.7 us
    dot_general x4, matrix products, run_block(): jnp.dot(shaped, qkv_weights, preferred_element_type=jnp.float32)  22.7 us
    unnamed x65, local copies, waits for them, and re-layouts  20.5 us
    ppermute x3, waiting for transfers between devices, passed_along(): lax.ppermute(value, axis, [(source, source + steps) for source in range(l...  17.8 us
    dynamic_update_slice x4, local copies, waits for them, and re-layouts, run_block(): lax.dynamic_update_slice_in_dim(key_cache, jnp.where(mask, fresh_keys, wi...  15.3 us
    dynamic_update_slice x4, local copies, waits for them, and re-layouts, run_block(): lax.dynamic_update_slice_in_dim(value_cache, jnp.where(mask, fresh_values...  15.3 us
    ppermute x3, starting transfers between devices, passed_along(): lax.ppermute(value, axis, [(source, source + steps) for source in range(l...  13.3 us
  transfers between devices with their start and end apart: 11, of which 10 were waited for; matrix products, arithmetic and copies ran while one was open for 7% of the time, Pallas kernels for 0%

profile of v1, /device:TPU:0, one launch (start us, length us, event | category | flops | bytes accessed | tf_op | source)
XLA Modules:
  0.0 406.4 jit_solution(4400224548617300417)
XLA Ops:
  13.5 12.8 %all-gather = bf16[512,768]{1,0:T(8,128)(2,1)} all-gather(bf16[256,768]{1,0:T(8,128)(2,1)S(1)} %fusion.59), channel_id=2, replica_groups=mesh['groups'=2,'section'=4,'seq_chip'=2,'seq_core'=2] {'seq_chip'}, dimensions={0}, use_global_device_ids=true | all-gather | bytes 1179648 | tf_op jit(solution)/shard_map/all_gather | solution.py:27
  31.0 2.3 copy.184
  33.3 2.4 copy.179
  35.7 2.4 concatenate.10
  40.4 12.7 %copy.181 = bf16[1,3072,1536]{1,2,0:T(8,128)(2,1)} copy(bf16[1,3072,1536]{2,1,0:T(8,128)(2,1)} %param.14) | data formatting | bytes 18874368 | tf_op args[5]
  60.8 2.6 copy.180
  63.4 5.8 %fusion.105 = f32[256,4,3,128]{0,3,2,1:T(8,128)S(1)} fusion(bf16[256,3072,1,1]{0,1,3,2:T(8,128)(2,1)} %bitcast.260, bf16[4,3,128,3072]{3,2,1,0:T(8,128)(2,1)} %bitcast.247), kind=kOutput, calls=%fused_computation.172 | convolution fusion | flops 2415919104 | bytes 12582912 | tf_op jit(solution)/shard_map/dot_general | solution.py:56
  70.5 3.5 dynamic_update_slice.24
  74.0 3.5 dynamic_update_slice.25
  83.0 10.9 %all_gather.88 = bf16[2,256,512]{2,1,0:T(8,128)(2,1)} all-gather(bf16[1,256,512]{2,1,0:T(8,128)(2,1)} %copy.187), channel_id=1, replica_groups=mesh['groups'=2,'section'=4,'seq_chip'=2,'seq_core'=2] {'seq_chip'}, dimensions={0}, use_global_device_ids=true | all-gather | bytes 786432 | tf_op jit(solution)/shard_map/all_gather | solution.py:27
  94.7 9.6 %all-gather.23.cloned.1.call-done = bf16[2,512,512]{2,1,0:T(8,128)(2,1)} async-done(((bf16[2,256,512]{2,1,0:T(8,128)(2,1)}), bf16[2,512,512]{2,1,0:T(8,128)(2,1)}) %all-gather.23.cloned.1.call-update) | async-done | bytes 1048592 | tf_op jit(solution)/shard_map/all_gather | solution.py:28
  106.6 3.0 fusion.38
  109.6 4.4 %collective-permute-start = (bf16[256,768]{1,0:T(8,128)(2,1)}, bf16[256,768]{1,0:T(8,128)(2,1)}, u32[]{:S(2)}, u32[]{:S(2)}) collective-permute-start(bf16[256,768]{1,0:T(8,128)(2,1)} %fusion.38), channel_id=1, source_target_pairs={{0,4},{4,8},{8,12},{1,5},{5,9},{9,13},{2,6},{6,10},{10,14},{3,7},{... | collective-permute-start | bytes 1179656 | tf_op jit(solution)/shard_map/ppermute | solution.py:12
  116.4 6.0 %collective-permute-done = bf16[256,768]{1,0:T(8,128)(2,1)} collective-permute-done((bf16[256,768]{1,0:T(8,128)(2,1)}, bf16[256,768]{1,0:T(8,128)(2,1)}, u32[]{:S(2)}, u32[]{:S(2)}) %collective-permute-start) | collective-permute-done | bytes 393248 | tf_op jit(solution)/shard_map/ppermute | solution.py:12
  123.6 11.3 %all-gather.3 = bf16[512,768]{1,0:T(8,128)(2,1)} all-gather(bf16[256,768]{1,0:T(8,128)(2,1)S(1)} %fusion.61), channel_id=5, replica_groups=mesh['groups'=2,'section'=4,'seq_chip'=2,'seq_core'=2] {'seq_chip'}, dimensions={0}, use_global_device_ids=true | all-gather | bytes 1179648 | tf_op jit(solution)/shard_map/all_gather | solution.py:27
  137.0 9.9 %all-gather.25.cloned.1.call-done = bf16[2,512,768]{2,1,0:T(8,128)(2,1)} async-done(((bf16[2,256,768]{2,1,0:T(8,128)(2,1)}), bf16[2,512,768]{2,1,0:T(8,128)(2,1)}) %all-gather.25.cloned.1.call-update) | async-done | bytes 1572880 | tf_op jit(solution)/shard_map/all_gather | solution.py:28
  154.1 2.6 copy.189
  156.7 5.6 %fusion.106 = f32[256,4,3,128]{0,3,2,1:T(8,128)S(1)} fusion(bf16[256,3072,1,1]{0,1,3,2:T(8,128)(2,1)} %bitcast.261, bf16[4,3,128,3072]{3,2,1,0:T(8,128)(2,1)} %bitcast.248), kind=kOutput, calls=%fused_computation.173 | convolution fusion | flops 2415919104 | bytes 12582912 | tf_op jit(solution)/shard_map/dot_general | solution.py:56
  163.5 2.3 fusion.83
  165.7 3.9 dynamic_update_slice.26
  169.7 4.0 dynamic_update_slice.27
  179.2 12.4 %all_gather.95 = bf16[2,256,512]{2,1,0:T(8,128)(2,1)} all-gather(bf16[1,256,512]{2,1,0:T(8,128)(2,1)} %copy.195), channel_id=1, replica_groups=mesh['groups'=2,'section'=4,'seq_chip'=2,'seq_core'=2] {'seq_chip'}, dimensions={0}, use_global_device_ids=true | all-gather | bytes 786432 | tf_op jit(solution)/shard_map/all_gather | solution.py:27
  191.6 9.1 %all-gather.27.cloned.1.call-done = bf16[2,512,512]{2,1,0:T(8,128)(2,1)} async-done(((bf16[2,256,512]{2,1,0:T(8,128)(2,1)}), bf16[2,512,512]{2,1,0:T(8,128)(2,1)}) %all-gather.27.cloned.1.call-update) | async-done | bytes 1048592 | tf_op jit(solution)/shard_map/all_gather | solution.py:28
  202.9 3.0 select_convert_fusion.2
  206.0 4.4 %collective-permute-start.1 = (bf16[256,768]{1,0:T(8,128)(2,1)}, bf16[256,768]{1,0:T(8,128)(2,1)}, u32[]{:S(2)}, u32[]{:S(2)}) collective-permute-start(bf16[256,768]{1,0:T(8,128)(2,1)} %select_convert_fusion.2), channel_id=1, source_target_pairs={{0,4},{4,8},{8,12},{1,5},{5,9},{9,13},{2,6},{6,10},{10,14},{3,7},{... | collective-permute-start | bytes 1179656 | tf_op jit(solution)/shard_map/ppermute | solution.py:12
  212.7 6.1 %collective-permute-done.1 = bf16[256,768]{1,0:T(8,128)(2,1)} collective-permute-done((bf16[256,768]{1,0:T(8,128)(2,1)}, bf16[256,768]{1,0:T(8,128)(2,1)}, u32[]{:S(2)}, u32[]{:S(2)}) %collective-permute-start.1) | collective-permute-done | bytes 393248 | tf_op jit(solution)/shard_map/ppermute | solution.py:12
  220.0 11.3 %all-gather.6 = bf16[512,768]{1,0:T(8,128)(2,1)} all-gather(bf16[256,768]{1,0:T(8,128)(2,1)S(1)} %fusion.63), channel_id=8, replica_groups=mesh['groups'=2,'section'=4,'seq_chip'=2,'seq_core'=2] {'seq_chip'}, dimensions={0}, use_global_device_ids=true | all-gather | bytes 1179648 | tf_op jit(solution)/shard_map/all_gather | solution.py:27
  233.5 9.8 %all-gather.29.cloned.1.call-done = bf16[2,512,768]{2,1,0:T(8,128)(2,1)} async-done(((bf16[2,256,768]{2,1,0:T(8,128)(2,1)}), bf16[2,512,768]{2,1,0:T(8,128)(2,1)}) %all-gather.29.cloned.1.call-update) | async-done | bytes 1572880 | tf_op jit(solution)/shard_map/all_gather | solution.py:28
  250.4 2.6 copy.197
  253.0 5.6 %fusion.107 = f32[256,4,3,128]{0,3,2,1:T(8,128)S(1)} fusion(bf16[256,3072,1,1]{0,1,3,2:T(8,128)(2,1)} %bitcast.262, bf16[4,3,128,3072]{3,2,1,0:T(8,128)(2,1)} %bitcast.249), kind=kOutput, calls=%fused_computation.174 | convolution fusion | flops 2415919104 | bytes 12582912 | tf_op jit(solution)/shard_map/dot_general | solution.py:56
  259.8 2.3 fusion.85
  262.1 3.9 dynamic_update_slice.28
  266.0 3.9 dynamic_update_slice.29
  275.4 12.4 %all_gather.102 = bf16[2,256,512]{2,1,0:T(8,128)(2,1)} all-gather(bf16[1,256,512]{2,1,0:T(8,128)(2,1)} %copy.203), channel_id=1, replica_groups=mesh['groups'=2,'section'=4,'seq_chip'=2,'seq_core'=2] {'seq_chip'}, dimensions={0}, use_global_device_ids=true | all-gather | bytes 786432 | tf_op jit(solution)/shard_map/all_gather | solution.py:27
  287.9 9.2 %all-gather.31.cloned.1.call-done = bf16[2,512,512]{2,1,0:T(8,128)(2,1)} async-done(((bf16[2,256,512]{2,1,0:T(8,128)(2,1)}), bf16[2,512,512]{2,1,0:T(8,128)(2,1)}) %all-gather.31.cloned.1.call-update) | async-done | bytes 1048592 | tf_op jit(solution)/shard_map/all_gather | solution.py:28
  299.3 3.0 select_convert_fusion.1
  302.4 4.4 %collective-permute-start.2 = (bf16[256,768]{1,0:T(8,128)(2,1)}, bf16[256,768]{1,0:T(8,128)(2,1)}, u32[]{:S(2)}, u32[]{:S(2)}) collective-permute-start(bf16[256,768]{1,0:T(8,128)(2,1)} %select_convert_fusion.1), channel_id=1, source_target_pairs={{0,4},{4,8},{8,12},{1,5},{5,9},{9,13},{2,6},{6,10},{10,14},{3,7},{... | collective-permute-start | bytes 1179656 | tf_op jit(solution)/shard_map/ppermute | solution.py:12
  309.4 5.7 %collective-permute-done.2 = bf16[256,768]{1,0:T(8,128)(2,1)} collective-permute-done((bf16[256,768]{1,0:T(8,128)(2,1)}, bf16[256,768]{1,0:T(8,128)(2,1)}, u32[]{:S(2)}, u32[]{:S(2)}) %collective-permute-start.2) | collective-permute-done | bytes 393248 | tf_op jit(solution)/shard_map/ppermute | solution.py:12
  316.3 11.3 %all-gather.9 = bf16[512,768]{1,0:T(8,128)(2,1)} all-gather(bf16[256,768]{1,0:T(8,128)(2,1)S(1)} %fusion.65), channel_id=11, replica_groups=mesh['groups'=2,'section'=4,'seq_chip'=2,'seq_core'=2] {'seq_chip'}, dimensions={0}, use_global_device_ids=true | all-gather | bytes 1179648 | tf_op jit(solution)/shard_map/all_gather | solution.py:27
  329.8 9.8 %all-gather.33.cloned.1.call-done = bf16[2,512,768]{2,1,0:T(8,128)(2,1)} async-done(((bf16[2,256,768]{2,1,0:T(8,128)(2,1)}), bf16[2,512,768]{2,1,0:T(8,128)(2,1)}) %all-gather.33.cloned.1.call-update) | async-done | bytes 1572880 | tf_op jit(solution)/shard_map/all_gather | solution.py:28
  346.8 2.6 copy.205
  349.4 5.6 %fusion.108 = f32[256,4,3,128]{0,3,2,1:T(8,128)S(1)} fusion(bf16[256,3072,1,1]{0,1,3,2:T(8,128)(2,1)} %bitcast.259, bf16[4,3,128,3072]{3,2,1,0:T(8,128)(2,1)} %bitcast.250), kind=kOutput, calls=%fused_computation.175 | convolution fusion | flops 2415919104 | bytes 12582912 | tf_op jit(solution)/shard_map/dot_general | solution.py:56
  356.2 2.3 fusion.87
  358.5 3.9 dynamic_update_slice.30
  362.4 3.9 dynamic_update_slice.31
  371.8 12.4 %all_gather.109 = bf16[2,256,512]{2,1,0:T(8,128)(2,1)} all-gather(bf16[1,256,512]{2,1,0:T(8,128)(2,1)} %copy.211), channel_id=1, replica_groups=mesh['groups'=2,'section'=4,'seq_chip'=2,'seq_core'=2] {'seq_chip'}, dimensions={0}, use_global_device_ids=true | all-gather | bytes 786432 | tf_op jit(solution)/shard_map/all_gather | solution.py:27
  384.2 8.3 %all-gather.35.cloned.1.call-done = bf16[2,512,512]{2,1,0:T(8,128)(2,1)} async-done(((bf16[2,256,512]{2,1,0:T(8,128)(2,1)}), bf16[2,512,512]{2,1,0:T(8,128)(2,1)}) %all-gather.35.cloned.1.call-update) | async-done | bytes 1048592 | tf_op jit(solution)/shard_map/all_gather | solution.py:28
  397.0 2.6 maximum_bitcast_fusion
  (159 shorter events, 84.5 us)
Async XLA Ops:
  6.5 100.0 %copy-start = (bf16[1,2048,768]{2,1,0:T(8,128)(2,1)S(1)}, bf16[1,2048,768]{2,1,0:T(8,128)(2,1)}, u32[]{:S(2)}) copy-start(bf16[1,2048,768]{2,1,0:T(8,128)(2,1)} %param.15) | copy-start | bytes 9437188
  6.5 47.1 %all-gather.21.cloned.1.call-start = ((), (), s32[]{:S(2)}) async-start(), calls=%async_computation | async-start | bytes 2359296 | tf_op jit(solution)/shard_map/all_gather | solution.py:28
  9.6 19.4 %copy-start.29 = (pred[256]{0:T(512)(128)(4,1)}, pred[256]{0:T(512)(128)(4,1)S(1)}, u32[]{:S(2)}) copy-start(pred[256]{0:T(512)(128)(4,1)S(1)} %iota_compare_fusion.3) | copy-start | bytes 772
  26.4 77.9 %all-gather.23.cloned.1.call-start = ((), (), s32[]{:S(2)}) async-start(), calls=%async_computation.1 | async-start | bytes 1572864 | tf_op jit(solution)/shard_map/all_gather | solution.py:28
  56.6 2.2 copy-start.1
  56.7 2.3 copy-start.15
  63.4 5.9 %copy-start.5 = (bf16[1,4,768,128]{2,3,1,0:T(8,128)(2,1)S(1)}, bf16[1,4,768,128]{2,3,1,0:T(8,128)(2,1)}, u32[]{:S(2)}) copy-start(bf16[1,4,768,128]{2,3,1,0:T(8,128)(2,1)} %copy.184) | copy-start | bytes 2359300
  63.4 5.9 %copy-start.6 = (bf16[1,4,768,128]{2,3,1,0:T(8,128)(2,1)S(1)}, bf16[1,4,768,128]{2,3,1,0:T(8,128)(2,1)}, u32[]{:S(2)}) copy-start(bf16[1,4,768,128]{2,3,1,0:T(8,128)(2,1)} %copy.179) | copy-start | bytes 2359300
  63.4 5.9 %copy-start.30 = (pred[256]{0:T(512)(128)(4,1)S(1)}, pred[256]{0:T(512)(128)(4,1)}, u32[]{:S(2)}) copy-start(pred[256]{0:T(512)(128)(4,1)} %copy-done.29) | copy-start | bytes 772
  69.2 1.3 copy-start.7
  77.5 2.2 copy-start.11
  93.9 53.0 %all-gather.25.cloned.1.call-start = ((), (), s32[]{:S(2)}) async-start(), calls=%async_computation.2 | async-start | bytes 2359296 | tf_op jit(solution)/shard_map/all_gather | solution.py:28
  94.7 14.9 %copy-start.19 = (f32[768]{0:T(1024)}, f32[768]{0:T(1024)S(1)}, u32[]{:S(2)}) copy-start(f32[768]{0:T(1024)S(1)} %reduce.24) | copy-start | bytes 9220
  109.6 12.8 %collective-permute-start = (bf16[256,768]{1,0:T(8,128)(2,1)}, bf16[256,768]{1,0:T(8,128)(2,1)}, u32[]{:S(2)}, u32[]{:S(2)}) collective-permute-start(bf16[256,768]{1,0:T(8,128)(2,1)} %fusion.38), channel_id=1, source_target_pairs={{0,4},{4,8},{8,12},{1,5},{5,9},{9,13},{2,6},{6,10},{10,14},{3,7},{... | collective-permute-start | bytes 1179656 | tf_op jit(solution)/shard_map/ppermute | solution.py:12
  116.4 6.0 %copy-start.25 = (pred[256]{0:T(512)(128)(4,1)}, pred[256]{0:T(512)(128)(4,1)S(1)}, u32[]{:S(2)}) copy-start(pred[256]{0:T(512)(128)(4,1)S(1)} %iota_compare_fusion.2) | copy-start | bytes 772
  134.9 65.8 %all-gather.27.cloned.1.call-start = ((), (), s32[]{:S(2)}) async-start(), calls=%async_computation.3 | async-start | bytes 1572864 | tf_op jit(solution)/shard_map/all_gather | solution.py:28
  149.9 2.2 copy-start.3
  149.9 2.3 copy-start.16
  156.7 6.8 %copy-start.26 = (pred[256]{0:T(512)(128)(4,1)S(1)}, pred[256]{0:T(512)(128)(4,1)}, u32[]{:S(2)}) copy-start(pred[256]{0:T(512)(128)(4,1)} %copy-done.25) | copy-start | bytes 772
  162.3 1.1 copy-start.9
  173.6 2.2 copy-start.12
  177.3 25.6 %copy-start.20 = (f32[768]{0:T(1024)S(1)}, f32[768]{0:T(1024)}, u32[]{:S(2)}) copy-start(f32[768]{0:T(1024)} %copy-done.19) | copy-start | bytes 9220
  191.5 51.7 %all-gather.29.cloned.1.call-start = ((), (), s32[]{:S(2)}) async-start(), calls=%async_computation.4 | async-start | bytes 2359296 | tf_op jit(solution)/shard_map/all_gather | solution.py:28
  206.0 12.8 %collective-permute-start.1 = (bf16[256,768]{1,0:T(8,128)(2,1)}, bf16[256,768]{1,0:T(8,128)(2,1)}, u32[]{:S(2)}, u32[]{:S(2)}) collective-permute-start(bf16[256,768]{1,0:T(8,128)(2,1)} %select_convert_fusion.2), channel_id=1, source_target_pairs={{0,4},{4,8},{8,12},{1,5},{5,9},{9,13},{2,6},{6,10},{10,14},{3,7},{... | collective-permute-start | bytes 1179656 | tf_op jit(solution)/shard_map/ppermute | solution.py:12
  212.7 6.1 %copy-start.27 = (pred[256]{0:T(512)(128)(4,1)}, pred[256]{0:T(512)(128)(4,1)S(1)}, u32[]{:S(2)}) copy-start(pred[256]{0:T(512)(128)(4,1)S(1)} %iota_compare_fusion.1) | copy-start | bytes 772
  231.3 65.8 %all-gather.31.cloned.1.call-start = ((), (), s32[]{:S(2)}) async-start(), calls=%async_computation.5 | async-start | bytes 1572864 | tf_op jit(solution)/shard_map/all_gather | solution.py:28
  246.3 2.2 copy-start.4
  246.3 2.3 copy-start.17
  253.0 6.8 %copy-start.28 = (pred[256]{0:T(512)(128)(4,1)S(1)}, pred[256]{0:T(512)(128)(4,1)}, u32[]{:S(2)}) copy-start(pred[256]{0:T(512)(128)(4,1)} %copy-done.27) | copy-start | bytes 772
  258.7 1.1 copy-start.10
  269.9 2.2 copy-start.13
  273.6 25.7 %copy-start.21 = (f32[768]{0:T(1024)S(1)}, f32[768]{0:T(1024)}, u32[]{:S(2)}) copy-start(f32[768]{0:T(1024)} %copy-done.19) | copy-start | bytes 9220
  287.8 51.8 %all-gather.33.cloned.1.call-start = ((), (), s32[]{:S(2)}) async-start(), calls=%async_computation.6 | async-start | bytes 2359296 | tf_op jit(solution)/shard_map/all_gather | solution.py:28
  302.4 12.8 %collective-permute-start.2 = (bf16[256,768]{1,0:T(8,128)(2,1)}, bf16[256,768]{1,0:T(8,128)(2,1)}, u32[]{:S(2)}, u32[]{:S(2)}) collective-permute-start(bf16[256,768]{1,0:T(8,128)(2,1)} %select_convert_fusion.1), channel_id=1, source_target_pairs={{0,4},{4,8},{8,12},{1,5},{5,9},{9,13},{2,6},{6,10},{10,14},{3,7},{... | collective-permute-start | bytes 1179656 | tf_op jit(solution)/shard_map/ppermute | solution.py:12
  309.4 5.8 %copy-start.23 = (pred[256]{0:T(512)(128)(4,1)}, pred[256]{0:T(512)(128)(4,1)S(1)}, u32[]{:S(2)}) copy-start(pred[256]{0:T(512)(128)(4,1)S(1)} %iota_compare_fusion) | copy-start | bytes 772
  327.7 64.8 %all-gather.35.cloned.1.call-start = ((), (), s32[]{:S(2)}) async-start(), calls=%async_computation.7 | async-start | bytes 1572864 | tf_op jit(solution)/shard_map/all_gather | solution.py:28
  342.6 2.2 copy-start.2
  342.6 2.3 copy-start.18
  349.4 6.8 %copy-start.24 = (pred[256]{0:T(512)(128)(4,1)S(1)}, pred[256]{0:T(512)(128)(4,1)}, u32[]{:S(2)}) copy-start(pred[256]{0:T(512)(128)(4,1)} %copy-done.23) | copy-start | bytes 772
  355.1 1.1 copy-start.8
  366.3 2.2 copy-start.14
  370.0 24.7 %copy-start.22 = (f32[768]{0:T(1024)S(1)}, f32[768]{0:T(1024)}, u32[]{:S(2)}) copy-start(f32[768]{0:T(1024)} %copy-done.19) | copy-start | bytes 9220
Sparse Core Ops, SparseCore 0:
  26.5 11.3 all-gather.20
  94.0 10.2 all-gather.22
  135.0 11.8 all-gather.24
  191.7 8.9 all-gather.26
  231.4 11.8 all-gather.28
  288.0 9.0 all-gather.30
  327.8 11.8 all-gather.32
  384.3 8.1 all-gather.34

commit v2 on v0

--- a/solution.py
+++ b/solution.py
@@ -1,6 +1,10 @@
+import functools
+
 import jax
 import jax.numpy as jnp
 from jax import lax
+from jax.experimental import pallas as pl
+from jax.experimental.pallas import tpu as pltpu
 from jax.sharding import PartitionSpec as P
 
 epsilon = 1e-06
@@ -27,11 +31,74 @@
     return jnp.sum(jnp.where(jnp.arange(vector.shape[0]) == position, vector, 0))
 
 
+def attention_kernel(where_ref, mixed_ref, keys_ref, values_ref, heads_ref, keys_out, values_out):
+    head_dim = keys_ref.shape[2]
+    seq_len = keys_ref.shape[1]
+    span = mixed_ref.shape[0]
+    start = where_ref[0]
+    count = where_ref[1]
+    block = mixed_ref[...]
+    queries = rms_norm(block[:, :head_dim]).astype(jnp.bfloat16)
+    fresh_keys = rms_norm(block[:, head_dim : 2 * head_dim]).astype(jnp.bfloat16)
+    fresh_values = block[:, 2 * head_dim :].astype(jnp.bfloat16)
+    rows = lax.broadcasted_iota(jnp.int32, (seq_len, span), 0)
+    picks = lax.broadcasted_iota(jnp.int32, (seq_len, span), 1)
+    placing = ((rows == picks + start) & (picks < count)).astype(jnp.bfloat16)
+    row_ids = lax.broadcasted_iota(jnp.int32, (seq_len, 1), 0)
+    inside = (row_ids >= start) & (row_ids < start + count)
+    placed_keys = jnp.dot(placing, fresh_keys, preferred_element_type=jnp.float32)
+    placed_values = jnp.dot(placing, fresh_values, preferred_element_type=jnp.float32)
+    keys = jnp.where(inside, placed_keys.astype(jnp.bfloat16), keys_ref[0])
+    values = jnp.where(inside, placed_values.astype(jnp.bfloat16), values_ref[0])
+    keys_out[0] = keys
+    values_out[0] = values
+    scores = lax.dot_general(
+        queries, keys, (((1,), (1,)), ((), ())), preferred_element_type=jnp.float32
+    ) * head_dim ** (-0.5)
+    expos = jnp.exp(scores)
+    weights = (expos / jnp.sum(expos, axis=-1, keepdims=True)).astype(jnp.bfloat16)
+    heads_ref[...] = jnp.dot(weights, values, preferred_element_type=jnp.float32).astype(
+        jnp.bfloat16
+    )
+
+
+def attend(mixed, key_cache, value_cache, patch_start, patch_count):
+    heads_here, seq_len, head_dim = key_cache.shape
+    span = mixed.shape[0]
+    where = jnp.stack([patch_start, patch_count]).astype(jnp.int32)
+    cache_spec = pl.BlockSpec((1, seq_len, head_dim), lambda h, where: (h, 0, 0))
+    grid_spec = pltpu.PrefetchScalarGridSpec(
+        num_scalar_prefetch=1,
+        grid=(heads_here,),
+        in_specs=[
+            pl.BlockSpec((span, 3 * head_dim), lambda h, where: (0, h)),
+            cache_spec,
+            cache_spec,
+        ],
+        out_specs=[
+            pl.BlockSpec((span, head_dim), lambda h, where: (0, h)),
+            cache_spec,
+            cache_spec,
+        ],
+    )
+    return pl.pallas_call(
+        attention_kernel,
+        grid_spec=grid_spec,
+        out_shape=[
+            jax.ShapeDtypeStruct((span, heads_here * head_dim), jnp.bfloat16),
+            jax.ShapeDtypeStruct(key_cache.shape, key_cache.dtype),
+            jax.ShapeDtypeStruct(value_cache.shape, value_cache.dtype),
+        ],
+        input_output_aliases={2: 1, 3: 2},
+    )(where, mixed, key_cache, value_cache)
+
+
 def run_block(
     full_rows,
     own_rows,
     live_rows,
     patch_start,
+    patch_count,
     key_cache,
     value_cache,
     qkv_weights,
@@ -39,37 +106,13 @@
     gating_here,
     project,
 ):
-    biggest_patch_span = full_rows.shape[0]
-    heads_here = key_cache.shape[0]
-    head_dim = key_cache.shape[2]
-    seq_len = key_cache.shape[1] - biggest_patch_span
     shaped = (
         layer_norm(full_rows.astype(jnp.float32)) * (1.0 + shift_scale[1]) + shift_scale[0]
     ).astype(jnp.bfloat16)
-    mixed = jnp.dot(shaped, qkv_weights, preferred_element_type=jnp.float32).reshape(
-        biggest_patch_span, heads_here, 3, head_dim
-    )
-    queries = rms_norm(mixed[:, :, 0]).astype(jnp.bfloat16)
-    fresh_keys = jnp.transpose(rms_norm(mixed[:, :, 1]).astype(jnp.bfloat16), (1, 0, 2))
-    fresh_values = jnp.transpose(mixed[:, :, 2].astype(jnp.bfloat16), (1, 0, 2))
-    mask = live_rows[None, :, None]
-    window = lax.dynamic_slice_in_dim(key_cache, patch_start, biggest_patch_span, 1)
-    key_cache = lax.dynamic_update_slice_in_dim(
-        key_cache, jnp.where(mask, fresh_keys, window), patch_start, 1
-    )
-    window = lax.dynamic_slice_in_dim(value_cache, patch_start, biggest_patch_span, 1)
-    value_cache = lax.dynamic_update_slice_in_dim(
-        value_cache, jnp.where(mask, fresh_values, window), patch_start, 1
-    )
-    scores = jnp.einsum(
-        "qhd,hkd->hqk", queries, key_cache[:, :seq_len], preferred_element_type=jnp.float32
-    ) * head_dim ** (-0.5)
-    expos = jnp.exp(scores)
-    weights = (expos / jnp.sum(expos, axis=-1, keepdims=True)).astype(jnp.bfloat16)
-    attended = jnp.einsum(
-        "hqk,hkd->qhd", weights, value_cache[:, :seq_len], preferred_element_type=jnp.float32
-    ).astype(jnp.bfloat16)
-    head_rows = attended.reshape(biggest_patch_span, heads_here * head_dim)
+    mixed = jnp.dot(shaped, qkv_weights, preferred_element_type=jnp.float32)
+    head_rows, key_cache, value_cache = attend(
+        mixed, key_cache, value_cache, patch_start, patch_count
+    )
     projected = project(head_rows)
     updated = own_rows.astype(jnp.float32) + gating_here * projected
     updated = jnp.where(live_rows[:, None], updated, 0.0).astype(jnp.bfloat16)
@@ -94,9 +137,8 @@
     heads_here = outdated_lookups.shape[1]
     head_dim = outdated_lookups.shape[3]
     starts = jnp.cumsum(patch_sizes_list) - patch_sizes_list
-    padding = jnp.zeros((heads_here, biggest_patch_span, head_dim), jnp.bfloat16)
-    key_cache = jnp.concatenate([outdated_lookups[0], padding], axis=1)
-    value_cache = jnp.concatenate([outdated_contents[0], padding], axis=1)
+    key_cache = outdated_lookups[0]
+    value_cache = outdated_contents[0]
     qkv_weights = attention_projection[0]
     out_weights = exit_projection[0]
     shift_scale = shift_and_scale[0]
@@ -128,6 +170,7 @@
             own_rows,
             live_rows,
             patch_start,
+            patch_count,
             key_cache,
             value_cache,
             qkv_weights,

time: 330 us -> 307 us (0.930)
  local copies, waits for them, and re-layouts: 55.9 us -> 5.01 us
  Pallas kernels: 0 us -> 26.8 us
  waiting for transfers between devices: 143 us -> 163 us
  between operations: 29.6 us -> 20.9 us
  matrix products: 48.4 us -> 41 us
    dynamic_update_slice x8 -> x0, local copies, waits for them, and re-layouts: 30.2 us -> none  [the longest x4 15.3 us: run_block(): lax.dynamic_update_slice_in_dim(value_cache, jnp.where(mask, fresh_values...]
    pallas_call x0 -> x4, Pallas kernels: none -> 26.8 us  [attend(): pl.pallas_call(attention_kernel, grid_spec=grid_spec, out_shape=[jax.Shap...]
    all_gather x4, waiting for transfers between devices: 56 us -> 75.8 us  [shards(): full_rows = lax.all_gather(own_rows, 'seq', axis=1, tiled=True)]
    unnamed x67 -> x42, local copies, waits for them, and re-layouts: 20.5 us -> 4.41 us
    select_n x4 -> x0, other arithmetic: 7.38 us -> none  [run_block(): jnp.where(mask, fresh_values, window)]
    dot_general x12 -> x4, matrix products: 37.1 us -> 29.9 us  [run_block(): mixed = jnp.dot(shaped, qkv_weights, preferred_element_type=jnp.float32)]
    another operation x1 -> x5, other arithmetic: 0.98 us -> 7.81 us  [the longest x4 7.63 us: attend(): where = jnp.stack([patch_start, patch_count]).astype(jnp.int32)]
    concatenate x2 -> x0, local copies, waits for them, and re-layouts: 4.54 us -> none  [the longest x1 2.28 us: shards(): key_cache = jnp.concatenate([outdated_lookups[0], padding], axis=1)]
  transfers between devices with their start and end apart: 11 -> 11, of which waited for: 10 -> 11; matrix products, arithmetic and copies ran while one was open for 7% -> 4% of each run, Pallas kernels for 0% -> 0%
where the time goes in v2:
time: 307 us; the launch traced here: 305 us
  waiting for transfers between devices  163 us (53%)
  matrix products  41 us (13%)
  other arithmetic  38.2 us (12%)
  Pallas kernels  26.8 us (9%)
  between operations  20.9 us (7%)
  starting transfers between devices  10.7 us (3%)
  local copies, waits for them, and re-layouts  5.01 us (2%)
    all_gather x4, waiting for transfers between devices, shards(): full_rows = lax.all_gather(own_rows, 'seq', axis=1, tiled=True)  75.8 us
    all_gather x4, waiting for transfers between devices, gather_heads(): every_head = lax.all_gather(head_rows, 'seq', axis=1, tiled=True)  66.7 us
    dot_general x4, matrix products, run_block(): mixed = jnp.dot(shaped, qkv_weights, preferred_element_type=jnp.float32)  29.9 us
    pallas_call x4, Pallas kernels, attend(): pl.pallas_call(attention_kernel, grid_spec=grid_spec, out_shape=[jax.Shap...  26.8 us
    ppermute x3, waiting for transfers between devices, passed_along(): lax.ppermute(value, axis, [(source, source + steps) for source in range(l...  19.9 us
    dot_general x4, matrix products, gather_heads(): return jnp.dot(every_head, out_weights, preferred_element_type=jnp.float32)  11.1 us
    ppermute x3, starting transfers between devices, passed_along(): lax.ppermute(value, axis, [(source, source + steps) for source in range(l...  10.2 us
    reduce_sum x4, other arithmetic, layer_norm(): spread = jnp.mean(centred * centred, axis=-1, keepdims=True)  7.84 us
  transfers between devices with their start and end apart: 11, of which 11 were waited for; matrix products, arithmetic and copies ran while one was open for 4% of the time, Pallas kernels for 0%

profile of v2, /device:TPU:0, one launch (start us, length us, event | category | flops | bytes accessed | tf_op | source)
XLA Modules:
  0.0 305.1 jit_solution(13865025915265511057)
XLA Ops:
  6.5 2.3 copy.29
  8.8 2.1 copy.30
  11.1 0.8 fusion.103
  15.1 2.0 fusion.83
  17.1 2.0 pad_add_fusion.where_ref
  19.1 0.8 slice_add_fusion
  19.9 19.6 %all-gather.9.cloned.1.call-done = bf16[256,3072]{1,0:T(8,128)(2,1)} async-done(((bf16[256,768]{1,0:T(8,128)(2,1)}), bf16[256,3072]{1,0:T(8,128)(2,1)}) %all-gather.9.cloned.1.call-update) | async-done | bytes 1572880 | tf_op jit(solution)/shard_map/all_gather | solution.py:167
  39.6 1.8 convert_reduce_fusion.3
  41.4 2.0 fusion.28
  43.4 7.5 %fusion.6.mixed_ref = f32[256,1536]{1,0:T(8,128)} fusion(bf16[1,3072,1536]{2,1,0:T(8,128)(2,1)} %param.14, bf16[256,3072]{1,0:T(8,128)(2,1)S(1)} %copy-done.1, f32[3072]{0:T(1024)S(1)} %bitcast.79, f32[3072]{0:T(1024)S(1)} %bitcast.75, f32[256]{0:T(256)S(1)} %add_rsqrt_fusion.3, f32[256]{0:T(256)S(1)} %broadcast_multiply_fusion.3), kind=kOutput, calls=%fused_computation.6 | convolution fusion | flops 2420637696 | bytes 12609536 | tf_op jit(solution)/shard_map/dot_general | solution.py:112
  50.9 6.7 %shard_map.91 = (bf16[256,512]{1,0:T(8,128)(2,1)}, bf16[4,768,128]{2,1,0:T(8,128)(2,1)}, bf16[4,768,128]{2,1,0:T(8,128)(2,1)}) custom-call(s32[2]{0:T(128)} %pad_add_fusion.where_ref, f32[256,1536]{1,0:T(8,128)} %fusion.6.mixed_ref, bf16[4,768,128]{2,1,0:T(8,128)(2,1)} %bitcast.73, ...), custom_call_target="tpu_custom_call", output_to_operand_aliasing={{1}: (2, {}), {2}: (3, {})} | custom-call | tf_op jit(solution)/shard_map/pallas_call | solution.py:84
  57.7 0.7 reduce
  58.4 16.1 %all-gather.11.cloned.1.call-done = bf16[256,2048]{1,0:T(8,128)(2,1)} async-done(((bf16[256,512]{1,0:T(8,128)(2,1)}), bf16[256,2048]{1,0:T(8,128)(2,1)}) %all-gather.11.cloned.1.call-update) | async-done | bytes 1048592 | tf_op jit(solution)/shard_map/all_gather | solution.py:149
  74.5 3.0 fusion.78
  77.5 3.4 %collective-permute-start = (bf16[256,768]{1,0:T(8,128)(2,1)}, bf16[256,768]{1,0:T(8,128)(2,1)S(1)}, u32[]{:S(2)}, u32[]{:S(2)}) collective-permute-start(bf16[256,768]{1,0:T(8,128)(2,1)} %fusion.78), channel_id=1, source_target_pairs={{0,4},{4,8},{8,12},{1,5},{5,9},{9,13},{2,6},{6,10},{10,14},{3,7},{... | collective-permute-start | bytes 1179656 | tf_op jit(solution)/shard_map/ppermute | solution.py:16
  83.2 6.7 %collective-permute-done = bf16[256,768]{1,0:T(8,128)(2,1)S(1)} collective-permute-done((bf16[256,768]{1,0:T(8,128)(2,1)}, bf16[256,768]{1,0:T(8,128)(2,1)S(1)}, u32[]{:S(2)}, u32[]{:S(2)}) %collective-permute-start) | collective-permute-done | bytes 393248 | tf_op jit(solution)/shard_map/ppermute | solution.py:16
  89.9 2.0 fusion.85
  92.0 2.0 pad_add_fusion.1.where_ref
  93.9 18.7 %all-gather.13.cloned.1.call-done = bf16[256,3072]{1,0:T(8,128)(2,1)} async-done(((bf16[256,768]{1,0:T(8,128)(2,1)}), bf16[256,3072]{1,0:T(8,128)(2,1)}) %all-gather.13.cloned.1.call-update) | async-done | bytes 1572880 | tf_op jit(solution)/shard_map/all_gather | solution.py:167
  112.6 1.8 convert_reduce_fusion.2
  114.4 2.0 fusion.24
  116.4 7.5 %fusion.4.mixed_ref = f32[256,1536]{1,0:T(8,128)} fusion(bf16[1,3072,1536]{2,1,0:T(8,128)(2,1)} %param.14, bf16[256,3072]{1,0:T(8,128)(2,1)S(1)} %copy-done.3, f32[256]{0:T(256)S(1)} %add_rsqrt_fusion.2, f32[256]{0:T(256)S(1)} %broadcast_multiply_fusion.2, f32[3072]{0:T(1024)S(1)} %bitcast.80, f32[3072]{0:T(1024)S(1)} %bitcast.76), kind=kOutput, calls=%fused_computation.4 | convolution fusion | flops 2420637696 | bytes 12609536 | tf_op jit(solution)/shard_map/dot_general | solution.py:112
  123.9 6.7 %shard_map.92 = (bf16[256,512]{1,0:T(8,128)(2,1)}, bf16[4,768,128]{2,1,0:T(8,128)(2,1)}, bf16[4,768,128]{2,1,0:T(8,128)(2,1)}) custom-call(s32[2]{0:T(128)} %pad_add_fusion.1.where_ref, f32[256,1536]{1,0:T(8,128)} %fusion.4.mixed_ref, bf16[4,768,128]{2,1,0:T(8,128)(2,1)} %get-tuple-element.16.keys_ref, ...), custom_call_target="tpu_custom_call", output_to_operand_aliasing={{1}: (2, {}), {2}: (3, {})} | custom-call | tf_op jit(solution)/shard_map/pallas_call | solution.py:84
  130.7 16.8 %all-gather.15.cloned.1.call-done = bf16[256,2048]{1,0:T(8,128)(2,1)} async-done(((bf16[256,512]{1,0:T(8,128)(2,1)}), bf16[256,2048]{1,0:T(8,128)(2,1)}) %all-gather.15.cloned.1.call-update) | async-done | bytes 1048592 | tf_op jit(solution)/shard_map/all_gather | solution.py:149
  147.5 3.0 select_convert_fusion.2
  150.5 3.4 %collective-permute-start.1 = (bf16[256,768]{1,0:T(8,128)(2,1)}, bf16[256,768]{1,0:T(8,128)(2,1)S(1)}, u32[]{:S(2)}, u32[]{:S(2)}) collective-permute-start(bf16[256,768]{1,0:T(8,128)(2,1)} %select_convert_fusion.2), channel_id=1, source_target_pairs={{0,4},{4,8},{8,12},{1,5},{5,9},{9,13},{2,6},{6,10},{10,14},{3,7},{... | collective-permute-start | bytes 1179656 | tf_op jit(solution)/shard_map/ppermute | solution.py:16
  156.3 6.6 %collective-permute-done.1 = bf16[256,768]{1,0:T(8,128)(2,1)S(1)} collective-permute-done((bf16[256,768]{1,0:T(8,128)(2,1)}, bf16[256,768]{1,0:T(8,128)(2,1)S(1)}, u32[]{:S(2)}, u32[]{:S(2)}) %collective-permute-start.1) | collective-permute-done | bytes 393248 | tf_op jit(solution)/shard_map/ppermute | solution.py:16
  162.9 1.9 fusion.87
  165.1 1.9 pad_add_fusion.2.where_ref
  167.0 18.6 %all-gather.17.cloned.1.call-done = bf16[256,3072]{1,0:T(8,128)(2,1)} async-done(((bf16[256,768]{1,0:T(8,128)(2,1)}), bf16[256,3072]{1,0:T(8,128)(2,1)}) %all-gather.17.cloned.1.call-update) | async-done | bytes 1572880 | tf_op jit(solution)/shard_map/all_gather | solution.py:167
  185.6 1.8 convert_reduce_fusion.1
  187.4 2.0 fusion.20
  189.4 7.5 %fusion.2.mixed_ref = f32[256,1536]{1,0:T(8,128)} fusion(bf16[1,3072,1536]{2,1,0:T(8,128)(2,1)} %param.14, bf16[256,3072]{1,0:T(8,128)(2,1)S(1)} %copy-done.4, f32[256]{0:T(256)S(1)} %add_rsqrt_fusion.1, f32[256]{0:T(256)S(1)} %broadcast_multiply_fusion.1, f32[3072]{0:T(1024)S(1)} %bitcast.81, f32[3072]{0:T(1024)S(1)} %bitcast.77), kind=kOutput, calls=%fused_computation.2 | convolution fusion | flops 2420637696 | bytes 12609536 | tf_op jit(solution)/shard_map/dot_general | solution.py:112
  196.9 6.7 %shard_map.93 = (bf16[256,512]{1,0:T(8,128)(2,1)}, bf16[4,768,128]{2,1,0:T(8,128)(2,1)}, bf16[4,768,128]{2,1,0:T(8,128)(2,1)}) custom-call(s32[2]{0:T(128)} %pad_add_fusion.2.where_ref, f32[256,1536]{1,0:T(8,128)} %fusion.2.mixed_ref, bf16[4,768,128]{2,1,0:T(8,128)(2,1)} %get-tuple-element.19.keys_ref, ...), custom_call_target="tpu_custom_call", output_to_operand_aliasing={{1}: (2, {}), {2}: (3, {})} | custom-call | tf_op jit(solution)/shard_map/pallas_call | solution.py:84
  203.7 16.8 %all-gather.19.cloned.1.call-done = bf16[256,2048]{1,0:T(8,128)(2,1)} async-done(((bf16[256,512]{1,0:T(8,128)(2,1)}), bf16[256,2048]{1,0:T(8,128)(2,1)}) %all-gather.19.cloned.1.call-update) | async-done | bytes 1048592 | tf_op jit(solution)/shard_map/all_gather | solution.py:149
  220.5 3.0 select_convert_fusion.1
  223.5 3.4 %collective-permute-start.2 = (bf16[256,768]{1,0:T(8,128)(2,1)}, bf16[256,768]{1,0:T(8,128)(2,1)S(1)}, u32[]{:S(2)}, u32[]{:S(2)}) collective-permute-start(bf16[256,768]{1,0:T(8,128)(2,1)} %select_convert_fusion.1), channel_id=1, source_target_pairs={{0,4},{4,8},{8,12},{1,5},{5,9},{9,13},{2,6},{6,10},{10,14},{3,7},{... | collective-permute-start | bytes 1179656 | tf_op jit(solution)/shard_map/ppermute | solution.py:16
  229.3 6.6 %collective-permute-done.2 = bf16[256,768]{1,0:T(8,128)(2,1)S(1)} collective-permute-done((bf16[256,768]{1,0:T(8,128)(2,1)}, bf16[256,768]{1,0:T(8,128)(2,1)S(1)}, u32[]{:S(2)}, u32[]{:S(2)}) %collective-permute-start.2) | collective-permute-done | bytes 393248 | tf_op jit(solution)/shard_map/ppermute | solution.py:16
  235.9 1.9 fusion.89
  237.9 1.8 pad_add_fusion.3.where_ref
  239.7 18.9 %all-gather.21.cloned.1.call-done = bf16[256,3072]{1,0:T(8,128)(2,1)} async-done(((bf16[256,768]{1,0:T(8,128)(2,1)}), bf16[256,3072]{1,0:T(8,128)(2,1)}) %all-gather.21.cloned.1.call-update) | async-done | bytes 1572880 | tf_op jit(solution)/shard_map/all_gather | solution.py:167
  258.6 1.8 convert_reduce_fusion
  260.4 2.0 fusion.16
  262.4 7.5 %fusion.mixed_ref = f32[256,1536]{1,0:T(8,128)} fusion(bf16[1,3072,1536]{2,1,0:T(8,128)(2,1)} %param.14, bf16[256,3072]{1,0:T(8,128)(2,1)S(1)} %copy-done.2, f32[256]{0:T(256)S(1)} %add_rsqrt_fusion, f32[256]{0:T(256)S(1)} %broadcast_multiply_fusion, f32[3072]{0:T(1024)S(1)} %bitcast.82, f32[3072]{0:T(1024)S(1)} %bitcast.78), kind=kOutput, calls=%fused_computation | convolution fusion | flops 2420637696 | bytes 12609536 | tf_op jit(solution)/shard_map/dot_general | solution.py:112
  269.9 6.7 %shard_map.94 = (bf16[256,512]{1,0:T(8,128)(2,1)}, bf16[4,768,128]{2,1,0:T(8,128)(2,1)}, bf16[4,768,128]{2,1,0:T(8,128)(2,1)}) custom-call(s32[2]{0:T(128)} %pad_add_fusion.3.where_ref, f32[256,1536]{1,0:T(8,128)} %fusion.mixed_ref, bf16[4,768,128]{2,1,0:T(8,128)(2,1)} %get-tuple-element.22.keys_ref, ...), custom_call_target="tpu_custom_call", output_to_operand_aliasing={{1}: (2, {}), {2}: (3, {})} | custom-call | tf_op jit(solution)/shard_map/pallas_call | solution.py:84
  276.6 16.9 %all-gather.23.cloned.1.call-done = bf16[256,2048]{1,0:T(8,128)(2,1)} async-done(((bf16[256,512]{1,0:T(8,128)(2,1)}), bf16[256,2048]{1,0:T(8,128)(2,1)}) %all-gather.23.cloned.1.call-update) | async-done | bytes 1048592 | tf_op jit(solution)/shard_map/all_gather | solution.py:149
  293.5 2.2 fusion.81
  295.7 2.6 maximum_bitcast_fusion
  (70 shorter events, 4.1 us)
Async XLA Ops:
  6.5 68.0 %copy-start = (bf16[1,2048,768]{2,1,0:T(8,128)(2,1)S(1)}, bf16[1,2048,768]{2,1,0:T(8,128)(2,1)}, u32[]{:S(2)}) copy-start(bf16[1,2048,768]{2,1,0:T(8,128)(2,1)} %param.15) | copy-start | bytes 9437188
  6.5 8.5 %copy-start.9 = (bf16[1,256,768]{2,1,0:T(8,128)(2,1)S(1)}, bf16[1,256,768]{2,1,0:T(8,128)(2,1)}, u32[]{:S(2)}) copy-start(bf16[1,256,768]{2,1,0:T(8,128)(2,1)} %param.10) | copy-start | bytes 1179652
  6.5 4.3 %copy-start.14 = (s32[4]{0:T(128)S(1)}, s32[4]{0:T(128)}, u32[]{:S(2)}) copy-start(s32[4]{0:T(128)} %param.11) | copy-start | bytes 52
  6.5 33.0 %all-gather.9.cloned.1.call-start = ((), (), s32[]{:S(2)}) async-start(), calls=%async_computation | async-start | bytes 1966080 | tf_op jit(solution)/shard_map/all_gather | solution.py:167
  12.6 4.6 %copy-start.15 = (pred[256]{0:T(512)(128)(4,1)}, pred[256]{0:T(512)(128)(4,1)S(1)}, u32[]{:S(2)}) copy-start(pred[256]{0:T(512)(128)(4,1)S(1)} %iota_compare_fusion.3) | copy-start | bytes 772
  17.1 57.4 %all-gather.11.cloned.1.call-start = ((), (), s32[]{:S(2)}) async-start(), calls=%async_computation.1 | async-start | bytes 1310720 | tf_op jit(solution)/shard_map/all_gather | solution.py:149
  19.9 23.5 %copy-start.10 = (f32[1,1,3072]{2,1,0:T(1,128)}, f32[1,1,3072]{2,1,0:T(1,128)S(1)}, u32[]{:S(2)}) copy-start(f32[1,1,3072]{2,1,0:T(1,128)S(1)} %get-tuple-element.35) | copy-start | bytes 36868
  39.6 3.8 %copy-start.1 = (bf16[256,3072]{1,0:T(8,128)(2,1)S(1)}, bf16[256,3072]{1,0:T(8,128)(2,1)}, u32[]{:S(2)}) copy-start(bf16[256,3072]{1,0:T(8,128)(2,1)} %all-gather.9.cloned.1.call-done) | copy-start | bytes 4718596
  50.9 23.6 %copy-start.6 = (bf16[256,768]{1,0:T(8,128)(2,1)S(1)}, bf16[256,768]{1,0:T(8,128)(2,1)}, u32[]{:S(2)}) copy-start(bf16[256,768]{1,0:T(8,128)(2,1)} %fusion.83) | copy-start | bytes 1179652
  57.6 55.0 %all-gather.13.cloned.1.call-start = ((), (), s32[]{:S(2)}) async-start(), calls=%async_computation.2 | async-start | bytes 1966080 | tf_op jit(solution)/shard_map/all_gather | solution.py:167
  77.5 12.5 %collective-permute-start = (bf16[256,768]{1,0:T(8,128)(2,1)}, bf16[256,768]{1,0:T(8,128)(2,1)S(1)}, u32[]{:S(2)}, u32[]{:S(2)}) collective-permute-start(bf16[256,768]{1,0:T(8,128)(2,1)} %fusion.78), channel_id=1, source_target_pairs={{0,4},{4,8},{8,12},{1,5},{5,9},{9,13},{2,6},{6,10},{10,14},{3,7},{... | collective-permute-start | bytes 1179656 | tf_op jit(solution)/shard_map/ppermute | solution.py:16
  83.2 6.7 %copy-start.18 = (pred[256]{0:T(512)(128)(4,1)}, pred[256]{0:T(512)(128)(4,1)S(1)}, u32[]{:S(2)}) copy-start(pred[256]{0:T(512)(128)(4,1)S(1)} %iota_compare_fusion.2) | copy-start | bytes 772
  91.9 24.5 %copy-start.11 = (f32[1,1,3072]{2,1,0:T(1,128)S(1)}, f32[1,1,3072]{2,1,0:T(1,128)}, u32[]{:S(2)}) copy-start(f32[1,1,3072]{2,1,0:T(1,128)} %copy-done.10) | copy-start | bytes 36868
  91.9 55.6 %all-gather.15.cloned.1.call-start = ((), (), s32[]{:S(2)}) async-start(), calls=%async_computation.3 | async-start | bytes 1310720 | tf_op jit(solution)/shard_map/all_gather | solution.py:149
  112.6 3.8 %copy-start.3 = (bf16[256,3072]{1,0:T(8,128)(2,1)S(1)}, bf16[256,3072]{1,0:T(8,128)(2,1)}, u32[]{:S(2)}) copy-start(bf16[256,3072]{1,0:T(8,128)(2,1)} %all-gather.13.cloned.1.call-done) | copy-start | bytes 4718596
  123.9 23.6 %copy-start.7 = (bf16[256,768]{1,0:T(8,128)(2,1)S(1)}, bf16[256,768]{1,0:T(8,128)(2,1)}, u32[]{:S(2)}) copy-start(bf16[256,768]{1,0:T(8,128)(2,1)} %fusion.85) | copy-start | bytes 1179652
  130.6 55.0 %all-gather.17.cloned.1.call-start = ((), (), s32[]{:S(2)}) async-start(), calls=%async_computation.4 | async-start | bytes 1966080 | tf_op jit(solution)/shard_map/all_gather | solution.py:167
  150.5 12.5 %collective-permute-start.1 = (bf16[256,768]{1,0:T(8,128)(2,1)}, bf16[256,768]{1,0:T(8,128)(2,1)S(1)}, u32[]{:S(2)}, u32[]{:S(2)}) collective-permute-start(bf16[256,768]{1,0:T(8,128)(2,1)} %select_convert_fusion.2), channel_id=1, source_target_pairs={{0,4},{4,8},{8,12},{1,5},{5,9},{9,13},{2,6},{6,10},{10,14},{3,7},{... | collective-permute-start | bytes 1179656 | tf_op jit(solution)/shard_map/ppermute | solution.py:16
  156.3 6.6 %copy-start.19 = (pred[256]{0:T(512)(128)(4,1)}, pred[256]{0:T(512)(128)(4,1)S(1)}, u32[]{:S(2)}) copy-start(pred[256]{0:T(512)(128)(4,1)S(1)} %iota_compare_fusion.1) | copy-start | bytes 772
  164.9 24.5 %copy-start.12 = (f32[1,1,3072]{2,1,0:T(1,128)S(1)}, f32[1,1,3072]{2,1,0:T(1,128)}, u32[]{:S(2)}) copy-start(f32[1,1,3072]{2,1,0:T(1,128)} %copy-done.10) | copy-start | bytes 36868
  164.9 55.6 %all-gather.19.cloned.1.call-start = ((), (), s32[]{:S(2)}) async-start(), calls=%async_computation.5 | async-start | bytes 1310720 | tf_op jit(solution)/shard_map/all_gather | solution.py:149
  185.6 3.8 %copy-start.4 = (bf16[256,3072]{1,0:T(8,128)(2,1)S(1)}, bf16[256,3072]{1,0:T(8,128)(2,1)}, u32[]{:S(2)}) copy-start(bf16[256,3072]{1,0:T(8,128)(2,1)} %all-gather.17.cloned.1.call-done) | copy-start | bytes 4718596
  196.9 23.6 %copy-start.8 = (bf16[256,768]{1,0:T(8,128)(2,1)S(1)}, bf16[256,768]{1,0:T(8,128)(2,1)}, u32[]{:S(2)}) copy-start(bf16[256,768]{1,0:T(8,128)(2,1)} %fusion.87) | copy-start | bytes 1179652
  203.6 54.9 %all-gather.21.cloned.1.call-start = ((), (), s32[]{:S(2)}) async-start(), calls=%async_computation.6 | async-start | bytes 1966080 | tf_op jit(solution)/shard_map/all_gather | solution.py:167
  223.5 12.5 %collective-permute-start.2 = (bf16[256,768]{1,0:T(8,128)(2,1)}, bf16[256,768]{1,0:T(8,128)(2,1)S(1)}, u32[]{:S(2)}, u32[]{:S(2)}) collective-permute-start(bf16[256,768]{1,0:T(8,128)(2,1)} %select_convert_fusion.1), channel_id=1, source_target_pairs={{0,4},{4,8},{8,12},{1,5},{5,9},{9,13},{2,6},{6,10},{10,14},{3,7},{... | collective-permute-start | bytes 1179656 | tf_op jit(solution)/shard_map/ppermute | solution.py:16
  229.3 6.6 %copy-start.16 = (pred[256]{0:T(512)(128)(4,1)}, pred[256]{0:T(512)(128)(4,1)S(1)}, u32[]{:S(2)}) copy-start(pred[256]{0:T(512)(128)(4,1)S(1)} %iota_compare_fusion) | copy-start | bytes 772
  237.8 24.6 %copy-start.13 = (f32[1,1,3072]{2,1,0:T(1,128)S(1)}, f32[1,1,3072]{2,1,0:T(1,128)}, u32[]{:S(2)}) copy-start(f32[1,1,3072]{2,1,0:T(1,128)} %copy-done.10) | copy-start | bytes 36868
  237.8 55.6 %all-gather.23.cloned.1.call-start = ((), (), s32[]{:S(2)}) async-start(), calls=%async_computation.7 | async-start | bytes 1310720 | tf_op jit(solution)/shard_map/all_gather | solution.py:149
  258.6 3.8 %copy-start.2 = (bf16[256,3072]{1,0:T(8,128)(2,1)S(1)}, bf16[256,3072]{1,0:T(8,128)(2,1)}, u32[]{:S(2)}) copy-start(bf16[256,3072]{1,0:T(8,128)(2,1)} %all-gather.21.cloned.1.call-done) | copy-start | bytes 4718596
  269.9 23.6 %copy-start.5 = (bf16[256,768]{1,0:T(8,128)(2,1)S(1)}, bf16[256,768]{1,0:T(8,128)(2,1)}, u32[]{:S(2)}) copy-start(bf16[256,768]{1,0:T(8,128)(2,1)} %fusion.89) | copy-start | bytes 1179652
  269.9 23.6 %copy-start.17 = (pred[256]{0:T(512)(128)(4,1)S(1)}, pred[256]{0:T(512)(128)(4,1)}, u32[]{:S(2)}) copy-start(pred[256]{0:T(512)(128)(4,1)} %copy-done.16) | copy-start | bytes 772
Sparse Core Ops, SparseCore 0:
  17.2 22.3 all-gather.8
  57.7 16.7 all-gather.10
  92.0 20.5 all-gather.12
  130.8 16.7 all-gather.14
  165.0 20.5 all-gather.16
  203.8 16.7 all-gather.18
  238.0 20.5 all-gather.20
  276.7 16.7 all-gather.22

commit v3 on v2

--- a/solution.py
+++ b/solution.py
@@ -25,6 +25,19 @@
 
 def rms_norm(values):
     return values * lax.rsqrt(jnp.mean(values * values, axis=-1, keepdims=True) + epsilon)
+
+
+def gather_columns(block):
+    count = lax.axis_size("seq")
+    here = lax.axis_index("seq")
+    arrived = [block] + [
+        lax.ppermute(block, "seq", [(source, (source + shift) % count) for source in range(count)])
+        for shift in range(1, count)
+    ]
+    slots = jnp.remainder(here - jnp.arange(count), count)
+    order = jnp.argsort(slots)
+    stacked = jnp.take(jnp.stack(arrived), order, axis=0)
+    return jnp.transpose(stacked, (1, 0, 2)).reshape(block.shape[0], count * block.shape[1])
 
 
 def pick_entry(vector, position):
@@ -146,7 +159,7 @@
     row_numbers = jnp.arange(biggest_patch_span)
 
     def gather_heads(head_rows):
-        every_head = lax.all_gather(head_rows, "seq", axis=1, tiled=True)
+        every_head = gather_columns(head_rows)
         return jnp.dot(every_head, out_weights, preferred_element_type=jnp.float32)
 
     results = []
@@ -164,7 +177,7 @@
         )
         own_rows = jnp.where(section_index == 0, entry_patch, earlier_result)
         own_rows = jnp.where(live_rows[:, None], own_rows, jnp.zeros_like(own_rows))
-        full_rows = lax.all_gather(own_rows, "seq", axis=1, tiled=True)
+        full_rows = gather_columns(own_rows)
         updated, key_cache, value_cache = run_block(
             full_rows,
             own_rows,

time: 307 us -> 345 us (1.12)
  local copies, waits for them, and re-layouts: 5.01 us -> 50.5 us
  waiting for transfers between devices: 163 us -> 122 us
  other arithmetic: 38.2 us -> 65.9 us
  starting transfers between devices: 10.7 us -> 27.5 us
  between operations: 20.9 us -> 8.03 us
    all_gather x8 -> x0, waiting for transfers between devices: 142 us -> none  [the longest x4 75.8 us: shards(): full_rows = lax.all_gather(own_rows, 'seq', axis=1, tiled=True)]
    ppermute x0 -> x24, waiting for transfers between devices: none -> 109 us  [gather_columns(): lax.ppermute(block, 'seq', [(source, (source + shift) % count) for source...]
    gather x0 -> x8, local copies, waits for them, and re-layouts: none -> 25.1 us  [gather_columns(): stacked = jnp.take(jnp.stack(arrived), order, axis=0)]
    another operation x1 -> x9, other arithmetic: 0.18 us -> 15.2 us  [the longest x8 15 us: gather_columns(): stacked = jnp.take(jnp.stack(arrived), order, axis=0)]
    ppermute x0 -> x24, starting transfers between devices: none -> 12.7 us  [gather_columns(): lax.ppermute(block, 'seq', [(source, (source + shift) % count) for source...]
    convert_element_type x0 -> x4, local copies, waits for them, and re-layouts: none -> 10.4 us  [run_block(): shaped = (layer_norm(full_rows.astype(jnp.float32)) * (1.0 + shift_scale[...]
    transpose x0 -> x4, other arithmetic: none -> 9.43 us  [gather_columns(): jnp.transpose(stacked, (1, 0, 2))]
    transpose x0 -> x4, local copies, waits for them, and re-layouts: none -> 9.1 us  [gather_columns(): jnp.transpose(stacked, (1, 0, 2))]
  transfers between devices with their start and end apart: 11 -> 27, of which waited for: 11 -> 25; matrix products, arithmetic and copies ran while one was open for 4% -> 5% of each run, Pallas kernels for 0% -> 0%
where the time goes in v3:
time: 345 us; the launch traced here: 343 us
  waiting for transfers between devices  122 us (35%)
  other arithmetic  65.9 us (19%)
  local copies, waits for them, and re-layouts  50.5 us (15%)
  matrix products  42.9 us (12%)
  starting transfers between devices  27.5 us (8%)
  Pallas kernels  26.2 us (8%)
  between operations  8.03 us (2%)
    ppermute x24, waiting for transfers between devices, gather_columns(): lax.ppermute(block, 'seq', [(source, (source + shift) % count) for source...  109 us
    dot_general x4, matrix products, run_block(): mixed = jnp.dot(shaped, qkv_weights, preferred_element_type=jnp.float32)  31.7 us
    pallas_call x4, Pallas kernels, attend(): pl.pallas_call(attention_kernel, grid_spec=grid_spec, out_shape=[jax.Shap...  26.2 us
    gather x8, local copies, waits for them, and re-layouts, gather_columns(): stacked = jnp.take(jnp.stack(arrived), order, axis=0)  25.1 us
    another operation x8, other arithmetic, gather_columns(): stacked = jnp.take(jnp.stack(arrived), order, axis=0)  15 us
    ppermute x3, starting transfers between devices, passed_along(): lax.ppermute(value, axis, [(source, source + steps) for source in range(l...  14.8 us
    ppermute x24, starting transfers between devices, gather_columns(): lax.ppermute(block, 'seq', [(source, (source + shift) % count) for source...  12.7 us
    ppermute x3, waiting for transfers between devices, passed_along(): lax.ppermute(value, axis, [(source, source + steps) for source in range(l...  12.4 us
  transfers between devices with their start and end apart: 27, of which 25 were waited for; matrix products, arithmetic and copies ran while one was open for 5% of the time, Pallas kernels for 0%

profile of v3, /device:TPU:0, one launch (start us, length us, event | category | flops | bytes accessed | tf_op | source)
XLA Modules:
  0.0 342.8 jit_solution(14660363918563334950)
XLA Ops:
  8.6 2.4 collective-permute-start.2
  20.4 9.5 %collective-permute-done.1 = bf16[256,768]{1,0:T(8,128)(2,1)} collective-permute-done((bf16[256,768]{1,0:T(8,128)(2,1)S(1)}, bf16[256,768]{1,0:T(8,128)(2,1)}, u32[]{:S(2)}, u32[]{:S(2)}) %collective-permute-start.1) | collective-permute-done | bytes 393248 | tf_op jit(solution)/shard_map/ppermute | solution.py:34
  29.9 2.6 pad_maximum_fusion
  32.5 3.3 gather_fusion
  40.5 2.6 copy.19
  43.1 7.9 %fusion.6.mixed_ref = f32[256,1536]{1,0:T(8,128)} fusion(bf16[256,3072]{0,1:T(8,128)(2,1)} %bitcast.133, bf16[1,3072,1536]{2,1,0:T(8,128)(2,1)} %param.18), kind=kOutput, calls=%fused_computation.14 | convolution fusion | flops 2415919104 | bytes 12582912 | tf_op jit(solution)/shard_map/dot_general | solution.py:125
  51.0 6.6 %shard_map.91 = (bf16[256,512]{1,0:T(8,128)(2,1)}, bf16[4,768,128]{2,1,0:T(8,128)(2,1)}, bf16[4,768,128]{2,1,0:T(8,128)(2,1)}) custom-call(s32[2]{0:T(128)} %pad_add_fusion.where_ref, f32[256,1536]{1,0:T(8,128)} %fusion.6.mixed_ref, bf16[4,768,128]{2,1,0:T(8,128)(2,1)} %bitcast.131, ...), custom_call_target="tpu_custom_call", output_to_operand_aliasing={{1}: (2, {}), {2}: (3, {})} | custom-call | tf_op jit(solution)/shard_map/pallas_call | solution.py:97
  60.7 2.7 collective-permute-done.5
  63.4 8.8 %collective-permute-done.4 = bf16[256,512]{1,0:T(8,128)(2,1)} collective-permute-done((bf16[256,512]{1,0:T(8,128)(2,1)}, bf16[256,512]{1,0:T(8,128)(2,1)}, u32[]{:S(2)}, u32[]{:S(2)}) %collective-permute-start.4) | collective-permute-done | bytes 262176 | tf_op jit(solution)/shard_map/ppermute | solution.py:34
  74.5 2.9 gather_fusion.1
  77.5 2.4 select_bitcast_fusion.3
  82.1 3.0 fusion.62
  85.1 4.3 %collective-permute-start.6 = (bf16[256,768]{1,0:T(8,128)(2,1)}, bf16[256,768]{1,0:T(8,128)(2,1)}, u32[]{:S(2)}, u32[]{:S(2)}) collective-permute-start(bf16[256,768]{1,0:T(8,128)(2,1)} %fusion.62), channel_id=1, source_target_pairs={{0,4},{4,8},{8,12},{1,5},{5,9},{9,13},{2,6},{6,10},{10,14},{3,7},{... | collective-permute-start | bytes 1179656 | tf_op jit(solution)/shard_map/ppermute | solution.py:16
  91.8 3.9 %collective-permute-done.6 = bf16[256,768]{1,0:T(8,128)(2,1)} collective-permute-done((bf16[256,768]{1,0:T(8,128)(2,1)}, bf16[256,768]{1,0:T(8,128)(2,1)}, u32[]{:S(2)}, u32[]{:S(2)}) %collective-permute-start.6) | collective-permute-done | bytes 393248 | tf_op jit(solution)/shard_map/ppermute | solution.py:16
  100.5 4.9 %collective-permute-done.9 = bf16[256,768]{1,0:T(8,128)(2,1)S(1)} collective-permute-done((bf16[256,768]{1,0:T(8,128)(2,1)S(1)}, bf16[256,768]{1,0:T(8,128)(2,1)S(1)}, u32[]{:S(2)}, u32[]{:S(2)}) %collective-permute-start.9) | collective-permute-done | bytes 393248 | tf_op jit(solution)/shard_map/ppermute | solution.py:34
  105.4 11.3 %collective-permute-done.8 = bf16[256,768]{1,0:T(8,128)(2,1)S(1)} collective-permute-done((bf16[256,768]{1,0:T(8,128)(2,1)S(1)}, bf16[256,768]{1,0:T(8,128)(2,1)S(1)}, u32[]{:S(2)}, u32[]{:S(2)}) %collective-permute-start.8) | collective-permute-done | bytes 393248 | tf_op jit(solution)/shard_map/ppermute | solution.py:34
  118.2 3.3 gather_fusion.2
  126.2 2.6 copy.21
  128.8 7.9 %fusion.4.mixed_ref = f32[256,1536]{1,0:T(8,128)} fusion(bf16[256,3072]{0,1:T(8,128)(2,1)} %bitcast.134, bf16[1,3072,1536]{2,1,0:T(8,128)(2,1)} %param.18), kind=kOutput, calls=%fused_computation.12 | convolution fusion | flops 2415919104 | bytes 12582912 | tf_op jit(solution)/shard_map/dot_general | solution.py:125
  136.7 6.6 %shard_map.92 = (bf16[256,512]{1,0:T(8,128)(2,1)}, bf16[4,768,128]{2,1,0:T(8,128)(2,1)}, bf16[4,768,128]{2,1,0:T(8,128)(2,1)}) custom-call(s32[2]{0:T(128)} %pad_add_fusion.1.where_ref, f32[256,1536]{1,0:T(8,128)} %fusion.4.mixed_ref, bf16[4,768,128]{2,1,0:T(8,128)(2,1)} %get-tuple-element.20.keys_ref, ...), custom_call_target="tpu_custom_call", output_to_operand_aliasing={{1}: (2, {}), {2}: (3, {})} | custom-call | tf_op jit(solution)/shard_map/pallas_call | solution.py:97
  144.0 6.2 %collective-permute-done.12 = bf16[256,512]{1,0:T(8,128)(2,1)S(1)} collective-permute-done((bf16[256,512]{1,0:T(8,128)(2,1)}, bf16[256,512]{1,0:T(8,128)(2,1)S(1)}, u32[]{:S(2)}, u32[]{:S(2)}) %collective-permute-start.12) | collective-permute-done | bytes 262176 | tf_op jit(solution)/shard_map/ppermute | solution.py:34
  150.2 5.6 %collective-permute-done.11 = bf16[256,512]{1,0:T(8,128)(2,1)S(1)} collective-permute-done((bf16[256,512]{1,0:T(8,128)(2,1)}, bf16[256,512]{1,0:T(8,128)(2,1)S(1)}, u32[]{:S(2)}, u32[]{:S(2)}) %collective-permute-start.11) | collective-permute-done | bytes 262176 | tf_op jit(solution)/shard_map/ppermute | solution.py:34
  158.8 2.9 gather_fusion.3
  166.4 3.0 select_convert_fusion.2
  169.4 5.2 %collective-permute-start.13 = (bf16[256,768]{1,0:T(8,128)(2,1)}, bf16[256,768]{1,0:T(8,128)(2,1)}, u32[]{:S(2)}, u32[]{:S(2)}) collective-permute-start(bf16[256,768]{1,0:T(8,128)(2,1)} %select_convert_fusion.2), channel_id=1, source_target_pairs={{0,4},{4,8},{8,12},{1,5},{5,9},{9,13},{2,6},{6,10},{10,14},{3,7},{... | collective-permute-start | bytes 1179656 | tf_op jit(solution)/shard_map/ppermute | solution.py:16
  177.2 4.8 %collective-permute-done.13 = bf16[256,768]{1,0:T(8,128)(2,1)} collective-permute-done((bf16[256,768]{1,0:T(8,128)(2,1)}, bf16[256,768]{1,0:T(8,128)(2,1)}, u32[]{:S(2)}, u32[]{:S(2)}) %collective-permute-start.13) | collective-permute-done | bytes 393248 | tf_op jit(solution)/shard_map/ppermute | solution.py:16
  185.9 6.8 %collective-permute-done.16 = bf16[256,768]{1,0:T(8,128)(2,1)S(1)} collective-permute-done((bf16[256,768]{1,0:T(8,128)(2,1)S(1)}, bf16[256,768]{1,0:T(8,128)(2,1)S(1)}, u32[]{:S(2)}, u32[]{:S(2)}) %collective-permute-start.16) | collective-permute-done | bytes 393248 | tf_op jit(solution)/shard_map/ppermute | solution.py:34
  192.7 8.4 %collective-permute-done.15 = bf16[256,768]{1,0:T(8,128)(2,1)S(1)} collective-permute-done((bf16[256,768]{1,0:T(8,128)(2,1)S(1)}, bf16[256,768]{1,0:T(8,128)(2,1)S(1)}, u32[]{:S(2)}, u32[]{:S(2)}) %collective-permute-start.15) | collective-permute-done | bytes 393248 | tf_op jit(solution)/shard_map/ppermute | solution.py:34
  203.5 3.3 gather_fusion.4
  211.5 2.6 copy.23
  214.1 7.9 %fusion.2.mixed_ref = f32[256,1536]{1,0:T(8,128)} fusion(bf16[256,3072]{0,1:T(8,128)(2,1)} %bitcast.135, bf16[1,3072,1536]{2,1,0:T(8,128)(2,1)} %param.18), kind=kOutput, calls=%fused_computation.10 | convolution fusion | flops 2415919104 | bytes 12582912 | tf_op jit(solution)/shard_map/dot_general | solution.py:125
  222.0 6.6 %shard_map.93 = (bf16[256,512]{1,0:T(8,128)(2,1)}, bf16[4,768,128]{2,1,0:T(8,128)(2,1)}, bf16[4,768,128]{2,1,0:T(8,128)(2,1)}) custom-call(s32[2]{0:T(128)} %pad_add_fusion.2.where_ref, f32[256,1536]{1,0:T(8,128)} %fusion.2.mixed_ref, bf16[4,768,128]{2,1,0:T(8,128)(2,1)} %get-tuple-element.23.keys_ref, ...), custom_call_target="tpu_custom_call", output_to_operand_aliasing={{1}: (2, {}), {2}: (3, {})} | custom-call | tf_op jit(solution)/shard_map/pallas_call | solution.py:97
  230.3 4.3 %collective-permute-done.19 = bf16[256,512]{1,0:T(8,128)(2,1)S(1)} collective-permute-done((bf16[256,512]{1,0:T(8,128)(2,1)}, bf16[256,512]{1,0:T(8,128)(2,1)S(1)}, u32[]{:S(2)}, u32[]{:S(2)}) %collective-permute-start.19) | collective-permute-done | bytes 262176 | tf_op jit(solution)/shard_map/ppermute | solution.py:34
  234.6 8.4 %collective-permute-done.18 = bf16[256,512]{1,0:T(8,128)(2,1)S(1)} collective-permute-done((bf16[256,512]{1,0:T(8,128)(2,1)}, bf16[256,512]{1,0:T(8,128)(2,1)S(1)}, u32[]{:S(2)}, u32[]{:S(2)}) %collective-permute-start.18) | collective-permute-done | bytes 262176 | tf_op jit(solution)/shard_map/ppermute | solution.py:34
  245.1 2.9 gather_fusion.5
  252.7 3.0 select_convert_fusion.1
  255.7 5.2 %collective-permute-start.20 = (bf16[256,768]{1,0:T(8,128)(2,1)}, bf16[256,768]{1,0:T(8,128)(2,1)}, u32[]{:S(2)}, u32[]{:S(2)}) collective-permute-start(bf16[256,768]{1,0:T(8,128)(2,1)} %select_convert_fusion.1), channel_id=1, source_target_pairs={{0,4},{4,8},{8,12},{1,5},{5,9},{9,13},{2,6},{6,10},{10,14},{3,7},{... | collective-permute-start | bytes 1179656 | tf_op jit(solution)/shard_map/ppermute | solution.py:16
  263.6 3.7 %collective-permute-done.20 = bf16[256,768]{1,0:T(8,128)(2,1)} collective-permute-done((bf16[256,768]{1,0:T(8,128)(2,1)}, bf16[256,768]{1,0:T(8,128)(2,1)}, u32[]{:S(2)}, u32[]{:S(2)}) %collective-permute-start.20) | collective-permute-done | bytes 393248 | tf_op jit(solution)/shard_map/ppermute | solution.py:16
  272.2 4.8 %collective-permute-done.23 = bf16[256,768]{1,0:T(8,128)(2,1)S(1)} collective-permute-done((bf16[256,768]{1,0:T(8,128)(2,1)S(1)}, bf16[256,768]{1,0:T(8,128)(2,1)S(1)}, u32[]{:S(2)}, u32[]{:S(2)}) %collective-permute-start.23) | collective-permute-done | bytes 393248 | tf_op jit(solution)/shard_map/ppermute | solution.py:34
  277.0 11.4 %collective-permute-done.22 = bf16[256,768]{1,0:T(8,128)(2,1)S(1)} collective-permute-done((bf16[256,768]{1,0:T(8,128)(2,1)S(1)}, bf16[256,768]{1,0:T(8,128)(2,1)S(1)}, u32[]{:S(2)}, u32[]{:S(2)}) %collective-permute-start.22) | collective-permute-done | bytes 393248 | tf_op jit(solution)/shard_map/ppermute | solution.py:34
  289.8 3.3 gather_fusion.6
  297.8 2.6 copy.25
  300.4 7.9 %fusion.mixed_ref = f32[256,1536]{1,0:T(8,128)} fusion(bf16[256,3072]{0,1:T(8,128)(2,1)} %bitcast.136, bf16[1,3072,1536]{2,1,0:T(8,128)(2,1)} %param.18), kind=kOutput, calls=%fused_computation.8 | convolution fusion | flops 2415919104 | bytes 12582912 | tf_op jit(solution)/shard_map/dot_general | solution.py:125
  308.3 6.6 %shard_map.94 = (bf16[256,512]{1,0:T(8,128)(2,1)}, bf16[4,768,128]{2,1,0:T(8,128)(2,1)}, bf16[4,768,128]{2,1,0:T(8,128)(2,1)}) custom-call(s32[2]{0:T(128)} %pad_add_fusion.3.where_ref, f32[256,1536]{1,0:T(8,128)} %fusion.mixed_ref, bf16[4,768,128]{2,1,0:T(8,128)(2,1)} %get-tuple-element.26.keys_ref, ...), custom_call_target="tpu_custom_call", output_to_operand_aliasing={{1}: (2, {}), {2}: (3, {})} | custom-call | tf_op jit(solution)/shard_map/pallas_call | solution.py:97
  315.6 6.2 %collective-permute-done.26 = bf16[256,512]{1,0:T(8,128)(2,1)S(1)} collective-permute-done((bf16[256,512]{1,0:T(8,128)(2,1)}, bf16[256,512]{1,0:T(8,128)(2,1)S(1)}, u32[]{:S(2)}, u32[]{:S(2)}) %collective-permute-start.26) | collective-permute-done | bytes 262176 | tf_op jit(solution)/shard_map/ppermute | solution.py:34
  321.8 5.6 %collective-permute-done.25 = bf16[256,512]{1,0:T(8,128)(2,1)S(1)} collective-permute-done((bf16[256,512]{1,0:T(8,128)(2,1)}, bf16[256,512]{1,0:T(8,128)(2,1)S(1)}, u32[]{:S(2)}, u32[]{:S(2)}) %collective-permute-start.25) | collective-permute-done | bytes 262176 | tf_op jit(solution)/shard_map/ppermute | solution.py:34
  330.4 2.9 gather_fusion.7
  340.3 2.6 maximum_bitcast_fusion
  (129 shorter events, 90.4 us)
Async XLA Ops:
  0.0 82.1 %copy-start = (bf16[1,2048,768]{2,1,0:T(8,128)(2,1)S(1)}, bf16[1,2048,768]{2,1,0:T(8,128)(2,1)}, u32[]{:S(2)}) copy-start(bf16[1,2048,768]{2,1,0:T(8,128)(2,1)} %param.19) | copy-start | bytes 9437188
  0.0 3.2 copy-start.11
  0.0 2.3 copy-start.5
  4.7 9.4 %copy-start.12 = (pred[256]{0:T(512)(128)(4,1)}, pred[256]{0:T(512)(128)(4,1)S(1)}, u32[]{:S(2)}) copy-start(pred[256]{0:T(512)(128)(4,1)S(1)} %iota_compare_fusion.3) | copy-start | bytes 772
  8.6 11.8 %collective-permute-start.2 = (bf16[256,768]{1,0:T(8,128)(2,1)S(1)}, bf16[256,768]{1,0:T(8,128)(2,1)}, u32[]{:S(2)}, u32[]{:S(2)}) collective-permute-start(bf16[256,768]{1,0:T(8,128)(2,1)S(1)} %fusion.67), channel_id=1, source_target_pairs={{0,3},{1,0},{2,1},{3,2},{4,7},{5,4},{6,5},{7,6},{8,11},{9,8},{10,9... | collective-permute-start | bytes 1179656 | tf_op jit(solution)/shard_map/ppermute | solution.py:34
  11.1 18.9 %collective-permute-start.1 = (bf16[256,768]{1,0:T(8,128)(2,1)S(1)}, bf16[256,768]{1,0:T(8,128)(2,1)}, u32[]{:S(2)}, u32[]{:S(2)}) collective-permute-start(bf16[256,768]{1,0:T(8,128)(2,1)S(1)} %fusion.67), channel_id=1, source_target_pairs={{0,2},{1,3},{2,0},{3,1},{4,6},{5,7},{6,4},{7,5},{8,10},{9,11},{10,... | collective-permute-start | bytes 1179656 | tf_op jit(solution)/shard_map/ppermute | solution.py:34
  11.7 18.2 %collective-permute-start = (bf16[256,768]{1,0:T(8,128)(2,1)S(1)}, bf16[256,768]{1,0:T(8,128)(2,1)}, u32[]{:S(2)}, u32[]{:S(2)}) collective-permute-start(bf16[256,768]{1,0:T(8,128)(2,1)S(1)} %fusion.67), channel_id=1, source_target_pairs={{0,1},{1,2},{2,3},{3,0},{4,5},{5,6},{6,7},{7,4},{8,9},{9,10},{10,1... | collective-permute-start | bytes 1179656 | tf_op jit(solution)/shard_map/ppermute | solution.py:34
  12.6 1.5 copy-start.17
  35.8 2.0 copy-start.2
  35.8 2.7 copy-start.6
  57.6 5.8 %collective-permute-start.5 = (bf16[256,512]{1,0:T(8,128)(2,1)}, bf16[256,512]{1,0:T(8,128)(2,1)}, u32[]{:S(2)}, u32[]{:S(2)}) collective-permute-start(bf16[256,512]{1,0:T(8,128)(2,1)} %get-tuple-element.19), channel_id=1, source_target_pairs={{0,3},{1,0},{2,1},{3,2},{4,7},{5,4},{6,5},{7,6},{8,11},{9,8},{10,9... | collective-permute-start | bytes 786440 | tf_op jit(solution)/shard_map/ppermute | solution.py:34
  57.6 14.7 %collective-permute-start.4 = (bf16[256,512]{1,0:T(8,128)(2,1)}, bf16[256,512]{1,0:T(8,128)(2,1)}, u32[]{:S(2)}, u32[]{:S(2)}) collective-permute-start(bf16[256,512]{1,0:T(8,128)(2,1)} %get-tuple-element.19), channel_id=1, source_target_pairs={{0,2},{1,3},{2,0},{3,1},{4,6},{5,7},{6,4},{7,5},{8,10},{9,11},{10,... | collective-permute-start | bytes 786440 | tf_op jit(solution)/shard_map/ppermute | solution.py:34
  59.3 13.0 %collective-permute-start.3 = (bf16[256,512]{1,0:T(8,128)(2,1)}, bf16[256,512]{1,0:T(8,128)(2,1)}, u32[]{:S(2)}, u32[]{:S(2)}) collective-permute-start(bf16[256,512]{1,0:T(8,128)(2,1)} %get-tuple-element.19), channel_id=1, source_target_pairs={{0,1},{1,2},{2,3},{3,0},{4,5},{5,6},{6,7},{7,4},{8,9},{9,10},{10,1... | collective-permute-start | bytes 786440 | tf_op jit(solution)/shard_map/ppermute | solution.py:34
  85.1 10.6 %collective-permute-start.6 = (bf16[256,768]{1,0:T(8,128)(2,1)}, bf16[256,768]{1,0:T(8,128)(2,1)}, u32[]{:S(2)}, u32[]{:S(2)}) collective-permute-start(bf16[256,768]{1,0:T(8,128)(2,1)} %fusion.62), channel_id=1, source_target_pairs={{0,4},{4,8},{8,12},{1,5},{5,9},{9,13},{2,6},{6,10},{10,14},{3,7},{... | collective-permute-start | bytes 1179656 | tf_op jit(solution)/shard_map/ppermute | solution.py:16
  91.8 25.0 %copy-start.15 = (pred[256]{0:T(512)(128)(4,1)}, pred[256]{0:T(512)(128)(4,1)S(1)}, u32[]{:S(2)}) copy-start(pred[256]{0:T(512)(128)(4,1)S(1)} %iota_compare_fusion.2) | copy-start | bytes 772
  96.9 8.5 %collective-permute-start.9 = (bf16[256,768]{1,0:T(8,128)(2,1)S(1)}, bf16[256,768]{1,0:T(8,128)(2,1)S(1)}, u32[]{:S(2)}, u32[]{:S(2)}) collective-permute-start(bf16[256,768]{1,0:T(8,128)(2,1)S(1)} %fusion.69), channel_id=1, source_target_pairs={{0,3},{1,0},{2,1},{3,2},{4,7},{5,4},{6,5},{7,6},{8,11},{9,8},{10,9... | collective-permute-start | bytes 1179656 | tf_op jit(solution)/shard_map/ppermute | solution.py:34
  97.0 19.8 %collective-permute-start.8 = (bf16[256,768]{1,0:T(8,128)(2,1)S(1)}, bf16[256,768]{1,0:T(8,128)(2,1)S(1)}, u32[]{:S(2)}, u32[]{:S(2)}) collective-permute-start(bf16[256,768]{1,0:T(8,128)(2,1)S(1)} %fusion.69), channel_id=1, source_target_pairs={{0,2},{1,3},{2,0},{3,1},{4,6},{5,7},{6,4},{7,5},{8,10},{9,11},{10,... | collective-permute-start | bytes 1179656 | tf_op jit(solution)/shard_map/ppermute | solution.py:34
  98.5 18.3 %collective-permute-start.7 = (bf16[256,768]{1,0:T(8,128)(2,1)S(1)}, bf16[256,768]{1,0:T(8,128)(2,1)S(1)}, u32[]{:S(2)}, u32[]{:S(2)}) collective-permute-start(bf16[256,768]{1,0:T(8,128)(2,1)S(1)} %fusion.69), channel_id=1, source_target_pairs={{0,1},{1,2},{2,3},{3,0},{4,5},{5,6},{6,7},{7,4},{8,9},{9,10},{10,1... | collective-permute-start | bytes 1179656 | tf_op jit(solution)/shard_map/ppermute | solution.py:34
  121.5 2.0 copy-start.3
  121.5 2.7 copy-start.7
  143.2 6.9 %collective-permute-start.12 = (bf16[256,512]{1,0:T(8,128)(2,1)}, bf16[256,512]{1,0:T(8,128)(2,1)S(1)}, u32[]{:S(2)}, u32[]{:S(2)}) collective-permute-start(bf16[256,512]{1,0:T(8,128)(2,1)} %get-tuple-element.22), channel_id=1, source_target_pairs={{0,3},{1,0},{2,1},{3,2},{4,7},{5,4},{6,5},{7,6},{8,11},{9,8},{10,9... | collective-permute-start | bytes 786440 | tf_op jit(solution)/shard_map/ppermute | solution.py:34
  143.2 12.5 %collective-permute-start.11 = (bf16[256,512]{1,0:T(8,128)(2,1)}, bf16[256,512]{1,0:T(8,128)(2,1)S(1)}, u32[]{:S(2)}, u32[]{:S(2)}) collective-permute-start(bf16[256,512]{1,0:T(8,128)(2,1)} %get-tuple-element.22), channel_id=1, source_target_pairs={{0,2},{1,3},{2,0},{3,1},{4,6},{5,7},{6,4},{7,5},{8,10},{9,11},{10,... | collective-permute-start | bytes 786440 | tf_op jit(solution)/shard_map/ppermute | solution.py:34
  143.9 12.9 %collective-permute-start.10 = (bf16[256,512]{1,0:T(8,128)(2,1)}, bf16[256,512]{1,0:T(8,128)(2,1)S(1)}, u32[]{:S(2)}, u32[]{:S(2)}) collective-permute-start(bf16[256,512]{1,0:T(8,128)(2,1)} %get-tuple-element.22), channel_id=1, source_target_pairs={{0,1},{1,2},{2,3},{3,0},{4,5},{5,6},{6,7},{7,4},{8,9},{9,10},{10,1... | collective-permute-start | bytes 786440 | tf_op jit(solution)/shard_map/ppermute | solution.py:34
  169.4 12.6 %collective-permute-start.13 = (bf16[256,768]{1,0:T(8,128)(2,1)}, bf16[256,768]{1,0:T(8,128)(2,1)}, u32[]{:S(2)}, u32[]{:S(2)}) collective-permute-start(bf16[256,768]{1,0:T(8,128)(2,1)} %select_convert_fusion.2), channel_id=1, source_target_pairs={{0,4},{4,8},{8,12},{1,5},{5,9},{9,13},{2,6},{6,10},{10,14},{3,7},{... | collective-permute-start | bytes 1179656 | tf_op jit(solution)/shard_map/ppermute | solution.py:16
  177.2 25.0 %copy-start.16 = (pred[256]{0:T(512)(128)(4,1)}, pred[256]{0:T(512)(128)(4,1)S(1)}, u32[]{:S(2)}) copy-start(pred[256]{0:T(512)(128)(4,1)S(1)} %iota_compare_fusion.1) | copy-start | bytes 772
  183.2 9.5 %collective-permute-start.16 = (bf16[256,768]{1,0:T(8,128)(2,1)S(1)}, bf16[256,768]{1,0:T(8,128)(2,1)S(1)}, u32[]{:S(2)}, u32[]{:S(2)}) collective-permute-start(bf16[256,768]{1,0:T(8,128)(2,1)S(1)} %fusion.71), channel_id=1, source_target_pairs={{0,3},{1,0},{2,1},{3,2},{4,7},{5,4},{6,5},{7,6},{8,11},{9,8},{10,9... | collective-permute-start | bytes 1179656 | tf_op jit(solution)/shard_map/ppermute | solution.py:34
  183.3 17.9 %collective-permute-start.15 = (bf16[256,768]{1,0:T(8,128)(2,1)S(1)}, bf16[256,768]{1,0:T(8,128)(2,1)S(1)}, u32[]{:S(2)}, u32[]{:S(2)}) collective-permute-start(bf16[256,768]{1,0:T(8,128)(2,1)S(1)} %fusion.71), channel_id=1, source_target_pairs={{0,2},{1,3},{2,0},{3,1},{4,6},{5,7},{6,4},{7,5},{8,10},{9,11},{10,... | collective-permute-start | bytes 1179656 | tf_op jit(solution)/shard_map/ppermute | solution.py:34
  183.8 18.3 %collective-permute-start.14 = (bf16[256,768]{1,0:T(8,128)(2,1)S(1)}, bf16[256,768]{1,0:T(8,128)(2,1)S(1)}, u32[]{:S(2)}, u32[]{:S(2)}) collective-permute-start(bf16[256,768]{1,0:T(8,128)(2,1)S(1)} %fusion.71), channel_id=1, source_target_pairs={{0,1},{1,2},{2,3},{3,0},{4,5},{5,6},{6,7},{7,4},{8,9},{9,10},{10,1... | collective-permute-start | bytes 1179656 | tf_op jit(solution)/shard_map/ppermute | solution.py:34
  206.8 2.0 copy-start.4
  206.8 2.7 copy-start.8
  228.6 6.0 %collective-permute-start.19 = (bf16[256,512]{1,0:T(8,128)(2,1)}, bf16[256,512]{1,0:T(8,128)(2,1)S(1)}, u32[]{:S(2)}, u32[]{:S(2)}) collective-permute-start(bf16[256,512]{1,0:T(8,128)(2,1)} %get-tuple-element.25), channel_id=1, source_target_pairs={{0,3},{1,0},{2,1},{3,2},{4,7},{5,4},{6,5},{7,6},{8,11},{9,8},{10,9... | collective-permute-start | bytes 786440 | tf_op jit(solution)/shard_map/ppermute | solution.py:34
  228.6 14.4 %collective-permute-start.18 = (bf16[256,512]{1,0:T(8,128)(2,1)}, bf16[256,512]{1,0:T(8,128)(2,1)S(1)}, u32[]{:S(2)}, u32[]{:S(2)}) collective-permute-start(bf16[256,512]{1,0:T(8,128)(2,1)} %get-tuple-element.25), channel_id=1, source_target_pairs={{0,2},{1,3},{2,0},{3,1},{4,6},{5,7},{6,4},{7,5},{8,10},{9,11},{10,... | collective-permute-start | bytes 786440 | tf_op jit(solution)/shard_map/ppermute | solution.py:34
  230.1 12.9 %collective-permute-start.17 = (bf16[256,512]{1,0:T(8,128)(2,1)}, bf16[256,512]{1,0:T(8,128)(2,1)S(1)}, u32[]{:S(2)}, u32[]{:S(2)}) collective-permute-start(bf16[256,512]{1,0:T(8,128)(2,1)} %get-tuple-element.25), channel_id=1, source_target_pairs={{0,1},{1,2},{2,3},{3,0},{4,5},{5,6},{6,7},{7,4},{8,9},{9,10},{10,1... | collective-permute-start | bytes 786440 | tf_op jit(solution)/shard_map/ppermute | solution.py:34
  255.7 11.6 %collective-permute-start.20 = (bf16[256,768]{1,0:T(8,128)(2,1)}, bf16[256,768]{1,0:T(8,128)(2,1)}, u32[]{:S(2)}, u32[]{:S(2)}) collective-permute-start(bf16[256,768]{1,0:T(8,128)(2,1)} %select_convert_fusion.1), channel_id=1, source_target_pairs={{0,4},{4,8},{8,12},{1,5},{5,9},{9,13},{2,6},{6,10},{10,14},{3,7},{... | collective-permute-start | bytes 1179656 | tf_op jit(solution)/shard_map/ppermute | solution.py:16
  263.6 24.9 %copy-start.13 = (pred[256]{0:T(512)(128)(4,1)}, pred[256]{0:T(512)(128)(4,1)S(1)}, u32[]{:S(2)}) copy-start(pred[256]{0:T(512)(128)(4,1)S(1)} %iota_compare_fusion) | copy-start | bytes 772
  268.5 8.5 %collective-permute-start.23 = (bf16[256,768]{1,0:T(8,128)(2,1)S(1)}, bf16[256,768]{1,0:T(8,128)(2,1)S(1)}, u32[]{:S(2)}, u32[]{:S(2)}) collective-permute-start(bf16[256,768]{1,0:T(8,128)(2,1)S(1)} %fusion.73), channel_id=1, source_target_pairs={{0,3},{1,0},{2,1},{3,2},{4,7},{5,4},{6,5},{7,6},{8,11},{9,8},{10,9... | collective-permute-start | bytes 1179656 | tf_op jit(solution)/shard_map/ppermute | solution.py:34
  268.6 19.8 %collective-permute-start.22 = (bf16[256,768]{1,0:T(8,128)(2,1)S(1)}, bf16[256,768]{1,0:T(8,128)(2,1)S(1)}, u32[]{:S(2)}, u32[]{:S(2)}) collective-permute-start(bf16[256,768]{1,0:T(8,128)(2,1)S(1)} %fusion.73), channel_id=1, source_target_pairs={{0,2},{1,3},{2,0},{3,1},{4,6},{5,7},{6,4},{7,5},{8,10},{9,11},{10,... | collective-permute-start | bytes 1179656 | tf_op jit(solution)/shard_map/ppermute | solution.py:34
  270.1 18.3 %collective-permute-start.21 = (bf16[256,768]{1,0:T(8,128)(2,1)S(1)}, bf16[256,768]{1,0:T(8,128)(2,1)S(1)}, u32[]{:S(2)}, u32[]{:S(2)}) collective-permute-start(bf16[256,768]{1,0:T(8,128)(2,1)S(1)} %fusion.73), channel_id=1, source_target_pairs={{0,1},{1,2},{2,3},{3,0},{4,5},{5,6},{6,7},{7,4},{8,9},{9,10},{10,1... | collective-permute-start | bytes 1179656 | tf_op jit(solution)/shard_map/ppermute | solution.py:34
  293.1 2.0 copy-start.1
  293.1 2.7 copy-start.9
  314.9 7.0 %collective-permute-start.26 = (bf16[256,512]{1,0:T(8,128)(2,1)}, bf16[256,512]{1,0:T(8,128)(2,1)S(1)}, u32[]{:S(2)}, u32[]{:S(2)}) collective-permute-start(bf16[256,512]{1,0:T(8,128)(2,1)} %get-tuple-element.28), channel_id=1, source_target_pairs={{0,3},{1,0},{2,1},{3,2},{4,7},{5,4},{6,5},{7,6},{8,11},{9,8},{10,9... | collective-permute-start | bytes 786440 | tf_op jit(solution)/shard_map/ppermute | solution.py:34
  314.9 12.6 %collective-permute-start.25 = (bf16[256,512]{1,0:T(8,128)(2,1)}, bf16[256,512]{1,0:T(8,128)(2,1)S(1)}, u32[]{:S(2)}, u32[]{:S(2)}) collective-permute-start(bf16[256,512]{1,0:T(8,128)(2,1)} %get-tuple-element.28), channel_id=1, source_target_pairs={{0,2},{1,3},{2,0},{3,1},{4,6},{5,7},{6,4},{7,5},{8,10},{9,11},{10,... | collective-permute-start | bytes 786440 | tf_op jit(solution)/shard_map/ppermute | solution.py:34
  315.5 12.9 %collective-permute-start.24 = (bf16[256,512]{1,0:T(8,128)(2,1)}, bf16[256,512]{1,0:T(8,128)(2,1)S(1)}, u32[]{:S(2)}, u32[]{:S(2)}) collective-permute-start(bf16[256,512]{1,0:T(8,128)(2,1)} %get-tuple-element.28), channel_id=1, source_target_pairs={{0,1},{1,2},{2,3},{3,0},{4,5},{5,6},{6,7},{7,4},{8,9},{9,10},{10,1... | collective-permute-start | bytes 786440 | tf_op jit(solution)/shard_map/ppermute | solution.py:34
  335.7 2.3 copy-start.10
  335.7 2.3 copy-start.14

commit v4 on v2

v4 whole, which is shorter than its diff:
```python
import jax
import jax.numpy as jnp
from jax import lax
from jax.experimental import pallas as pl
from jax.experimental.pallas import tpu as pltpu
from jax.sharding import PartitionSpec as P

epsilon = 1e-06


def passed_along(value, axis, steps):
    count = lax.axis_size(axis)
    leading, last = (max(0, -steps), min(count, count - steps))
    return lax.ppermute(value, axis, [(source, source + steps) for source in range(leading, last)])


def rms_norm(values):
    return values * lax.rsqrt(jnp.mean(values * values, axis=-1, keepdims=True) + epsilon)


def pick_entry(vector, position):
    return jnp.sum(jnp.where(jnp.arange(vector.shape[0]) == position, vector, 0))


def spread_over_seq(block):
    count = lax.axis_size("seq")
    return [block] + [
        lax.ppermute(block, "seq", [(source, (source + shift) % count) for source in range(count)])
        for shift in range(1, count)
    ]


def block_kernel(*refs):
    where_ref = refs[0]
    count = (len(refs) - 9) // 1
    part_refs = refs[1 : 1 + count]
    scale_ref, weights_ref, keys_ref, values_ref = refs[1 + count : 5 + count]
    heads_ref, keys_out, values_out = refs[5 + count : 8 + count]
    shaped_ref = refs[8 + count]
    start = where_ref[0]
    patch_count = where_ref[1]
    here = where_ref[2]
    head_dim = keys_ref.shape[2]
    seq_len = keys_ref.shape[1]
    span, width = part_refs[0].shape
    features = width * count

    @pl.when(pl.program_id(0) == 0)
    def _():
        parts = [part[...].astype(jnp.float32) for part in part_refs]
        row_mean = sum(jnp.sum(part, axis=-1, keepdims=True) for part in parts) / features
        centred = [part - row_mean for part in parts]
        spread = sum(jnp.sum(c * c, axis=-1, keepdims=True) for c in centred) / features
        inverse = lax.rsqrt(spread + epsilon)
        for shift in range(count):
            slot = lax.rem(here - shift + count, count)
            shift_scale = scale_ref[slot]
            shaped_ref[slot] = (
                (centred[shift] * inverse) * (1.0 + shift_scale[1:2]) + shift_scale[0:1]
            ).astype(jnp.bfloat16)

    mixed = sum(
        jnp.dot(
            shaped_ref[slot],
            weights_ref[slot * width : (slot + 1) * width, :],
            preferred_element_type=jnp.float32,
        )
        for slot in range(count)
    )
    queries = rms_norm(mixed[:, :head_dim]).astype(jnp.bfloat16)
    fresh_keys = rms_norm(mixed[:, head_dim : 2 * head_dim]).astype(jnp.bfloat16)
    fresh_values = mixed[:, 2 * head_dim :].astype(jnp.bfloat16)
    rows = lax.broadcasted_iota(jnp.int32, (seq_len, span), 0)
    picks = lax.broadcasted_iota(jnp.int32, (seq_len, span), 1)
    placing = ((rows == picks + start) & (picks < patch_count)).astype(jnp.bfloat16)
    row_ids = lax.broadcasted_iota(jnp.int32, (seq_len, 1), 0)
    inside = (row_ids >= start) & (row_ids < start + patch_count)
    placed_keys = jnp.dot(placing, fresh_keys, preferred_element_type=jnp.float32)
    placed_values = jnp.dot(placing, fresh_values, preferred_element_type=jnp.float32)
    keys = jnp.where(inside, placed_keys.astype(jnp.bfloat16), keys_ref[0])
    values = jnp.where(inside, placed_values.astype(jnp.bfloat16), values_ref[0])
    keys_out[0] = keys
    values_out[0] = values
    scores = lax.dot_general(
        queries, keys, (((1,), (1,)), ((), ())), preferred_element_type=jnp.float32
    ) * head_dim ** (-0.5)
    expos = jnp.exp(scores)
    weights = (expos / jnp.sum(expos, axis=-1, keepdims=True)).astype(jnp.bfloat16)
    heads_ref[...] = jnp.dot(weights, values, preferred_element_type=jnp.float32).astype(
        jnp.bfloat16
    )


def attend_block(parts, shift_scale, qkv_weights, key_cache, value_cache, where):
    count = len(parts)
    span, width = parts[0].shape
    heads_here, seq_len, head_dim = key_cache.shape
    features = qkv_weights.shape[0]
    scale_blocks = jnp.transpose(shift_scale.reshape(2, count, width), (1, 0, 2))
    whole = lambda shape: pl.BlockSpec(shape, lambda h, where: (0,) * len(shape))
    cache_spec = pl.BlockSpec((1, seq_len, head_dim), lambda h, where: (h, 0, 0))
    grid_spec = pltpu.PrefetchScalarGridSpec(
        num_scalar_prefetch=1,
        grid=(heads_here,),
        in_specs=[whole((span, width)) for _ in parts]
        + [
            whole((count, 2, width)),
            pl.BlockSpec((features, 3 * head_dim), lambda h, where: (0, h)),
            cache_spec,
            cache_spec,
        ],
        out_specs=[
            pl.BlockSpec((span, head_dim), lambda h, where: (0, h)),
            cache_spec,
            cache_spec,
        ],
        scratch_shapes=[pltpu.VMEM((count, span, width), jnp.bfloat16)],
    )
    return pl.pallas_call(
        block_kernel,
        grid_spec=grid_spec,
        out_shape=[
            jax.ShapeDtypeStruct((span, heads_here * head_dim), jnp.bfloat16),
            jax.ShapeDtypeStruct(key_cache.shape, key_cache.dtype),
            jax.ShapeDtypeStruct(value_cache.shape, value_cache.dtype),
        ],
        input_output_aliases={count + 3: 1, count + 4: 2},
        compiler_params=pltpu.CompilerParams(dimension_semantics=("arbitrary",)),
    )(where, *parts, scale_blocks, qkv_weights, key_cache, value_cache)


def exit_kernel(*refs):
    where_ref = refs[0]
    count = len(refs) - 5
    part_refs = refs[1 : 1 + count]
    weights_ref, own_ref, gate_ref = refs[1 + count : 4 + count]
    out_ref = refs[4 + count]
    patch_count = where_ref[1]
    here = where_ref[2]
    projected = sum(
        jnp.dot(
            part_refs[shift][...],
            weights_ref[lax.rem(here - shift + count, count)],
            preferred_element_type=jnp.float32,
        )
        for shift in range(count)
    )
    updated = own_ref[...].astype(jnp.float32) + gate_ref[...] * projected
    live = lax.broadcasted_iota(jnp.int32, updated.shape, 0) < patch_count
    out_ref[...] = jnp.where(live, updated, 0.0).astype(out_ref.dtype)


def leave_block(parts, out_weights, own_rows, gating_here, where):
    count = len(parts)
    span, head_width = parts[0].shape
    vmem = pl.BlockSpec(memory_space=pltpu.VMEM)
    smem = pl.BlockSpec(memory_space=pltpu.SMEM)
    return pl.pallas_call(
        exit_kernel,
        in_specs=[smem] + [vmem] * (count + 3),
        out_specs=vmem,
        out_shape=jax.ShapeDtypeStruct(own_rows.shape, own_rows.dtype),
    )(
        where,
        *parts,
        out_weights.reshape(count, head_width, out_weights.shape[1]),
        own_rows,
        gating_here.reshape(1, -1),
    )


def shards(
    incoming_states,
    transit_states,
    patch_sizes_list,
    outdated_lookups,
    outdated_contents,
    attention_projection,
    exit_projection,
    shift_and_scale,
    branch_gates,
):
    section_index = lax.axis_index("section")
    seq_index = lax.axis_index("seq")
    patches = patch_sizes_list.shape[0]
    biggest_patch_span = transit_states.shape[1]
    columns = incoming_states.shape[1]
    starts = jnp.cumsum(patch_sizes_list) - patch_sizes_list
    key_cache = outdated_lookups[0]
    value_cache = outdated_contents[0]
    qkv_weights = attention_projection[0]
    out_weights = exit_projection[0]
    shift_scale = shift_and_scale[0]
    gating_here = branch_gates[0]
    row_numbers = jnp.arange(biggest_patch_span)

    results = []
    entering_ext = jnp.concatenate(
        [incoming_states, jnp.zeros((biggest_patch_span, columns), jnp.bfloat16)], axis=0
    )
    earlier_result = transit_states[0]
    for turn_number in range(patches):
        patch_index = jnp.remainder(turn_number - section_index, patches)
        patch_count = pick_entry(patch_sizes_list, patch_index)
        patch_start = pick_entry(starts, patch_index)
        where = jnp.stack([patch_start, patch_count, seq_index]).astype(jnp.int32)
        live_rows = row_numbers < patch_count
        entry_patch = lax.dynamic_slice_in_dim(
            entering_ext, starts[turn_number], biggest_patch_span, 0
        )
        own_rows = jnp.where(section_index == 0, entry_patch, earlier_result)
        own_rows = jnp.where(live_rows[:, None], own_rows, jnp.zeros_like(own_rows))
        head_rows, key_cache, value_cache = attend_block(
            spread_over_seq(own_rows), shift_scale, qkv_weights, key_cache, value_cache, where
        )
        updated = leave_block(spread_over_seq(head_rows), out_weights, own_rows, gating_here, where)
        results.append(updated)
        if turn_number + 1 < patches:
            earlier_result = passed_along(updated, "section", 1)
    return jnp.stack(results)[:, None]


def solution(mesh):
    return jax.shard_map(
        shards,
        mesh=mesh,
        in_specs=(
            P("groups", "seq"),
            P("section", "groups", "seq"),
            P("groups"),
            P("section", "seq", "groups", None),
            P("section", "seq", "groups", None),
            P("section", None, "seq"),
            P("section", None, "seq"),
            P("section", None, None),
            P("section", "seq"),
        ),
        out_specs=P(None, "section", "groups", "seq"),
        check_vma=False,
    )
```

time: 307 us -> 255 us (0.83)
  matrix products: 41 us -> 0 us
  Pallas kernels: 26.8 us -> 66.3 us
  waiting for transfers between devices: 163 us -> 130 us
  other arithmetic: 38.2 us -> 14.2 us
  starting transfers between devices: 10.7 us -> 24.7 us
  between operations: 20.9 us -> 7.35 us
  local copies, waits for them, and re-layouts: 5.01 us -> 11.6 us
    all_gather x8 -> x0, waiting for transfers between devices: 142 us -> none  [the longest x4 75.8 us: shards(): full_rows = lax.all_gather(own_rows, 'seq', axis=1, tiled=True)]
    ppermute x0 -> x24, waiting for transfers between devices: none -> 116 us  [spread_over_seq(): lax.ppermute(block, 'seq', [(source, (source + shift) % count) for source...]
    dot_general x8 -> x0, matrix products: 41 us -> none  [the longest x4 29.9 us: run_block(): mixed = jnp.dot(shaped, qkv_weights, preferred_element_type=jnp.float32)]
    pallas_call x4 -> x8, Pallas kernels: 26.8 us -> 66.3 us  [the longest x4 49.8 us: attend_block(): pl.pallas_call(block_kernel, grid_spec=grid_spec, out_shape=[jax.ShapeDty...]
    reduce_sum x8 -> x0, other arithmetic: 15.1 us -> none  [the longest x4 7.84 us: layer_norm(): spread = jnp.mean(centred * centred, axis=-1, keepdims=True)]
    ppermute x0 -> x24, starting transfers between devices: none -> 12.6 us  [spread_over_seq(): lax.ppermute(block, 'seq', [(source, (source + shift) % count) for source...]
    select_n x4, other arithmetic: 7.74 us -> 0.89 us  [shards(): own_rows = jnp.where(live_rows[:, None], own_rows, jnp.zeros_like(own_rows))]
    unnamed x42 -> x70, local copies, waits for them, and re-layouts: 4.41 us -> 10.9 us
  transfers between devices with their start and end apart: 11 -> 27, of which waited for: 11 -> 25; matrix products, arithmetic and copies ran while one was open for 4% -> 4% of each run, Pallas kernels for 0% -> 0%
where the time goes in v4:
time: 255 us; the launch traced here: 254 us
  waiting for transfers between devices  130 us (51%)
  Pallas kernels  66.3 us (26%)
  starting transfers between devices  24.7 us (10%)
  other arithmetic  14.2 us (6%)
  local copies, waits for them, and re-layouts  11.6 us (5%)
  between operations  7.35 us (3%)
    ppermute x24, waiting for transfers between devices, spread_over_seq(): lax.ppermute(block, 'seq', [(source, (source + shift) % count) for source...  116 us
    pallas_call x4, Pallas kernels, attend_block(): pl.pallas_call(block_kernel, grid_spec=grid_spec, out_shape=[jax.ShapeDty...  49.8 us
    pallas_call x4, Pallas kernels, leave_block(): pl.pallas_call(exit_kernel, in_specs=[smem] + [vmem] * (count + 3), out_s...  16.5 us
    ppermute x3, waiting for transfers between devices, passed_along(): lax.ppermute(value, axis, [(source, source + steps) for source in range(l...  14.5 us
    ppermute x24, starting transfers between devices, spread_over_seq(): lax.ppermute(block, 'seq', [(source, (source + shift) % count) for source...  12.6 us
    ppermute x3, starting transfers between devices, passed_along(): lax.ppermute(value, axis, [(source, source + steps) for source in range(l...  12 us
    unnamed x70, local copies, waits for them, and re-layouts  10.9 us
    another operation x4, other arithmetic, shards(): where = jnp.stack([patch_start, patch_count, seq_index]).astype(jnp.int32)  7.51 us
  transfers between devices with their start and end apart: 27, of which 25 were waited for; matrix products, arithmetic and copies ran while one was open for 4% of the time, Pallas kernels for 0%

profile of v4, /device:TPU:0, one launch (start us, length us, event | category | flops | bytes accessed | tf_op | source)
XLA Modules:
  0.0 254.5 jit_solution(10193518091279309283)
XLA Ops:
  0.0 2.2 copy.29
  2.2 2.1 copy.30
  4.5 0.8 fusion.8
  8.5 2.4 collective-permute-start.2
  11.8 1.8 add_add_fusion.refs_0_
  13.6 6.8 %collective-permute-done.2.refs_4_ = bf16[256,768]{1,0:T(8,128)(2,1)S(1)} collective-permute-done((bf16[256,768]{1,0:T(8,128)(2,1)S(1)}, bf16[256,768]{1,0:T(8,128)(2,1)S(1)}, u32[]{:S(2)}, u32[]{:S(2)}) %collective-permute-start.2) | collective-permute-done | bytes 393248 | tf_op jit(solution)/shard_map/ppermute | solution.py:28
  20.4 9.4 %collective-permute-done.1.refs_3_ = bf16[256,768]{1,0:T(8,128)(2,1)S(1)} collective-permute-done((bf16[256,768]{1,0:T(8,128)(2,1)S(1)}, bf16[256,768]{1,0:T(8,128)(2,1)S(1)}, u32[]{:S(2)}, u32[]{:S(2)}) %collective-permute-start.1) | collective-permute-done | bytes 393248 | tf_op jit(solution)/shard_map/ppermute | solution.py:28
  29.8 0.7 copy-done.10
  30.6 12.5 %shard_map.91 = (bf16[256,512]{1,0:T(8,128)(2,1)}, bf16[4,768,128]{2,1,0:T(8,128)(2,1)}, bf16[4,768,128]{2,1,0:T(8,128)(2,1)}) custom-call(s32[3]{0:T(128)} %add_add_fusion.refs_0_, bf16[256,768]{1,0:T(8,128)(2,1)} %copy-done.2, bf16[256,768]{1,0:T(8,128)(2,1)} %copy-done.14, ...), custom_call_target="tpu_custom_call", output_to_operand_aliasing={{1}: (7, {}), {2}: (8, {})} | custom-call | tf_op jit(solution)/shard_map/pallas_call | solution.py:119
  43.1 1.6 collective-permute-start.4
  44.8 4.2 %collective-permute-done.5.refs_4_ = bf16[256,512]{1,0:T(8,128)(2,1)S(1)} collective-permute-done((bf16[256,512]{1,0:T(8,128)(2,1)}, bf16[256,512]{1,0:T(8,128)(2,1)S(1)}, u32[]{:S(2)}, u32[]{:S(2)}) %collective-permute-start.5) | collective-permute-done | bytes 262176 | tf_op jit(solution)/shard_map/ppermute | solution.py:28
  49.0 8.5 %collective-permute-done.4.refs_3_ = bf16[256,512]{1,0:T(8,128)(2,1)S(1)} collective-permute-done((bf16[256,512]{1,0:T(8,128)(2,1)}, bf16[256,512]{1,0:T(8,128)(2,1)S(1)}, u32[]{:S(2)}, u32[]{:S(2)}) %collective-permute-start.4) | collective-permute-done | bytes 262176 | tf_op jit(solution)/shard_map/ppermute | solution.py:28
  58.4 4.1 %shard_map.92 = bf16[256,768]{1,0:T(8,128)(2,1)} custom-call(s32[3]{0:T(128)} %add_add_fusion.refs_0_, bf16[256,512]{1,0:T(8,128)(2,1)} %get-tuple-element.15.refs_1_, bf16[256,512]{1,0:T(8,128)(2,1)} %copy-done.29, bf16[256,512]{1,0:T(8,128)(2,1)} %copy-done.25, bf16[256,512]{1,0:T(8,128)(2,1)} %copy-done.21, bf16[4,512,768]{2,1,0:T(8,128)(2,1)} %bitcast.38, ...), custom_call_target="tpu_custom_call" | custom-call | tf_op jit(solution)/shard_map/pallas_call | solution.py:158
  62.5 3.4 %collective-permute-start.6 = (bf16[256,768]{1,0:T(8,128)(2,1)}, bf16[256,768]{1,0:T(8,128)(2,1)S(1)}, u32[]{:S(2)}, u32[]{:S(2)}) collective-permute-start(bf16[256,768]{1,0:T(8,128)(2,1)} %shard_map.92), channel_id=1, source_target_pairs={{0,4},{4,8},{8,12},{1,5},{5,9},{9,13},{2,6},{6,10},{10,14},{3,7},{... | collective-permute-start | bytes 1179656 | tf_op jit(solution)/shard_map/ppermute | solution.py:14
  68.3 4.8 %collective-permute-done.6 = bf16[256,768]{1,0:T(8,128)(2,1)S(1)} collective-permute-done((bf16[256,768]{1,0:T(8,128)(2,1)}, bf16[256,768]{1,0:T(8,128)(2,1)S(1)}, u32[]{:S(2)}, u32[]{:S(2)}) %collective-permute-start.6) | collective-permute-done | bytes 393248 | tf_op jit(solution)/shard_map/ppermute | solution.py:14
  73.4 1.5 collective-permute-start.8
  75.0 1.9 add_add_fusion.1.refs_0_
  76.9 5.1 %collective-permute-done.9.refs_4_ = bf16[256,768]{1,0:T(8,128)(2,1)S(1)} collective-permute-done((bf16[256,768]{1,0:T(8,128)(2,1)S(1)}, bf16[256,768]{1,0:T(8,128)(2,1)S(1)}, u32[]{:S(2)}, u32[]{:S(2)}) %collective-permute-start.9) | collective-permute-done | bytes 393248 | tf_op jit(solution)/shard_map/ppermute | solution.py:28
  82.0 11.1 %collective-permute-done.8.refs_3_ = bf16[256,768]{1,0:T(8,128)(2,1)S(1)} collective-permute-done((bf16[256,768]{1,0:T(8,128)(2,1)S(1)}, bf16[256,768]{1,0:T(8,128)(2,1)S(1)}, u32[]{:S(2)}, u32[]{:S(2)}) %collective-permute-start.8) | collective-permute-done | bytes 393248 | tf_op jit(solution)/shard_map/ppermute | solution.py:28
  94.0 12.4 %shard_map.93 = (bf16[256,512]{1,0:T(8,128)(2,1)}, bf16[4,768,128]{2,1,0:T(8,128)(2,1)}, bf16[4,768,128]{2,1,0:T(8,128)(2,1)}) custom-call(s32[3]{0:T(128)} %add_add_fusion.1.refs_0_, bf16[256,768]{1,0:T(8,128)(2,1)} %copy-done.3, bf16[256,768]{1,0:T(8,128)(2,1)} %copy-done.18, ...), custom_call_target="tpu_custom_call", output_to_operand_aliasing={{1}: (7, {}), {2}: (8, {})} | custom-call | tf_op jit(solution)/shard_map/pallas_call | solution.py:119
  107.2 6.0 %collective-permute-done.12.refs_4_ = bf16[256,512]{1,0:T(8,128)(2,1)S(1)} collective-permute-done((bf16[256,512]{1,0:T(8,128)(2,1)}, bf16[256,512]{1,0:T(8,128)(2,1)S(1)}, u32[]{:S(2)}, u32[]{:S(2)}) %collective-permute-start.12) | collective-permute-done | bytes 262176 | tf_op jit(solution)/shard_map/ppermute | solution.py:28
  113.3 5.8 %collective-permute-done.11.refs_3_ = bf16[256,512]{1,0:T(8,128)(2,1)S(1)} collective-permute-done((bf16[256,512]{1,0:T(8,128)(2,1)}, bf16[256,512]{1,0:T(8,128)(2,1)S(1)}, u32[]{:S(2)}, u32[]{:S(2)}) %collective-permute-start.11) | collective-permute-done | bytes 262176 | tf_op jit(solution)/shard_map/ppermute | solution.py:28
  119.0 0.9 collective-permute-done.10.refs_2_
  120.7 4.1 %shard_map.94 = bf16[256,768]{1,0:T(8,128)(2,1)} custom-call(s32[3]{0:T(128)} %add_add_fusion.1.refs_0_, bf16[256,512]{1,0:T(8,128)(2,1)} %get-tuple-element.18.refs_1_, bf16[256,512]{1,0:T(8,128)(2,1)} %copy-done.30, bf16[256,512]{1,0:T(8,128)(2,1)} %copy-done.26, bf16[256,512]{1,0:T(8,128)(2,1)} %copy-done.22, bf16[4,512,768]{2,1,0:T(8,128)(2,1)} %bitcast.39, ...), custom_call_target="tpu_custom_call" | custom-call | tf_op jit(solution)/shard_map/pallas_call | solution.py:158
  124.8 4.3 %collective-permute-start.13 = (bf16[256,768]{1,0:T(8,128)(2,1)}, bf16[256,768]{1,0:T(8,128)(2,1)S(1)}, u32[]{:S(2)}, u32[]{:S(2)}) collective-permute-start(bf16[256,768]{1,0:T(8,128)(2,1)} %shard_map.94), channel_id=1, source_target_pairs={{0,4},{4,8},{8,12},{1,5},{5,9},{9,13},{2,6},{6,10},{10,14},{3,7},{... | collective-permute-start | bytes 1179656 | tf_op jit(solution)/shard_map/ppermute | solution.py:14
  131.6 5.5 %collective-permute-done.13 = bf16[256,768]{1,0:T(8,128)(2,1)S(1)} collective-permute-done((bf16[256,768]{1,0:T(8,128)(2,1)}, bf16[256,768]{1,0:T(8,128)(2,1)S(1)}, u32[]{:S(2)}, u32[]{:S(2)}) %collective-permute-start.13) | collective-permute-done | bytes 393248 | tf_op jit(solution)/shard_map/ppermute | solution.py:14
  138.2 2.0 add_add_fusion.2.refs_0_
  140.2 6.5 %collective-permute-done.16.refs_4_ = bf16[256,768]{1,0:T(8,128)(2,1)S(1)} collective-permute-done((bf16[256,768]{1,0:T(8,128)(2,1)S(1)}, bf16[256,768]{1,0:T(8,128)(2,1)S(1)}, u32[]{:S(2)}, u32[]{:S(2)}) %collective-permute-start.16) | collective-permute-done | bytes 393248 | tf_op jit(solution)/shard_map/ppermute | solution.py:28
  146.7 8.7 %collective-permute-done.15.refs_3_ = bf16[256,768]{1,0:T(8,128)(2,1)S(1)} collective-permute-done((bf16[256,768]{1,0:T(8,128)(2,1)S(1)}, bf16[256,768]{1,0:T(8,128)(2,1)S(1)}, u32[]{:S(2)}, u32[]{:S(2)}) %collective-permute-start.15) | collective-permute-done | bytes 393248 | tf_op jit(solution)/shard_map/ppermute | solution.py:28
  155.5 0.9 collective-permute-done.14.refs_2_
  156.4 0.7 copy-done.19
  157.2 12.4 %shard_map.95 = (bf16[256,512]{1,0:T(8,128)(2,1)}, bf16[4,768,128]{2,1,0:T(8,128)(2,1)}, bf16[4,768,128]{2,1,0:T(8,128)(2,1)}) custom-call(s32[3]{0:T(128)} %add_add_fusion.2.refs_0_, bf16[256,768]{1,0:T(8,128)(2,1)} %copy-done.4, bf16[256,768]{1,0:T(8,128)(2,1)} %copy-done.19, ...), custom_call_target="tpu_custom_call", output_to_operand_aliasing={{1}: (7, {}), {2}: (8, {})} | custom-call | tf_op jit(solution)/shard_map/pallas_call | solution.py:119
  169.6 1.5 collective-permute-start.18
  171.2 4.5 %collective-permute-done.19.refs_4_ = bf16[256,512]{1,0:T(8,128)(2,1)S(1)} collective-permute-done((bf16[256,512]{1,0:T(8,128)(2,1)}, bf16[256,512]{1,0:T(8,128)(2,1)S(1)}, u32[]{:S(2)}, u32[]{:S(2)}) %collective-permute-start.19) | collective-permute-done | bytes 262176 | tf_op jit(solution)/shard_map/ppermute | solution.py:28
  175.7 8.1 %collective-permute-done.18.refs_3_ = bf16[256,512]{1,0:T(8,128)(2,1)S(1)} collective-permute-done((bf16[256,512]{1,0:T(8,128)(2,1)}, bf16[256,512]{1,0:T(8,128)(2,1)S(1)}, u32[]{:S(2)}, u32[]{:S(2)}) %collective-permute-start.18) | collective-permute-done | bytes 262176 | tf_op jit(solution)/shard_map/ppermute | solution.py:28
  185.2 4.1 %shard_map.96 = bf16[256,768]{1,0:T(8,128)(2,1)} custom-call(s32[3]{0:T(128)} %add_add_fusion.2.refs_0_, bf16[256,512]{1,0:T(8,128)(2,1)} %get-tuple-element.21.refs_1_, bf16[256,512]{1,0:T(8,128)(2,1)} %copy-done.31, bf16[256,512]{1,0:T(8,128)(2,1)} %copy-done.27, bf16[256,512]{1,0:T(8,128)(2,1)} %copy-done.23, bf16[4,512,768]{2,1,0:T(8,128)(2,1)} %bitcast.40, ...), custom_call_target="tpu_custom_call" | custom-call | tf_op jit(solution)/shard_map/pallas_call | solution.py:158
  189.4 4.3 %collective-permute-start.20 = (bf16[256,768]{1,0:T(8,128)(2,1)}, bf16[256,768]{1,0:T(8,128)(2,1)S(1)}, u32[]{:S(2)}, u32[]{:S(2)}) collective-permute-start(bf16[256,768]{1,0:T(8,128)(2,1)} %shard_map.96), channel_id=1, source_target_pairs={{0,4},{4,8},{8,12},{1,5},{5,9},{9,13},{2,6},{6,10},{10,14},{3,7},{... | collective-permute-start | bytes 1179656 | tf_op jit(solution)/shard_map/ppermute | solution.py:14
  196.1 4.2 %collective-permute-done.20 = bf16[256,768]{1,0:T(8,128)(2,1)S(1)} collective-permute-done((bf16[256,768]{1,0:T(8,128)(2,1)}, bf16[256,768]{1,0:T(8,128)(2,1)S(1)}, u32[]{:S(2)}, u32[]{:S(2)}) %collective-permute-start.20) | collective-permute-done | bytes 393248 | tf_op jit(solution)/shard_map/ppermute | solution.py:14
  200.6 1.5 collective-permute-start.22
  202.2 1.8 add_add_fusion.3.refs_0_
  204.1 5.1 %collective-permute-done.23.refs_4_ = bf16[256,768]{1,0:T(8,128)(2,1)S(1)} collective-permute-done((bf16[256,768]{1,0:T(8,128)(2,1)S(1)}, bf16[256,768]{1,0:T(8,128)(2,1)S(1)}, u32[]{:S(2)}, u32[]{:S(2)}) %collective-permute-start.23) | collective-permute-done | bytes 393248 | tf_op jit(solution)/shard_map/ppermute | solution.py:28
  209.2 11.1 %collective-permute-done.22.refs_3_ = bf16[256,768]{1,0:T(8,128)(2,1)S(1)} collective-permute-done((bf16[256,768]{1,0:T(8,128)(2,1)S(1)}, bf16[256,768]{1,0:T(8,128)(2,1)S(1)}, u32[]{:S(2)}, u32[]{:S(2)}) %collective-permute-start.22) | collective-permute-done | bytes 393248 | tf_op jit(solution)/shard_map/ppermute | solution.py:28
  221.2 12.4 %shard_map.97 = (bf16[256,512]{1,0:T(8,128)(2,1)}, bf16[4,768,128]{2,1,0:T(8,128)(2,1)}, bf16[4,768,128]{2,1,0:T(8,128)(2,1)}) custom-call(s32[3]{0:T(128)} %add_add_fusion.3.refs_0_, bf16[256,768]{1,0:T(8,128)(2,1)} %copy-done.1, bf16[256,768]{1,0:T(8,128)(2,1)} %copy-done.17, ...), custom_call_target="tpu_custom_call", output_to_operand_aliasing={{1}: (7, {}), {2}: (8, {})} | custom-call | tf_op jit(solution)/shard_map/pallas_call | solution.py:119
  234.5 6.0 %collective-permute-done.26.refs_4_ = bf16[256,512]{1,0:T(8,128)(2,1)S(1)} collective-permute-done((bf16[256,512]{1,0:T(8,128)(2,1)}, bf16[256,512]{1,0:T(8,128)(2,1)S(1)}, u32[]{:S(2)}, u32[]{:S(2)}) %collective-permute-start.26) | collective-permute-done | bytes 262176 | tf_op jit(solution)/shard_map/ppermute | solution.py:28
  240.5 5.8 %collective-permute-done.25.refs_3_ = bf16[256,512]{1,0:T(8,128)(2,1)S(1)} collective-permute-done((bf16[256,512]{1,0:T(8,128)(2,1)}, bf16[256,512]{1,0:T(8,128)(2,1)S(1)}, u32[]{:S(2)}, u32[]{:S(2)}) %collective-permute-start.25) | collective-permute-done | bytes 262176 | tf_op jit(solution)/shard_map/ppermute | solution.py:28
  246.3 0.9 collective-permute-done.24.refs_2_
  248.0 4.1 %shard_map.98 = bf16[256,768]{1,0:T(8,128)(2,1)} custom-call(s32[3]{0:T(128)} %add_add_fusion.3.refs_0_, bf16[256,512]{1,0:T(8,128)(2,1)} %get-tuple-element.24.refs_1_, bf16[256,512]{1,0:T(8,128)(2,1)} %copy-done.32, bf16[256,512]{1,0:T(8,128)(2,1)} %copy-done.28, bf16[256,512]{1,0:T(8,128)(2,1)} %copy-done.24, bf16[4,512,768]{2,1,0:T(8,128)(2,1)} %bitcast.41, ...), custom_call_target="tpu_custom_call" | custom-call | tf_op jit(solution)/shard_map/pallas_call | solution.py:158
  252.1 2.3 maximum_bitcast_fusion
  (100 shorter events, 14.2 us)
Async XLA Ops:
  0.0 8.3 %copy-start = (bf16[768,768]{1,0:T(8,128)(2,1)S(1)}, bf16[768,768]{1,0:T(8,128)(2,1)}, u32[]{:S(2)}) copy-start(bf16[768,768]{1,0:T(8,128)(2,1)} %param.9) | copy-start | bytes 3538948
  0.0 8.3 %copy-start.20 = (bf16[1,256,768]{2,1,0:T(8,128)(2,1)S(1)}, bf16[1,256,768]{2,1,0:T(8,128)(2,1)}, u32[]{:S(2)}) copy-start(bf16[1,256,768]{2,1,0:T(8,128)(2,1)} %param.10) | copy-start | bytes 1179652
  0.0 4.3 %copy-start.33 = (s32[4]{0:T(128)S(1)}, s32[4]{0:T(128)}, u32[]{:S(2)}) copy-start(s32[4]{0:T(128)} %param.11) | copy-start | bytes 52
  8.5 21.2 %copy-start.2 = (bf16[256,768]{1,0:T(8,128)(2,1)}, bf16[256,768]{1,0:T(8,128)(2,1)S(1)}, u32[]{:S(2)}) copy-start(bf16[256,768]{1,0:T(8,128)(2,1)S(1)} %fusion.1.refs_1_.refs_6_) | copy-start | bytes 1179652
  8.5 11.8 %collective-permute-start.2 = (bf16[256,768]{1,0:T(8,128)(2,1)S(1)}, bf16[256,768]{1,0:T(8,128)(2,1)S(1)}, u32[]{:S(2)}, u32[]{:S(2)}) collective-permute-start(bf16[256,768]{1,0:T(8,128)(2,1)S(1)} %fusion.1.refs_1_.refs_6_), channel_id=1, source_target_pairs={{0,3},{1,0},{2,1},{3,2},{4,7},{5,4},{6,5},{7,6},{8,11},{9,8},{10,9... | collective-permute-start | bytes 1179656 | tf_op jit(solution)/shard_map/ppermute | solution.py:28
  11.0 18.8 %collective-permute-start.1 = (bf16[256,768]{1,0:T(8,128)(2,1)S(1)}, bf16[256,768]{1,0:T(8,128)(2,1)S(1)}, u32[]{:S(2)}, u32[]{:S(2)}) collective-permute-start(bf16[256,768]{1,0:T(8,128)(2,1)S(1)} %fusion.1.refs_1_.refs_6_), channel_id=1, source_target_pairs={{0,2},{1,3},{2,0},{3,1},{4,6},{5,7},{6,4},{7,5},{8,10},{9,11},{10,... | collective-permute-start | bytes 1179656 | tf_op jit(solution)/shard_map/ppermute | solution.py:28
  11.6 18.1 %collective-permute-start = (bf16[256,768]{1,0:T(8,128)(2,1)S(1)}, bf16[256,768]{1,0:T(8,128)(2,1)S(1)}, u32[]{:S(2)}, u32[]{:S(2)}) collective-permute-start(bf16[256,768]{1,0:T(8,128)(2,1)S(1)} %fusion.1.refs_1_.refs_6_), channel_id=1, source_target_pairs={{0,1},{1,2},{2,3},{3,0},{4,5},{5,6},{6,7},{7,4},{8,9},{9,10},{10,1... | collective-permute-start | bytes 1179656 | tf_op jit(solution)/shard_map/ppermute | solution.py:28
  20.4 9.4 %copy-start.8 = (bf16[256,768]{1,0:T(8,128)(2,1)}, bf16[256,768]{1,0:T(8,128)(2,1)S(1)}, u32[]{:S(2)}) copy-start(bf16[256,768]{1,0:T(8,128)(2,1)S(1)} %collective-permute-done.2.refs_4_) | copy-start | bytes 1179652
  43.1 6.0 %collective-permute-start.5 = (bf16[256,512]{1,0:T(8,128)(2,1)}, bf16[256,512]{1,0:T(8,128)(2,1)S(1)}, u32[]{:S(2)}, u32[]{:S(2)}) collective-permute-start(bf16[256,512]{1,0:T(8,128)(2,1)} %get-tuple-element.15.refs_1_), channel_id=1, source_target_pairs={{0,3},{1,0},{2,1},{3,2},{4,7},{5,4},{6,5},{7,6},{8,11},{9,8},{10,9... | collective-permute-start | bytes 786440 | tf_op jit(solution)/shard_map/ppermute | solution.py:28
  43.1 14.5 %collective-permute-start.4 = (bf16[256,512]{1,0:T(8,128)(2,1)}, bf16[256,512]{1,0:T(8,128)(2,1)S(1)}, u32[]{:S(2)}, u32[]{:S(2)}) collective-permute-start(bf16[256,512]{1,0:T(8,128)(2,1)} %get-tuple-element.15.refs_1_), channel_id=1, source_target_pairs={{0,2},{1,3},{2,0},{3,1},{4,6},{5,7},{6,4},{7,5},{8,10},{9,11},{10,... | collective-permute-start | bytes 786440 | tf_op jit(solution)/shard_map/ppermute | solution.py:28
  44.7 12.9 %collective-permute-start.3 = (bf16[256,512]{1,0:T(8,128)(2,1)}, bf16[256,512]{1,0:T(8,128)(2,1)S(1)}, u32[]{:S(2)}, u32[]{:S(2)}) collective-permute-start(bf16[256,512]{1,0:T(8,128)(2,1)} %get-tuple-element.15.refs_1_), channel_id=1, source_target_pairs={{0,1},{1,2},{2,3},{3,0},{4,5},{5,6},{6,7},{7,4},{8,9},{9,10},{10,1... | collective-permute-start | bytes 786440 | tf_op jit(solution)/shard_map/ppermute | solution.py:28
  49.0 8.6 %copy-start.21 = (bf16[256,512]{1,0:T(8,128)(2,1)}, bf16[256,512]{1,0:T(8,128)(2,1)S(1)}, u32[]{:S(2)}) copy-start(bf16[256,512]{1,0:T(8,128)(2,1)S(1)} %collective-permute-done.5.refs_4_) | copy-start | bytes 786436
  62.5 10.6 %collective-permute-start.6 = (bf16[256,768]{1,0:T(8,128)(2,1)}, bf16[256,768]{1,0:T(8,128)(2,1)S(1)}, u32[]{:S(2)}, u32[]{:S(2)}) collective-permute-start(bf16[256,768]{1,0:T(8,128)(2,1)} %shard_map.92), channel_id=1, source_target_pairs={{0,4},{4,8},{8,12},{1,5},{5,9},{9,13},{2,6},{6,10},{10,14},{3,7},{... | collective-permute-start | bytes 1179656 | tf_op jit(solution)/shard_map/ppermute | solution.py:14
  73.3 19.9 %copy-start.3 = (bf16[256,768]{1,0:T(8,128)(2,1)}, bf16[256,768]{1,0:T(8,128)(2,1)S(1)}, u32[]{:S(2)}) copy-start(bf16[256,768]{1,0:T(8,128)(2,1)S(1)} %fusion.3.refs_1_.refs_6_) | copy-start | bytes 1179652
  73.3 8.6 %collective-permute-start.9 = (bf16[256,768]{1,0:T(8,128)(2,1)S(1)}, bf16[256,768]{1,0:T(8,128)(2,1)S(1)}, u32[]{:S(2)}, u32[]{:S(2)}) collective-permute-start(bf16[256,768]{1,0:T(8,128)(2,1)S(1)} %fusion.3.refs_1_.refs_6_), channel_id=1, source_target_pairs={{0,3},{1,0},{2,1},{3,2},{4,7},{5,4},{6,5},{7,6},{8,11},{9,8},{10,9... | collective-permute-start | bytes 1179656 | tf_op jit(solution)/shard_map/ppermute | solution.py:28
  73.4 19.6 %collective-permute-start.8 = (bf16[256,768]{1,0:T(8,128)(2,1)S(1)}, bf16[256,768]{1,0:T(8,128)(2,1)S(1)}, u32[]{:S(2)}, u32[]{:S(2)}) collective-permute-start(bf16[256,768]{1,0:T(8,128)(2,1)S(1)} %fusion.3.refs_1_.refs_6_), channel_id=1, source_target_pairs={{0,2},{1,3},{2,0},{3,1},{4,6},{5,7},{6,4},{7,5},{8,10},{9,11},{10,... | collective-permute-start | bytes 1179656 | tf_op jit(solution)/shard_map/ppermute | solution.py:28
  74.9 18.3 %collective-permute-start.7 = (bf16[256,768]{1,0:T(8,128)(2,1)S(1)}, bf16[256,768]{1,0:T(8,128)(2,1)S(1)}, u32[]{:S(2)}, u32[]{:S(2)}) collective-permute-start(bf16[256,768]{1,0:T(8,128)(2,1)S(1)} %fusion.3.refs_1_.refs_6_), channel_id=1, source_target_pairs={{0,1},{1,2},{2,3},{3,0},{4,5},{5,6},{6,7},{7,4},{8,9},{9,10},{10,1... | collective-permute-start | bytes 1179656 | tf_op jit(solution)/shard_map/ppermute | solution.py:28
  82.0 11.2 %copy-start.11 = (bf16[256,768]{1,0:T(8,128)(2,1)}, bf16[256,768]{1,0:T(8,128)(2,1)S(1)}, u32[]{:S(2)}) copy-start(bf16[256,768]{1,0:T(8,128)(2,1)S(1)} %collective-permute-done.9.refs_4_) | copy-start | bytes 1179652
  106.4 6.9 %collective-permute-start.12 = (bf16[256,512]{1,0:T(8,128)(2,1)}, bf16[256,512]{1,0:T(8,128)(2,1)S(1)}, u32[]{:S(2)}, u32[]{:S(2)}) collective-permute-start(bf16[256,512]{1,0:T(8,128)(2,1)} %get-tuple-element.18.refs_1_), channel_id=1, source_target_pairs={{0,3},{1,0},{2,1},{3,2},{4,7},{5,4},{6,5},{7,6},{8,11},{9,8},{10,9... | collective-permute-start | bytes 786440 | tf_op jit(solution)/shard_map/ppermute | solution.py:28
  106.4 12.6 %collective-permute-start.11 = (bf16[256,512]{1,0:T(8,128)(2,1)}, bf16[256,512]{1,0:T(8,128)(2,1)S(1)}, u32[]{:S(2)}, u32[]{:S(2)}) collective-permute-start(bf16[256,512]{1,0:T(8,128)(2,1)} %get-tuple-element.18.refs_1_), channel_id=1, source_target_pairs={{0,2},{1,3},{2,0},{3,1},{4,6},{5,7},{6,4},{7,5},{8,10},{9,11},{10,... | collective-permute-start | bytes 786440 | tf_op jit(solution)/shard_map/ppermute | solution.py:28
  107.1 12.9 %collective-permute-start.10 = (bf16[256,512]{1,0:T(8,128)(2,1)}, bf16[256,512]{1,0:T(8,128)(2,1)S(1)}, u32[]{:S(2)}, u32[]{:S(2)}) collective-permute-start(bf16[256,512]{1,0:T(8,128)(2,1)} %get-tuple-element.18.refs_1_), channel_id=1, source_target_pairs={{0,1},{1,2},{2,3},{3,0},{4,5},{5,6},{6,7},{7,4},{8,9},{9,10},{10,1... | collective-permute-start | bytes 786440 | tf_op jit(solution)/shard_map/ppermute | solution.py:28
  113.3 6.7 %copy-start.22 = (bf16[256,512]{1,0:T(8,128)(2,1)}, bf16[256,512]{1,0:T(8,128)(2,1)S(1)}, u32[]{:S(2)}) copy-start(bf16[256,512]{1,0:T(8,128)(2,1)S(1)} %collective-permute-done.12.refs_4_) | copy-start | bytes 786436
  119.0 1.0 copy-start.26
  124.8 12.3 %collective-permute-start.13 = (bf16[256,768]{1,0:T(8,128)(2,1)}, bf16[256,768]{1,0:T(8,128)(2,1)S(1)}, u32[]{:S(2)}, u32[]{:S(2)}) collective-permute-start(bf16[256,768]{1,0:T(8,128)(2,1)} %shard_map.94), channel_id=1, source_target_pairs={{0,4},{4,8},{8,12},{1,5},{5,9},{9,13},{2,6},{6,10},{10,14},{3,7},{... | collective-permute-start | bytes 1179656 | tf_op jit(solution)/shard_map/ppermute | solution.py:14
  137.3 19.1 %copy-start.4 = (bf16[256,768]{1,0:T(8,128)(2,1)}, bf16[256,768]{1,0:T(8,128)(2,1)S(1)}, u32[]{:S(2)}) copy-start(bf16[256,768]{1,0:T(8,128)(2,1)S(1)} %fusion.5.refs_1_.refs_6_) | copy-start | bytes 1179652
  137.3 9.4 %collective-permute-start.16 = (bf16[256,768]{1,0:T(8,128)(2,1)S(1)}, bf16[256,768]{1,0:T(8,128)(2,1)S(1)}, u32[]{:S(2)}, u32[]{:S(2)}) collective-permute-start(bf16[256,768]{1,0:T(8,128)(2,1)S(1)} %fusion.5.refs_1_.refs_6_), channel_id=1, source_target_pairs={{0,3},{1,0},{2,1},{3,2},{4,7},{5,4},{6,5},{7,6},{8,11},{9,8},{10,9... | collective-permute-start | bytes 1179656 | tf_op jit(solution)/shard_map/ppermute | solution.py:28
  137.4 18.1 %collective-permute-start.15 = (bf16[256,768]{1,0:T(8,128)(2,1)S(1)}, bf16[256,768]{1,0:T(8,128)(2,1)S(1)}, u32[]{:S(2)}, u32[]{:S(2)}) collective-permute-start(bf16[256,768]{1,0:T(8,128)(2,1)S(1)} %fusion.5.refs_1_.refs_6_), channel_id=1, source_target_pairs={{0,2},{1,3},{2,0},{3,1},{4,6},{5,7},{6,4},{7,5},{8,10},{9,11},{10,... | collective-permute-start | bytes 1179656 | tf_op jit(solution)/shard_map/ppermute | solution.py:28
  138.1 18.3 %collective-permute-start.14 = (bf16[256,768]{1,0:T(8,128)(2,1)S(1)}, bf16[256,768]{1,0:T(8,128)(2,1)S(1)}, u32[]{:S(2)}, u32[]{:S(2)}) collective-permute-start(bf16[256,768]{1,0:T(8,128)(2,1)S(1)} %fusion.5.refs_1_.refs_6_), channel_id=1, source_target_pairs={{0,1},{1,2},{2,3},{3,0},{4,5},{5,6},{6,7},{7,4},{8,9},{9,10},{10,1... | collective-permute-start | bytes 1179656 | tf_op jit(solution)/shard_map/ppermute | solution.py:28
  146.7 9.7 %copy-start.12 = (bf16[256,768]{1,0:T(8,128)(2,1)}, bf16[256,768]{1,0:T(8,128)(2,1)S(1)}, u32[]{:S(2)}) copy-start(bf16[256,768]{1,0:T(8,128)(2,1)S(1)} %collective-permute-done.16.refs_4_) | copy-start | bytes 1179652
  155.5 1.0 copy-start.16
  169.6 6.1 %collective-permute-start.19 = (bf16[256,512]{1,0:T(8,128)(2,1)}, bf16[256,512]{1,0:T(8,128)(2,1)S(1)}, u32[]{:S(2)}, u32[]{:S(2)}) collective-permute-start(bf16[256,512]{1,0:T(8,128)(2,1)} %get-tuple-element.21.refs_1_), channel_id=1, source_target_pairs={{0,3},{1,0},{2,1},{3,2},{4,7},{5,4},{6,5},{7,6},{8,11},{9,8},{10,9... | collective-permute-start | bytes 786440 | tf_op jit(solution)/shard_map/ppermute | solution.py:28
  169.6 14.2 %collective-permute-start.18 = (bf16[256,512]{1,0:T(8,128)(2,1)}, bf16[256,512]{1,0:T(8,128)(2,1)S(1)}, u32[]{:S(2)}, u32[]{:S(2)}) collective-permute-start(bf16[256,512]{1,0:T(8,128)(2,1)} %get-tuple-element.21.refs_1_), channel_id=1, source_target_pairs={{0,2},{1,3},{2,0},{3,1},{4,6},{5,7},{6,4},{7,5},{8,10},{9,11},{10,... | collective-permute-start | bytes 786440 | tf_op jit(solution)/shard_map/ppermute | solution.py:28
  171.1 12.9 %collective-permute-start.17 = (bf16[256,512]{1,0:T(8,128)(2,1)}, bf16[256,512]{1,0:T(8,128)(2,1)S(1)}, u32[]{:S(2)}, u32[]{:S(2)}) collective-permute-start(bf16[256,512]{1,0:T(8,128)(2,1)} %get-tuple-element.21.refs_1_), channel_id=1, source_target_pairs={{0,1},{1,2},{2,3},{3,0},{4,5},{5,6},{6,7},{7,4},{8,9},{9,10},{10,1... | collective-permute-start | bytes 786440 | tf_op jit(solution)/shard_map/ppermute | solution.py:28
  175.7 8.3 %copy-start.23 = (bf16[256,512]{1,0:T(8,128)(2,1)}, bf16[256,512]{1,0:T(8,128)(2,1)S(1)}, u32[]{:S(2)}) copy-start(bf16[256,512]{1,0:T(8,128)(2,1)S(1)} %collective-permute-done.19.refs_4_) | copy-start | bytes 786436
  189.4 10.9 %collective-permute-start.20 = (bf16[256,768]{1,0:T(8,128)(2,1)}, bf16[256,768]{1,0:T(8,128)(2,1)S(1)}, u32[]{:S(2)}, u32[]{:S(2)}) collective-permute-start(bf16[256,768]{1,0:T(8,128)(2,1)} %shard_map.96), channel_id=1, source_target_pairs={{0,4},{4,8},{8,12},{1,5},{5,9},{9,13},{2,6},{6,10},{10,14},{3,7},{... | collective-permute-start | bytes 1179656 | tf_op jit(solution)/shard_map/ppermute | solution.py:14
  200.5 19.9 %copy-start.1 = (bf16[256,768]{1,0:T(8,128)(2,1)}, bf16[256,768]{1,0:T(8,128)(2,1)S(1)}, u32[]{:S(2)}) copy-start(bf16[256,768]{1,0:T(8,128)(2,1)S(1)} %fusion.7.refs_1_.refs_6_) | copy-start | bytes 1179652
  200.5 8.6 %collective-permute-start.23 = (bf16[256,768]{1,0:T(8,128)(2,1)S(1)}, bf16[256,768]{1,0:T(8,128)(2,1)S(1)}, u32[]{:S(2)}, u32[]{:S(2)}) collective-permute-start(bf16[256,768]{1,0:T(8,128)(2,1)S(1)} %fusion.7.refs_1_.refs_6_), channel_id=1, source_target_pairs={{0,3},{1,0},{2,1},{3,2},{4,7},{5,4},{6,5},{7,6},{8,11},{9,8},{10,9... | collective-permute-start | bytes 1179656 | tf_op jit(solution)/shard_map/ppermute | solution.py:28
  200.6 19.6 %collective-permute-start.22 = (bf16[256,768]{1,0:T(8,128)(2,1)S(1)}, bf16[256,768]{1,0:T(8,128)(2,1)S(1)}, u32[]{:S(2)}, u32[]{:S(2)}) collective-permute-start(bf16[256,768]{1,0:T(8,128)(2,1)S(1)} %fusion.7.refs_1_.refs_6_), channel_id=1, source_target_pairs={{0,2},{1,3},{2,0},{3,1},{4,6},{5,7},{6,4},{7,5},{8,10},{9,11},{10,... | collective-permute-start | bytes 1179656 | tf_op jit(solution)/shard_map/ppermute | solution.py:28
  202.1 18.3 %collective-permute-start.21 = (bf16[256,768]{1,0:T(8,128)(2,1)S(1)}, bf16[256,768]{1,0:T(8,128)(2,1)S(1)}, u32[]{:S(2)}, u32[]{:S(2)}) collective-permute-start(bf16[256,768]{1,0:T(8,128)(2,1)S(1)} %fusion.7.refs_1_.refs_6_), channel_id=1, source_target_pairs={{0,1},{1,2},{2,3},{3,0},{4,5},{5,6},{6,7},{7,4},{8,9},{9,10},{10,1... | collective-permute-start | bytes 1179656 | tf_op jit(solution)/shard_map/ppermute | solution.py:28
  209.2 11.2 %copy-start.9 = (bf16[256,768]{1,0:T(8,128)(2,1)}, bf16[256,768]{1,0:T(8,128)(2,1)S(1)}, u32[]{:S(2)}) copy-start(bf16[256,768]{1,0:T(8,128)(2,1)S(1)} %collective-permute-done.23.refs_4_) | copy-start | bytes 1179652
  233.6 18.5 %copy-start.5 = (bf16[256,768]{1,0:T(8,128)(2,1)S(1)}, bf16[256,768]{1,0:T(8,128)(2,1)}, u32[]{:S(2)}) copy-start(bf16[256,768]{1,0:T(8,128)(2,1)} %shard_map.92) | copy-start | bytes 1179652
  233.6 18.5 %copy-start.6 = (bf16[256,768]{1,0:T(8,128)(2,1)S(1)}, bf16[256,768]{1,0:T(8,128)(2,1)}, u32[]{:S(2)}) copy-start(bf16[256,768]{1,0:T(8,128)(2,1)} %shard_map.94) | copy-start | bytes 1179652
  233.6 18.5 %copy-start.7 = (bf16[256,768]{1,0:T(8,128)(2,1)S(1)}, bf16[256,768]{1,0:T(8,128)(2,1)}, u32[]{:S(2)}) copy-start(bf16[256,768]{1,0:T(8,128)(2,1)} %shard_map.96) | copy-start | bytes 1179652
  233.6 6.9 %collective-permute-start.26 = (bf16[256,512]{1,0:T(8,128)(2,1)}, bf16[256,512]{1,0:T(8,128)(2,1)S(1)}, u32[]{:S(2)}, u32[]{:S(2)}) collective-permute-start(bf16[256,512]{1,0:T(8,128)(2,1)} %get-tuple-element.24.refs_1_), channel_id=1, source_target_pairs={{0,3},{1,0},{2,1},{3,2},{4,7},{5,4},{6,5},{7,6},{8,11},{9,8},{10,9... | collective-permute-start | bytes 786440 | tf_op jit(solution)/shard_map/ppermute | solution.py:28
  233.7 12.7 %collective-permute-start.25 = (bf16[256,512]{1,0:T(8,128)(2,1)}, bf16[256,512]{1,0:T(8,128)(2,1)S(1)}, u32[]{:S(2)}, u32[]{:S(2)}) collective-permute-start(bf16[256,512]{1,0:T(8,128)(2,1)} %get-tuple-element.24.refs_1_), channel_id=1, source_target_pairs={{0,2},{1,3},{2,0},{3,1},{4,6},{5,7},{6,4},{7,5},{8,10},{9,11},{10,... | collective-permute-start | bytes 786440 | tf_op jit(solution)/shard_map/ppermute | solution.py:28
  234.4 12.9 %collective-permute-start.24 = (bf16[256,512]{1,0:T(8,128)(2,1)}, bf16[256,512]{1,0:T(8,128)(2,1)S(1)}, u32[]{:S(2)}, u32[]{:S(2)}) collective-permute-start(bf16[256,512]{1,0:T(8,128)(2,1)} %get-tuple-element.24.refs_1_), channel_id=1, source_target_pairs={{0,1},{1,2},{2,3},{3,0},{4,5},{5,6},{6,7},{7,4},{8,9},{9,10},{10,1... | collective-permute-start | bytes 786440 | tf_op jit(solution)/shard_map/ppermute | solution.py:28
  240.5 6.8 %copy-start.24 = (bf16[256,512]{1,0:T(8,128)(2,1)}, bf16[256,512]{1,0:T(8,128)(2,1)S(1)}, u32[]{:S(2)}) copy-start(bf16[256,512]{1,0:T(8,128)(2,1)S(1)} %collective-permute-done.26.refs_4_) | copy-start | bytes 786436
  246.3 0.9 copy-start.28
  (13 other events, 9.7 us)

commit v5 on v4

--- a/solution.py
+++ b/solution.py
@@ -24,22 +24,33 @@
 
 def spread_over_seq(block):
     count = lax.axis_size("seq")
-    return [block] + [
-        lax.ppermute(block, "seq", [(source, (source + shift) % count) for source in range(count)])
-        for shift in range(1, count)
+    here = lax.axis_index("seq")
+    partner = jnp.bitwise_xor(here, 1)
+    to_partner = [(source, source ^ 1) for source in range(count)]
+    across = [
+        lax.ppermute(block, "seq", [(source, (source + step) % count) for source in range(count)])
+        for step in range(2, count, 2)
     ]
+    from_partner = lax.ppermute(block, "seq", to_partner)
+    relayed = [lax.ppermute(part, "seq", to_partner) for part in across]
+    sources = (
+        [here]
+        + [jnp.remainder(here - step, count) for step in range(2, count, 2)]
+        + [partner]
+        + [jnp.remainder(partner - step, count) for step in range(2, count, 2)]
+    )
+    return [block] + across + [from_partner] + relayed, sources
 
 
 def block_kernel(*refs):
     where_ref = refs[0]
-    count = (len(refs) - 9) // 1
+    count = len(refs) - 9
     part_refs = refs[1 : 1 + count]
     scale_ref, weights_ref, keys_ref, values_ref = refs[1 + count : 5 + count]
     heads_ref, keys_out, values_out = refs[5 + count : 8 + count]
     shaped_ref = refs[8 + count]
     start = where_ref[0]
     patch_count = where_ref[1]
-    here = where_ref[2]
     head_dim = keys_ref.shape[2]
     seq_len = keys_ref.shape[1]
     span, width = part_refs[0].shape
@@ -52,11 +63,11 @@
         centred = [part - row_mean for part in parts]
         spread = sum(jnp.sum(c * c, axis=-1, keepdims=True) for c in centred) / features
         inverse = lax.rsqrt(spread + epsilon)
-        for shift in range(count):
-            slot = lax.rem(here - shift + count, count)
+        for part in range(count):
+            slot = where_ref[2 + part]
             shift_scale = scale_ref[slot]
             shaped_ref[slot] = (
-                (centred[shift] * inverse) * (1.0 + shift_scale[1:2]) + shift_scale[0:1]
+                (centred[part] * inverse) * (1.0 + shift_scale[1:2]) + shift_scale[0:1]
             ).astype(jnp.bfloat16)
 
     mixed = sum(
@@ -136,14 +147,13 @@
     weights_ref, own_ref, gate_ref = refs[1 + count : 4 + count]
     out_ref = refs[4 + count]
     patch_count = where_ref[1]
-    here = where_ref[2]
     projected = sum(
         jnp.dot(
-            part_refs[shift][...],
-            weights_ref[lax.rem(here - shift + count, count)],
+            part_refs[part][...],
+            weights_ref[where_ref[2 + part]],
             preferred_element_type=jnp.float32,
         )
-        for shift in range(count)
+        for part in range(count)
     )
     updated = own_ref[...].astype(jnp.float32) + gate_ref[...] * projected
     live = lax.broadcasted_iota(jnp.int32, updated.shape, 0) < patch_count
@@ -181,7 +191,6 @@
     branch_gates,
 ):
     section_index = lax.axis_index("section")
-    seq_index = lax.axis_index("seq")
     patches = patch_sizes_list.shape[0]
     biggest_patch_span = transit_states.shape[1]
     columns = incoming_states.shape[1]
@@ -203,17 +212,30 @@
         patch_index = jnp.remainder(turn_number - section_index, patches)
         patch_count = pick_entry(patch_sizes_list, patch_index)
         patch_start = pick_entry(starts, patch_index)
-        where = jnp.stack([patch_start, patch_count, seq_index]).astype(jnp.int32)
+        where = jnp.stack([patch_start, patch_count]).astype(jnp.int32)
         live_rows = row_numbers < patch_count
         entry_patch = lax.dynamic_slice_in_dim(
             entering_ext, starts[turn_number], biggest_patch_span, 0
         )
         own_rows = jnp.where(section_index == 0, entry_patch, earlier_result)
         own_rows = jnp.where(live_rows[:, None], own_rows, jnp.zeros_like(own_rows))
+        row_parts, row_sources = spread_over_seq(own_rows)
         head_rows, key_cache, value_cache = attend_block(
-            spread_over_seq(own_rows), shift_scale, qkv_weights, key_cache, value_cache, where
-        )
-        updated = leave_block(spread_over_seq(head_rows), out_weights, own_rows, gating_here, where)
+            row_parts,
+            shift_scale,
+            qkv_weights,
+            key_cache,
+            value_cache,
+            jnp.concatenate([where, jnp.stack(row_sources).astype(jnp.int32)]),
+        )
+        head_parts, head_sources = spread_over_seq(head_rows)
+        updated = leave_block(
+            head_parts,
+            out_weights,
+            own_rows,
+            gating_here,
+            jnp.concatenate([where, jnp.stack(head_sources).astype(jnp.int32)]),
+        )
         results.append(updated)
         if turn_number + 1 < patches:
             earlier_result = passed_along(updated, "section", 1)

time: 255 us -> 217 us (0.85)
  waiting for transfers between devices: 130 us -> 89.8 us
  other arithmetic: 14.2 us -> 6.73 us
  local copies, waits for them, and re-layouts: 11.6 us -> 18.7 us
  starting transfers between devices: 24.7 us -> 27.4 us
    ppermute x24, waiting for transfers between devices: 116 us -> 70.3 us  [the longest x8 64.2 us: spread_over_seq(): lax.ppermute(block, 'seq', [(source, (source + step) % count) for source...]
    another operation x5 -> x1, other arithmetic: 7.69 us -> 0.18 us  [the longest x4 7.51 us: shards(): where = jnp.stack([patch_start, patch_count, seq_index]).astype(jnp.int32)]
    concatenate x0 -> x4, local copies, waits for them, and re-layouts: none -> 7.46 us  [shards(): jnp.concatenate([where, jnp.stack(head_sources).astype(jnp.int32)])]
    ppermute x3, waiting for transfers between devices: 14.5 us -> 19.5 us  [passed_along(): lax.ppermute(value, axis, [(source, source + steps) for source in range(l...]
  transfers between devices with their start and end apart: 27 -> 27, of which waited for: 25 -> 15; matrix products, arithmetic and copies ran while one was open for 4% -> 4% of each run, Pallas kernels for 0% -> 0%
where the time goes in v5:
time: 217 us
  waiting for transfers between devices  89.8 us (41%)
  Pallas kernels  66.6 us (31%)
  starting transfers between devices  27.4 us (13%)
  local copies, waits for them, and re-layouts  18.7 us (9%)
  between operations  7.54 us (3%)
  other arithmetic  6.73 us (3%)
    ppermute x8, waiting for transfers between devices, spread_over_seq(): lax.ppermute(block, 'seq', [(source, (source + step) % count) for source...  64.2 us
    pallas_call x4, Pallas kernels, attend_block(): pl.pallas_call(block_kernel, grid_spec=grid_spec, out_shape=[jax.ShapeDty...  50.1 us
    ppermute x3, waiting for transfers between devices, passed_along(): lax.ppermute(value, axis, [(source, source + steps) for source in range(l...  19.5 us
    pallas_call x4, Pallas kernels, leave_block(): pl.pallas_call(exit_kernel, in_specs=[smem] + [vmem] * (count + 3), out_s...  16.5 us
    ppermute x8, starting transfers between devices, spread_over_seq(): lax.ppermute(block, 'seq', [(source, (source + step) % count) for source...  13.9 us
    ppermute x3, starting transfers between devices, passed_along(): lax.ppermute(value, axis, [(source, source + steps) for source in range(l...  12.5 us
    unnamed x70, local copies, waits for them, and re-layouts  10.6 us
    concatenate x4, local copies, waits for them, and re-layouts, shards(): jnp.concatenate([where, jnp.stack(head_sources).astype(jnp.int32)])  7.46 us
  transfers between devices with their start and end apart: 27, of which 15 were waited for; matrix products, arithmetic and copies ran while one was open for 4% of the time, Pallas kernels for 0%

profile of v5, /device:TPU:0, one launch (start us, length us, event | category | flops | bytes accessed | tf_op | source)
XLA Modules:
  0.0 216.7 jit_solution(9629505676773524308)
XLA Ops:
  0.0 2.2 %copy.29 = bf16[1,4,768,128]{3,2,1,0:T(8,128)(2,1)} copy(bf16[1,4,768,128]{3,2,1,0:T(8,128)(2,1)} %param.12) | data formatting | bytes 1572864
  2.2 2.1 copy.30
  4.5 0.8 fusion.9
  8.7 3.0 %collective-permute-start = (bf16[256,768]{1,0:T(8,128)(2,1)S(1)}, bf16[256,768]{1,0:T(8,128)(2,1)S(1)}, u32[]{:S(2)}, u32[]{:S(2)}) collective-permute-start(bf16[256,768]{1,0:T(8,128)(2,1)S(1)} %fusion.1.refs_1_.refs_6_), channel_id=1, source_target_pairs={{0,2},{1,3},{2,0},{3,1},{4,6},{5,7},{6,4},{7,5},{8,10},{9,11},{10,... | collective-permute-start | bytes 1179656 | tf_op jit(solution)/shard_map/ppermute | solution.py:31
  11.7 9.1 %collective-permute-done.refs_2_ = bf16[256,768]{1,0:T(8,128)(2,1)S(1)} collective-permute-done((bf16[256,768]{1,0:T(8,128)(2,1)S(1)}, bf16[256,768]{1,0:T(8,128)(2,1)S(1)}, u32[]{:S(2)}, u32[]{:S(2)}) %collective-permute-start) | collective-permute-done | bytes 393248 | tf_op jit(solution)/shard_map/ppermute | solution.py:31
  20.8 1.8 concatenate.27.refs_0_
  22.7 0.7 copy-done.9
  23.5 12.5 %shard_map.91 = (bf16[256,512]{1,0:T(8,128)(2,1)}, bf16[4,768,128]{2,1,0:T(8,128)(2,1)}, bf16[4,768,128]{2,1,0:T(8,128)(2,1)}) custom-call(s32[6]{0:T(128)} %concatenate.27.refs_0_, bf16[256,768]{1,0:T(8,128)(2,1)} %copy-done.1, bf16[256,768]{1,0:T(8,128)(2,1)} %copy-done.8, ...), custom_call_target="tpu_custom_call", output_to_operand_aliasing={{1}: (7, {}), {2}: (8, {})} | custom-call | tf_op jit(solution)/shard_map/pallas_call | solution.py:130
  36.1 1.8 collective-permute-start.3
  38.0 7.0 %collective-permute-done.3.refs_2_ = bf16[256,512]{1,0:T(8,128)(2,1)S(1)} collective-permute-done((bf16[256,512]{1,0:T(8,128)(2,1)}, bf16[256,512]{1,0:T(8,128)(2,1)S(1)}, u32[]{:S(2)}, u32[]{:S(2)}) %collective-permute-start.3) | collective-permute-done | bytes 262176 | tf_op jit(solution)/shard_map/ppermute | solution.py:31
  45.0 1.5 collective-permute-done.5.refs_4_
  47.2 4.1 %shard_map.92 = bf16[256,768]{1,0:T(8,128)(2,1)} custom-call(s32[6]{0:T(128)} %concatenate.27.refs_0_, bf16[256,512]{1,0:T(8,128)(2,1)} %get-tuple-element.15.refs_1_, bf16[256,512]{1,0:T(8,128)(2,1)} %copy-done.21, bf16[256,512]{1,0:T(8,128)(2,1)} %copy-done.25, bf16[256,512]{1,0:T(8,128)(2,1)} %copy-done.29, bf16[4,512,768]{2,1,0:T(8,128)(2,1)} %bitcast.41, ...), custom_call_target="tpu_custom_call" | custom-call | tf_op jit(solution)/shard_map/pallas_call | solution.py:168
  51.4 3.7 %collective-permute-start.6 = (bf16[256,768]{1,0:T(8,128)(2,1)}, bf16[256,768]{1,0:T(8,128)(2,1)S(1)}, u32[]{:S(2)}, u32[]{:S(2)}) collective-permute-start(bf16[256,768]{1,0:T(8,128)(2,1)} %shard_map.92), channel_id=1, source_target_pairs={{0,4},{4,8},{8,12},{1,5},{5,9},{9,13},{2,6},{6,10},{10,14},{3,7},{... | collective-permute-start | bytes 1179656 | tf_op jit(solution)/shard_map/ppermute | solution.py:14
  57.4 6.7 %collective-permute-done.6 = bf16[256,768]{1,0:T(8,128)(2,1)S(1)} collective-permute-done((bf16[256,768]{1,0:T(8,128)(2,1)}, bf16[256,768]{1,0:T(8,128)(2,1)S(1)}, u32[]{:S(2)}, u32[]{:S(2)}) %collective-permute-start.6) | collective-permute-done | bytes 393248 | tf_op jit(solution)/shard_map/ppermute | solution.py:14
  64.3 1.6 collective-permute-start.7
  65.9 8.8 %collective-permute-done.7.refs_2_ = bf16[256,768]{1,0:T(8,128)(2,1)S(1)} collective-permute-done((bf16[256,768]{1,0:T(8,128)(2,1)S(1)}, bf16[256,768]{1,0:T(8,128)(2,1)S(1)}, u32[]{:S(2)}, u32[]{:S(2)}) %collective-permute-start.7) | collective-permute-done | bytes 393248 | tf_op jit(solution)/shard_map/ppermute | solution.py:31
  74.7 1.9 concatenate.29.refs_0_
  76.6 0.7 copy-done.15
  77.5 12.5 %shard_map.93 = (bf16[256,512]{1,0:T(8,128)(2,1)}, bf16[4,768,128]{2,1,0:T(8,128)(2,1)}, bf16[4,768,128]{2,1,0:T(8,128)(2,1)}) custom-call(s32[6]{0:T(128)} %concatenate.29.refs_0_, bf16[256,768]{1,0:T(8,128)(2,1)} %copy-done.3, bf16[256,768]{1,0:T(8,128)(2,1)} %copy-done.13, ...), custom_call_target="tpu_custom_call", output_to_operand_aliasing={{1}: (7, {}), {2}: (8, {})} | custom-call | tf_op jit(solution)/shard_map/pallas_call | solution.py:130
  90.0 1.5 collective-permute-start.10
  91.7 7.2 %collective-permute-done.10.refs_2_ = bf16[256,512]{1,0:T(8,128)(2,1)S(1)} collective-permute-done((bf16[256,512]{1,0:T(8,128)(2,1)}, bf16[256,512]{1,0:T(8,128)(2,1)S(1)}, u32[]{:S(2)}, u32[]{:S(2)}) %collective-permute-start.10) | collective-permute-done | bytes 262176 | tf_op jit(solution)/shard_map/ppermute | solution.py:31
  98.9 1.5 collective-permute-done.12.refs_4_
  100.4 0.7 copy-done.30
  101.2 4.1 %shard_map.94 = bf16[256,768]{1,0:T(8,128)(2,1)} custom-call(s32[6]{0:T(128)} %concatenate.29.refs_0_, bf16[256,512]{1,0:T(8,128)(2,1)} %get-tuple-element.18.refs_1_, bf16[256,512]{1,0:T(8,128)(2,1)} %copy-done.22, bf16[256,512]{1,0:T(8,128)(2,1)} %copy-done.26, bf16[256,512]{1,0:T(8,128)(2,1)} %copy-done.30, bf16[4,512,768]{2,1,0:T(8,128)(2,1)} %bitcast.42, ...), custom_call_target="tpu_custom_call" | custom-call | tf_op jit(solution)/shard_map/pallas_call | solution.py:168
  105.3 4.5 %collective-permute-start.13 = (bf16[256,768]{1,0:T(8,128)(2,1)}, bf16[256,768]{1,0:T(8,128)(2,1)S(1)}, u32[]{:S(2)}, u32[]{:S(2)}) collective-permute-start(bf16[256,768]{1,0:T(8,128)(2,1)} %shard_map.94), channel_id=1, source_target_pairs={{0,4},{4,8},{8,12},{1,5},{5,9},{9,13},{2,6},{6,10},{10,14},{3,7},{... | collective-permute-start | bytes 1179656 | tf_op jit(solution)/shard_map/ppermute | solution.py:14
  112.3 6.2 %collective-permute-done.13 = bf16[256,768]{1,0:T(8,128)(2,1)S(1)} collective-permute-done((bf16[256,768]{1,0:T(8,128)(2,1)}, bf16[256,768]{1,0:T(8,128)(2,1)S(1)}, u32[]{:S(2)}, u32[]{:S(2)}) %collective-permute-start.13) | collective-permute-done | bytes 393248 | tf_op jit(solution)/shard_map/ppermute | solution.py:14
  118.8 1.6 collective-permute-start.14
  120.3 8.8 %collective-permute-done.14.refs_2_ = bf16[256,768]{1,0:T(8,128)(2,1)S(1)} collective-permute-done((bf16[256,768]{1,0:T(8,128)(2,1)S(1)}, bf16[256,768]{1,0:T(8,128)(2,1)S(1)}, u32[]{:S(2)}, u32[]{:S(2)}) %collective-permute-start.14) | collective-permute-done | bytes 393248 | tf_op jit(solution)/shard_map/ppermute | solution.py:31
  129.2 1.9 concatenate.30.refs_0_
  131.1 0.7 copy-done.16
  132.0 12.5 %shard_map.95 = (bf16[256,512]{1,0:T(8,128)(2,1)}, bf16[4,768,128]{2,1,0:T(8,128)(2,1)}, bf16[4,768,128]{2,1,0:T(8,128)(2,1)}) custom-call(s32[6]{0:T(128)} %concatenate.30.refs_0_, bf16[256,768]{1,0:T(8,128)(2,1)} %copy-done.4, bf16[256,768]{1,0:T(8,128)(2,1)} %copy-done.14, ...), custom_call_target="tpu_custom_call", output_to_operand_aliasing={{1}: (7, {}), {2}: (8, {})} | custom-call | tf_op jit(solution)/shard_map/pallas_call | solution.py:130
  144.5 1.5 collective-permute-start.17
  146.2 7.2 %collective-permute-done.17.refs_2_ = bf16[256,512]{1,0:T(8,128)(2,1)S(1)} collective-permute-done((bf16[256,512]{1,0:T(8,128)(2,1)}, bf16[256,512]{1,0:T(8,128)(2,1)S(1)}, u32[]{:S(2)}, u32[]{:S(2)}) %collective-permute-start.17) | collective-permute-done | bytes 262176 | tf_op jit(solution)/shard_map/ppermute | solution.py:31
  153.5 1.5 collective-permute-done.19.refs_4_
  155.7 4.1 %shard_map.96 = bf16[256,768]{1,0:T(8,128)(2,1)} custom-call(s32[6]{0:T(128)} %concatenate.30.refs_0_, bf16[256,512]{1,0:T(8,128)(2,1)} %get-tuple-element.21.refs_1_, bf16[256,512]{1,0:T(8,128)(2,1)} %copy-done.23, bf16[256,512]{1,0:T(8,128)(2,1)} %copy-done.27, bf16[256,512]{1,0:T(8,128)(2,1)} %copy-done.31, bf16[4,512,768]{2,1,0:T(8,128)(2,1)} %bitcast.43, ...), custom_call_target="tpu_custom_call" | custom-call | tf_op jit(solution)/shard_map/pallas_call | solution.py:168
  159.8 4.3 %collective-permute-start.20 = (bf16[256,768]{1,0:T(8,128)(2,1)}, bf16[256,768]{1,0:T(8,128)(2,1)S(1)}, u32[]{:S(2)}, u32[]{:S(2)}) collective-permute-start(bf16[256,768]{1,0:T(8,128)(2,1)} %shard_map.96), channel_id=1, source_target_pairs={{0,4},{4,8},{8,12},{1,5},{5,9},{9,13},{2,6},{6,10},{10,14},{3,7},{... | collective-permute-start | bytes 1179656 | tf_op jit(solution)/shard_map/ppermute | solution.py:14
  166.4 6.6 %collective-permute-done.20 = bf16[256,768]{1,0:T(8,128)(2,1)S(1)} collective-permute-done((bf16[256,768]{1,0:T(8,128)(2,1)}, bf16[256,768]{1,0:T(8,128)(2,1)S(1)}, u32[]{:S(2)}, u32[]{:S(2)}) %collective-permute-start.20) | collective-permute-done | bytes 393248 | tf_op jit(solution)/shard_map/ppermute | solution.py:14
  173.3 1.6 collective-permute-start.21
  174.9 8.8 %collective-permute-done.21.refs_2_ = bf16[256,768]{1,0:T(8,128)(2,1)S(1)} collective-permute-done((bf16[256,768]{1,0:T(8,128)(2,1)S(1)}, bf16[256,768]{1,0:T(8,128)(2,1)S(1)}, u32[]{:S(2)}, u32[]{:S(2)}) %collective-permute-start.21) | collective-permute-done | bytes 393248 | tf_op jit(solution)/shard_map/ppermute | solution.py:31
  183.7 1.9 concatenate.31.refs_0_
  185.6 0.7 copy-done.12
  186.5 12.5 %shard_map.97 = (bf16[256,512]{1,0:T(8,128)(2,1)}, bf16[4,768,128]{2,1,0:T(8,128)(2,1)}, bf16[4,768,128]{2,1,0:T(8,128)(2,1)}) custom-call(s32[6]{0:T(128)} %concatenate.31.refs_0_, bf16[256,768]{1,0:T(8,128)(2,1)} %copy-done.2, bf16[256,768]{1,0:T(8,128)(2,1)} %copy-done.11, ...), custom_call_target="tpu_custom_call", output_to_operand_aliasing={{1}: (7, {}), {2}: (8, {})} | custom-call | tf_op jit(solution)/shard_map/pallas_call | solution.py:130
  199.0 1.5 collective-permute-start.24
  200.8 7.2 %collective-permute-done.24.refs_2_ = bf16[256,512]{1,0:T(8,128)(2,1)S(1)} collective-permute-done((bf16[256,512]{1,0:T(8,128)(2,1)}, bf16[256,512]{1,0:T(8,128)(2,1)S(1)}, u32[]{:S(2)}, u32[]{:S(2)}) %collective-permute-start.24) | collective-permute-done | bytes 262176 | tf_op jit(solution)/shard_map/ppermute | solution.py:31
  208.0 1.5 collective-permute-done.26.refs_4_
  209.6 0.7 copy-done.32
  210.3 4.1 %shard_map.98 = bf16[256,768]{1,0:T(8,128)(2,1)} custom-call(s32[6]{0:T(128)} %concatenate.31.refs_0_, bf16[256,512]{1,0:T(8,128)(2,1)} %get-tuple-element.24.refs_1_, bf16[256,512]{1,0:T(8,128)(2,1)} %copy-done.24, bf16[256,512]{1,0:T(8,128)(2,1)} %copy-done.28, bf16[256,512]{1,0:T(8,128)(2,1)} %copy-done.32, bf16[4,512,768]{2,1,0:T(8,128)(2,1)} %bitcast.44, ...), custom_call_target="tpu_custom_call" | custom-call | tf_op jit(solution)/shard_map/pallas_call | solution.py:168
  214.4 2.3 %maximum_bitcast_fusion = bf16[4,1,256,768]{3,2,1,0:T(8,128)(2,1)} fusion(bf16[1,256,768]{2,1,0:T(8,128)(2,1)} %bitcast.50, bf16[1,256,768]{2,1,0:T(8,128)(2,1)S(1)} %bitcast.49, bf16[1,256,768]{2,1,0:T(8,128)(2,1)S(1)} %bitcast.48, bf16[1,256,768]{2,1,0:T(8,128)(2,1)S(1)} %bitcast.47), kind=kLoop, calls=%fused_computation.4 | loop fusion | flops 2359296 | bytes 3145728 | tf_op jit(solution)/shard_map/broadcast_in_dim | solution.py:242
  (100 shorter events, 7.2 us)
Async XLA Ops:
  0.0 8.5 %copy-start = (bf16[768,768]{1,0:T(8,128)(2,1)S(1)}, bf16[768,768]{1,0:T(8,128)(2,1)}, u32[]{:S(2)}) copy-start(bf16[768,768]{1,0:T(8,128)(2,1)} %param.9) | copy-start | bytes 3538948
  0.0 8.5 %copy-start.20 = (bf16[1,256,768]{2,1,0:T(8,128)(2,1)S(1)}, bf16[1,256,768]{2,1,0:T(8,128)(2,1)}, u32[]{:S(2)}) copy-start(bf16[1,256,768]{2,1,0:T(8,128)(2,1)} %param.10) | copy-start | bytes 1179652
  0.0 4.3 %copy-start.33 = (s32[4]{0:T(128)S(1)}, s32[4]{0:T(128)}, u32[]{:S(2)}) copy-start(s32[4]{0:T(128)} %param.11) | copy-start | bytes 52
  8.7 14.0 %copy-start.1 = (bf16[256,768]{1,0:T(8,128)(2,1)}, bf16[256,768]{1,0:T(8,128)(2,1)S(1)}, u32[]{:S(2)}) copy-start(bf16[256,768]{1,0:T(8,128)(2,1)S(1)} %fusion.1.refs_1_.refs_6_) | copy-start | bytes 1179652
  8.7 12.1 %collective-permute-start = (bf16[256,768]{1,0:T(8,128)(2,1)S(1)}, bf16[256,768]{1,0:T(8,128)(2,1)S(1)}, u32[]{:S(2)}, u32[]{:S(2)}) collective-permute-start(bf16[256,768]{1,0:T(8,128)(2,1)S(1)} %fusion.1.refs_1_.refs_6_), channel_id=1, source_target_pairs={{0,2},{1,3},{2,0},{3,1},{4,6},{5,7},{6,4},{7,5},{8,10},{9,11},{10,... | collective-permute-start | bytes 1179656 | tf_op jit(solution)/shard_map/ppermute | solution.py:31
  11.7 10.9 %collective-permute-start.1 = (bf16[256,768]{1,0:T(8,128)(2,1)S(1)}, bf16[256,768]{1,0:T(8,128)(2,1)S(1)}, u32[]{:S(2)}, u32[]{:S(2)}) collective-permute-start(bf16[256,768]{1,0:T(8,128)(2,1)S(1)} %fusion.1.refs_1_.refs_6_), channel_id=1, source_target_pairs={{0,1},{1,0},{2,3},{3,2},{4,5},{5,4},{6,7},{7,6},{8,9},{9,8},{10,11... | collective-permute-start | bytes 1179656 | tf_op jit(solution)/shard_map/ppermute | solution.py:34
  20.8 1.8 copy-start.8
  20.8 1.8 collective-permute-start.2
  36.1 8.9 %collective-permute-start.3 = (bf16[256,512]{1,0:T(8,128)(2,1)}, bf16[256,512]{1,0:T(8,128)(2,1)S(1)}, u32[]{:S(2)}, u32[]{:S(2)}) collective-permute-start(bf16[256,512]{1,0:T(8,128)(2,1)} %get-tuple-element.15.refs_1_), channel_id=1, source_target_pairs={{0,2},{1,3},{2,0},{3,1},{4,6},{5,7},{6,4},{7,5},{8,10},{9,11},{10,... | collective-permute-start | bytes 786440 | tf_op jit(solution)/shard_map/ppermute | solution.py:31
  37.8 7.2 %collective-permute-start.4 = (bf16[256,512]{1,0:T(8,128)(2,1)}, bf16[256,512]{1,0:T(8,128)(2,1)S(1)}, u32[]{:S(2)}, u32[]{:S(2)}) collective-permute-start(bf16[256,512]{1,0:T(8,128)(2,1)} %get-tuple-element.15.refs_1_), channel_id=1, source_target_pairs={{0,1},{1,0},{2,3},{3,2},{4,5},{5,4},{6,7},{7,6},{8,9},{9,8},{10,11... | collective-permute-start | bytes 786440 | tf_op jit(solution)/shard_map/ppermute | solution.py:34
  45.0 1.5 copy-start.21
  45.0 1.5 collective-permute-start.5
  45.0 1.5 copy-start.25
  51.4 12.7 %collective-permute-start.6 = (bf16[256,768]{1,0:T(8,128)(2,1)}, bf16[256,768]{1,0:T(8,128)(2,1)S(1)}, u32[]{:S(2)}, u32[]{:S(2)}) collective-permute-start(bf16[256,768]{1,0:T(8,128)(2,1)} %shard_map.92), channel_id=1, source_target_pairs={{0,4},{4,8},{8,12},{1,5},{5,9},{9,13},{2,6},{6,10},{10,14},{3,7},{... | collective-permute-start | bytes 1179656 | tf_op jit(solution)/shard_map/ppermute | solution.py:14
  64.3 12.3 %copy-start.3 = (bf16[256,768]{1,0:T(8,128)(2,1)}, bf16[256,768]{1,0:T(8,128)(2,1)S(1)}, u32[]{:S(2)}) copy-start(bf16[256,768]{1,0:T(8,128)(2,1)S(1)} %fusion.3.refs_1_.refs_6_) | copy-start | bytes 1179652
  64.3 10.4 %collective-permute-start.7 = (bf16[256,768]{1,0:T(8,128)(2,1)S(1)}, bf16[256,768]{1,0:T(8,128)(2,1)S(1)}, u32[]{:S(2)}, u32[]{:S(2)}) collective-permute-start(bf16[256,768]{1,0:T(8,128)(2,1)S(1)} %fusion.3.refs_1_.refs_6_), channel_id=1, source_target_pairs={{0,2},{1,3},{2,0},{3,1},{4,6},{5,7},{6,4},{7,5},{8,10},{9,11},{10,... | collective-permute-start | bytes 1179656 | tf_op jit(solution)/shard_map/ppermute | solution.py:31
  65.8 10.7 %collective-permute-start.8 = (bf16[256,768]{1,0:T(8,128)(2,1)S(1)}, bf16[256,768]{1,0:T(8,128)(2,1)S(1)}, u32[]{:S(2)}, u32[]{:S(2)}) collective-permute-start(bf16[256,768]{1,0:T(8,128)(2,1)S(1)} %fusion.3.refs_1_.refs_6_), channel_id=1, source_target_pairs={{0,1},{1,0},{2,3},{3,2},{4,5},{5,4},{6,7},{7,6},{8,9},{9,8},{10,11... | collective-permute-start | bytes 1179656 | tf_op jit(solution)/shard_map/ppermute | solution.py:34
  74.7 1.9 copy-start.13
  74.7 1.9 collective-permute-start.9
  90.0 8.9 %collective-permute-start.10 = (bf16[256,512]{1,0:T(8,128)(2,1)}, bf16[256,512]{1,0:T(8,128)(2,1)S(1)}, u32[]{:S(2)}, u32[]{:S(2)}) collective-permute-start(bf16[256,512]{1,0:T(8,128)(2,1)} %get-tuple-element.18.refs_1_), channel_id=1, source_target_pairs={{0,2},{1,3},{2,0},{3,1},{4,6},{5,7},{6,4},{7,5},{8,10},{9,11},{10,... | collective-permute-start | bytes 786440 | tf_op jit(solution)/shard_map/ppermute | solution.py:31
  91.5 7.4 %collective-permute-start.11 = (bf16[256,512]{1,0:T(8,128)(2,1)}, bf16[256,512]{1,0:T(8,128)(2,1)S(1)}, u32[]{:S(2)}, u32[]{:S(2)}) collective-permute-start(bf16[256,512]{1,0:T(8,128)(2,1)} %get-tuple-element.18.refs_1_), channel_id=1, source_target_pairs={{0,1},{1,0},{2,3},{3,2},{4,5},{5,4},{6,7},{7,6},{8,9},{9,8},{10,11... | collective-permute-start | bytes 786440 | tf_op jit(solution)/shard_map/ppermute | solution.py:34
  98.9 1.5 copy-start.22
  98.9 1.5 collective-permute-start.12
  98.9 1.5 copy-start.26
  105.3 13.2 %collective-permute-start.13 = (bf16[256,768]{1,0:T(8,128)(2,1)}, bf16[256,768]{1,0:T(8,128)(2,1)S(1)}, u32[]{:S(2)}, u32[]{:S(2)}) collective-permute-start(bf16[256,768]{1,0:T(8,128)(2,1)} %shard_map.94), channel_id=1, source_target_pairs={{0,4},{4,8},{8,12},{1,5},{5,9},{9,13},{2,6},{6,10},{10,14},{3,7},{... | collective-permute-start | bytes 1179656 | tf_op jit(solution)/shard_map/ppermute | solution.py:14
  118.8 12.4 %copy-start.4 = (bf16[256,768]{1,0:T(8,128)(2,1)}, bf16[256,768]{1,0:T(8,128)(2,1)S(1)}, u32[]{:S(2)}) copy-start(bf16[256,768]{1,0:T(8,128)(2,1)S(1)} %fusion.5.refs_1_.refs_6_) | copy-start | bytes 1179652
  118.8 10.4 %collective-permute-start.14 = (bf16[256,768]{1,0:T(8,128)(2,1)S(1)}, bf16[256,768]{1,0:T(8,128)(2,1)S(1)}, u32[]{:S(2)}, u32[]{:S(2)}) collective-permute-start(bf16[256,768]{1,0:T(8,128)(2,1)S(1)} %fusion.5.refs_1_.refs_6_), channel_id=1, source_target_pairs={{0,2},{1,3},{2,0},{3,1},{4,6},{5,7},{6,4},{7,5},{8,10},{9,11},{10,... | collective-permute-start | bytes 1179656 | tf_op jit(solution)/shard_map/ppermute | solution.py:31
  120.3 10.8 %collective-permute-start.15 = (bf16[256,768]{1,0:T(8,128)(2,1)S(1)}, bf16[256,768]{1,0:T(8,128)(2,1)S(1)}, u32[]{:S(2)}, u32[]{:S(2)}) collective-permute-start(bf16[256,768]{1,0:T(8,128)(2,1)S(1)} %fusion.5.refs_1_.refs_6_), channel_id=1, source_target_pairs={{0,1},{1,0},{2,3},{3,2},{4,5},{5,4},{6,7},{7,6},{8,9},{9,8},{10,11... | collective-permute-start | bytes 1179656 | tf_op jit(solution)/shard_map/ppermute | solution.py:34
  129.2 2.0 copy-start.14
  129.2 1.9 collective-permute-start.16
  144.5 8.9 %collective-permute-start.17 = (bf16[256,512]{1,0:T(8,128)(2,1)}, bf16[256,512]{1,0:T(8,128)(2,1)S(1)}, u32[]{:S(2)}, u32[]{:S(2)}) collective-permute-start(bf16[256,512]{1,0:T(8,128)(2,1)} %get-tuple-element.21.refs_1_), channel_id=1, source_target_pairs={{0,2},{1,3},{2,0},{3,1},{4,6},{5,7},{6,4},{7,5},{8,10},{9,11},{10,... | collective-permute-start | bytes 786440 | tf_op jit(solution)/shard_map/ppermute | solution.py:31
  146.0 7.5 %collective-permute-start.18 = (bf16[256,512]{1,0:T(8,128)(2,1)}, bf16[256,512]{1,0:T(8,128)(2,1)S(1)}, u32[]{:S(2)}, u32[]{:S(2)}) collective-permute-start(bf16[256,512]{1,0:T(8,128)(2,1)} %get-tuple-element.21.refs_1_), channel_id=1, source_target_pairs={{0,1},{1,0},{2,3},{3,2},{4,5},{5,4},{6,7},{7,6},{8,9},{9,8},{10,11... | collective-permute-start | bytes 786440 | tf_op jit(solution)/shard_map/ppermute | solution.py:34
  153.4 1.5 copy-start.23
  153.4 1.5 collective-permute-start.19
  153.5 1.5 copy-start.27
  159.8 13.2 %collective-permute-start.20 = (bf16[256,768]{1,0:T(8,128)(2,1)}, bf16[256,768]{1,0:T(8,128)(2,1)S(1)}, u32[]{:S(2)}, u32[]{:S(2)}) collective-permute-start(bf16[256,768]{1,0:T(8,128)(2,1)} %shard_map.96), channel_id=1, source_target_pairs={{0,4},{4,8},{8,12},{1,5},{5,9},{9,13},{2,6},{6,10},{10,14},{3,7},{... | collective-permute-start | bytes 1179656 | tf_op jit(solution)/shard_map/ppermute | solution.py:14
  173.3 12.3 %copy-start.2 = (bf16[256,768]{1,0:T(8,128)(2,1)}, bf16[256,768]{1,0:T(8,128)(2,1)S(1)}, u32[]{:S(2)}) copy-start(bf16[256,768]{1,0:T(8,128)(2,1)S(1)} %fusion.7.refs_1_.refs_6_) | copy-start | bytes 1179652
  173.3 10.4 %collective-permute-start.21 = (bf16[256,768]{1,0:T(8,128)(2,1)S(1)}, bf16[256,768]{1,0:T(8,128)(2,1)S(1)}, u32[]{:S(2)}, u32[]{:S(2)}) collective-permute-start(bf16[256,768]{1,0:T(8,128)(2,1)S(1)} %fusion.7.refs_1_.refs_6_), channel_id=1, source_target_pairs={{0,2},{1,3},{2,0},{3,1},{4,6},{5,7},{6,4},{7,5},{8,10},{9,11},{10,... | collective-permute-start | bytes 1179656 | tf_op jit(solution)/shard_map/ppermute | solution.py:31
  174.9 10.7 %collective-permute-start.22 = (bf16[256,768]{1,0:T(8,128)(2,1)S(1)}, bf16[256,768]{1,0:T(8,128)(2,1)S(1)}, u32[]{:S(2)}, u32[]{:S(2)}) collective-permute-start(bf16[256,768]{1,0:T(8,128)(2,1)S(1)} %fusion.7.refs_1_.refs_6_), channel_id=1, source_target_pairs={{0,1},{1,0},{2,3},{3,2},{4,5},{5,4},{6,7},{7,6},{8,9},{9,8},{10,11... | collective-permute-start | bytes 1179656 | tf_op jit(solution)/shard_map/ppermute | solution.py:34
  183.7 1.9 copy-start.11
  183.7 1.9 collective-permute-start.23
  199.0 15.4 %copy-start.5 = (bf16[256,768]{1,0:T(8,128)(2,1)S(1)}, bf16[256,768]{1,0:T(8,128)(2,1)}, u32[]{:S(2)}) copy-start(bf16[256,768]{1,0:T(8,128)(2,1)} %shard_map.92) | copy-start | bytes 1179652
  199.0 15.4 %copy-start.6 = (bf16[256,768]{1,0:T(8,128)(2,1)S(1)}, bf16[256,768]{1,0:T(8,128)(2,1)}, u32[]{:S(2)}) copy-start(bf16[256,768]{1,0:T(8,128)(2,1)} %shard_map.94) | copy-start | bytes 1179652
  199.0 15.4 %copy-start.7 = (bf16[256,768]{1,0:T(8,128)(2,1)S(1)}, bf16[256,768]{1,0:T(8,128)(2,1)}, u32[]{:S(2)}) copy-start(bf16[256,768]{1,0:T(8,128)(2,1)} %shard_map.96) | copy-start | bytes 1179652
  199.0 9.0 %collective-permute-start.24 = (bf16[256,512]{1,0:T(8,128)(2,1)}, bf16[256,512]{1,0:T(8,128)(2,1)S(1)}, u32[]{:S(2)}, u32[]{:S(2)}) collective-permute-start(bf16[256,512]{1,0:T(8,128)(2,1)} %get-tuple-element.24.refs_1_), channel_id=1, source_target_pairs={{0,2},{1,3},{2,0},{3,1},{4,6},{5,7},{6,4},{7,5},{8,10},{9,11},{10,... | collective-permute-start | bytes 786440 | tf_op jit(solution)/shard_map/ppermute | solution.py:31
  200.6 7.5 %collective-permute-start.25 = (bf16[256,512]{1,0:T(8,128)(2,1)}, bf16[256,512]{1,0:T(8,128)(2,1)S(1)}, u32[]{:S(2)}, u32[]{:S(2)}) collective-permute-start(bf16[256,512]{1,0:T(8,128)(2,1)} %get-tuple-element.24.refs_1_), channel_id=1, source_target_pairs={{0,1},{1,0},{2,3},{3,2},{4,5},{5,4},{6,7},{7,6},{8,9},{9,8},{10,11... | collective-permute-start | bytes 786440 | tf_op jit(solution)/shard_map/ppermute | solution.py:34
  208.0 1.5 copy-start.24
  208.0 1.5 collective-permute-start.26
  (13 other events, 11.0 us)

commit v6 on v5

--- a/solution.py
+++ b/solution.py
@@ -24,8 +24,6 @@
 
 def spread_over_seq(block):
     count = lax.axis_size("seq")
-    here = lax.axis_index("seq")
-    partner = jnp.bitwise_xor(here, 1)
     to_partner = [(source, source ^ 1) for source in range(count)]
     across = [
         lax.ppermute(block, "seq", [(source, (source + step) % count) for source in range(count)])
@@ -33,13 +31,19 @@
     ]
     from_partner = lax.ppermute(block, "seq", to_partner)
     relayed = [lax.ppermute(part, "seq", to_partner) for part in across]
-    sources = (
-        [here]
-        + [jnp.remainder(here - step, count) for step in range(2, count, 2)]
-        + [partner]
-        + [jnp.remainder(partner - step, count) for step in range(2, count, 2)]
-    )
-    return [block] + across + [from_partner] + relayed, sources
+    return [block] + across + [from_partner] + relayed
+
+
+def kernel_table(patch_start, patch_count):
+    count = lax.axis_size("seq")
+    here = lax.axis_index("seq")
+    chips = count // 2
+    entry = jnp.arange(count + 2) - 2
+    base = jnp.where(entry < chips, here, jnp.bitwise_xor(here, 1))
+    sources = jnp.remainder(base - 2 * jnp.remainder(entry, chips) + count, count)
+    return jnp.where(entry == -2, patch_start, jnp.where(entry == -1, patch_count, sources)).astype(
+        jnp.int32
+    )
 
 
 def block_kernel(*refs):
@@ -102,7 +106,7 @@
     )
 
 
-def attend_block(parts, shift_scale, qkv_weights, key_cache, value_cache, where):
+def attend_block(parts, shift_scale, qkv_weights, key_cache, value_cache, where, in_place):
     count = len(parts)
     span, width = parts[0].shape
     heads_here, seq_len, head_dim = key_cache.shape
@@ -135,7 +139,7 @@
             jax.ShapeDtypeStruct(key_cache.shape, key_cache.dtype),
             jax.ShapeDtypeStruct(value_cache.shape, value_cache.dtype),
         ],
-        input_output_aliases={count + 3: 1, count + 4: 2},
+        input_output_aliases={count + 3: 1, count + 4: 2} if in_place else {},
         compiler_params=pltpu.CompilerParams(dimension_semantics=("arbitrary",)),
     )(where, *parts, scale_blocks, qkv_weights, key_cache, value_cache)
 
@@ -212,29 +216,24 @@
         patch_index = jnp.remainder(turn_number - section_index, patches)
         patch_count = pick_entry(patch_sizes_list, patch_index)
         patch_start = pick_entry(starts, patch_index)
-        where = jnp.stack([patch_start, patch_count]).astype(jnp.int32)
+        where = kernel_table(patch_start, patch_count)
         live_rows = row_numbers < patch_count
         entry_patch = lax.dynamic_slice_in_dim(
             entering_ext, starts[turn_number], biggest_patch_span, 0
         )
         own_rows = jnp.where(section_index == 0, entry_patch, earlier_result)
         own_rows = jnp.where(live_rows[:, None], own_rows, jnp.zeros_like(own_rows))
-        row_parts, row_sources = spread_over_seq(own_rows)
         head_rows, key_cache, value_cache = attend_block(
-            row_parts,
+            spread_over_seq(own_rows),
             shift_scale,
             qkv_weights,
             key_cache,
             value_cache,
-            jnp.concatenate([where, jnp.stack(row_sources).astype(jnp.int32)]),
-        )
-        head_parts, head_sources = spread_over_seq(head_rows)
+            where,
+            turn_number > 0,
+        )
         updated = leave_block(
-            head_parts,
-            out_weights,
-            own_rows,
-            gating_here,
-            jnp.concatenate([where, jnp.stack(head_sources).astype(jnp.int32)]),
+            spread_over_seq(head_rows), out_weights, own_rows, gating_here, where
         )
         results.append(updated)
         if turn_number + 1 < patches:

time: 217 us -> 217 us (level)
  local copies, waits for them, and re-layouts: 18.7 us -> 6.79 us
  other arithmetic: 6.73 us -> 15.3 us
  waiting for transfers between devices: 89.8 us -> 92.5 us
    concatenate x4 -> x0, local copies, waits for them, and re-layouts: 7.46 us -> none  [shards(): jnp.concatenate([where, jnp.stack(head_sources).astype(jnp.int32)])]
    select_n x0 -> x2, other arithmetic: none -> 6.14 us  [kernel_table(): jnp.where(entry == -2, patch_start, jnp.where(entry == -1, patch_count, s...]
    unnamed x70 -> x64, local copies, waits for them, and re-layouts: 10.6 us -> 6.12 us
    ppermute x8, waiting for transfers between devices: 6.08 us -> 9.48 us  [spread_over_seq(): relayed = [lax.ppermute(part, 'seq', to_partner) for part in across]]
  transfers between devices with their start and end apart: 27 -> 27, of which waited for: 15 -> 17; matrix products, arithmetic and copies ran while one was open for 4% -> 4% of each run, Pallas kernels for 0% -> 0%
where the time goes in v6:
time: 217 us; the launch traced here: 216 us
  waiting for transfers between devices  92.5 us (43%)
  Pallas kernels  66.7 us (31%)
  starting transfers between devices  27 us (12%)
  other arithmetic  15.3 us (7%)
  between operations  7.8 us (4%)
  local copies, waits for them, and re-layouts  6.79 us (3%)
    ppermute x8, waiting for transfers between devices, spread_over_seq(): lax.ppermute(block, 'seq', [(source, (source + step) % count) for source...  63.9 us
    pallas_call x4, Pallas kernels, attend_block(): pl.pallas_call(block_kernel, grid_spec=grid_spec, out_shape=[jax.ShapeDty...  50.1 us
    ppermute x3, waiting for transfers between devices, passed_along(): lax.ppermute(value, axis, [(source, source + steps) for source in range(l...  19.1 us
    pallas_call x4, Pallas kernels, leave_block(): pl.pallas_call(exit_kernel, in_specs=[smem] + [vmem] * (count + 3), out_s...  16.5 us
    ppermute x8, starting transfers between devices, spread_over_seq(): lax.ppermute(block, 'seq', [(source, (source + step) % count) for source...  14 us
    ppermute x3, starting transfers between devices, passed_along(): lax.ppermute(value, axis, [(source, source + steps) for source in range(l...  12.5 us
    ppermute x8, waiting for transfers between devices, spread_over_seq(): relayed = [lax.ppermute(part, 'seq', to_partner) for part in across]  9.48 us
    select_n x2, other arithmetic, kernel_table(): jnp.where(entry == -2, patch_start, jnp.where(entry == -1, patch_count, s...  6.14 us
  transfers between devices with their start and end apart: 27, of which 17 were waited for; matrix products, arithmetic and copies ran while one was open for 4% of the time, Pallas kernels for 0%

profile of v6, /device:TPU:0, one launch (start us, length us, event | category | flops | bytes accessed | tf_op | source)
XLA Modules:
  0.0 216.0 jit_solution(16902211617094683405)
XLA Ops:
  0.0 0.8 reduce-window.9
  0.8 1.5 fusion.8
  5.5 1.3 fusion.1.refs_1_.refs_6_
  6.8 3.0 %collective-permute-start = (bf16[256,768]{1,0:T(8,128)(2,1)S(1)}, bf16[256,768]{1,0:T(8,128)(2,1)S(1)}, u32[]{:S(2)}, u32[]{:S(2)}) collective-permute-start(bf16[256,768]{1,0:T(8,128)(2,1)S(1)} %fusion.1.refs_1_.refs_6_), channel_id=1, source_target_pairs={{0,2},{1,3},{2,0},{3,1},{4,6},{5,7},{6,4},{7,5},{8,10},{9,11},{10,... | collective-permute-start | bytes 1179656 | tf_op jit(solution)/shard_map/ppermute | solution.py:29
  9.8 9.1 %collective-permute-done.refs_2_ = bf16[256,768]{1,0:T(8,128)(2,1)S(1)} collective-permute-done((bf16[256,768]{1,0:T(8,128)(2,1)S(1)}, bf16[256,768]{1,0:T(8,128)(2,1)S(1)}, u32[]{:S(2)}, u32[]{:S(2)}) %collective-permute-start) | collective-permute-done | bytes 393248 | tf_op jit(solution)/shard_map/ppermute | solution.py:29
  19.0 1.8 select_select_fusion.3
  20.8 0.7 copy-done.10
  21.7 12.6 %shard_map.91 = (bf16[256,512]{1,0:T(8,128)(2,1)}, bf16[4,768,128]{2,1,0:T(8,128)(2,1)}, bf16[4,768,128]{2,1,0:T(8,128)(2,1)}) custom-call(s32[6]{0:T(128)} %get-tuple-element.33.refs_0_, bf16[256,768]{1,0:T(8,128)(2,1)} %copy-done.2, bf16[256,768]{1,0:T(8,128)(2,1)} %copy-done.8, bf16[256,768]{1,0:T(8,128)(2,1)} %copy-done.10, bf16[256,768]{1,0:T(8,128)(2,1)} %copy-done.12, ...), custom_call_target="tpu_custom_call" | custom-call | tf_op jit(solution)/shard_map/pallas_call | solution.py:134
  34.2 1.7 collective-permute-start.3
  36.2 7.0 %collective-permute-done.3.refs_2_ = bf16[256,512]{1,0:T(8,128)(2,1)S(1)} collective-permute-done((bf16[256,512]{1,0:T(8,128)(2,1)}, bf16[256,512]{1,0:T(8,128)(2,1)S(1)}, u32[]{:S(2)}, u32[]{:S(2)}) %collective-permute-start.3) | collective-permute-done | bytes 262176 | tf_op jit(solution)/shard_map/ppermute | solution.py:29
  43.2 1.5 collective-permute-done.5.refs_4_
  45.4 4.2 %shard_map.92 = bf16[256,768]{1,0:T(8,128)(2,1)} custom-call(s32[6]{0:T(128)} %get-tuple-element.33.refs_0_, bf16[256,512]{1,0:T(8,128)(2,1)} %get-tuple-element.15.refs_1_, bf16[256,512]{1,0:T(8,128)(2,1)} %copy-done.20, bf16[256,512]{1,0:T(8,128)(2,1)} %copy-done.24, bf16[256,512]{1,0:T(8,128)(2,1)} %copy-done.28, bf16[4,512,768]{2,1,0:T(8,128)(2,1)} %bitcast.29, ...), custom_call_target="tpu_custom_call" | custom-call | tf_op jit(solution)/shard_map/pallas_call | solution.py:172
  49.6 3.7 %collective-permute-start.6 = (bf16[256,768]{1,0:T(8,128)(2,1)}, bf16[256,768]{1,0:T(8,128)(2,1)S(1)}, u32[]{:S(2)}, u32[]{:S(2)}) collective-permute-start(bf16[256,768]{1,0:T(8,128)(2,1)} %shard_map.92), channel_id=1, source_target_pairs={{0,4},{4,8},{8,12},{1,5},{5,9},{9,13},{2,6},{6,10},{10,14},{3,7},{... | collective-permute-start | bytes 1179656 | tf_op jit(solution)/shard_map/ppermute | solution.py:14
  56.0 6.3 %collective-permute-done.6 = bf16[256,768]{1,0:T(8,128)(2,1)S(1)} collective-permute-done((bf16[256,768]{1,0:T(8,128)(2,1)}, bf16[256,768]{1,0:T(8,128)(2,1)S(1)}, u32[]{:S(2)}, u32[]{:S(2)}) %collective-permute-start.6) | collective-permute-done | bytes 393248 | tf_op jit(solution)/shard_map/ppermute | solution.py:14
  62.5 1.6 collective-permute-start.7
  64.1 8.8 %collective-permute-done.7.refs_2_ = bf16[256,768]{1,0:T(8,128)(2,1)S(1)} collective-permute-done((bf16[256,768]{1,0:T(8,128)(2,1)S(1)}, bf16[256,768]{1,0:T(8,128)(2,1)S(1)}, u32[]{:S(2)}, u32[]{:S(2)}) %collective-permute-start.7) | collective-permute-done | bytes 393248 | tf_op jit(solution)/shard_map/ppermute | solution.py:29
  72.9 4.3 %select_select_fusion.2 = (s32[6]{0:T(128)}, s32[6]{0:T(128)}, s32[6]{0:T(128)}) fusion(s32[6]{0:T(128)S(1)} %get-tuple-element.34, s32[]{:T(128)} %get-tuple-element.45, s32[]{:T(128)} %get-tuple-element.28, s32[]{:T(128)} %get-tuple-element.43, s32[]{:T(128)} %get-tuple-element.27, s32[]{:T(128)} %get-tuple-element.44, s32[]{:T(128)} %get-tuple-element.26), kind=kLoop, calls=%fused_computation.48 | loop fusion | flops 54 | bytes 120 | tf_op jit(solution)/shard_map/jit(_where)/select_n | solution.py:44
  77.3 0.7 copy-done.11
  78.1 12.5 %shard_map.93 = (bf16[256,512]{1,0:T(8,128)(2,1)}, bf16[4,768,128]{2,1,0:T(8,128)(2,1)}, bf16[4,768,128]{2,1,0:T(8,128)(2,1)}) custom-call(s32[6]{0:T(128)} %get-tuple-element.40.refs_0_, bf16[256,768]{1,0:T(8,128)(2,1)} %copy-done.1, bf16[256,768]{1,0:T(8,128)(2,1)} %copy-done.9, ...), custom_call_target="tpu_custom_call", output_to_operand_aliasing={{1}: (7, {}), {2}: (8, {})} | custom-call | tf_op jit(solution)/shard_map/pallas_call | solution.py:134
  90.6 1.5 collective-permute-start.10
  92.4 7.2 %collective-permute-done.10.refs_2_ = bf16[256,512]{1,0:T(8,128)(2,1)S(1)} collective-permute-done((bf16[256,512]{1,0:T(8,128)(2,1)}, bf16[256,512]{1,0:T(8,128)(2,1)S(1)}, u32[]{:S(2)}, u32[]{:S(2)}) %collective-permute-start.10) | collective-permute-done | bytes 262176 | tf_op jit(solution)/shard_map/ppermute | solution.py:29
  99.6 1.5 collective-permute-done.12.refs_4_
  101.1 0.7 copy-done.29
  101.8 4.1 %shard_map.94 = bf16[256,768]{1,0:T(8,128)(2,1)} custom-call(s32[6]{0:T(128)} %get-tuple-element.40.refs_0_, bf16[256,512]{1,0:T(8,128)(2,1)} %get-tuple-element.18.refs_1_, bf16[256,512]{1,0:T(8,128)(2,1)} %copy-done.21, bf16[256,512]{1,0:T(8,128)(2,1)} %copy-done.25, bf16[256,512]{1,0:T(8,128)(2,1)} %copy-done.29, bf16[4,512,768]{2,1,0:T(8,128)(2,1)} %bitcast.30, ...), custom_call_target="tpu_custom_call" | custom-call | tf_op jit(solution)/shard_map/pallas_call | solution.py:172
  106.0 4.5 %collective-permute-start.13 = (bf16[256,768]{1,0:T(8,128)(2,1)}, bf16[256,768]{1,0:T(8,128)(2,1)S(1)}, u32[]{:S(2)}, u32[]{:S(2)}) collective-permute-start(bf16[256,768]{1,0:T(8,128)(2,1)} %shard_map.94), channel_id=1, source_target_pairs={{0,4},{4,8},{8,12},{1,5},{5,9},{9,13},{2,6},{6,10},{10,14},{3,7},{... | collective-permute-start | bytes 1179656 | tf_op jit(solution)/shard_map/ppermute | solution.py:14
  113.0 6.2 %collective-permute-done.13 = bf16[256,768]{1,0:T(8,128)(2,1)S(1)} collective-permute-done((bf16[256,768]{1,0:T(8,128)(2,1)}, bf16[256,768]{1,0:T(8,128)(2,1)S(1)}, u32[]{:S(2)}, u32[]{:S(2)}) %collective-permute-start.13) | collective-permute-done | bytes 393248 | tf_op jit(solution)/shard_map/ppermute | solution.py:14
  119.4 1.6 collective-permute-start.14
  121.0 8.8 %collective-permute-done.14.refs_2_ = bf16[256,768]{1,0:T(8,128)(2,1)S(1)} collective-permute-done((bf16[256,768]{1,0:T(8,128)(2,1)S(1)}, bf16[256,768]{1,0:T(8,128)(2,1)S(1)}, u32[]{:S(2)}, u32[]{:S(2)}) %collective-permute-start.14) | collective-permute-done | bytes 393248 | tf_op jit(solution)/shard_map/ppermute | solution.py:29
  129.9 1.7 collective-permute-done.16.refs_4_
  131.6 0.7 copy-done.19
  132.3 12.5 %shard_map.95 = (bf16[256,512]{1,0:T(8,128)(2,1)}, bf16[4,768,128]{2,1,0:T(8,128)(2,1)}, bf16[4,768,128]{2,1,0:T(8,128)(2,1)}) custom-call(s32[6]{0:T(128)} %get-tuple-element.41.refs_0_, bf16[256,768]{1,0:T(8,128)(2,1)} %copy-done.4, bf16[256,768]{1,0:T(8,128)(2,1)} %copy-done.15, ...), custom_call_target="tpu_custom_call", output_to_operand_aliasing={{1}: (7, {}), {2}: (8, {})} | custom-call | tf_op jit(solution)/shard_map/pallas_call | solution.py:134
  144.8 1.5 collective-permute-start.17
  146.3 7.1 %collective-permute-done.17.refs_2_ = bf16[256,512]{1,0:T(8,128)(2,1)S(1)} collective-permute-done((bf16[256,512]{1,0:T(8,128)(2,1)}, bf16[256,512]{1,0:T(8,128)(2,1)S(1)}, u32[]{:S(2)}, u32[]{:S(2)}) %collective-permute-start.17) | collective-permute-done | bytes 262176 | tf_op jit(solution)/shard_map/ppermute | solution.py:29
  153.4 1.5 collective-permute-done.19.refs_4_
  155.7 4.1 %shard_map.96 = bf16[256,768]{1,0:T(8,128)(2,1)} custom-call(s32[6]{0:T(128)} %get-tuple-element.41.refs_0_, bf16[256,512]{1,0:T(8,128)(2,1)} %get-tuple-element.21.refs_1_, bf16[256,512]{1,0:T(8,128)(2,1)} %copy-done.22, bf16[256,512]{1,0:T(8,128)(2,1)} %copy-done.26, bf16[256,512]{1,0:T(8,128)(2,1)} %copy-done.30, bf16[4,512,768]{2,1,0:T(8,128)(2,1)} %bitcast.31, ...), custom_call_target="tpu_custom_call" | custom-call | tf_op jit(solution)/shard_map/pallas_call | solution.py:172
  159.8 4.3 %collective-permute-start.20 = (bf16[256,768]{1,0:T(8,128)(2,1)}, bf16[256,768]{1,0:T(8,128)(2,1)S(1)}, u32[]{:S(2)}, u32[]{:S(2)}) collective-permute-start(bf16[256,768]{1,0:T(8,128)(2,1)} %shard_map.96), channel_id=1, source_target_pairs={{0,4},{4,8},{8,12},{1,5},{5,9},{9,13},{2,6},{6,10},{10,14},{3,7},{... | collective-permute-start | bytes 1179656 | tf_op jit(solution)/shard_map/ppermute | solution.py:14
  166.4 6.7 %collective-permute-done.20 = bf16[256,768]{1,0:T(8,128)(2,1)S(1)} collective-permute-done((bf16[256,768]{1,0:T(8,128)(2,1)}, bf16[256,768]{1,0:T(8,128)(2,1)S(1)}, u32[]{:S(2)}, u32[]{:S(2)}) %collective-permute-start.20) | collective-permute-done | bytes 393248 | tf_op jit(solution)/shard_map/ppermute | solution.py:14
  173.3 1.6 collective-permute-start.21
  174.8 8.8 %collective-permute-done.21.refs_2_ = bf16[256,768]{1,0:T(8,128)(2,1)S(1)} collective-permute-done((bf16[256,768]{1,0:T(8,128)(2,1)S(1)}, bf16[256,768]{1,0:T(8,128)(2,1)S(1)}, u32[]{:S(2)}, u32[]{:S(2)}) %collective-permute-start.21) | collective-permute-done | bytes 393248 | tf_op jit(solution)/shard_map/ppermute | solution.py:29
  183.7 1.7 collective-permute-done.23.refs_4_
  185.4 0.8 copy-done.18
  186.1 12.5 %shard_map.97 = (bf16[256,512]{1,0:T(8,128)(2,1)}, bf16[4,768,128]{2,1,0:T(8,128)(2,1)}, bf16[4,768,128]{2,1,0:T(8,128)(2,1)}) custom-call(s32[6]{0:T(128)} %get-tuple-element.42.refs_0_, bf16[256,768]{1,0:T(8,128)(2,1)} %copy-done.3, bf16[256,768]{1,0:T(8,128)(2,1)} %copy-done.14, ...), custom_call_target="tpu_custom_call", output_to_operand_aliasing={{1}: (7, {}), {2}: (8, {})} | custom-call | tf_op jit(solution)/shard_map/pallas_call | solution.py:134
  198.7 1.6 collective-permute-start.24
  200.3 7.1 %collective-permute-done.24.refs_2_ = bf16[256,512]{1,0:T(8,128)(2,1)S(1)} collective-permute-done((bf16[256,512]{1,0:T(8,128)(2,1)}, bf16[256,512]{1,0:T(8,128)(2,1)S(1)}, u32[]{:S(2)}, u32[]{:S(2)}) %collective-permute-start.24) | collective-permute-done | bytes 262176 | tf_op jit(solution)/shard_map/ppermute | solution.py:29
  207.3 1.5 collective-permute-done.26.refs_4_
  208.9 0.7 copy-done.31
  209.6 4.1 %shard_map.98 = bf16[256,768]{1,0:T(8,128)(2,1)} custom-call(s32[6]{0:T(128)} %get-tuple-element.42.refs_0_, bf16[256,512]{1,0:T(8,128)(2,1)} %get-tuple-element.24.refs_1_, bf16[256,512]{1,0:T(8,128)(2,1)} %copy-done.23, bf16[256,512]{1,0:T(8,128)(2,1)} %copy-done.27, bf16[256,512]{1,0:T(8,128)(2,1)} %copy-done.31, bf16[4,512,768]{2,1,0:T(8,128)(2,1)} %bitcast.32, ...), custom_call_target="tpu_custom_call" | custom-call | tf_op jit(solution)/shard_map/pallas_call | solution.py:172
  213.7 2.3 %maximum_bitcast_fusion = bf16[4,1,256,768]{3,2,1,0:T(8,128)(2,1)} fusion(bf16[1,256,768]{2,1,0:T(8,128)(2,1)} %bitcast.36, bf16[1,256,768]{2,1,0:T(8,128)(2,1)S(1)} %bitcast.35, bf16[1,256,768]{2,1,0:T(8,128)(2,1)S(1)} %bitcast.34, bf16[1,256,768]{2,1,0:T(8,128)(2,1)S(1)} %bitcast.33), kind=kLoop, calls=%fused_computation.4 | loop fusion | flops 2359296 | bytes 3145728 | tf_op jit(solution)/shard_map/broadcast_in_dim | solution.py:241
  (92 shorter events, 6.2 us)
Async XLA Ops:
  6.8 14.0 %copy-start.2 = (bf16[256,768]{1,0:T(8,128)(2,1)}, bf16[256,768]{1,0:T(8,128)(2,1)S(1)}, u32[]{:S(2)}) copy-start(bf16[256,768]{1,0:T(8,128)(2,1)S(1)} %fusion.1.refs_1_.refs_6_) | copy-start | bytes 1179652
  6.8 12.1 %collective-permute-start = (bf16[256,768]{1,0:T(8,128)(2,1)S(1)}, bf16[256,768]{1,0:T(8,128)(2,1)S(1)}, u32[]{:S(2)}, u32[]{:S(2)}) collective-permute-start(bf16[256,768]{1,0:T(8,128)(2,1)S(1)} %fusion.1.refs_1_.refs_6_), channel_id=1, source_target_pairs={{0,2},{1,3},{2,0},{3,1},{4,6},{5,7},{6,4},{7,5},{8,10},{9,11},{10,... | collective-permute-start | bytes 1179656 | tf_op jit(solution)/shard_map/ppermute | solution.py:29
  9.8 10.9 %collective-permute-start.1 = (bf16[256,768]{1,0:T(8,128)(2,1)S(1)}, bf16[256,768]{1,0:T(8,128)(2,1)S(1)}, u32[]{:S(2)}, u32[]{:S(2)}) collective-permute-start(bf16[256,768]{1,0:T(8,128)(2,1)S(1)} %fusion.1.refs_1_.refs_6_), channel_id=1, source_target_pairs={{0,1},{1,0},{2,3},{3,2},{4,5},{5,4},{6,7},{7,6},{8,9},{9,8},{10,11... | collective-permute-start | bytes 1179656 | tf_op jit(solution)/shard_map/ppermute | solution.py:32
  19.0 1.9 copy-start.8
  19.0 1.8 collective-permute-start.2
  34.2 8.9 %collective-permute-start.3 = (bf16[256,512]{1,0:T(8,128)(2,1)}, bf16[256,512]{1,0:T(8,128)(2,1)S(1)}, u32[]{:S(2)}, u32[]{:S(2)}) collective-permute-start(bf16[256,512]{1,0:T(8,128)(2,1)} %get-tuple-element.15.refs_1_), channel_id=1, source_target_pairs={{0,2},{1,3},{2,0},{3,1},{4,6},{5,7},{6,4},{7,5},{8,10},{9,11},{10,... | collective-permute-start | bytes 786440 | tf_op jit(solution)/shard_map/ppermute | solution.py:29
  35.9 7.2 %collective-permute-start.4 = (bf16[256,512]{1,0:T(8,128)(2,1)}, bf16[256,512]{1,0:T(8,128)(2,1)S(1)}, u32[]{:S(2)}, u32[]{:S(2)}) collective-permute-start(bf16[256,512]{1,0:T(8,128)(2,1)} %get-tuple-element.15.refs_1_), channel_id=1, source_target_pairs={{0,1},{1,0},{2,3},{3,2},{4,5},{5,4},{6,7},{7,6},{8,9},{9,8},{10,11... | collective-permute-start | bytes 786440 | tf_op jit(solution)/shard_map/ppermute | solution.py:32
  43.1 1.5 copy-start.20
  43.1 1.5 collective-permute-start.5
  43.1 1.5 copy-start.24
  45.4 16.9 %copy-start = (bf16[768,768]{1,0:T(8,128)(2,1)S(1)}, bf16[768,768]{1,0:T(8,128)(2,1)}, u32[]{:S(2)}) copy-start(bf16[768,768]{1,0:T(8,128)(2,1)} %param.9) | copy-start | bytes 3538948
  49.6 12.7 %collective-permute-start.6 = (bf16[256,768]{1,0:T(8,128)(2,1)}, bf16[256,768]{1,0:T(8,128)(2,1)S(1)}, u32[]{:S(2)}, u32[]{:S(2)}) collective-permute-start(bf16[256,768]{1,0:T(8,128)(2,1)} %shard_map.92), channel_id=1, source_target_pairs={{0,4},{4,8},{8,12},{1,5},{5,9},{9,13},{2,6},{6,10},{10,14},{3,7},{... | collective-permute-start | bytes 1179656 | tf_op jit(solution)/shard_map/ppermute | solution.py:14
  62.5 14.8 %copy-start.1 = (bf16[256,768]{1,0:T(8,128)(2,1)}, bf16[256,768]{1,0:T(8,128)(2,1)S(1)}, u32[]{:S(2)}) copy-start(bf16[256,768]{1,0:T(8,128)(2,1)S(1)} %fusion.3.refs_1_.refs_6_) | copy-start | bytes 1179652
  62.5 10.4 %collective-permute-start.7 = (bf16[256,768]{1,0:T(8,128)(2,1)S(1)}, bf16[256,768]{1,0:T(8,128)(2,1)S(1)}, u32[]{:S(2)}, u32[]{:S(2)}) collective-permute-start(bf16[256,768]{1,0:T(8,128)(2,1)S(1)} %fusion.3.refs_1_.refs_6_), channel_id=1, source_target_pairs={{0,2},{1,3},{2,0},{3,1},{4,6},{5,7},{6,4},{7,5},{8,10},{9,11},{10,... | collective-permute-start | bytes 1179656 | tf_op jit(solution)/shard_map/ppermute | solution.py:29
  64.1 13.2 %collective-permute-start.8 = (bf16[256,768]{1,0:T(8,128)(2,1)S(1)}, bf16[256,768]{1,0:T(8,128)(2,1)S(1)}, u32[]{:S(2)}, u32[]{:S(2)}) collective-permute-start(bf16[256,768]{1,0:T(8,128)(2,1)S(1)} %fusion.3.refs_1_.refs_6_), channel_id=1, source_target_pairs={{0,1},{1,0},{2,3},{3,2},{4,5},{5,4},{6,7},{7,6},{8,9},{9,8},{10,11... | collective-permute-start | bytes 1179656 | tf_op jit(solution)/shard_map/ppermute | solution.py:32
  72.9 4.4 %copy-start.9 = (bf16[256,768]{1,0:T(8,128)(2,1)}, bf16[256,768]{1,0:T(8,128)(2,1)S(1)}, u32[]{:S(2)}) copy-start(bf16[256,768]{1,0:T(8,128)(2,1)S(1)} %collective-permute-done.7.refs_2_) | copy-start | bytes 1179652
  72.9 4.3 %collective-permute-start.9 = (bf16[256,768]{1,0:T(8,128)(2,1)S(1)}, bf16[256,768]{1,0:T(8,128)(2,1)S(1)}, u32[]{:S(2)}, u32[]{:S(2)}) collective-permute-start(bf16[256,768]{1,0:T(8,128)(2,1)S(1)} %collective-permute-done.7.refs_2_), channel_id=1, source_target_pairs={{0,1},{1,0},{2,3},{3,2},{4,5},{5,4},{6,7},{7,6},{8,9},{9,8},{10,11... | collective-permute-start | bytes 1179656 | tf_op jit(solution)/shard_map/ppermute | solution.py:33
  90.6 8.9 %collective-permute-start.10 = (bf16[256,512]{1,0:T(8,128)(2,1)}, bf16[256,512]{1,0:T(8,128)(2,1)S(1)}, u32[]{:S(2)}, u32[]{:S(2)}) collective-permute-start(bf16[256,512]{1,0:T(8,128)(2,1)} %get-tuple-element.18.refs_1_), channel_id=1, source_target_pairs={{0,2},{1,3},{2,0},{3,1},{4,6},{5,7},{6,4},{7,5},{8,10},{9,11},{10,... | collective-permute-start | bytes 786440 | tf_op jit(solution)/shard_map/ppermute | solution.py:29
  92.1 7.4 %collective-permute-start.11 = (bf16[256,512]{1,0:T(8,128)(2,1)}, bf16[256,512]{1,0:T(8,128)(2,1)S(1)}, u32[]{:S(2)}, u32[]{:S(2)}) collective-permute-start(bf16[256,512]{1,0:T(8,128)(2,1)} %get-tuple-element.18.refs_1_), channel_id=1, source_target_pairs={{0,1},{1,0},{2,3},{3,2},{4,5},{5,4},{6,7},{7,6},{8,9},{9,8},{10,11... | collective-permute-start | bytes 786440 | tf_op jit(solution)/shard_map/ppermute | solution.py:32
  99.6 1.5 copy-start.21
  99.6 1.5 collective-permute-start.12
  99.6 1.5 copy-start.25
  106.0 13.2 %collective-permute-start.13 = (bf16[256,768]{1,0:T(8,128)(2,1)}, bf16[256,768]{1,0:T(8,128)(2,1)S(1)}, u32[]{:S(2)}, u32[]{:S(2)}) collective-permute-start(bf16[256,768]{1,0:T(8,128)(2,1)} %shard_map.94), channel_id=1, source_target_pairs={{0,4},{4,8},{8,12},{1,5},{5,9},{9,13},{2,6},{6,10},{10,14},{3,7},{... | collective-permute-start | bytes 1179656 | tf_op jit(solution)/shard_map/ppermute | solution.py:14
  119.4 12.1 %copy-start.4 = (bf16[256,768]{1,0:T(8,128)(2,1)}, bf16[256,768]{1,0:T(8,128)(2,1)S(1)}, u32[]{:S(2)}) copy-start(bf16[256,768]{1,0:T(8,128)(2,1)S(1)} %fusion.5.refs_1_.refs_6_) | copy-start | bytes 1179652
  119.4 10.4 %collective-permute-start.14 = (bf16[256,768]{1,0:T(8,128)(2,1)S(1)}, bf16[256,768]{1,0:T(8,128)(2,1)S(1)}, u32[]{:S(2)}, u32[]{:S(2)}) collective-permute-start(bf16[256,768]{1,0:T(8,128)(2,1)S(1)} %fusion.5.refs_1_.refs_6_), channel_id=1, source_target_pairs={{0,2},{1,3},{2,0},{3,1},{4,6},{5,7},{6,4},{7,5},{8,10},{9,11},{10,... | collective-permute-start | bytes 1179656 | tf_op jit(solution)/shard_map/ppermute | solution.py:29
  121.0 8.8 %collective-permute-start.15 = (bf16[256,768]{1,0:T(8,128)(2,1)S(1)}, bf16[256,768]{1,0:T(8,128)(2,1)S(1)}, u32[]{:S(2)}, u32[]{:S(2)}) collective-permute-start(bf16[256,768]{1,0:T(8,128)(2,1)S(1)} %fusion.5.refs_1_.refs_6_), channel_id=1, source_target_pairs={{0,1},{1,0},{2,3},{3,2},{4,5},{5,4},{6,7},{7,6},{8,9},{9,8},{10,11... | collective-permute-start | bytes 1179656 | tf_op jit(solution)/shard_map/ppermute | solution.py:32
  129.8 1.7 copy-start.15
  129.8 1.7 collective-permute-start.16
  129.8 1.7 copy-start.17
  144.8 8.6 %collective-permute-start.17 = (bf16[256,512]{1,0:T(8,128)(2,1)}, bf16[256,512]{1,0:T(8,128)(2,1)S(1)}, u32[]{:S(2)}, u32[]{:S(2)}) collective-permute-start(bf16[256,512]{1,0:T(8,128)(2,1)} %get-tuple-element.21.refs_1_), channel_id=1, source_target_pairs={{0,2},{1,3},{2,0},{3,1},{4,6},{5,7},{6,4},{7,5},{8,10},{9,11},{10,... | collective-permute-start | bytes 786440 | tf_op jit(solution)/shard_map/ppermute | solution.py:29
  146.3 7.1 %collective-permute-start.18 = (bf16[256,512]{1,0:T(8,128)(2,1)}, bf16[256,512]{1,0:T(8,128)(2,1)S(1)}, u32[]{:S(2)}, u32[]{:S(2)}) collective-permute-start(bf16[256,512]{1,0:T(8,128)(2,1)} %get-tuple-element.21.refs_1_), channel_id=1, source_target_pairs={{0,1},{1,0},{2,3},{3,2},{4,5},{5,4},{6,7},{7,6},{8,9},{9,8},{10,11... | collective-permute-start | bytes 786440 | tf_op jit(solution)/shard_map/ppermute | solution.py:32
  153.4 1.5 copy-start.22
  153.4 1.5 collective-permute-start.19
  153.4 1.5 copy-start.26
  159.8 13.2 %collective-permute-start.20 = (bf16[256,768]{1,0:T(8,128)(2,1)}, bf16[256,768]{1,0:T(8,128)(2,1)S(1)}, u32[]{:S(2)}, u32[]{:S(2)}) collective-permute-start(bf16[256,768]{1,0:T(8,128)(2,1)} %shard_map.96), channel_id=1, source_target_pairs={{0,4},{4,8},{8,12},{1,5},{5,9},{9,13},{2,6},{6,10},{10,14},{3,7},{... | collective-permute-start | bytes 1179656 | tf_op jit(solution)/shard_map/ppermute | solution.py:14
  173.2 12.1 %copy-start.3 = (bf16[256,768]{1,0:T(8,128)(2,1)}, bf16[256,768]{1,0:T(8,128)(2,1)S(1)}, u32[]{:S(2)}) copy-start(bf16[256,768]{1,0:T(8,128)(2,1)S(1)} %fusion.7.refs_1_.refs_6_) | copy-start | bytes 1179652
  173.3 10.4 %collective-permute-start.21 = (bf16[256,768]{1,0:T(8,128)(2,1)S(1)}, bf16[256,768]{1,0:T(8,128)(2,1)S(1)}, u32[]{:S(2)}, u32[]{:S(2)}) collective-permute-start(bf16[256,768]{1,0:T(8,128)(2,1)S(1)} %fusion.7.refs_1_.refs_6_), channel_id=1, source_target_pairs={{0,2},{1,3},{2,0},{3,1},{4,6},{5,7},{6,4},{7,5},{8,10},{9,11},{10,... | collective-permute-start | bytes 1179656 | tf_op jit(solution)/shard_map/ppermute | solution.py:29
  174.8 8.8 %collective-permute-start.22 = (bf16[256,768]{1,0:T(8,128)(2,1)S(1)}, bf16[256,768]{1,0:T(8,128)(2,1)S(1)}, u32[]{:S(2)}, u32[]{:S(2)}) collective-permute-start(bf16[256,768]{1,0:T(8,128)(2,1)S(1)} %fusion.7.refs_1_.refs_6_), channel_id=1, source_target_pairs={{0,1},{1,0},{2,3},{3,2},{4,5},{5,4},{6,7},{7,6},{8,9},{9,8},{10,11... | collective-permute-start | bytes 1179656 | tf_op jit(solution)/shard_map/ppermute | solution.py:32
  183.6 1.7 copy-start.14
  183.7 1.7 collective-permute-start.23
  183.7 1.7 copy-start.16
  198.7 15.0 %copy-start.5 = (bf16[256,768]{1,0:T(8,128)(2,1)S(1)}, bf16[256,768]{1,0:T(8,128)(2,1)}, u32[]{:S(2)}) copy-start(bf16[256,768]{1,0:T(8,128)(2,1)} %shard_map.92) | copy-start | bytes 1179652
  198.7 15.0 %copy-start.6 = (bf16[256,768]{1,0:T(8,128)(2,1)S(1)}, bf16[256,768]{1,0:T(8,128)(2,1)}, u32[]{:S(2)}) copy-start(bf16[256,768]{1,0:T(8,128)(2,1)} %shard_map.94) | copy-start | bytes 1179652
  198.7 15.0 %copy-start.7 = (bf16[256,768]{1,0:T(8,128)(2,1)S(1)}, bf16[256,768]{1,0:T(8,128)(2,1)}, u32[]{:S(2)}) copy-start(bf16[256,768]{1,0:T(8,128)(2,1)} %shard_map.96) | copy-start | bytes 1179652
  198.7 8.6 %collective-permute-start.24 = (bf16[256,512]{1,0:T(8,128)(2,1)}, bf16[256,512]{1,0:T(8,128)(2,1)S(1)}, u32[]{:S(2)}, u32[]{:S(2)}) collective-permute-start(bf16[256,512]{1,0:T(8,128)(2,1)} %get-tuple-element.24.refs_1_), channel_id=1, source_target_pairs={{0,2},{1,3},{2,0},{3,1},{4,6},{5,7},{6,4},{7,5},{8,10},{9,11},{10,... | collective-permute-start | bytes 786440 | tf_op jit(solution)/shard_map/ppermute | solution.py:29
  200.3 7.1 %collective-permute-start.25 = (bf16[256,512]{1,0:T(8,128)(2,1)}, bf16[256,512]{1,0:T(8,128)(2,1)S(1)}, u32[]{:S(2)}, u32[]{:S(2)}) collective-permute-start(bf16[256,512]{1,0:T(8,128)(2,1)} %get-tuple-element.24.refs_1_), channel_id=1, source_target_pairs={{0,1},{1,0},{2,3},{3,2},{4,5},{5,4},{6,7},{7,6},{8,9},{9,8},{10,11... | collective-permute-start | bytes 786440 | tf_op jit(solution)/shard_map/ppermute | solution.py:32
  207.3 1.5 copy-start.23
  207.3 1.5 collective-permute-start.26
  (11 other events, 9.2 us)

commit v7 on v6

--- a/solution.py
+++ b/solution.py
@@ -8,12 +8,6 @@
 epsilon = 1e-06
 
 
-def passed_along(value, axis, steps):
-    count = lax.axis_size(axis)
-    leading, last = (max(0, -steps), min(count, count - steps))
-    return lax.ppermute(value, axis, [(source, source + steps) for source in range(leading, last)])
-
-
 def rms_norm(values):
     return values * lax.rsqrt(jnp.mean(values * values, axis=-1, keepdims=True) + epsilon)
 
@@ -22,16 +16,45 @@
     return jnp.sum(jnp.where(jnp.arange(vector.shape[0]) == position, vector, 0))
 
 
-def spread_over_seq(block):
-    count = lax.axis_size("seq")
-    to_partner = [(source, source ^ 1) for source in range(count)]
-    across = [
+def across_chips(block):
+    count = lax.axis_size("seq")
+    return [
         lax.ppermute(block, "seq", [(source, (source + step) % count) for source in range(count)])
         for step in range(2, count, 2)
     ]
-    from_partner = lax.ppermute(block, "seq", to_partner)
-    relayed = [lax.ppermute(part, "seq", to_partner) for part in across]
-    return [block] + across + [from_partner] + relayed
+
+
+def across_chips_first_section(block):
+    count = lax.axis_size("seq")
+    return [
+        lax.ppermute(
+            block, ("section", "seq"), [(source, (source + step) % count) for source in range(count)]
+        )
+        for step in range(2, count, 2)
+    ]
+
+
+def with_partner(parts):
+    count = lax.axis_size("seq")
+    to_partner = [(source, source ^ 1) for source in range(count)]
+    return parts + [lax.ppermute(part, "seq", to_partner) for part in parts]
+
+
+def to_next_section(block):
+    sections = lax.axis_size("section")
+    count = lax.axis_size("seq")
+    return [
+        lax.ppermute(
+            block,
+            ("section", "seq"),
+            [
+                (section * count + source, (section + 1) * count + (source + step) % count)
+                for section in range(sections - 1)
+                for source in range(count)
+            ],
+        )
+        for step in range(0, count, 2)
+    ]
 
 
 def kernel_table(patch_start, patch_count):
@@ -211,20 +234,21 @@
     entering_ext = jnp.concatenate(
         [incoming_states, jnp.zeros((biggest_patch_span, columns), jnp.bfloat16)], axis=0
     )
-    earlier_result = transit_states[0]
+    section_zero = section_index == 0
+    own_rows = jnp.where(section_zero, entering_ext[:biggest_patch_span], transit_states[0])
+    own_rows = jnp.where(
+        (row_numbers < pick_entry(patch_sizes_list, jnp.remainder(-section_index, patches)))[:, None],
+        own_rows,
+        0,
+    )
+    row_parts = [own_rows] + across_chips(own_rows)
     for turn_number in range(patches):
         patch_index = jnp.remainder(turn_number - section_index, patches)
         patch_count = pick_entry(patch_sizes_list, patch_index)
         patch_start = pick_entry(starts, patch_index)
         where = kernel_table(patch_start, patch_count)
-        live_rows = row_numbers < patch_count
-        entry_patch = lax.dynamic_slice_in_dim(
-            entering_ext, starts[turn_number], biggest_patch_span, 0
-        )
-        own_rows = jnp.where(section_index == 0, entry_patch, earlier_result)
-        own_rows = jnp.where(live_rows[:, None], own_rows, jnp.zeros_like(own_rows))
         head_rows, key_cache, value_cache = attend_block(
-            spread_over_seq(own_rows),
+            with_partner(row_parts),
             shift_scale,
             qkv_weights,
             key_cache,
@@ -233,11 +257,25 @@
             turn_number > 0,
         )
         updated = leave_block(
-            spread_over_seq(head_rows), out_weights, own_rows, gating_here, where
+            with_partner([head_rows] + across_chips(head_rows)),
+            out_weights,
+            row_parts[0],
+            gating_here,
+            where,
         )
         results.append(updated)
         if turn_number + 1 < patches:
-            earlier_result = passed_along(updated, "section", 1)
+            entry_patch = lax.dynamic_slice_in_dim(
+                entering_ext, starts[turn_number + 1], biggest_patch_span, 0
+            )
+            entry_patch = jnp.where(
+                (row_numbers < patch_sizes_list[turn_number + 1])[:, None], entry_patch, 0
+            )
+            arrived = to_next_section(updated)
+            entry_parts = [entry_patch] + across_chips_first_section(entry_patch)
+            row_parts = [
+                jnp.where(section_zero, entry, passed) for entry, passed in zip(entry_parts, arrived)
+            ]
     return jnp.stack(results)[:, None]
 
 

time: 217 us -> 215 us (level)
  waiting for transfers between devices: 92.5 us -> 81.9 us
  starting transfers between devices: 27 us -> 37.4 us
    ppermute x27 -> x30, waiting for transfers between devices: 92.5 us -> 81.9 us  [the longest x5 37.4 us: across_chips(): lax.ppermute(block, 'seq', [(source, (source + step) % count) for source...]
    ppermute x27 -> x30, starting transfers between devices: 27 us -> 37.4 us  [the longest x6 16.7 us: to_next_section(): lax.ppermute(block, ('section', 'seq'), [(section * count + source, (sect...]
    unnamed x64 -> x66, local copies, waits for them, and re-layouts: 6.12 us -> 6.11 us
  transfers between devices with their start and end apart: 27 -> 30, of which waited for: 17 -> 20; matrix products, arithmetic and copies ran while one was open for 4% -> 5% of each run, Pallas kernels for 0% -> 0%
where the time goes in v7:
time: 215 us; the launch traced here: 214 us
  waiting for transfers between devices  81.9 us (38%)
  Pallas kernels  66.6 us (31%)
  starting transfers between devices  37.4 us (17%)
  other arithmetic  15.2 us (7%)
  local copies, waits for them, and re-layouts  7.35 us (3%)
  between operations  5.89 us (3%)
    pallas_call x4, Pallas kernels, attend_block(): pl.pallas_call(block_kernel, grid_spec=grid_spec, out_shape=[jax.ShapeDty...  50.1 us
    ppermute x5, waiting for transfers between devices, across_chips(): lax.ppermute(block, 'seq', [(source, (source + step) % count) for source...  37.4 us
    ppermute x6, waiting for transfers between devices, to_next_section(): lax.ppermute(block, ('section', 'seq'), [(section * count + source, (sect...  22.2 us
    ppermute x6, starting transfers between devices, to_next_section(): lax.ppermute(block, ('section', 'seq'), [(section * count + source, (sect...  16.7 us
    pallas_call x4, Pallas kernels, leave_block(): pl.pallas_call(exit_kernel, in_specs=[smem] + [vmem] * (count + 3), out_s...  16.5 us
    ppermute x3, waiting for transfers between devices, across_chips_first_section(): lax.ppermute(block, ('section', 'seq'), [(source, (source + step) % count...  12.8 us
    ppermute x3, starting transfers between devices, across_chips_first_section(): lax.ppermute(block, ('section', 'seq'), [(source, (source + step) % count...  10.5 us
    ppermute x16, waiting for transfers between devices, with_partner(): return parts + [lax.ppermute(part, 'seq', to_partner) for part in parts]  9.47 us
  transfers between devices with their start and end apart: 30, of which 20 were waited for; matrix products, arithmetic and copies ran while one was open for 5% of the time, Pallas kernels for 0%

profile of v7, /device:TPU:0, one launch (start us, length us, event | category | flops | bytes accessed | tf_op | source)
XLA Modules:
  0.0 214.3 jit_solution(9195008688130463364)
XLA Ops:
  0.0 0.8 reduce-window.9
  0.8 1.5 fusion.4
  2.9 1.2 fusion.3.refs_1_.refs_6_
  4.1 3.0 %collective-permute-start = (bf16[256,768]{1,0:T(8,128)(2,1)S(1)}, bf16[256,768]{1,0:T(8,128)(2,1)S(1)}, u32[]{:S(2)}, u32[]{:S(2)}) collective-permute-start(bf16[256,768]{1,0:T(8,128)(2,1)S(1)} %fusion.3.refs_1_.refs_6_), channel_id=1, source_target_pairs={{0,2},{1,3},{2,0},{3,1},{4,6},{5,7},{6,4},{7,5},{8,10},{9,11},{10,... | collective-permute-start | bytes 1179656 | tf_op jit(solution)/shard_map/ppermute | solution.py:22
  7.1 9.1 %collective-permute-done.refs_2_ = bf16[256,768]{1,0:T(8,128)(2,1)S(1)} collective-permute-done((bf16[256,768]{1,0:T(8,128)(2,1)S(1)}, bf16[256,768]{1,0:T(8,128)(2,1)S(1)}, u32[]{:S(2)}, u32[]{:S(2)}) %collective-permute-start) | collective-permute-done | bytes 393248 | tf_op jit(solution)/shard_map/ppermute | solution.py:22
  16.2 1.9 select_select_fusion.3
  19.0 12.5 %shard_map.91 = (bf16[256,512]{1,0:T(8,128)(2,1)}, bf16[4,768,128]{2,1,0:T(8,128)(2,1)}, bf16[4,768,128]{2,1,0:T(8,128)(2,1)}) custom-call(s32[6]{0:T(128)} %get-tuple-element.40.refs_0_, bf16[256,768]{1,0:T(8,128)(2,1)} %copy-done.4, bf16[256,768]{1,0:T(8,128)(2,1)} %copy-done.12, bf16[256,768]{1,0:T(8,128)(2,1)} %copy-done.13, ...), custom_call_target="tpu_custom_call" | custom-call | tf_op jit(solution)/shard_map/pallas_call | solution.py:157
  31.5 1.7 collective-permute-start.3
  33.5 7.0 %collective-permute-done.3.refs_2_ = bf16[256,512]{1,0:T(8,128)(2,1)S(1)} collective-permute-done((bf16[256,512]{1,0:T(8,128)(2,1)}, bf16[256,512]{1,0:T(8,128)(2,1)S(1)}, u32[]{:S(2)}, u32[]{:S(2)}) %collective-permute-start.3) | collective-permute-done | bytes 262176 | tf_op jit(solution)/shard_map/ppermute | solution.py:22
  40.4 1.5 collective-permute-done.5.refs_4_
  42.7 4.2 %shard_map.92 = bf16[256,768]{1,0:T(8,128)(2,1)} custom-call(s32[6]{0:T(128)} %get-tuple-element.40.refs_0_, bf16[256,512]{1,0:T(8,128)(2,1)} %get-tuple-element.15.refs_1_, bf16[256,512]{1,0:T(8,128)(2,1)} %copy-done.20, bf16[256,512]{1,0:T(8,128)(2,1)} %copy-done.24, bf16[256,512]{1,0:T(8,128)(2,1)} %copy-done.28, bf16[4,512,768]{2,1,0:T(8,128)(2,1)} %bitcast.33, ...), custom_call_target="tpu_custom_call" | custom-call | tf_op jit(solution)/shard_map/pallas_call | solution.py:195
  46.9 3.7 %collective-permute-start.6 = (bf16[256,768]{1,0:T(8,128)(2,1)}, bf16[256,768]{1,0:T(8,128)(2,1)S(1)}, u32[]{:S(2)}, u32[]{:S(2)}) collective-permute-start(bf16[256,768]{1,0:T(8,128)(2,1)} %shard_map.92), channel_id=1, source_target_pairs={{0,4},{1,5},{2,6},{3,7},{4,8},{5,9},{6,10},{7,11},{8,12},{9,13},{1... | collective-permute-start | bytes 1179656 | tf_op jit(solution)/shard_map/ppermute | solution.py:47
  54.2 4.4 %collective-permute-start.8 = (bf16[256,768]{1,0:T(8,128)(2,1)}, bf16[256,768]{1,0:T(8,128)(2,1)S(1)}, u32[]{:S(2)}, u32[]{:S(2)}) collective-permute-start(bf16[256,768]{1,0:T(8,128)(2,1)} %shard_map.92), channel_id=1, source_target_pairs={{0,6},{1,7},{2,4},{3,5},{4,10},{5,11},{6,8},{7,9},{8,14},{9,15},{1... | collective-permute-start | bytes 1179656 | tf_op jit(solution)/shard_map/ppermute | solution.py:47
  58.6 1.6 collective-permute-done.6
  60.5 3.6 %collective-permute-start.7 = (bf16[256,768]{1,0:T(8,128)(2,1)S(1)}, bf16[256,768]{1,0:T(8,128)(2,1)S(1)}, u32[]{:S(2)}, u32[]{:S(2)}) collective-permute-start(bf16[256,768]{1,0:T(8,128)(2,1)S(1)} %get-tuple-element.39), channel_id=1, source_target_pairs={{0,2},{1,3},{2,0},{3,1},{16,18},{17,19},{18,16},{19,17}} | collective-permute-start | bytes 1179656 | tf_op jit(solution)/shard_map/ppermute | solution.py:30
  64.1 3.9 %collective-permute-done.8 = bf16[256,768]{1,0:T(8,128)(2,1)S(1)} collective-permute-done((bf16[256,768]{1,0:T(8,128)(2,1)}, bf16[256,768]{1,0:T(8,128)(2,1)S(1)}, u32[]{:S(2)}, u32[]{:S(2)}) %collective-permute-start.8) | collective-permute-done | bytes 393248 | tf_op jit(solution)/shard_map/ppermute | solution.py:47
  68.0 4.1 %collective-permute-done.7 = bf16[256,768]{1,0:T(8,128)(2,1)S(1)} collective-permute-done((bf16[256,768]{1,0:T(8,128)(2,1)S(1)}, bf16[256,768]{1,0:T(8,128)(2,1)S(1)}, u32[]{:S(2)}, u32[]{:S(2)}) %collective-permute-start.7) | collective-permute-done | bytes 393248 | tf_op jit(solution)/shard_map/ppermute | solution.py:30
  72.2 4.3 %select_select_fusion.2 = (s32[6]{0:T(128)}, s32[6]{0:T(128)}, s32[6]{0:T(128)}) fusion(s32[6]{0:T(128)S(1)} %get-tuple-element.41, s32[]{:T(128)} %get-tuple-element.54, s32[]{:T(128)} %get-tuple-element.33, s32[]{:T(128)} %get-tuple-element.55, s32[]{:T(128)} %get-tuple-element.32, s32[]{:T(128)} %get-tuple-element.52, s32[]{:T(128)} %get-tuple-element.31), kind=kLoop, calls=%fused_computation.52 | loop fusion | flops 54 | bytes 120 | tf_op jit(solution)/shard_map/jit(_where)/select_n | solution.py:67
  77.4 12.5 %shard_map.93 = (bf16[256,512]{1,0:T(8,128)(2,1)}, bf16[4,768,128]{2,1,0:T(8,128)(2,1)}, bf16[4,768,128]{2,1,0:T(8,128)(2,1)}) custom-call(s32[6]{0:T(128)} %get-tuple-element.49.refs_0_, bf16[256,768]{1,0:T(8,128)(2,1)} %copy-done.1, bf16[256,768]{1,0:T(8,128)(2,1)} %copy-done.5, ...), custom_call_target="tpu_custom_call", output_to_operand_aliasing={{1}: (7, {}), {2}: (8, {})} | custom-call | tf_op jit(solution)/shard_map/pallas_call | solution.py:157
  89.9 1.5 collective-permute-start.11
  91.6 7.2 %collective-permute-done.11.refs_2_ = bf16[256,512]{1,0:T(8,128)(2,1)S(1)} collective-permute-done((bf16[256,512]{1,0:T(8,128)(2,1)}, bf16[256,512]{1,0:T(8,128)(2,1)S(1)}, u32[]{:S(2)}, u32[]{:S(2)}) %collective-permute-start.11) | collective-permute-done | bytes 262176 | tf_op jit(solution)/shard_map/ppermute | solution.py:22
  98.8 1.5 collective-permute-done.13.refs_4_
  101.0 4.1 %shard_map.94 = bf16[256,768]{1,0:T(8,128)(2,1)} custom-call(s32[6]{0:T(128)} %get-tuple-element.49.refs_0_, bf16[256,512]{1,0:T(8,128)(2,1)} %get-tuple-element.18.refs_1_, bf16[256,512]{1,0:T(8,128)(2,1)} %copy-done.21, bf16[256,512]{1,0:T(8,128)(2,1)} %copy-done.25, bf16[256,512]{1,0:T(8,128)(2,1)} %copy-done.29, bf16[4,512,768]{2,1,0:T(8,128)(2,1)} %bitcast.34, ...), custom_call_target="tpu_custom_call" | custom-call | tf_op jit(solution)/shard_map/pallas_call | solution.py:195
  105.1 1.3 collective-permute-start.14
  108.9 3.3 %collective-permute-start.16 = (bf16[256,768]{1,0:T(8,128)(2,1)}, bf16[256,768]{1,0:T(8,128)(2,1)S(1)}, u32[]{:S(2)}, u32[]{:S(2)}) collective-permute-start(bf16[256,768]{1,0:T(8,128)(2,1)} %shard_map.94), channel_id=1, source_target_pairs={{0,6},{1,7},{2,4},{3,5},{4,10},{5,11},{6,8},{7,9},{8,14},{9,15},{1... | collective-permute-start | bytes 1179656 | tf_op jit(solution)/shard_map/ppermute | solution.py:47
  112.3 3.9 %collective-permute-done.14 = bf16[256,768]{1,0:T(8,128)(2,1)S(1)} collective-permute-done((bf16[256,768]{1,0:T(8,128)(2,1)}, bf16[256,768]{1,0:T(8,128)(2,1)S(1)}, u32[]{:S(2)}, u32[]{:S(2)}) %collective-permute-start.14) | collective-permute-done | bytes 393248 | tf_op jit(solution)/shard_map/ppermute | solution.py:47
  116.4 3.6 %collective-permute-start.15 = (bf16[256,768]{1,0:T(8,128)(2,1)S(1)}, bf16[256,768]{1,0:T(8,128)(2,1)S(1)}, u32[]{:S(2)}, u32[]{:S(2)}) collective-permute-start(bf16[256,768]{1,0:T(8,128)(2,1)S(1)} %get-tuple-element.37), channel_id=1, source_target_pairs={{0,2},{1,3},{2,0},{3,1},{16,18},{17,19},{18,16},{19,17}} | collective-permute-start | bytes 1179656 | tf_op jit(solution)/shard_map/ppermute | solution.py:30
  120.1 4.0 %collective-permute-done.16 = bf16[256,768]{1,0:T(8,128)(2,1)S(1)} collective-permute-done((bf16[256,768]{1,0:T(8,128)(2,1)}, bf16[256,768]{1,0:T(8,128)(2,1)S(1)}, u32[]{:S(2)}, u32[]{:S(2)}) %collective-permute-start.16) | collective-permute-done | bytes 393248 | tf_op jit(solution)/shard_map/ppermute | solution.py:47
  124.1 4.4 %collective-permute-done.15 = bf16[256,768]{1,0:T(8,128)(2,1)S(1)} collective-permute-done((bf16[256,768]{1,0:T(8,128)(2,1)S(1)}, bf16[256,768]{1,0:T(8,128)(2,1)S(1)}, u32[]{:S(2)}, u32[]{:S(2)}) %collective-permute-start.15) | collective-permute-done | bytes 393248 | tf_op jit(solution)/shard_map/ppermute | solution.py:30
  128.6 1.7 collective-permute-done.18.refs_4_
  131.1 12.5 %shard_map.95 = (bf16[256,512]{1,0:T(8,128)(2,1)}, bf16[4,768,128]{2,1,0:T(8,128)(2,1)}, bf16[4,768,128]{2,1,0:T(8,128)(2,1)}) custom-call(s32[6]{0:T(128)} %get-tuple-element.50.refs_0_, bf16[256,768]{1,0:T(8,128)(2,1)} %copy-done.3, bf16[256,768]{1,0:T(8,128)(2,1)} %copy-done.7, ...), custom_call_target="tpu_custom_call", output_to_operand_aliasing={{1}: (7, {}), {2}: (8, {})} | custom-call | tf_op jit(solution)/shard_map/pallas_call | solution.py:157
  143.6 1.5 collective-permute-start.19
  145.1 7.1 %collective-permute-done.19.refs_2_ = bf16[256,512]{1,0:T(8,128)(2,1)S(1)} collective-permute-done((bf16[256,512]{1,0:T(8,128)(2,1)}, bf16[256,512]{1,0:T(8,128)(2,1)S(1)}, u32[]{:S(2)}, u32[]{:S(2)}) %collective-permute-start.19) | collective-permute-done | bytes 262176 | tf_op jit(solution)/shard_map/ppermute | solution.py:22
  152.2 1.5 collective-permute-done.21.refs_4_
  154.4 4.1 %shard_map.96 = bf16[256,768]{1,0:T(8,128)(2,1)} custom-call(s32[6]{0:T(128)} %get-tuple-element.50.refs_0_, bf16[256,512]{1,0:T(8,128)(2,1)} %get-tuple-element.21.refs_1_, bf16[256,512]{1,0:T(8,128)(2,1)} %copy-done.22, bf16[256,512]{1,0:T(8,128)(2,1)} %copy-done.26, bf16[256,512]{1,0:T(8,128)(2,1)} %copy-done.30, bf16[4,512,768]{2,1,0:T(8,128)(2,1)} %bitcast.35, ...), custom_call_target="tpu_custom_call" | custom-call | tf_op jit(solution)/shard_map/pallas_call | solution.py:195
  158.5 1.3 collective-permute-start.22
  162.3 2.6 %collective-permute-start.24 = (bf16[256,768]{1,0:T(8,128)(2,1)}, bf16[256,768]{1,0:T(8,128)(2,1)S(1)}, u32[]{:S(2)}, u32[]{:S(2)}) collective-permute-start(bf16[256,768]{1,0:T(8,128)(2,1)} %shard_map.96), channel_id=1, source_target_pairs={{0,6},{1,7},{2,4},{3,5},{4,10},{5,11},{6,8},{7,9},{8,14},{9,15},{1... | collective-permute-start | bytes 1179656 | tf_op jit(solution)/shard_map/ppermute | solution.py:47
  164.9 4.6 %collective-permute-done.22 = bf16[256,768]{1,0:T(8,128)(2,1)S(1)} collective-permute-done((bf16[256,768]{1,0:T(8,128)(2,1)}, bf16[256,768]{1,0:T(8,128)(2,1)S(1)}, u32[]{:S(2)}, u32[]{:S(2)}) %collective-permute-start.22) | collective-permute-done | bytes 393248 | tf_op jit(solution)/shard_map/ppermute | solution.py:47
  169.8 3.4 %collective-permute-start.23 = (bf16[256,768]{1,0:T(8,128)(2,1)S(1)}, bf16[256,768]{1,0:T(8,128)(2,1)S(1)}, u32[]{:S(2)}, u32[]{:S(2)}) collective-permute-start(bf16[256,768]{1,0:T(8,128)(2,1)S(1)} %get-tuple-element.35), channel_id=1, source_target_pairs={{0,2},{1,3},{2,0},{3,1},{16,18},{17,19},{18,16},{19,17}} | collective-permute-start | bytes 1179656 | tf_op jit(solution)/shard_map/ppermute | solution.py:30
  173.3 4.2 %collective-permute-done.24 = bf16[256,768]{1,0:T(8,128)(2,1)S(1)} collective-permute-done((bf16[256,768]{1,0:T(8,128)(2,1)}, bf16[256,768]{1,0:T(8,128)(2,1)S(1)}, u32[]{:S(2)}, u32[]{:S(2)}) %collective-permute-start.24) | collective-permute-done | bytes 393248 | tf_op jit(solution)/shard_map/ppermute | solution.py:47
  177.5 4.4 %collective-permute-done.23 = bf16[256,768]{1,0:T(8,128)(2,1)S(1)} collective-permute-done((bf16[256,768]{1,0:T(8,128)(2,1)S(1)}, bf16[256,768]{1,0:T(8,128)(2,1)S(1)}, u32[]{:S(2)}, u32[]{:S(2)}) %collective-permute-start.23) | collective-permute-done | bytes 393248 | tf_op jit(solution)/shard_map/ppermute | solution.py:30
  182.0 1.7 collective-permute-done.26.refs_4_
  184.4 12.5 %shard_map.97 = (bf16[256,512]{1,0:T(8,128)(2,1)}, bf16[4,768,128]{2,1,0:T(8,128)(2,1)}, bf16[4,768,128]{2,1,0:T(8,128)(2,1)}) custom-call(s32[6]{0:T(128)} %get-tuple-element.51.refs_0_, bf16[256,768]{1,0:T(8,128)(2,1)} %copy-done.2, bf16[256,768]{1,0:T(8,128)(2,1)} %copy-done.6, ...), custom_call_target="tpu_custom_call", output_to_operand_aliasing={{1}: (7, {}), {2}: (8, {})} | custom-call | tf_op jit(solution)/shard_map/pallas_call | solution.py:157
  197.0 1.6 collective-permute-start.27
  198.5 7.1 %collective-permute-done.27.refs_2_ = bf16[256,512]{1,0:T(8,128)(2,1)S(1)} collective-permute-done((bf16[256,512]{1,0:T(8,128)(2,1)}, bf16[256,512]{1,0:T(8,128)(2,1)S(1)}, u32[]{:S(2)}, u32[]{:S(2)}) %collective-permute-start.27) | collective-permute-done | bytes 262176 | tf_op jit(solution)/shard_map/ppermute | solution.py:22
  205.6 1.5 collective-permute-done.29.refs_4_
  207.9 4.1 %shard_map.98 = bf16[256,768]{1,0:T(8,128)(2,1)} custom-call(s32[6]{0:T(128)} %get-tuple-element.51.refs_0_, bf16[256,512]{1,0:T(8,128)(2,1)} %get-tuple-element.24.refs_1_, bf16[256,512]{1,0:T(8,128)(2,1)} %copy-done.23, bf16[256,512]{1,0:T(8,128)(2,1)} %copy-done.27, bf16[256,512]{1,0:T(8,128)(2,1)} %copy-done.31, bf16[4,512,768]{2,1,0:T(8,128)(2,1)} %bitcast.36, ...), custom_call_target="tpu_custom_call" | custom-call | tf_op jit(solution)/shard_map/pallas_call | solution.py:195
  212.0 2.3 %maximum_bitcast_fusion = bf16[4,1,256,768]{3,2,1,0:T(8,128)(2,1)} fusion(bf16[1,256,768]{2,1,0:T(8,128)(2,1)} %bitcast.40, bf16[1,256,768]{2,1,0:T(8,128)(2,1)S(1)} %bitcast.39, bf16[1,256,768]{2,1,0:T(8,128)(2,1)S(1)} %bitcast.38, bf16[1,256,768]{2,1,0:T(8,128)(2,1)S(1)} %bitcast.37), kind=kLoop, calls=%fused_computation.3 | loop fusion | flops 2359296 | bytes 3145728 | tf_op jit(solution)/shard_map/broadcast_in_dim | solution.py:279
  (104 shorter events, 11.4 us)
Async XLA Ops:
  4.1 14.0 %copy-start.4 = (bf16[256,768]{1,0:T(8,128)(2,1)}, bf16[256,768]{1,0:T(8,128)(2,1)S(1)}, u32[]{:S(2)}) copy-start(bf16[256,768]{1,0:T(8,128)(2,1)S(1)} %fusion.3.refs_1_.refs_6_) | copy-start | bytes 1179652
  4.1 12.1 %collective-permute-start = (bf16[256,768]{1,0:T(8,128)(2,1)S(1)}, bf16[256,768]{1,0:T(8,128)(2,1)S(1)}, u32[]{:S(2)}, u32[]{:S(2)}) collective-permute-start(bf16[256,768]{1,0:T(8,128)(2,1)S(1)} %fusion.3.refs_1_.refs_6_), channel_id=1, source_target_pairs={{0,2},{1,3},{2,0},{3,1},{4,6},{5,7},{6,4},{7,5},{8,10},{9,11},{10,... | collective-permute-start | bytes 1179656 | tf_op jit(solution)/shard_map/ppermute | solution.py:22
  7.1 11.0 %collective-permute-start.1 = (bf16[256,768]{1,0:T(8,128)(2,1)S(1)}, bf16[256,768]{1,0:T(8,128)(2,1)S(1)}, u32[]{:S(2)}, u32[]{:S(2)}) collective-permute-start(bf16[256,768]{1,0:T(8,128)(2,1)S(1)} %fusion.3.refs_1_.refs_6_), channel_id=1, source_target_pairs={{0,1},{1,0},{2,3},{3,2},{4,5},{5,4},{6,7},{7,6},{8,9},{9,8},{10,11... | collective-permute-start | bytes 1179656 | tf_op jit(solution)/shard_map/ppermute | solution.py:40
  16.2 1.9 copy-start.12
  16.2 1.9 collective-permute-start.2
  31.5 8.9 %collective-permute-start.3 = (bf16[256,512]{1,0:T(8,128)(2,1)}, bf16[256,512]{1,0:T(8,128)(2,1)S(1)}, u32[]{:S(2)}, u32[]{:S(2)}) collective-permute-start(bf16[256,512]{1,0:T(8,128)(2,1)} %get-tuple-element.15.refs_1_), channel_id=1, source_target_pairs={{0,2},{1,3},{2,0},{3,1},{4,6},{5,7},{6,4},{7,5},{8,10},{9,11},{10,... | collective-permute-start | bytes 786440 | tf_op jit(solution)/shard_map/ppermute | solution.py:22
  33.2 7.2 %collective-permute-start.4 = (bf16[256,512]{1,0:T(8,128)(2,1)}, bf16[256,512]{1,0:T(8,128)(2,1)S(1)}, u32[]{:S(2)}, u32[]{:S(2)}) collective-permute-start(bf16[256,512]{1,0:T(8,128)(2,1)} %get-tuple-element.15.refs_1_), channel_id=1, source_target_pairs={{0,1},{1,0},{2,3},{3,2},{4,5},{5,4},{6,7},{7,6},{8,9},{9,8},{10,11... | collective-permute-start | bytes 786440 | tf_op jit(solution)/shard_map/ppermute | solution.py:40
  40.4 1.5 copy-start.20
  40.4 1.5 collective-permute-start.5
  42.7 10.2 %copy-start.32 = (s32[4]{0:T(128)S(1)}, s32[4]{0:T(128)}, u32[]{:S(2)}) copy-start(s32[4]{0:T(128)} %param.11) | copy-start | bytes 52
  42.7 17.5 %copy-start = (bf16[768,768]{1,0:T(8,128)(2,1)S(1)}, bf16[768,768]{1,0:T(8,128)(2,1)}, u32[]{:S(2)}) copy-start(bf16[768,768]{1,0:T(8,128)(2,1)} %param.9) | copy-start | bytes 3538948
  46.9 13.3 %collective-permute-start.6 = (bf16[256,768]{1,0:T(8,128)(2,1)}, bf16[256,768]{1,0:T(8,128)(2,1)S(1)}, u32[]{:S(2)}, u32[]{:S(2)}) collective-permute-start(bf16[256,768]{1,0:T(8,128)(2,1)} %shard_map.92), channel_id=1, source_target_pairs={{0,4},{1,5},{2,6},{3,7},{4,8},{5,9},{6,10},{7,11},{8,12},{9,13},{1... | collective-permute-start | bytes 1179656 | tf_op jit(solution)/shard_map/ppermute | solution.py:47
  54.2 13.8 %collective-permute-start.8 = (bf16[256,768]{1,0:T(8,128)(2,1)}, bf16[256,768]{1,0:T(8,128)(2,1)S(1)}, u32[]{:S(2)}, u32[]{:S(2)}) collective-permute-start(bf16[256,768]{1,0:T(8,128)(2,1)} %shard_map.92), channel_id=1, source_target_pairs={{0,6},{1,7},{2,4},{3,5},{4,10},{5,11},{6,8},{7,9},{8,14},{9,15},{1... | collective-permute-start | bytes 1179656 | tf_op jit(solution)/shard_map/ppermute | solution.py:47
  60.5 16.0 %copy-start.1 = (bf16[256,768]{1,0:T(8,128)(2,1)}, bf16[256,768]{1,0:T(8,128)(2,1)S(1)}, u32[]{:S(2)}) copy-start(bf16[256,768]{1,0:T(8,128)(2,1)S(1)} %get-tuple-element.38.refs_1_.refs_6_) | copy-start | bytes 1179652
  60.5 11.6 %collective-permute-start.7 = (bf16[256,768]{1,0:T(8,128)(2,1)S(1)}, bf16[256,768]{1,0:T(8,128)(2,1)S(1)}, u32[]{:S(2)}, u32[]{:S(2)}) collective-permute-start(bf16[256,768]{1,0:T(8,128)(2,1)S(1)} %get-tuple-element.39), channel_id=1, source_target_pairs={{0,2},{1,3},{2,0},{3,1},{16,18},{17,19},{18,16},{19,17}} | collective-permute-start | bytes 1179656 | tf_op jit(solution)/shard_map/ppermute | solution.py:30
  64.0 12.5 %collective-permute-start.9 = (bf16[256,768]{1,0:T(8,128)(2,1)S(1)}, bf16[256,768]{1,0:T(8,128)(2,1)S(1)}, u32[]{:S(2)}, u32[]{:S(2)}) collective-permute-start(bf16[256,768]{1,0:T(8,128)(2,1)S(1)} %get-tuple-element.38.refs_1_.refs_6_), channel_id=1, source_target_pairs={{0,1},{1,0},{2,3},{3,2},{4,5},{5,4},{6,7},{7,6},{8,9},{9,8},{10,11... | collective-permute-start | bytes 1179656 | tf_op jit(solution)/shard_map/ppermute | solution.py:40
  72.1 4.4 %copy-start.5 = (bf16[256,768]{1,0:T(8,128)(2,1)}, bf16[256,768]{1,0:T(8,128)(2,1)S(1)}, u32[]{:S(2)}) copy-start(bf16[256,768]{1,0:T(8,128)(2,1)S(1)} %broadcast_select_fusion.4.refs_2_) | copy-start | bytes 1179652
  72.1 4.4 %collective-permute-start.10 = (bf16[256,768]{1,0:T(8,128)(2,1)S(1)}, bf16[256,768]{1,0:T(8,128)(2,1)S(1)}, u32[]{:S(2)}, u32[]{:S(2)}) collective-permute-start(bf16[256,768]{1,0:T(8,128)(2,1)S(1)} %broadcast_select_fusion.4.refs_2_), channel_id=1, source_target_pairs={{0,1},{1,0},{2,3},{3,2},{4,5},{5,4},{6,7},{7,6},{8,9},{9,8},{10,11... | collective-permute-start | bytes 1179656 | tf_op jit(solution)/shard_map/ppermute | solution.py:40
  89.9 8.9 %collective-permute-start.11 = (bf16[256,512]{1,0:T(8,128)(2,1)}, bf16[256,512]{1,0:T(8,128)(2,1)S(1)}, u32[]{:S(2)}, u32[]{:S(2)}) collective-permute-start(bf16[256,512]{1,0:T(8,128)(2,1)} %get-tuple-element.18.refs_1_), channel_id=1, source_target_pairs={{0,2},{1,3},{2,0},{3,1},{4,6},{5,7},{6,4},{7,5},{8,10},{9,11},{10,... | collective-permute-start | bytes 786440 | tf_op jit(solution)/shard_map/ppermute | solution.py:22
  91.4 7.4 %collective-permute-start.12 = (bf16[256,512]{1,0:T(8,128)(2,1)}, bf16[256,512]{1,0:T(8,128)(2,1)S(1)}, u32[]{:S(2)}, u32[]{:S(2)}) collective-permute-start(bf16[256,512]{1,0:T(8,128)(2,1)} %get-tuple-element.18.refs_1_), channel_id=1, source_target_pairs={{0,1},{1,0},{2,3},{3,2},{4,5},{5,4},{6,7},{7,6},{8,9},{9,8},{10,11... | collective-permute-start | bytes 786440 | tf_op jit(solution)/shard_map/ppermute | solution.py:40
  98.8 1.5 copy-start.21
  98.8 1.5 collective-permute-start.13
  105.1 11.0 %collective-permute-start.14 = (bf16[256,768]{1,0:T(8,128)(2,1)}, bf16[256,768]{1,0:T(8,128)(2,1)S(1)}, u32[]{:S(2)}, u32[]{:S(2)}) collective-permute-start(bf16[256,768]{1,0:T(8,128)(2,1)} %shard_map.94), channel_id=1, source_target_pairs={{0,4},{1,5},{2,6},{3,7},{4,8},{5,9},{6,10},{7,11},{8,12},{9,13},{1... | collective-permute-start | bytes 1179656 | tf_op jit(solution)/shard_map/ppermute | solution.py:47
  108.9 15.2 %collective-permute-start.16 = (bf16[256,768]{1,0:T(8,128)(2,1)}, bf16[256,768]{1,0:T(8,128)(2,1)S(1)}, u32[]{:S(2)}, u32[]{:S(2)}) collective-permute-start(bf16[256,768]{1,0:T(8,128)(2,1)} %shard_map.94), channel_id=1, source_target_pairs={{0,6},{1,7},{2,4},{3,5},{4,10},{5,11},{6,8},{7,9},{8,14},{9,15},{1... | collective-permute-start | bytes 1179656 | tf_op jit(solution)/shard_map/ppermute | solution.py:47
  116.4 13.9 %copy-start.3 = (bf16[256,768]{1,0:T(8,128)(2,1)}, bf16[256,768]{1,0:T(8,128)(2,1)S(1)}, u32[]{:S(2)}) copy-start(bf16[256,768]{1,0:T(8,128)(2,1)S(1)} %get-tuple-element.36.refs_1_.refs_6_) | copy-start | bytes 1179652
  116.4 12.1 %collective-permute-start.15 = (bf16[256,768]{1,0:T(8,128)(2,1)S(1)}, bf16[256,768]{1,0:T(8,128)(2,1)S(1)}, u32[]{:S(2)}, u32[]{:S(2)}) collective-permute-start(bf16[256,768]{1,0:T(8,128)(2,1)S(1)} %get-tuple-element.37), channel_id=1, source_target_pairs={{0,2},{1,3},{2,0},{3,1},{16,18},{17,19},{18,16},{19,17}} | collective-permute-start | bytes 1179656 | tf_op jit(solution)/shard_map/ppermute | solution.py:30
  120.0 8.6 %collective-permute-start.17 = (bf16[256,768]{1,0:T(8,128)(2,1)S(1)}, bf16[256,768]{1,0:T(8,128)(2,1)S(1)}, u32[]{:S(2)}, u32[]{:S(2)}) collective-permute-start(bf16[256,768]{1,0:T(8,128)(2,1)S(1)} %get-tuple-element.36.refs_1_.refs_6_), channel_id=1, source_target_pairs={{0,1},{1,0},{2,3},{3,2},{4,5},{5,4},{6,7},{7,6},{8,9},{9,8},{10,11... | collective-permute-start | bytes 1179656 | tf_op jit(solution)/shard_map/ppermute | solution.py:40
  128.5 1.8 copy-start.7
  128.5 1.8 collective-permute-start.18
  128.6 1.7 copy-start.16
  143.6 8.6 %collective-permute-start.19 = (bf16[256,512]{1,0:T(8,128)(2,1)}, bf16[256,512]{1,0:T(8,128)(2,1)S(1)}, u32[]{:S(2)}, u32[]{:S(2)}) collective-permute-start(bf16[256,512]{1,0:T(8,128)(2,1)} %get-tuple-element.21.refs_1_), channel_id=1, source_target_pairs={{0,2},{1,3},{2,0},{3,1},{4,6},{5,7},{6,4},{7,5},{8,10},{9,11},{10,... | collective-permute-start | bytes 786440 | tf_op jit(solution)/shard_map/ppermute | solution.py:22
  145.1 7.1 %collective-permute-start.20 = (bf16[256,512]{1,0:T(8,128)(2,1)}, bf16[256,512]{1,0:T(8,128)(2,1)S(1)}, u32[]{:S(2)}, u32[]{:S(2)}) collective-permute-start(bf16[256,512]{1,0:T(8,128)(2,1)} %get-tuple-element.21.refs_1_), channel_id=1, source_target_pairs={{0,1},{1,0},{2,3},{3,2},{4,5},{5,4},{6,7},{7,6},{8,9},{9,8},{10,11... | collective-permute-start | bytes 786440 | tf_op jit(solution)/shard_map/ppermute | solution.py:40
  152.2 1.5 copy-start.22
  152.2 1.5 collective-permute-start.21
  158.5 11.0 %collective-permute-start.22 = (bf16[256,768]{1,0:T(8,128)(2,1)}, bf16[256,768]{1,0:T(8,128)(2,1)S(1)}, u32[]{:S(2)}, u32[]{:S(2)}) collective-permute-start(bf16[256,768]{1,0:T(8,128)(2,1)} %shard_map.96), channel_id=1, source_target_pairs={{0,4},{1,5},{2,6},{3,7},{4,8},{5,9},{6,10},{7,11},{8,12},{9,13},{1... | collective-permute-start | bytes 1179656 | tf_op jit(solution)/shard_map/ppermute | solution.py:47
  162.3 15.2 %collective-permute-start.24 = (bf16[256,768]{1,0:T(8,128)(2,1)}, bf16[256,768]{1,0:T(8,128)(2,1)S(1)}, u32[]{:S(2)}, u32[]{:S(2)}) collective-permute-start(bf16[256,768]{1,0:T(8,128)(2,1)} %shard_map.96), channel_id=1, source_target_pairs={{0,6},{1,7},{2,4},{3,5},{4,10},{5,11},{6,8},{7,9},{8,14},{9,15},{1... | collective-permute-start | bytes 1179656 | tf_op jit(solution)/shard_map/ppermute | solution.py:47
  169.8 13.9 %copy-start.2 = (bf16[256,768]{1,0:T(8,128)(2,1)}, bf16[256,768]{1,0:T(8,128)(2,1)S(1)}, u32[]{:S(2)}) copy-start(bf16[256,768]{1,0:T(8,128)(2,1)S(1)} %get-tuple-element.34.refs_1_.refs_6_) | copy-start | bytes 1179652
  169.8 12.0 %collective-permute-start.23 = (bf16[256,768]{1,0:T(8,128)(2,1)S(1)}, bf16[256,768]{1,0:T(8,128)(2,1)S(1)}, u32[]{:S(2)}, u32[]{:S(2)}) collective-permute-start(bf16[256,768]{1,0:T(8,128)(2,1)S(1)} %get-tuple-element.35), channel_id=1, source_target_pairs={{0,2},{1,3},{2,0},{3,1},{16,18},{17,19},{18,16},{19,17}} | collective-permute-start | bytes 1179656 | tf_op jit(solution)/shard_map/ppermute | solution.py:30
  173.2 8.8 %collective-permute-start.25 = (bf16[256,768]{1,0:T(8,128)(2,1)S(1)}, bf16[256,768]{1,0:T(8,128)(2,1)S(1)}, u32[]{:S(2)}, u32[]{:S(2)}) collective-permute-start(bf16[256,768]{1,0:T(8,128)(2,1)S(1)} %get-tuple-element.34.refs_1_.refs_6_), channel_id=1, source_target_pairs={{0,1},{1,0},{2,3},{3,2},{4,5},{5,4},{6,7},{7,6},{8,9},{9,8},{10,11... | collective-permute-start | bytes 1179656 | tf_op jit(solution)/shard_map/ppermute | solution.py:40
  181.9 1.8 copy-start.6
  181.9 1.8 collective-permute-start.26
  182.0 1.7 copy-start.14
  196.9 15.0 %copy-start.8 = (bf16[256,768]{1,0:T(8,128)(2,1)S(1)}, bf16[256,768]{1,0:T(8,128)(2,1)}, u32[]{:S(2)}) copy-start(bf16[256,768]{1,0:T(8,128)(2,1)} %shard_map.92) | copy-start | bytes 1179652
  197.0 15.0 %copy-start.9 = (bf16[256,768]{1,0:T(8,128)(2,1)S(1)}, bf16[256,768]{1,0:T(8,128)(2,1)}, u32[]{:S(2)}) copy-start(bf16[256,768]{1,0:T(8,128)(2,1)} %shard_map.94) | copy-start | bytes 1179652
  197.0 15.0 %copy-start.10 = (bf16[256,768]{1,0:T(8,128)(2,1)S(1)}, bf16[256,768]{1,0:T(8,128)(2,1)}, u32[]{:S(2)}) copy-start(bf16[256,768]{1,0:T(8,128)(2,1)} %shard_map.96) | copy-start | bytes 1179652
  197.0 8.6 %collective-permute-start.27 = (bf16[256,512]{1,0:T(8,128)(2,1)}, bf16[256,512]{1,0:T(8,128)(2,1)S(1)}, u32[]{:S(2)}, u32[]{:S(2)}) collective-permute-start(bf16[256,512]{1,0:T(8,128)(2,1)} %get-tuple-element.24.refs_1_), channel_id=1, source_target_pairs={{0,2},{1,3},{2,0},{3,1},{4,6},{5,7},{6,4},{7,5},{8,10},{9,11},{10,... | collective-permute-start | bytes 786440 | tf_op jit(solution)/shard_map/ppermute | solution.py:22
  198.5 7.1 %collective-permute-start.28 = (bf16[256,512]{1,0:T(8,128)(2,1)}, bf16[256,512]{1,0:T(8,128)(2,1)S(1)}, u32[]{:S(2)}, u32[]{:S(2)}) collective-permute-start(bf16[256,512]{1,0:T(8,128)(2,1)} %get-tuple-element.24.refs_1_), channel_id=1, source_target_pairs={{0,1},{1,0},{2,3},{3,2},{4,5},{5,4},{6,7},{7,6},{8,9},{9,8},{10,11... | collective-permute-start | bytes 786440 | tf_op jit(solution)/shard_map/ppermute | solution.py:40
  205.6 1.5 collective-permute-start.29
  (15 other events, 15.3 us)

commit v8 on v7

--- a/solution.py
+++ b/solution.py
@@ -71,19 +71,17 @@
 
 def block_kernel(*refs):
     where_ref = refs[0]
-    count = len(refs) - 9
+    count = len(refs) - 10
     part_refs = refs[1 : 1 + count]
     scale_ref, weights_ref, keys_ref, values_ref = refs[1 + count : 5 + count]
     heads_ref, keys_out, values_out = refs[5 + count : 8 + count]
-    shaped_ref = refs[8 + count]
-    start = where_ref[0]
-    patch_count = where_ref[1]
-    head_dim = keys_ref.shape[2]
-    seq_len = keys_ref.shape[1]
+    shaped_ref, mixed_ref = refs[8 + count :]
+    slot = pl.program_id(0)
     span, width = part_refs[0].shape
+    heads_here, seq_len, head_dim = keys_ref.shape
     features = width * count
 
-    @pl.when(pl.program_id(0) == 0)
+    @pl.when(slot == 0)
     def _():
         parts = [part[...].astype(jnp.float32) for part in part_refs]
         row_mean = sum(jnp.sum(part, axis=-1, keepdims=True) for part in parts) / features
@@ -91,68 +89,71 @@
         spread = sum(jnp.sum(c * c, axis=-1, keepdims=True) for c in centred) / features
         inverse = lax.rsqrt(spread + epsilon)
         for part in range(count):
-            slot = where_ref[2 + part]
-            shift_scale = scale_ref[slot]
-            shaped_ref[slot] = (
+            source = where_ref[2 + part]
+            shift_scale = scale_ref[source]
+            shaped_ref[source] = (
                 (centred[part] * inverse) * (1.0 + shift_scale[1:2]) + shift_scale[0:1]
             ).astype(jnp.bfloat16)
-
-    mixed = sum(
-        jnp.dot(
-            shaped_ref[slot],
-            weights_ref[slot * width : (slot + 1) * width, :],
-            preferred_element_type=jnp.float32,
-        )
-        for slot in range(count)
-    )
-    queries = rms_norm(mixed[:, :head_dim]).astype(jnp.bfloat16)
-    fresh_keys = rms_norm(mixed[:, head_dim : 2 * head_dim]).astype(jnp.bfloat16)
-    fresh_values = mixed[:, 2 * head_dim :].astype(jnp.bfloat16)
-    rows = lax.broadcasted_iota(jnp.int32, (seq_len, span), 0)
-    picks = lax.broadcasted_iota(jnp.int32, (seq_len, span), 1)
-    placing = ((rows == picks + start) & (picks < patch_count)).astype(jnp.bfloat16)
-    row_ids = lax.broadcasted_iota(jnp.int32, (seq_len, 1), 0)
-    inside = (row_ids >= start) & (row_ids < start + patch_count)
-    placed_keys = jnp.dot(placing, fresh_keys, preferred_element_type=jnp.float32)
-    placed_values = jnp.dot(placing, fresh_values, preferred_element_type=jnp.float32)
-    keys = jnp.where(inside, placed_keys.astype(jnp.bfloat16), keys_ref[0])
-    values = jnp.where(inside, placed_values.astype(jnp.bfloat16), values_ref[0])
-    keys_out[0] = keys
-    values_out[0] = values
-    scores = lax.dot_general(
-        queries, keys, (((1,), (1,)), ((), ())), preferred_element_type=jnp.float32
-    ) * head_dim ** (-0.5)
-    expos = jnp.exp(scores)
-    weights = (expos / jnp.sum(expos, axis=-1, keepdims=True)).astype(jnp.bfloat16)
-    heads_ref[...] = jnp.dot(weights, values, preferred_element_type=jnp.float32).astype(
-        jnp.bfloat16
-    )
+        mixed_ref[...] = jnp.zeros_like(mixed_ref)
+
+    mixed_ref[...] += jnp.dot(shaped_ref[slot], weights_ref[...], preferred_element_type=jnp.float32)
+
+    @pl.when(slot == count - 1)
+    def _():
+        start = where_ref[0]
+        patch_count = where_ref[1]
+        rows = lax.broadcasted_iota(jnp.int32, (seq_len, span), 0)
+        picks = lax.broadcasted_iota(jnp.int32, (seq_len, span), 1)
+        placing = ((rows == picks + start) & (picks < patch_count)).astype(jnp.bfloat16)
+        row_ids = lax.broadcasted_iota(jnp.int32, (seq_len, 1), 0)
+        inside = (row_ids >= start) & (row_ids < start + patch_count)
+        for head in range(heads_here):
+            mixed = mixed_ref[:, 3 * head * head_dim : 3 * (head + 1) * head_dim]
+            queries = rms_norm(mixed[:, :head_dim]).astype(jnp.bfloat16)
+            fresh_keys = rms_norm(mixed[:, head_dim : 2 * head_dim]).astype(jnp.bfloat16)
+            fresh_values = mixed[:, 2 * head_dim :].astype(jnp.bfloat16)
+            placed_keys = jnp.dot(placing, fresh_keys, preferred_element_type=jnp.float32)
+            placed_values = jnp.dot(placing, fresh_values, preferred_element_type=jnp.float32)
+            keys = jnp.where(inside, placed_keys.astype(jnp.bfloat16), keys_ref[head])
+            values = jnp.where(inside, placed_values.astype(jnp.bfloat16), values_ref[head])
+            keys_out[head] = keys
+            values_out[head] = values
+            scores = lax.dot_general(
+                queries, keys, (((1,), (1,)), ((), ())), preferred_element_type=jnp.float32
+            ) * head_dim ** (-0.5)
+            expos = jnp.exp(scores)
+            weights = (expos / jnp.sum(expos, axis=-1, keepdims=True)).astype(jnp.bfloat16)
+            heads_ref[:, head * head_dim : (head + 1) * head_dim] = jnp.dot(
+                weights, values, preferred_element_type=jnp.float32
+            ).astype(jnp.bfloat16)
 
 
 def attend_block(parts, shift_scale, qkv_weights, key_cache, value_cache, where, in_place):
     count = len(parts)
     span, width = parts[0].shape
     heads_here, seq_len, head_dim = key_cache.shape
-    features = qkv_weights.shape[0]
+    columns = qkv_weights.shape[1]
     scale_blocks = jnp.transpose(shift_scale.reshape(2, count, width), (1, 0, 2))
-    whole = lambda shape: pl.BlockSpec(shape, lambda h, where: (0,) * len(shape))
-    cache_spec = pl.BlockSpec((1, seq_len, head_dim), lambda h, where: (h, 0, 0))
+    whole = lambda shape: pl.BlockSpec(shape, lambda j, where: (0,) * len(shape))
     grid_spec = pltpu.PrefetchScalarGridSpec(
         num_scalar_prefetch=1,
-        grid=(heads_here,),
+        grid=(count,),
         in_specs=[whole((span, width)) for _ in parts]
         + [
             whole((count, 2, width)),
-            pl.BlockSpec((features, 3 * head_dim), lambda h, where: (0, h)),
-            cache_spec,
-            cache_spec,
+            pl.BlockSpec((width, columns), lambda j, where: (j, 0)),
+            whole(key_cache.shape),
+            whole(value_cache.shape),
         ],
         out_specs=[
-            pl.BlockSpec((span, head_dim), lambda h, where: (0, h)),
-            cache_spec,
-            cache_spec,
-        ],
-        scratch_shapes=[pltpu.VMEM((count, span, width), jnp.bfloat16)],
+            whole((span, heads_here * head_dim)),
+            whole(key_cache.shape),
+            whole(value_cache.shape),
+        ],
+        scratch_shapes=[
+            pltpu.VMEM((count, span, width), jnp.bfloat16),
+            pltpu.VMEM((span, columns), jnp.float32),
+        ],
     )
     return pl.pallas_call(
         block_kernel,
@@ -169,38 +170,54 @@
 
 def exit_kernel(*refs):
     where_ref = refs[0]
-    count = len(refs) - 5
+    count = len(refs) - 6
     part_refs = refs[1 : 1 + count]
     weights_ref, own_ref, gate_ref = refs[1 + count : 4 + count]
-    out_ref = refs[4 + count]
-    patch_count = where_ref[1]
-    projected = sum(
-        jnp.dot(
-            part_refs[part][...],
-            weights_ref[where_ref[2 + part]],
-            preferred_element_type=jnp.float32,
-        )
-        for part in range(count)
-    )
-    updated = own_ref[...].astype(jnp.float32) + gate_ref[...] * projected
-    live = lax.broadcasted_iota(jnp.int32, updated.shape, 0) < patch_count
-    out_ref[...] = jnp.where(live, updated, 0.0).astype(out_ref.dtype)
+    out_ref, projected_ref = refs[4 + count :]
+    step = pl.program_id(0)
+    for part in range(count):
+
+        @pl.when(step == part)
+        def _():
+            product = jnp.dot(part_refs[part][...], weights_ref[0], preferred_element_type=jnp.float32)
+            if part == 0:
+                projected_ref[...] = product
+            else:
+                projected_ref[...] += product
+
+    @pl.when(step == count - 1)
+    def _():
+        updated = own_ref[...].astype(jnp.float32) + gate_ref[...] * projected_ref[...]
+        live = lax.broadcasted_iota(jnp.int32, updated.shape, 0) < where_ref[1]
+        out_ref[...] = jnp.where(live, updated, 0.0).astype(out_ref.dtype)
 
 
 def leave_block(parts, out_weights, own_rows, gating_here, where):
     count = len(parts)
     span, head_width = parts[0].shape
-    vmem = pl.BlockSpec(memory_space=pltpu.VMEM)
-    smem = pl.BlockSpec(memory_space=pltpu.SMEM)
+    width = out_weights.shape[1]
+    whole = lambda shape: pl.BlockSpec(shape, lambda p, where: (0,) * len(shape))
+    grid_spec = pltpu.PrefetchScalarGridSpec(
+        num_scalar_prefetch=1,
+        grid=(count,),
+        in_specs=[whole((span, head_width)) for _ in parts]
+        + [
+            pl.BlockSpec((1, head_width, width), lambda p, where: (where[2 + p], 0, 0)),
+            whole(own_rows.shape),
+            whole((1, width)),
+        ],
+        out_specs=whole(own_rows.shape),
+        scratch_shapes=[pltpu.VMEM((span, width), jnp.float32)],
+    )
     return pl.pallas_call(
         exit_kernel,
-        in_specs=[smem] + [vmem] * (count + 3),
-        out_specs=vmem,
+        grid_spec=grid_spec,
         out_shape=jax.ShapeDtypeStruct(own_rows.shape, own_rows.dtype),
+        compiler_params=pltpu.CompilerParams(dimension_semantics=("arbitrary",)),
     )(
         where,
         *parts,
-        out_weights.reshape(count, head_width, out_weights.shape[1]),
+        out_weights.reshape(count, head_width, width),
         own_rows,
         gating_here.reshape(1, -1),
     )

time: 215 us -> 222 us (1.033)
  Pallas kernels: 66.6 us -> 73.4 us
    pallas_call x4, Pallas kernels: 16.5 us -> 21.7 us  [leave_block(): pl.pallas_call(exit_kernel, grid_spec=grid_spec, out_shape=jax.ShapeDtype...]
where the time goes in v8:
time: 222 us; the launch traced here: 221 us
  waiting for transfers between devices  81.5 us (37%)
  Pallas kernels  73.4 us (33%)
  starting transfers between devices  37.8 us (17%)
  other arithmetic  15.2 us (7%)
  local copies, waits for them, and re-layouts  7.35 us (3%)
  between operations  5.88 us (3%)
    pallas_call x4, Pallas kernels, attend_block(): pl.pallas_call(block_kernel, grid_spec=grid_spec, out_shape=[jax.ShapeDty...  51.6 us
    ppermute x5, waiting for transfers between devices, across_chips(): lax.ppermute(block, 'seq', [(source, (source + step) % count) for source...  37.4 us
    ppermute x6, waiting for transfers between devices, to_next_section(): lax.ppermute(block, ('section', 'seq'), [(section * count + source, (sect...  21.8 us
    pallas_call x4, Pallas kernels, leave_block(): pl.pallas_call(exit_kernel, grid_spec=grid_spec, out_shape=jax.ShapeDtype...  21.7 us
    ppermute x6, starting transfers between devices, to_next_section(): lax.ppermute(block, ('section', 'seq'), [(section * count + source, (sect...  16.7 us
    ppermute x3, waiting for transfers between devices, across_chips_first_section(): lax.ppermute(block, ('section', 'seq'), [(source, (source + step) % count...  12.8 us
    ppermute x3, starting transfers between devices, across_chips_first_section(): lax.ppermute(block, ('section', 'seq'), [(source, (source + step) % count...  11 us
    ppermute x16, waiting for transfers between devices, with_partner(): return parts + [lax.ppermute(part, 'seq', to_partner) for part in parts]  9.47 us
  transfers between devices with their start and end apart: 30, of which 20 were waited for; matrix products, arithmetic and copies ran while one was open for 5% of the time, Pallas kernels for 0%

profile of v8, /device:TPU:0, one launch (start us, length us, event | category | flops | bytes accessed | tf_op | source)
XLA Modules:
  0.0 221.1 jit_solution(3274972240347046142)
XLA Ops:
  0.0 0.8 reduce-window.9
  0.8 1.5 fusion.4
  2.9 1.2 fusion.3.refs_1_.refs_6_
  4.1 3.0 %collective-permute-start = (bf16[256,768]{1,0:T(8,128)(2,1)S(1)}, bf16[256,768]{1,0:T(8,128)(2,1)S(1)}, u32[]{:S(2)}, u32[]{:S(2)}) collective-permute-start(bf16[256,768]{1,0:T(8,128)(2,1)S(1)} %fusion.3.refs_1_.refs_6_), channel_id=1, source_target_pairs={{0,2},{1,3},{2,0},{3,1},{4,6},{5,7},{6,4},{7,5},{8,10},{9,11},{10,... | collective-permute-start | bytes 1179656 | tf_op jit(solution)/shard_map/ppermute | solution.py:22
  7.1 9.1 %collective-permute-done.refs_2_ = bf16[256,768]{1,0:T(8,128)(2,1)S(1)} collective-permute-done((bf16[256,768]{1,0:T(8,128)(2,1)S(1)}, bf16[256,768]{1,0:T(8,128)(2,1)S(1)}, u32[]{:S(2)}, u32[]{:S(2)}) %collective-permute-start) | collective-permute-done | bytes 393248 | tf_op jit(solution)/shard_map/ppermute | solution.py:22
  16.2 1.9 select_select_fusion.3
  19.0 12.9 %shard_map.91 = (bf16[256,512]{1,0:T(8,128)(2,1)}, bf16[4,768,128]{2,1,0:T(8,128)(2,1)}, bf16[4,768,128]{2,1,0:T(8,128)(2,1)}) custom-call(s32[6]{0:T(128)} %get-tuple-element.40.refs_0_, bf16[256,768]{1,0:T(8,128)(2,1)} %copy-done.4, bf16[256,768]{1,0:T(8,128)(2,1)} %copy-done.12, bf16[256,768]{1,0:T(8,128)(2,1)} %copy-done.13, ...), custom_call_target="tpu_custom_call" | custom-call | tf_op jit(solution)/shard_map/pallas_call | solution.py:158
  31.9 1.7 collective-permute-start.3
  33.9 7.0 %collective-permute-done.3.refs_2_ = bf16[256,512]{1,0:T(8,128)(2,1)S(1)} collective-permute-done((bf16[256,512]{1,0:T(8,128)(2,1)}, bf16[256,512]{1,0:T(8,128)(2,1)S(1)}, u32[]{:S(2)}, u32[]{:S(2)}) %collective-permute-start.3) | collective-permute-done | bytes 262176 | tf_op jit(solution)/shard_map/ppermute | solution.py:22
  40.8 1.5 collective-permute-done.5.refs_4_
  43.1 5.5 %shard_map.92 = bf16[256,768]{1,0:T(8,128)(2,1)} custom-call(s32[6]{0:T(128)} %get-tuple-element.40.refs_0_, bf16[256,512]{1,0:T(8,128)(2,1)} %get-tuple-element.15.refs_1_, bf16[256,512]{1,0:T(8,128)(2,1)} %copy-done.20, bf16[256,512]{1,0:T(8,128)(2,1)} %copy-done.24, bf16[256,512]{1,0:T(8,128)(2,1)} %copy-done.28, bf16[4,512,768]{2,1,0:T(8,128)(2,1)} %bitcast.33, ...), custom_call_target="tpu_custom_call" | custom-call | tf_op jit(solution)/shard_map/pallas_call | solution.py:212
  48.6 3.7 %collective-permute-start.6 = (bf16[256,768]{1,0:T(8,128)(2,1)}, bf16[256,768]{1,0:T(8,128)(2,1)S(1)}, u32[]{:S(2)}, u32[]{:S(2)}) collective-permute-start(bf16[256,768]{1,0:T(8,128)(2,1)} %shard_map.92), channel_id=1, source_target_pairs={{0,4},{1,5},{2,6},{3,7},{4,8},{5,9},{6,10},{7,11},{8,12},{9,13},{1... | collective-permute-start | bytes 1179656 | tf_op jit(solution)/shard_map/ppermute | solution.py:47
  55.9 4.4 %collective-permute-start.8 = (bf16[256,768]{1,0:T(8,128)(2,1)}, bf16[256,768]{1,0:T(8,128)(2,1)S(1)}, u32[]{:S(2)}, u32[]{:S(2)}) collective-permute-start(bf16[256,768]{1,0:T(8,128)(2,1)} %shard_map.92), channel_id=1, source_target_pairs={{0,6},{1,7},{2,4},{3,5},{4,10},{5,11},{6,8},{7,9},{8,14},{9,15},{1... | collective-permute-start | bytes 1179656 | tf_op jit(solution)/shard_map/ppermute | solution.py:47
  60.3 1.6 collective-permute-done.6
  62.2 3.7 %collective-permute-start.7 = (bf16[256,768]{1,0:T(8,128)(2,1)S(1)}, bf16[256,768]{1,0:T(8,128)(2,1)S(1)}, u32[]{:S(2)}, u32[]{:S(2)}) collective-permute-start(bf16[256,768]{1,0:T(8,128)(2,1)S(1)} %get-tuple-element.39), channel_id=1, source_target_pairs={{0,2},{1,3},{2,0},{3,1},{16,18},{17,19},{18,16},{19,17}} | collective-permute-start | bytes 1179656 | tf_op jit(solution)/shard_map/ppermute | solution.py:30
  66.0 3.7 %collective-permute-done.8 = bf16[256,768]{1,0:T(8,128)(2,1)S(1)} collective-permute-done((bf16[256,768]{1,0:T(8,128)(2,1)}, bf16[256,768]{1,0:T(8,128)(2,1)S(1)}, u32[]{:S(2)}, u32[]{:S(2)}) %collective-permute-start.8) | collective-permute-done | bytes 393248 | tf_op jit(solution)/shard_map/ppermute | solution.py:47
  69.7 4.1 %collective-permute-done.7 = bf16[256,768]{1,0:T(8,128)(2,1)S(1)} collective-permute-done((bf16[256,768]{1,0:T(8,128)(2,1)S(1)}, bf16[256,768]{1,0:T(8,128)(2,1)S(1)}, u32[]{:S(2)}, u32[]{:S(2)}) %collective-permute-start.7) | collective-permute-done | bytes 393248 | tf_op jit(solution)/shard_map/ppermute | solution.py:30
  73.9 4.3 %select_select_fusion.2 = (s32[6]{0:T(128)}, s32[6]{0:T(128)}, s32[6]{0:T(128)}) fusion(s32[6]{0:T(128)S(1)} %get-tuple-element.41, s32[]{:T(128)} %get-tuple-element.54, s32[]{:T(128)} %get-tuple-element.33, s32[]{:T(128)} %get-tuple-element.55, s32[]{:T(128)} %get-tuple-element.32, s32[]{:T(128)} %get-tuple-element.52, s32[]{:T(128)} %get-tuple-element.31), kind=kLoop, calls=%fused_computation.52 | loop fusion | flops 54 | bytes 120 | tf_op jit(solution)/shard_map/jit(_where)/select_n | solution.py:67
  79.1 12.9 %shard_map.93 = (bf16[256,512]{1,0:T(8,128)(2,1)}, bf16[4,768,128]{2,1,0:T(8,128)(2,1)}, bf16[4,768,128]{2,1,0:T(8,128)(2,1)}) custom-call(s32[6]{0:T(128)} %get-tuple-element.49.refs_0_, bf16[256,768]{1,0:T(8,128)(2,1)} %copy-done.1, bf16[256,768]{1,0:T(8,128)(2,1)} %copy-done.5, ...), custom_call_target="tpu_custom_call", output_to_operand_aliasing={{1}: (7, {}), {2}: (8, {})} | custom-call | tf_op jit(solution)/shard_map/pallas_call | solution.py:158
  92.0 1.5 collective-permute-start.11
  93.7 7.2 %collective-permute-done.11.refs_2_ = bf16[256,512]{1,0:T(8,128)(2,1)S(1)} collective-permute-done((bf16[256,512]{1,0:T(8,128)(2,1)}, bf16[256,512]{1,0:T(8,128)(2,1)S(1)}, u32[]{:S(2)}, u32[]{:S(2)}) %collective-permute-start.11) | collective-permute-done | bytes 262176 | tf_op jit(solution)/shard_map/ppermute | solution.py:22
  100.9 1.5 collective-permute-done.13.refs_4_
  103.2 5.4 %shard_map.94 = bf16[256,768]{1,0:T(8,128)(2,1)} custom-call(s32[6]{0:T(128)} %get-tuple-element.49.refs_0_, bf16[256,512]{1,0:T(8,128)(2,1)} %get-tuple-element.18.refs_1_, bf16[256,512]{1,0:T(8,128)(2,1)} %copy-done.21, bf16[256,512]{1,0:T(8,128)(2,1)} %copy-done.25, bf16[256,512]{1,0:T(8,128)(2,1)} %copy-done.29, bf16[4,512,768]{2,1,0:T(8,128)(2,1)} %bitcast.34, ...), custom_call_target="tpu_custom_call" | custom-call | tf_op jit(solution)/shard_map/pallas_call | solution.py:212
  108.6 1.3 collective-permute-start.14
  112.3 3.3 %collective-permute-start.16 = (bf16[256,768]{1,0:T(8,128)(2,1)}, bf16[256,768]{1,0:T(8,128)(2,1)S(1)}, u32[]{:S(2)}, u32[]{:S(2)}) collective-permute-start(bf16[256,768]{1,0:T(8,128)(2,1)} %shard_map.94), channel_id=1, source_target_pairs={{0,6},{1,7},{2,4},{3,5},{4,10},{5,11},{6,8},{7,9},{8,14},{9,15},{1... | collective-permute-start | bytes 1179656 | tf_op jit(solution)/shard_map/ppermute | solution.py:47
  115.7 3.9 %collective-permute-done.14 = bf16[256,768]{1,0:T(8,128)(2,1)S(1)} collective-permute-done((bf16[256,768]{1,0:T(8,128)(2,1)}, bf16[256,768]{1,0:T(8,128)(2,1)S(1)}, u32[]{:S(2)}, u32[]{:S(2)}) %collective-permute-start.14) | collective-permute-done | bytes 393248 | tf_op jit(solution)/shard_map/ppermute | solution.py:47
  119.8 3.6 %collective-permute-start.15 = (bf16[256,768]{1,0:T(8,128)(2,1)S(1)}, bf16[256,768]{1,0:T(8,128)(2,1)S(1)}, u32[]{:S(2)}, u32[]{:S(2)}) collective-permute-start(bf16[256,768]{1,0:T(8,128)(2,1)S(1)} %get-tuple-element.37), channel_id=1, source_target_pairs={{0,2},{1,3},{2,0},{3,1},{16,18},{17,19},{18,16},{19,17}} | collective-permute-start | bytes 1179656 | tf_op jit(solution)/shard_map/ppermute | solution.py:30
  123.6 4.0 %collective-permute-done.16 = bf16[256,768]{1,0:T(8,128)(2,1)S(1)} collective-permute-done((bf16[256,768]{1,0:T(8,128)(2,1)}, bf16[256,768]{1,0:T(8,128)(2,1)S(1)}, u32[]{:S(2)}, u32[]{:S(2)}) %collective-permute-start.16) | collective-permute-done | bytes 393248 | tf_op jit(solution)/shard_map/ppermute | solution.py:47
  127.5 4.4 %collective-permute-done.15 = bf16[256,768]{1,0:T(8,128)(2,1)S(1)} collective-permute-done((bf16[256,768]{1,0:T(8,128)(2,1)S(1)}, bf16[256,768]{1,0:T(8,128)(2,1)S(1)}, u32[]{:S(2)}, u32[]{:S(2)}) %collective-permute-start.15) | collective-permute-done | bytes 393248 | tf_op jit(solution)/shard_map/ppermute | solution.py:30
  132.1 1.7 collective-permute-done.18.refs_4_
  134.5 12.9 %shard_map.95 = (bf16[256,512]{1,0:T(8,128)(2,1)}, bf16[4,768,128]{2,1,0:T(8,128)(2,1)}, bf16[4,768,128]{2,1,0:T(8,128)(2,1)}) custom-call(s32[6]{0:T(128)} %get-tuple-element.50.refs_0_, bf16[256,768]{1,0:T(8,128)(2,1)} %copy-done.3, bf16[256,768]{1,0:T(8,128)(2,1)} %copy-done.7, ...), custom_call_target="tpu_custom_call", output_to_operand_aliasing={{1}: (7, {}), {2}: (8, {})} | custom-call | tf_op jit(solution)/shard_map/pallas_call | solution.py:158
  147.4 1.5 collective-permute-start.19
  148.9 7.1 %collective-permute-done.19.refs_2_ = bf16[256,512]{1,0:T(8,128)(2,1)S(1)} collective-permute-done((bf16[256,512]{1,0:T(8,128)(2,1)}, bf16[256,512]{1,0:T(8,128)(2,1)S(1)}, u32[]{:S(2)}, u32[]{:S(2)}) %collective-permute-start.19) | collective-permute-done | bytes 262176 | tf_op jit(solution)/shard_map/ppermute | solution.py:22
  156.0 1.5 collective-permute-done.21.refs_4_
  158.2 5.4 %shard_map.96 = bf16[256,768]{1,0:T(8,128)(2,1)} custom-call(s32[6]{0:T(128)} %get-tuple-element.50.refs_0_, bf16[256,512]{1,0:T(8,128)(2,1)} %get-tuple-element.21.refs_1_, bf16[256,512]{1,0:T(8,128)(2,1)} %copy-done.22, bf16[256,512]{1,0:T(8,128)(2,1)} %copy-done.26, bf16[256,512]{1,0:T(8,128)(2,1)} %copy-done.30, bf16[4,512,768]{2,1,0:T(8,128)(2,1)} %bitcast.35, ...), custom_call_target="tpu_custom_call" | custom-call | tf_op jit(solution)/shard_map/pallas_call | solution.py:212
  163.6 1.3 collective-permute-start.22
  167.4 2.6 %collective-permute-start.24 = (bf16[256,768]{1,0:T(8,128)(2,1)}, bf16[256,768]{1,0:T(8,128)(2,1)S(1)}, u32[]{:S(2)}, u32[]{:S(2)}) collective-permute-start(bf16[256,768]{1,0:T(8,128)(2,1)} %shard_map.96), channel_id=1, source_target_pairs={{0,6},{1,7},{2,4},{3,5},{4,10},{5,11},{6,8},{7,9},{8,14},{9,15},{1... | collective-permute-start | bytes 1179656 | tf_op jit(solution)/shard_map/ppermute | solution.py:47
  170.0 4.6 %collective-permute-done.22 = bf16[256,768]{1,0:T(8,128)(2,1)S(1)} collective-permute-done((bf16[256,768]{1,0:T(8,128)(2,1)}, bf16[256,768]{1,0:T(8,128)(2,1)S(1)}, u32[]{:S(2)}, u32[]{:S(2)}) %collective-permute-start.22) | collective-permute-done | bytes 393248 | tf_op jit(solution)/shard_map/ppermute | solution.py:47
  174.9 3.7 %collective-permute-start.23 = (bf16[256,768]{1,0:T(8,128)(2,1)S(1)}, bf16[256,768]{1,0:T(8,128)(2,1)S(1)}, u32[]{:S(2)}, u32[]{:S(2)}) collective-permute-start(bf16[256,768]{1,0:T(8,128)(2,1)S(1)} %get-tuple-element.35), channel_id=1, source_target_pairs={{0,2},{1,3},{2,0},{3,1},{16,18},{17,19},{18,16},{19,17}} | collective-permute-start | bytes 1179656 | tf_op jit(solution)/shard_map/ppermute | solution.py:30
  178.7 3.9 %collective-permute-done.24 = bf16[256,768]{1,0:T(8,128)(2,1)S(1)} collective-permute-done((bf16[256,768]{1,0:T(8,128)(2,1)}, bf16[256,768]{1,0:T(8,128)(2,1)S(1)}, u32[]{:S(2)}, u32[]{:S(2)}) %collective-permute-start.24) | collective-permute-done | bytes 393248 | tf_op jit(solution)/shard_map/ppermute | solution.py:47
  182.6 4.4 %collective-permute-done.23 = bf16[256,768]{1,0:T(8,128)(2,1)S(1)} collective-permute-done((bf16[256,768]{1,0:T(8,128)(2,1)S(1)}, bf16[256,768]{1,0:T(8,128)(2,1)S(1)}, u32[]{:S(2)}, u32[]{:S(2)}) %collective-permute-start.23) | collective-permute-done | bytes 393248 | tf_op jit(solution)/shard_map/ppermute | solution.py:30
  187.1 1.7 collective-permute-done.26.refs_4_
  189.6 12.9 %shard_map.97 = (bf16[256,512]{1,0:T(8,128)(2,1)}, bf16[4,768,128]{2,1,0:T(8,128)(2,1)}, bf16[4,768,128]{2,1,0:T(8,128)(2,1)}) custom-call(s32[6]{0:T(128)} %get-tuple-element.51.refs_0_, bf16[256,768]{1,0:T(8,128)(2,1)} %copy-done.2, bf16[256,768]{1,0:T(8,128)(2,1)} %copy-done.6, ...), custom_call_target="tpu_custom_call", output_to_operand_aliasing={{1}: (7, {}), {2}: (8, {})} | custom-call | tf_op jit(solution)/shard_map/pallas_call | solution.py:158
  202.5 1.6 collective-permute-start.27
  204.0 7.1 %collective-permute-done.27.refs_2_ = bf16[256,512]{1,0:T(8,128)(2,1)S(1)} collective-permute-done((bf16[256,512]{1,0:T(8,128)(2,1)}, bf16[256,512]{1,0:T(8,128)(2,1)S(1)}, u32[]{:S(2)}, u32[]{:S(2)}) %collective-permute-start.27) | collective-permute-done | bytes 262176 | tf_op jit(solution)/shard_map/ppermute | solution.py:22
  211.1 1.5 collective-permute-done.29.refs_4_
  213.4 5.4 %shard_map.98 = bf16[256,768]{1,0:T(8,128)(2,1)} custom-call(s32[6]{0:T(128)} %get-tuple-element.51.refs_0_, bf16[256,512]{1,0:T(8,128)(2,1)} %get-tuple-element.24.refs_1_, bf16[256,512]{1,0:T(8,128)(2,1)} %copy-done.23, bf16[256,512]{1,0:T(8,128)(2,1)} %copy-done.27, bf16[256,512]{1,0:T(8,128)(2,1)} %copy-done.31, bf16[4,512,768]{2,1,0:T(8,128)(2,1)} %bitcast.36, ...), custom_call_target="tpu_custom_call" | custom-call | tf_op jit(solution)/shard_map/pallas_call | solution.py:212
  218.8 2.3 %maximum_bitcast_fusion = bf16[4,1,256,768]{3,2,1,0:T(8,128)(2,1)} fusion(bf16[1,256,768]{2,1,0:T(8,128)(2,1)} %bitcast.40, bf16[1,256,768]{2,1,0:T(8,128)(2,1)S(1)} %bitcast.39, bf16[1,256,768]{2,1,0:T(8,128)(2,1)S(1)} %bitcast.38, bf16[1,256,768]{2,1,0:T(8,128)(2,1)S(1)} %bitcast.37), kind=kLoop, calls=%fused_computation.3 | loop fusion | flops 2359296 | bytes 3145728 | tf_op jit(solution)/shard_map/broadcast_in_dim | solution.py:296
  (104 shorter events, 11.4 us)
Async XLA Ops:
  4.1 14.0 %copy-start.4 = (bf16[256,768]{1,0:T(8,128)(2,1)}, bf16[256,768]{1,0:T(8,128)(2,1)S(1)}, u32[]{:S(2)}) copy-start(bf16[256,768]{1,0:T(8,128)(2,1)S(1)} %fusion.3.refs_1_.refs_6_) | copy-start | bytes 1179652
  4.1 12.1 %collective-permute-start = (bf16[256,768]{1,0:T(8,128)(2,1)S(1)}, bf16[256,768]{1,0:T(8,128)(2,1)S(1)}, u32[]{:S(2)}, u32[]{:S(2)}) collective-permute-start(bf16[256,768]{1,0:T(8,128)(2,1)S(1)} %fusion.3.refs_1_.refs_6_), channel_id=1, source_target_pairs={{0,2},{1,3},{2,0},{3,1},{4,6},{5,7},{6,4},{7,5},{8,10},{9,11},{10,... | collective-permute-start | bytes 1179656 | tf_op jit(solution)/shard_map/ppermute | solution.py:22
  7.1 11.0 %collective-permute-start.1 = (bf16[256,768]{1,0:T(8,128)(2,1)S(1)}, bf16[256,768]{1,0:T(8,128)(2,1)S(1)}, u32[]{:S(2)}, u32[]{:S(2)}) collective-permute-start(bf16[256,768]{1,0:T(8,128)(2,1)S(1)} %fusion.3.refs_1_.refs_6_), channel_id=1, source_target_pairs={{0,1},{1,0},{2,3},{3,2},{4,5},{5,4},{6,7},{7,6},{8,9},{9,8},{10,11... | collective-permute-start | bytes 1179656 | tf_op jit(solution)/shard_map/ppermute | solution.py:40
  16.2 1.9 copy-start.12
  16.2 1.9 collective-permute-start.2
  31.9 8.9 %collective-permute-start.3 = (bf16[256,512]{1,0:T(8,128)(2,1)}, bf16[256,512]{1,0:T(8,128)(2,1)S(1)}, u32[]{:S(2)}, u32[]{:S(2)}) collective-permute-start(bf16[256,512]{1,0:T(8,128)(2,1)} %get-tuple-element.15.refs_1_), channel_id=1, source_target_pairs={{0,2},{1,3},{2,0},{3,1},{4,6},{5,7},{6,4},{7,5},{8,10},{9,11},{10,... | collective-permute-start | bytes 786440 | tf_op jit(solution)/shard_map/ppermute | solution.py:22
  33.6 7.2 %collective-permute-start.4 = (bf16[256,512]{1,0:T(8,128)(2,1)}, bf16[256,512]{1,0:T(8,128)(2,1)S(1)}, u32[]{:S(2)}, u32[]{:S(2)}) collective-permute-start(bf16[256,512]{1,0:T(8,128)(2,1)} %get-tuple-element.15.refs_1_), channel_id=1, source_target_pairs={{0,1},{1,0},{2,3},{3,2},{4,5},{5,4},{6,7},{7,6},{8,9},{9,8},{10,11... | collective-permute-start | bytes 786440 | tf_op jit(solution)/shard_map/ppermute | solution.py:40
  40.8 1.5 copy-start.20
  40.8 1.5 collective-permute-start.5
  43.1 11.6 %copy-start.32 = (s32[4]{0:T(128)S(1)}, s32[4]{0:T(128)}, u32[]{:S(2)}) copy-start(s32[4]{0:T(128)} %param.11) | copy-start | bytes 52
  43.1 18.9 %copy-start = (bf16[768,768]{1,0:T(8,128)(2,1)S(1)}, bf16[768,768]{1,0:T(8,128)(2,1)}, u32[]{:S(2)}) copy-start(bf16[768,768]{1,0:T(8,128)(2,1)} %param.9) | copy-start | bytes 3538948
  48.6 13.4 %collective-permute-start.6 = (bf16[256,768]{1,0:T(8,128)(2,1)}, bf16[256,768]{1,0:T(8,128)(2,1)S(1)}, u32[]{:S(2)}, u32[]{:S(2)}) collective-permute-start(bf16[256,768]{1,0:T(8,128)(2,1)} %shard_map.92), channel_id=1, source_target_pairs={{0,4},{1,5},{2,6},{3,7},{4,8},{5,9},{6,10},{7,11},{8,12},{9,13},{1... | collective-permute-start | bytes 1179656 | tf_op jit(solution)/shard_map/ppermute | solution.py:47
  55.9 13.8 %collective-permute-start.8 = (bf16[256,768]{1,0:T(8,128)(2,1)}, bf16[256,768]{1,0:T(8,128)(2,1)S(1)}, u32[]{:S(2)}, u32[]{:S(2)}) collective-permute-start(bf16[256,768]{1,0:T(8,128)(2,1)} %shard_map.92), channel_id=1, source_target_pairs={{0,6},{1,7},{2,4},{3,5},{4,10},{5,11},{6,8},{7,9},{8,14},{9,15},{1... | collective-permute-start | bytes 1179656 | tf_op jit(solution)/shard_map/ppermute | solution.py:47
  62.2 16.0 %copy-start.1 = (bf16[256,768]{1,0:T(8,128)(2,1)}, bf16[256,768]{1,0:T(8,128)(2,1)S(1)}, u32[]{:S(2)}) copy-start(bf16[256,768]{1,0:T(8,128)(2,1)S(1)} %get-tuple-element.38.refs_1_.refs_6_) | copy-start | bytes 1179652
  62.2 11.6 %collective-permute-start.7 = (bf16[256,768]{1,0:T(8,128)(2,1)S(1)}, bf16[256,768]{1,0:T(8,128)(2,1)S(1)}, u32[]{:S(2)}, u32[]{:S(2)}) collective-permute-start(bf16[256,768]{1,0:T(8,128)(2,1)S(1)} %get-tuple-element.39), channel_id=1, source_target_pairs={{0,2},{1,3},{2,0},{3,1},{16,18},{17,19},{18,16},{19,17}} | collective-permute-start | bytes 1179656 | tf_op jit(solution)/shard_map/ppermute | solution.py:30
  65.9 12.3 %collective-permute-start.9 = (bf16[256,768]{1,0:T(8,128)(2,1)S(1)}, bf16[256,768]{1,0:T(8,128)(2,1)S(1)}, u32[]{:S(2)}, u32[]{:S(2)}) collective-permute-start(bf16[256,768]{1,0:T(8,128)(2,1)S(1)} %get-tuple-element.38.refs_1_.refs_6_), channel_id=1, source_target_pairs={{0,1},{1,0},{2,3},{3,2},{4,5},{5,4},{6,7},{7,6},{8,9},{9,8},{10,11... | collective-permute-start | bytes 1179656 | tf_op jit(solution)/shard_map/ppermute | solution.py:40
  73.8 4.4 %copy-start.5 = (bf16[256,768]{1,0:T(8,128)(2,1)}, bf16[256,768]{1,0:T(8,128)(2,1)S(1)}, u32[]{:S(2)}) copy-start(bf16[256,768]{1,0:T(8,128)(2,1)S(1)} %broadcast_select_fusion.4.refs_2_) | copy-start | bytes 1179652
  73.8 4.4 %collective-permute-start.10 = (bf16[256,768]{1,0:T(8,128)(2,1)S(1)}, bf16[256,768]{1,0:T(8,128)(2,1)S(1)}, u32[]{:S(2)}, u32[]{:S(2)}) collective-permute-start(bf16[256,768]{1,0:T(8,128)(2,1)S(1)} %broadcast_select_fusion.4.refs_2_), channel_id=1, source_target_pairs={{0,1},{1,0},{2,3},{3,2},{4,5},{5,4},{6,7},{7,6},{8,9},{9,8},{10,11... | collective-permute-start | bytes 1179656 | tf_op jit(solution)/shard_map/ppermute | solution.py:40
  92.0 8.9 %collective-permute-start.11 = (bf16[256,512]{1,0:T(8,128)(2,1)}, bf16[256,512]{1,0:T(8,128)(2,1)S(1)}, u32[]{:S(2)}, u32[]{:S(2)}) collective-permute-start(bf16[256,512]{1,0:T(8,128)(2,1)} %get-tuple-element.18.refs_1_), channel_id=1, source_target_pairs={{0,2},{1,3},{2,0},{3,1},{4,6},{5,7},{6,4},{7,5},{8,10},{9,11},{10,... | collective-permute-start | bytes 786440 | tf_op jit(solution)/shard_map/ppermute | solution.py:22
  93.5 7.4 %collective-permute-start.12 = (bf16[256,512]{1,0:T(8,128)(2,1)}, bf16[256,512]{1,0:T(8,128)(2,1)S(1)}, u32[]{:S(2)}, u32[]{:S(2)}) collective-permute-start(bf16[256,512]{1,0:T(8,128)(2,1)} %get-tuple-element.18.refs_1_), channel_id=1, source_target_pairs={{0,1},{1,0},{2,3},{3,2},{4,5},{5,4},{6,7},{7,6},{8,9},{9,8},{10,11... | collective-permute-start | bytes 786440 | tf_op jit(solution)/shard_map/ppermute | solution.py:40
  100.9 1.5 copy-start.21
  100.9 1.5 collective-permute-start.13
  108.6 11.0 %collective-permute-start.14 = (bf16[256,768]{1,0:T(8,128)(2,1)}, bf16[256,768]{1,0:T(8,128)(2,1)S(1)}, u32[]{:S(2)}, u32[]{:S(2)}) collective-permute-start(bf16[256,768]{1,0:T(8,128)(2,1)} %shard_map.94), channel_id=1, source_target_pairs={{0,4},{1,5},{2,6},{3,7},{4,8},{5,9},{6,10},{7,11},{8,12},{9,13},{1... | collective-permute-start | bytes 1179656 | tf_op jit(solution)/shard_map/ppermute | solution.py:47
  112.3 15.2 %collective-permute-start.16 = (bf16[256,768]{1,0:T(8,128)(2,1)}, bf16[256,768]{1,0:T(8,128)(2,1)S(1)}, u32[]{:S(2)}, u32[]{:S(2)}) collective-permute-start(bf16[256,768]{1,0:T(8,128)(2,1)} %shard_map.94), channel_id=1, source_target_pairs={{0,6},{1,7},{2,4},{3,5},{4,10},{5,11},{6,8},{7,9},{8,14},{9,15},{1... | collective-permute-start | bytes 1179656 | tf_op jit(solution)/shard_map/ppermute | solution.py:47
  119.8 13.9 %copy-start.3 = (bf16[256,768]{1,0:T(8,128)(2,1)}, bf16[256,768]{1,0:T(8,128)(2,1)S(1)}, u32[]{:S(2)}) copy-start(bf16[256,768]{1,0:T(8,128)(2,1)S(1)} %get-tuple-element.36.refs_1_.refs_6_) | copy-start | bytes 1179652
  119.8 12.1 %collective-permute-start.15 = (bf16[256,768]{1,0:T(8,128)(2,1)S(1)}, bf16[256,768]{1,0:T(8,128)(2,1)S(1)}, u32[]{:S(2)}, u32[]{:S(2)}) collective-permute-start(bf16[256,768]{1,0:T(8,128)(2,1)S(1)} %get-tuple-element.37), channel_id=1, source_target_pairs={{0,2},{1,3},{2,0},{3,1},{16,18},{17,19},{18,16},{19,17}} | collective-permute-start | bytes 1179656 | tf_op jit(solution)/shard_map/ppermute | solution.py:30
  123.5 8.6 %collective-permute-start.17 = (bf16[256,768]{1,0:T(8,128)(2,1)S(1)}, bf16[256,768]{1,0:T(8,128)(2,1)S(1)}, u32[]{:S(2)}, u32[]{:S(2)}) collective-permute-start(bf16[256,768]{1,0:T(8,128)(2,1)S(1)} %get-tuple-element.36.refs_1_.refs_6_), channel_id=1, source_target_pairs={{0,1},{1,0},{2,3},{3,2},{4,5},{5,4},{6,7},{7,6},{8,9},{9,8},{10,11... | collective-permute-start | bytes 1179656 | tf_op jit(solution)/shard_map/ppermute | solution.py:40
  132.0 1.8 copy-start.7
  132.0 1.8 collective-permute-start.18
  132.1 1.7 copy-start.16
  147.4 8.6 %collective-permute-start.19 = (bf16[256,512]{1,0:T(8,128)(2,1)}, bf16[256,512]{1,0:T(8,128)(2,1)S(1)}, u32[]{:S(2)}, u32[]{:S(2)}) collective-permute-start(bf16[256,512]{1,0:T(8,128)(2,1)} %get-tuple-element.21.refs_1_), channel_id=1, source_target_pairs={{0,2},{1,3},{2,0},{3,1},{4,6},{5,7},{6,4},{7,5},{8,10},{9,11},{10,... | collective-permute-start | bytes 786440 | tf_op jit(solution)/shard_map/ppermute | solution.py:22
  148.9 7.1 %collective-permute-start.20 = (bf16[256,512]{1,0:T(8,128)(2,1)}, bf16[256,512]{1,0:T(8,128)(2,1)S(1)}, u32[]{:S(2)}, u32[]{:S(2)}) collective-permute-start(bf16[256,512]{1,0:T(8,128)(2,1)} %get-tuple-element.21.refs_1_), channel_id=1, source_target_pairs={{0,1},{1,0},{2,3},{3,2},{4,5},{5,4},{6,7},{7,6},{8,9},{9,8},{10,11... | collective-permute-start | bytes 786440 | tf_op jit(solution)/shard_map/ppermute | solution.py:40
  156.0 1.5 copy-start.22
  156.0 1.5 collective-permute-start.21
  163.6 11.0 %collective-permute-start.22 = (bf16[256,768]{1,0:T(8,128)(2,1)}, bf16[256,768]{1,0:T(8,128)(2,1)S(1)}, u32[]{:S(2)}, u32[]{:S(2)}) collective-permute-start(bf16[256,768]{1,0:T(8,128)(2,1)} %shard_map.96), channel_id=1, source_target_pairs={{0,4},{1,5},{2,6},{3,7},{4,8},{5,9},{6,10},{7,11},{8,12},{9,13},{1... | collective-permute-start | bytes 1179656 | tf_op jit(solution)/shard_map/ppermute | solution.py:47
  167.4 15.2 %collective-permute-start.24 = (bf16[256,768]{1,0:T(8,128)(2,1)}, bf16[256,768]{1,0:T(8,128)(2,1)S(1)}, u32[]{:S(2)}, u32[]{:S(2)}) collective-permute-start(bf16[256,768]{1,0:T(8,128)(2,1)} %shard_map.96), channel_id=1, source_target_pairs={{0,6},{1,7},{2,4},{3,5},{4,10},{5,11},{6,8},{7,9},{8,14},{9,15},{1... | collective-permute-start | bytes 1179656 | tf_op jit(solution)/shard_map/ppermute | solution.py:47
  174.9 13.9 %copy-start.2 = (bf16[256,768]{1,0:T(8,128)(2,1)}, bf16[256,768]{1,0:T(8,128)(2,1)S(1)}, u32[]{:S(2)}) copy-start(bf16[256,768]{1,0:T(8,128)(2,1)S(1)} %get-tuple-element.34.refs_1_.refs_6_) | copy-start | bytes 1179652
  174.9 12.0 %collective-permute-start.23 = (bf16[256,768]{1,0:T(8,128)(2,1)S(1)}, bf16[256,768]{1,0:T(8,128)(2,1)S(1)}, u32[]{:S(2)}, u32[]{:S(2)}) collective-permute-start(bf16[256,768]{1,0:T(8,128)(2,1)S(1)} %get-tuple-element.35), channel_id=1, source_target_pairs={{0,2},{1,3},{2,0},{3,1},{16,18},{17,19},{18,16},{19,17}} | collective-permute-start | bytes 1179656 | tf_op jit(solution)/shard_map/ppermute | solution.py:30
  178.6 8.5 %collective-permute-start.25 = (bf16[256,768]{1,0:T(8,128)(2,1)S(1)}, bf16[256,768]{1,0:T(8,128)(2,1)S(1)}, u32[]{:S(2)}, u32[]{:S(2)}) collective-permute-start(bf16[256,768]{1,0:T(8,128)(2,1)S(1)} %get-tuple-element.34.refs_1_.refs_6_), channel_id=1, source_target_pairs={{0,1},{1,0},{2,3},{3,2},{4,5},{5,4},{6,7},{7,6},{8,9},{9,8},{10,11... | collective-permute-start | bytes 1179656 | tf_op jit(solution)/shard_map/ppermute | solution.py:40
  187.0 1.8 copy-start.6
  187.0 1.8 collective-permute-start.26
  187.1 1.7 copy-start.14
  202.5 16.3 %copy-start.8 = (bf16[256,768]{1,0:T(8,128)(2,1)S(1)}, bf16[256,768]{1,0:T(8,128)(2,1)}, u32[]{:S(2)}) copy-start(bf16[256,768]{1,0:T(8,128)(2,1)} %shard_map.92) | copy-start | bytes 1179652
  202.5 16.3 %copy-start.9 = (bf16[256,768]{1,0:T(8,128)(2,1)S(1)}, bf16[256,768]{1,0:T(8,128)(2,1)}, u32[]{:S(2)}) copy-start(bf16[256,768]{1,0:T(8,128)(2,1)} %shard_map.94) | copy-start | bytes 1179652
  202.5 16.3 %copy-start.10 = (bf16[256,768]{1,0:T(8,128)(2,1)S(1)}, bf16[256,768]{1,0:T(8,128)(2,1)}, u32[]{:S(2)}) copy-start(bf16[256,768]{1,0:T(8,128)(2,1)} %shard_map.96) | copy-start | bytes 1179652
  202.5 8.6 %collective-permute-start.27 = (bf16[256,512]{1,0:T(8,128)(2,1)}, bf16[256,512]{1,0:T(8,128)(2,1)S(1)}, u32[]{:S(2)}, u32[]{:S(2)}) collective-permute-start(bf16[256,512]{1,0:T(8,128)(2,1)} %get-tuple-element.24.refs_1_), channel_id=1, source_target_pairs={{0,2},{1,3},{2,0},{3,1},{4,6},{5,7},{6,4},{7,5},{8,10},{9,11},{10,... | collective-permute-start | bytes 786440 | tf_op jit(solution)/shard_map/ppermute | solution.py:22
  204.0 7.1 %collective-permute-start.28 = (bf16[256,512]{1,0:T(8,128)(2,1)}, bf16[256,512]{1,0:T(8,128)(2,1)S(1)}, u32[]{:S(2)}, u32[]{:S(2)}) collective-permute-start(bf16[256,512]{1,0:T(8,128)(2,1)} %get-tuple-element.24.refs_1_), channel_id=1, source_target_pairs={{0,1},{1,0},{2,3},{3,2},{4,5},{5,4},{6,7},{7,6},{8,9},{9,8},{10,11... | collective-permute-start | bytes 786440 | tf_op jit(solution)/shard_map/ppermute | solution.py:40
  211.1 1.5 collective-permute-start.29
  (15 other events, 15.3 us)

commit v9 on v7

--- a/solution.py
+++ b/solution.py
@@ -57,11 +57,19 @@
     ]
 
 
-def kernel_table(patch_start, patch_count):
+def kernel_tables(patch_sizes_list, section_index):
+    patches = patch_sizes_list.shape[0]
     count = lax.axis_size("seq")
     here = lax.axis_index("seq")
     chips = count // 2
-    entry = jnp.arange(count + 2) - 2
+    turn = lax.broadcasted_iota(jnp.int32, (patches, count + 2), 0)
+    entry = lax.broadcasted_iota(jnp.int32, (patches, count + 2), 1) - 2
+    patch_index = jnp.remainder(turn - section_index + patches, patches)
+    patch_ids = jnp.arange(patches).reshape(1, 1, patches)
+    sizes = patch_sizes_list.reshape(1, 1, patches)
+    chosen = patch_ids == patch_index[:, :, None]
+    patch_count = jnp.sum(jnp.where(chosen, sizes, 0), axis=-1)
+    patch_start = jnp.sum(jnp.where(patch_ids < patch_index[:, :, None], sizes, 0), axis=-1)
     base = jnp.where(entry < chips, here, jnp.bitwise_xor(here, 1))
     sources = jnp.remainder(base - 2 * jnp.remainder(entry, chips) + count, count)
     return jnp.where(entry == -2, patch_start, jnp.where(entry == -1, patch_count, sources)).astype(
@@ -241,12 +249,12 @@
         own_rows,
         0,
     )
+    tables, own_rows = lax.optimization_barrier(
+        (kernel_tables(patch_sizes_list, section_index), own_rows)
+    )
     row_parts = [own_rows] + across_chips(own_rows)
     for turn_number in range(patches):
-        patch_index = jnp.remainder(turn_number - section_index, patches)
-        patch_count = pick_entry(patch_sizes_list, patch_index)
-        patch_start = pick_entry(starts, patch_index)
-        where = kernel_table(patch_start, patch_count)
+        where = tables[turn_number]
         head_rows, key_cache, value_cache = attend_block(
             with_partner(row_parts),
             shift_scale,

time: 215 us -> 212 us (0.986)
  other arithmetic: 15.2 us -> 9.95 us
    select_n x2 -> x3, other arithmetic: 6.17 us -> 0.09 us  [the longest x1 0.07 us: kernel_tables(): patch_index = jnp.remainder(turn - section_index + patches, patches)]
    ppermute x16, waiting for transfers between devices: 9.47 us -> 12.2 us  [with_partner(): return parts + [lax.ppermute(part, 'seq', to_partner) for part in parts]]
  transfers between devices with their start and end apart: 30 -> 30, of which waited for: 20 -> 22; matrix products, arithmetic and copies ran while one was open for 5% -> 2% of each run, Pallas kernels for 0% -> 0%
where the time goes in v9:
time: 212 us; the launch traced here: 211 us
  waiting for transfers between devices  83.7 us (39%)
  Pallas kernels  66.6 us (31%)
  starting transfers between devices  37.2 us (18%)
  other arithmetic  9.95 us (5%)
  local copies, waits for them, and re-layouts  7.81 us (4%)
  between operations  6.26 us (3%)
    pallas_call x4, Pallas kernels, attend_block(): pl.pallas_call(block_kernel, grid_spec=grid_spec, out_shape=[jax.ShapeDty...  50.1 us
    ppermute x5, waiting for transfers between devices, across_chips(): lax.ppermute(block, 'seq', [(source, (source + step) % count) for source...  37.1 us
    ppermute x6, waiting for transfers between devices, to_next_section(): lax.ppermute(block, ('section', 'seq'), [(section * count + source, (sect...  21.5 us
    ppermute x6, starting transfers between devices, to_next_section(): lax.ppermute(block, ('section', 'seq'), [(section * count + source, (sect...  16.6 us
    pallas_call x4, Pallas kernels, leave_block(): pl.pallas_call(exit_kernel, in_specs=[smem] + [vmem] * (count + 3), out_s...  16.5 us
    ppermute x3, waiting for transfers between devices, across_chips_first_section(): lax.ppermute(block, ('section', 'seq'), [(source, (source + step) % count...  12.8 us
    ppermute x16, waiting for transfers between devices, with_partner(): return parts + [lax.ppermute(part, 'seq', to_partner) for part in parts]  12.2 us
    ppermute x3, starting transfers between devices, across_chips_first_section(): lax.ppermute(block, ('section', 'seq'), [(source, (source + step) % count...  10.8 us
  transfers between devices with their start and end apart: 30, of which 22 were waited for; matrix products, arithmetic and copies ran while one was open for 2% of the time, Pallas kernels for 0%

profile of v9, /device:TPU:0, one launch (start us, length us, event | category | flops | bytes accessed | tf_op | source)
XLA Modules:
  0.0 211.4 jit_solution(2306492641416558582)
XLA Ops:
  0.1 0.8 reduce-window.9
  0.9 1.3 bitcast_subtract_fusion
  3.7 1.2 fusion.3.refs_1_.refs_6_
  4.9 3.0 %collective-permute-start = (bf16[256,768]{1,0:T(8,128)(2,1)S(1)}, bf16[256,768]{1,0:T(8,128)(2,1)S(1)}, u32[]{:S(2)}, u32[]{:S(2)}) collective-permute-start(bf16[256,768]{1,0:T(8,128)(2,1)S(1)} %fusion.3.refs_1_.refs_6_), channel_id=1, source_target_pairs={{0,2},{1,3},{2,0},{3,1},{4,6},{5,7},{6,4},{7,5},{8,10},{9,11},{10,... | collective-permute-start | bytes 1179656 | tf_op jit(solution)/shard_map/ppermute | solution.py:22
  7.9 9.1 %collective-permute-done.refs_2_ = bf16[256,768]{1,0:T(8,128)(2,1)S(1)} collective-permute-done((bf16[256,768]{1,0:T(8,128)(2,1)S(1)}, bf16[256,768]{1,0:T(8,128)(2,1)S(1)}, u32[]{:S(2)}, u32[]{:S(2)}) %collective-permute-start) | collective-permute-done | bytes 393248 | tf_op jit(solution)/shard_map/ppermute | solution.py:22
  17.7 1.1 collective-permute-done.2.refs_4_
  19.6 12.5 %shard_map.91 = (bf16[256,512]{1,0:T(8,128)(2,1)}, bf16[4,768,128]{2,1,0:T(8,128)(2,1)}, bf16[4,768,128]{2,1,0:T(8,128)(2,1)}) custom-call(s32[6]{0:T(128)} %get-tuple-element.37.refs_0_, bf16[256,768]{1,0:T(8,128)(2,1)} %copy-done.4, bf16[256,768]{1,0:T(8,128)(2,1)} %copy-done.12, bf16[256,768]{1,0:T(8,128)(2,1)} %copy-done.15, ...), custom_call_target="tpu_custom_call" | custom-call | tf_op jit(solution)/shard_map/pallas_call | solution.py:165
  32.1 1.8 collective-permute-start.3
  33.8 6.8 %collective-permute-done.3.refs_2_ = bf16[256,512]{1,0:T(8,128)(2,1)S(1)} collective-permute-done((bf16[256,512]{1,0:T(8,128)(2,1)}, bf16[256,512]{1,0:T(8,128)(2,1)S(1)}, u32[]{:S(2)}, u32[]{:S(2)}) %collective-permute-start.3) | collective-permute-done | bytes 262176 | tf_op jit(solution)/shard_map/ppermute | solution.py:22
  40.7 1.5 collective-permute-done.5.refs_4_
  42.9 4.2 %shard_map.92 = bf16[256,768]{1,0:T(8,128)(2,1)} custom-call(s32[6]{0:T(128)} %get-tuple-element.37.refs_0_, bf16[256,512]{1,0:T(8,128)(2,1)} %get-tuple-element.19.refs_1_, bf16[256,512]{1,0:T(8,128)(2,1)} %copy-done.20, bf16[256,512]{1,0:T(8,128)(2,1)} %copy-done.24, bf16[256,512]{1,0:T(8,128)(2,1)} %copy-done.28, bf16[4,512,768]{2,1,0:T(8,128)(2,1)} %bitcast.40, ...), custom_call_target="tpu_custom_call" | custom-call | tf_op jit(solution)/shard_map/pallas_call | solution.py:203
  47.1 3.7 %collective-permute-start.6 = (bf16[256,768]{1,0:T(8,128)(2,1)}, bf16[256,768]{1,0:T(8,128)(2,1)S(1)}, u32[]{:S(2)}, u32[]{:S(2)}) collective-permute-start(bf16[256,768]{1,0:T(8,128)(2,1)} %shard_map.92), channel_id=1, source_target_pairs={{0,4},{1,5},{2,6},{3,7},{4,8},{5,9},{6,10},{7,11},{8,12},{9,13},{1... | collective-permute-start | bytes 1179656 | tf_op jit(solution)/shard_map/ppermute | solution.py:47
  54.6 4.4 %collective-permute-start.8 = (bf16[256,768]{1,0:T(8,128)(2,1)}, bf16[256,768]{1,0:T(8,128)(2,1)S(1)}, u32[]{:S(2)}, u32[]{:S(2)}) collective-permute-start(bf16[256,768]{1,0:T(8,128)(2,1)} %shard_map.92), channel_id=1, source_target_pairs={{0,6},{1,7},{2,4},{3,5},{4,10},{5,11},{6,8},{7,9},{8,14},{9,15},{1... | collective-permute-start | bytes 1179656 | tf_op jit(solution)/shard_map/ppermute | solution.py:47
  59.0 1.1 collective-permute-done.6
  60.4 3.8 %collective-permute-start.7 = (bf16[256,768]{1,0:T(8,128)(2,1)S(1)}, bf16[256,768]{1,0:T(8,128)(2,1)S(1)}, u32[]{:S(2)}, u32[]{:S(2)}) collective-permute-start(bf16[256,768]{1,0:T(8,128)(2,1)S(1)} %get-tuple-element.36), channel_id=1, source_target_pairs={{0,2},{1,3},{2,0},{3,1},{16,18},{17,19},{18,16},{19,17}} | collective-permute-start | bytes 1179656 | tf_op jit(solution)/shard_map/ppermute | solution.py:30
  64.3 3.9 %collective-permute-done.8 = bf16[256,768]{1,0:T(8,128)(2,1)S(1)} collective-permute-done((bf16[256,768]{1,0:T(8,128)(2,1)}, bf16[256,768]{1,0:T(8,128)(2,1)S(1)}, u32[]{:S(2)}, u32[]{:S(2)}) %collective-permute-start.8) | collective-permute-done | bytes 393248 | tf_op jit(solution)/shard_map/ppermute | solution.py:47
  68.2 4.1 %collective-permute-done.7 = bf16[256,768]{1,0:T(8,128)(2,1)S(1)} collective-permute-done((bf16[256,768]{1,0:T(8,128)(2,1)S(1)}, bf16[256,768]{1,0:T(8,128)(2,1)S(1)}, u32[]{:S(2)}, u32[]{:S(2)}) %collective-permute-start.7) | collective-permute-done | bytes 393248 | tf_op jit(solution)/shard_map/ppermute | solution.py:30
  72.4 1.7 collective-permute-done.10.refs_4_
  74.8 12.5 %shard_map.93 = (bf16[256,512]{1,0:T(8,128)(2,1)}, bf16[4,768,128]{2,1,0:T(8,128)(2,1)}, bf16[4,768,128]{2,1,0:T(8,128)(2,1)}) custom-call(s32[6]{0:T(128)} %get-tuple-element.40.refs_0_, bf16[256,768]{1,0:T(8,128)(2,1)} %copy-done.2, bf16[256,768]{1,0:T(8,128)(2,1)} %copy-done.6, ...), custom_call_target="tpu_custom_call", output_to_operand_aliasing={{1}: (7, {}), {2}: (8, {})} | custom-call | tf_op jit(solution)/shard_map/pallas_call | solution.py:165
  87.4 1.5 collective-permute-start.11
  88.9 7.1 %collective-permute-done.11.refs_2_ = bf16[256,512]{1,0:T(8,128)(2,1)S(1)} collective-permute-done((bf16[256,512]{1,0:T(8,128)(2,1)}, bf16[256,512]{1,0:T(8,128)(2,1)S(1)}, u32[]{:S(2)}, u32[]{:S(2)}) %collective-permute-start.11) | collective-permute-done | bytes 262176 | tf_op jit(solution)/shard_map/ppermute | solution.py:22
  96.0 1.5 collective-permute-done.13.refs_4_
  98.2 4.1 %shard_map.94 = bf16[256,768]{1,0:T(8,128)(2,1)} custom-call(s32[6]{0:T(128)} %get-tuple-element.40.refs_0_, bf16[256,512]{1,0:T(8,128)(2,1)} %get-tuple-element.22.refs_1_, bf16[256,512]{1,0:T(8,128)(2,1)} %copy-done.21, bf16[256,512]{1,0:T(8,128)(2,1)} %copy-done.25, bf16[256,512]{1,0:T(8,128)(2,1)} %copy-done.29, bf16[4,512,768]{2,1,0:T(8,128)(2,1)} %bitcast.41, ...), custom_call_target="tpu_custom_call" | custom-call | tf_op jit(solution)/shard_map/pallas_call | solution.py:203
  102.3 1.3 collective-permute-start.14
  106.3 3.3 %collective-permute-start.16 = (bf16[256,768]{1,0:T(8,128)(2,1)}, bf16[256,768]{1,0:T(8,128)(2,1)S(1)}, u32[]{:S(2)}, u32[]{:S(2)}) collective-permute-start(bf16[256,768]{1,0:T(8,128)(2,1)} %shard_map.94), channel_id=1, source_target_pairs={{0,6},{1,7},{2,4},{3,5},{4,10},{5,11},{6,8},{7,9},{8,14},{9,15},{1... | collective-permute-start | bytes 1179656 | tf_op jit(solution)/shard_map/ppermute | solution.py:47
  109.6 3.7 %collective-permute-done.14 = bf16[256,768]{1,0:T(8,128)(2,1)S(1)} collective-permute-done((bf16[256,768]{1,0:T(8,128)(2,1)}, bf16[256,768]{1,0:T(8,128)(2,1)S(1)}, u32[]{:S(2)}, u32[]{:S(2)}) %collective-permute-start.14) | collective-permute-done | bytes 393248 | tf_op jit(solution)/shard_map/ppermute | solution.py:47
  113.6 3.6 %collective-permute-start.15 = (bf16[256,768]{1,0:T(8,128)(2,1)S(1)}, bf16[256,768]{1,0:T(8,128)(2,1)S(1)}, u32[]{:S(2)}, u32[]{:S(2)}) collective-permute-start(bf16[256,768]{1,0:T(8,128)(2,1)S(1)} %get-tuple-element.34), channel_id=1, source_target_pairs={{0,2},{1,3},{2,0},{3,1},{16,18},{17,19},{18,16},{19,17}} | collective-permute-start | bytes 1179656 | tf_op jit(solution)/shard_map/ppermute | solution.py:30
  117.2 4.0 %collective-permute-done.16 = bf16[256,768]{1,0:T(8,128)(2,1)S(1)} collective-permute-done((bf16[256,768]{1,0:T(8,128)(2,1)}, bf16[256,768]{1,0:T(8,128)(2,1)S(1)}, u32[]{:S(2)}, u32[]{:S(2)}) %collective-permute-start.16) | collective-permute-done | bytes 393248 | tf_op jit(solution)/shard_map/ppermute | solution.py:47
  121.2 4.4 %collective-permute-done.15 = bf16[256,768]{1,0:T(8,128)(2,1)S(1)} collective-permute-done((bf16[256,768]{1,0:T(8,128)(2,1)S(1)}, bf16[256,768]{1,0:T(8,128)(2,1)S(1)}, u32[]{:S(2)}, u32[]{:S(2)}) %collective-permute-start.15) | collective-permute-done | bytes 393248 | tf_op jit(solution)/shard_map/ppermute | solution.py:30
  125.8 1.7 collective-permute-done.18.refs_4_
  128.2 12.5 %shard_map.95 = (bf16[256,512]{1,0:T(8,128)(2,1)}, bf16[4,768,128]{2,1,0:T(8,128)(2,1)}, bf16[4,768,128]{2,1,0:T(8,128)(2,1)}) custom-call(s32[6]{0:T(128)} %get-tuple-element.39.refs_0_, bf16[256,768]{1,0:T(8,128)(2,1)} %copy-done.3, bf16[256,768]{1,0:T(8,128)(2,1)} %copy-done.7, ...), custom_call_target="tpu_custom_call", output_to_operand_aliasing={{1}: (7, {}), {2}: (8, {})} | custom-call | tf_op jit(solution)/shard_map/pallas_call | solution.py:165
  140.7 1.5 collective-permute-start.19
  142.2 7.1 %collective-permute-done.19.refs_2_ = bf16[256,512]{1,0:T(8,128)(2,1)S(1)} collective-permute-done((bf16[256,512]{1,0:T(8,128)(2,1)}, bf16[256,512]{1,0:T(8,128)(2,1)S(1)}, u32[]{:S(2)}, u32[]{:S(2)}) %collective-permute-start.19) | collective-permute-done | bytes 262176 | tf_op jit(solution)/shard_map/ppermute | solution.py:22
  149.3 1.5 collective-permute-done.21.refs_4_
  151.5 4.1 %shard_map.96 = bf16[256,768]{1,0:T(8,128)(2,1)} custom-call(s32[6]{0:T(128)} %get-tuple-element.39.refs_0_, bf16[256,512]{1,0:T(8,128)(2,1)} %get-tuple-element.25.refs_1_, bf16[256,512]{1,0:T(8,128)(2,1)} %copy-done.22, bf16[256,512]{1,0:T(8,128)(2,1)} %copy-done.26, bf16[256,512]{1,0:T(8,128)(2,1)} %copy-done.30, bf16[4,512,768]{2,1,0:T(8,128)(2,1)} %bitcast.42, ...), custom_call_target="tpu_custom_call" | custom-call | tf_op jit(solution)/shard_map/pallas_call | solution.py:203
  155.7 1.3 collective-permute-start.22
  159.5 2.6 %collective-permute-start.24 = (bf16[256,768]{1,0:T(8,128)(2,1)}, bf16[256,768]{1,0:T(8,128)(2,1)S(1)}, u32[]{:S(2)}, u32[]{:S(2)}) collective-permute-start(bf16[256,768]{1,0:T(8,128)(2,1)} %shard_map.96), channel_id=1, source_target_pairs={{0,6},{1,7},{2,4},{3,5},{4,10},{5,11},{6,8},{7,9},{8,14},{9,15},{1... | collective-permute-start | bytes 1179656 | tf_op jit(solution)/shard_map/ppermute | solution.py:47
  162.1 4.6 %collective-permute-done.22 = bf16[256,768]{1,0:T(8,128)(2,1)S(1)} collective-permute-done((bf16[256,768]{1,0:T(8,128)(2,1)}, bf16[256,768]{1,0:T(8,128)(2,1)S(1)}, u32[]{:S(2)}, u32[]{:S(2)}) %collective-permute-start.22) | collective-permute-done | bytes 393248 | tf_op jit(solution)/shard_map/ppermute | solution.py:47
  166.9 3.4 %collective-permute-start.23 = (bf16[256,768]{1,0:T(8,128)(2,1)S(1)}, bf16[256,768]{1,0:T(8,128)(2,1)S(1)}, u32[]{:S(2)}, u32[]{:S(2)}) collective-permute-start(bf16[256,768]{1,0:T(8,128)(2,1)S(1)} %get-tuple-element.32), channel_id=1, source_target_pairs={{0,2},{1,3},{2,0},{3,1},{16,18},{17,19},{18,16},{19,17}} | collective-permute-start | bytes 1179656 | tf_op jit(solution)/shard_map/ppermute | solution.py:30
  170.4 4.2 %collective-permute-done.24 = bf16[256,768]{1,0:T(8,128)(2,1)S(1)} collective-permute-done((bf16[256,768]{1,0:T(8,128)(2,1)}, bf16[256,768]{1,0:T(8,128)(2,1)S(1)}, u32[]{:S(2)}, u32[]{:S(2)}) %collective-permute-start.24) | collective-permute-done | bytes 393248 | tf_op jit(solution)/shard_map/ppermute | solution.py:47
  174.6 4.4 %collective-permute-done.23 = bf16[256,768]{1,0:T(8,128)(2,1)S(1)} collective-permute-done((bf16[256,768]{1,0:T(8,128)(2,1)S(1)}, bf16[256,768]{1,0:T(8,128)(2,1)S(1)}, u32[]{:S(2)}, u32[]{:S(2)}) %collective-permute-start.23) | collective-permute-done | bytes 393248 | tf_op jit(solution)/shard_map/ppermute | solution.py:30
  179.1 1.7 collective-permute-done.26.refs_4_
  181.6 12.5 %shard_map.97 = (bf16[256,512]{1,0:T(8,128)(2,1)}, bf16[4,768,128]{2,1,0:T(8,128)(2,1)}, bf16[4,768,128]{2,1,0:T(8,128)(2,1)}) custom-call(s32[6]{0:T(128)} %get-tuple-element.38.refs_0_, bf16[256,768]{1,0:T(8,128)(2,1)} %copy-done.1, bf16[256,768]{1,0:T(8,128)(2,1)} %copy-done.5, ...), custom_call_target="tpu_custom_call", output_to_operand_aliasing={{1}: (7, {}), {2}: (8, {})} | custom-call | tf_op jit(solution)/shard_map/pallas_call | solution.py:165
  194.1 1.6 collective-permute-start.27
  195.7 7.1 %collective-permute-done.27.refs_2_ = bf16[256,512]{1,0:T(8,128)(2,1)S(1)} collective-permute-done((bf16[256,512]{1,0:T(8,128)(2,1)}, bf16[256,512]{1,0:T(8,128)(2,1)S(1)}, u32[]{:S(2)}, u32[]{:S(2)}) %collective-permute-start.27) | collective-permute-done | bytes 262176 | tf_op jit(solution)/shard_map/ppermute | solution.py:22
  202.7 1.5 collective-permute-done.29.refs_4_
  205.0 4.1 %shard_map.98 = bf16[256,768]{1,0:T(8,128)(2,1)} custom-call(s32[6]{0:T(128)} %get-tuple-element.38.refs_0_, bf16[256,512]{1,0:T(8,128)(2,1)} %get-tuple-element.28.refs_1_, bf16[256,512]{1,0:T(8,128)(2,1)} %copy-done.23, bf16[256,512]{1,0:T(8,128)(2,1)} %copy-done.27, bf16[256,512]{1,0:T(8,128)(2,1)} %copy-done.31, bf16[4,512,768]{2,1,0:T(8,128)(2,1)} %bitcast.43, ...), custom_call_target="tpu_custom_call" | custom-call | tf_op jit(solution)/shard_map/pallas_call | solution.py:203
  209.1 2.3 %maximum_bitcast_fusion = bf16[4,1,256,768]{3,2,1,0:T(8,128)(2,1)} fusion(bf16[1,256,768]{2,1,0:T(8,128)(2,1)} %bitcast.47, bf16[1,256,768]{2,1,0:T(8,128)(2,1)S(1)} %bitcast.46, bf16[1,256,768]{2,1,0:T(8,128)(2,1)S(1)} %bitcast.45, bf16[1,256,768]{2,1,0:T(8,128)(2,1)S(1)} %bitcast.44), kind=kLoop, calls=%fused_computation.3 | loop fusion | flops 2359296 | bytes 3145728 | tf_op jit(solution)/shard_map/broadcast_in_dim | solution.py:287
  (112 shorter events, 12.6 us)
Async XLA Ops:
  4.9 13.9 %copy-start.4 = (bf16[256,768]{1,0:T(8,128)(2,1)}, bf16[256,768]{1,0:T(8,128)(2,1)S(1)}, u32[]{:S(2)}) copy-start(bf16[256,768]{1,0:T(8,128)(2,1)S(1)} %fusion.3.refs_1_.refs_6_) | copy-start | bytes 1179652
  4.9 12.1 %collective-permute-start = (bf16[256,768]{1,0:T(8,128)(2,1)S(1)}, bf16[256,768]{1,0:T(8,128)(2,1)S(1)}, u32[]{:S(2)}, u32[]{:S(2)}) collective-permute-start(bf16[256,768]{1,0:T(8,128)(2,1)S(1)} %fusion.3.refs_1_.refs_6_), channel_id=1, source_target_pairs={{0,2},{1,3},{2,0},{3,1},{4,6},{5,7},{6,4},{7,5},{8,10},{9,11},{10,... | collective-permute-start | bytes 1179656 | tf_op jit(solution)/shard_map/ppermute | solution.py:22
  7.9 9.8 %collective-permute-start.1 = (bf16[256,768]{1,0:T(8,128)(2,1)S(1)}, bf16[256,768]{1,0:T(8,128)(2,1)S(1)}, u32[]{:S(2)}, u32[]{:S(2)}) collective-permute-start(bf16[256,768]{1,0:T(8,128)(2,1)S(1)} %fusion.3.refs_1_.refs_6_), channel_id=1, source_target_pairs={{0,1},{1,0},{2,3},{3,2},{4,5},{5,4},{6,7},{7,6},{8,9},{9,8},{10,11... | collective-permute-start | bytes 1179656 | tf_op jit(solution)/shard_map/ppermute | solution.py:40
  17.1 1.7 copy-start.12
  17.1 1.7 collective-permute-start.2
  32.1 8.6 %collective-permute-start.3 = (bf16[256,512]{1,0:T(8,128)(2,1)}, bf16[256,512]{1,0:T(8,128)(2,1)S(1)}, u32[]{:S(2)}, u32[]{:S(2)}) collective-permute-start(bf16[256,512]{1,0:T(8,128)(2,1)} %get-tuple-element.19.refs_1_), channel_id=1, source_target_pairs={{0,2},{1,3},{2,0},{3,1},{4,6},{5,7},{6,4},{7,5},{8,10},{9,11},{10,... | collective-permute-start | bytes 786440 | tf_op jit(solution)/shard_map/ppermute | solution.py:22
  33.8 6.8 %collective-permute-start.4 = (bf16[256,512]{1,0:T(8,128)(2,1)}, bf16[256,512]{1,0:T(8,128)(2,1)S(1)}, u32[]{:S(2)}, u32[]{:S(2)}) collective-permute-start(bf16[256,512]{1,0:T(8,128)(2,1)} %get-tuple-element.19.refs_1_), channel_id=1, source_target_pairs={{0,1},{1,0},{2,3},{3,2},{4,5},{5,4},{6,7},{7,6},{8,9},{9,8},{10,11... | collective-permute-start | bytes 786440 | tf_op jit(solution)/shard_map/ppermute | solution.py:40
  40.6 1.5 copy-start.20
  40.6 1.5 collective-permute-start.5
  42.9 10.5 %copy-start.32 = (s32[4]{0:T(128)S(1)}, s32[4]{0:T(128)}, u32[]{:S(2)}) copy-start(s32[4]{0:T(128)} %param.11) | copy-start | bytes 52
  42.9 17.3 %copy-start = (bf16[768,768]{1,0:T(8,128)(2,1)S(1)}, bf16[768,768]{1,0:T(8,128)(2,1)}, u32[]{:S(2)}) copy-start(bf16[768,768]{1,0:T(8,128)(2,1)} %param.9) | copy-start | bytes 3538948
  47.1 13.1 %collective-permute-start.6 = (bf16[256,768]{1,0:T(8,128)(2,1)}, bf16[256,768]{1,0:T(8,128)(2,1)S(1)}, u32[]{:S(2)}, u32[]{:S(2)}) collective-permute-start(bf16[256,768]{1,0:T(8,128)(2,1)} %shard_map.92), channel_id=1, source_target_pairs={{0,4},{1,5},{2,6},{3,7},{4,8},{5,9},{6,10},{7,11},{8,12},{9,13},{1... | collective-permute-start | bytes 1179656 | tf_op jit(solution)/shard_map/ppermute | solution.py:47
  54.6 13.6 %collective-permute-start.8 = (bf16[256,768]{1,0:T(8,128)(2,1)}, bf16[256,768]{1,0:T(8,128)(2,1)S(1)}, u32[]{:S(2)}, u32[]{:S(2)}) collective-permute-start(bf16[256,768]{1,0:T(8,128)(2,1)} %shard_map.92), channel_id=1, source_target_pairs={{0,6},{1,7},{2,4},{3,5},{4,10},{5,11},{6,8},{7,9},{8,14},{9,15},{1... | collective-permute-start | bytes 1179656 | tf_op jit(solution)/shard_map/ppermute | solution.py:47
  60.4 13.7 %copy-start.2 = (bf16[256,768]{1,0:T(8,128)(2,1)}, bf16[256,768]{1,0:T(8,128)(2,1)S(1)}, u32[]{:S(2)}) copy-start(bf16[256,768]{1,0:T(8,128)(2,1)S(1)} %get-tuple-element.35.refs_1_.refs_6_) | copy-start | bytes 1179652
  60.4 11.8 %collective-permute-start.7 = (bf16[256,768]{1,0:T(8,128)(2,1)S(1)}, bf16[256,768]{1,0:T(8,128)(2,1)S(1)}, u32[]{:S(2)}, u32[]{:S(2)}) collective-permute-start(bf16[256,768]{1,0:T(8,128)(2,1)S(1)} %get-tuple-element.36), channel_id=1, source_target_pairs={{0,2},{1,3},{2,0},{3,1},{16,18},{17,19},{18,16},{19,17}} | collective-permute-start | bytes 1179656 | tf_op jit(solution)/shard_map/ppermute | solution.py:30
  64.2 8.1 %collective-permute-start.9 = (bf16[256,768]{1,0:T(8,128)(2,1)S(1)}, bf16[256,768]{1,0:T(8,128)(2,1)S(1)}, u32[]{:S(2)}, u32[]{:S(2)}) collective-permute-start(bf16[256,768]{1,0:T(8,128)(2,1)S(1)} %get-tuple-element.35.refs_1_.refs_6_), channel_id=1, source_target_pairs={{0,1},{1,0},{2,3},{3,2},{4,5},{5,4},{6,7},{7,6},{8,9},{9,8},{10,11... | collective-permute-start | bytes 1179656 | tf_op jit(solution)/shard_map/ppermute | solution.py:40
  72.3 1.8 copy-start.6
  72.3 1.8 collective-permute-start.10
  72.4 1.7 copy-start.13
  87.4 8.6 %collective-permute-start.11 = (bf16[256,512]{1,0:T(8,128)(2,1)}, bf16[256,512]{1,0:T(8,128)(2,1)S(1)}, u32[]{:S(2)}, u32[]{:S(2)}) collective-permute-start(bf16[256,512]{1,0:T(8,128)(2,1)} %get-tuple-element.22.refs_1_), channel_id=1, source_target_pairs={{0,2},{1,3},{2,0},{3,1},{4,6},{5,7},{6,4},{7,5},{8,10},{9,11},{10,... | collective-permute-start | bytes 786440 | tf_op jit(solution)/shard_map/ppermute | solution.py:22
  88.9 7.1 %collective-permute-start.12 = (bf16[256,512]{1,0:T(8,128)(2,1)}, bf16[256,512]{1,0:T(8,128)(2,1)S(1)}, u32[]{:S(2)}, u32[]{:S(2)}) collective-permute-start(bf16[256,512]{1,0:T(8,128)(2,1)} %get-tuple-element.22.refs_1_), channel_id=1, source_target_pairs={{0,1},{1,0},{2,3},{3,2},{4,5},{5,4},{6,7},{7,6},{8,9},{9,8},{10,11... | collective-permute-start | bytes 786440 | tf_op jit(solution)/shard_map/ppermute | solution.py:40
  95.9 1.5 copy-start.21
  95.9 1.5 collective-permute-start.13
  102.3 11.0 %collective-permute-start.14 = (bf16[256,768]{1,0:T(8,128)(2,1)}, bf16[256,768]{1,0:T(8,128)(2,1)S(1)}, u32[]{:S(2)}, u32[]{:S(2)}) collective-permute-start(bf16[256,768]{1,0:T(8,128)(2,1)} %shard_map.94), channel_id=1, source_target_pairs={{0,4},{1,5},{2,6},{3,7},{4,8},{5,9},{6,10},{7,11},{8,12},{9,13},{1... | collective-permute-start | bytes 1179656 | tf_op jit(solution)/shard_map/ppermute | solution.py:47
  106.3 14.9 %collective-permute-start.16 = (bf16[256,768]{1,0:T(8,128)(2,1)}, bf16[256,768]{1,0:T(8,128)(2,1)S(1)}, u32[]{:S(2)}, u32[]{:S(2)}) collective-permute-start(bf16[256,768]{1,0:T(8,128)(2,1)} %shard_map.94), channel_id=1, source_target_pairs={{0,6},{1,7},{2,4},{3,5},{4,10},{5,11},{6,8},{7,9},{8,14},{9,15},{1... | collective-permute-start | bytes 1179656 | tf_op jit(solution)/shard_map/ppermute | solution.py:47
  113.6 13.9 %copy-start.3 = (bf16[256,768]{1,0:T(8,128)(2,1)}, bf16[256,768]{1,0:T(8,128)(2,1)S(1)}, u32[]{:S(2)}) copy-start(bf16[256,768]{1,0:T(8,128)(2,1)S(1)} %get-tuple-element.33.refs_1_.refs_6_) | copy-start | bytes 1179652
  113.6 12.0 %collective-permute-start.15 = (bf16[256,768]{1,0:T(8,128)(2,1)S(1)}, bf16[256,768]{1,0:T(8,128)(2,1)S(1)}, u32[]{:S(2)}, u32[]{:S(2)}) collective-permute-start(bf16[256,768]{1,0:T(8,128)(2,1)S(1)} %get-tuple-element.34), channel_id=1, source_target_pairs={{0,2},{1,3},{2,0},{3,1},{16,18},{17,19},{18,16},{19,17}} | collective-permute-start | bytes 1179656 | tf_op jit(solution)/shard_map/ppermute | solution.py:30
  117.1 8.6 %collective-permute-start.17 = (bf16[256,768]{1,0:T(8,128)(2,1)S(1)}, bf16[256,768]{1,0:T(8,128)(2,1)S(1)}, u32[]{:S(2)}, u32[]{:S(2)}) collective-permute-start(bf16[256,768]{1,0:T(8,128)(2,1)S(1)} %get-tuple-element.33.refs_1_.refs_6_), channel_id=1, source_target_pairs={{0,1},{1,0},{2,3},{3,2},{4,5},{5,4},{6,7},{7,6},{8,9},{9,8},{10,11... | collective-permute-start | bytes 1179656 | tf_op jit(solution)/shard_map/ppermute | solution.py:40
  125.7 1.8 copy-start.7
  125.7 1.8 collective-permute-start.18
  125.8 1.7 copy-start.14
  140.7 8.6 %collective-permute-start.19 = (bf16[256,512]{1,0:T(8,128)(2,1)}, bf16[256,512]{1,0:T(8,128)(2,1)S(1)}, u32[]{:S(2)}, u32[]{:S(2)}) collective-permute-start(bf16[256,512]{1,0:T(8,128)(2,1)} %get-tuple-element.25.refs_1_), channel_id=1, source_target_pairs={{0,2},{1,3},{2,0},{3,1},{4,6},{5,7},{6,4},{7,5},{8,10},{9,11},{10,... | collective-permute-start | bytes 786440 | tf_op jit(solution)/shard_map/ppermute | solution.py:22
  142.2 7.1 %collective-permute-start.20 = (bf16[256,512]{1,0:T(8,128)(2,1)}, bf16[256,512]{1,0:T(8,128)(2,1)S(1)}, u32[]{:S(2)}, u32[]{:S(2)}) collective-permute-start(bf16[256,512]{1,0:T(8,128)(2,1)} %get-tuple-element.25.refs_1_), channel_id=1, source_target_pairs={{0,1},{1,0},{2,3},{3,2},{4,5},{5,4},{6,7},{7,6},{8,9},{9,8},{10,11... | collective-permute-start | bytes 786440 | tf_op jit(solution)/shard_map/ppermute | solution.py:40
  149.3 1.5 collective-permute-start.21
  155.7 11.0 %collective-permute-start.22 = (bf16[256,768]{1,0:T(8,128)(2,1)}, bf16[256,768]{1,0:T(8,128)(2,1)S(1)}, u32[]{:S(2)}, u32[]{:S(2)}) collective-permute-start(bf16[256,768]{1,0:T(8,128)(2,1)} %shard_map.96), channel_id=1, source_target_pairs={{0,4},{1,5},{2,6},{3,7},{4,8},{5,9},{6,10},{7,11},{8,12},{9,13},{1... | collective-permute-start | bytes 1179656 | tf_op jit(solution)/shard_map/ppermute | solution.py:47
  159.5 15.1 %collective-permute-start.24 = (bf16[256,768]{1,0:T(8,128)(2,1)}, bf16[256,768]{1,0:T(8,128)(2,1)S(1)}, u32[]{:S(2)}, u32[]{:S(2)}) collective-permute-start(bf16[256,768]{1,0:T(8,128)(2,1)} %shard_map.96), channel_id=1, source_target_pairs={{0,6},{1,7},{2,4},{3,5},{4,10},{5,11},{6,8},{7,9},{8,14},{9,15},{1... | collective-permute-start | bytes 1179656 | tf_op jit(solution)/shard_map/ppermute | solution.py:47
  166.9 13.9 %copy-start.1 = (bf16[256,768]{1,0:T(8,128)(2,1)}, bf16[256,768]{1,0:T(8,128)(2,1)S(1)}, u32[]{:S(2)}) copy-start(bf16[256,768]{1,0:T(8,128)(2,1)S(1)} %get-tuple-element.31.refs_1_.refs_6_) | copy-start | bytes 1179652
  166.9 12.0 %collective-permute-start.23 = (bf16[256,768]{1,0:T(8,128)(2,1)S(1)}, bf16[256,768]{1,0:T(8,128)(2,1)S(1)}, u32[]{:S(2)}, u32[]{:S(2)}) collective-permute-start(bf16[256,768]{1,0:T(8,128)(2,1)S(1)} %get-tuple-element.32), channel_id=1, source_target_pairs={{0,2},{1,3},{2,0},{3,1},{16,18},{17,19},{18,16},{19,17}} | collective-permute-start | bytes 1179656 | tf_op jit(solution)/shard_map/ppermute | solution.py:30
  170.3 8.8 %collective-permute-start.25 = (bf16[256,768]{1,0:T(8,128)(2,1)S(1)}, bf16[256,768]{1,0:T(8,128)(2,1)S(1)}, u32[]{:S(2)}, u32[]{:S(2)}) collective-permute-start(bf16[256,768]{1,0:T(8,128)(2,1)S(1)} %get-tuple-element.31.refs_1_.refs_6_), channel_id=1, source_target_pairs={{0,1},{1,0},{2,3},{3,2},{4,5},{5,4},{6,7},{7,6},{8,9},{9,8},{10,11... | collective-permute-start | bytes 1179656 | tf_op jit(solution)/shard_map/ppermute | solution.py:40
  179.0 1.8 copy-start.5
  179.0 1.8 collective-permute-start.26
  179.1 1.7 copy-start.11
  194.1 15.0 %copy-start.8 = (bf16[256,768]{1,0:T(8,128)(2,1)S(1)}, bf16[256,768]{1,0:T(8,128)(2,1)}, u32[]{:S(2)}) copy-start(bf16[256,768]{1,0:T(8,128)(2,1)} %shard_map.92) | copy-start | bytes 1179652
  194.1 15.0 %copy-start.9 = (bf16[256,768]{1,0:T(8,128)(2,1)S(1)}, bf16[256,768]{1,0:T(8,128)(2,1)}, u32[]{:S(2)}) copy-start(bf16[256,768]{1,0:T(8,128)(2,1)} %shard_map.94) | copy-start | bytes 1179652
  194.1 15.0 %copy-start.10 = (bf16[256,768]{1,0:T(8,128)(2,1)S(1)}, bf16[256,768]{1,0:T(8,128)(2,1)}, u32[]{:S(2)}) copy-start(bf16[256,768]{1,0:T(8,128)(2,1)} %shard_map.96) | copy-start | bytes 1179652
  194.1 8.6 %collective-permute-start.27 = (bf16[256,512]{1,0:T(8,128)(2,1)}, bf16[256,512]{1,0:T(8,128)(2,1)S(1)}, u32[]{:S(2)}, u32[]{:S(2)}) collective-permute-start(bf16[256,512]{1,0:T(8,128)(2,1)} %get-tuple-element.28.refs_1_), channel_id=1, source_target_pairs={{0,2},{1,3},{2,0},{3,1},{4,6},{5,7},{6,4},{7,5},{8,10},{9,11},{10,... | collective-permute-start | bytes 786440 | tf_op jit(solution)/shard_map/ppermute | solution.py:22
  195.7 7.1 %collective-permute-start.28 = (bf16[256,512]{1,0:T(8,128)(2,1)}, bf16[256,512]{1,0:T(8,128)(2,1)S(1)}, u32[]{:S(2)}, u32[]{:S(2)}) collective-permute-start(bf16[256,512]{1,0:T(8,128)(2,1)} %get-tuple-element.28.refs_1_), channel_id=1, source_target_pairs={{0,1},{1,0},{2,3},{3,2},{4,5},{5,4},{6,7},{7,6},{8,9},{9,8},{10,11... | collective-permute-start | bytes 786440 | tf_op jit(solution)/shard_map/ppermute | solution.py:40
  202.7 1.5 collective-permute-start.29
  (15 other events, 16.1 us)

commit v10 on v9

--- a/solution.py
+++ b/solution.py
@@ -24,37 +24,26 @@
     ]
 
 
-def across_chips_first_section(block):
-    count = lax.axis_size("seq")
-    return [
-        lax.ppermute(
-            block, ("section", "seq"), [(source, (source + step) % count) for source in range(count)]
-        )
-        for step in range(2, count, 2)
-    ]
-
-
 def with_partner(parts):
     count = lax.axis_size("seq")
     to_partner = [(source, source ^ 1) for source in range(count)]
     return parts + [lax.ppermute(part, "seq", to_partner) for part in parts]
 
 
-def to_next_section(block):
+def to_next_section(block, entry_block):
     sections = lax.axis_size("section")
     count = lax.axis_size("seq")
-    return [
-        lax.ppermute(
-            block,
-            ("section", "seq"),
-            [
-                (section * count + source, (section + 1) * count + (source + step) % count)
-                for section in range(sections - 1)
-                for source in range(count)
-            ],
-        )
-        for step in range(0, count, 2)
-    ]
+    last = lax.axis_index("section") == sections - 1
+    payload = jnp.where(last, entry_block, block)
+    arrived = []
+    for step in range(0, count, 2):
+        pairs = [
+            (section * count + source, (section + 1) % sections * count + (source + step) % count)
+            for section in range(sections - (1 if step == 0 else 0))
+            for source in range(count)
+        ]
+        arrived.append(lax.ppermute(block if step == 0 else payload, ("section", "seq"), pairs))
+    return arrived
 
 
 def kernel_tables(patch_sizes_list, section_index):
@@ -279,11 +268,8 @@
             entry_patch = jnp.where(
                 (row_numbers < patch_sizes_list[turn_number + 1])[:, None], entry_patch, 0
             )
-            arrived = to_next_section(updated)
-            entry_parts = [entry_patch] + across_chips_first_section(entry_patch)
-            row_parts = [
-                jnp.where(section_zero, entry, passed) for entry, passed in zip(entry_parts, arrived)
-            ]
+            arrived = to_next_section(updated, entry_patch)
+            row_parts = [jnp.where(section_zero, entry_patch, arrived[0])] + arrived[1:]
     return jnp.stack(results)[:, None]
 
 

time: 212 us -> 219 us (1.033)
  waiting for transfers between devices: 83.7 us -> 96.4 us
  starting transfers between devices: 37.2 us -> 28.3 us
  other arithmetic: 9.95 us -> 13.6 us
    ppermute x9 -> x6, waiting for transfers between devices: 34.3 us -> 47 us  [to_next_section(): lax.ppermute(block if step == 0 else payload, ('section', 'seq'), pairs)]
    ppermute x9 -> x6, starting transfers between devices: 27.4 us -> 19 us  [to_next_section(): lax.ppermute(block if step == 0 else payload, ('section', 'seq'), pairs)]
    select_n x6 -> x3, other arithmetic: 0.84 us -> 4.37 us  [to_next_section(): payload = jnp.where(last, entry_block, block)]
  transfers between devices with their start and end apart: 30 -> 27, of which waited for: 22 -> 19; matrix products, arithmetic and copies ran while one was open for 2% -> 2% of each run, Pallas kernels for 0% -> 0%
where the time goes in v10:
time: 219 us
  waiting for transfers between devices  96.4 us (44%)
  Pallas kernels  66.6 us (30%)
  starting transfers between devices  28.3 us (13%)
  other arithmetic  13.6 us (6%)
  local copies, waits for them, and re-layouts  7.9 us (4%)
  between operations  5.99 us (3%)
    pallas_call x4, Pallas kernels, attend_block(): pl.pallas_call(block_kernel, grid_spec=grid_spec, out_shape=[jax.ShapeDty...  50.1 us
    ppermute x6, waiting for transfers between devices, to_next_section(): lax.ppermute(block if step == 0 else payload, ('section', 'seq'), pairs)  47 us
    ppermute x5, waiting for transfers between devices, across_chips(): lax.ppermute(block, 'seq', [(source, (source + step) % count) for source...  37.2 us
    ppermute x6, starting transfers between devices, to_next_section(): lax.ppermute(block if step == 0 else payload, ('section', 'seq'), pairs)  19 us
    pallas_call x4, Pallas kernels, leave_block(): pl.pallas_call(exit_kernel, in_specs=[smem] + [vmem] * (count + 3), out_s...  16.5 us
    ppermute x16, waiting for transfers between devices, with_partner(): return parts + [lax.ppermute(part, 'seq', to_partner) for part in parts]  12.3 us
    ppermute x5, starting transfers between devices, across_chips(): lax.ppermute(block, 'seq', [(source, (source + step) % count) for source...  9.26 us
    unnamed x66, local copies, waits for them, and re-layouts  5.93 us
  transfers between devices with their start and end apart: 27, of which 19 were waited for; matrix products, arithmetic and copies ran while one was open for 2% of the time, Pallas kernels for 0%

profile of v10, /device:TPU:0, one launch (start us, length us, event | category | flops | bytes accessed | tf_op | source)
XLA Modules:
  0.0 218.7 jit_solution(17120218844522983518)
XLA Ops:
  0.1 0.8 reduce-window.9
  0.9 1.3 bitcast_subtract_fusion
  2.9 0.7 select_reduce_fusion
  3.7 1.2 fusion.3.refs_1_.refs_6_
  4.9 3.0 %collective-permute-start = (bf16[256,768]{1,0:T(8,128)(2,1)S(1)}, bf16[256,768]{1,0:T(8,128)(2,1)S(1)}, u32[]{:S(2)}, u32[]{:S(2)}) collective-permute-start(bf16[256,768]{1,0:T(8,128)(2,1)S(1)} %fusion.3.refs_1_.refs_6_), channel_id=1, source_target_pairs={{0,2},{1,3},{2,0},{3,1},{4,6},{5,7},{6,4},{7,5},{8,10},{9,11},{10,... | collective-permute-start | bytes 1179656 | tf_op jit(solution)/shard_map/ppermute | solution.py:22
  7.9 9.1 %collective-permute-done.refs_2_ = bf16[256,768]{1,0:T(8,128)(2,1)S(1)} collective-permute-done((bf16[256,768]{1,0:T(8,128)(2,1)S(1)}, bf16[256,768]{1,0:T(8,128)(2,1)S(1)}, u32[]{:S(2)}, u32[]{:S(2)}) %collective-permute-start) | collective-permute-done | bytes 393248 | tf_op jit(solution)/shard_map/ppermute | solution.py:22
  17.7 1.1 collective-permute-done.2.refs_4_
  18.8 0.7 copy-done.16
  19.5 12.5 %shard_map.91 = (bf16[256,512]{1,0:T(8,128)(2,1)}, bf16[4,768,128]{2,1,0:T(8,128)(2,1)}, bf16[4,768,128]{2,1,0:T(8,128)(2,1)}) custom-call(s32[6]{0:T(128)} %get-tuple-element.37.refs_0_, bf16[256,768]{1,0:T(8,128)(2,1)} %copy-done.4, bf16[256,768]{1,0:T(8,128)(2,1)} %copy-done.8, bf16[256,768]{1,0:T(8,128)(2,1)} %copy-done.12, bf16[256,768]{1,0:T(8,128)(2,1)} %copy-done.16, ...), custom_call_target="tpu_custom_call" | custom-call | tf_op jit(solution)/shard_map/pallas_call | solution.py:154
  32.1 1.7 collective-permute-start.3
  33.8 6.8 %collective-permute-done.3.refs_2_ = bf16[256,512]{1,0:T(8,128)(2,1)S(1)} collective-permute-done((bf16[256,512]{1,0:T(8,128)(2,1)}, bf16[256,512]{1,0:T(8,128)(2,1)S(1)}, u32[]{:S(2)}, u32[]{:S(2)}) %collective-permute-start.3) | collective-permute-done | bytes 262176 | tf_op jit(solution)/shard_map/ppermute | solution.py:22
  40.7 1.5 collective-permute-done.5.refs_4_
  42.9 4.2 %shard_map.92 = bf16[256,768]{1,0:T(8,128)(2,1)} custom-call(s32[6]{0:T(128)} %get-tuple-element.37.refs_0_, bf16[256,512]{1,0:T(8,128)(2,1)} %get-tuple-element.19.refs_1_, bf16[256,512]{1,0:T(8,128)(2,1)} %copy-done.20, bf16[256,512]{1,0:T(8,128)(2,1)} %copy-done.24, bf16[256,512]{1,0:T(8,128)(2,1)} %copy-done.28, bf16[4,512,768]{2,1,0:T(8,128)(2,1)} %bitcast.40, ...), custom_call_target="tpu_custom_call" | custom-call | tf_op jit(solution)/shard_map/pallas_call | solution.py:192
  47.1 3.7 %collective-permute-start.6 = (bf16[256,768]{1,0:T(8,128)(2,1)}, bf16[256,768]{1,0:T(8,128)(2,1)S(1)}, u32[]{:S(2)}, u32[]{:S(2)}) collective-permute-start(bf16[256,768]{1,0:T(8,128)(2,1)} %shard_map.92), channel_id=1, source_target_pairs={{0,4},{1,5},{2,6},{3,7},{4,8},{5,9},{6,10},{7,11},{8,12},{9,13},{1... | collective-permute-start | bytes 1179656 | tf_op jit(solution)/shard_map/ppermute | solution.py:45
  54.9 4.9 %collective-permute-done.6 = bf16[256,768]{1,0:T(8,128)(2,1)S(1)} collective-permute-done((bf16[256,768]{1,0:T(8,128)(2,1)}, bf16[256,768]{1,0:T(8,128)(2,1)S(1)}, u32[]{:S(2)}, u32[]{:S(2)}) %collective-permute-start.6) | collective-permute-done | bytes 393248 | tf_op jit(solution)/shard_map/ppermute | solution.py:45
  59.8 1.5 broadcast_select_fusion.2
  61.3 3.4 %collective-permute-start.7 = (bf16[256,768]{1,0:T(8,128)(2,1)S(1)}, bf16[256,768]{1,0:T(8,128)(2,1)S(1)}, u32[]{:S(2)}, u32[]{:S(2)}) collective-permute-start(bf16[256,768]{1,0:T(8,128)(2,1)S(1)} %get-tuple-element.35), channel_id=1, source_target_pairs={{0,6},{1,7},{2,4},{3,5},{4,10},{5,11},{6,8},{7,9},{8,14},{9,15},{1... | collective-permute-start | bytes 1179656 | tf_op jit(solution)/shard_map/ppermute | solution.py:45
  64.6 9.7 %collective-permute-done.7.refs_2_ = bf16[256,768]{1,0:T(8,128)(2,1)S(1)} collective-permute-done((bf16[256,768]{1,0:T(8,128)(2,1)S(1)}, bf16[256,768]{1,0:T(8,128)(2,1)S(1)}, u32[]{:S(2)}, u32[]{:S(2)}) %collective-permute-start.7) | collective-permute-done | bytes 393248 | tf_op jit(solution)/shard_map/ppermute | solution.py:45
  74.4 1.7 collective-permute-done.9.refs_4_
  76.8 12.5 %shard_map.93 = (bf16[256,512]{1,0:T(8,128)(2,1)}, bf16[4,768,128]{2,1,0:T(8,128)(2,1)}, bf16[4,768,128]{2,1,0:T(8,128)(2,1)}) custom-call(s32[6]{0:T(128)} %get-tuple-element.40.refs_0_, bf16[256,768]{1,0:T(8,128)(2,1)} %copy-done.2, bf16[256,768]{1,0:T(8,128)(2,1)} %copy-done.10, ...), custom_call_target="tpu_custom_call", output_to_operand_aliasing={{1}: (7, {}), {2}: (8, {})} | custom-call | tf_op jit(solution)/shard_map/pallas_call | solution.py:154
  89.3 1.5 collective-permute-start.10
  90.8 7.1 %collective-permute-done.10.refs_2_ = bf16[256,512]{1,0:T(8,128)(2,1)S(1)} collective-permute-done((bf16[256,512]{1,0:T(8,128)(2,1)}, bf16[256,512]{1,0:T(8,128)(2,1)S(1)}, u32[]{:S(2)}, u32[]{:S(2)}) %collective-permute-start.10) | collective-permute-done | bytes 262176 | tf_op jit(solution)/shard_map/ppermute | solution.py:22
  97.9 1.5 collective-permute-done.12.refs_4_
  100.1 4.1 %shard_map.94 = bf16[256,768]{1,0:T(8,128)(2,1)} custom-call(s32[6]{0:T(128)} %get-tuple-element.40.refs_0_, bf16[256,512]{1,0:T(8,128)(2,1)} %get-tuple-element.22.refs_1_, bf16[256,512]{1,0:T(8,128)(2,1)} %copy-done.21, bf16[256,512]{1,0:T(8,128)(2,1)} %copy-done.25, bf16[256,512]{1,0:T(8,128)(2,1)} %copy-done.29, bf16[4,512,768]{2,1,0:T(8,128)(2,1)} %bitcast.41, ...), custom_call_target="tpu_custom_call" | custom-call | tf_op jit(solution)/shard_map/pallas_call | solution.py:192
  104.3 2.5 %collective-permute-start.13 = (bf16[256,768]{1,0:T(8,128)(2,1)}, bf16[256,768]{1,0:T(8,128)(2,1)S(1)}, u32[]{:S(2)}, u32[]{:S(2)}) collective-permute-start(bf16[256,768]{1,0:T(8,128)(2,1)} %shard_map.94), channel_id=1, source_target_pairs={{0,4},{1,5},{2,6},{3,7},{4,8},{5,9},{6,10},{7,11},{8,12},{9,13},{1... | collective-permute-start | bytes 1179656 | tf_op jit(solution)/shard_map/ppermute | solution.py:45
  109.3 6.4 %collective-permute-done.13 = bf16[256,768]{1,0:T(8,128)(2,1)S(1)} collective-permute-done((bf16[256,768]{1,0:T(8,128)(2,1)}, bf16[256,768]{1,0:T(8,128)(2,1)S(1)}, u32[]{:S(2)}, u32[]{:S(2)}) %collective-permute-start.13) | collective-permute-done | bytes 393248 | tf_op jit(solution)/shard_map/ppermute | solution.py:45
  115.7 1.5 broadcast_select_fusion.1
  117.2 3.5 %collective-permute-start.14 = (bf16[256,768]{1,0:T(8,128)(2,1)S(1)}, bf16[256,768]{1,0:T(8,128)(2,1)S(1)}, u32[]{:S(2)}, u32[]{:S(2)}) collective-permute-start(bf16[256,768]{1,0:T(8,128)(2,1)S(1)} %get-tuple-element.33), channel_id=1, source_target_pairs={{0,6},{1,7},{2,4},{3,5},{4,10},{5,11},{6,8},{7,9},{8,14},{9,15},{1... | collective-permute-start | bytes 1179656 | tf_op jit(solution)/shard_map/ppermute | solution.py:45
  120.7 9.7 %collective-permute-done.14.refs_2_ = bf16[256,768]{1,0:T(8,128)(2,1)S(1)} collective-permute-done((bf16[256,768]{1,0:T(8,128)(2,1)S(1)}, bf16[256,768]{1,0:T(8,128)(2,1)S(1)}, u32[]{:S(2)}, u32[]{:S(2)}) %collective-permute-start.14) | collective-permute-done | bytes 393248 | tf_op jit(solution)/shard_map/ppermute | solution.py:45
  130.4 1.7 collective-permute-done.16.refs_4_
  132.2 0.8 copy-done.19
  132.9 12.5 %shard_map.95 = (bf16[256,512]{1,0:T(8,128)(2,1)}, bf16[4,768,128]{2,1,0:T(8,128)(2,1)}, bf16[4,768,128]{2,1,0:T(8,128)(2,1)}) custom-call(s32[6]{0:T(128)} %get-tuple-element.39.refs_0_, bf16[256,768]{1,0:T(8,128)(2,1)} %copy-done.3, bf16[256,768]{1,0:T(8,128)(2,1)} %copy-done.11, ...), custom_call_target="tpu_custom_call", output_to_operand_aliasing={{1}: (7, {}), {2}: (8, {})} | custom-call | tf_op jit(solution)/shard_map/pallas_call | solution.py:154
  145.4 1.5 collective-permute-start.17
  146.9 7.1 %collective-permute-done.17.refs_2_ = bf16[256,512]{1,0:T(8,128)(2,1)S(1)} collective-permute-done((bf16[256,512]{1,0:T(8,128)(2,1)}, bf16[256,512]{1,0:T(8,128)(2,1)S(1)}, u32[]{:S(2)}, u32[]{:S(2)}) %collective-permute-start.17) | collective-permute-done | bytes 262176 | tf_op jit(solution)/shard_map/ppermute | solution.py:22
  154.0 1.5 collective-permute-done.19.refs_4_
  156.3 4.1 %shard_map.96 = bf16[256,768]{1,0:T(8,128)(2,1)} custom-call(s32[6]{0:T(128)} %get-tuple-element.39.refs_0_, bf16[256,512]{1,0:T(8,128)(2,1)} %get-tuple-element.25.refs_1_, bf16[256,512]{1,0:T(8,128)(2,1)} %copy-done.22, bf16[256,512]{1,0:T(8,128)(2,1)} %copy-done.26, bf16[256,512]{1,0:T(8,128)(2,1)} %copy-done.30, bf16[4,512,768]{2,1,0:T(8,128)(2,1)} %bitcast.42, ...), custom_call_target="tpu_custom_call" | custom-call | tf_op jit(solution)/shard_map/pallas_call | solution.py:192
  160.4 2.5 %collective-permute-start.20 = (bf16[256,768]{1,0:T(8,128)(2,1)}, bf16[256,768]{1,0:T(8,128)(2,1)S(1)}, u32[]{:S(2)}, u32[]{:S(2)}) collective-permute-start(bf16[256,768]{1,0:T(8,128)(2,1)} %shard_map.96), channel_id=1, source_target_pairs={{0,4},{1,5},{2,6},{3,7},{4,8},{5,9},{6,10},{7,11},{8,12},{9,13},{1... | collective-permute-start | bytes 1179656 | tf_op jit(solution)/shard_map/ppermute | solution.py:45
  165.3 6.5 %collective-permute-done.20 = bf16[256,768]{1,0:T(8,128)(2,1)S(1)} collective-permute-done((bf16[256,768]{1,0:T(8,128)(2,1)}, bf16[256,768]{1,0:T(8,128)(2,1)S(1)}, u32[]{:S(2)}, u32[]{:S(2)}) %collective-permute-start.20) | collective-permute-done | bytes 393248 | tf_op jit(solution)/shard_map/ppermute | solution.py:45
  171.8 1.5 broadcast_select_fusion
  173.3 3.4 %collective-permute-start.21 = (bf16[256,768]{1,0:T(8,128)(2,1)S(1)}, bf16[256,768]{1,0:T(8,128)(2,1)S(1)}, u32[]{:S(2)}, u32[]{:S(2)}) collective-permute-start(bf16[256,768]{1,0:T(8,128)(2,1)S(1)} %get-tuple-element.31), channel_id=1, source_target_pairs={{0,6},{1,7},{2,4},{3,5},{4,10},{5,11},{6,8},{7,9},{8,14},{9,15},{1... | collective-permute-start | bytes 1179656 | tf_op jit(solution)/shard_map/ppermute | solution.py:45
  176.7 9.7 %collective-permute-done.21.refs_2_ = bf16[256,768]{1,0:T(8,128)(2,1)S(1)} collective-permute-done((bf16[256,768]{1,0:T(8,128)(2,1)S(1)}, bf16[256,768]{1,0:T(8,128)(2,1)S(1)}, u32[]{:S(2)}, u32[]{:S(2)}) %collective-permute-start.21) | collective-permute-done | bytes 393248 | tf_op jit(solution)/shard_map/ppermute | solution.py:45
  186.4 1.7 collective-permute-done.23.refs_4_
  188.9 12.5 %shard_map.97 = (bf16[256,512]{1,0:T(8,128)(2,1)}, bf16[4,768,128]{2,1,0:T(8,128)(2,1)}, bf16[4,768,128]{2,1,0:T(8,128)(2,1)}) custom-call(s32[6]{0:T(128)} %get-tuple-element.38.refs_0_, bf16[256,768]{1,0:T(8,128)(2,1)} %copy-done.1, bf16[256,768]{1,0:T(8,128)(2,1)} %copy-done.9, ...), custom_call_target="tpu_custom_call", output_to_operand_aliasing={{1}: (7, {}), {2}: (8, {})} | custom-call | tf_op jit(solution)/shard_map/pallas_call | solution.py:154
  201.4 1.6 collective-permute-start.24
  203.0 7.1 %collective-permute-done.24.refs_2_ = bf16[256,512]{1,0:T(8,128)(2,1)S(1)} collective-permute-done((bf16[256,512]{1,0:T(8,128)(2,1)}, bf16[256,512]{1,0:T(8,128)(2,1)S(1)}, u32[]{:S(2)}, u32[]{:S(2)}) %collective-permute-start.24) | collective-permute-done | bytes 262176 | tf_op jit(solution)/shard_map/ppermute | solution.py:22
  210.1 1.5 collective-permute-done.26.refs_4_
  212.3 4.1 %shard_map.98 = bf16[256,768]{1,0:T(8,128)(2,1)} custom-call(s32[6]{0:T(128)} %get-tuple-element.38.refs_0_, bf16[256,512]{1,0:T(8,128)(2,1)} %get-tuple-element.28.refs_1_, bf16[256,512]{1,0:T(8,128)(2,1)} %copy-done.23, bf16[256,512]{1,0:T(8,128)(2,1)} %copy-done.27, bf16[256,512]{1,0:T(8,128)(2,1)} %copy-done.31, bf16[4,512,768]{2,1,0:T(8,128)(2,1)} %bitcast.43, ...), custom_call_target="tpu_custom_call" | custom-call | tf_op jit(solution)/shard_map/pallas_call | solution.py:192
  216.4 2.3 %maximum_bitcast_fusion = bf16[4,1,256,768]{3,2,1,0:T(8,128)(2,1)} fusion(bf16[1,256,768]{2,1,0:T(8,128)(2,1)} %bitcast.47, bf16[1,256,768]{2,1,0:T(8,128)(2,1)S(1)} %bitcast.46, bf16[1,256,768]{2,1,0:T(8,128)(2,1)S(1)} %bitcast.45, bf16[1,256,768]{2,1,0:T(8,128)(2,1)S(1)} %bitcast.44), kind=kLoop, calls=%fused_computation.3 | loop fusion | flops 2359296 | bytes 3145728 | tf_op jit(solution)/shard_map/broadcast_in_dim | solution.py:273
  (103 shorter events, 9.2 us)
Async XLA Ops:
  4.9 13.9 %copy-start.4 = (bf16[256,768]{1,0:T(8,128)(2,1)}, bf16[256,768]{1,0:T(8,128)(2,1)S(1)}, u32[]{:S(2)}) copy-start(bf16[256,768]{1,0:T(8,128)(2,1)S(1)} %fusion.3.refs_1_.refs_6_) | copy-start | bytes 1179652
  4.9 12.1 %collective-permute-start = (bf16[256,768]{1,0:T(8,128)(2,1)S(1)}, bf16[256,768]{1,0:T(8,128)(2,1)S(1)}, u32[]{:S(2)}, u32[]{:S(2)}) collective-permute-start(bf16[256,768]{1,0:T(8,128)(2,1)S(1)} %fusion.3.refs_1_.refs_6_), channel_id=1, source_target_pairs={{0,2},{1,3},{2,0},{3,1},{4,6},{5,7},{6,4},{7,5},{8,10},{9,11},{10,... | collective-permute-start | bytes 1179656 | tf_op jit(solution)/shard_map/ppermute | solution.py:22
  7.9 9.8 %collective-permute-start.1 = (bf16[256,768]{1,0:T(8,128)(2,1)S(1)}, bf16[256,768]{1,0:T(8,128)(2,1)S(1)}, u32[]{:S(2)}, u32[]{:S(2)}) collective-permute-start(bf16[256,768]{1,0:T(8,128)(2,1)S(1)} %fusion.3.refs_1_.refs_6_), channel_id=1, source_target_pairs={{0,1},{1,0},{2,3},{3,2},{4,5},{5,4},{6,7},{7,6},{8,9},{9,8},{10,11... | collective-permute-start | bytes 1179656 | tf_op jit(solution)/shard_map/ppermute | solution.py:30
  17.1 1.7 copy-start.8
  17.1 1.7 collective-permute-start.2
  32.1 8.6 %collective-permute-start.3 = (bf16[256,512]{1,0:T(8,128)(2,1)}, bf16[256,512]{1,0:T(8,128)(2,1)S(1)}, u32[]{:S(2)}, u32[]{:S(2)}) collective-permute-start(bf16[256,512]{1,0:T(8,128)(2,1)} %get-tuple-element.19.refs_1_), channel_id=1, source_target_pairs={{0,2},{1,3},{2,0},{3,1},{4,6},{5,7},{6,4},{7,5},{8,10},{9,11},{10,... | collective-permute-start | bytes 786440 | tf_op jit(solution)/shard_map/ppermute | solution.py:22
  33.8 6.8 %collective-permute-start.4 = (bf16[256,512]{1,0:T(8,128)(2,1)}, bf16[256,512]{1,0:T(8,128)(2,1)S(1)}, u32[]{:S(2)}, u32[]{:S(2)}) collective-permute-start(bf16[256,512]{1,0:T(8,128)(2,1)} %get-tuple-element.19.refs_1_), channel_id=1, source_target_pairs={{0,1},{1,0},{2,3},{3,2},{4,5},{5,4},{6,7},{7,6},{8,9},{9,8},{10,11... | collective-permute-start | bytes 786440 | tf_op jit(solution)/shard_map/ppermute | solution.py:30
  40.6 1.5 copy-start.20
  40.6 1.5 collective-permute-start.5
  40.6 1.5 copy-start.24
  42.9 10.7 %copy-start.32 = (s32[4]{0:T(128)S(1)}, s32[4]{0:T(128)}, u32[]{:S(2)}) copy-start(s32[4]{0:T(128)} %param.11) | copy-start | bytes 52
  42.9 16.9 %copy-start = (bf16[768,768]{1,0:T(8,128)(2,1)S(1)}, bf16[768,768]{1,0:T(8,128)(2,1)}, u32[]{:S(2)}) copy-start(bf16[768,768]{1,0:T(8,128)(2,1)} %param.9) | copy-start | bytes 3538948
  47.1 12.7 %collective-permute-start.6 = (bf16[256,768]{1,0:T(8,128)(2,1)}, bf16[256,768]{1,0:T(8,128)(2,1)S(1)}, u32[]{:S(2)}, u32[]{:S(2)}) collective-permute-start(bf16[256,768]{1,0:T(8,128)(2,1)} %shard_map.92), channel_id=1, source_target_pairs={{0,4},{1,5},{2,6},{3,7},{4,8},{5,9},{6,10},{7,11},{8,12},{9,13},{1... | collective-permute-start | bytes 1179656 | tf_op jit(solution)/shard_map/ppermute | solution.py:45
  61.3 14.8 %copy-start.2 = (bf16[256,768]{1,0:T(8,128)(2,1)}, bf16[256,768]{1,0:T(8,128)(2,1)S(1)}, u32[]{:S(2)}) copy-start(bf16[256,768]{1,0:T(8,128)(2,1)S(1)} %get-tuple-element.36.refs_1_.refs_6_) | copy-start | bytes 1179652
  61.3 13.1 %collective-permute-start.7 = (bf16[256,768]{1,0:T(8,128)(2,1)S(1)}, bf16[256,768]{1,0:T(8,128)(2,1)S(1)}, u32[]{:S(2)}, u32[]{:S(2)}) collective-permute-start(bf16[256,768]{1,0:T(8,128)(2,1)S(1)} %get-tuple-element.35), channel_id=1, source_target_pairs={{0,6},{1,7},{2,4},{3,5},{4,10},{5,11},{6,8},{7,9},{8,14},{9,15},{1... | collective-permute-start | bytes 1179656 | tf_op jit(solution)/shard_map/ppermute | solution.py:45
  64.6 9.7 %collective-permute-start.8 = (bf16[256,768]{1,0:T(8,128)(2,1)S(1)}, bf16[256,768]{1,0:T(8,128)(2,1)S(1)}, u32[]{:S(2)}, u32[]{:S(2)}) collective-permute-start(bf16[256,768]{1,0:T(8,128)(2,1)S(1)} %get-tuple-element.36.refs_1_.refs_6_), channel_id=1, source_target_pairs={{0,1},{1,0},{2,3},{3,2},{4,5},{5,4},{6,7},{7,6},{8,9},{9,8},{10,11... | collective-permute-start | bytes 1179656 | tf_op jit(solution)/shard_map/ppermute | solution.py:30
  74.3 1.7 copy-start.10
  74.3 1.7 collective-permute-start.9
  74.4 1.7 copy-start.14
  89.3 8.6 %collective-permute-start.10 = (bf16[256,512]{1,0:T(8,128)(2,1)}, bf16[256,512]{1,0:T(8,128)(2,1)S(1)}, u32[]{:S(2)}, u32[]{:S(2)}) collective-permute-start(bf16[256,512]{1,0:T(8,128)(2,1)} %get-tuple-element.22.refs_1_), channel_id=1, source_target_pairs={{0,2},{1,3},{2,0},{3,1},{4,6},{5,7},{6,4},{7,5},{8,10},{9,11},{10,... | collective-permute-start | bytes 786440 | tf_op jit(solution)/shard_map/ppermute | solution.py:22
  90.8 7.1 %collective-permute-start.11 = (bf16[256,512]{1,0:T(8,128)(2,1)}, bf16[256,512]{1,0:T(8,128)(2,1)S(1)}, u32[]{:S(2)}, u32[]{:S(2)}) collective-permute-start(bf16[256,512]{1,0:T(8,128)(2,1)} %get-tuple-element.22.refs_1_), channel_id=1, source_target_pairs={{0,1},{1,0},{2,3},{3,2},{4,5},{5,4},{6,7},{7,6},{8,9},{9,8},{10,11... | collective-permute-start | bytes 786440 | tf_op jit(solution)/shard_map/ppermute | solution.py:30
  97.9 1.5 copy-start.21
  97.9 1.5 collective-permute-start.12
  104.3 11.5 %collective-permute-start.13 = (bf16[256,768]{1,0:T(8,128)(2,1)}, bf16[256,768]{1,0:T(8,128)(2,1)S(1)}, u32[]{:S(2)}, u32[]{:S(2)}) collective-permute-start(bf16[256,768]{1,0:T(8,128)(2,1)} %shard_map.94), channel_id=1, source_target_pairs={{0,4},{1,5},{2,6},{3,7},{4,8},{5,9},{6,10},{7,11},{8,12},{9,13},{1... | collective-permute-start | bytes 1179656 | tf_op jit(solution)/shard_map/ppermute | solution.py:45
  117.2 15.0 %copy-start.3 = (bf16[256,768]{1,0:T(8,128)(2,1)}, bf16[256,768]{1,0:T(8,128)(2,1)S(1)}, u32[]{:S(2)}) copy-start(bf16[256,768]{1,0:T(8,128)(2,1)S(1)} %get-tuple-element.34.refs_1_.refs_6_) | copy-start | bytes 1179652
  117.2 13.3 %collective-permute-start.14 = (bf16[256,768]{1,0:T(8,128)(2,1)S(1)}, bf16[256,768]{1,0:T(8,128)(2,1)S(1)}, u32[]{:S(2)}, u32[]{:S(2)}) collective-permute-start(bf16[256,768]{1,0:T(8,128)(2,1)S(1)} %get-tuple-element.33), channel_id=1, source_target_pairs={{0,6},{1,7},{2,4},{3,5},{4,10},{5,11},{6,8},{7,9},{8,14},{9,15},{1... | collective-permute-start | bytes 1179656 | tf_op jit(solution)/shard_map/ppermute | solution.py:45
  120.7 9.7 %collective-permute-start.15 = (bf16[256,768]{1,0:T(8,128)(2,1)S(1)}, bf16[256,768]{1,0:T(8,128)(2,1)S(1)}, u32[]{:S(2)}, u32[]{:S(2)}) collective-permute-start(bf16[256,768]{1,0:T(8,128)(2,1)S(1)} %get-tuple-element.34.refs_1_.refs_6_), channel_id=1, source_target_pairs={{0,1},{1,0},{2,3},{3,2},{4,5},{5,4},{6,7},{7,6},{8,9},{9,8},{10,11... | collective-permute-start | bytes 1179656 | tf_op jit(solution)/shard_map/ppermute | solution.py:30
  130.4 1.7 copy-start.11
  130.4 1.7 collective-permute-start.16
  130.4 1.7 copy-start.15
  145.4 8.6 %collective-permute-start.17 = (bf16[256,512]{1,0:T(8,128)(2,1)}, bf16[256,512]{1,0:T(8,128)(2,1)S(1)}, u32[]{:S(2)}, u32[]{:S(2)}) collective-permute-start(bf16[256,512]{1,0:T(8,128)(2,1)} %get-tuple-element.25.refs_1_), channel_id=1, source_target_pairs={{0,2},{1,3},{2,0},{3,1},{4,6},{5,7},{6,4},{7,5},{8,10},{9,11},{10,... | collective-permute-start | bytes 786440 | tf_op jit(solution)/shard_map/ppermute | solution.py:22
  146.9 7.1 %collective-permute-start.18 = (bf16[256,512]{1,0:T(8,128)(2,1)}, bf16[256,512]{1,0:T(8,128)(2,1)S(1)}, u32[]{:S(2)}, u32[]{:S(2)}) collective-permute-start(bf16[256,512]{1,0:T(8,128)(2,1)} %get-tuple-element.25.refs_1_), channel_id=1, source_target_pairs={{0,1},{1,0},{2,3},{3,2},{4,5},{5,4},{6,7},{7,6},{8,9},{9,8},{10,11... | collective-permute-start | bytes 786440 | tf_op jit(solution)/shard_map/ppermute | solution.py:30
  154.0 1.5 copy-start.22
  154.0 1.5 collective-permute-start.19
  160.4 11.4 %collective-permute-start.20 = (bf16[256,768]{1,0:T(8,128)(2,1)}, bf16[256,768]{1,0:T(8,128)(2,1)S(1)}, u32[]{:S(2)}, u32[]{:S(2)}) collective-permute-start(bf16[256,768]{1,0:T(8,128)(2,1)} %shard_map.96), channel_id=1, source_target_pairs={{0,4},{1,5},{2,6},{3,7},{4,8},{5,9},{6,10},{7,11},{8,12},{9,13},{1... | collective-permute-start | bytes 1179656 | tf_op jit(solution)/shard_map/ppermute | solution.py:45
  173.3 14.8 %copy-start.1 = (bf16[256,768]{1,0:T(8,128)(2,1)}, bf16[256,768]{1,0:T(8,128)(2,1)S(1)}, u32[]{:S(2)}) copy-start(bf16[256,768]{1,0:T(8,128)(2,1)S(1)} %get-tuple-element.32.refs_1_.refs_6_) | copy-start | bytes 1179652
  173.3 13.1 %collective-permute-start.21 = (bf16[256,768]{1,0:T(8,128)(2,1)S(1)}, bf16[256,768]{1,0:T(8,128)(2,1)S(1)}, u32[]{:S(2)}, u32[]{:S(2)}) collective-permute-start(bf16[256,768]{1,0:T(8,128)(2,1)S(1)} %get-tuple-element.31), channel_id=1, source_target_pairs={{0,6},{1,7},{2,4},{3,5},{4,10},{5,11},{6,8},{7,9},{8,14},{9,15},{1... | collective-permute-start | bytes 1179656 | tf_op jit(solution)/shard_map/ppermute | solution.py:45
  176.7 9.7 %collective-permute-start.22 = (bf16[256,768]{1,0:T(8,128)(2,1)S(1)}, bf16[256,768]{1,0:T(8,128)(2,1)S(1)}, u32[]{:S(2)}, u32[]{:S(2)}) collective-permute-start(bf16[256,768]{1,0:T(8,128)(2,1)S(1)} %get-tuple-element.32.refs_1_.refs_6_), channel_id=1, source_target_pairs={{0,1},{1,0},{2,3},{3,2},{4,5},{5,4},{6,7},{7,6},{8,9},{9,8},{10,11... | collective-permute-start | bytes 1179656 | tf_op jit(solution)/shard_map/ppermute | solution.py:30
  186.4 1.7 copy-start.9
  186.4 1.7 collective-permute-start.23
  186.4 1.7 copy-start.13
  201.4 15.0 %copy-start.5 = (bf16[256,768]{1,0:T(8,128)(2,1)S(1)}, bf16[256,768]{1,0:T(8,128)(2,1)}, u32[]{:S(2)}) copy-start(bf16[256,768]{1,0:T(8,128)(2,1)} %shard_map.92) | copy-start | bytes 1179652
  201.4 15.0 %copy-start.6 = (bf16[256,768]{1,0:T(8,128)(2,1)S(1)}, bf16[256,768]{1,0:T(8,128)(2,1)}, u32[]{:S(2)}) copy-start(bf16[256,768]{1,0:T(8,128)(2,1)} %shard_map.94) | copy-start | bytes 1179652
  201.4 15.0 %copy-start.7 = (bf16[256,768]{1,0:T(8,128)(2,1)S(1)}, bf16[256,768]{1,0:T(8,128)(2,1)}, u32[]{:S(2)}) copy-start(bf16[256,768]{1,0:T(8,128)(2,1)} %shard_map.96) | copy-start | bytes 1179652
  201.4 8.6 %collective-permute-start.24 = (bf16[256,512]{1,0:T(8,128)(2,1)}, bf16[256,512]{1,0:T(8,128)(2,1)S(1)}, u32[]{:S(2)}, u32[]{:S(2)}) collective-permute-start(bf16[256,512]{1,0:T(8,128)(2,1)} %get-tuple-element.28.refs_1_), channel_id=1, source_target_pairs={{0,2},{1,3},{2,0},{3,1},{4,6},{5,7},{6,4},{7,5},{8,10},{9,11},{10,... | collective-permute-start | bytes 786440 | tf_op jit(solution)/shard_map/ppermute | solution.py:22
  203.0 7.1 %collective-permute-start.25 = (bf16[256,512]{1,0:T(8,128)(2,1)}, bf16[256,512]{1,0:T(8,128)(2,1)S(1)}, u32[]{:S(2)}, u32[]{:S(2)}) collective-permute-start(bf16[256,512]{1,0:T(8,128)(2,1)} %get-tuple-element.28.refs_1_), channel_id=1, source_target_pairs={{0,1},{1,0},{2,3},{3,2},{4,5},{5,4},{6,7},{7,6},{8,9},{9,8},{10,11... | collective-permute-start | bytes 786440 | tf_op jit(solution)/shard_map/ppermute | solution.py:30
  210.0 1.5 copy-start.23
  210.0 1.5 collective-permute-start.26
  (12 other events, 11.6 us)

commit v11 on v6

--- a/solution.py
+++ b/solution.py
@@ -34,11 +34,19 @@
     return [block] + across + [from_partner] + relayed
 
 
-def kernel_table(patch_start, patch_count):
+def kernel_tables(patch_sizes_list, section_index):
+    patches = patch_sizes_list.shape[0]
     count = lax.axis_size("seq")
     here = lax.axis_index("seq")
     chips = count // 2
-    entry = jnp.arange(count + 2) - 2
+    turn = lax.broadcasted_iota(jnp.int32, (patches, count + 2), 0)
+    entry = lax.broadcasted_iota(jnp.int32, (patches, count + 2), 1) - 2
+    patch_index = jnp.remainder(turn - section_index + patches, patches)
+    patch_ids = jnp.arange(patches).reshape(1, 1, patches)
+    sizes = patch_sizes_list.reshape(1, 1, patches)
+    chosen = patch_ids == patch_index[:, :, None]
+    patch_count = jnp.sum(jnp.where(chosen, sizes, 0), axis=-1)
+    patch_start = jnp.sum(jnp.where(patch_ids < patch_index[:, :, None], sizes, 0), axis=-1)
     base = jnp.where(entry < chips, here, jnp.bitwise_xor(here, 1))
     sources = jnp.remainder(base - 2 * jnp.remainder(entry, chips) + count, count)
     return jnp.where(entry == -2, patch_start, jnp.where(entry == -1, patch_count, sources)).astype(
@@ -212,17 +220,19 @@
         [incoming_states, jnp.zeros((biggest_patch_span, columns), jnp.bfloat16)], axis=0
     )
     earlier_result = transit_states[0]
+    tables = kernel_tables(patch_sizes_list, section_index)
     for turn_number in range(patches):
         patch_index = jnp.remainder(turn_number - section_index, patches)
         patch_count = pick_entry(patch_sizes_list, patch_index)
-        patch_start = pick_entry(starts, patch_index)
-        where = kernel_table(patch_start, patch_count)
         live_rows = row_numbers < patch_count
         entry_patch = lax.dynamic_slice_in_dim(
             entering_ext, starts[turn_number], biggest_patch_span, 0
         )
         own_rows = jnp.where(section_index == 0, entry_patch, earlier_result)
         own_rows = jnp.where(live_rows[:, None], own_rows, jnp.zeros_like(own_rows))
+        if turn_number == 0:
+            tables, own_rows = lax.optimization_barrier((tables, own_rows))
+        where = tables[turn_number]
         head_rows, key_cache, value_cache = attend_block(
             spread_over_seq(own_rows),
             shift_scale,

time: 217 us -> 214 us (0.986)
  other arithmetic: 15.3 us -> 9.82 us
  waiting for transfers between devices: 92.5 us -> 94.7 us
    select_n x2 -> x3, other arithmetic: 6.14 us -> 0.09 us  [the longest x1 0.07 us: kernel_tables(): patch_index = jnp.remainder(turn - section_index + patches, patches)]
    ppermute x8, waiting for transfers between devices: 9.48 us -> 12.3 us  [spread_over_seq(): relayed = [lax.ppermute(part, 'seq', to_partner) for part in across]]
  transfers between devices with their start and end apart: 27 -> 27, of which waited for: 17 -> 19; matrix products, arithmetic and copies ran while one was open for 4% -> 1% of each run, Pallas kernels for 0% -> 0%
where the time goes in v11:
time: 214 us; the launch traced here: 213 us
  waiting for transfers between devices  94.7 us (44%)
  Pallas kernels  66.6 us (31%)
  starting transfers between devices  26.6 us (12%)
  other arithmetic  9.82 us (5%)
  between operations  8.19 us (4%)
  local copies, waits for them, and re-layouts  7.18 us (3%)
    ppermute x8, waiting for transfers between devices, spread_over_seq(): lax.ppermute(block, 'seq', [(source, (source + step) % count) for source...  63.5 us
    pallas_call x4, Pallas kernels, attend_block(): pl.pallas_call(block_kernel, grid_spec=grid_spec, out_shape=[jax.ShapeDty...  50.1 us
    ppermute x3, waiting for transfers between devices, passed_along(): lax.ppermute(value, axis, [(source, source + steps) for source in range(l...  18.9 us
    pallas_call x4, Pallas kernels, leave_block(): pl.pallas_call(exit_kernel, in_specs=[smem] + [vmem] * (count + 3), out_s...  16.5 us
    ppermute x8, starting transfers between devices, spread_over_seq(): lax.ppermute(block, 'seq', [(source, (source + step) % count) for source...  14.1 us
    ppermute x3, starting transfers between devices, passed_along(): lax.ppermute(value, axis, [(source, source + steps) for source in range(l...  12.5 us
    ppermute x8, waiting for transfers between devices, spread_over_seq(): relayed = [lax.ppermute(part, 'seq', to_partner) for part in across]  12.3 us
    unnamed x64, local copies, waits for them, and re-layouts  5.9 us
  transfers between devices with their start and end apart: 27, of which 19 were waited for; matrix products, arithmetic and copies ran while one was open for 1% of the time, Pallas kernels for 0%

profile of v11, /device:TPU:0, one launch (start us, length us, event | category | flops | bytes accessed | tf_op | source)
XLA Modules:
  0.0 213.1 jit_solution(15961917273416539021)
XLA Ops:
  0.1 0.8 reduce-window.9
  0.9 1.3 fusion.14
  4.9 0.7 select_reduce_fusion
  6.3 1.3 fusion.1.refs_1_.refs_6_
  7.7 3.0 %collective-permute-start = (bf16[256,768]{1,0:T(8,128)(2,1)S(1)}, bf16[256,768]{1,0:T(8,128)(2,1)S(1)}, u32[]{:S(2)}, u32[]{:S(2)}) collective-permute-start(bf16[256,768]{1,0:T(8,128)(2,1)S(1)} %fusion.1.refs_1_.refs_6_), channel_id=1, source_target_pairs={{0,2},{1,3},{2,0},{3,1},{4,6},{5,7},{6,4},{7,5},{8,10},{9,11},{10,... | collective-permute-start | bytes 1179656 | tf_op jit(solution)/shard_map/ppermute | solution.py:29
  10.7 9.1 %collective-permute-done.refs_2_ = bf16[256,768]{1,0:T(8,128)(2,1)S(1)} collective-permute-done((bf16[256,768]{1,0:T(8,128)(2,1)S(1)}, bf16[256,768]{1,0:T(8,128)(2,1)S(1)}, u32[]{:S(2)}, u32[]{:S(2)}) %collective-permute-start) | collective-permute-done | bytes 393248 | tf_op jit(solution)/shard_map/ppermute | solution.py:29
  20.5 1.1 collective-permute-done.2.refs_4_
  21.6 0.8 copy-done.16
  22.3 12.5 %shard_map.91 = (bf16[256,512]{1,0:T(8,128)(2,1)}, bf16[4,768,128]{2,1,0:T(8,128)(2,1)}, bf16[4,768,128]{2,1,0:T(8,128)(2,1)}) custom-call(s32[6]{0:T(128)} %get-tuple-element.35.refs_0_, bf16[256,768]{1,0:T(8,128)(2,1)} %copy-done.1, bf16[256,768]{1,0:T(8,128)(2,1)} %copy-done.8, bf16[256,768]{1,0:T(8,128)(2,1)} %copy-done.10, bf16[256,768]{1,0:T(8,128)(2,1)} %copy-done.16, ...), custom_call_target="tpu_custom_call" | custom-call | tf_op jit(solution)/shard_map/pallas_call | solution.py:142
  34.9 1.7 collective-permute-start.3
  36.6 6.8 %collective-permute-done.3.refs_2_ = bf16[256,512]{1,0:T(8,128)(2,1)S(1)} collective-permute-done((bf16[256,512]{1,0:T(8,128)(2,1)}, bf16[256,512]{1,0:T(8,128)(2,1)S(1)}, u32[]{:S(2)}, u32[]{:S(2)}) %collective-permute-start.3) | collective-permute-done | bytes 262176 | tf_op jit(solution)/shard_map/ppermute | solution.py:29
  43.4 1.5 collective-permute-done.5.refs_4_
  45.0 0.7 copy-done.28
  45.7 4.2 %shard_map.92 = bf16[256,768]{1,0:T(8,128)(2,1)} custom-call(s32[6]{0:T(128)} %get-tuple-element.35.refs_0_, bf16[256,512]{1,0:T(8,128)(2,1)} %get-tuple-element.19.refs_1_, bf16[256,512]{1,0:T(8,128)(2,1)} %copy-done.20, bf16[256,512]{1,0:T(8,128)(2,1)} %copy-done.24, bf16[256,512]{1,0:T(8,128)(2,1)} %copy-done.28, bf16[4,512,768]{2,1,0:T(8,128)(2,1)} %bitcast.36, ...), custom_call_target="tpu_custom_call" | custom-call | tf_op jit(solution)/shard_map/pallas_call | solution.py:180
  49.9 3.7 %collective-permute-start.6 = (bf16[256,768]{1,0:T(8,128)(2,1)}, bf16[256,768]{1,0:T(8,128)(2,1)S(1)}, u32[]{:S(2)}, u32[]{:S(2)}) collective-permute-start(bf16[256,768]{1,0:T(8,128)(2,1)} %shard_map.92), channel_id=1, source_target_pairs={{0,4},{4,8},{8,12},{1,5},{5,9},{9,13},{2,6},{6,10},{10,14},{3,7},{... | collective-permute-start | bytes 1179656 | tf_op jit(solution)/shard_map/ppermute | solution.py:14
  56.1 6.5 %collective-permute-done.6 = bf16[256,768]{1,0:T(8,128)(2,1)S(1)} collective-permute-done((bf16[256,768]{1,0:T(8,128)(2,1)}, bf16[256,768]{1,0:T(8,128)(2,1)S(1)}, u32[]{:S(2)}, u32[]{:S(2)}) %collective-permute-start.6) | collective-permute-done | bytes 393248 | tf_op jit(solution)/shard_map/ppermute | solution.py:14
  62.8 1.6 collective-permute-start.7
  64.4 8.8 %collective-permute-done.7.refs_2_ = bf16[256,768]{1,0:T(8,128)(2,1)S(1)} collective-permute-done((bf16[256,768]{1,0:T(8,128)(2,1)S(1)}, bf16[256,768]{1,0:T(8,128)(2,1)S(1)}, u32[]{:S(2)}, u32[]{:S(2)}) %collective-permute-start.7) | collective-permute-done | bytes 393248 | tf_op jit(solution)/shard_map/ppermute | solution.py:29
  73.2 1.7 collective-permute-done.9.refs_4_
  74.9 0.7 copy-done.18
  75.7 12.5 %shard_map.93 = (bf16[256,512]{1,0:T(8,128)(2,1)}, bf16[4,768,128]{2,1,0:T(8,128)(2,1)}, bf16[4,768,128]{2,1,0:T(8,128)(2,1)}) custom-call(s32[6]{0:T(128)} %get-tuple-element.38.refs_0_, bf16[256,768]{1,0:T(8,128)(2,1)} %copy-done.3, bf16[256,768]{1,0:T(8,128)(2,1)} %copy-done.11, ...), custom_call_target="tpu_custom_call", output_to_operand_aliasing={{1}: (7, {}), {2}: (8, {})} | custom-call | tf_op jit(solution)/shard_map/pallas_call | solution.py:142
  88.2 1.5 collective-permute-start.10
  89.7 7.1 %collective-permute-done.10.refs_2_ = bf16[256,512]{1,0:T(8,128)(2,1)S(1)} collective-permute-done((bf16[256,512]{1,0:T(8,128)(2,1)}, bf16[256,512]{1,0:T(8,128)(2,1)S(1)}, u32[]{:S(2)}, u32[]{:S(2)}) %collective-permute-start.10) | collective-permute-done | bytes 262176 | tf_op jit(solution)/shard_map/ppermute | solution.py:29
  96.8 1.5 collective-permute-done.12.refs_4_
  99.0 4.1 %shard_map.94 = bf16[256,768]{1,0:T(8,128)(2,1)} custom-call(s32[6]{0:T(128)} %get-tuple-element.38.refs_0_, bf16[256,512]{1,0:T(8,128)(2,1)} %get-tuple-element.22.refs_1_, bf16[256,512]{1,0:T(8,128)(2,1)} %copy-done.21, bf16[256,512]{1,0:T(8,128)(2,1)} %copy-done.25, bf16[256,512]{1,0:T(8,128)(2,1)} %copy-done.29, bf16[4,512,768]{2,1,0:T(8,128)(2,1)} %bitcast.37, ...), custom_call_target="tpu_custom_call" | custom-call | tf_op jit(solution)/shard_map/pallas_call | solution.py:180
  103.1 4.5 %collective-permute-start.13 = (bf16[256,768]{1,0:T(8,128)(2,1)}, bf16[256,768]{1,0:T(8,128)(2,1)S(1)}, u32[]{:S(2)}, u32[]{:S(2)}) collective-permute-start(bf16[256,768]{1,0:T(8,128)(2,1)} %shard_map.94), channel_id=1, source_target_pairs={{0,4},{4,8},{8,12},{1,5},{5,9},{9,13},{2,6},{6,10},{10,14},{3,7},{... | collective-permute-start | bytes 1179656 | tf_op jit(solution)/shard_map/ppermute | solution.py:14
  110.2 6.2 %collective-permute-done.13 = bf16[256,768]{1,0:T(8,128)(2,1)S(1)} collective-permute-done((bf16[256,768]{1,0:T(8,128)(2,1)}, bf16[256,768]{1,0:T(8,128)(2,1)S(1)}, u32[]{:S(2)}, u32[]{:S(2)}) %collective-permute-start.13) | collective-permute-done | bytes 393248 | tf_op jit(solution)/shard_map/ppermute | solution.py:14
  116.6 1.6 collective-permute-start.14
  118.2 8.8 %collective-permute-done.14.refs_2_ = bf16[256,768]{1,0:T(8,128)(2,1)S(1)} collective-permute-done((bf16[256,768]{1,0:T(8,128)(2,1)S(1)}, bf16[256,768]{1,0:T(8,128)(2,1)S(1)}, u32[]{:S(2)}, u32[]{:S(2)}) %collective-permute-start.14) | collective-permute-done | bytes 393248 | tf_op jit(solution)/shard_map/ppermute | solution.py:29
  127.0 1.7 collective-permute-done.16.refs_4_
  128.8 0.7 copy-done.19
  129.5 12.5 %shard_map.95 = (bf16[256,512]{1,0:T(8,128)(2,1)}, bf16[4,768,128]{2,1,0:T(8,128)(2,1)}, bf16[4,768,128]{2,1,0:T(8,128)(2,1)}) custom-call(s32[6]{0:T(128)} %get-tuple-element.37.refs_0_, bf16[256,768]{1,0:T(8,128)(2,1)} %copy-done.4, bf16[256,768]{1,0:T(8,128)(2,1)} %copy-done.12, ...), custom_call_target="tpu_custom_call", output_to_operand_aliasing={{1}: (7, {}), {2}: (8, {})} | custom-call | tf_op jit(solution)/shard_map/pallas_call | solution.py:142
  142.0 1.5 collective-permute-start.17
  143.5 7.1 %collective-permute-done.17.refs_2_ = bf16[256,512]{1,0:T(8,128)(2,1)S(1)} collective-permute-done((bf16[256,512]{1,0:T(8,128)(2,1)}, bf16[256,512]{1,0:T(8,128)(2,1)S(1)}, u32[]{:S(2)}, u32[]{:S(2)}) %collective-permute-start.17) | collective-permute-done | bytes 262176 | tf_op jit(solution)/shard_map/ppermute | solution.py:29
  150.6 1.5 collective-permute-done.19.refs_4_
  152.8 4.1 %shard_map.96 = bf16[256,768]{1,0:T(8,128)(2,1)} custom-call(s32[6]{0:T(128)} %get-tuple-element.37.refs_0_, bf16[256,512]{1,0:T(8,128)(2,1)} %get-tuple-element.25.refs_1_, bf16[256,512]{1,0:T(8,128)(2,1)} %copy-done.22, bf16[256,512]{1,0:T(8,128)(2,1)} %copy-done.26, bf16[256,512]{1,0:T(8,128)(2,1)} %copy-done.30, bf16[4,512,768]{2,1,0:T(8,128)(2,1)} %bitcast.38, ...), custom_call_target="tpu_custom_call" | custom-call | tf_op jit(solution)/shard_map/pallas_call | solution.py:180
  156.9 4.3 %collective-permute-start.20 = (bf16[256,768]{1,0:T(8,128)(2,1)}, bf16[256,768]{1,0:T(8,128)(2,1)S(1)}, u32[]{:S(2)}, u32[]{:S(2)}) collective-permute-start(bf16[256,768]{1,0:T(8,128)(2,1)} %shard_map.96), channel_id=1, source_target_pairs={{0,4},{4,8},{8,12},{1,5},{5,9},{9,13},{2,6},{6,10},{10,14},{3,7},{... | collective-permute-start | bytes 1179656 | tf_op jit(solution)/shard_map/ppermute | solution.py:14
  163.9 6.3 %collective-permute-done.20 = bf16[256,768]{1,0:T(8,128)(2,1)S(1)} collective-permute-done((bf16[256,768]{1,0:T(8,128)(2,1)}, bf16[256,768]{1,0:T(8,128)(2,1)S(1)}, u32[]{:S(2)}, u32[]{:S(2)}) %collective-permute-start.20) | collective-permute-done | bytes 393248 | tf_op jit(solution)/shard_map/ppermute | solution.py:14
  170.4 1.6 collective-permute-start.21
  172.0 8.8 %collective-permute-done.21.refs_2_ = bf16[256,768]{1,0:T(8,128)(2,1)S(1)} collective-permute-done((bf16[256,768]{1,0:T(8,128)(2,1)S(1)}, bf16[256,768]{1,0:T(8,128)(2,1)S(1)}, u32[]{:S(2)}, u32[]{:S(2)}) %collective-permute-start.21) | collective-permute-done | bytes 393248 | tf_op jit(solution)/shard_map/ppermute | solution.py:29
  180.8 1.7 collective-permute-done.23.refs_4_
  182.5 0.7 copy-done.17
  183.3 12.5 %shard_map.97 = (bf16[256,512]{1,0:T(8,128)(2,1)}, bf16[4,768,128]{2,1,0:T(8,128)(2,1)}, bf16[4,768,128]{2,1,0:T(8,128)(2,1)}) custom-call(s32[6]{0:T(128)} %get-tuple-element.36.refs_0_, bf16[256,768]{1,0:T(8,128)(2,1)} %copy-done.2, bf16[256,768]{1,0:T(8,128)(2,1)} %copy-done.9, ...), custom_call_target="tpu_custom_call", output_to_operand_aliasing={{1}: (7, {}), {2}: (8, {})} | custom-call | tf_op jit(solution)/shard_map/pallas_call | solution.py:142
  195.8 1.6 collective-permute-start.24
  197.4 7.0 %collective-permute-done.24.refs_2_ = bf16[256,512]{1,0:T(8,128)(2,1)S(1)} collective-permute-done((bf16[256,512]{1,0:T(8,128)(2,1)}, bf16[256,512]{1,0:T(8,128)(2,1)S(1)}, u32[]{:S(2)}, u32[]{:S(2)}) %collective-permute-start.24) | collective-permute-done | bytes 262176 | tf_op jit(solution)/shard_map/ppermute | solution.py:29
  204.4 1.5 collective-permute-done.26.refs_4_
  206.7 4.1 %shard_map.98 = bf16[256,768]{1,0:T(8,128)(2,1)} custom-call(s32[6]{0:T(128)} %get-tuple-element.36.refs_0_, bf16[256,512]{1,0:T(8,128)(2,1)} %get-tuple-element.28.refs_1_, bf16[256,512]{1,0:T(8,128)(2,1)} %copy-done.23, bf16[256,512]{1,0:T(8,128)(2,1)} %copy-done.27, bf16[256,512]{1,0:T(8,128)(2,1)} %copy-done.31, bf16[4,512,768]{2,1,0:T(8,128)(2,1)} %bitcast.39, ...), custom_call_target="tpu_custom_call" | custom-call | tf_op jit(solution)/shard_map/pallas_call | solution.py:180
  210.8 2.3 %maximum_bitcast_fusion = bf16[4,1,256,768]{3,2,1,0:T(8,128)(2,1)} fusion(bf16[1,256,768]{2,1,0:T(8,128)(2,1)} %bitcast.43, bf16[1,256,768]{2,1,0:T(8,128)(2,1)S(1)} %bitcast.42, bf16[1,256,768]{2,1,0:T(8,128)(2,1)S(1)} %bitcast.41, bf16[1,256,768]{2,1,0:T(8,128)(2,1)S(1)} %bitcast.40), kind=kLoop, calls=%fused_computation.4 | loop fusion | flops 2359296 | bytes 3145728 | tf_op jit(solution)/shard_map/broadcast_in_dim | solution.py:251
  (100 shorter events, 6.8 us)
Async XLA Ops:
  7.7 13.9 %copy-start.1 = (bf16[256,768]{1,0:T(8,128)(2,1)}, bf16[256,768]{1,0:T(8,128)(2,1)S(1)}, u32[]{:S(2)}) copy-start(bf16[256,768]{1,0:T(8,128)(2,1)S(1)} %fusion.1.refs_1_.refs_6_) | copy-start | bytes 1179652
  7.7 12.1 %collective-permute-start = (bf16[256,768]{1,0:T(8,128)(2,1)S(1)}, bf16[256,768]{1,0:T(8,128)(2,1)S(1)}, u32[]{:S(2)}, u32[]{:S(2)}) collective-permute-start(bf16[256,768]{1,0:T(8,128)(2,1)S(1)} %fusion.1.refs_1_.refs_6_), channel_id=1, source_target_pairs={{0,2},{1,3},{2,0},{3,1},{4,6},{5,7},{6,4},{7,5},{8,10},{9,11},{10,... | collective-permute-start | bytes 1179656 | tf_op jit(solution)/shard_map/ppermute | solution.py:29
  10.7 9.7 %collective-permute-start.1 = (bf16[256,768]{1,0:T(8,128)(2,1)S(1)}, bf16[256,768]{1,0:T(8,128)(2,1)S(1)}, u32[]{:S(2)}, u32[]{:S(2)}) collective-permute-start(bf16[256,768]{1,0:T(8,128)(2,1)S(1)} %fusion.1.refs_1_.refs_6_), channel_id=1, source_target_pairs={{0,1},{1,0},{2,3},{3,2},{4,5},{5,4},{6,7},{7,6},{8,9},{9,8},{10,11... | collective-permute-start | bytes 1179656 | tf_op jit(solution)/shard_map/ppermute | solution.py:32
  19.8 1.7 copy-start.8
  19.8 1.7 collective-permute-start.2
  34.9 8.6 %collective-permute-start.3 = (bf16[256,512]{1,0:T(8,128)(2,1)}, bf16[256,512]{1,0:T(8,128)(2,1)S(1)}, u32[]{:S(2)}, u32[]{:S(2)}) collective-permute-start(bf16[256,512]{1,0:T(8,128)(2,1)} %get-tuple-element.19.refs_1_), channel_id=1, source_target_pairs={{0,2},{1,3},{2,0},{3,1},{4,6},{5,7},{6,4},{7,5},{8,10},{9,11},{10,... | collective-permute-start | bytes 786440 | tf_op jit(solution)/shard_map/ppermute | solution.py:29
  36.6 6.8 %collective-permute-start.4 = (bf16[256,512]{1,0:T(8,128)(2,1)}, bf16[256,512]{1,0:T(8,128)(2,1)S(1)}, u32[]{:S(2)}, u32[]{:S(2)}) collective-permute-start(bf16[256,512]{1,0:T(8,128)(2,1)} %get-tuple-element.19.refs_1_), channel_id=1, source_target_pairs={{0,1},{1,0},{2,3},{3,2},{4,5},{5,4},{6,7},{7,6},{8,9},{9,8},{10,11... | collective-permute-start | bytes 786440 | tf_op jit(solution)/shard_map/ppermute | solution.py:32
  43.4 1.5 copy-start.20
  43.4 1.5 collective-permute-start.5
  43.4 1.5 copy-start.24
  45.7 16.9 %copy-start = (bf16[768,768]{1,0:T(8,128)(2,1)S(1)}, bf16[768,768]{1,0:T(8,128)(2,1)}, u32[]{:S(2)}) copy-start(bf16[768,768]{1,0:T(8,128)(2,1)} %param.9) | copy-start | bytes 3538948
  49.9 12.7 %collective-permute-start.6 = (bf16[256,768]{1,0:T(8,128)(2,1)}, bf16[256,768]{1,0:T(8,128)(2,1)S(1)}, u32[]{:S(2)}, u32[]{:S(2)}) collective-permute-start(bf16[256,768]{1,0:T(8,128)(2,1)} %shard_map.92), channel_id=1, source_target_pairs={{0,4},{4,8},{8,12},{1,5},{5,9},{9,13},{2,6},{6,10},{10,14},{3,7},{... | collective-permute-start | bytes 1179656 | tf_op jit(solution)/shard_map/ppermute | solution.py:14
  62.8 12.1 %copy-start.3 = (bf16[256,768]{1,0:T(8,128)(2,1)}, bf16[256,768]{1,0:T(8,128)(2,1)S(1)}, u32[]{:S(2)}) copy-start(bf16[256,768]{1,0:T(8,128)(2,1)S(1)} %fusion.3.refs_1_.refs_6_) | copy-start | bytes 1179652
  62.8 10.4 %collective-permute-start.7 = (bf16[256,768]{1,0:T(8,128)(2,1)S(1)}, bf16[256,768]{1,0:T(8,128)(2,1)S(1)}, u32[]{:S(2)}, u32[]{:S(2)}) collective-permute-start(bf16[256,768]{1,0:T(8,128)(2,1)S(1)} %fusion.3.refs_1_.refs_6_), channel_id=1, source_target_pairs={{0,2},{1,3},{2,0},{3,1},{4,6},{5,7},{6,4},{7,5},{8,10},{9,11},{10,... | collective-permute-start | bytes 1179656 | tf_op jit(solution)/shard_map/ppermute | solution.py:29
  64.4 8.8 %collective-permute-start.8 = (bf16[256,768]{1,0:T(8,128)(2,1)S(1)}, bf16[256,768]{1,0:T(8,128)(2,1)S(1)}, u32[]{:S(2)}, u32[]{:S(2)}) collective-permute-start(bf16[256,768]{1,0:T(8,128)(2,1)S(1)} %fusion.3.refs_1_.refs_6_), channel_id=1, source_target_pairs={{0,1},{1,0},{2,3},{3,2},{4,5},{5,4},{6,7},{7,6},{8,9},{9,8},{10,11... | collective-permute-start | bytes 1179656 | tf_op jit(solution)/shard_map/ppermute | solution.py:32
  73.2 1.7 copy-start.11
  73.2 1.7 collective-permute-start.9
  73.2 1.7 copy-start.14
  88.2 8.6 %collective-permute-start.10 = (bf16[256,512]{1,0:T(8,128)(2,1)}, bf16[256,512]{1,0:T(8,128)(2,1)S(1)}, u32[]{:S(2)}, u32[]{:S(2)}) collective-permute-start(bf16[256,512]{1,0:T(8,128)(2,1)} %get-tuple-element.22.refs_1_), channel_id=1, source_target_pairs={{0,2},{1,3},{2,0},{3,1},{4,6},{5,7},{6,4},{7,5},{8,10},{9,11},{10,... | collective-permute-start | bytes 786440 | tf_op jit(solution)/shard_map/ppermute | solution.py:29
  89.7 7.1 %collective-permute-start.11 = (bf16[256,512]{1,0:T(8,128)(2,1)}, bf16[256,512]{1,0:T(8,128)(2,1)S(1)}, u32[]{:S(2)}, u32[]{:S(2)}) collective-permute-start(bf16[256,512]{1,0:T(8,128)(2,1)} %get-tuple-element.22.refs_1_), channel_id=1, source_target_pairs={{0,1},{1,0},{2,3},{3,2},{4,5},{5,4},{6,7},{7,6},{8,9},{9,8},{10,11... | collective-permute-start | bytes 786440 | tf_op jit(solution)/shard_map/ppermute | solution.py:32
  96.7 1.5 copy-start.21
  96.7 1.5 collective-permute-start.12
  96.7 1.5 copy-start.25
  103.1 13.2 %collective-permute-start.13 = (bf16[256,768]{1,0:T(8,128)(2,1)}, bf16[256,768]{1,0:T(8,128)(2,1)S(1)}, u32[]{:S(2)}, u32[]{:S(2)}) collective-permute-start(bf16[256,768]{1,0:T(8,128)(2,1)} %shard_map.94), channel_id=1, source_target_pairs={{0,4},{4,8},{8,12},{1,5},{5,9},{9,13},{2,6},{6,10},{10,14},{3,7},{... | collective-permute-start | bytes 1179656 | tf_op jit(solution)/shard_map/ppermute | solution.py:14
  116.6 12.1 %copy-start.4 = (bf16[256,768]{1,0:T(8,128)(2,1)}, bf16[256,768]{1,0:T(8,128)(2,1)S(1)}, u32[]{:S(2)}) copy-start(bf16[256,768]{1,0:T(8,128)(2,1)S(1)} %fusion.5.refs_1_.refs_6_) | copy-start | bytes 1179652
  116.6 10.4 %collective-permute-start.14 = (bf16[256,768]{1,0:T(8,128)(2,1)S(1)}, bf16[256,768]{1,0:T(8,128)(2,1)S(1)}, u32[]{:S(2)}, u32[]{:S(2)}) collective-permute-start(bf16[256,768]{1,0:T(8,128)(2,1)S(1)} %fusion.5.refs_1_.refs_6_), channel_id=1, source_target_pairs={{0,2},{1,3},{2,0},{3,1},{4,6},{5,7},{6,4},{7,5},{8,10},{9,11},{10,... | collective-permute-start | bytes 1179656 | tf_op jit(solution)/shard_map/ppermute | solution.py:29
  118.2 8.8 %collective-permute-start.15 = (bf16[256,768]{1,0:T(8,128)(2,1)S(1)}, bf16[256,768]{1,0:T(8,128)(2,1)S(1)}, u32[]{:S(2)}, u32[]{:S(2)}) collective-permute-start(bf16[256,768]{1,0:T(8,128)(2,1)S(1)} %fusion.5.refs_1_.refs_6_), channel_id=1, source_target_pairs={{0,1},{1,0},{2,3},{3,2},{4,5},{5,4},{6,7},{7,6},{8,9},{9,8},{10,11... | collective-permute-start | bytes 1179656 | tf_op jit(solution)/shard_map/ppermute | solution.py:32
  127.0 1.7 copy-start.12
  127.0 1.7 collective-permute-start.16
  127.0 1.7 copy-start.15
  142.0 8.6 %collective-permute-start.17 = (bf16[256,512]{1,0:T(8,128)(2,1)}, bf16[256,512]{1,0:T(8,128)(2,1)S(1)}, u32[]{:S(2)}, u32[]{:S(2)}) collective-permute-start(bf16[256,512]{1,0:T(8,128)(2,1)} %get-tuple-element.25.refs_1_), channel_id=1, source_target_pairs={{0,2},{1,3},{2,0},{3,1},{4,6},{5,7},{6,4},{7,5},{8,10},{9,11},{10,... | collective-permute-start | bytes 786440 | tf_op jit(solution)/shard_map/ppermute | solution.py:29
  143.5 7.1 %collective-permute-start.18 = (bf16[256,512]{1,0:T(8,128)(2,1)}, bf16[256,512]{1,0:T(8,128)(2,1)S(1)}, u32[]{:S(2)}, u32[]{:S(2)}) collective-permute-start(bf16[256,512]{1,0:T(8,128)(2,1)} %get-tuple-element.25.refs_1_), channel_id=1, source_target_pairs={{0,1},{1,0},{2,3},{3,2},{4,5},{5,4},{6,7},{7,6},{8,9},{9,8},{10,11... | collective-permute-start | bytes 786440 | tf_op jit(solution)/shard_map/ppermute | solution.py:32
  150.6 1.5 copy-start.22
  150.6 1.5 collective-permute-start.19
  156.9 13.2 %collective-permute-start.20 = (bf16[256,768]{1,0:T(8,128)(2,1)}, bf16[256,768]{1,0:T(8,128)(2,1)S(1)}, u32[]{:S(2)}, u32[]{:S(2)}) collective-permute-start(bf16[256,768]{1,0:T(8,128)(2,1)} %shard_map.96), channel_id=1, source_target_pairs={{0,4},{4,8},{8,12},{1,5},{5,9},{9,13},{2,6},{6,10},{10,14},{3,7},{... | collective-permute-start | bytes 1179656 | tf_op jit(solution)/shard_map/ppermute | solution.py:14
  170.4 12.1 %copy-start.2 = (bf16[256,768]{1,0:T(8,128)(2,1)}, bf16[256,768]{1,0:T(8,128)(2,1)S(1)}, u32[]{:S(2)}) copy-start(bf16[256,768]{1,0:T(8,128)(2,1)S(1)} %fusion.7.refs_1_.refs_6_) | copy-start | bytes 1179652
  170.4 10.4 %collective-permute-start.21 = (bf16[256,768]{1,0:T(8,128)(2,1)S(1)}, bf16[256,768]{1,0:T(8,128)(2,1)S(1)}, u32[]{:S(2)}, u32[]{:S(2)}) collective-permute-start(bf16[256,768]{1,0:T(8,128)(2,1)S(1)} %fusion.7.refs_1_.refs_6_), channel_id=1, source_target_pairs={{0,2},{1,3},{2,0},{3,1},{4,6},{5,7},{6,4},{7,5},{8,10},{9,11},{10,... | collective-permute-start | bytes 1179656 | tf_op jit(solution)/shard_map/ppermute | solution.py:29
  172.0 8.8 %collective-permute-start.22 = (bf16[256,768]{1,0:T(8,128)(2,1)S(1)}, bf16[256,768]{1,0:T(8,128)(2,1)S(1)}, u32[]{:S(2)}, u32[]{:S(2)}) collective-permute-start(bf16[256,768]{1,0:T(8,128)(2,1)S(1)} %fusion.7.refs_1_.refs_6_), channel_id=1, source_target_pairs={{0,1},{1,0},{2,3},{3,2},{4,5},{5,4},{6,7},{7,6},{8,9},{9,8},{10,11... | collective-permute-start | bytes 1179656 | tf_op jit(solution)/shard_map/ppermute | solution.py:32
  180.8 1.7 copy-start.9
  180.8 1.7 collective-permute-start.23
  180.8 1.7 copy-start.13
  195.8 15.0 %copy-start.5 = (bf16[256,768]{1,0:T(8,128)(2,1)S(1)}, bf16[256,768]{1,0:T(8,128)(2,1)}, u32[]{:S(2)}) copy-start(bf16[256,768]{1,0:T(8,128)(2,1)} %shard_map.92) | copy-start | bytes 1179652
  195.8 15.0 %copy-start.6 = (bf16[256,768]{1,0:T(8,128)(2,1)S(1)}, bf16[256,768]{1,0:T(8,128)(2,1)}, u32[]{:S(2)}) copy-start(bf16[256,768]{1,0:T(8,128)(2,1)} %shard_map.94) | copy-start | bytes 1179652
  195.8 15.0 %copy-start.7 = (bf16[256,768]{1,0:T(8,128)(2,1)S(1)}, bf16[256,768]{1,0:T(8,128)(2,1)}, u32[]{:S(2)}) copy-start(bf16[256,768]{1,0:T(8,128)(2,1)} %shard_map.96) | copy-start | bytes 1179652
  195.8 8.6 %collective-permute-start.24 = (bf16[256,512]{1,0:T(8,128)(2,1)}, bf16[256,512]{1,0:T(8,128)(2,1)S(1)}, u32[]{:S(2)}, u32[]{:S(2)}) collective-permute-start(bf16[256,512]{1,0:T(8,128)(2,1)} %get-tuple-element.28.refs_1_), channel_id=1, source_target_pairs={{0,2},{1,3},{2,0},{3,1},{4,6},{5,7},{6,4},{7,5},{8,10},{9,11},{10,... | collective-permute-start | bytes 786440 | tf_op jit(solution)/shard_map/ppermute | solution.py:29
  197.4 7.0 %collective-permute-start.25 = (bf16[256,512]{1,0:T(8,128)(2,1)}, bf16[256,512]{1,0:T(8,128)(2,1)S(1)}, u32[]{:S(2)}, u32[]{:S(2)}) collective-permute-start(bf16[256,512]{1,0:T(8,128)(2,1)} %get-tuple-element.28.refs_1_), channel_id=1, source_target_pairs={{0,1},{1,0},{2,3},{3,2},{4,5},{5,4},{6,7},{7,6},{8,9},{9,8},{10,11... | collective-permute-start | bytes 786440 | tf_op jit(solution)/shard_map/ppermute | solution.py:32
  204.4 1.5 copy-start.23
  204.4 1.5 collective-permute-start.26
  (11 other events, 10.0 us)

commit v12 on v9

--- a/solution.py
+++ b/solution.py
@@ -1,3 +1,5 @@
+import functools
+
 import jax
 import jax.numpy as jnp
 from jax import lax
@@ -175,12 +177,12 @@
     )(where, *parts, scale_blocks, qkv_weights, key_cache, value_cache)
 
 
-def exit_kernel(*refs):
+def exit_kernel(turn, *refs):
     where_ref = refs[0]
-    count = len(refs) - 5
+    count = len(refs) - 8
     part_refs = refs[1 : 1 + count]
     weights_ref, own_ref, gate_ref = refs[1 + count : 4 + count]
-    out_ref = refs[4 + count]
+    out_ref, turns_ref, copied = refs[5 + count :]
     patch_count = where_ref[1]
     projected = sum(
         jnp.dot(
@@ -193,24 +195,34 @@
     updated = own_ref[...].astype(jnp.float32) + gate_ref[...] * projected
     live = lax.broadcasted_iota(jnp.int32, updated.shape, 0) < patch_count
     out_ref[...] = jnp.where(live, updated, 0.0).astype(out_ref.dtype)
-
-
-def leave_block(parts, out_weights, own_rows, gating_here, where):
+    store = pltpu.make_async_copy(out_ref, turns_ref.at[turn], copied)
+    store.start()
+    store.wait()
+
+
+def leave_block(parts, out_weights, own_rows, gating_here, where, every_turn, turn):
     count = len(parts)
     span, head_width = parts[0].shape
     vmem = pl.BlockSpec(memory_space=pltpu.VMEM)
     smem = pl.BlockSpec(memory_space=pltpu.SMEM)
+    anywhere = pl.BlockSpec(memory_space=pl.ANY)
     return pl.pallas_call(
-        exit_kernel,
-        in_specs=[smem] + [vmem] * (count + 3),
-        out_specs=vmem,
-        out_shape=jax.ShapeDtypeStruct(own_rows.shape, own_rows.dtype),
+        functools.partial(exit_kernel, turn),
+        in_specs=[smem] + [vmem] * (count + 3) + [anywhere],
+        out_specs=[vmem, anywhere],
+        out_shape=[
+            jax.ShapeDtypeStruct(own_rows.shape, own_rows.dtype),
+            jax.ShapeDtypeStruct(every_turn.shape, every_turn.dtype),
+        ],
+        scratch_shapes=[pltpu.SemaphoreType.DMA(())],
+        input_output_aliases={count + 4: 1},
     )(
         where,
         *parts,
         out_weights.reshape(count, head_width, out_weights.shape[1]),
         own_rows,
         gating_here.reshape(1, -1),
+        every_turn,
     )
 
 
@@ -238,7 +250,7 @@
     gating_here = branch_gates[0]
     row_numbers = jnp.arange(biggest_patch_span)
 
-    results = []
+    every_turn = jnp.zeros((patches, biggest_patch_span, incoming_states.shape[1]), jnp.bfloat16)
     entering_ext = jnp.concatenate(
         [incoming_states, jnp.zeros((biggest_patch_span, columns), jnp.bfloat16)], axis=0
     )
@@ -264,14 +276,15 @@
             where,
             turn_number > 0,
         )
-        updated = leave_block(
+        updated, every_turn = leave_block(
             with_partner([head_rows] + across_chips(head_rows)),
             out_weights,
             row_parts[0],
             gating_here,
             where,
-        )
-        results.append(updated)
+            every_turn,
+            turn_number,
+        )
         if turn_number + 1 < patches:
             entry_patch = lax.dynamic_slice_in_dim(
                 entering_ext, starts[turn_number + 1], biggest_patch_span, 0
@@ -284,7 +297,7 @@
             row_parts = [
                 jnp.where(section_zero, entry, passed) for entry, passed in zip(entry_parts, arrived)
             ]
-    return jnp.stack(results)[:, None]
+    return every_turn[:, None]
 
 
 def solution(mesh):

time: 212 us -> 213 us (level)
  Pallas kernels: 66.6 us -> 69.7 us
  other arithmetic: 9.95 us -> 7.63 us
    pallas_call x4, Pallas kernels: 16.5 us -> 19.6 us  [leave_block(): pl.pallas_call(functools.partial(exit_kernel, turn), in_specs=[smem] + [v...]
    broadcast_in_dim x1 -> x0, other arithmetic: 2.34 us -> none  [shards(): return jnp.stack(results)[:, None]]
    unnamed x66 -> x60, local copies, waits for them, and re-layouts: 5.86 us -> 5.14 us
where the time goes in v12:
time: 213 us
  waiting for transfers between devices  83.3 us (39%)
  Pallas kernels  69.7 us (33%)
  starting transfers between devices  37.2 us (17%)
  local copies, waits for them, and re-layouts  8.39 us (4%)
  other arithmetic  7.63 us (4%)
  between operations  6.62 us (3%)
    pallas_call x4, Pallas kernels, attend_block(): pl.pallas_call(block_kernel, grid_spec=grid_spec, out_shape=[jax.ShapeDty...  50.1 us
    ppermute x5, waiting for transfers between devices, across_chips(): lax.ppermute(block, 'seq', [(source, (source + step) % count) for source...  37.1 us
    ppermute x6, waiting for transfers between devices, to_next_section(): lax.ppermute(block, ('section', 'seq'), [(section * count + source, (sect...  21.2 us
    pallas_call x4, Pallas kernels, leave_block(): pl.pallas_call(functools.partial(exit_kernel, turn), in_specs=[smem] + [v...  19.6 us
    ppermute x6, starting transfers between devices, to_next_section(): lax.ppermute(block, ('section', 'seq'), [(section * count + source, (sect...  16.7 us
    ppermute x3, waiting for transfers between devices, across_chips_first_section(): lax.ppermute(block, ('section', 'seq'), [(source, (source + step) % count...  12.8 us
    ppermute x16, waiting for transfers between devices, with_partner(): return parts + [lax.ppermute(part, 'seq', to_partner) for part in parts]  12.2 us
    ppermute x3, starting transfers between devices, across_chips_first_section(): lax.ppermute(block, ('section', 'seq'), [(source, (source + step) % count...  10.9 us
  transfers between devices with their start and end apart: 30, of which 22 were waited for; matrix products, arithmetic and copies ran while one was open for 2% of the time, Pallas kernels for 0%

profile of v12, /device:TPU:0, one launch (start us, length us, event | category | flops | bytes accessed | tf_op | source)
XLA Modules:
  0.0 212.8 jit_solution(15771441175768195226)
XLA Ops:
  0.1 0.8 reduce-window.9
  0.9 1.3 bitcast_subtract_fusion
  3.7 1.2 fusion.3.refs_1_.refs_6_
  4.9 3.0 %collective-permute-start = (bf16[256,768]{1,0:T(8,128)(2,1)S(1)}, bf16[256,768]{1,0:T(8,128)(2,1)S(1)}, u32[]{:S(2)}, u32[]{:S(2)}) collective-permute-start(bf16[256,768]{1,0:T(8,128)(2,1)S(1)} %fusion.3.refs_1_.refs_6_), channel_id=1, source_target_pairs={{0,2},{1,3},{2,0},{3,1},{4,6},{5,7},{6,4},{7,5},{8,10},{9,11},{10,... | collective-permute-start | bytes 1179656 | tf_op jit(solution)/shard_map/ppermute | solution.py:24
  8.0 9.1 %collective-permute-done.refs_2_ = bf16[256,768]{1,0:T(8,128)(2,1)S(1)} collective-permute-done((bf16[256,768]{1,0:T(8,128)(2,1)S(1)}, bf16[256,768]{1,0:T(8,128)(2,1)S(1)}, u32[]{:S(2)}, u32[]{:S(2)}) %collective-permute-start) | collective-permute-done | bytes 393248 | tf_op jit(solution)/shard_map/ppermute | solution.py:24
  17.7 1.0 collective-permute-done.2.refs_4_
  19.5 12.5 %shard_map.91 = (bf16[256,512]{1,0:T(8,128)(2,1)}, bf16[4,768,128]{2,1,0:T(8,128)(2,1)}, bf16[4,768,128]{2,1,0:T(8,128)(2,1)}) custom-call(s32[6]{0:T(128)} %get-tuple-element.51.refs_0_, bf16[256,768]{1,0:T(8,128)(2,1)} %copy-done.4, bf16[256,768]{1,0:T(8,128)(2,1)} %copy-done.11, bf16[256,768]{1,0:T(8,128)(2,1)} %copy-done.12, ...), custom_call_target="tpu_custom_call" | custom-call | tf_op jit(solution)/shard_map/pallas_call | solution.py:167
  32.1 1.7 collective-permute-start.3
  33.8 6.8 %collective-permute-done.3.refs_2_ = bf16[256,512]{1,0:T(8,128)(2,1)S(1)} collective-permute-done((bf16[256,512]{1,0:T(8,128)(2,1)}, bf16[256,512]{1,0:T(8,128)(2,1)S(1)}, u32[]{:S(2)}, u32[]{:S(2)}) %collective-permute-start.3) | collective-permute-done | bytes 262176 | tf_op jit(solution)/shard_map/ppermute | solution.py:24
  40.6 1.5 collective-permute-done.5.refs_4_
  42.2 1.2 broadcast_in_dim.78.refs_8_
  43.4 4.9 %shard_map.92 = (bf16[256,768]{1,0:T(8,128)(2,1)}, bf16[4,256,768]{2,1,0:T(8,128)(2,1)}) custom-call(s32[6]{0:T(128)} %get-tuple-element.51.refs_0_, bf16[256,512]{1,0:T(8,128)(2,1)} %get-tuple-element.26.refs_1_, bf16[256,512]{1,0:T(8,128)(2,1)} %copy-done.17, bf16[256,512]{1,0:T(8,128)(2,1)} %copy-done.21, ...), custom_call_target="tpu_custom_call", output_to_operand_aliasing={{1}: (8, {})} | custom-call | tf_op jit(solution)/shard_map/pallas_call | solution.py:209
  48.4 3.8 %collective-permute-start.6 = (bf16[256,768]{1,0:T(8,128)(2,1)}, bf16[256,768]{1,0:T(8,128)(2,1)S(1)}, u32[]{:S(2)}, u32[]{:S(2)}) collective-permute-start(bf16[256,768]{1,0:T(8,128)(2,1)} %get-tuple-element.27), channel_id=1, source_target_pairs={{0,4},{1,5},{2,6},{3,7},{4,8},{5,9},{6,10},{7,11},{8,12},{9,13},{1... | collective-permute-start | bytes 1179656 | tf_op jit(solution)/shard_map/ppermute | solution.py:49
  56.1 4.4 %collective-permute-start.8 = (bf16[256,768]{1,0:T(8,128)(2,1)}, bf16[256,768]{1,0:T(8,128)(2,1)S(1)}, u32[]{:S(2)}, u32[]{:S(2)}) collective-permute-start(bf16[256,768]{1,0:T(8,128)(2,1)} %get-tuple-element.27), channel_id=1, source_target_pairs={{0,6},{1,7},{2,4},{3,5},{4,10},{5,11},{6,8},{7,9},{8,14},{9,15},{1... | collective-permute-start | bytes 1179656 | tf_op jit(solution)/shard_map/ppermute | solution.py:49
  60.5 0.9 collective-permute-done.6
  61.7 3.9 %collective-permute-start.7 = (bf16[256,768]{1,0:T(8,128)(2,1)S(1)}, bf16[256,768]{1,0:T(8,128)(2,1)S(1)}, u32[]{:S(2)}, u32[]{:S(2)}) collective-permute-start(bf16[256,768]{1,0:T(8,128)(2,1)S(1)} %get-tuple-element.50), channel_id=1, source_target_pairs={{0,2},{1,3},{2,0},{3,1},{16,18},{17,19},{18,16},{19,17}} | collective-permute-start | bytes 1179656 | tf_op jit(solution)/shard_map/ppermute | solution.py:32
  65.6 3.9 %collective-permute-done.8 = bf16[256,768]{1,0:T(8,128)(2,1)S(1)} collective-permute-done((bf16[256,768]{1,0:T(8,128)(2,1)}, bf16[256,768]{1,0:T(8,128)(2,1)S(1)}, u32[]{:S(2)}, u32[]{:S(2)}) %collective-permute-start.8) | collective-permute-done | bytes 393248 | tf_op jit(solution)/shard_map/ppermute | solution.py:49
  69.5 4.0 %collective-permute-done.7 = bf16[256,768]{1,0:T(8,128)(2,1)S(1)} collective-permute-done((bf16[256,768]{1,0:T(8,128)(2,1)S(1)}, bf16[256,768]{1,0:T(8,128)(2,1)S(1)}, u32[]{:S(2)}, u32[]{:S(2)}) %collective-permute-start.7) | collective-permute-done | bytes 393248 | tf_op jit(solution)/shard_map/ppermute | solution.py:32
  73.7 1.7 collective-permute-done.10.refs_4_
  76.2 12.5 %shard_map.93 = (bf16[256,512]{1,0:T(8,128)(2,1)}, bf16[4,768,128]{2,1,0:T(8,128)(2,1)}, bf16[4,768,128]{2,1,0:T(8,128)(2,1)}) custom-call(s32[6]{0:T(128)} %get-tuple-element.52.refs_0_, bf16[256,768]{1,0:T(8,128)(2,1)} %copy-done.2, bf16[256,768]{1,0:T(8,128)(2,1)} %copy-done.6, ...), custom_call_target="tpu_custom_call", output_to_operand_aliasing={{1}: (7, {}), {2}: (8, {})} | custom-call | tf_op jit(solution)/shard_map/pallas_call | solution.py:167
  88.7 1.5 collective-permute-start.11
  90.2 7.1 %collective-permute-done.11.refs_2_ = bf16[256,512]{1,0:T(8,128)(2,1)S(1)} collective-permute-done((bf16[256,512]{1,0:T(8,128)(2,1)}, bf16[256,512]{1,0:T(8,128)(2,1)S(1)}, u32[]{:S(2)}, u32[]{:S(2)}) %collective-permute-start.11) | collective-permute-done | bytes 262176 | tf_op jit(solution)/shard_map/ppermute | solution.py:24
  97.3 1.5 collective-permute-done.13.refs_4_
  99.5 4.9 %shard_map.94 = (bf16[256,768]{1,0:T(8,128)(2,1)}, bf16[4,256,768]{2,1,0:T(8,128)(2,1)}) custom-call(s32[6]{0:T(128)} %get-tuple-element.52.refs_0_, bf16[256,512]{1,0:T(8,128)(2,1)} %get-tuple-element.30.refs_1_, bf16[256,512]{1,0:T(8,128)(2,1)} %copy-done.18, bf16[256,512]{1,0:T(8,128)(2,1)} %copy-done.22, ...), custom_call_target="tpu_custom_call", output_to_operand_aliasing={{1}: (8, {})} | custom-call | tf_op jit(solution)/shard_map/pallas_call | solution.py:209
  104.4 1.3 collective-permute-start.14
  108.3 3.3 %collective-permute-start.16 = (bf16[256,768]{1,0:T(8,128)(2,1)}, bf16[256,768]{1,0:T(8,128)(2,1)S(1)}, u32[]{:S(2)}, u32[]{:S(2)}) collective-permute-start(bf16[256,768]{1,0:T(8,128)(2,1)} %get-tuple-element.32), channel_id=1, source_target_pairs={{0,6},{1,7},{2,4},{3,5},{4,10},{5,11},{6,8},{7,9},{8,14},{9,15},{1... | collective-permute-start | bytes 1179656 | tf_op jit(solution)/shard_map/ppermute | solution.py:49
  111.6 3.8 %collective-permute-done.14 = bf16[256,768]{1,0:T(8,128)(2,1)S(1)} collective-permute-done((bf16[256,768]{1,0:T(8,128)(2,1)}, bf16[256,768]{1,0:T(8,128)(2,1)S(1)}, u32[]{:S(2)}, u32[]{:S(2)}) %collective-permute-start.14) | collective-permute-done | bytes 393248 | tf_op jit(solution)/shard_map/ppermute | solution.py:49
  115.7 3.6 %collective-permute-start.15 = (bf16[256,768]{1,0:T(8,128)(2,1)S(1)}, bf16[256,768]{1,0:T(8,128)(2,1)S(1)}, u32[]{:S(2)}, u32[]{:S(2)}) collective-permute-start(bf16[256,768]{1,0:T(8,128)(2,1)S(1)} %get-tuple-element.48), channel_id=1, source_target_pairs={{0,2},{1,3},{2,0},{3,1},{16,18},{17,19},{18,16},{19,17}} | collective-permute-start | bytes 1179656 | tf_op jit(solution)/shard_map/ppermute | solution.py:32
  119.3 4.0 %collective-permute-done.16 = bf16[256,768]{1,0:T(8,128)(2,1)S(1)} collective-permute-done((bf16[256,768]{1,0:T(8,128)(2,1)}, bf16[256,768]{1,0:T(8,128)(2,1)S(1)}, u32[]{:S(2)}, u32[]{:S(2)}) %collective-permute-start.16) | collective-permute-done | bytes 393248 | tf_op jit(solution)/shard_map/ppermute | solution.py:49
  123.3 4.4 %collective-permute-done.15 = bf16[256,768]{1,0:T(8,128)(2,1)S(1)} collective-permute-done((bf16[256,768]{1,0:T(8,128)(2,1)S(1)}, bf16[256,768]{1,0:T(8,128)(2,1)S(1)}, u32[]{:S(2)}, u32[]{:S(2)}) %collective-permute-start.15) | collective-permute-done | bytes 393248 | tf_op jit(solution)/shard_map/ppermute | solution.py:32
  127.9 1.7 collective-permute-done.18.refs_4_
  130.3 12.5 %shard_map.95 = (bf16[256,512]{1,0:T(8,128)(2,1)}, bf16[4,768,128]{2,1,0:T(8,128)(2,1)}, bf16[4,768,128]{2,1,0:T(8,128)(2,1)}) custom-call(s32[6]{0:T(128)} %get-tuple-element.53.refs_0_, bf16[256,768]{1,0:T(8,128)(2,1)} %copy-done.3, bf16[256,768]{1,0:T(8,128)(2,1)} %copy-done.7, ...), custom_call_target="tpu_custom_call", output_to_operand_aliasing={{1}: (7, {}), {2}: (8, {})} | custom-call | tf_op jit(solution)/shard_map/pallas_call | solution.py:167
  142.8 1.5 collective-permute-start.19
  144.3 7.1 %collective-permute-done.19.refs_2_ = bf16[256,512]{1,0:T(8,128)(2,1)S(1)} collective-permute-done((bf16[256,512]{1,0:T(8,128)(2,1)}, bf16[256,512]{1,0:T(8,128)(2,1)S(1)}, u32[]{:S(2)}, u32[]{:S(2)}) %collective-permute-start.19) | collective-permute-done | bytes 262176 | tf_op jit(solution)/shard_map/ppermute | solution.py:24
  151.4 1.5 collective-permute-done.21.refs_4_
  153.7 4.9 %shard_map.96 = (bf16[256,768]{1,0:T(8,128)(2,1)}, bf16[4,256,768]{2,1,0:T(8,128)(2,1)}) custom-call(s32[6]{0:T(128)} %get-tuple-element.53.refs_0_, bf16[256,512]{1,0:T(8,128)(2,1)} %get-tuple-element.35.refs_1_, bf16[256,512]{1,0:T(8,128)(2,1)} %copy-done.19, bf16[256,512]{1,0:T(8,128)(2,1)} %copy-done.23, ...), custom_call_target="tpu_custom_call", output_to_operand_aliasing={{1}: (8, {})} | custom-call | tf_op jit(solution)/shard_map/pallas_call | solution.py:209
  158.5 1.3 collective-permute-start.22
  162.6 2.6 %collective-permute-start.24 = (bf16[256,768]{1,0:T(8,128)(2,1)}, bf16[256,768]{1,0:T(8,128)(2,1)S(1)}, u32[]{:S(2)}, u32[]{:S(2)}) collective-permute-start(bf16[256,768]{1,0:T(8,128)(2,1)} %get-tuple-element.37), channel_id=1, source_target_pairs={{0,6},{1,7},{2,4},{3,5},{4,10},{5,11},{6,8},{7,9},{8,14},{9,15},{1... | collective-permute-start | bytes 1179656 | tf_op jit(solution)/shard_map/ppermute | solution.py:49
  165.1 4.4 %collective-permute-done.22 = bf16[256,768]{1,0:T(8,128)(2,1)S(1)} collective-permute-done((bf16[256,768]{1,0:T(8,128)(2,1)}, bf16[256,768]{1,0:T(8,128)(2,1)S(1)}, u32[]{:S(2)}, u32[]{:S(2)}) %collective-permute-start.22) | collective-permute-done | bytes 393248 | tf_op jit(solution)/shard_map/ppermute | solution.py:49
  169.8 3.4 %collective-permute-start.23 = (bf16[256,768]{1,0:T(8,128)(2,1)S(1)}, bf16[256,768]{1,0:T(8,128)(2,1)S(1)}, u32[]{:S(2)}, u32[]{:S(2)}) collective-permute-start(bf16[256,768]{1,0:T(8,128)(2,1)S(1)} %get-tuple-element.46), channel_id=1, source_target_pairs={{0,2},{1,3},{2,0},{3,1},{16,18},{17,19},{18,16},{19,17}} | collective-permute-start | bytes 1179656 | tf_op jit(solution)/shard_map/ppermute | solution.py:32
  173.3 4.2 %collective-permute-done.24 = bf16[256,768]{1,0:T(8,128)(2,1)S(1)} collective-permute-done((bf16[256,768]{1,0:T(8,128)(2,1)}, bf16[256,768]{1,0:T(8,128)(2,1)S(1)}, u32[]{:S(2)}, u32[]{:S(2)}) %collective-permute-start.24) | collective-permute-done | bytes 393248 | tf_op jit(solution)/shard_map/ppermute | solution.py:49
  177.5 4.4 %collective-permute-done.23 = bf16[256,768]{1,0:T(8,128)(2,1)S(1)} collective-permute-done((bf16[256,768]{1,0:T(8,128)(2,1)S(1)}, bf16[256,768]{1,0:T(8,128)(2,1)S(1)}, u32[]{:S(2)}, u32[]{:S(2)}) %collective-permute-start.23) | collective-permute-done | bytes 393248 | tf_op jit(solution)/shard_map/ppermute | solution.py:32
  182.0 1.7 collective-permute-done.26.refs_4_
  184.5 12.5 %shard_map.97 = (bf16[256,512]{1,0:T(8,128)(2,1)}, bf16[4,768,128]{2,1,0:T(8,128)(2,1)}, bf16[4,768,128]{2,1,0:T(8,128)(2,1)}) custom-call(s32[6]{0:T(128)} %get-tuple-element.54.refs_0_, bf16[256,768]{1,0:T(8,128)(2,1)} %copy-done.1, bf16[256,768]{1,0:T(8,128)(2,1)} %copy-done.5, ...), custom_call_target="tpu_custom_call", output_to_operand_aliasing={{1}: (7, {}), {2}: (8, {})} | custom-call | tf_op jit(solution)/shard_map/pallas_call | solution.py:167
  197.0 1.5 collective-permute-start.27
  198.5 7.1 %collective-permute-done.27.refs_2_ = bf16[256,512]{1,0:T(8,128)(2,1)S(1)} collective-permute-done((bf16[256,512]{1,0:T(8,128)(2,1)}, bf16[256,512]{1,0:T(8,128)(2,1)S(1)}, u32[]{:S(2)}, u32[]{:S(2)}) %collective-permute-start.27) | collective-permute-done | bytes 262176 | tf_op jit(solution)/shard_map/ppermute | solution.py:24
  205.6 1.5 collective-permute-done.29.refs_4_
  207.8 4.9 %shard_map.98 = (bf16[256,768]{1,0:T(8,128)(2,1)}, bf16[4,256,768]{2,1,0:T(8,128)(2,1)}) custom-call(s32[6]{0:T(128)} %get-tuple-element.54.refs_0_, bf16[256,512]{1,0:T(8,128)(2,1)} %get-tuple-element.40.refs_1_, bf16[256,512]{1,0:T(8,128)(2,1)} %copy-done.20, bf16[256,512]{1,0:T(8,128)(2,1)} %copy-done.24, ...), custom_call_target="tpu_custom_call", output_to_operand_aliasing={{1}: (8, {})} | custom-call | tf_op jit(solution)/shard_map/pallas_call | solution.py:209
  (106 shorter events, 11.9 us)
Async XLA Ops:
  4.9 13.9 %copy-start.4 = (bf16[256,768]{1,0:T(8,128)(2,1)}, bf16[256,768]{1,0:T(8,128)(2,1)S(1)}, u32[]{:S(2)}) copy-start(bf16[256,768]{1,0:T(8,128)(2,1)S(1)} %fusion.3.refs_1_.refs_6_) | copy-start | bytes 1179652
  4.9 12.1 %collective-permute-start = (bf16[256,768]{1,0:T(8,128)(2,1)S(1)}, bf16[256,768]{1,0:T(8,128)(2,1)S(1)}, u32[]{:S(2)}, u32[]{:S(2)}) collective-permute-start(bf16[256,768]{1,0:T(8,128)(2,1)S(1)} %fusion.3.refs_1_.refs_6_), channel_id=1, source_target_pairs={{0,2},{1,3},{2,0},{3,1},{4,6},{5,7},{6,4},{7,5},{8,10},{9,11},{10,... | collective-permute-start | bytes 1179656 | tf_op jit(solution)/shard_map/ppermute | solution.py:24
  8.0 9.8 %collective-permute-start.1 = (bf16[256,768]{1,0:T(8,128)(2,1)S(1)}, bf16[256,768]{1,0:T(8,128)(2,1)S(1)}, u32[]{:S(2)}, u32[]{:S(2)}) collective-permute-start(bf16[256,768]{1,0:T(8,128)(2,1)S(1)} %fusion.3.refs_1_.refs_6_), channel_id=1, source_target_pairs={{0,1},{1,0},{2,3},{3,2},{4,5},{5,4},{6,7},{7,6},{8,9},{9,8},{10,11... | collective-permute-start | bytes 1179656 | tf_op jit(solution)/shard_map/ppermute | solution.py:42
  17.1 1.7 copy-start.11
  17.1 1.7 collective-permute-start.2
  32.1 8.5 %collective-permute-start.3 = (bf16[256,512]{1,0:T(8,128)(2,1)}, bf16[256,512]{1,0:T(8,128)(2,1)S(1)}, u32[]{:S(2)}, u32[]{:S(2)}) collective-permute-start(bf16[256,512]{1,0:T(8,128)(2,1)} %get-tuple-element.26.refs_1_), channel_id=1, source_target_pairs={{0,2},{1,3},{2,0},{3,1},{4,6},{5,7},{6,4},{7,5},{8,10},{9,11},{10,... | collective-permute-start | bytes 786440 | tf_op jit(solution)/shard_map/ppermute | solution.py:24
  33.8 6.8 %collective-permute-start.4 = (bf16[256,512]{1,0:T(8,128)(2,1)}, bf16[256,512]{1,0:T(8,128)(2,1)S(1)}, u32[]{:S(2)}, u32[]{:S(2)}) collective-permute-start(bf16[256,512]{1,0:T(8,128)(2,1)} %get-tuple-element.26.refs_1_), channel_id=1, source_target_pairs={{0,1},{1,0},{2,3},{3,2},{4,5},{5,4},{6,7},{7,6},{8,9},{9,8},{10,11... | collective-permute-start | bytes 786440 | tf_op jit(solution)/shard_map/ppermute | solution.py:42
  40.6 2.8 %copy-start.17 = (bf16[256,512]{1,0:T(8,128)(2,1)}, bf16[256,512]{1,0:T(8,128)(2,1)S(1)}, u32[]{:S(2)}) copy-start(bf16[256,512]{1,0:T(8,128)(2,1)S(1)} %collective-permute-done.3.refs_2_) | copy-start | bytes 786436
  40.6 1.5 collective-permute-start.5
  40.6 2.8 %copy-start.21 = (bf16[256,512]{1,0:T(8,128)(2,1)}, bf16[256,512]{1,0:T(8,128)(2,1)S(1)}, u32[]{:S(2)}) copy-start(bf16[256,512]{1,0:T(8,128)(2,1)S(1)} %collective-permute-done.4.refs_3_) | copy-start | bytes 786436
  43.4 11.3 %copy-start.29 = (s32[4]{0:T(128)S(1)}, s32[4]{0:T(128)}, u32[]{:S(2)}) copy-start(s32[4]{0:T(128)} %param.11) | copy-start | bytes 52
  43.4 18.0 %copy-start = (bf16[768,768]{1,0:T(8,128)(2,1)S(1)}, bf16[768,768]{1,0:T(8,128)(2,1)}, u32[]{:S(2)}) copy-start(bf16[768,768]{1,0:T(8,128)(2,1)} %param.9) | copy-start | bytes 3538948
  48.4 13.0 %collective-permute-start.6 = (bf16[256,768]{1,0:T(8,128)(2,1)}, bf16[256,768]{1,0:T(8,128)(2,1)S(1)}, u32[]{:S(2)}, u32[]{:S(2)}) collective-permute-start(bf16[256,768]{1,0:T(8,128)(2,1)} %get-tuple-element.27), channel_id=1, source_target_pairs={{0,4},{1,5},{2,6},{3,7},{4,8},{5,9},{6,10},{7,11},{8,12},{9,13},{1... | collective-permute-start | bytes 1179656 | tf_op jit(solution)/shard_map/ppermute | solution.py:49
  56.1 13.4 %collective-permute-start.8 = (bf16[256,768]{1,0:T(8,128)(2,1)}, bf16[256,768]{1,0:T(8,128)(2,1)S(1)}, u32[]{:S(2)}, u32[]{:S(2)}) collective-permute-start(bf16[256,768]{1,0:T(8,128)(2,1)} %get-tuple-element.27), channel_id=1, source_target_pairs={{0,6},{1,7},{2,4},{3,5},{4,10},{5,11},{6,8},{7,9},{8,14},{9,15},{1... | collective-permute-start | bytes 1179656 | tf_op jit(solution)/shard_map/ppermute | solution.py:49
  61.6 13.8 %copy-start.2 = (bf16[256,768]{1,0:T(8,128)(2,1)}, bf16[256,768]{1,0:T(8,128)(2,1)S(1)}, u32[]{:S(2)}) copy-start(bf16[256,768]{1,0:T(8,128)(2,1)S(1)} %get-tuple-element.49.refs_1_.refs_6_) | copy-start | bytes 1179652
  61.7 11.9 %collective-permute-start.7 = (bf16[256,768]{1,0:T(8,128)(2,1)S(1)}, bf16[256,768]{1,0:T(8,128)(2,1)S(1)}, u32[]{:S(2)}, u32[]{:S(2)}) collective-permute-start(bf16[256,768]{1,0:T(8,128)(2,1)S(1)} %get-tuple-element.50), channel_id=1, source_target_pairs={{0,2},{1,3},{2,0},{3,1},{16,18},{17,19},{18,16},{19,17}} | collective-permute-start | bytes 1179656 | tf_op jit(solution)/shard_map/ppermute | solution.py:32
  65.6 8.2 %collective-permute-start.9 = (bf16[256,768]{1,0:T(8,128)(2,1)S(1)}, bf16[256,768]{1,0:T(8,128)(2,1)S(1)}, u32[]{:S(2)}, u32[]{:S(2)}) collective-permute-start(bf16[256,768]{1,0:T(8,128)(2,1)S(1)} %get-tuple-element.49.refs_1_.refs_6_), channel_id=1, source_target_pairs={{0,1},{1,0},{2,3},{3,2},{4,5},{5,4},{6,7},{7,6},{8,9},{9,8},{10,11... | collective-permute-start | bytes 1179656 | tf_op jit(solution)/shard_map/ppermute | solution.py:42
  73.6 1.8 copy-start.6
  73.6 1.8 collective-permute-start.10
  73.7 1.7 copy-start.9
  88.7 8.6 %collective-permute-start.11 = (bf16[256,512]{1,0:T(8,128)(2,1)}, bf16[256,512]{1,0:T(8,128)(2,1)S(1)}, u32[]{:S(2)}, u32[]{:S(2)}) collective-permute-start(bf16[256,512]{1,0:T(8,128)(2,1)} %get-tuple-element.30.refs_1_), channel_id=1, source_target_pairs={{0,2},{1,3},{2,0},{3,1},{4,6},{5,7},{6,4},{7,5},{8,10},{9,11},{10,... | collective-permute-start | bytes 786440 | tf_op jit(solution)/shard_map/ppermute | solution.py:24
  90.2 7.1 %collective-permute-start.12 = (bf16[256,512]{1,0:T(8,128)(2,1)}, bf16[256,512]{1,0:T(8,128)(2,1)S(1)}, u32[]{:S(2)}, u32[]{:S(2)}) collective-permute-start(bf16[256,512]{1,0:T(8,128)(2,1)} %get-tuple-element.30.refs_1_), channel_id=1, source_target_pairs={{0,1},{1,0},{2,3},{3,2},{4,5},{5,4},{6,7},{7,6},{8,9},{9,8},{10,11... | collective-permute-start | bytes 786440 | tf_op jit(solution)/shard_map/ppermute | solution.py:42
  97.3 1.5 copy-start.18
  97.3 1.5 collective-permute-start.13
  104.4 11.0 %collective-permute-start.14 = (bf16[256,768]{1,0:T(8,128)(2,1)}, bf16[256,768]{1,0:T(8,128)(2,1)S(1)}, u32[]{:S(2)}, u32[]{:S(2)}) collective-permute-start(bf16[256,768]{1,0:T(8,128)(2,1)} %get-tuple-element.32), channel_id=1, source_target_pairs={{0,4},{1,5},{2,6},{3,7},{4,8},{5,9},{6,10},{7,11},{8,12},{9,13},{1... | collective-permute-start | bytes 1179656 | tf_op jit(solution)/shard_map/ppermute | solution.py:49
  108.3 15.0 %collective-permute-start.16 = (bf16[256,768]{1,0:T(8,128)(2,1)}, bf16[256,768]{1,0:T(8,128)(2,1)S(1)}, u32[]{:S(2)}, u32[]{:S(2)}) collective-permute-start(bf16[256,768]{1,0:T(8,128)(2,1)} %get-tuple-element.32), channel_id=1, source_target_pairs={{0,6},{1,7},{2,4},{3,5},{4,10},{5,11},{6,8},{7,9},{8,14},{9,15},{1... | collective-permute-start | bytes 1179656 | tf_op jit(solution)/shard_map/ppermute | solution.py:49
  115.6 13.9 %copy-start.3 = (bf16[256,768]{1,0:T(8,128)(2,1)}, bf16[256,768]{1,0:T(8,128)(2,1)S(1)}, u32[]{:S(2)}) copy-start(bf16[256,768]{1,0:T(8,128)(2,1)S(1)} %get-tuple-element.47.refs_1_.refs_6_) | copy-start | bytes 1179652
  115.7 12.1 %collective-permute-start.15 = (bf16[256,768]{1,0:T(8,128)(2,1)S(1)}, bf16[256,768]{1,0:T(8,128)(2,1)S(1)}, u32[]{:S(2)}, u32[]{:S(2)}) collective-permute-start(bf16[256,768]{1,0:T(8,128)(2,1)S(1)} %get-tuple-element.48), channel_id=1, source_target_pairs={{0,2},{1,3},{2,0},{3,1},{16,18},{17,19},{18,16},{19,17}} | collective-permute-start | bytes 1179656 | tf_op jit(solution)/shard_map/ppermute | solution.py:32
  119.2 8.6 %collective-permute-start.17 = (bf16[256,768]{1,0:T(8,128)(2,1)S(1)}, bf16[256,768]{1,0:T(8,128)(2,1)S(1)}, u32[]{:S(2)}, u32[]{:S(2)}) collective-permute-start(bf16[256,768]{1,0:T(8,128)(2,1)S(1)} %get-tuple-element.47.refs_1_.refs_6_), channel_id=1, source_target_pairs={{0,1},{1,0},{2,3},{3,2},{4,5},{5,4},{6,7},{7,6},{8,9},{9,8},{10,11... | collective-permute-start | bytes 1179656 | tf_op jit(solution)/shard_map/ppermute | solution.py:42
  127.8 1.8 copy-start.7
  127.8 1.8 collective-permute-start.18
  127.9 1.7 copy-start.10
  142.8 8.6 %collective-permute-start.19 = (bf16[256,512]{1,0:T(8,128)(2,1)}, bf16[256,512]{1,0:T(8,128)(2,1)S(1)}, u32[]{:S(2)}, u32[]{:S(2)}) collective-permute-start(bf16[256,512]{1,0:T(8,128)(2,1)} %get-tuple-element.35.refs_1_), channel_id=1, source_target_pairs={{0,2},{1,3},{2,0},{3,1},{4,6},{5,7},{6,4},{7,5},{8,10},{9,11},{10,... | collective-permute-start | bytes 786440 | tf_op jit(solution)/shard_map/ppermute | solution.py:24
  144.3 7.1 %collective-permute-start.20 = (bf16[256,512]{1,0:T(8,128)(2,1)}, bf16[256,512]{1,0:T(8,128)(2,1)S(1)}, u32[]{:S(2)}, u32[]{:S(2)}) collective-permute-start(bf16[256,512]{1,0:T(8,128)(2,1)} %get-tuple-element.35.refs_1_), channel_id=1, source_target_pairs={{0,1},{1,0},{2,3},{3,2},{4,5},{5,4},{6,7},{7,6},{8,9},{9,8},{10,11... | collective-permute-start | bytes 786440 | tf_op jit(solution)/shard_map/ppermute | solution.py:42
  151.4 1.5 copy-start.19
  151.4 1.5 collective-permute-start.21
  158.5 11.0 %collective-permute-start.22 = (bf16[256,768]{1,0:T(8,128)(2,1)}, bf16[256,768]{1,0:T(8,128)(2,1)S(1)}, u32[]{:S(2)}, u32[]{:S(2)}) collective-permute-start(bf16[256,768]{1,0:T(8,128)(2,1)} %get-tuple-element.37), channel_id=1, source_target_pairs={{0,4},{1,5},{2,6},{3,7},{4,8},{5,9},{6,10},{7,11},{8,12},{9,13},{1... | collective-permute-start | bytes 1179656 | tf_op jit(solution)/shard_map/ppermute | solution.py:49
  162.6 14.9 %collective-permute-start.24 = (bf16[256,768]{1,0:T(8,128)(2,1)}, bf16[256,768]{1,0:T(8,128)(2,1)S(1)}, u32[]{:S(2)}, u32[]{:S(2)}) collective-permute-start(bf16[256,768]{1,0:T(8,128)(2,1)} %get-tuple-element.37), channel_id=1, source_target_pairs={{0,6},{1,7},{2,4},{3,5},{4,10},{5,11},{6,8},{7,9},{8,14},{9,15},{1... | collective-permute-start | bytes 1179656 | tf_op jit(solution)/shard_map/ppermute | solution.py:49
  169.8 13.9 %copy-start.1 = (bf16[256,768]{1,0:T(8,128)(2,1)}, bf16[256,768]{1,0:T(8,128)(2,1)S(1)}, u32[]{:S(2)}) copy-start(bf16[256,768]{1,0:T(8,128)(2,1)S(1)} %get-tuple-element.45.refs_1_.refs_6_) | copy-start | bytes 1179652
  169.8 12.1 %collective-permute-start.23 = (bf16[256,768]{1,0:T(8,128)(2,1)S(1)}, bf16[256,768]{1,0:T(8,128)(2,1)S(1)}, u32[]{:S(2)}, u32[]{:S(2)}) collective-permute-start(bf16[256,768]{1,0:T(8,128)(2,1)S(1)} %get-tuple-element.46), channel_id=1, source_target_pairs={{0,2},{1,3},{2,0},{3,1},{16,18},{17,19},{18,16},{19,17}} | collective-permute-start | bytes 1179656 | tf_op jit(solution)/shard_map/ppermute | solution.py:32
  173.2 8.8 %collective-permute-start.25 = (bf16[256,768]{1,0:T(8,128)(2,1)S(1)}, bf16[256,768]{1,0:T(8,128)(2,1)S(1)}, u32[]{:S(2)}, u32[]{:S(2)}) collective-permute-start(bf16[256,768]{1,0:T(8,128)(2,1)S(1)} %get-tuple-element.45.refs_1_.refs_6_), channel_id=1, source_target_pairs={{0,1},{1,0},{2,3},{3,2},{4,5},{5,4},{6,7},{7,6},{8,9},{9,8},{10,11... | collective-permute-start | bytes 1179656 | tf_op jit(solution)/shard_map/ppermute | solution.py:42
  181.9 1.8 copy-start.5
  181.9 1.8 collective-permute-start.26
  182.0 1.7 copy-start.8
  197.0 8.5 %collective-permute-start.27 = (bf16[256,512]{1,0:T(8,128)(2,1)}, bf16[256,512]{1,0:T(8,128)(2,1)S(1)}, u32[]{:S(2)}, u32[]{:S(2)}) collective-permute-start(bf16[256,512]{1,0:T(8,128)(2,1)} %get-tuple-element.40.refs_1_), channel_id=1, source_target_pairs={{0,2},{1,3},{2,0},{3,1},{4,6},{5,7},{6,4},{7,5},{8,10},{9,11},{10,... | collective-permute-start | bytes 786440 | tf_op jit(solution)/shard_map/ppermute | solution.py:24
  198.5 7.1 %collective-permute-start.28 = (bf16[256,512]{1,0:T(8,128)(2,1)}, bf16[256,512]{1,0:T(8,128)(2,1)S(1)}, u32[]{:S(2)}, u32[]{:S(2)}) collective-permute-start(bf16[256,512]{1,0:T(8,128)(2,1)} %get-tuple-element.40.refs_1_), channel_id=1, source_target_pairs={{0,1},{1,0},{2,3},{3,2},{4,5},{5,4},{6,7},{7,6},{8,9},{9,8},{10,11... | collective-permute-start | bytes 786440 | tf_op jit(solution)/shard_map/ppermute | solution.py:42
  205.5 1.5 copy-start.20
  205.5 1.5 collective-permute-start.29
  (12 other events, 12.0 us)

commit v13 on v9

--- a/solution.py
+++ b/solution.py
@@ -79,21 +79,29 @@
 
 def block_kernel(*refs):
     where_ref = refs[0]
-    count = len(refs) - 9
+    count = len(refs) - 11
     part_refs = refs[1 : 1 + count]
     scale_ref, weights_ref, keys_ref, values_ref = refs[1 + count : 5 + count]
     heads_ref, keys_out, values_out = refs[5 + count : 8 + count]
-    shaped_ref = refs[8 + count]
+    shaped_ref, landed_ref, arrived = refs[8 + count :]
     start = where_ref[0]
     patch_count = where_ref[1]
     head_dim = keys_ref.shape[2]
     seq_len = keys_ref.shape[1]
-    span, width = part_refs[0].shape
+    span, width = landed_ref.shape[1:]
     features = width * count
 
     @pl.when(pl.program_id(0) == 0)
     def _():
-        parts = [part[...].astype(jnp.float32) for part in part_refs]
+        copies = [
+            pltpu.make_async_copy(part_refs[part], landed_ref.at[part], arrived.at[part])
+            for part in range(count)
+        ]
+        for copy in copies:
+            copy.start()
+        for copy in copies:
+            copy.wait()
+        parts = [landed_ref[part].astype(jnp.float32) for part in range(count)]
         row_mean = sum(jnp.sum(part, axis=-1, keepdims=True) for part in parts) / features
         centred = [part - row_mean for part in parts]
         spread = sum(jnp.sum(c * c, axis=-1, keepdims=True) for c in centred) / features
@@ -148,7 +156,7 @@
     grid_spec = pltpu.PrefetchScalarGridSpec(
         num_scalar_prefetch=1,
         grid=(heads_here,),
-        in_specs=[whole((span, width)) for _ in parts]
+        in_specs=[pl.BlockSpec(memory_space=pl.ANY) for _ in parts]
         + [
             whole((count, 2, width)),
             pl.BlockSpec((features, 3 * head_dim), lambda h, where: (0, h)),
@@ -160,7 +168,11 @@
             cache_spec,
             cache_spec,
         ],
-        scratch_shapes=[pltpu.VMEM((count, span, width), jnp.bfloat16)],
+        scratch_shapes=[
+            pltpu.VMEM((count, span, width), jnp.bfloat16),
+            pltpu.VMEM((count, span, width), jnp.bfloat16),
+            pltpu.SemaphoreType.DMA((count,)),
+        ],
     )
     return pl.pallas_call(
         block_kernel,
@@ -177,14 +189,22 @@
 
 def exit_kernel(*refs):
     where_ref = refs[0]
-    count = len(refs) - 5
+    count = len(refs) - 7
     part_refs = refs[1 : 1 + count]
     weights_ref, own_ref, gate_ref = refs[1 + count : 4 + count]
-    out_ref = refs[4 + count]
+    out_ref, landed_ref, arrived = refs[4 + count :]
     patch_count = where_ref[1]
+    copies = [
+        pltpu.make_async_copy(part_refs[part], landed_ref.at[part], arrived.at[part])
+        for part in range(count)
+    ]
+    for copy in copies:
+        copy.start()
+    for copy in copies:
+        copy.wait()
     projected = sum(
         jnp.dot(
-            part_refs[part][...],
+            landed_ref[part],
             weights_ref[where_ref[2 + part]],
             preferred_element_type=jnp.float32,
         )
@@ -202,9 +222,13 @@
     smem = pl.BlockSpec(memory_space=pltpu.SMEM)
     return pl.pallas_call(
         exit_kernel,
-        in_specs=[smem] + [vmem] * (count + 3),
+        in_specs=[smem] + [pl.BlockSpec(memory_space=pl.ANY)] * count + [vmem] * 3,
         out_specs=vmem,
         out_shape=jax.ShapeDtypeStruct(own_rows.shape, own_rows.dtype),
+        scratch_shapes=[
+            pltpu.VMEM((count, span, head_width), parts[0].dtype),
+            pltpu.SemaphoreType.DMA((count,)),
+        ],
     )(
         where,
         *parts,

time: 212 us -> 220 us (1.038)
  Pallas kernels: 66.6 us -> 74 us
    pallas_call x4, Pallas kernels: 50.1 us -> 53.8 us  [attend_block(): pl.pallas_call(block_kernel, grid_spec=grid_spec, out_shape=[jax.ShapeDty...]
    pallas_call x4, Pallas kernels: 16.5 us -> 20.1 us  [leave_block(): pl.pallas_call(exit_kernel, in_specs=[smem] + [pl.BlockSpec(memory_space=...]
where the time goes in v13:
time: 220 us; the launch traced here: 219 us
  waiting for transfers between devices  83.7 us (38%)
  Pallas kernels  74 us (34%)
  starting transfers between devices  37.4 us (17%)
  other arithmetic  9.95 us (5%)
  local copies, waits for them, and re-layouts  7.81 us (4%)
  between operations  6.35 us (3%)
    pallas_call x4, Pallas kernels, attend_block(): pl.pallas_call(block_kernel, grid_spec=grid_spec, out_shape=[jax.ShapeDty...  53.8 us
    ppermute x5, waiting for transfers between devices, across_chips(): lax.ppermute(block, 'seq', [(source, (source + step) % count) for source...  37.2 us
    ppermute x6, waiting for transfers between devices, to_next_section(): lax.ppermute(block, ('section', 'seq'), [(section * count + source, (sect...  21.5 us
    pallas_call x4, Pallas kernels, leave_block(): pl.pallas_call(exit_kernel, in_specs=[smem] + [pl.BlockSpec(memory_space=...  20.1 us
    ppermute x6, starting transfers between devices, to_next_section(): lax.ppermute(block, ('section', 'seq'), [(section * count + source, (sect...  16.7 us
    ppermute x3, waiting for transfers between devices, across_chips_first_section(): lax.ppermute(block, ('section', 'seq'), [(source, (source + step) % count...  12.8 us
    ppermute x16, waiting for transfers between devices, with_partner(): return parts + [lax.ppermute(part, 'seq', to_partner) for part in parts]  12.2 us
    ppermute x3, starting transfers between devices, across_chips_first_section(): lax.ppermute(block, ('section', 'seq'), [(source, (source + step) % count...  10.7 us
  transfers between devices with their start and end apart: 30, of which 22 were waited for; matrix products, arithmetic and copies ran while one was open for 2% of the time, Pallas kernels for 0%

profile of v13, /device:TPU:0, one launch (start us, length us, event | category | flops | bytes accessed | tf_op | source)
XLA Modules:
  0.0 219.1 jit_solution(16669583934698323267)
XLA Ops:
  0.1 0.8 reduce-window.9
  0.9 1.3 bitcast_subtract_fusion
  3.7 1.2 fusion.3.refs_1_.refs_6_
  4.9 3.0 %collective-permute-start = (bf16[256,768]{1,0:T(8,128)(2,1)S(1)}, bf16[256,768]{1,0:T(8,128)(2,1)S(1)}, u32[]{:S(2)}, u32[]{:S(2)}) collective-permute-start(bf16[256,768]{1,0:T(8,128)(2,1)S(1)} %fusion.3.refs_1_.refs_6_), channel_id=1, source_target_pairs={{0,2},{1,3},{2,0},{3,1},{4,6},{5,7},{6,4},{7,5},{8,10},{9,11},{10,... | collective-permute-start | bytes 1179656 | tf_op jit(solution)/shard_map/ppermute | solution.py:22
  7.9 9.1 %collective-permute-done.refs_2_ = bf16[256,768]{1,0:T(8,128)(2,1)S(1)} collective-permute-done((bf16[256,768]{1,0:T(8,128)(2,1)S(1)}, bf16[256,768]{1,0:T(8,128)(2,1)S(1)}, u32[]{:S(2)}, u32[]{:S(2)}) %collective-permute-start) | collective-permute-done | bytes 393248 | tf_op jit(solution)/shard_map/ppermute | solution.py:22
  17.7 1.1 collective-permute-done.2.refs_4_
  19.6 13.5 %shard_map.91 = (bf16[256,512]{1,0:T(8,128)(2,1)}, bf16[4,768,128]{2,1,0:T(8,128)(2,1)}, bf16[4,768,128]{2,1,0:T(8,128)(2,1)}) custom-call(s32[6]{0:T(128)} %get-tuple-element.37.refs_0_, bf16[256,768]{1,0:T(8,128)(2,1)} %copy-done.4, bf16[256,768]{1,0:T(8,128)(2,1)} %copy-done.12, bf16[256,768]{1,0:T(8,128)(2,1)} %copy-done.15, ...), custom_call_target="tpu_custom_call" | custom-call | tf_op jit(solution)/shard_map/pallas_call | solution.py:177
  33.0 1.8 collective-permute-start.3
  34.8 6.8 %collective-permute-done.3.refs_2_ = bf16[256,512]{1,0:T(8,128)(2,1)S(1)} collective-permute-done((bf16[256,512]{1,0:T(8,128)(2,1)}, bf16[256,512]{1,0:T(8,128)(2,1)S(1)}, u32[]{:S(2)}, u32[]{:S(2)}) %collective-permute-start.3) | collective-permute-done | bytes 262176 | tf_op jit(solution)/shard_map/ppermute | solution.py:22
  41.7 1.5 collective-permute-done.5.refs_4_
  43.9 5.1 %shard_map.92 = bf16[256,768]{1,0:T(8,128)(2,1)} custom-call(s32[6]{0:T(128)} %get-tuple-element.37.refs_0_, bf16[256,512]{1,0:T(8,128)(2,1)} %get-tuple-element.19.refs_1_, bf16[256,512]{1,0:T(8,128)(2,1)} %copy-done.20, bf16[256,512]{1,0:T(8,128)(2,1)} %copy-done.24, bf16[256,512]{1,0:T(8,128)(2,1)} %copy-done.28, bf16[4,512,768]{2,1,0:T(8,128)(2,1)} %bitcast.40, ...), custom_call_target="tpu_custom_call" | custom-call | tf_op jit(solution)/shard_map/pallas_call | solution.py:223
  49.0 3.7 %collective-permute-start.6 = (bf16[256,768]{1,0:T(8,128)(2,1)}, bf16[256,768]{1,0:T(8,128)(2,1)S(1)}, u32[]{:S(2)}, u32[]{:S(2)}) collective-permute-start(bf16[256,768]{1,0:T(8,128)(2,1)} %shard_map.92), channel_id=1, source_target_pairs={{0,4},{1,5},{2,6},{3,7},{4,8},{5,9},{6,10},{7,11},{8,12},{9,13},{1... | collective-permute-start | bytes 1179656 | tf_op jit(solution)/shard_map/ppermute | solution.py:47
  56.5 4.4 %collective-permute-start.8 = (bf16[256,768]{1,0:T(8,128)(2,1)}, bf16[256,768]{1,0:T(8,128)(2,1)S(1)}, u32[]{:S(2)}, u32[]{:S(2)}) collective-permute-start(bf16[256,768]{1,0:T(8,128)(2,1)} %shard_map.92), channel_id=1, source_target_pairs={{0,6},{1,7},{2,4},{3,5},{4,10},{5,11},{6,8},{7,9},{8,14},{9,15},{1... | collective-permute-start | bytes 1179656 | tf_op jit(solution)/shard_map/ppermute | solution.py:47
  61.0 1.1 collective-permute-done.6
  62.4 3.8 %collective-permute-start.7 = (bf16[256,768]{1,0:T(8,128)(2,1)S(1)}, bf16[256,768]{1,0:T(8,128)(2,1)S(1)}, u32[]{:S(2)}, u32[]{:S(2)}) collective-permute-start(bf16[256,768]{1,0:T(8,128)(2,1)S(1)} %get-tuple-element.36), channel_id=1, source_target_pairs={{0,2},{1,3},{2,0},{3,1},{16,18},{17,19},{18,16},{19,17}} | collective-permute-start | bytes 1179656 | tf_op jit(solution)/shard_map/ppermute | solution.py:30
  66.2 3.9 %collective-permute-done.8 = bf16[256,768]{1,0:T(8,128)(2,1)S(1)} collective-permute-done((bf16[256,768]{1,0:T(8,128)(2,1)}, bf16[256,768]{1,0:T(8,128)(2,1)S(1)}, u32[]{:S(2)}, u32[]{:S(2)}) %collective-permute-start.8) | collective-permute-done | bytes 393248 | tf_op jit(solution)/shard_map/ppermute | solution.py:47
  70.1 4.0 %collective-permute-done.7 = bf16[256,768]{1,0:T(8,128)(2,1)S(1)} collective-permute-done((bf16[256,768]{1,0:T(8,128)(2,1)S(1)}, bf16[256,768]{1,0:T(8,128)(2,1)S(1)}, u32[]{:S(2)}, u32[]{:S(2)}) %collective-permute-start.7) | collective-permute-done | bytes 393248 | tf_op jit(solution)/shard_map/ppermute | solution.py:30
  74.3 1.7 collective-permute-done.10.refs_4_
  76.8 13.5 %shard_map.93 = (bf16[256,512]{1,0:T(8,128)(2,1)}, bf16[4,768,128]{2,1,0:T(8,128)(2,1)}, bf16[4,768,128]{2,1,0:T(8,128)(2,1)}) custom-call(s32[6]{0:T(128)} %get-tuple-element.40.refs_0_, bf16[256,768]{1,0:T(8,128)(2,1)} %copy-done.2, bf16[256,768]{1,0:T(8,128)(2,1)} %copy-done.6, ...), custom_call_target="tpu_custom_call", output_to_operand_aliasing={{1}: (7, {}), {2}: (8, {})} | custom-call | tf_op jit(solution)/shard_map/pallas_call | solution.py:177
  90.2 1.6 collective-permute-start.11
  91.8 7.1 %collective-permute-done.11.refs_2_ = bf16[256,512]{1,0:T(8,128)(2,1)S(1)} collective-permute-done((bf16[256,512]{1,0:T(8,128)(2,1)}, bf16[256,512]{1,0:T(8,128)(2,1)S(1)}, u32[]{:S(2)}, u32[]{:S(2)}) %collective-permute-start.11) | collective-permute-done | bytes 262176 | tf_op jit(solution)/shard_map/ppermute | solution.py:22
  98.9 1.5 collective-permute-done.13.refs_4_
  101.1 5.0 %shard_map.94 = bf16[256,768]{1,0:T(8,128)(2,1)} custom-call(s32[6]{0:T(128)} %get-tuple-element.40.refs_0_, bf16[256,512]{1,0:T(8,128)(2,1)} %get-tuple-element.22.refs_1_, bf16[256,512]{1,0:T(8,128)(2,1)} %copy-done.21, bf16[256,512]{1,0:T(8,128)(2,1)} %copy-done.25, bf16[256,512]{1,0:T(8,128)(2,1)} %copy-done.29, bf16[4,512,768]{2,1,0:T(8,128)(2,1)} %bitcast.41, ...), custom_call_target="tpu_custom_call" | custom-call | tf_op jit(solution)/shard_map/pallas_call | solution.py:223
  106.1 1.3 collective-permute-start.14
  110.2 3.3 %collective-permute-start.16 = (bf16[256,768]{1,0:T(8,128)(2,1)}, bf16[256,768]{1,0:T(8,128)(2,1)S(1)}, u32[]{:S(2)}, u32[]{:S(2)}) collective-permute-start(bf16[256,768]{1,0:T(8,128)(2,1)} %shard_map.94), channel_id=1, source_target_pairs={{0,6},{1,7},{2,4},{3,5},{4,10},{5,11},{6,8},{7,9},{8,14},{9,15},{1... | collective-permute-start | bytes 1179656 | tf_op jit(solution)/shard_map/ppermute | solution.py:47
  113.5 3.7 %collective-permute-done.14 = bf16[256,768]{1,0:T(8,128)(2,1)S(1)} collective-permute-done((bf16[256,768]{1,0:T(8,128)(2,1)}, bf16[256,768]{1,0:T(8,128)(2,1)S(1)}, u32[]{:S(2)}, u32[]{:S(2)}) %collective-permute-start.14) | collective-permute-done | bytes 393248 | tf_op jit(solution)/shard_map/ppermute | solution.py:47
  117.4 3.6 %collective-permute-start.15 = (bf16[256,768]{1,0:T(8,128)(2,1)S(1)}, bf16[256,768]{1,0:T(8,128)(2,1)S(1)}, u32[]{:S(2)}, u32[]{:S(2)}) collective-permute-start(bf16[256,768]{1,0:T(8,128)(2,1)S(1)} %get-tuple-element.34), channel_id=1, source_target_pairs={{0,2},{1,3},{2,0},{3,1},{16,18},{17,19},{18,16},{19,17}} | collective-permute-start | bytes 1179656 | tf_op jit(solution)/shard_map/ppermute | solution.py:30
  121.1 4.0 %collective-permute-done.16 = bf16[256,768]{1,0:T(8,128)(2,1)S(1)} collective-permute-done((bf16[256,768]{1,0:T(8,128)(2,1)}, bf16[256,768]{1,0:T(8,128)(2,1)S(1)}, u32[]{:S(2)}, u32[]{:S(2)}) %collective-permute-start.16) | collective-permute-done | bytes 393248 | tf_op jit(solution)/shard_map/ppermute | solution.py:47
  125.1 4.4 %collective-permute-done.15 = bf16[256,768]{1,0:T(8,128)(2,1)S(1)} collective-permute-done((bf16[256,768]{1,0:T(8,128)(2,1)S(1)}, bf16[256,768]{1,0:T(8,128)(2,1)S(1)}, u32[]{:S(2)}, u32[]{:S(2)}) %collective-permute-start.15) | collective-permute-done | bytes 393248 | tf_op jit(solution)/shard_map/ppermute | solution.py:30
  129.6 1.7 collective-permute-done.18.refs_4_
  132.1 13.5 %shard_map.95 = (bf16[256,512]{1,0:T(8,128)(2,1)}, bf16[4,768,128]{2,1,0:T(8,128)(2,1)}, bf16[4,768,128]{2,1,0:T(8,128)(2,1)}) custom-call(s32[6]{0:T(128)} %get-tuple-element.39.refs_0_, bf16[256,768]{1,0:T(8,128)(2,1)} %copy-done.3, bf16[256,768]{1,0:T(8,128)(2,1)} %copy-done.7, ...), custom_call_target="tpu_custom_call", output_to_operand_aliasing={{1}: (7, {}), {2}: (8, {})} | custom-call | tf_op jit(solution)/shard_map/pallas_call | solution.py:177
  145.5 1.5 collective-permute-start.19
  147.1 7.1 %collective-permute-done.19.refs_2_ = bf16[256,512]{1,0:T(8,128)(2,1)S(1)} collective-permute-done((bf16[256,512]{1,0:T(8,128)(2,1)}, bf16[256,512]{1,0:T(8,128)(2,1)S(1)}, u32[]{:S(2)}, u32[]{:S(2)}) %collective-permute-start.19) | collective-permute-done | bytes 262176 | tf_op jit(solution)/shard_map/ppermute | solution.py:22
  154.2 1.5 collective-permute-done.21.refs_4_
  156.4 5.0 %shard_map.96 = bf16[256,768]{1,0:T(8,128)(2,1)} custom-call(s32[6]{0:T(128)} %get-tuple-element.39.refs_0_, bf16[256,512]{1,0:T(8,128)(2,1)} %get-tuple-element.25.refs_1_, bf16[256,512]{1,0:T(8,128)(2,1)} %copy-done.22, bf16[256,512]{1,0:T(8,128)(2,1)} %copy-done.26, bf16[256,512]{1,0:T(8,128)(2,1)} %copy-done.30, bf16[4,512,768]{2,1,0:T(8,128)(2,1)} %bitcast.42, ...), custom_call_target="tpu_custom_call" | custom-call | tf_op jit(solution)/shard_map/pallas_call | solution.py:223
  161.4 1.3 collective-permute-start.22
  165.3 2.6 %collective-permute-start.24 = (bf16[256,768]{1,0:T(8,128)(2,1)}, bf16[256,768]{1,0:T(8,128)(2,1)S(1)}, u32[]{:S(2)}, u32[]{:S(2)}) collective-permute-start(bf16[256,768]{1,0:T(8,128)(2,1)} %shard_map.96), channel_id=1, source_target_pairs={{0,6},{1,7},{2,4},{3,5},{4,10},{5,11},{6,8},{7,9},{8,14},{9,15},{1... | collective-permute-start | bytes 1179656 | tf_op jit(solution)/shard_map/ppermute | solution.py:47
  167.9 4.6 %collective-permute-done.22 = bf16[256,768]{1,0:T(8,128)(2,1)S(1)} collective-permute-done((bf16[256,768]{1,0:T(8,128)(2,1)}, bf16[256,768]{1,0:T(8,128)(2,1)S(1)}, u32[]{:S(2)}, u32[]{:S(2)}) %collective-permute-start.22) | collective-permute-done | bytes 393248 | tf_op jit(solution)/shard_map/ppermute | solution.py:47
  172.7 3.4 %collective-permute-start.23 = (bf16[256,768]{1,0:T(8,128)(2,1)S(1)}, bf16[256,768]{1,0:T(8,128)(2,1)S(1)}, u32[]{:S(2)}, u32[]{:S(2)}) collective-permute-start(bf16[256,768]{1,0:T(8,128)(2,1)S(1)} %get-tuple-element.32), channel_id=1, source_target_pairs={{0,2},{1,3},{2,0},{3,1},{16,18},{17,19},{18,16},{19,17}} | collective-permute-start | bytes 1179656 | tf_op jit(solution)/shard_map/ppermute | solution.py:30
  176.2 4.2 %collective-permute-done.24 = bf16[256,768]{1,0:T(8,128)(2,1)S(1)} collective-permute-done((bf16[256,768]{1,0:T(8,128)(2,1)}, bf16[256,768]{1,0:T(8,128)(2,1)S(1)}, u32[]{:S(2)}, u32[]{:S(2)}) %collective-permute-start.24) | collective-permute-done | bytes 393248 | tf_op jit(solution)/shard_map/ppermute | solution.py:47
  180.4 4.4 %collective-permute-done.23 = bf16[256,768]{1,0:T(8,128)(2,1)S(1)} collective-permute-done((bf16[256,768]{1,0:T(8,128)(2,1)S(1)}, bf16[256,768]{1,0:T(8,128)(2,1)S(1)}, u32[]{:S(2)}, u32[]{:S(2)}) %collective-permute-start.23) | collective-permute-done | bytes 393248 | tf_op jit(solution)/shard_map/ppermute | solution.py:30
  184.9 1.7 collective-permute-done.26.refs_4_
  187.4 13.5 %shard_map.97 = (bf16[256,512]{1,0:T(8,128)(2,1)}, bf16[4,768,128]{2,1,0:T(8,128)(2,1)}, bf16[4,768,128]{2,1,0:T(8,128)(2,1)}) custom-call(s32[6]{0:T(128)} %get-tuple-element.38.refs_0_, bf16[256,768]{1,0:T(8,128)(2,1)} %copy-done.1, bf16[256,768]{1,0:T(8,128)(2,1)} %copy-done.5, ...), custom_call_target="tpu_custom_call", output_to_operand_aliasing={{1}: (7, {}), {2}: (8, {})} | custom-call | tf_op jit(solution)/shard_map/pallas_call | solution.py:177
  200.9 1.5 collective-permute-start.27
  202.4 7.1 %collective-permute-done.27.refs_2_ = bf16[256,512]{1,0:T(8,128)(2,1)S(1)} collective-permute-done((bf16[256,512]{1,0:T(8,128)(2,1)}, bf16[256,512]{1,0:T(8,128)(2,1)S(1)}, u32[]{:S(2)}, u32[]{:S(2)}) %collective-permute-start.27) | collective-permute-done | bytes 262176 | tf_op jit(solution)/shard_map/ppermute | solution.py:22
  209.5 1.5 collective-permute-done.29.refs_4_
  211.7 5.0 %shard_map.98 = bf16[256,768]{1,0:T(8,128)(2,1)} custom-call(s32[6]{0:T(128)} %get-tuple-element.38.refs_0_, bf16[256,512]{1,0:T(8,128)(2,1)} %get-tuple-element.28.refs_1_, bf16[256,512]{1,0:T(8,128)(2,1)} %copy-done.23, bf16[256,512]{1,0:T(8,128)(2,1)} %copy-done.27, bf16[256,512]{1,0:T(8,128)(2,1)} %copy-done.31, bf16[4,512,768]{2,1,0:T(8,128)(2,1)} %bitcast.43, ...), custom_call_target="tpu_custom_call" | custom-call | tf_op jit(solution)/shard_map/pallas_call | solution.py:223
  216.8 2.3 %maximum_bitcast_fusion = bf16[4,1,256,768]{3,2,1,0:T(8,128)(2,1)} fusion(bf16[1,256,768]{2,1,0:T(8,128)(2,1)} %bitcast.47, bf16[1,256,768]{2,1,0:T(8,128)(2,1)S(1)} %bitcast.46, bf16[1,256,768]{2,1,0:T(8,128)(2,1)S(1)} %bitcast.45, bf16[1,256,768]{2,1,0:T(8,128)(2,1)S(1)} %bitcast.44), kind=kLoop, calls=%fused_computation.3 | loop fusion | flops 2359296 | bytes 3145728 | tf_op jit(solution)/shard_map/broadcast_in_dim | solution.py:311
  (112 shorter events, 12.6 us)
Async XLA Ops:
  4.9 13.9 %copy-start.4 = (bf16[256,768]{1,0:T(8,128)(2,1)}, bf16[256,768]{1,0:T(8,128)(2,1)S(1)}, u32[]{:S(2)}) copy-start(bf16[256,768]{1,0:T(8,128)(2,1)S(1)} %fusion.3.refs_1_.refs_6_) | copy-start | bytes 1179652
  4.9 12.1 %collective-permute-start = (bf16[256,768]{1,0:T(8,128)(2,1)S(1)}, bf16[256,768]{1,0:T(8,128)(2,1)S(1)}, u32[]{:S(2)}, u32[]{:S(2)}) collective-permute-start(bf16[256,768]{1,0:T(8,128)(2,1)S(1)} %fusion.3.refs_1_.refs_6_), channel_id=1, source_target_pairs={{0,2},{1,3},{2,0},{3,1},{4,6},{5,7},{6,4},{7,5},{8,10},{9,11},{10,... | collective-permute-start | bytes 1179656 | tf_op jit(solution)/shard_map/ppermute | solution.py:22
  7.9 9.8 %collective-permute-start.1 = (bf16[256,768]{1,0:T(8,128)(2,1)S(1)}, bf16[256,768]{1,0:T(8,128)(2,1)S(1)}, u32[]{:S(2)}, u32[]{:S(2)}) collective-permute-start(bf16[256,768]{1,0:T(8,128)(2,1)S(1)} %fusion.3.refs_1_.refs_6_), channel_id=1, source_target_pairs={{0,1},{1,0},{2,3},{3,2},{4,5},{5,4},{6,7},{7,6},{8,9},{9,8},{10,11... | collective-permute-start | bytes 1179656 | tf_op jit(solution)/shard_map/ppermute | solution.py:40
  17.1 1.7 copy-start.12
  17.1 1.7 collective-permute-start.2
  33.0 8.6 %collective-permute-start.3 = (bf16[256,512]{1,0:T(8,128)(2,1)}, bf16[256,512]{1,0:T(8,128)(2,1)S(1)}, u32[]{:S(2)}, u32[]{:S(2)}) collective-permute-start(bf16[256,512]{1,0:T(8,128)(2,1)} %get-tuple-element.19.refs_1_), channel_id=1, source_target_pairs={{0,2},{1,3},{2,0},{3,1},{4,6},{5,7},{6,4},{7,5},{8,10},{9,11},{10,... | collective-permute-start | bytes 786440 | tf_op jit(solution)/shard_map/ppermute | solution.py:22
  34.8 6.8 %collective-permute-start.4 = (bf16[256,512]{1,0:T(8,128)(2,1)}, bf16[256,512]{1,0:T(8,128)(2,1)S(1)}, u32[]{:S(2)}, u32[]{:S(2)}) collective-permute-start(bf16[256,512]{1,0:T(8,128)(2,1)} %get-tuple-element.19.refs_1_), channel_id=1, source_target_pairs={{0,1},{1,0},{2,3},{3,2},{4,5},{5,4},{6,7},{7,6},{8,9},{9,8},{10,11... | collective-permute-start | bytes 786440 | tf_op jit(solution)/shard_map/ppermute | solution.py:40
  41.6 1.5 copy-start.20
  41.6 1.5 collective-permute-start.5
  43.9 11.4 %copy-start.32 = (s32[4]{0:T(128)S(1)}, s32[4]{0:T(128)}, u32[]{:S(2)}) copy-start(s32[4]{0:T(128)} %param.11) | copy-start | bytes 52
  43.9 18.2 %copy-start = (bf16[768,768]{1,0:T(8,128)(2,1)S(1)}, bf16[768,768]{1,0:T(8,128)(2,1)}, u32[]{:S(2)}) copy-start(bf16[768,768]{1,0:T(8,128)(2,1)} %param.9) | copy-start | bytes 3538948
  49.0 13.1 %collective-permute-start.6 = (bf16[256,768]{1,0:T(8,128)(2,1)}, bf16[256,768]{1,0:T(8,128)(2,1)S(1)}, u32[]{:S(2)}, u32[]{:S(2)}) collective-permute-start(bf16[256,768]{1,0:T(8,128)(2,1)} %shard_map.92), channel_id=1, source_target_pairs={{0,4},{1,5},{2,6},{3,7},{4,8},{5,9},{6,10},{7,11},{8,12},{9,13},{1... | collective-permute-start | bytes 1179656 | tf_op jit(solution)/shard_map/ppermute | solution.py:47
  56.5 13.6 %collective-permute-start.8 = (bf16[256,768]{1,0:T(8,128)(2,1)}, bf16[256,768]{1,0:T(8,128)(2,1)S(1)}, u32[]{:S(2)}, u32[]{:S(2)}) collective-permute-start(bf16[256,768]{1,0:T(8,128)(2,1)} %shard_map.92), channel_id=1, source_target_pairs={{0,6},{1,7},{2,4},{3,5},{4,10},{5,11},{6,8},{7,9},{8,14},{9,15},{1... | collective-permute-start | bytes 1179656 | tf_op jit(solution)/shard_map/ppermute | solution.py:47
  62.3 13.7 %copy-start.2 = (bf16[256,768]{1,0:T(8,128)(2,1)}, bf16[256,768]{1,0:T(8,128)(2,1)S(1)}, u32[]{:S(2)}) copy-start(bf16[256,768]{1,0:T(8,128)(2,1)S(1)} %get-tuple-element.35.refs_1_.refs_6_) | copy-start | bytes 1179652
  62.4 11.8 %collective-permute-start.7 = (bf16[256,768]{1,0:T(8,128)(2,1)S(1)}, bf16[256,768]{1,0:T(8,128)(2,1)S(1)}, u32[]{:S(2)}, u32[]{:S(2)}) collective-permute-start(bf16[256,768]{1,0:T(8,128)(2,1)S(1)} %get-tuple-element.36), channel_id=1, source_target_pairs={{0,2},{1,3},{2,0},{3,1},{16,18},{17,19},{18,16},{19,17}} | collective-permute-start | bytes 1179656 | tf_op jit(solution)/shard_map/ppermute | solution.py:30
  66.2 8.1 %collective-permute-start.9 = (bf16[256,768]{1,0:T(8,128)(2,1)S(1)}, bf16[256,768]{1,0:T(8,128)(2,1)S(1)}, u32[]{:S(2)}, u32[]{:S(2)}) collective-permute-start(bf16[256,768]{1,0:T(8,128)(2,1)S(1)} %get-tuple-element.35.refs_1_.refs_6_), channel_id=1, source_target_pairs={{0,1},{1,0},{2,3},{3,2},{4,5},{5,4},{6,7},{7,6},{8,9},{9,8},{10,11... | collective-permute-start | bytes 1179656 | tf_op jit(solution)/shard_map/ppermute | solution.py:40
  74.2 1.8 copy-start.6
  74.2 1.8 collective-permute-start.10
  74.3 1.7 copy-start.13
  90.2 8.6 %collective-permute-start.11 = (bf16[256,512]{1,0:T(8,128)(2,1)}, bf16[256,512]{1,0:T(8,128)(2,1)S(1)}, u32[]{:S(2)}, u32[]{:S(2)}) collective-permute-start(bf16[256,512]{1,0:T(8,128)(2,1)} %get-tuple-element.22.refs_1_), channel_id=1, source_target_pairs={{0,2},{1,3},{2,0},{3,1},{4,6},{5,7},{6,4},{7,5},{8,10},{9,11},{10,... | collective-permute-start | bytes 786440 | tf_op jit(solution)/shard_map/ppermute | solution.py:22
  91.8 7.1 %collective-permute-start.12 = (bf16[256,512]{1,0:T(8,128)(2,1)}, bf16[256,512]{1,0:T(8,128)(2,1)S(1)}, u32[]{:S(2)}, u32[]{:S(2)}) collective-permute-start(bf16[256,512]{1,0:T(8,128)(2,1)} %get-tuple-element.22.refs_1_), channel_id=1, source_target_pairs={{0,1},{1,0},{2,3},{3,2},{4,5},{5,4},{6,7},{7,6},{8,9},{9,8},{10,11... | collective-permute-start | bytes 786440 | tf_op jit(solution)/shard_map/ppermute | solution.py:40
  98.9 1.5 collective-permute-start.13
  106.1 11.0 %collective-permute-start.14 = (bf16[256,768]{1,0:T(8,128)(2,1)}, bf16[256,768]{1,0:T(8,128)(2,1)S(1)}, u32[]{:S(2)}, u32[]{:S(2)}) collective-permute-start(bf16[256,768]{1,0:T(8,128)(2,1)} %shard_map.94), channel_id=1, source_target_pairs={{0,4},{1,5},{2,6},{3,7},{4,8},{5,9},{6,10},{7,11},{8,12},{9,13},{1... | collective-permute-start | bytes 1179656 | tf_op jit(solution)/shard_map/ppermute | solution.py:47
  110.2 14.9 %collective-permute-start.16 = (bf16[256,768]{1,0:T(8,128)(2,1)}, bf16[256,768]{1,0:T(8,128)(2,1)S(1)}, u32[]{:S(2)}, u32[]{:S(2)}) collective-permute-start(bf16[256,768]{1,0:T(8,128)(2,1)} %shard_map.94), channel_id=1, source_target_pairs={{0,6},{1,7},{2,4},{3,5},{4,10},{5,11},{6,8},{7,9},{8,14},{9,15},{1... | collective-permute-start | bytes 1179656 | tf_op jit(solution)/shard_map/ppermute | solution.py:47
  117.4 13.9 %copy-start.3 = (bf16[256,768]{1,0:T(8,128)(2,1)}, bf16[256,768]{1,0:T(8,128)(2,1)S(1)}, u32[]{:S(2)}) copy-start(bf16[256,768]{1,0:T(8,128)(2,1)S(1)} %get-tuple-element.33.refs_1_.refs_6_) | copy-start | bytes 1179652
  117.4 12.1 %collective-permute-start.15 = (bf16[256,768]{1,0:T(8,128)(2,1)S(1)}, bf16[256,768]{1,0:T(8,128)(2,1)S(1)}, u32[]{:S(2)}, u32[]{:S(2)}) collective-permute-start(bf16[256,768]{1,0:T(8,128)(2,1)S(1)} %get-tuple-element.34), channel_id=1, source_target_pairs={{0,2},{1,3},{2,0},{3,1},{16,18},{17,19},{18,16},{19,17}} | collective-permute-start | bytes 1179656 | tf_op jit(solution)/shard_map/ppermute | solution.py:30
  121.0 8.6 %collective-permute-start.17 = (bf16[256,768]{1,0:T(8,128)(2,1)S(1)}, bf16[256,768]{1,0:T(8,128)(2,1)S(1)}, u32[]{:S(2)}, u32[]{:S(2)}) collective-permute-start(bf16[256,768]{1,0:T(8,128)(2,1)S(1)} %get-tuple-element.33.refs_1_.refs_6_), channel_id=1, source_target_pairs={{0,1},{1,0},{2,3},{3,2},{4,5},{5,4},{6,7},{7,6},{8,9},{9,8},{10,11... | collective-permute-start | bytes 1179656 | tf_op jit(solution)/shard_map/ppermute | solution.py:40
  129.5 1.8 copy-start.7
  129.5 1.8 collective-permute-start.18
  129.6 1.7 copy-start.14
  145.5 8.6 %collective-permute-start.19 = (bf16[256,512]{1,0:T(8,128)(2,1)}, bf16[256,512]{1,0:T(8,128)(2,1)S(1)}, u32[]{:S(2)}, u32[]{:S(2)}) collective-permute-start(bf16[256,512]{1,0:T(8,128)(2,1)} %get-tuple-element.25.refs_1_), channel_id=1, source_target_pairs={{0,2},{1,3},{2,0},{3,1},{4,6},{5,7},{6,4},{7,5},{8,10},{9,11},{10,... | collective-permute-start | bytes 786440 | tf_op jit(solution)/shard_map/ppermute | solution.py:22
  147.1 7.1 %collective-permute-start.20 = (bf16[256,512]{1,0:T(8,128)(2,1)}, bf16[256,512]{1,0:T(8,128)(2,1)S(1)}, u32[]{:S(2)}, u32[]{:S(2)}) collective-permute-start(bf16[256,512]{1,0:T(8,128)(2,1)} %get-tuple-element.25.refs_1_), channel_id=1, source_target_pairs={{0,1},{1,0},{2,3},{3,2},{4,5},{5,4},{6,7},{7,6},{8,9},{9,8},{10,11... | collective-permute-start | bytes 786440 | tf_op jit(solution)/shard_map/ppermute | solution.py:40
  154.2 1.5 copy-start.22
  154.2 1.5 collective-permute-start.21
  161.4 11.0 %collective-permute-start.22 = (bf16[256,768]{1,0:T(8,128)(2,1)}, bf16[256,768]{1,0:T(8,128)(2,1)S(1)}, u32[]{:S(2)}, u32[]{:S(2)}) collective-permute-start(bf16[256,768]{1,0:T(8,128)(2,1)} %shard_map.96), channel_id=1, source_target_pairs={{0,4},{1,5},{2,6},{3,7},{4,8},{5,9},{6,10},{7,11},{8,12},{9,13},{1... | collective-permute-start | bytes 1179656 | tf_op jit(solution)/shard_map/ppermute | solution.py:47
  165.3 15.1 %collective-permute-start.24 = (bf16[256,768]{1,0:T(8,128)(2,1)}, bf16[256,768]{1,0:T(8,128)(2,1)S(1)}, u32[]{:S(2)}, u32[]{:S(2)}) collective-permute-start(bf16[256,768]{1,0:T(8,128)(2,1)} %shard_map.96), channel_id=1, source_target_pairs={{0,6},{1,7},{2,4},{3,5},{4,10},{5,11},{6,8},{7,9},{8,14},{9,15},{1... | collective-permute-start | bytes 1179656 | tf_op jit(solution)/shard_map/ppermute | solution.py:47
  172.7 13.9 %copy-start.1 = (bf16[256,768]{1,0:T(8,128)(2,1)}, bf16[256,768]{1,0:T(8,128)(2,1)S(1)}, u32[]{:S(2)}) copy-start(bf16[256,768]{1,0:T(8,128)(2,1)S(1)} %get-tuple-element.31.refs_1_.refs_6_) | copy-start | bytes 1179652
  172.7 12.1 %collective-permute-start.23 = (bf16[256,768]{1,0:T(8,128)(2,1)S(1)}, bf16[256,768]{1,0:T(8,128)(2,1)S(1)}, u32[]{:S(2)}, u32[]{:S(2)}) collective-permute-start(bf16[256,768]{1,0:T(8,128)(2,1)S(1)} %get-tuple-element.32), channel_id=1, source_target_pairs={{0,2},{1,3},{2,0},{3,1},{16,18},{17,19},{18,16},{19,17}} | collective-permute-start | bytes 1179656 | tf_op jit(solution)/shard_map/ppermute | solution.py:30
  176.1 8.8 %collective-permute-start.25 = (bf16[256,768]{1,0:T(8,128)(2,1)S(1)}, bf16[256,768]{1,0:T(8,128)(2,1)S(1)}, u32[]{:S(2)}, u32[]{:S(2)}) collective-permute-start(bf16[256,768]{1,0:T(8,128)(2,1)S(1)} %get-tuple-element.31.refs_1_.refs_6_), channel_id=1, source_target_pairs={{0,1},{1,0},{2,3},{3,2},{4,5},{5,4},{6,7},{7,6},{8,9},{9,8},{10,11... | collective-permute-start | bytes 1179656 | tf_op jit(solution)/shard_map/ppermute | solution.py:40
  184.8 1.8 copy-start.5
  184.8 1.8 collective-permute-start.26
  184.9 1.7 copy-start.11
  200.8 15.9 %copy-start.8 = (bf16[256,768]{1,0:T(8,128)(2,1)S(1)}, bf16[256,768]{1,0:T(8,128)(2,1)}, u32[]{:S(2)}) copy-start(bf16[256,768]{1,0:T(8,128)(2,1)} %shard_map.92) | copy-start | bytes 1179652
  200.8 15.9 %copy-start.9 = (bf16[256,768]{1,0:T(8,128)(2,1)S(1)}, bf16[256,768]{1,0:T(8,128)(2,1)}, u32[]{:S(2)}) copy-start(bf16[256,768]{1,0:T(8,128)(2,1)} %shard_map.94) | copy-start | bytes 1179652
  200.9 15.9 %copy-start.10 = (bf16[256,768]{1,0:T(8,128)(2,1)S(1)}, bf16[256,768]{1,0:T(8,128)(2,1)}, u32[]{:S(2)}) copy-start(bf16[256,768]{1,0:T(8,128)(2,1)} %shard_map.96) | copy-start | bytes 1179652
  200.9 8.6 %collective-permute-start.27 = (bf16[256,512]{1,0:T(8,128)(2,1)}, bf16[256,512]{1,0:T(8,128)(2,1)S(1)}, u32[]{:S(2)}, u32[]{:S(2)}) collective-permute-start(bf16[256,512]{1,0:T(8,128)(2,1)} %get-tuple-element.28.refs_1_), channel_id=1, source_target_pairs={{0,2},{1,3},{2,0},{3,1},{4,6},{5,7},{6,4},{7,5},{8,10},{9,11},{10,... | collective-permute-start | bytes 786440 | tf_op jit(solution)/shard_map/ppermute | solution.py:22
  202.4 7.1 %collective-permute-start.28 = (bf16[256,512]{1,0:T(8,128)(2,1)}, bf16[256,512]{1,0:T(8,128)(2,1)S(1)}, u32[]{:S(2)}, u32[]{:S(2)}) collective-permute-start(bf16[256,512]{1,0:T(8,128)(2,1)} %get-tuple-element.28.refs_1_), channel_id=1, source_target_pairs={{0,1},{1,0},{2,3},{3,2},{4,5},{5,4},{6,7},{7,6},{8,9},{9,8},{10,11... | collective-permute-start | bytes 786440 | tf_op jit(solution)/shard_map/ppermute | solution.py:40
  209.5 1.5 collective-permute-start.29
  (15 other events, 16.1 us)

commit v14 on v9

--- a/solution.py
+++ b/solution.py
@@ -253,6 +253,10 @@
         (kernel_tables(patch_sizes_list, section_index), own_rows)
     )
     row_parts = [own_rows] + across_chips(own_rows)
+    entering_across = [
+        jnp.concatenate([rows, jnp.zeros((biggest_patch_span, columns), jnp.bfloat16)], axis=0)
+        for rows in across_chips_first_section(incoming_states)
+    ]
     for turn_number in range(patches):
         where = tables[turn_number]
         head_rows, key_cache, value_cache = attend_block(
@@ -273,14 +277,18 @@
         )
         results.append(updated)
         if turn_number + 1 < patches:
-            entry_patch = lax.dynamic_slice_in_dim(
-                entering_ext, starts[turn_number + 1], biggest_patch_span, 0
-            )
-            entry_patch = jnp.where(
-                (row_numbers < patch_sizes_list[turn_number + 1])[:, None], entry_patch, 0
-            )
+            entry_live = (row_numbers < patch_sizes_list[turn_number + 1])[:, None]
+            entry_parts = [
+                jnp.where(
+                    entry_live,
+                    lax.dynamic_slice_in_dim(
+                        rows, starts[turn_number + 1], biggest_patch_span, 0
+                    ),
+                    0,
+                )
+                for rows in [entering_ext] + entering_across
+            ]
             arrived = to_next_section(updated)
-            entry_parts = [entry_patch] + across_chips_first_section(entry_patch)
             row_parts = [
                 jnp.where(section_zero, entry, passed) for entry, passed in zip(entry_parts, arrived)
             ]

time: 212 us -> 222 us (1.047)
  waiting for transfers between devices: 83.7 us -> 96.5 us
  starting transfers between devices: 37.2 us -> 32.8 us
    ppermute x6, waiting for transfers between devices: 21.5 us -> 35.9 us  [to_next_section(): lax.ppermute(block, ('section', 'seq'), [(section * count + source, (sect...]
    ppermute x3 -> x1, waiting for transfers between devices: 12.8 us -> 0.01 us  [across_chips_first_section(): lax.ppermute(block, ('section', 'seq'), [(source, (source + step) % count...]
    ppermute x5, waiting for transfers between devices: 37.1 us -> 49.1 us  [across_chips(): lax.ppermute(block, 'seq', [(source, (source + step) % count) for source...]
    ppermute x3 -> x1, starting transfers between devices: 10.8 us -> 3.64 us  [across_chips_first_section(): lax.ppermute(block, ('section', 'seq'), [(source, (source + step) % count...]
    ppermute x6, starting transfers between devices: 16.6 us -> 20.3 us  [to_next_section(): lax.ppermute(block, ('section', 'seq'), [(section * count + source, (sect...]
  transfers between devices with their start and end apart: 30 -> 28, of which waited for: 22 -> 21; matrix products, arithmetic and copies ran while one was open for 2% -> 2% of each run, Pallas kernels for 0% -> 8%
where the time goes in v14:
time: 222 us; the launch traced here: 221 us
  waiting for transfers between devices  96.5 us (43%)
  Pallas kernels  66.6 us (30%)
  starting transfers between devices  32.8 us (15%)
  other arithmetic  10.9 us (5%)
  local copies, waits for them, and re-layouts  7.97 us (4%)
  between operations  6.24 us (3%)
    pallas_call x4, Pallas kernels, attend_block(): pl.pallas_call(block_kernel, grid_spec=grid_spec, out_shape=[jax.ShapeDty...  50.1 us
    ppermute x5, waiting for transfers between devices, across_chips(): lax.ppermute(block, 'seq', [(source, (source + step) % count) for source...  49.1 us
    ppermute x6, waiting for transfers between devices, to_next_section(): lax.ppermute(block, ('section', 'seq'), [(section * count + source, (sect...  35.9 us
    ppermute x6, starting transfers between devices, to_next_section(): lax.ppermute(block, ('section', 'seq'), [(section * count + source, (sect...  20.3 us
    pallas_call x4, Pallas kernels, leave_block(): pl.pallas_call(exit_kernel, in_specs=[smem] + [vmem] * (count + 3), out_s...  16.5 us
    ppermute x16, waiting for transfers between devices, with_partner(): return parts + [lax.ppermute(part, 'seq', to_partner) for part in parts]  11.4 us
    ppermute x5, starting transfers between devices, across_chips(): lax.ppermute(block, 'seq', [(source, (source + step) % count) for source...  7.14 us
    unnamed x66, local copies, waits for them, and re-layouts  6.04 us
  transfers between devices with their start and end apart: 28, of which 21 were waited for; matrix products, arithmetic and copies ran while one was open for 2% of the time, Pallas kernels for 8%

profile of v14, /device:TPU:0, one launch (start us, length us, event | category | flops | bytes accessed | tf_op | source)
XLA Modules:
  0.0 220.9 jit_solution(11549745727912128868)
XLA Ops:
  0.1 0.8 reduce-window.9
  0.9 1.3 bitcast_subtract_fusion
  2.9 0.7 select_reduce_fusion
  3.7 1.2 fusion.12.refs_1_.refs_6_
  4.9 3.0 %collective-permute-start = (bf16[256,768]{1,0:T(8,128)(2,1)S(1)}, bf16[256,768]{1,0:T(8,128)(2,1)S(1)}, u32[]{:S(2)}, u32[]{:S(2)}) collective-permute-start(bf16[256,768]{1,0:T(8,128)(2,1)S(1)} %fusion.12.refs_1_.refs_6_), channel_id=1, source_target_pairs={{0,2},{1,3},{2,0},{3,1},{4,6},{5,7},{6,4},{7,5},{8,10},{9,11},{10,... | collective-permute-start | bytes 1179656 | tf_op jit(solution)/shard_map/ppermute | solution.py:22
  7.9 9.1 %collective-permute-done.refs_2_ = bf16[256,768]{1,0:T(8,128)(2,1)S(1)} collective-permute-done((bf16[256,768]{1,0:T(8,128)(2,1)S(1)}, bf16[256,768]{1,0:T(8,128)(2,1)S(1)}, u32[]{:S(2)}, u32[]{:S(2)}) %collective-permute-start) | collective-permute-done | bytes 393248 | tf_op jit(solution)/shard_map/ppermute | solution.py:22
  17.1 3.6 %collective-permute-start.7 = (bf16[768,768]{1,0:T(8,128)(2,1)}, bf16[768,768]{1,0:T(8,128)(2,1)S(1)}, u32[]{:S(2)}, u32[]{:S(2)}) collective-permute-start(bf16[768,768]{1,0:T(8,128)(2,1)} %param.9), channel_id=1, source_target_pairs={{0,2},{1,3},{2,0},{3,1},{16,18},{17,19},{18,16},{19,17}} | collective-permute-start | bytes 3538952 | tf_op jit(solution)/shard_map/ppermute | solution.py:30
  21.4 0.7 copy-done.12
  22.2 12.5 %shard_map.91 = (bf16[256,512]{1,0:T(8,128)(2,1)}, bf16[4,768,128]{2,1,0:T(8,128)(2,1)}, bf16[4,768,128]{2,1,0:T(8,128)(2,1)}) custom-call(s32[6]{0:T(128)} %get-tuple-element.31.refs_0_, bf16[256,768]{1,0:T(8,128)(2,1)} %copy-done.4, bf16[256,768]{1,0:T(8,128)(2,1)} %copy-done.11, bf16[256,768]{1,0:T(8,128)(2,1)} %copy-done.12, ...), custom_call_target="tpu_custom_call" | custom-call | tf_op jit(solution)/shard_map/pallas_call | solution.py:165
  35.0 18.1 %collective-permute-done.3.refs_2_ = bf16[256,512]{1,0:T(8,128)(2,1)S(1)} collective-permute-done((bf16[256,512]{1,0:T(8,128)(2,1)}, bf16[256,512]{1,0:T(8,128)(2,1)S(1)}, u32[]{:S(2)}, u32[]{:S(2)}) %collective-permute-start.3) | collective-permute-done | bytes 262176 | tf_op jit(solution)/shard_map/ppermute | solution.py:22
  53.2 1.5 collective-permute-done.5.refs_4_
  54.7 0.7 copy-done.28
  55.4 4.2 %shard_map.92 = bf16[256,768]{1,0:T(8,128)(2,1)} custom-call(s32[6]{0:T(128)} %get-tuple-element.31.refs_0_, bf16[256,512]{1,0:T(8,128)(2,1)} %get-tuple-element.19.refs_1_, bf16[256,512]{1,0:T(8,128)(2,1)} %copy-done.20, bf16[256,512]{1,0:T(8,128)(2,1)} %copy-done.24, bf16[256,512]{1,0:T(8,128)(2,1)} %copy-done.28, bf16[4,512,768]{2,1,0:T(8,128)(2,1)} %bitcast.40, ...), custom_call_target="tpu_custom_call" | custom-call | tf_op jit(solution)/shard_map/pallas_call | solution.py:203
  59.6 1.3 collective-permute-start.8
  60.9 2.0 collective-permute-start.6
  66.9 3.7 %collective-permute-done.8 = bf16[256,768]{1,0:T(8,128)(2,1)S(1)} collective-permute-done((bf16[256,768]{1,0:T(8,128)(2,1)}, bf16[256,768]{1,0:T(8,128)(2,1)S(1)}, u32[]{:S(2)}, u32[]{:S(2)}) %collective-permute-start.8) | collective-permute-done | bytes 393248 | tf_op jit(solution)/shard_map/ppermute | solution.py:47
  70.6 7.9 %collective-permute-done.6 = bf16[256,768]{1,0:T(8,128)(2,1)} collective-permute-done((bf16[256,768]{1,0:T(8,128)(2,1)}, bf16[256,768]{1,0:T(8,128)(2,1)}, u32[]{:S(2)}, u32[]{:S(2)}) %collective-permute-start.6) | collective-permute-done | bytes 393248 | tf_op jit(solution)/shard_map/ppermute | solution.py:47
  79.7 1.2 collective-permute-done.10.refs_4_
  81.5 0.8 copy-done.18
  82.3 12.5 %shard_map.93 = (bf16[256,512]{1,0:T(8,128)(2,1)}, bf16[4,768,128]{2,1,0:T(8,128)(2,1)}, bf16[4,768,128]{2,1,0:T(8,128)(2,1)}) custom-call(s32[6]{0:T(128)} %get-tuple-element.34.refs_0_, bf16[256,768]{1,0:T(8,128)(2,1)} %copy-done.2, bf16[256,768]{1,0:T(8,128)(2,1)} %copy-done.6, ...), custom_call_target="tpu_custom_call", output_to_operand_aliasing={{1}: (7, {}), {2}: (8, {})} | custom-call | tf_op jit(solution)/shard_map/pallas_call | solution.py:165
  94.8 1.7 collective-permute-start.11
  96.6 6.8 %collective-permute-done.11.refs_2_ = bf16[256,512]{1,0:T(8,128)(2,1)S(1)} collective-permute-done((bf16[256,512]{1,0:T(8,128)(2,1)}, bf16[256,512]{1,0:T(8,128)(2,1)S(1)}, u32[]{:S(2)}, u32[]{:S(2)}) %collective-permute-start.11) | collective-permute-done | bytes 262176 | tf_op jit(solution)/shard_map/ppermute | solution.py:22
  103.4 1.5 collective-permute-done.13.refs_4_
  104.9 0.7 copy-done.29
  105.6 4.1 %shard_map.94 = bf16[256,768]{1,0:T(8,128)(2,1)} custom-call(s32[6]{0:T(128)} %get-tuple-element.34.refs_0_, bf16[256,512]{1,0:T(8,128)(2,1)} %get-tuple-element.22.refs_1_, bf16[256,512]{1,0:T(8,128)(2,1)} %copy-done.21, bf16[256,512]{1,0:T(8,128)(2,1)} %copy-done.25, bf16[256,512]{1,0:T(8,128)(2,1)} %copy-done.29, bf16[4,512,768]{2,1,0:T(8,128)(2,1)} %bitcast.41, ...), custom_call_target="tpu_custom_call" | custom-call | tf_op jit(solution)/shard_map/pallas_call | solution.py:203
  109.7 6.6 %collective-permute-start.15 = (bf16[256,768]{1,0:T(8,128)(2,1)}, bf16[256,768]{1,0:T(8,128)(2,1)S(1)}, u32[]{:S(2)}, u32[]{:S(2)}) collective-permute-start(bf16[256,768]{1,0:T(8,128)(2,1)} %shard_map.94), channel_id=1, source_target_pairs={{0,6},{1,7},{2,4},{3,5},{4,10},{5,11},{6,8},{7,9},{8,14},{9,15},{1... | collective-permute-start | bytes 1179656 | tf_op jit(solution)/shard_map/ppermute | solution.py:47
  116.3 2.0 collective-permute-start.14
  120.9 5.2 %collective-permute-done.15 = bf16[256,768]{1,0:T(8,128)(2,1)S(1)} collective-permute-done((bf16[256,768]{1,0:T(8,128)(2,1)}, bf16[256,768]{1,0:T(8,128)(2,1)S(1)}, u32[]{:S(2)}, u32[]{:S(2)}) %collective-permute-start.15) | collective-permute-done | bytes 393248 | tf_op jit(solution)/shard_map/ppermute | solution.py:47
  126.1 7.6 %collective-permute-done.14 = bf16[256,768]{1,0:T(8,128)(2,1)} collective-permute-done((bf16[256,768]{1,0:T(8,128)(2,1)}, bf16[256,768]{1,0:T(8,128)(2,1)}, u32[]{:S(2)}, u32[]{:S(2)}) %collective-permute-start.14) | collective-permute-done | bytes 393248 | tf_op jit(solution)/shard_map/ppermute | solution.py:47
  134.9 1.2 collective-permute-done.17.refs_4_
  136.6 0.7 copy-done.19
  137.4 12.5 %shard_map.95 = (bf16[256,512]{1,0:T(8,128)(2,1)}, bf16[4,768,128]{2,1,0:T(8,128)(2,1)}, bf16[4,768,128]{2,1,0:T(8,128)(2,1)}) custom-call(s32[6]{0:T(128)} %get-tuple-element.33.refs_0_, bf16[256,768]{1,0:T(8,128)(2,1)} %copy-done.3, bf16[256,768]{1,0:T(8,128)(2,1)} %copy-done.7, ...), custom_call_target="tpu_custom_call", output_to_operand_aliasing={{1}: (7, {}), {2}: (8, {})} | custom-call | tf_op jit(solution)/shard_map/pallas_call | solution.py:165
  150.2 8.3 %collective-permute-done.18.refs_2_ = bf16[256,512]{1,0:T(8,128)(2,1)S(1)} collective-permute-done((bf16[256,512]{1,0:T(8,128)(2,1)}, bf16[256,512]{1,0:T(8,128)(2,1)S(1)}, u32[]{:S(2)}, u32[]{:S(2)}) %collective-permute-start.18) | collective-permute-done | bytes 262176 | tf_op jit(solution)/shard_map/ppermute | solution.py:22
  158.5 1.5 collective-permute-done.20.refs_4_
  160.0 0.7 copy-done.30
  160.7 4.1 %shard_map.96 = bf16[256,768]{1,0:T(8,128)(2,1)} custom-call(s32[6]{0:T(128)} %get-tuple-element.33.refs_0_, bf16[256,512]{1,0:T(8,128)(2,1)} %get-tuple-element.25.refs_1_, bf16[256,512]{1,0:T(8,128)(2,1)} %copy-done.22, bf16[256,512]{1,0:T(8,128)(2,1)} %copy-done.26, bf16[256,512]{1,0:T(8,128)(2,1)} %copy-done.30, bf16[4,512,768]{2,1,0:T(8,128)(2,1)} %bitcast.42, ...), custom_call_target="tpu_custom_call" | custom-call | tf_op jit(solution)/shard_map/pallas_call | solution.py:203
  164.8 5.1 %collective-permute-start.22 = (bf16[256,768]{1,0:T(8,128)(2,1)}, bf16[256,768]{1,0:T(8,128)(2,1)S(1)}, u32[]{:S(2)}, u32[]{:S(2)}) collective-permute-start(bf16[256,768]{1,0:T(8,128)(2,1)} %shard_map.96), channel_id=1, source_target_pairs={{0,6},{1,7},{2,4},{3,5},{4,10},{5,11},{6,8},{7,9},{8,14},{9,15},{1... | collective-permute-start | bytes 1179656 | tf_op jit(solution)/shard_map/ppermute | solution.py:47
  170.0 3.2 %collective-permute-start.21 = (bf16[256,768]{1,0:T(8,128)(2,1)}, bf16[256,768]{1,0:T(8,128)(2,1)}, u32[]{:S(2)}, u32[]{:S(2)}) collective-permute-start(bf16[256,768]{1,0:T(8,128)(2,1)} %shard_map.96), channel_id=1, source_target_pairs={{0,4},{1,5},{2,6},{3,7},{4,8},{5,9},{6,10},{7,11},{8,12},{9,13},{1... | collective-permute-start | bytes 1179656 | tf_op jit(solution)/shard_map/ppermute | solution.py:47
  175.9 3.8 %collective-permute-done.22 = bf16[256,768]{1,0:T(8,128)(2,1)S(1)} collective-permute-done((bf16[256,768]{1,0:T(8,128)(2,1)}, bf16[256,768]{1,0:T(8,128)(2,1)S(1)}, u32[]{:S(2)}, u32[]{:S(2)}) %collective-permute-start.22) | collective-permute-done | bytes 393248 | tf_op jit(solution)/shard_map/ppermute | solution.py:47
  179.7 7.6 %collective-permute-done.21 = bf16[256,768]{1,0:T(8,128)(2,1)} collective-permute-done((bf16[256,768]{1,0:T(8,128)(2,1)}, bf16[256,768]{1,0:T(8,128)(2,1)}, u32[]{:S(2)}, u32[]{:S(2)}) %collective-permute-start.21) | collective-permute-done | bytes 393248 | tf_op jit(solution)/shard_map/ppermute | solution.py:47
  188.5 1.2 collective-permute-done.24.refs_4_
  191.0 12.5 %shard_map.97 = (bf16[256,512]{1,0:T(8,128)(2,1)}, bf16[4,768,128]{2,1,0:T(8,128)(2,1)}, bf16[4,768,128]{2,1,0:T(8,128)(2,1)}) custom-call(s32[6]{0:T(128)} %get-tuple-element.32.refs_0_, bf16[256,768]{1,0:T(8,128)(2,1)} %copy-done.1, bf16[256,768]{1,0:T(8,128)(2,1)} %copy-done.5, ...), custom_call_target="tpu_custom_call", output_to_operand_aliasing={{1}: (7, {}), {2}: (8, {})} | custom-call | tf_op jit(solution)/shard_map/pallas_call | solution.py:165
  203.6 1.8 collective-permute-start.25
  205.4 6.8 %collective-permute-done.25.refs_2_ = bf16[256,512]{1,0:T(8,128)(2,1)S(1)} collective-permute-done((bf16[256,512]{1,0:T(8,128)(2,1)}, bf16[256,512]{1,0:T(8,128)(2,1)S(1)}, u32[]{:S(2)}, u32[]{:S(2)}) %collective-permute-start.25) | collective-permute-done | bytes 262176 | tf_op jit(solution)/shard_map/ppermute | solution.py:22
  212.2 1.5 collective-permute-done.27.refs_4_
  213.7 0.7 copy-done.31
  214.4 4.1 %shard_map.98 = bf16[256,768]{1,0:T(8,128)(2,1)} custom-call(s32[6]{0:T(128)} %get-tuple-element.32.refs_0_, bf16[256,512]{1,0:T(8,128)(2,1)} %get-tuple-element.28.refs_1_, bf16[256,512]{1,0:T(8,128)(2,1)} %copy-done.23, bf16[256,512]{1,0:T(8,128)(2,1)} %copy-done.27, bf16[256,512]{1,0:T(8,128)(2,1)} %copy-done.31, bf16[4,512,768]{2,1,0:T(8,128)(2,1)} %bitcast.43, ...), custom_call_target="tpu_custom_call" | custom-call | tf_op jit(solution)/shard_map/pallas_call | solution.py:203
  218.6 2.3 %maximum_bitcast_fusion = bf16[4,1,256,768]{3,2,1,0:T(8,128)(2,1)} fusion(bf16[1,256,768]{2,1,0:T(8,128)(2,1)} %bitcast.47, bf16[1,256,768]{2,1,0:T(8,128)(2,1)S(1)} %bitcast.46, bf16[1,256,768]{2,1,0:T(8,128)(2,1)S(1)} %bitcast.45, bf16[1,256,768]{2,1,0:T(8,128)(2,1)S(1)} %bitcast.44), kind=kLoop, calls=%fused_computation.6 | loop fusion | flops 2359296 | bytes 3145728 | tf_op jit(solution)/shard_map/broadcast_in_dim | solution.py:295
  (105 shorter events, 11.4 us)
Async XLA Ops:
  4.9 16.4 %copy-start.4 = (bf16[256,768]{1,0:T(8,128)(2,1)}, bf16[256,768]{1,0:T(8,128)(2,1)S(1)}, u32[]{:S(2)}) copy-start(bf16[256,768]{1,0:T(8,128)(2,1)S(1)} %fusion.12.refs_1_.refs_6_) | copy-start | bytes 1179652
  4.9 12.1 %collective-permute-start = (bf16[256,768]{1,0:T(8,128)(2,1)S(1)}, bf16[256,768]{1,0:T(8,128)(2,1)S(1)}, u32[]{:S(2)}, u32[]{:S(2)}) collective-permute-start(bf16[256,768]{1,0:T(8,128)(2,1)S(1)} %fusion.12.refs_1_.refs_6_), channel_id=1, source_target_pairs={{0,2},{1,3},{2,0},{3,1},{4,6},{5,7},{6,4},{7,5},{8,10},{9,11},{10,... | collective-permute-start | bytes 1179656 | tf_op jit(solution)/shard_map/ppermute | solution.py:22
  7.9 13.4 %collective-permute-start.1 = (bf16[256,768]{1,0:T(8,128)(2,1)S(1)}, bf16[256,768]{1,0:T(8,128)(2,1)S(1)}, u32[]{:S(2)}, u32[]{:S(2)}) collective-permute-start(bf16[256,768]{1,0:T(8,128)(2,1)S(1)} %fusion.12.refs_1_.refs_6_), channel_id=1, source_target_pairs={{0,1},{1,0},{2,3},{3,2},{4,5},{5,4},{6,7},{7,6},{8,9},{9,8},{10,11... | collective-permute-start | bytes 1179656 | tf_op jit(solution)/shard_map/ppermute | solution.py:40
  17.1 4.3 %copy-start.11 = (bf16[256,768]{1,0:T(8,128)(2,1)}, bf16[256,768]{1,0:T(8,128)(2,1)S(1)}, u32[]{:S(2)}) copy-start(bf16[256,768]{1,0:T(8,128)(2,1)S(1)} %collective-permute-done.refs_2_) | copy-start | bytes 1179652
  17.1 4.3 %collective-permute-start.2 = (bf16[256,768]{1,0:T(8,128)(2,1)S(1)}, bf16[256,768]{1,0:T(8,128)(2,1)S(1)}, u32[]{:S(2)}, u32[]{:S(2)}) collective-permute-start(bf16[256,768]{1,0:T(8,128)(2,1)S(1)} %collective-permute-done.refs_2_), channel_id=1, source_target_pairs={{0,1},{1,0},{2,3},{3,2},{4,5},{5,4},{6,7},{7,6},{8,9},{9,8},{10,11... | collective-permute-start | bytes 1179656 | tf_op jit(solution)/shard_map/ppermute | solution.py:40
  17.1 49.8 %collective-permute-start.7 = (bf16[768,768]{1,0:T(8,128)(2,1)}, bf16[768,768]{1,0:T(8,128)(2,1)S(1)}, u32[]{:S(2)}, u32[]{:S(2)}) collective-permute-start(bf16[768,768]{1,0:T(8,128)(2,1)} %param.9), channel_id=1, source_target_pairs={{0,2},{1,3},{2,0},{3,1},{16,18},{17,19},{18,16},{19,17}} | collective-permute-start | bytes 3538952 | tf_op jit(solution)/shard_map/ppermute | solution.py:30
  34.7 18.4 %collective-permute-start.3 = (bf16[256,512]{1,0:T(8,128)(2,1)}, bf16[256,512]{1,0:T(8,128)(2,1)S(1)}, u32[]{:S(2)}, u32[]{:S(2)}) collective-permute-start(bf16[256,512]{1,0:T(8,128)(2,1)} %get-tuple-element.19.refs_1_), channel_id=1, source_target_pairs={{0,2},{1,3},{2,0},{3,1},{4,6},{5,7},{6,4},{7,5},{8,10},{9,11},{10,... | collective-permute-start | bytes 786440 | tf_op jit(solution)/shard_map/ppermute | solution.py:22
  35.0 18.1 %collective-permute-start.4 = (bf16[256,512]{1,0:T(8,128)(2,1)}, bf16[256,512]{1,0:T(8,128)(2,1)S(1)}, u32[]{:S(2)}, u32[]{:S(2)}) collective-permute-start(bf16[256,512]{1,0:T(8,128)(2,1)} %get-tuple-element.19.refs_1_), channel_id=1, source_target_pairs={{0,1},{1,0},{2,3},{3,2},{4,5},{5,4},{6,7},{7,6},{8,9},{9,8},{10,11... | collective-permute-start | bytes 786440 | tf_op jit(solution)/shard_map/ppermute | solution.py:40
  53.2 1.5 copy-start.20
  53.2 1.5 collective-permute-start.5
  53.2 1.5 copy-start.24
  55.4 10.1 %copy-start.32 = (s32[4]{0:T(128)S(1)}, s32[4]{0:T(128)}, u32[]{:S(2)}) copy-start(s32[4]{0:T(128)} %param.11) | copy-start | bytes 52
  55.4 23.2 %copy-start = (bf16[768,768]{1,0:T(8,128)(2,1)S(1)}, bf16[768,768]{1,0:T(8,128)(2,1)}, u32[]{:S(2)}) copy-start(bf16[768,768]{1,0:T(8,128)(2,1)} %param.9) | copy-start | bytes 3538948
  59.6 11.0 %collective-permute-start.8 = (bf16[256,768]{1,0:T(8,128)(2,1)}, bf16[256,768]{1,0:T(8,128)(2,1)S(1)}, u32[]{:S(2)}, u32[]{:S(2)}) collective-permute-start(bf16[256,768]{1,0:T(8,128)(2,1)} %shard_map.92), channel_id=1, source_target_pairs={{0,6},{1,7},{2,4},{3,5},{4,10},{5,11},{6,8},{7,9},{8,14},{9,15},{1... | collective-permute-start | bytes 1179656 | tf_op jit(solution)/shard_map/ppermute | solution.py:47
  60.9 17.7 %collective-permute-start.6 = (bf16[256,768]{1,0:T(8,128)(2,1)}, bf16[256,768]{1,0:T(8,128)(2,1)}, u32[]{:S(2)}, u32[]{:S(2)}) collective-permute-start(bf16[256,768]{1,0:T(8,128)(2,1)} %shard_map.92), channel_id=1, source_target_pairs={{0,4},{1,5},{2,6},{3,7},{4,8},{5,9},{6,10},{7,11},{8,12},{9,13},{1... | collective-permute-start | bytes 1179656 | tf_op jit(solution)/shard_map/ppermute | solution.py:47
  79.1 3.1 %copy-start.2 = (bf16[256,768]{1,0:T(8,128)(2,1)}, bf16[256,768]{1,0:T(8,128)(2,1)S(1)}, u32[]{:S(2)}) copy-start(bf16[256,768]{1,0:T(8,128)(2,1)S(1)} %get-tuple-element.46.refs_1_.refs_6_) | copy-start | bytes 1179652
  79.2 3.1 %copy-start.6 = (bf16[256,768]{1,0:T(8,128)(2,1)}, bf16[256,768]{1,0:T(8,128)(2,1)S(1)}, u32[]{:S(2)}) copy-start(bf16[256,768]{1,0:T(8,128)(2,1)S(1)} %get-tuple-element.45.refs_2_) | copy-start | bytes 1179652
  79.2 1.8 collective-permute-start.10
  79.2 2.3 %collective-permute-start.9 = (bf16[256,768]{1,0:T(8,128)(2,1)S(1)}, bf16[256,768]{1,0:T(8,128)(2,1)S(1)}, u32[]{:S(2)}, u32[]{:S(2)}) collective-permute-start(bf16[256,768]{1,0:T(8,128)(2,1)S(1)} %get-tuple-element.46.refs_1_.refs_6_), channel_id=1, source_target_pairs={{0,1},{1,0},{2,3},{3,2},{4,5},{5,4},{6,7},{7,6},{8,9},{9,8},{10,11... | collective-permute-start | bytes 1179656 | tf_op jit(solution)/shard_map/ppermute | solution.py:40
  94.8 8.6 %collective-permute-start.11 = (bf16[256,512]{1,0:T(8,128)(2,1)}, bf16[256,512]{1,0:T(8,128)(2,1)S(1)}, u32[]{:S(2)}, u32[]{:S(2)}) collective-permute-start(bf16[256,512]{1,0:T(8,128)(2,1)} %get-tuple-element.22.refs_1_), channel_id=1, source_target_pairs={{0,2},{1,3},{2,0},{3,1},{4,6},{5,7},{6,4},{7,5},{8,10},{9,11},{10,... | collective-permute-start | bytes 786440 | tf_op jit(solution)/shard_map/ppermute | solution.py:22
  96.6 6.8 %collective-permute-start.12 = (bf16[256,512]{1,0:T(8,128)(2,1)}, bf16[256,512]{1,0:T(8,128)(2,1)S(1)}, u32[]{:S(2)}, u32[]{:S(2)}) collective-permute-start(bf16[256,512]{1,0:T(8,128)(2,1)} %get-tuple-element.22.refs_1_), channel_id=1, source_target_pairs={{0,1},{1,0},{2,3},{3,2},{4,5},{5,4},{6,7},{7,6},{8,9},{9,8},{10,11... | collective-permute-start | bytes 786440 | tf_op jit(solution)/shard_map/ppermute | solution.py:40
  103.4 1.5 copy-start.21
  103.4 1.5 collective-permute-start.13
  103.4 1.5 copy-start.25
  109.7 16.3 %collective-permute-start.15 = (bf16[256,768]{1,0:T(8,128)(2,1)}, bf16[256,768]{1,0:T(8,128)(2,1)S(1)}, u32[]{:S(2)}, u32[]{:S(2)}) collective-permute-start(bf16[256,768]{1,0:T(8,128)(2,1)} %shard_map.94), channel_id=1, source_target_pairs={{0,6},{1,7},{2,4},{3,5},{4,10},{5,11},{6,8},{7,9},{8,14},{9,15},{1... | collective-permute-start | bytes 1179656 | tf_op jit(solution)/shard_map/ppermute | solution.py:47
  116.3 17.4 %collective-permute-start.14 = (bf16[256,768]{1,0:T(8,128)(2,1)}, bf16[256,768]{1,0:T(8,128)(2,1)}, u32[]{:S(2)}, u32[]{:S(2)}) collective-permute-start(bf16[256,768]{1,0:T(8,128)(2,1)} %shard_map.94), channel_id=1, source_target_pairs={{0,4},{1,5},{2,6},{3,7},{4,8},{5,9},{6,10},{7,11},{8,12},{9,13},{1... | collective-permute-start | bytes 1179656 | tf_op jit(solution)/shard_map/ppermute | solution.py:47
  134.3 3.1 %copy-start.3 = (bf16[256,768]{1,0:T(8,128)(2,1)}, bf16[256,768]{1,0:T(8,128)(2,1)S(1)}, u32[]{:S(2)}) copy-start(bf16[256,768]{1,0:T(8,128)(2,1)S(1)} %get-tuple-element.44.refs_1_.refs_6_) | copy-start | bytes 1179652
  134.3 3.1 %copy-start.7 = (bf16[256,768]{1,0:T(8,128)(2,1)}, bf16[256,768]{1,0:T(8,128)(2,1)S(1)}, u32[]{:S(2)}) copy-start(bf16[256,768]{1,0:T(8,128)(2,1)S(1)} %get-tuple-element.43.refs_2_) | copy-start | bytes 1179652
  134.3 1.8 collective-permute-start.17
  134.4 2.3 %collective-permute-start.16 = (bf16[256,768]{1,0:T(8,128)(2,1)S(1)}, bf16[256,768]{1,0:T(8,128)(2,1)S(1)}, u32[]{:S(2)}, u32[]{:S(2)}) collective-permute-start(bf16[256,768]{1,0:T(8,128)(2,1)S(1)} %get-tuple-element.44.refs_1_.refs_6_), channel_id=1, source_target_pairs={{0,1},{1,0},{2,3},{3,2},{4,5},{5,4},{6,7},{7,6},{8,9},{9,8},{10,11... | collective-permute-start | bytes 1179656 | tf_op jit(solution)/shard_map/ppermute | solution.py:40
  149.9 8.6 %collective-permute-start.18 = (bf16[256,512]{1,0:T(8,128)(2,1)}, bf16[256,512]{1,0:T(8,128)(2,1)S(1)}, u32[]{:S(2)}, u32[]{:S(2)}) collective-permute-start(bf16[256,512]{1,0:T(8,128)(2,1)} %get-tuple-element.25.refs_1_), channel_id=1, source_target_pairs={{0,2},{1,3},{2,0},{3,1},{4,6},{5,7},{6,4},{7,5},{8,10},{9,11},{10,... | collective-permute-start | bytes 786440 | tf_op jit(solution)/shard_map/ppermute | solution.py:22
  150.2 8.3 %collective-permute-start.19 = (bf16[256,512]{1,0:T(8,128)(2,1)}, bf16[256,512]{1,0:T(8,128)(2,1)S(1)}, u32[]{:S(2)}, u32[]{:S(2)}) collective-permute-start(bf16[256,512]{1,0:T(8,128)(2,1)} %get-tuple-element.25.refs_1_), channel_id=1, source_target_pairs={{0,1},{1,0},{2,3},{3,2},{4,5},{5,4},{6,7},{7,6},{8,9},{9,8},{10,11... | collective-permute-start | bytes 786440 | tf_op jit(solution)/shard_map/ppermute | solution.py:40
  158.5 1.5 copy-start.22
  158.5 1.5 collective-permute-start.20
  158.5 1.5 copy-start.26
  164.8 14.9 %collective-permute-start.22 = (bf16[256,768]{1,0:T(8,128)(2,1)}, bf16[256,768]{1,0:T(8,128)(2,1)S(1)}, u32[]{:S(2)}, u32[]{:S(2)}) collective-permute-start(bf16[256,768]{1,0:T(8,128)(2,1)} %shard_map.96), channel_id=1, source_target_pairs={{0,6},{1,7},{2,4},{3,5},{4,10},{5,11},{6,8},{7,9},{8,14},{9,15},{1... | collective-permute-start | bytes 1179656 | tf_op jit(solution)/shard_map/ppermute | solution.py:47
  170.0 17.4 %collective-permute-start.21 = (bf16[256,768]{1,0:T(8,128)(2,1)}, bf16[256,768]{1,0:T(8,128)(2,1)}, u32[]{:S(2)}, u32[]{:S(2)}) collective-permute-start(bf16[256,768]{1,0:T(8,128)(2,1)} %shard_map.96), channel_id=1, source_target_pairs={{0,4},{1,5},{2,6},{3,7},{4,8},{5,9},{6,10},{7,11},{8,12},{9,13},{1... | collective-permute-start | bytes 1179656 | tf_op jit(solution)/shard_map/ppermute | solution.py:47
  187.9 2.4 %copy-start.1 = (bf16[256,768]{1,0:T(8,128)(2,1)}, bf16[256,768]{1,0:T(8,128)(2,1)S(1)}, u32[]{:S(2)}) copy-start(bf16[256,768]{1,0:T(8,128)(2,1)S(1)} %get-tuple-element.36.refs_1_.refs_6_) | copy-start | bytes 1179652
  187.9 2.4 %copy-start.5 = (bf16[256,768]{1,0:T(8,128)(2,1)}, bf16[256,768]{1,0:T(8,128)(2,1)S(1)}, u32[]{:S(2)}) copy-start(bf16[256,768]{1,0:T(8,128)(2,1)S(1)} %get-tuple-element.35.refs_2_) | copy-start | bytes 1179652
  187.9 1.8 collective-permute-start.24
  188.0 2.3 %collective-permute-start.23 = (bf16[256,768]{1,0:T(8,128)(2,1)S(1)}, bf16[256,768]{1,0:T(8,128)(2,1)S(1)}, u32[]{:S(2)}, u32[]{:S(2)}) collective-permute-start(bf16[256,768]{1,0:T(8,128)(2,1)S(1)} %get-tuple-element.36.refs_1_.refs_6_), channel_id=1, source_target_pairs={{0,1},{1,0},{2,3},{3,2},{4,5},{5,4},{6,7},{7,6},{8,9},{9,8},{10,11... | collective-permute-start | bytes 1179656 | tf_op jit(solution)/shard_map/ppermute | solution.py:40
  203.5 15.0 %copy-start.8 = (bf16[256,768]{1,0:T(8,128)(2,1)S(1)}, bf16[256,768]{1,0:T(8,128)(2,1)}, u32[]{:S(2)}) copy-start(bf16[256,768]{1,0:T(8,128)(2,1)} %shard_map.92) | copy-start | bytes 1179652
  203.5 15.0 %copy-start.9 = (bf16[256,768]{1,0:T(8,128)(2,1)S(1)}, bf16[256,768]{1,0:T(8,128)(2,1)}, u32[]{:S(2)}) copy-start(bf16[256,768]{1,0:T(8,128)(2,1)} %shard_map.94) | copy-start | bytes 1179652
  203.6 15.0 %copy-start.10 = (bf16[256,768]{1,0:T(8,128)(2,1)S(1)}, bf16[256,768]{1,0:T(8,128)(2,1)}, u32[]{:S(2)}) copy-start(bf16[256,768]{1,0:T(8,128)(2,1)} %shard_map.96) | copy-start | bytes 1179652
  203.6 8.6 %collective-permute-start.25 = (bf16[256,512]{1,0:T(8,128)(2,1)}, bf16[256,512]{1,0:T(8,128)(2,1)S(1)}, u32[]{:S(2)}, u32[]{:S(2)}) collective-permute-start(bf16[256,512]{1,0:T(8,128)(2,1)} %get-tuple-element.28.refs_1_), channel_id=1, source_target_pairs={{0,2},{1,3},{2,0},{3,1},{4,6},{5,7},{6,4},{7,5},{8,10},{9,11},{10,... | collective-permute-start | bytes 786440 | tf_op jit(solution)/shard_map/ppermute | solution.py:22
  205.4 6.8 %collective-permute-start.26 = (bf16[256,512]{1,0:T(8,128)(2,1)}, bf16[256,512]{1,0:T(8,128)(2,1)S(1)}, u32[]{:S(2)}, u32[]{:S(2)}) collective-permute-start(bf16[256,512]{1,0:T(8,128)(2,1)} %get-tuple-element.28.refs_1_), channel_id=1, source_target_pairs={{0,1},{1,0},{2,3},{3,2},{4,5},{5,4},{6,7},{7,6},{8,9},{9,8},{10,11... | collective-permute-start | bytes 786440 | tf_op jit(solution)/shard_map/ppermute | solution.py:40
  212.2 1.5 copy-start.23
  212.2 1.5 collective-permute-start.27
  (13 other events, 11.7 us)

commit v15 on v9

--- a/solution.py
+++ b/solution.py
@@ -255,23 +255,7 @@
     row_parts = [own_rows] + across_chips(own_rows)
     for turn_number in range(patches):
         where = tables[turn_number]
-        head_rows, key_cache, value_cache = attend_block(
-            with_partner(row_parts),
-            shift_scale,
-            qkv_weights,
-            key_cache,
-            value_cache,
-            where,
-            turn_number > 0,
-        )
-        updated = leave_block(
-            with_partner([head_rows] + across_chips(head_rows)),
-            out_weights,
-            row_parts[0],
-            gating_here,
-            where,
-        )
-        results.append(updated)
+        rows_here = with_partner(row_parts)
         if turn_number + 1 < patches:
             entry_patch = lax.dynamic_slice_in_dim(
                 entering_ext, starts[turn_number + 1], biggest_patch_span, 0
@@ -279,8 +263,27 @@
             entry_patch = jnp.where(
                 (row_numbers < patch_sizes_list[turn_number + 1])[:, None], entry_patch, 0
             )
+            entry_patch, rows_here = lax.optimization_barrier((entry_patch, rows_here))
+            entry_parts = [entry_patch] + across_chips_first_section(entry_patch)
+        head_rows, key_cache, value_cache = attend_block(
+            rows_here,
+            shift_scale,
+            qkv_weights,
+            key_cache,
+            value_cache,
+            where,
+            turn_number > 0,
+        )
+        updated = leave_block(
+            with_partner([head_rows] + across_chips(head_rows)),
+            out_weights,
+            row_parts[0],
+            gating_here,
+            where,
+        )
+        results.append(updated)
+        if turn_number + 1 < patches:
             arrived = to_next_section(updated)
-            entry_parts = [entry_patch] + across_chips_first_section(entry_patch)
             row_parts = [
                 jnp.where(section_zero, entry, passed) for entry, passed in zip(entry_parts, arrived)
             ]

time: 212 us -> 217 us (1.024)
  waiting for transfers between devices: 83.7 us -> 88.5 us
    ppermute x6, waiting for transfers between devices: 21.5 us -> 33 us  [to_next_section(): lax.ppermute(block, ('section', 'seq'), [(section * count + source, (sect...]
    ppermute x3, waiting for transfers between devices: 12.8 us -> 5.74 us  [across_chips_first_section(): lax.ppermute(block, ('section', 'seq'), [(source, (source + step) % count...]
    unnamed x66 -> x62, local copies, waits for them, and re-layouts: 5.86 us -> 5.98 us
  transfers between devices with their start and end apart: 30 -> 30, of which waited for: 22 -> 20; matrix products, arithmetic and copies ran while one was open for 2% -> 0% of each run, Pallas kernels for 0% -> 2%
where the time goes in v15:
time: 217 us; the launch traced here: 216 us
  waiting for transfers between devices  88.5 us (41%)
  Pallas kernels  66.5 us (31%)
  starting transfers between devices  35.4 us (16%)
  other arithmetic  10.2 us (5%)
  local copies, waits for them, and re-layouts  8.74 us (4%)
  between operations  6.28 us (3%)
    pallas_call x4, Pallas kernels, attend_block(): pl.pallas_call(block_kernel, grid_spec=grid_spec, out_shape=[jax.ShapeDty...  50.1 us
    ppermute x5, waiting for transfers between devices, across_chips(): lax.ppermute(block, 'seq', [(source, (source + step) % count) for source...  39 us
    ppermute x6, waiting for transfers between devices, to_next_section(): lax.ppermute(block, ('section', 'seq'), [(section * count + source, (sect...  33 us
    ppermute x6, starting transfers between devices, to_next_section(): lax.ppermute(block, ('section', 'seq'), [(section * count + source, (sect...  18.1 us
    pallas_call x4, Pallas kernels, leave_block(): pl.pallas_call(exit_kernel, in_specs=[smem] + [vmem] * (count + 3), out_s...  16.4 us
    ppermute x16, waiting for transfers between devices, with_partner(): return parts + [lax.ppermute(part, 'seq', to_partner) for part in parts]  10.7 us
    ppermute x3, starting transfers between devices, across_chips_first_section(): lax.ppermute(block, ('section', 'seq'), [(source, (source + step) % count...  9.48 us
    ppermute x5, starting transfers between devices, across_chips(): lax.ppermute(block, 'seq', [(source, (source + step) % count) for source...  7.36 us
  transfers between devices with their start and end apart: 30, of which 20 were waited for; matrix products, arithmetic and copies ran while one was open for 0% of the time, Pallas kernels for 2%

profile of v15, /device:TPU:0, one launch (start us, length us, event | category | flops | bytes accessed | tf_op | source)
XLA Modules:
  0.0 215.6 jit_solution(5413113158623772382)
XLA Ops:
  0.0 0.8 reduce-window.9
  0.9 1.3 bitcast_subtract_fusion
  6.7 1.4 fusion.12
  12.2 1.3 iota_compare_fusion.2
  13.5 2.0 fusion
  15.5 3.0 %collective-permute-start = (bf16[256,768]{1,0:T(8,128)(2,1)S(1)}, bf16[256,768]{1,0:T(8,128)(2,1)S(1)}, u32[]{:S(2)}, u32[]{:S(2)}) collective-permute-start(bf16[256,768]{1,0:T(8,128)(2,1)S(1)} %get-tuple-element.34.refs_1_.refs_6_), channel_id=1, source_target_pairs={{0,2},{1,3},{2,0},{3,1},{4,6},{5,7},{6,4},{7,5},{8,10},{9,11},{10,... | collective-permute-start | bytes 1179656 | tf_op jit(solution)/shard_map/ppermute | solution.py:22
  18.5 9.1 %collective-permute-done.refs_2_ = bf16[256,768]{1,0:T(8,128)(2,1)S(1)} collective-permute-done((bf16[256,768]{1,0:T(8,128)(2,1)S(1)}, bf16[256,768]{1,0:T(8,128)(2,1)S(1)}, u32[]{:S(2)}, u32[]{:S(2)}) %collective-permute-start) | collective-permute-done | bytes 393248 | tf_op jit(solution)/shard_map/ppermute | solution.py:22
  28.3 1.0 collective-permute-done.2.refs_4_
  29.4 0.7 copy-done.15
  30.1 12.5 %shard_map.91 = (bf16[256,512]{1,0:T(8,128)(2,1)}, bf16[4,768,128]{2,1,0:T(8,128)(2,1)}, bf16[4,768,128]{2,1,0:T(8,128)(2,1)}) custom-call(s32[6]{0:T(128)} %get-tuple-element.68.refs_0_, bf16[256,768]{1,0:T(8,128)(2,1)} %copy-done.3, bf16[256,768]{1,0:T(8,128)(2,1)} %copy-done.12, bf16[256,768]{1,0:T(8,128)(2,1)} %copy-done.13, ...), custom_call_target="tpu_custom_call" | custom-call | tf_op jit(solution)/shard_map/pallas_call | solution.py:165
  42.7 1.7 collective-permute-start.3
  44.4 6.8 %collective-permute-done.3.refs_2_ = bf16[256,512]{1,0:T(8,128)(2,1)S(1)} collective-permute-done((bf16[256,512]{1,0:T(8,128)(2,1)}, bf16[256,512]{1,0:T(8,128)(2,1)S(1)}, u32[]{:S(2)}, u32[]{:S(2)}) %collective-permute-start.3) | collective-permute-done | bytes 262176 | tf_op jit(solution)/shard_map/ppermute | solution.py:22
  51.2 3.6 %collective-permute-start.7 = (bf16[256,768]{1,0:T(8,128)(2,1)S(1)}, bf16[256,768]{1,0:T(8,128)(2,1)S(1)}, u32[]{:S(2)}, u32[]{:S(2)}) collective-permute-start(bf16[256,768]{1,0:T(8,128)(2,1)S(1)} %get-tuple-element.39), channel_id=1, source_target_pairs={{0,2},{1,3},{2,0},{3,1},{16,18},{17,19},{18,16},{19,17}} | collective-permute-start | bytes 1179656 | tf_op jit(solution)/shard_map/ppermute | solution.py:30
  55.7 4.1 %shard_map.92 = bf16[256,768]{1,0:T(8,128)(2,1)} custom-call(s32[6]{0:T(128)} %get-tuple-element.68.refs_0_, bf16[256,512]{1,0:T(8,128)(2,1)} %get-tuple-element.38.refs_1_, bf16[256,512]{1,0:T(8,128)(2,1)} %copy-done.19, bf16[256,512]{1,0:T(8,128)(2,1)} %copy-done.20, bf16[256,512]{1,0:T(8,128)(2,1)} %copy-done.27, bf16[4,512,768]{2,1,0:T(8,128)(2,1)} %bitcast.40, ...), custom_call_target="tpu_custom_call" | custom-call | tf_op jit(solution)/shard_map/pallas_call | solution.py:203
  59.8 2.5 %collective-permute-start.8 = (bf16[256,768]{1,0:T(8,128)(2,1)}, bf16[256,768]{1,0:T(8,128)(2,1)S(1)}, u32[]{:S(2)}, u32[]{:S(2)}) collective-permute-start(bf16[256,768]{1,0:T(8,128)(2,1)} %shard_map.92), channel_id=1, source_target_pairs={{0,6},{1,7},{2,4},{3,5},{4,10},{5,11},{6,8},{7,9},{8,14},{9,15},{1... | collective-permute-start | bytes 1179656 | tf_op jit(solution)/shard_map/ppermute | solution.py:47
  62.2 3.5 %collective-permute-start.6 = (bf16[256,768]{1,0:T(8,128)(2,1)}, bf16[256,768]{1,0:T(8,128)(2,1)S(1)}, u32[]{:S(2)}, u32[]{:S(2)}) collective-permute-start(bf16[256,768]{1,0:T(8,128)(2,1)} %shard_map.92), channel_id=1, source_target_pairs={{0,4},{1,5},{2,6},{3,7},{4,8},{5,9},{6,10},{7,11},{8,12},{9,13},{1... | collective-permute-start | bytes 1179656 | tf_op jit(solution)/shard_map/ppermute | solution.py:47
  65.8 6.3 %collective-permute-done.8 = bf16[256,768]{1,0:T(8,128)(2,1)S(1)} collective-permute-done((bf16[256,768]{1,0:T(8,128)(2,1)}, bf16[256,768]{1,0:T(8,128)(2,1)S(1)}, u32[]{:S(2)}, u32[]{:S(2)}) %collective-permute-start.8) | collective-permute-done | bytes 393248 | tf_op jit(solution)/shard_map/ppermute | solution.py:47
  72.1 7.5 %collective-permute-done.6 = bf16[256,768]{1,0:T(8,128)(2,1)S(1)} collective-permute-done((bf16[256,768]{1,0:T(8,128)(2,1)}, bf16[256,768]{1,0:T(8,128)(2,1)S(1)}, u32[]{:S(2)}, u32[]{:S(2)}) %collective-permute-start.6) | collective-permute-done | bytes 393248 | tf_op jit(solution)/shard_map/ppermute | solution.py:47
  79.8 1.7 collective-permute-done.9.refs_3_
  82.2 12.5 %shard_map.93 = (bf16[256,512]{1,0:T(8,128)(2,1)}, bf16[4,768,128]{2,1,0:T(8,128)(2,1)}, bf16[4,768,128]{2,1,0:T(8,128)(2,1)}) custom-call(s32[6]{0:T(128)} %get-tuple-element.67.refs_0_, bf16[256,768]{1,0:T(8,128)(2,1)} %copy-done.2, bf16[256,768]{1,0:T(8,128)(2,1)} %copy-done.4, ...), custom_call_target="tpu_custom_call", output_to_operand_aliasing={{1}: (7, {}), {2}: (8, {})} | custom-call | tf_op jit(solution)/shard_map/pallas_call | solution.py:165
  95.3 8.0 %collective-permute-done.11.refs_2_ = bf16[256,512]{1,0:T(8,128)(2,1)S(1)} collective-permute-done((bf16[256,512]{1,0:T(8,128)(2,1)}, bf16[256,512]{1,0:T(8,128)(2,1)S(1)}, u32[]{:S(2)}, u32[]{:S(2)}) %collective-permute-start.11) | collective-permute-done | bytes 262176 | tf_op jit(solution)/shard_map/ppermute | solution.py:22
  103.3 1.5 collective-permute-done.13.refs_4_
  105.6 4.1 %shard_map.94 = bf16[256,768]{1,0:T(8,128)(2,1)} custom-call(s32[6]{0:T(128)} %get-tuple-element.67.refs_0_, bf16[256,512]{1,0:T(8,128)(2,1)} %get-tuple-element.46.refs_1_, bf16[256,512]{1,0:T(8,128)(2,1)} %copy-done.21, bf16[256,512]{1,0:T(8,128)(2,1)} %copy-done.24, bf16[256,512]{1,0:T(8,128)(2,1)} %copy-done.28, bf16[4,512,768]{2,1,0:T(8,128)(2,1)} %bitcast.41, ...), custom_call_target="tpu_custom_call" | custom-call | tf_op jit(solution)/shard_map/pallas_call | solution.py:203
  109.7 4.3 %collective-permute-start.14 = (bf16[256,768]{1,0:T(8,128)(2,1)}, bf16[256,768]{1,0:T(8,128)(2,1)S(1)}, u32[]{:S(2)}, u32[]{:S(2)}) collective-permute-start(bf16[256,768]{1,0:T(8,128)(2,1)} %shard_map.94), channel_id=1, source_target_pairs={{0,4},{1,5},{2,6},{3,7},{4,8},{5,9},{6,10},{7,11},{8,12},{9,13},{1... | collective-permute-start | bytes 1179656 | tf_op jit(solution)/shard_map/ppermute | solution.py:47
  114.0 2.5 %collective-permute-start.15 = (bf16[256,768]{1,0:T(8,128)(2,1)S(1)}, bf16[256,768]{1,0:T(8,128)(2,1)S(1)}, u32[]{:S(2)}, u32[]{:S(2)}) collective-permute-start(bf16[256,768]{1,0:T(8,128)(2,1)S(1)} %get-tuple-element.47), channel_id=1, source_target_pairs={{0,2},{1,3},{2,0},{3,1},{16,18},{17,19},{18,16},{19,17}} | collective-permute-start | bytes 1179656 | tf_op jit(solution)/shard_map/ppermute | solution.py:30
  116.4 1.9 collective-permute-start.16
  118.3 5.4 %collective-permute-done.14 = bf16[256,768]{1,0:T(8,128)(2,1)S(1)} collective-permute-done((bf16[256,768]{1,0:T(8,128)(2,1)}, bf16[256,768]{1,0:T(8,128)(2,1)S(1)}, u32[]{:S(2)}, u32[]{:S(2)}) %collective-permute-start.14) | collective-permute-done | bytes 393248 | tf_op jit(solution)/shard_map/ppermute | solution.py:47
  123.9 2.9 %collective-permute-done.15 = bf16[256,768]{1,0:T(8,128)(2,1)S(1)} collective-permute-done((bf16[256,768]{1,0:T(8,128)(2,1)S(1)}, bf16[256,768]{1,0:T(8,128)(2,1)S(1)}, u32[]{:S(2)}, u32[]{:S(2)}) %collective-permute-start.15) | collective-permute-done | bytes 393248 | tf_op jit(solution)/shard_map/ppermute | solution.py:30
  126.7 4.6 %collective-permute-done.16 = bf16[256,768]{1,0:T(8,128)(2,1)S(1)} collective-permute-done((bf16[256,768]{1,0:T(8,128)(2,1)}, bf16[256,768]{1,0:T(8,128)(2,1)S(1)}, u32[]{:S(2)}, u32[]{:S(2)}) %collective-permute-start.16) | collective-permute-done | bytes 393248 | tf_op jit(solution)/shard_map/ppermute | solution.py:47
  131.5 1.7 collective-permute-done.18.refs_4_
  133.2 0.8 copy-done.16
  134.0 12.5 %shard_map.95 = (bf16[256,512]{1,0:T(8,128)(2,1)}, bf16[4,768,128]{2,1,0:T(8,128)(2,1)}, bf16[4,768,128]{2,1,0:T(8,128)(2,1)}) custom-call(s32[6]{0:T(128)} %get-tuple-element.65.refs_0_, bf16[256,768]{1,0:T(8,128)(2,1)} %copy-done.1, bf16[256,768]{1,0:T(8,128)(2,1)} %copy-done.6, ...), custom_call_target="tpu_custom_call", output_to_operand_aliasing={{1}: (7, {}), {2}: (8, {})} | custom-call | tf_op jit(solution)/shard_map/pallas_call | solution.py:165
  147.0 8.0 %collective-permute-done.19.refs_2_ = bf16[256,512]{1,0:T(8,128)(2,1)S(1)} collective-permute-done((bf16[256,512]{1,0:T(8,128)(2,1)}, bf16[256,512]{1,0:T(8,128)(2,1)S(1)}, u32[]{:S(2)}, u32[]{:S(2)}) %collective-permute-start.19) | collective-permute-done | bytes 262176 | tf_op jit(solution)/shard_map/ppermute | solution.py:22
  155.1 1.5 collective-permute-done.21.refs_4_
  157.3 4.1 %shard_map.96 = bf16[256,768]{1,0:T(8,128)(2,1)} custom-call(s32[6]{0:T(128)} %get-tuple-element.65.refs_0_, bf16[256,512]{1,0:T(8,128)(2,1)} %get-tuple-element.54.refs_1_, bf16[256,512]{1,0:T(8,128)(2,1)} %copy-done.22, bf16[256,512]{1,0:T(8,128)(2,1)} %copy-done.25, bf16[256,512]{1,0:T(8,128)(2,1)} %copy-done.29, bf16[4,512,768]{2,1,0:T(8,128)(2,1)} %bitcast.42, ...), custom_call_target="tpu_custom_call" | custom-call | tf_op jit(solution)/shard_map/pallas_call | solution.py:203
  161.4 4.3 %collective-permute-start.22 = (bf16[256,768]{1,0:T(8,128)(2,1)}, bf16[256,768]{1,0:T(8,128)(2,1)S(1)}, u32[]{:S(2)}, u32[]{:S(2)}) collective-permute-start(bf16[256,768]{1,0:T(8,128)(2,1)} %shard_map.96), channel_id=1, source_target_pairs={{0,4},{1,5},{2,6},{3,7},{4,8},{5,9},{6,10},{7,11},{8,12},{9,13},{1... | collective-permute-start | bytes 1179656 | tf_op jit(solution)/shard_map/ppermute | solution.py:47
  165.7 3.4 %collective-permute-start.23 = (bf16[256,768]{1,0:T(8,128)(2,1)S(1)}, bf16[256,768]{1,0:T(8,128)(2,1)S(1)}, u32[]{:S(2)}, u32[]{:S(2)}) collective-permute-start(bf16[256,768]{1,0:T(8,128)(2,1)S(1)} %get-tuple-element.55), channel_id=1, source_target_pairs={{0,2},{1,3},{2,0},{3,1},{16,18},{17,19},{18,16},{19,17}} | collective-permute-start | bytes 1179656 | tf_op jit(solution)/shard_map/ppermute | solution.py:30
  169.1 1.7 collective-permute-start.24
  170.8 4.7 %collective-permute-done.22 = bf16[256,768]{1,0:T(8,128)(2,1)S(1)} collective-permute-done((bf16[256,768]{1,0:T(8,128)(2,1)}, bf16[256,768]{1,0:T(8,128)(2,1)S(1)}, u32[]{:S(2)}, u32[]{:S(2)}) %collective-permute-start.22) | collective-permute-done | bytes 393248 | tf_op jit(solution)/shard_map/ppermute | solution.py:47
  175.6 2.9 %collective-permute-done.23 = bf16[256,768]{1,0:T(8,128)(2,1)S(1)} collective-permute-done((bf16[256,768]{1,0:T(8,128)(2,1)S(1)}, bf16[256,768]{1,0:T(8,128)(2,1)S(1)}, u32[]{:S(2)}, u32[]{:S(2)}) %collective-permute-start.23) | collective-permute-done | bytes 393248 | tf_op jit(solution)/shard_map/ppermute | solution.py:30
  178.5 4.6 %collective-permute-done.24 = bf16[256,768]{1,0:T(8,128)(2,1)S(1)} collective-permute-done((bf16[256,768]{1,0:T(8,128)(2,1)}, bf16[256,768]{1,0:T(8,128)(2,1)S(1)}, u32[]{:S(2)}, u32[]{:S(2)}) %collective-permute-start.24) | collective-permute-done | bytes 393248 | tf_op jit(solution)/shard_map/ppermute | solution.py:47
  183.2 1.7 collective-permute-done.26.refs_4_
  185.7 12.5 %shard_map.97 = (bf16[256,512]{1,0:T(8,128)(2,1)}, bf16[4,768,128]{2,1,0:T(8,128)(2,1)}, bf16[4,768,128]{2,1,0:T(8,128)(2,1)}) custom-call(s32[6]{0:T(128)} %get-tuple-element.66.refs_0_, bf16[256,768]{1,0:T(8,128)(2,1)} %copy-done, bf16[256,768]{1,0:T(8,128)(2,1)} %copy-done.5, ...), custom_call_target="tpu_custom_call", output_to_operand_aliasing={{1}: (7, {}), {2}: (8, {})} | custom-call | tf_op jit(solution)/shard_map/pallas_call | solution.py:165
  198.2 1.5 collective-permute-start.27
  199.8 7.1 %collective-permute-done.27.refs_2_ = bf16[256,512]{1,0:T(8,128)(2,1)S(1)} collective-permute-done((bf16[256,512]{1,0:T(8,128)(2,1)}, bf16[256,512]{1,0:T(8,128)(2,1)S(1)}, u32[]{:S(2)}, u32[]{:S(2)}) %collective-permute-start.27) | collective-permute-done | bytes 262176 | tf_op jit(solution)/shard_map/ppermute | solution.py:22
  206.9 1.5 collective-permute-done.29.refs_4_
  209.1 4.1 %shard_map.98 = bf16[256,768]{1,0:T(8,128)(2,1)} custom-call(s32[6]{0:T(128)} %get-tuple-element.66.refs_0_, bf16[256,512]{1,0:T(8,128)(2,1)} %get-tuple-element.58.refs_1_, bf16[256,512]{1,0:T(8,128)(2,1)} %copy-done.23, bf16[256,512]{1,0:T(8,128)(2,1)} %copy-done.26, bf16[256,512]{1,0:T(8,128)(2,1)} %copy-done.30, bf16[4,512,768]{2,1,0:T(8,128)(2,1)} %bitcast.43, ...), custom_call_target="tpu_custom_call" | custom-call | tf_op jit(solution)/shard_map/pallas_call | solution.py:203
  213.2 2.3 %maximum_bitcast_fusion = bf16[4,1,256,768]{3,2,1,0:T(8,128)(2,1)} fusion(bf16[1,256,768]{2,1,0:T(8,128)(2,1)} %bitcast.47, bf16[1,256,768]{2,1,0:T(8,128)(2,1)S(1)} %bitcast.46, bf16[1,256,768]{2,1,0:T(8,128)(2,1)S(1)} %bitcast.45, bf16[1,256,768]{2,1,0:T(8,128)(2,1)S(1)} %bitcast.44), kind=kLoop, calls=%fused_computation.3 | loop fusion | flops 2359296 | bytes 3145728 | tf_op jit(solution)/shard_map/broadcast_in_dim | solution.py:290
  (107 shorter events, 9.8 us)
Async XLA Ops:
  15.5 13.9 %copy-start.3 = (bf16[256,768]{1,0:T(8,128)(2,1)}, bf16[256,768]{1,0:T(8,128)(2,1)S(1)}, u32[]{:S(2)}) copy-start(bf16[256,768]{1,0:T(8,128)(2,1)S(1)} %get-tuple-element.34.refs_1_.refs_6_) | copy-start | bytes 1179652
  15.5 12.1 %collective-permute-start = (bf16[256,768]{1,0:T(8,128)(2,1)S(1)}, bf16[256,768]{1,0:T(8,128)(2,1)S(1)}, u32[]{:S(2)}, u32[]{:S(2)}) collective-permute-start(bf16[256,768]{1,0:T(8,128)(2,1)S(1)} %get-tuple-element.34.refs_1_.refs_6_), channel_id=1, source_target_pairs={{0,2},{1,3},{2,0},{3,1},{4,6},{5,7},{6,4},{7,5},{8,10},{9,11},{10,... | collective-permute-start | bytes 1179656 | tf_op jit(solution)/shard_map/ppermute | solution.py:22
  18.5 9.8 %collective-permute-start.1 = (bf16[256,768]{1,0:T(8,128)(2,1)S(1)}, bf16[256,768]{1,0:T(8,128)(2,1)S(1)}, u32[]{:S(2)}, u32[]{:S(2)}) collective-permute-start(bf16[256,768]{1,0:T(8,128)(2,1)S(1)} %get-tuple-element.34.refs_1_.refs_6_), channel_id=1, source_target_pairs={{0,1},{1,0},{2,3},{3,2},{4,5},{5,4},{6,7},{7,6},{8,9},{9,8},{10,11... | collective-permute-start | bytes 1179656 | tf_op jit(solution)/shard_map/ppermute | solution.py:40
  27.6 1.7 copy-start.12
  27.6 1.7 collective-permute-start.2
  42.7 8.5 %collective-permute-start.3 = (bf16[256,512]{1,0:T(8,128)(2,1)}, bf16[256,512]{1,0:T(8,128)(2,1)S(1)}, u32[]{:S(2)}, u32[]{:S(2)}) collective-permute-start(bf16[256,512]{1,0:T(8,128)(2,1)} %get-tuple-element.38.refs_1_), channel_id=1, source_target_pairs={{0,2},{1,3},{2,0},{3,1},{4,6},{5,7},{6,4},{7,5},{8,10},{9,11},{10,... | collective-permute-start | bytes 786440 | tf_op jit(solution)/shard_map/ppermute | solution.py:22
  44.4 10.5 %collective-permute-start.4 = (bf16[256,512]{1,0:T(8,128)(2,1)}, bf16[256,512]{1,0:T(8,128)(2,1)S(1)}, u32[]{:S(2)}, u32[]{:S(2)}) collective-permute-start(bf16[256,512]{1,0:T(8,128)(2,1)} %get-tuple-element.38.refs_1_), channel_id=1, source_target_pairs={{0,1},{1,0},{2,3},{3,2},{4,5},{5,4},{6,7},{7,6},{8,9},{9,8},{10,11... | collective-permute-start | bytes 786440 | tf_op jit(solution)/shard_map/ppermute | solution.py:40
  51.2 3.7 %copy-start.19 = (bf16[256,512]{1,0:T(8,128)(2,1)}, bf16[256,512]{1,0:T(8,128)(2,1)S(1)}, u32[]{:S(2)}) copy-start(bf16[256,512]{1,0:T(8,128)(2,1)S(1)} %collective-permute-done.3.refs_2_) | copy-start | bytes 786436
  51.2 3.7 %collective-permute-start.5 = (bf16[256,512]{1,0:T(8,128)(2,1)S(1)}, bf16[256,512]{1,0:T(8,128)(2,1)S(1)}, u32[]{:S(2)}, u32[]{:S(2)}) collective-permute-start(bf16[256,512]{1,0:T(8,128)(2,1)S(1)} %collective-permute-done.3.refs_2_), channel_id=1, source_target_pairs={{0,1},{1,0},{2,3},{3,2},{4,5},{5,4},{6,7},{7,6},{8,9},{9,8},{10,11... | collective-permute-start | bytes 786440 | tf_op jit(solution)/shard_map/ppermute | solution.py:40
  51.2 14.5 %collective-permute-start.7 = (bf16[256,768]{1,0:T(8,128)(2,1)S(1)}, bf16[256,768]{1,0:T(8,128)(2,1)S(1)}, u32[]{:S(2)}, u32[]{:S(2)}) collective-permute-start(bf16[256,768]{1,0:T(8,128)(2,1)S(1)} %get-tuple-element.39), channel_id=1, source_target_pairs={{0,2},{1,3},{2,0},{3,1},{16,18},{17,19},{18,16},{19,17}} | collective-permute-start | bytes 1179656 | tf_op jit(solution)/shard_map/ppermute | solution.py:30
  59.8 12.2 %collective-permute-start.8 = (bf16[256,768]{1,0:T(8,128)(2,1)}, bf16[256,768]{1,0:T(8,128)(2,1)S(1)}, u32[]{:S(2)}, u32[]{:S(2)}) collective-permute-start(bf16[256,768]{1,0:T(8,128)(2,1)} %shard_map.92), channel_id=1, source_target_pairs={{0,6},{1,7},{2,4},{3,5},{4,10},{5,11},{6,8},{7,9},{8,14},{9,15},{1... | collective-permute-start | bytes 1179656 | tf_op jit(solution)/shard_map/ppermute | solution.py:47
  62.2 17.4 %collective-permute-start.6 = (bf16[256,768]{1,0:T(8,128)(2,1)}, bf16[256,768]{1,0:T(8,128)(2,1)S(1)}, u32[]{:S(2)}, u32[]{:S(2)}) collective-permute-start(bf16[256,768]{1,0:T(8,128)(2,1)} %shard_map.92), channel_id=1, source_target_pairs={{0,4},{1,5},{2,6},{3,7},{4,8},{5,9},{6,10},{7,11},{8,12},{9,13},{1... | collective-permute-start | bytes 1179656 | tf_op jit(solution)/shard_map/ppermute | solution.py:47
  72.1 9.4 %copy-start.4 = (bf16[256,768]{1,0:T(8,128)(2,1)}, bf16[256,768]{1,0:T(8,128)(2,1)S(1)}, u32[]{:S(2)}) copy-start(bf16[256,768]{1,0:T(8,128)(2,1)S(1)} %broadcast_select_fusion.4.refs_2_) | copy-start | bytes 1179652
  72.1 7.7 %collective-permute-start.10 = (bf16[256,768]{1,0:T(8,128)(2,1)S(1)}, bf16[256,768]{1,0:T(8,128)(2,1)S(1)}, u32[]{:S(2)}, u32[]{:S(2)}) collective-permute-start(bf16[256,768]{1,0:T(8,128)(2,1)S(1)} %broadcast_select_fusion.4.refs_2_), channel_id=1, source_target_pairs={{0,1},{1,0},{2,3},{3,2},{4,5},{5,4},{6,7},{7,6},{8,9},{9,8},{10,11... | collective-permute-start | bytes 1179656 | tf_op jit(solution)/shard_map/ppermute | solution.py:40
  79.7 1.8 copy-start.2
  79.7 1.8 collective-permute-start.9
  79.8 1.7 copy-start.14
  94.8 8.6 %collective-permute-start.11 = (bf16[256,512]{1,0:T(8,128)(2,1)}, bf16[256,512]{1,0:T(8,128)(2,1)S(1)}, u32[]{:S(2)}, u32[]{:S(2)}) collective-permute-start(bf16[256,512]{1,0:T(8,128)(2,1)} %get-tuple-element.46.refs_1_), channel_id=1, source_target_pairs={{0,2},{1,3},{2,0},{3,1},{4,6},{5,7},{6,4},{7,5},{8,10},{9,11},{10,... | collective-permute-start | bytes 786440 | tf_op jit(solution)/shard_map/ppermute | solution.py:22
  95.3 8.0 %collective-permute-start.12 = (bf16[256,512]{1,0:T(8,128)(2,1)}, bf16[256,512]{1,0:T(8,128)(2,1)S(1)}, u32[]{:S(2)}, u32[]{:S(2)}) collective-permute-start(bf16[256,512]{1,0:T(8,128)(2,1)} %get-tuple-element.46.refs_1_), channel_id=1, source_target_pairs={{0,1},{1,0},{2,3},{3,2},{4,5},{5,4},{6,7},{7,6},{8,9},{9,8},{10,11... | collective-permute-start | bytes 786440 | tf_op jit(solution)/shard_map/ppermute | solution.py:40
  103.3 1.5 copy-start.21
  103.3 1.5 collective-permute-start.13
  109.7 14.1 %collective-permute-start.14 = (bf16[256,768]{1,0:T(8,128)(2,1)}, bf16[256,768]{1,0:T(8,128)(2,1)S(1)}, u32[]{:S(2)}, u32[]{:S(2)}) collective-permute-start(bf16[256,768]{1,0:T(8,128)(2,1)} %shard_map.94), channel_id=1, source_target_pairs={{0,4},{1,5},{2,6},{3,7},{4,8},{5,9},{6,10},{7,11},{8,12},{9,13},{1... | collective-permute-start | bytes 1179656 | tf_op jit(solution)/shard_map/ppermute | solution.py:47
  114.0 12.8 %collective-permute-start.15 = (bf16[256,768]{1,0:T(8,128)(2,1)S(1)}, bf16[256,768]{1,0:T(8,128)(2,1)S(1)}, u32[]{:S(2)}, u32[]{:S(2)}) collective-permute-start(bf16[256,768]{1,0:T(8,128)(2,1)S(1)} %get-tuple-element.47), channel_id=1, source_target_pairs={{0,2},{1,3},{2,0},{3,1},{16,18},{17,19},{18,16},{19,17}} | collective-permute-start | bytes 1179656 | tf_op jit(solution)/shard_map/ppermute | solution.py:30
  116.4 14.9 %collective-permute-start.16 = (bf16[256,768]{1,0:T(8,128)(2,1)}, bf16[256,768]{1,0:T(8,128)(2,1)S(1)}, u32[]{:S(2)}, u32[]{:S(2)}) collective-permute-start(bf16[256,768]{1,0:T(8,128)(2,1)} %shard_map.94), channel_id=1, source_target_pairs={{0,6},{1,7},{2,4},{3,5},{4,10},{5,11},{6,8},{7,9},{8,14},{9,15},{1... | collective-permute-start | bytes 1179656 | tf_op jit(solution)/shard_map/ppermute | solution.py:47
  123.8 9.4 %copy-start.1 = (bf16[256,768]{1,0:T(8,128)(2,1)}, bf16[256,768]{1,0:T(8,128)(2,1)S(1)}, u32[]{:S(2)}) copy-start(bf16[256,768]{1,0:T(8,128)(2,1)S(1)} %broadcast_select_fusion.3.refs_1_.refs_6_) | copy-start | bytes 1179652
  123.8 7.7 %collective-permute-start.17 = (bf16[256,768]{1,0:T(8,128)(2,1)S(1)}, bf16[256,768]{1,0:T(8,128)(2,1)S(1)}, u32[]{:S(2)}, u32[]{:S(2)}) collective-permute-start(bf16[256,768]{1,0:T(8,128)(2,1)S(1)} %broadcast_select_fusion.3.refs_1_.refs_6_), channel_id=1, source_target_pairs={{0,1},{1,0},{2,3},{3,2},{4,5},{5,4},{6,7},{7,6},{8,9},{9,8},{10,11... | collective-permute-start | bytes 1179656 | tf_op jit(solution)/shard_map/ppermute | solution.py:40
  131.4 1.8 copy-start.6
  131.4 1.8 collective-permute-start.18
  131.5 1.7 copy-start.11
  146.5 8.6 %collective-permute-start.19 = (bf16[256,512]{1,0:T(8,128)(2,1)}, bf16[256,512]{1,0:T(8,128)(2,1)S(1)}, u32[]{:S(2)}, u32[]{:S(2)}) collective-permute-start(bf16[256,512]{1,0:T(8,128)(2,1)} %get-tuple-element.54.refs_1_), channel_id=1, source_target_pairs={{0,2},{1,3},{2,0},{3,1},{4,6},{5,7},{6,4},{7,5},{8,10},{9,11},{10,... | collective-permute-start | bytes 786440 | tf_op jit(solution)/shard_map/ppermute | solution.py:22
  147.0 8.0 %collective-permute-start.20 = (bf16[256,512]{1,0:T(8,128)(2,1)}, bf16[256,512]{1,0:T(8,128)(2,1)S(1)}, u32[]{:S(2)}, u32[]{:S(2)}) collective-permute-start(bf16[256,512]{1,0:T(8,128)(2,1)} %get-tuple-element.54.refs_1_), channel_id=1, source_target_pairs={{0,1},{1,0},{2,3},{3,2},{4,5},{5,4},{6,7},{7,6},{8,9},{9,8},{10,11... | collective-permute-start | bytes 786440 | tf_op jit(solution)/shard_map/ppermute | solution.py:40
  155.0 1.5 copy-start.22
  155.0 1.5 collective-permute-start.21
  161.4 14.0 %collective-permute-start.22 = (bf16[256,768]{1,0:T(8,128)(2,1)}, bf16[256,768]{1,0:T(8,128)(2,1)S(1)}, u32[]{:S(2)}, u32[]{:S(2)}) collective-permute-start(bf16[256,768]{1,0:T(8,128)(2,1)} %shard_map.96), channel_id=1, source_target_pairs={{0,4},{1,5},{2,6},{3,7},{4,8},{5,9},{6,10},{7,11},{8,12},{9,13},{1... | collective-permute-start | bytes 1179656 | tf_op jit(solution)/shard_map/ppermute | solution.py:47
  165.7 12.8 %collective-permute-start.23 = (bf16[256,768]{1,0:T(8,128)(2,1)S(1)}, bf16[256,768]{1,0:T(8,128)(2,1)S(1)}, u32[]{:S(2)}, u32[]{:S(2)}) collective-permute-start(bf16[256,768]{1,0:T(8,128)(2,1)S(1)} %get-tuple-element.55), channel_id=1, source_target_pairs={{0,2},{1,3},{2,0},{3,1},{16,18},{17,19},{18,16},{19,17}} | collective-permute-start | bytes 1179656 | tf_op jit(solution)/shard_map/ppermute | solution.py:30
  169.1 14.0 %collective-permute-start.24 = (bf16[256,768]{1,0:T(8,128)(2,1)}, bf16[256,768]{1,0:T(8,128)(2,1)S(1)}, u32[]{:S(2)}, u32[]{:S(2)}) collective-permute-start(bf16[256,768]{1,0:T(8,128)(2,1)} %shard_map.96), channel_id=1, source_target_pairs={{0,6},{1,7},{2,4},{3,5},{4,10},{5,11},{6,8},{7,9},{8,14},{9,15},{1... | collective-permute-start | bytes 1179656 | tf_op jit(solution)/shard_map/ppermute | solution.py:47
  175.5 9.4 %copy-start = (bf16[256,768]{1,0:T(8,128)(2,1)}, bf16[256,768]{1,0:T(8,128)(2,1)S(1)}, u32[]{:S(2)}) copy-start(bf16[256,768]{1,0:T(8,128)(2,1)S(1)} %broadcast_select_fusion.1.refs_1_.refs_6_) | copy-start | bytes 1179652
  175.5 7.7 %collective-permute-start.25 = (bf16[256,768]{1,0:T(8,128)(2,1)S(1)}, bf16[256,768]{1,0:T(8,128)(2,1)S(1)}, u32[]{:S(2)}, u32[]{:S(2)}) collective-permute-start(bf16[256,768]{1,0:T(8,128)(2,1)S(1)} %broadcast_select_fusion.1.refs_1_.refs_6_), channel_id=1, source_target_pairs={{0,1},{1,0},{2,3},{3,2},{4,5},{5,4},{6,7},{7,6},{8,9},{9,8},{10,11... | collective-permute-start | bytes 1179656 | tf_op jit(solution)/shard_map/ppermute | solution.py:40
  183.1 1.8 copy-start.5
  183.1 1.8 collective-permute-start.26
  183.2 1.7 copy-start.10
  198.2 15.0 %copy-start.7 = (bf16[256,768]{1,0:T(8,128)(2,1)S(1)}, bf16[256,768]{1,0:T(8,128)(2,1)}, u32[]{:S(2)}) copy-start(bf16[256,768]{1,0:T(8,128)(2,1)} %shard_map.92) | copy-start | bytes 1179652
  198.2 15.0 %copy-start.8 = (bf16[256,768]{1,0:T(8,128)(2,1)S(1)}, bf16[256,768]{1,0:T(8,128)(2,1)}, u32[]{:S(2)}) copy-start(bf16[256,768]{1,0:T(8,128)(2,1)} %shard_map.94) | copy-start | bytes 1179652
  198.2 15.0 %copy-start.9 = (bf16[256,768]{1,0:T(8,128)(2,1)S(1)}, bf16[256,768]{1,0:T(8,128)(2,1)}, u32[]{:S(2)}) copy-start(bf16[256,768]{1,0:T(8,128)(2,1)} %shard_map.96) | copy-start | bytes 1179652
  198.2 8.6 %collective-permute-start.27 = (bf16[256,512]{1,0:T(8,128)(2,1)}, bf16[256,512]{1,0:T(8,128)(2,1)S(1)}, u32[]{:S(2)}, u32[]{:S(2)}) collective-permute-start(bf16[256,512]{1,0:T(8,128)(2,1)} %get-tuple-element.58.refs_1_), channel_id=1, source_target_pairs={{0,2},{1,3},{2,0},{3,1},{4,6},{5,7},{6,4},{7,5},{8,10},{9,11},{10,... | collective-permute-start | bytes 786440 | tf_op jit(solution)/shard_map/ppermute | solution.py:22
  199.8 7.1 %collective-permute-start.28 = (bf16[256,512]{1,0:T(8,128)(2,1)}, bf16[256,512]{1,0:T(8,128)(2,1)S(1)}, u32[]{:S(2)}, u32[]{:S(2)}) collective-permute-start(bf16[256,512]{1,0:T(8,128)(2,1)} %get-tuple-element.58.refs_1_), channel_id=1, source_target_pairs={{0,1},{1,0},{2,3},{3,2},{4,5},{5,4},{6,7},{7,6},{8,9},{9,8},{10,11... | collective-permute-start | bytes 786440 | tf_op jit(solution)/shard_map/ppermute | solution.py:40
  206.9 1.5 copy-start.23
  206.9 1.5 collective-permute-start.29
  (13 other events, 12.3 us)

commit v16 on v9

--- a/solution.py
+++ b/solution.py
@@ -249,10 +249,10 @@
         own_rows,
         0,
     )
-    tables, own_rows = lax.optimization_barrier(
-        (kernel_tables(patch_sizes_list, section_index), own_rows)
-    )
     row_parts = [own_rows] + across_chips(own_rows)
+    tables, row_parts = lax.optimization_barrier(
+        (kernel_tables(patch_sizes_list, section_index), row_parts)
+    )
     for turn_number in range(patches):
         where = tables[turn_number]
         head_rows, key_cache, value_cache = attend_block(

time: 212 us -> 212 us (level)
  transfers between devices with their start and end apart: 30 -> 30, of which waited for: 22 -> 23; matrix products, arithmetic and copies ran while one was open for 2% -> 3% of each run, Pallas kernels for 0% -> 0%
where the time goes in v16:
time: 212 us; the launch traced here: 211 us
  waiting for transfers between devices  82.6 us (39%)
  Pallas kernels  66.6 us (31%)
  starting transfers between devices  37.8 us (18%)
  other arithmetic  9.93 us (5%)
  local copies, waits for them, and re-layouts  7.81 us (4%)
  between operations  6.34 us (3%)
    pallas_call x4, Pallas kernels, attend_block(): pl.pallas_call(block_kernel, grid_spec=grid_spec, out_shape=[jax.ShapeDty...  50.1 us
    ppermute x5, waiting for transfers between devices, across_chips(): lax.ppermute(block, 'seq', [(source, (source + step) % count) for source...  36.2 us
    ppermute x6, waiting for transfers between devices, to_next_section(): lax.ppermute(block, ('section', 'seq'), [(section * count + source, (sect...  21.3 us
    ppermute x6, starting transfers between devices, to_next_section(): lax.ppermute(block, ('section', 'seq'), [(section * count + source, (sect...  16.6 us
    pallas_call x4, Pallas kernels, leave_block(): pl.pallas_call(exit_kernel, in_specs=[smem] + [vmem] * (count + 3), out_s...  16.5 us
    ppermute x3, waiting for transfers between devices, across_chips_first_section(): lax.ppermute(block, ('section', 'seq'), [(source, (source + step) % count...  12.8 us
    ppermute x16, waiting for transfers between devices, with_partner(): return parts + [lax.ppermute(part, 'seq', to_partner) for part in parts]  12.3 us
    ppermute x3, starting transfers between devices, across_chips_first_section(): lax.ppermute(block, ('section', 'seq'), [(source, (source + step) % count...  10.9 us
  transfers between devices with their start and end apart: 30, of which 23 were waited for; matrix products, arithmetic and copies ran while one was open for 3% of the time, Pallas kernels for 0%

profile of v16, /device:TPU:0, one launch (start us, length us, event | category | flops | bytes accessed | tf_op | source)
XLA Modules:
  0.0 211.1 jit_solution(9432817659866966165)
XLA Ops:
  0.0 0.8 reduce-window.9
  0.8 1.3 bitcast_subtract_fusion
  2.8 1.2 fusion.3.refs_1_.refs_6_
  4.0 3.0 %collective-permute-start = (bf16[256,768]{1,0:T(8,128)(2,1)S(1)}, bf16[256,768]{1,0:T(8,128)(2,1)S(1)}, u32[]{:S(2)}, u32[]{:S(2)}) collective-permute-start(bf16[256,768]{1,0:T(8,128)(2,1)S(1)} %fusion.3.refs_1_.refs_6_), channel_id=1, source_target_pairs={{0,2},{1,3},{2,0},{3,1},{4,6},{5,7},{6,4},{7,5},{8,10},{9,11},{10,... | collective-permute-start | bytes 1179656 | tf_op jit(solution)/shard_map/ppermute | solution.py:22
  7.9 8.2 %collective-permute-done.refs_2_ = bf16[256,768]{1,0:T(8,128)(2,1)S(1)} collective-permute-done((bf16[256,768]{1,0:T(8,128)(2,1)S(1)}, bf16[256,768]{1,0:T(8,128)(2,1)S(1)}, u32[]{:S(2)}, u32[]{:S(2)}) %collective-permute-start) | collective-permute-done | bytes 393248 | tf_op jit(solution)/shard_map/ppermute | solution.py:22
  19.2 12.5 %shard_map.91 = (bf16[256,512]{1,0:T(8,128)(2,1)}, bf16[4,768,128]{2,1,0:T(8,128)(2,1)}, bf16[4,768,128]{2,1,0:T(8,128)(2,1)}) custom-call(s32[6]{0:T(128)} %get-tuple-element.39.refs_0_, bf16[256,768]{1,0:T(8,128)(2,1)} %copy-done.4, bf16[256,768]{1,0:T(8,128)(2,1)} %copy-done.11, bf16[256,768]{1,0:T(8,128)(2,1)} %copy-done.16, ...), custom_call_target="tpu_custom_call" | custom-call | tf_op jit(solution)/shard_map/pallas_call | solution.py:165
  31.7 1.7 collective-permute-start.3
  33.4 6.8 %collective-permute-done.3.refs_2_ = bf16[256,512]{1,0:T(8,128)(2,1)S(1)} collective-permute-done((bf16[256,512]{1,0:T(8,128)(2,1)}, bf16[256,512]{1,0:T(8,128)(2,1)S(1)}, u32[]{:S(2)}, u32[]{:S(2)}) %collective-permute-start.3) | collective-permute-done | bytes 262176 | tf_op jit(solution)/shard_map/ppermute | solution.py:22
  40.3 1.5 collective-permute-done.5.refs_4_
  42.5 4.2 %shard_map.92 = bf16[256,768]{1,0:T(8,128)(2,1)} custom-call(s32[6]{0:T(128)} %get-tuple-element.39.refs_0_, bf16[256,512]{1,0:T(8,128)(2,1)} %get-tuple-element.21.refs_1_, bf16[256,512]{1,0:T(8,128)(2,1)} %copy-done.20, bf16[256,512]{1,0:T(8,128)(2,1)} %copy-done.24, bf16[256,512]{1,0:T(8,128)(2,1)} %copy-done.28, bf16[4,512,768]{2,1,0:T(8,128)(2,1)} %bitcast.40, ...), custom_call_target="tpu_custom_call" | custom-call | tf_op jit(solution)/shard_map/pallas_call | solution.py:203
  46.7 3.7 %collective-permute-start.6 = (bf16[256,768]{1,0:T(8,128)(2,1)}, bf16[256,768]{1,0:T(8,128)(2,1)S(1)}, u32[]{:S(2)}, u32[]{:S(2)}) collective-permute-start(bf16[256,768]{1,0:T(8,128)(2,1)} %shard_map.92), channel_id=1, source_target_pairs={{0,4},{1,5},{2,6},{3,7},{4,8},{5,9},{6,10},{7,11},{8,12},{9,13},{1... | collective-permute-start | bytes 1179656 | tf_op jit(solution)/shard_map/ppermute | solution.py:47
  54.4 4.4 %collective-permute-start.8 = (bf16[256,768]{1,0:T(8,128)(2,1)}, bf16[256,768]{1,0:T(8,128)(2,1)S(1)}, u32[]{:S(2)}, u32[]{:S(2)}) collective-permute-start(bf16[256,768]{1,0:T(8,128)(2,1)} %shard_map.92), channel_id=1, source_target_pairs={{0,6},{1,7},{2,4},{3,5},{4,10},{5,11},{6,8},{7,9},{8,14},{9,15},{1... | collective-permute-start | bytes 1179656 | tf_op jit(solution)/shard_map/ppermute | solution.py:47
  58.8 0.9 collective-permute-done.6
  59.9 3.9 %collective-permute-start.7 = (bf16[256,768]{1,0:T(8,128)(2,1)S(1)}, bf16[256,768]{1,0:T(8,128)(2,1)S(1)}, u32[]{:S(2)}, u32[]{:S(2)}) collective-permute-start(bf16[256,768]{1,0:T(8,128)(2,1)S(1)} %get-tuple-element.38), channel_id=1, source_target_pairs={{0,2},{1,3},{2,0},{3,1},{16,18},{17,19},{18,16},{19,17}} | collective-permute-start | bytes 1179656 | tf_op jit(solution)/shard_map/ppermute | solution.py:30
  63.9 3.9 %collective-permute-done.8 = bf16[256,768]{1,0:T(8,128)(2,1)S(1)} collective-permute-done((bf16[256,768]{1,0:T(8,128)(2,1)}, bf16[256,768]{1,0:T(8,128)(2,1)S(1)}, u32[]{:S(2)}, u32[]{:S(2)}) %collective-permute-start.8) | collective-permute-done | bytes 393248 | tf_op jit(solution)/shard_map/ppermute | solution.py:47
  67.8 4.1 %collective-permute-done.7 = bf16[256,768]{1,0:T(8,128)(2,1)S(1)} collective-permute-done((bf16[256,768]{1,0:T(8,128)(2,1)S(1)}, bf16[256,768]{1,0:T(8,128)(2,1)S(1)}, u32[]{:S(2)}, u32[]{:S(2)}) %collective-permute-start.7) | collective-permute-done | bytes 393248 | tf_op jit(solution)/shard_map/ppermute | solution.py:30
  72.0 1.7 collective-permute-done.10.refs_4_
  73.7 0.8 copy-done.18
  74.5 12.5 %shard_map.93 = (bf16[256,512]{1,0:T(8,128)(2,1)}, bf16[4,768,128]{2,1,0:T(8,128)(2,1)}, bf16[4,768,128]{2,1,0:T(8,128)(2,1)}) custom-call(s32[6]{0:T(128)} %get-tuple-element.42.refs_0_, bf16[256,768]{1,0:T(8,128)(2,1)} %copy-done.2, bf16[256,768]{1,0:T(8,128)(2,1)} %copy-done.6, ...), custom_call_target="tpu_custom_call", output_to_operand_aliasing={{1}: (7, {}), {2}: (8, {})} | custom-call | tf_op jit(solution)/shard_map/pallas_call | solution.py:165
  87.0 1.5 collective-permute-start.11
  88.5 7.1 %collective-permute-done.11.refs_2_ = bf16[256,512]{1,0:T(8,128)(2,1)S(1)} collective-permute-done((bf16[256,512]{1,0:T(8,128)(2,1)}, bf16[256,512]{1,0:T(8,128)(2,1)S(1)}, u32[]{:S(2)}, u32[]{:S(2)}) %collective-permute-start.11) | collective-permute-done | bytes 262176 | tf_op jit(solution)/shard_map/ppermute | solution.py:22
  95.6 1.5 collective-permute-done.13.refs_4_
  97.8 4.1 %shard_map.94 = bf16[256,768]{1,0:T(8,128)(2,1)} custom-call(s32[6]{0:T(128)} %get-tuple-element.42.refs_0_, bf16[256,512]{1,0:T(8,128)(2,1)} %get-tuple-element.24.refs_1_, bf16[256,512]{1,0:T(8,128)(2,1)} %copy-done.21, bf16[256,512]{1,0:T(8,128)(2,1)} %copy-done.25, bf16[256,512]{1,0:T(8,128)(2,1)} %copy-done.29, bf16[4,512,768]{2,1,0:T(8,128)(2,1)} %bitcast.41, ...), custom_call_target="tpu_custom_call" | custom-call | tf_op jit(solution)/shard_map/pallas_call | solution.py:203
  101.9 1.3 collective-permute-start.14
  105.9 3.3 %collective-permute-start.16 = (bf16[256,768]{1,0:T(8,128)(2,1)}, bf16[256,768]{1,0:T(8,128)(2,1)S(1)}, u32[]{:S(2)}, u32[]{:S(2)}) collective-permute-start(bf16[256,768]{1,0:T(8,128)(2,1)} %shard_map.94), channel_id=1, source_target_pairs={{0,6},{1,7},{2,4},{3,5},{4,10},{5,11},{6,8},{7,9},{8,14},{9,15},{1... | collective-permute-start | bytes 1179656 | tf_op jit(solution)/shard_map/ppermute | solution.py:47
  109.2 3.7 %collective-permute-done.14 = bf16[256,768]{1,0:T(8,128)(2,1)S(1)} collective-permute-done((bf16[256,768]{1,0:T(8,128)(2,1)}, bf16[256,768]{1,0:T(8,128)(2,1)S(1)}, u32[]{:S(2)}, u32[]{:S(2)}) %collective-permute-start.14) | collective-permute-done | bytes 393248 | tf_op jit(solution)/shard_map/ppermute | solution.py:47
  113.2 3.6 %collective-permute-start.15 = (bf16[256,768]{1,0:T(8,128)(2,1)S(1)}, bf16[256,768]{1,0:T(8,128)(2,1)S(1)}, u32[]{:S(2)}, u32[]{:S(2)}) collective-permute-start(bf16[256,768]{1,0:T(8,128)(2,1)S(1)} %get-tuple-element.36), channel_id=1, source_target_pairs={{0,2},{1,3},{2,0},{3,1},{16,18},{17,19},{18,16},{19,17}} | collective-permute-start | bytes 1179656 | tf_op jit(solution)/shard_map/ppermute | solution.py:30
  116.9 4.0 %collective-permute-done.16 = bf16[256,768]{1,0:T(8,128)(2,1)S(1)} collective-permute-done((bf16[256,768]{1,0:T(8,128)(2,1)}, bf16[256,768]{1,0:T(8,128)(2,1)S(1)}, u32[]{:S(2)}, u32[]{:S(2)}) %collective-permute-start.16) | collective-permute-done | bytes 393248 | tf_op jit(solution)/shard_map/ppermute | solution.py:47
  120.9 4.4 %collective-permute-done.15 = bf16[256,768]{1,0:T(8,128)(2,1)S(1)} collective-permute-done((bf16[256,768]{1,0:T(8,128)(2,1)S(1)}, bf16[256,768]{1,0:T(8,128)(2,1)S(1)}, u32[]{:S(2)}, u32[]{:S(2)}) %collective-permute-start.15) | collective-permute-done | bytes 393248 | tf_op jit(solution)/shard_map/ppermute | solution.py:30
  125.4 1.7 collective-permute-done.18.refs_4_
  127.9 12.5 %shard_map.95 = (bf16[256,512]{1,0:T(8,128)(2,1)}, bf16[4,768,128]{2,1,0:T(8,128)(2,1)}, bf16[4,768,128]{2,1,0:T(8,128)(2,1)}) custom-call(s32[6]{0:T(128)} %get-tuple-element.41.refs_0_, bf16[256,768]{1,0:T(8,128)(2,1)} %copy-done.3, bf16[256,768]{1,0:T(8,128)(2,1)} %copy-done.7, ...), custom_call_target="tpu_custom_call", output_to_operand_aliasing={{1}: (7, {}), {2}: (8, {})} | custom-call | tf_op jit(solution)/shard_map/pallas_call | solution.py:165
  140.4 1.5 collective-permute-start.19
  141.9 7.1 %collective-permute-done.19.refs_2_ = bf16[256,512]{1,0:T(8,128)(2,1)S(1)} collective-permute-done((bf16[256,512]{1,0:T(8,128)(2,1)}, bf16[256,512]{1,0:T(8,128)(2,1)S(1)}, u32[]{:S(2)}, u32[]{:S(2)}) %collective-permute-start.19) | collective-permute-done | bytes 262176 | tf_op jit(solution)/shard_map/ppermute | solution.py:22
  149.0 1.5 collective-permute-done.21.refs_4_
  151.2 4.1 %shard_map.96 = bf16[256,768]{1,0:T(8,128)(2,1)} custom-call(s32[6]{0:T(128)} %get-tuple-element.41.refs_0_, bf16[256,512]{1,0:T(8,128)(2,1)} %get-tuple-element.27.refs_1_, bf16[256,512]{1,0:T(8,128)(2,1)} %copy-done.22, bf16[256,512]{1,0:T(8,128)(2,1)} %copy-done.26, bf16[256,512]{1,0:T(8,128)(2,1)} %copy-done.30, bf16[4,512,768]{2,1,0:T(8,128)(2,1)} %bitcast.42, ...), custom_call_target="tpu_custom_call" | custom-call | tf_op jit(solution)/shard_map/pallas_call | solution.py:203
  155.3 1.3 collective-permute-start.22
  159.2 2.6 %collective-permute-start.24 = (bf16[256,768]{1,0:T(8,128)(2,1)}, bf16[256,768]{1,0:T(8,128)(2,1)S(1)}, u32[]{:S(2)}, u32[]{:S(2)}) collective-permute-start(bf16[256,768]{1,0:T(8,128)(2,1)} %shard_map.96), channel_id=1, source_target_pairs={{0,6},{1,7},{2,4},{3,5},{4,10},{5,11},{6,8},{7,9},{8,14},{9,15},{1... | collective-permute-start | bytes 1179656 | tf_op jit(solution)/shard_map/ppermute | solution.py:47
  161.8 4.6 %collective-permute-done.22 = bf16[256,768]{1,0:T(8,128)(2,1)S(1)} collective-permute-done((bf16[256,768]{1,0:T(8,128)(2,1)}, bf16[256,768]{1,0:T(8,128)(2,1)S(1)}, u32[]{:S(2)}, u32[]{:S(2)}) %collective-permute-start.22) | collective-permute-done | bytes 393248 | tf_op jit(solution)/shard_map/ppermute | solution.py:47
  166.6 3.4 %collective-permute-start.23 = (bf16[256,768]{1,0:T(8,128)(2,1)S(1)}, bf16[256,768]{1,0:T(8,128)(2,1)S(1)}, u32[]{:S(2)}, u32[]{:S(2)}) collective-permute-start(bf16[256,768]{1,0:T(8,128)(2,1)S(1)} %get-tuple-element.34), channel_id=1, source_target_pairs={{0,2},{1,3},{2,0},{3,1},{16,18},{17,19},{18,16},{19,17}} | collective-permute-start | bytes 1179656 | tf_op jit(solution)/shard_map/ppermute | solution.py:30
  170.1 4.2 %collective-permute-done.24 = bf16[256,768]{1,0:T(8,128)(2,1)S(1)} collective-permute-done((bf16[256,768]{1,0:T(8,128)(2,1)}, bf16[256,768]{1,0:T(8,128)(2,1)S(1)}, u32[]{:S(2)}, u32[]{:S(2)}) %collective-permute-start.24) | collective-permute-done | bytes 393248 | tf_op jit(solution)/shard_map/ppermute | solution.py:47
  174.3 4.4 %collective-permute-done.23 = bf16[256,768]{1,0:T(8,128)(2,1)S(1)} collective-permute-done((bf16[256,768]{1,0:T(8,128)(2,1)S(1)}, bf16[256,768]{1,0:T(8,128)(2,1)S(1)}, u32[]{:S(2)}, u32[]{:S(2)}) %collective-permute-start.23) | collective-permute-done | bytes 393248 | tf_op jit(solution)/shard_map/ppermute | solution.py:30
  178.8 1.7 collective-permute-done.26.refs_4_
  181.2 12.5 %shard_map.97 = (bf16[256,512]{1,0:T(8,128)(2,1)}, bf16[4,768,128]{2,1,0:T(8,128)(2,1)}, bf16[4,768,128]{2,1,0:T(8,128)(2,1)}) custom-call(s32[6]{0:T(128)} %get-tuple-element.40.refs_0_, bf16[256,768]{1,0:T(8,128)(2,1)} %copy-done.1, bf16[256,768]{1,0:T(8,128)(2,1)} %copy-done.5, ...), custom_call_target="tpu_custom_call", output_to_operand_aliasing={{1}: (7, {}), {2}: (8, {})} | custom-call | tf_op jit(solution)/shard_map/pallas_call | solution.py:165
  193.8 1.6 collective-permute-start.27
  195.3 7.1 %collective-permute-done.27.refs_2_ = bf16[256,512]{1,0:T(8,128)(2,1)S(1)} collective-permute-done((bf16[256,512]{1,0:T(8,128)(2,1)}, bf16[256,512]{1,0:T(8,128)(2,1)S(1)}, u32[]{:S(2)}, u32[]{:S(2)}) %collective-permute-start.27) | collective-permute-done | bytes 262176 | tf_op jit(solution)/shard_map/ppermute | solution.py:22
  202.4 1.5 collective-permute-done.29.refs_4_
  204.7 4.1 %shard_map.98 = bf16[256,768]{1,0:T(8,128)(2,1)} custom-call(s32[6]{0:T(128)} %get-tuple-element.40.refs_0_, bf16[256,512]{1,0:T(8,128)(2,1)} %get-tuple-element.30.refs_1_, bf16[256,512]{1,0:T(8,128)(2,1)} %copy-done.23, bf16[256,512]{1,0:T(8,128)(2,1)} %copy-done.27, bf16[256,512]{1,0:T(8,128)(2,1)} %copy-done.31, bf16[4,512,768]{2,1,0:T(8,128)(2,1)} %bitcast.43, ...), custom_call_target="tpu_custom_call" | custom-call | tf_op jit(solution)/shard_map/pallas_call | solution.py:203
  208.8 2.3 %maximum_bitcast_fusion = bf16[4,1,256,768]{3,2,1,0:T(8,128)(2,1)} fusion(bf16[1,256,768]{2,1,0:T(8,128)(2,1)} %bitcast.47, bf16[1,256,768]{2,1,0:T(8,128)(2,1)S(1)} %bitcast.46, bf16[1,256,768]{2,1,0:T(8,128)(2,1)S(1)} %bitcast.45, bf16[1,256,768]{2,1,0:T(8,128)(2,1)S(1)} %bitcast.44), kind=kLoop, calls=%fused_computation.3 | loop fusion | flops 2359296 | bytes 3145728 | tf_op jit(solution)/shard_map/broadcast_in_dim | solution.py:287
  (112 shorter events, 13.5 us)
Async XLA Ops:
  4.0 14.4 %copy-start.4 = (bf16[256,768]{1,0:T(8,128)(2,1)}, bf16[256,768]{1,0:T(8,128)(2,1)S(1)}, u32[]{:S(2)}) copy-start(bf16[256,768]{1,0:T(8,128)(2,1)S(1)} %fusion.3.refs_1_.refs_6_) | copy-start | bytes 1179652
  4.0 12.1 %collective-permute-start = (bf16[256,768]{1,0:T(8,128)(2,1)S(1)}, bf16[256,768]{1,0:T(8,128)(2,1)S(1)}, u32[]{:S(2)}, u32[]{:S(2)}) collective-permute-start(bf16[256,768]{1,0:T(8,128)(2,1)S(1)} %fusion.3.refs_1_.refs_6_), channel_id=1, source_target_pairs={{0,2},{1,3},{2,0},{3,1},{4,6},{5,7},{6,4},{7,5},{8,10},{9,11},{10,... | collective-permute-start | bytes 1179656 | tf_op jit(solution)/shard_map/ppermute | solution.py:22
  16.1 2.3 %copy-start.11 = (bf16[256,768]{1,0:T(8,128)(2,1)}, bf16[256,768]{1,0:T(8,128)(2,1)S(1)}, u32[]{:S(2)}) copy-start(bf16[256,768]{1,0:T(8,128)(2,1)S(1)} %collective-permute-done.refs_2_) | copy-start | bytes 1179652
  16.1 1.7 collective-permute-start.2
  16.1 2.3 %collective-permute-start.1 = (bf16[256,768]{1,0:T(8,128)(2,1)S(1)}, bf16[256,768]{1,0:T(8,128)(2,1)S(1)}, u32[]{:S(2)}, u32[]{:S(2)}) collective-permute-start(bf16[256,768]{1,0:T(8,128)(2,1)S(1)} %fusion.3.refs_1_.refs_6_), channel_id=1, source_target_pairs={{0,1},{1,0},{2,3},{3,2},{4,5},{5,4},{6,7},{7,6},{8,9},{9,8},{10,11... | collective-permute-start | bytes 1179656 | tf_op jit(solution)/shard_map/ppermute | solution.py:40
  31.7 8.6 %collective-permute-start.3 = (bf16[256,512]{1,0:T(8,128)(2,1)}, bf16[256,512]{1,0:T(8,128)(2,1)S(1)}, u32[]{:S(2)}, u32[]{:S(2)}) collective-permute-start(bf16[256,512]{1,0:T(8,128)(2,1)} %get-tuple-element.21.refs_1_), channel_id=1, source_target_pairs={{0,2},{1,3},{2,0},{3,1},{4,6},{5,7},{6,4},{7,5},{8,10},{9,11},{10,... | collective-permute-start | bytes 786440 | tf_op jit(solution)/shard_map/ppermute | solution.py:22
  33.4 6.8 %collective-permute-start.4 = (bf16[256,512]{1,0:T(8,128)(2,1)}, bf16[256,512]{1,0:T(8,128)(2,1)S(1)}, u32[]{:S(2)}, u32[]{:S(2)}) collective-permute-start(bf16[256,512]{1,0:T(8,128)(2,1)} %get-tuple-element.21.refs_1_), channel_id=1, source_target_pairs={{0,1},{1,0},{2,3},{3,2},{4,5},{5,4},{6,7},{7,6},{8,9},{9,8},{10,11... | collective-permute-start | bytes 786440 | tf_op jit(solution)/shard_map/ppermute | solution.py:40
  40.2 1.5 copy-start.20
  40.2 1.5 collective-permute-start.5
  42.5 10.5 %copy-start.32 = (s32[4]{0:T(128)S(1)}, s32[4]{0:T(128)}, u32[]{:S(2)}) copy-start(s32[4]{0:T(128)} %param.11) | copy-start | bytes 52
  42.5 17.2 %copy-start = (bf16[768,768]{1,0:T(8,128)(2,1)S(1)}, bf16[768,768]{1,0:T(8,128)(2,1)}, u32[]{:S(2)}) copy-start(bf16[768,768]{1,0:T(8,128)(2,1)} %param.9) | copy-start | bytes 3538948
  46.7 13.0 %collective-permute-start.6 = (bf16[256,768]{1,0:T(8,128)(2,1)}, bf16[256,768]{1,0:T(8,128)(2,1)S(1)}, u32[]{:S(2)}, u32[]{:S(2)}) collective-permute-start(bf16[256,768]{1,0:T(8,128)(2,1)} %shard_map.92), channel_id=1, source_target_pairs={{0,4},{1,5},{2,6},{3,7},{4,8},{5,9},{6,10},{7,11},{8,12},{9,13},{1... | collective-permute-start | bytes 1179656 | tf_op jit(solution)/shard_map/ppermute | solution.py:47
  54.4 13.4 %collective-permute-start.8 = (bf16[256,768]{1,0:T(8,128)(2,1)}, bf16[256,768]{1,0:T(8,128)(2,1)S(1)}, u32[]{:S(2)}, u32[]{:S(2)}) collective-permute-start(bf16[256,768]{1,0:T(8,128)(2,1)} %shard_map.92), channel_id=1, source_target_pairs={{0,6},{1,7},{2,4},{3,5},{4,10},{5,11},{6,8},{7,9},{8,14},{9,15},{1... | collective-permute-start | bytes 1179656 | tf_op jit(solution)/shard_map/ppermute | solution.py:47
  59.9 13.8 %copy-start.2 = (bf16[256,768]{1,0:T(8,128)(2,1)}, bf16[256,768]{1,0:T(8,128)(2,1)S(1)}, u32[]{:S(2)}) copy-start(bf16[256,768]{1,0:T(8,128)(2,1)S(1)} %get-tuple-element.37.refs_1_.refs_6_) | copy-start | bytes 1179652
  59.9 11.9 %collective-permute-start.7 = (bf16[256,768]{1,0:T(8,128)(2,1)S(1)}, bf16[256,768]{1,0:T(8,128)(2,1)S(1)}, u32[]{:S(2)}, u32[]{:S(2)}) collective-permute-start(bf16[256,768]{1,0:T(8,128)(2,1)S(1)} %get-tuple-element.38), channel_id=1, source_target_pairs={{0,2},{1,3},{2,0},{3,1},{16,18},{17,19},{18,16},{19,17}} | collective-permute-start | bytes 1179656 | tf_op jit(solution)/shard_map/ppermute | solution.py:30
  63.9 8.1 %collective-permute-start.9 = (bf16[256,768]{1,0:T(8,128)(2,1)S(1)}, bf16[256,768]{1,0:T(8,128)(2,1)S(1)}, u32[]{:S(2)}, u32[]{:S(2)}) collective-permute-start(bf16[256,768]{1,0:T(8,128)(2,1)S(1)} %get-tuple-element.37.refs_1_.refs_6_), channel_id=1, source_target_pairs={{0,1},{1,0},{2,3},{3,2},{4,5},{5,4},{6,7},{7,6},{8,9},{9,8},{10,11... | collective-permute-start | bytes 1179656 | tf_op jit(solution)/shard_map/ppermute | solution.py:40
  71.9 1.8 copy-start.6
  71.9 1.8 collective-permute-start.10
  72.0 1.7 copy-start.13
  87.0 8.6 %collective-permute-start.11 = (bf16[256,512]{1,0:T(8,128)(2,1)}, bf16[256,512]{1,0:T(8,128)(2,1)S(1)}, u32[]{:S(2)}, u32[]{:S(2)}) collective-permute-start(bf16[256,512]{1,0:T(8,128)(2,1)} %get-tuple-element.24.refs_1_), channel_id=1, source_target_pairs={{0,2},{1,3},{2,0},{3,1},{4,6},{5,7},{6,4},{7,5},{8,10},{9,11},{10,... | collective-permute-start | bytes 786440 | tf_op jit(solution)/shard_map/ppermute | solution.py:22
  88.5 7.1 %collective-permute-start.12 = (bf16[256,512]{1,0:T(8,128)(2,1)}, bf16[256,512]{1,0:T(8,128)(2,1)S(1)}, u32[]{:S(2)}, u32[]{:S(2)}) collective-permute-start(bf16[256,512]{1,0:T(8,128)(2,1)} %get-tuple-element.24.refs_1_), channel_id=1, source_target_pairs={{0,1},{1,0},{2,3},{3,2},{4,5},{5,4},{6,7},{7,6},{8,9},{9,8},{10,11... | collective-permute-start | bytes 786440 | tf_op jit(solution)/shard_map/ppermute | solution.py:40
  95.6 1.5 collective-permute-start.13
  101.9 11.0 %collective-permute-start.14 = (bf16[256,768]{1,0:T(8,128)(2,1)}, bf16[256,768]{1,0:T(8,128)(2,1)S(1)}, u32[]{:S(2)}, u32[]{:S(2)}) collective-permute-start(bf16[256,768]{1,0:T(8,128)(2,1)} %shard_map.94), channel_id=1, source_target_pairs={{0,4},{1,5},{2,6},{3,7},{4,8},{5,9},{6,10},{7,11},{8,12},{9,13},{1... | collective-permute-start | bytes 1179656 | tf_op jit(solution)/shard_map/ppermute | solution.py:47
  105.9 15.0 %collective-permute-start.16 = (bf16[256,768]{1,0:T(8,128)(2,1)}, bf16[256,768]{1,0:T(8,128)(2,1)S(1)}, u32[]{:S(2)}, u32[]{:S(2)}) collective-permute-start(bf16[256,768]{1,0:T(8,128)(2,1)} %shard_map.94), channel_id=1, source_target_pairs={{0,6},{1,7},{2,4},{3,5},{4,10},{5,11},{6,8},{7,9},{8,14},{9,15},{1... | collective-permute-start | bytes 1179656 | tf_op jit(solution)/shard_map/ppermute | solution.py:47
  113.2 13.9 %copy-start.3 = (bf16[256,768]{1,0:T(8,128)(2,1)}, bf16[256,768]{1,0:T(8,128)(2,1)S(1)}, u32[]{:S(2)}) copy-start(bf16[256,768]{1,0:T(8,128)(2,1)S(1)} %get-tuple-element.35.refs_1_.refs_6_) | copy-start | bytes 1179652
  113.2 12.1 %collective-permute-start.15 = (bf16[256,768]{1,0:T(8,128)(2,1)S(1)}, bf16[256,768]{1,0:T(8,128)(2,1)S(1)}, u32[]{:S(2)}, u32[]{:S(2)}) collective-permute-start(bf16[256,768]{1,0:T(8,128)(2,1)S(1)} %get-tuple-element.36), channel_id=1, source_target_pairs={{0,2},{1,3},{2,0},{3,1},{16,18},{17,19},{18,16},{19,17}} | collective-permute-start | bytes 1179656 | tf_op jit(solution)/shard_map/ppermute | solution.py:30
  116.8 8.6 %collective-permute-start.17 = (bf16[256,768]{1,0:T(8,128)(2,1)S(1)}, bf16[256,768]{1,0:T(8,128)(2,1)S(1)}, u32[]{:S(2)}, u32[]{:S(2)}) collective-permute-start(bf16[256,768]{1,0:T(8,128)(2,1)S(1)} %get-tuple-element.35.refs_1_.refs_6_), channel_id=1, source_target_pairs={{0,1},{1,0},{2,3},{3,2},{4,5},{5,4},{6,7},{7,6},{8,9},{9,8},{10,11... | collective-permute-start | bytes 1179656 | tf_op jit(solution)/shard_map/ppermute | solution.py:40
  125.3 1.8 copy-start.7
  125.3 1.8 collective-permute-start.18
  125.4 1.7 copy-start.14
  140.4 8.6 %collective-permute-start.19 = (bf16[256,512]{1,0:T(8,128)(2,1)}, bf16[256,512]{1,0:T(8,128)(2,1)S(1)}, u32[]{:S(2)}, u32[]{:S(2)}) collective-permute-start(bf16[256,512]{1,0:T(8,128)(2,1)} %get-tuple-element.27.refs_1_), channel_id=1, source_target_pairs={{0,2},{1,3},{2,0},{3,1},{4,6},{5,7},{6,4},{7,5},{8,10},{9,11},{10,... | collective-permute-start | bytes 786440 | tf_op jit(solution)/shard_map/ppermute | solution.py:22
  141.9 7.1 %collective-permute-start.20 = (bf16[256,512]{1,0:T(8,128)(2,1)}, bf16[256,512]{1,0:T(8,128)(2,1)S(1)}, u32[]{:S(2)}, u32[]{:S(2)}) collective-permute-start(bf16[256,512]{1,0:T(8,128)(2,1)} %get-tuple-element.27.refs_1_), channel_id=1, source_target_pairs={{0,1},{1,0},{2,3},{3,2},{4,5},{5,4},{6,7},{7,6},{8,9},{9,8},{10,11... | collective-permute-start | bytes 786440 | tf_op jit(solution)/shard_map/ppermute | solution.py:40
  148.9 1.5 collective-permute-start.21
  155.3 11.0 %collective-permute-start.22 = (bf16[256,768]{1,0:T(8,128)(2,1)}, bf16[256,768]{1,0:T(8,128)(2,1)S(1)}, u32[]{:S(2)}, u32[]{:S(2)}) collective-permute-start(bf16[256,768]{1,0:T(8,128)(2,1)} %shard_map.96), channel_id=1, source_target_pairs={{0,4},{1,5},{2,6},{3,7},{4,8},{5,9},{6,10},{7,11},{8,12},{9,13},{1... | collective-permute-start | bytes 1179656 | tf_op jit(solution)/shard_map/ppermute | solution.py:47
  159.2 15.1 %collective-permute-start.24 = (bf16[256,768]{1,0:T(8,128)(2,1)}, bf16[256,768]{1,0:T(8,128)(2,1)S(1)}, u32[]{:S(2)}, u32[]{:S(2)}) collective-permute-start(bf16[256,768]{1,0:T(8,128)(2,1)} %shard_map.96), channel_id=1, source_target_pairs={{0,6},{1,7},{2,4},{3,5},{4,10},{5,11},{6,8},{7,9},{8,14},{9,15},{1... | collective-permute-start | bytes 1179656 | tf_op jit(solution)/shard_map/ppermute | solution.py:47
  166.6 13.9 %copy-start.1 = (bf16[256,768]{1,0:T(8,128)(2,1)}, bf16[256,768]{1,0:T(8,128)(2,1)S(1)}, u32[]{:S(2)}) copy-start(bf16[256,768]{1,0:T(8,128)(2,1)S(1)} %get-tuple-element.33.refs_1_.refs_6_) | copy-start | bytes 1179652
  166.6 12.0 %collective-permute-start.23 = (bf16[256,768]{1,0:T(8,128)(2,1)S(1)}, bf16[256,768]{1,0:T(8,128)(2,1)S(1)}, u32[]{:S(2)}, u32[]{:S(2)}) collective-permute-start(bf16[256,768]{1,0:T(8,128)(2,1)S(1)} %get-tuple-element.34), channel_id=1, source_target_pairs={{0,2},{1,3},{2,0},{3,1},{16,18},{17,19},{18,16},{19,17}} | collective-permute-start | bytes 1179656 | tf_op jit(solution)/shard_map/ppermute | solution.py:30
  170.0 8.8 %collective-permute-start.25 = (bf16[256,768]{1,0:T(8,128)(2,1)S(1)}, bf16[256,768]{1,0:T(8,128)(2,1)S(1)}, u32[]{:S(2)}, u32[]{:S(2)}) collective-permute-start(bf16[256,768]{1,0:T(8,128)(2,1)S(1)} %get-tuple-element.33.refs_1_.refs_6_), channel_id=1, source_target_pairs={{0,1},{1,0},{2,3},{3,2},{4,5},{5,4},{6,7},{7,6},{8,9},{9,8},{10,11... | collective-permute-start | bytes 1179656 | tf_op jit(solution)/shard_map/ppermute | solution.py:40
  178.7 1.8 copy-start.5
  178.7 1.8 collective-permute-start.26
  178.8 1.7 copy-start.12
  193.7 15.0 %copy-start.8 = (bf16[256,768]{1,0:T(8,128)(2,1)S(1)}, bf16[256,768]{1,0:T(8,128)(2,1)}, u32[]{:S(2)}) copy-start(bf16[256,768]{1,0:T(8,128)(2,1)} %shard_map.92) | copy-start | bytes 1179652
  193.7 15.0 %copy-start.9 = (bf16[256,768]{1,0:T(8,128)(2,1)S(1)}, bf16[256,768]{1,0:T(8,128)(2,1)}, u32[]{:S(2)}) copy-start(bf16[256,768]{1,0:T(8,128)(2,1)} %shard_map.94) | copy-start | bytes 1179652
  193.8 15.0 %copy-start.10 = (bf16[256,768]{1,0:T(8,128)(2,1)S(1)}, bf16[256,768]{1,0:T(8,128)(2,1)}, u32[]{:S(2)}) copy-start(bf16[256,768]{1,0:T(8,128)(2,1)} %shard_map.96) | copy-start | bytes 1179652
  193.8 8.6 %collective-permute-start.27 = (bf16[256,512]{1,0:T(8,128)(2,1)}, bf16[256,512]{1,0:T(8,128)(2,1)S(1)}, u32[]{:S(2)}, u32[]{:S(2)}) collective-permute-start(bf16[256,512]{1,0:T(8,128)(2,1)} %get-tuple-element.30.refs_1_), channel_id=1, source_target_pairs={{0,2},{1,3},{2,0},{3,1},{4,6},{5,7},{6,4},{7,5},{8,10},{9,11},{10,... | collective-permute-start | bytes 786440 | tf_op jit(solution)/shard_map/ppermute | solution.py:22
  195.3 7.1 %collective-permute-start.28 = (bf16[256,512]{1,0:T(8,128)(2,1)}, bf16[256,512]{1,0:T(8,128)(2,1)S(1)}, u32[]{:S(2)}, u32[]{:S(2)}) collective-permute-start(bf16[256,512]{1,0:T(8,128)(2,1)} %get-tuple-element.30.refs_1_), channel_id=1, source_target_pairs={{0,1},{1,0},{2,3},{3,2},{4,5},{5,4},{6,7},{7,6},{8,9},{9,8},{10,11... | collective-permute-start | bytes 786440 | tf_op jit(solution)/shard_map/ppermute | solution.py:40
  202.4 1.5 copy-start.23
  202.4 1.5 collective-permute-start.29
  (15 other events, 15.8 us)

commit v17 on v14

--- a/solution.py
+++ b/solution.py
@@ -253,14 +253,19 @@
         (kernel_tables(patch_sizes_list, section_index), own_rows)
     )
     row_parts = [own_rows] + across_chips(own_rows)
-    entering_across = [
-        jnp.concatenate([rows, jnp.zeros((biggest_patch_span, columns), jnp.bfloat16)], axis=0)
-        for rows in across_chips_first_section(incoming_states)
-    ]
     for turn_number in range(patches):
         where = tables[turn_number]
+        rows_here = with_partner(row_parts)
+        if turn_number == 0:
+            later_entries, rows_here = lax.optimization_barrier((incoming_states, rows_here))
+            entering_across = [
+                jnp.concatenate(
+                    [rows, jnp.zeros((biggest_patch_span, columns), jnp.bfloat16)], axis=0
+                )
+                for rows in across_chips_first_section(later_entries)
+            ]
         head_rows, key_cache, value_cache = attend_block(
-            with_partner(row_parts),
+            rows_here,
             shift_scale,
             qkv_weights,
             key_cache,

time: 222 us -> 225 us (1.014)
  waiting for transfers between devices: 96.5 us -> 99.5 us
    unnamed x66 -> x68, local copies, waits for them, and re-layouts: 6.04 us -> 5.97 us
  transfers between devices with their start and end apart: 28 -> 28, of which waited for: 21 -> 22; matrix products, arithmetic and copies ran while one was open for 2% -> 2% of each run, Pallas kernels for 8% -> 7%
where the time goes in v17:
time: 225 us; the launch traced here: 223 us
  waiting for transfers between devices  99.5 us (44%)
  Pallas kernels  66.6 us (30%)
  starting transfers between devices  31.9 us (14%)
  other arithmetic  10.9 us (5%)
  local copies, waits for them, and re-layouts  7.89 us (4%)
  between operations  6.04 us (3%)
    pallas_call x4, Pallas kernels, attend_block(): pl.pallas_call(block_kernel, grid_spec=grid_spec, out_shape=[jax.ShapeDty...  50.1 us
    ppermute x5, waiting for transfers between devices, across_chips(): lax.ppermute(block, 'seq', [(source, (source + step) % count) for source...  49.7 us
    ppermute x6, waiting for transfers between devices, to_next_section(): lax.ppermute(block, ('section', 'seq'), [(section * count + source, (sect...  36.8 us
    ppermute x6, starting transfers between devices, to_next_section(): lax.ppermute(block, ('section', 'seq'), [(section * count + source, (sect...  19.5 us
    pallas_call x4, Pallas kernels, leave_block(): pl.pallas_call(exit_kernel, in_specs=[smem] + [vmem] * (count + 3), out_s...  16.5 us
    ppermute x16, waiting for transfers between devices, with_partner(): return parts + [lax.ppermute(part, 'seq', to_partner) for part in parts]  13.1 us
    ppermute x5, starting transfers between devices, across_chips(): lax.ppermute(block, 'seq', [(source, (source + step) % count) for source...  7.11 us
    unnamed x68, local copies, waits for them, and re-layouts  5.97 us
  transfers between devices with their start and end apart: 28, of which 22 were waited for; matrix products, arithmetic and copies ran while one was open for 2% of the time, Pallas kernels for 7%

profile of v17, /device:TPU:0, one launch (start us, length us, event | category | flops | bytes accessed | tf_op | source)
XLA Modules:
  0.0 222.9 jit_solution(10465438083633345707)
XLA Ops:
  0.1 0.8 reduce-window.9
  0.9 1.3 bitcast_subtract_fusion
  2.9 0.7 select_reduce_fusion
  3.7 1.2 fusion.12.refs_1_.refs_6_
  4.9 3.0 %collective-permute-start = (bf16[256,768]{1,0:T(8,128)(2,1)S(1)}, bf16[256,768]{1,0:T(8,128)(2,1)S(1)}, u32[]{:S(2)}, u32[]{:S(2)}) collective-permute-start(bf16[256,768]{1,0:T(8,128)(2,1)S(1)} %fusion.12.refs_1_.refs_6_), channel_id=1, source_target_pairs={{0,2},{1,3},{2,0},{3,1},{4,6},{5,7},{6,4},{7,5},{8,10},{9,11},{10,... | collective-permute-start | bytes 1179656 | tf_op jit(solution)/shard_map/ppermute | solution.py:22
  7.9 9.1 %collective-permute-done.refs_2_ = bf16[256,768]{1,0:T(8,128)(2,1)S(1)} collective-permute-done((bf16[256,768]{1,0:T(8,128)(2,1)S(1)}, bf16[256,768]{1,0:T(8,128)(2,1)S(1)}, u32[]{:S(2)}, u32[]{:S(2)}) %collective-permute-start) | collective-permute-done | bytes 393248 | tf_op jit(solution)/shard_map/ppermute | solution.py:22
  17.1 1.7 collective-permute-done.2.refs_4_
  18.8 3.6 %collective-permute-start.7 = (bf16[768,768]{1,0:T(8,128)(2,1)}, bf16[768,768]{1,0:T(8,128)(2,1)S(1)}, u32[]{:S(2)}, u32[]{:S(2)}) collective-permute-start(bf16[768,768]{1,0:T(8,128)(2,1)} %param.9), channel_id=1, source_target_pairs={{0,2},{1,3},{2,0},{3,1},{16,18},{17,19},{18,16},{19,17}} | collective-permute-start | bytes 3538952 | tf_op jit(solution)/shard_map/ppermute | solution.py:30
  23.1 12.5 %shard_map.91 = (bf16[256,512]{1,0:T(8,128)(2,1)}, bf16[4,768,128]{2,1,0:T(8,128)(2,1)}, bf16[4,768,128]{2,1,0:T(8,128)(2,1)}) custom-call(s32[6]{0:T(128)} %get-tuple-element.41.refs_0_, bf16[256,768]{1,0:T(8,128)(2,1)} %copy-done.4, bf16[256,768]{1,0:T(8,128)(2,1)} %copy-done.11, bf16[256,768]{1,0:T(8,128)(2,1)} %copy-done.12, ...), custom_call_target="tpu_custom_call" | custom-call | tf_op jit(solution)/shard_map/pallas_call | solution.py:165
  35.9 18.6 %collective-permute-done.3.refs_2_ = bf16[256,512]{1,0:T(8,128)(2,1)S(1)} collective-permute-done((bf16[256,512]{1,0:T(8,128)(2,1)}, bf16[256,512]{1,0:T(8,128)(2,1)S(1)}, u32[]{:S(2)}, u32[]{:S(2)}) %collective-permute-start.3) | collective-permute-done | bytes 262176 | tf_op jit(solution)/shard_map/ppermute | solution.py:22
  54.5 1.5 collective-permute-done.5.refs_4_
  56.1 0.7 copy-done.29
  56.8 4.2 %shard_map.92 = bf16[256,768]{1,0:T(8,128)(2,1)} custom-call(s32[6]{0:T(128)} %get-tuple-element.41.refs_0_, bf16[256,512]{1,0:T(8,128)(2,1)} %get-tuple-element.28.refs_1_, bf16[256,512]{1,0:T(8,128)(2,1)} %copy-done.21, bf16[256,512]{1,0:T(8,128)(2,1)} %copy-done.25, bf16[256,512]{1,0:T(8,128)(2,1)} %copy-done.29, bf16[4,512,768]{2,1,0:T(8,128)(2,1)} %bitcast.40, ...), custom_call_target="tpu_custom_call" | custom-call | tf_op jit(solution)/shard_map/pallas_call | solution.py:203
  61.0 1.3 collective-permute-start.8
  62.3 1.3 collective-permute-start.6
  67.5 4.5 %collective-permute-done.8 = bf16[256,768]{1,0:T(8,128)(2,1)S(1)} collective-permute-done((bf16[256,768]{1,0:T(8,128)(2,1)}, bf16[256,768]{1,0:T(8,128)(2,1)S(1)}, u32[]{:S(2)}, u32[]{:S(2)}) %collective-permute-start.8) | collective-permute-done | bytes 393248 | tf_op jit(solution)/shard_map/ppermute | solution.py:47
  72.0 7.9 %collective-permute-done.6 = bf16[256,768]{1,0:T(8,128)(2,1)S(1)} collective-permute-done((bf16[256,768]{1,0:T(8,128)(2,1)}, bf16[256,768]{1,0:T(8,128)(2,1)S(1)}, u32[]{:S(2)}, u32[]{:S(2)}) %collective-permute-start.6) | collective-permute-done | bytes 393248 | tf_op jit(solution)/shard_map/ppermute | solution.py:47
  79.9 0.8 copy-done.20
  81.8 1.2 collective-permute-done.10.refs_4_
  83.6 0.8 copy-done.18
  84.4 12.5 %shard_map.93 = (bf16[256,512]{1,0:T(8,128)(2,1)}, bf16[4,768,128]{2,1,0:T(8,128)(2,1)}, bf16[4,768,128]{2,1,0:T(8,128)(2,1)}) custom-call(s32[6]{0:T(128)} %get-tuple-element.44.refs_0_, bf16[256,768]{1,0:T(8,128)(2,1)} %copy-done.2, bf16[256,768]{1,0:T(8,128)(2,1)} %copy-done.6, ...), custom_call_target="tpu_custom_call", output_to_operand_aliasing={{1}: (7, {}), {2}: (8, {})} | custom-call | tf_op jit(solution)/shard_map/pallas_call | solution.py:165
  96.9 1.7 collective-permute-start.11
  98.7 6.8 %collective-permute-done.11.refs_2_ = bf16[256,512]{1,0:T(8,128)(2,1)S(1)} collective-permute-done((bf16[256,512]{1,0:T(8,128)(2,1)}, bf16[256,512]{1,0:T(8,128)(2,1)S(1)}, u32[]{:S(2)}, u32[]{:S(2)}) %collective-permute-start.11) | collective-permute-done | bytes 262176 | tf_op jit(solution)/shard_map/ppermute | solution.py:22
  105.5 1.5 collective-permute-done.13.refs_4_
  107.0 0.7 copy-done.30
  107.7 4.1 %shard_map.94 = bf16[256,768]{1,0:T(8,128)(2,1)} custom-call(s32[6]{0:T(128)} %get-tuple-element.44.refs_0_, bf16[256,512]{1,0:T(8,128)(2,1)} %get-tuple-element.32.refs_1_, bf16[256,512]{1,0:T(8,128)(2,1)} %copy-done.22, bf16[256,512]{1,0:T(8,128)(2,1)} %copy-done.26, bf16[256,512]{1,0:T(8,128)(2,1)} %copy-done.30, bf16[4,512,768]{2,1,0:T(8,128)(2,1)} %bitcast.41, ...), custom_call_target="tpu_custom_call" | custom-call | tf_op jit(solution)/shard_map/pallas_call | solution.py:203
  111.8 6.5 %collective-permute-start.15 = (bf16[256,768]{1,0:T(8,128)(2,1)}, bf16[256,768]{1,0:T(8,128)(2,1)S(1)}, u32[]{:S(2)}, u32[]{:S(2)}) collective-permute-start(bf16[256,768]{1,0:T(8,128)(2,1)} %shard_map.94), channel_id=1, source_target_pairs={{0,6},{1,7},{2,4},{3,5},{4,10},{5,11},{6,8},{7,9},{8,14},{9,15},{1... | collective-permute-start | bytes 1179656 | tf_op jit(solution)/shard_map/ppermute | solution.py:47
  118.3 2.0 collective-permute-start.14
  123.0 5.1 %collective-permute-done.15 = bf16[256,768]{1,0:T(8,128)(2,1)S(1)} collective-permute-done((bf16[256,768]{1,0:T(8,128)(2,1)}, bf16[256,768]{1,0:T(8,128)(2,1)S(1)}, u32[]{:S(2)}, u32[]{:S(2)}) %collective-permute-start.15) | collective-permute-done | bytes 393248 | tf_op jit(solution)/shard_map/ppermute | solution.py:47
  128.1 7.6 %collective-permute-done.14 = bf16[256,768]{1,0:T(8,128)(2,1)} collective-permute-done((bf16[256,768]{1,0:T(8,128)(2,1)}, bf16[256,768]{1,0:T(8,128)(2,1)}, u32[]{:S(2)}, u32[]{:S(2)}) %collective-permute-start.14) | collective-permute-done | bytes 393248 | tf_op jit(solution)/shard_map/ppermute | solution.py:47
  136.9 1.2 collective-permute-done.17.refs_4_
  138.6 0.8 copy-done.19
  139.4 12.5 %shard_map.95 = (bf16[256,512]{1,0:T(8,128)(2,1)}, bf16[4,768,128]{2,1,0:T(8,128)(2,1)}, bf16[4,768,128]{2,1,0:T(8,128)(2,1)}) custom-call(s32[6]{0:T(128)} %get-tuple-element.43.refs_0_, bf16[256,768]{1,0:T(8,128)(2,1)} %copy-done.3, bf16[256,768]{1,0:T(8,128)(2,1)} %copy-done.7, ...), custom_call_target="tpu_custom_call", output_to_operand_aliasing={{1}: (7, {}), {2}: (8, {})} | custom-call | tf_op jit(solution)/shard_map/pallas_call | solution.py:165
  152.2 8.3 %collective-permute-done.18.refs_2_ = bf16[256,512]{1,0:T(8,128)(2,1)S(1)} collective-permute-done((bf16[256,512]{1,0:T(8,128)(2,1)}, bf16[256,512]{1,0:T(8,128)(2,1)S(1)}, u32[]{:S(2)}, u32[]{:S(2)}) %collective-permute-start.18) | collective-permute-done | bytes 262176 | tf_op jit(solution)/shard_map/ppermute | solution.py:22
  160.5 1.5 collective-permute-done.20.refs_4_
  162.7 4.1 %shard_map.96 = bf16[256,768]{1,0:T(8,128)(2,1)} custom-call(s32[6]{0:T(128)} %get-tuple-element.43.refs_0_, bf16[256,512]{1,0:T(8,128)(2,1)} %get-tuple-element.35.refs_1_, bf16[256,512]{1,0:T(8,128)(2,1)} %copy-done.23, bf16[256,512]{1,0:T(8,128)(2,1)} %copy-done.27, bf16[256,512]{1,0:T(8,128)(2,1)} %copy-done.31, bf16[4,512,768]{2,1,0:T(8,128)(2,1)} %bitcast.42, ...), custom_call_target="tpu_custom_call" | custom-call | tf_op jit(solution)/shard_map/pallas_call | solution.py:203
  166.8 5.1 %collective-permute-start.22 = (bf16[256,768]{1,0:T(8,128)(2,1)}, bf16[256,768]{1,0:T(8,128)(2,1)S(1)}, u32[]{:S(2)}, u32[]{:S(2)}) collective-permute-start(bf16[256,768]{1,0:T(8,128)(2,1)} %shard_map.96), channel_id=1, source_target_pairs={{0,6},{1,7},{2,4},{3,5},{4,10},{5,11},{6,8},{7,9},{8,14},{9,15},{1... | collective-permute-start | bytes 1179656 | tf_op jit(solution)/shard_map/ppermute | solution.py:47
  172.0 3.2 %collective-permute-start.21 = (bf16[256,768]{1,0:T(8,128)(2,1)}, bf16[256,768]{1,0:T(8,128)(2,1)}, u32[]{:S(2)}, u32[]{:S(2)}) collective-permute-start(bf16[256,768]{1,0:T(8,128)(2,1)} %shard_map.96), channel_id=1, source_target_pairs={{0,4},{1,5},{2,6},{3,7},{4,8},{5,9},{6,10},{7,11},{8,12},{9,13},{1... | collective-permute-start | bytes 1179656 | tf_op jit(solution)/shard_map/ppermute | solution.py:47
  177.7 4.0 %collective-permute-done.22 = bf16[256,768]{1,0:T(8,128)(2,1)S(1)} collective-permute-done((bf16[256,768]{1,0:T(8,128)(2,1)}, bf16[256,768]{1,0:T(8,128)(2,1)S(1)}, u32[]{:S(2)}, u32[]{:S(2)}) %collective-permute-start.22) | collective-permute-done | bytes 393248 | tf_op jit(solution)/shard_map/ppermute | solution.py:47
  181.7 7.6 %collective-permute-done.21 = bf16[256,768]{1,0:T(8,128)(2,1)} collective-permute-done((bf16[256,768]{1,0:T(8,128)(2,1)}, bf16[256,768]{1,0:T(8,128)(2,1)}, u32[]{:S(2)}, u32[]{:S(2)}) %collective-permute-start.21) | collective-permute-done | bytes 393248 | tf_op jit(solution)/shard_map/ppermute | solution.py:47
  190.5 1.2 collective-permute-done.24.refs_4_
  193.1 12.5 %shard_map.97 = (bf16[256,512]{1,0:T(8,128)(2,1)}, bf16[4,768,128]{2,1,0:T(8,128)(2,1)}, bf16[4,768,128]{2,1,0:T(8,128)(2,1)}) custom-call(s32[6]{0:T(128)} %get-tuple-element.42.refs_0_, bf16[256,768]{1,0:T(8,128)(2,1)} %copy-done.1, bf16[256,768]{1,0:T(8,128)(2,1)} %copy-done.5, ...), custom_call_target="tpu_custom_call", output_to_operand_aliasing={{1}: (7, {}), {2}: (8, {})} | custom-call | tf_op jit(solution)/shard_map/pallas_call | solution.py:165
  205.6 1.8 collective-permute-start.25
  207.4 6.8 %collective-permute-done.25.refs_2_ = bf16[256,512]{1,0:T(8,128)(2,1)S(1)} collective-permute-done((bf16[256,512]{1,0:T(8,128)(2,1)}, bf16[256,512]{1,0:T(8,128)(2,1)S(1)}, u32[]{:S(2)}, u32[]{:S(2)}) %collective-permute-start.25) | collective-permute-done | bytes 262176 | tf_op jit(solution)/shard_map/ppermute | solution.py:22
  214.2 1.5 collective-permute-done.27.refs_4_
  215.8 0.7 copy-done.32
  216.5 4.1 %shard_map.98 = bf16[256,768]{1,0:T(8,128)(2,1)} custom-call(s32[6]{0:T(128)} %get-tuple-element.42.refs_0_, bf16[256,512]{1,0:T(8,128)(2,1)} %get-tuple-element.38.refs_1_, bf16[256,512]{1,0:T(8,128)(2,1)} %copy-done.24, bf16[256,512]{1,0:T(8,128)(2,1)} %copy-done.28, bf16[256,512]{1,0:T(8,128)(2,1)} %copy-done.32, bf16[4,512,768]{2,1,0:T(8,128)(2,1)} %bitcast.43, ...), custom_call_target="tpu_custom_call" | custom-call | tf_op jit(solution)/shard_map/pallas_call | solution.py:203
  220.6 2.3 %maximum_bitcast_fusion = bf16[4,1,256,768]{3,2,1,0:T(8,128)(2,1)} fusion(bf16[1,256,768]{2,1,0:T(8,128)(2,1)} %bitcast.47, bf16[1,256,768]{2,1,0:T(8,128)(2,1)S(1)} %bitcast.46, bf16[1,256,768]{2,1,0:T(8,128)(2,1)S(1)} %bitcast.45, bf16[1,256,768]{2,1,0:T(8,128)(2,1)S(1)} %bitcast.44), kind=kLoop, calls=%fused_computation.6 | loop fusion | flops 2359296 | bytes 3145728 | tf_op jit(solution)/shard_map/broadcast_in_dim | solution.py:300
  (107 shorter events, 12.0 us)
Async XLA Ops:
  4.9 18.1 %copy-start.4 = (bf16[256,768]{1,0:T(8,128)(2,1)}, bf16[256,768]{1,0:T(8,128)(2,1)S(1)}, u32[]{:S(2)}) copy-start(bf16[256,768]{1,0:T(8,128)(2,1)S(1)} %fusion.12.refs_1_.refs_6_) | copy-start | bytes 1179652
  4.9 12.1 %collective-permute-start = (bf16[256,768]{1,0:T(8,128)(2,1)S(1)}, bf16[256,768]{1,0:T(8,128)(2,1)S(1)}, u32[]{:S(2)}, u32[]{:S(2)}) collective-permute-start(bf16[256,768]{1,0:T(8,128)(2,1)S(1)} %fusion.12.refs_1_.refs_6_), channel_id=1, source_target_pairs={{0,2},{1,3},{2,0},{3,1},{4,6},{5,7},{6,4},{7,5},{8,10},{9,11},{10,... | collective-permute-start | bytes 1179656 | tf_op jit(solution)/shard_map/ppermute | solution.py:22
  7.9 9.1 %collective-permute-start.1 = (bf16[256,768]{1,0:T(8,128)(2,1)S(1)}, bf16[256,768]{1,0:T(8,128)(2,1)S(1)}, u32[]{:S(2)}, u32[]{:S(2)}) collective-permute-start(bf16[256,768]{1,0:T(8,128)(2,1)S(1)} %fusion.12.refs_1_.refs_6_), channel_id=1, source_target_pairs={{0,1},{1,0},{2,3},{3,2},{4,5},{5,4},{6,7},{7,6},{8,9},{9,8},{10,11... | collective-permute-start | bytes 1179656 | tf_op jit(solution)/shard_map/ppermute | solution.py:40
  17.1 6.0 %copy-start.11 = (bf16[256,768]{1,0:T(8,128)(2,1)}, bf16[256,768]{1,0:T(8,128)(2,1)S(1)}, u32[]{:S(2)}) copy-start(bf16[256,768]{1,0:T(8,128)(2,1)S(1)} %collective-permute-done.refs_2_) | copy-start | bytes 1179652
  17.1 1.7 collective-permute-start.2
  17.1 6.0 %copy-start.12 = (bf16[256,768]{1,0:T(8,128)(2,1)}, bf16[256,768]{1,0:T(8,128)(2,1)S(1)}, u32[]{:S(2)}) copy-start(bf16[256,768]{1,0:T(8,128)(2,1)S(1)} %collective-permute-done.1.refs_3_) | copy-start | bytes 1179652
  18.8 4.3 %copy-start.13 = (bf16[256,768]{1,0:T(8,128)(2,1)}, bf16[256,768]{1,0:T(8,128)(2,1)S(1)}, u32[]{:S(2)}) copy-start(bf16[256,768]{1,0:T(8,128)(2,1)S(1)} %collective-permute-done.2.refs_4_) | copy-start | bytes 1179652
  18.8 61.9 %collective-permute-start.7 = (bf16[768,768]{1,0:T(8,128)(2,1)}, bf16[768,768]{1,0:T(8,128)(2,1)S(1)}, u32[]{:S(2)}, u32[]{:S(2)}) collective-permute-start(bf16[768,768]{1,0:T(8,128)(2,1)} %param.9), channel_id=1, source_target_pairs={{0,2},{1,3},{2,0},{3,1},{16,18},{17,19},{18,16},{19,17}} | collective-permute-start | bytes 3538952 | tf_op jit(solution)/shard_map/ppermute | solution.py:30
  35.6 18.9 %collective-permute-start.3 = (bf16[256,512]{1,0:T(8,128)(2,1)}, bf16[256,512]{1,0:T(8,128)(2,1)S(1)}, u32[]{:S(2)}, u32[]{:S(2)}) collective-permute-start(bf16[256,512]{1,0:T(8,128)(2,1)} %get-tuple-element.28.refs_1_), channel_id=1, source_target_pairs={{0,2},{1,3},{2,0},{3,1},{4,6},{5,7},{6,4},{7,5},{8,10},{9,11},{10,... | collective-permute-start | bytes 786440 | tf_op jit(solution)/shard_map/ppermute | solution.py:22
  35.9 18.7 %collective-permute-start.4 = (bf16[256,512]{1,0:T(8,128)(2,1)}, bf16[256,512]{1,0:T(8,128)(2,1)S(1)}, u32[]{:S(2)}, u32[]{:S(2)}) collective-permute-start(bf16[256,512]{1,0:T(8,128)(2,1)} %get-tuple-element.28.refs_1_), channel_id=1, source_target_pairs={{0,1},{1,0},{2,3},{3,2},{4,5},{5,4},{6,7},{7,6},{8,9},{9,8},{10,11... | collective-permute-start | bytes 786440 | tf_op jit(solution)/shard_map/ppermute | solution.py:40
  54.5 1.5 copy-start.21
  54.5 1.5 collective-permute-start.5
  54.5 1.5 copy-start.25
  56.8 9.4 %copy-start.33 = (s32[4]{0:T(128)S(1)}, s32[4]{0:T(128)}, u32[]{:S(2)}) copy-start(s32[4]{0:T(128)} %param.11) | copy-start | bytes 52
  56.8 23.9 %copy-start = (bf16[768,768]{1,0:T(8,128)(2,1)S(1)}, bf16[768,768]{1,0:T(8,128)(2,1)}, u32[]{:S(2)}) copy-start(bf16[768,768]{1,0:T(8,128)(2,1)} %param.9) | copy-start | bytes 3538948
  61.0 11.0 %collective-permute-start.8 = (bf16[256,768]{1,0:T(8,128)(2,1)}, bf16[256,768]{1,0:T(8,128)(2,1)S(1)}, u32[]{:S(2)}, u32[]{:S(2)}) collective-permute-start(bf16[256,768]{1,0:T(8,128)(2,1)} %shard_map.92), channel_id=1, source_target_pairs={{0,6},{1,7},{2,4},{3,5},{4,10},{5,11},{6,8},{7,9},{8,14},{9,15},{1... | collective-permute-start | bytes 1179656 | tf_op jit(solution)/shard_map/ppermute | solution.py:47
  62.3 17.7 %collective-permute-start.6 = (bf16[256,768]{1,0:T(8,128)(2,1)}, bf16[256,768]{1,0:T(8,128)(2,1)S(1)}, u32[]{:S(2)}, u32[]{:S(2)}) collective-permute-start(bf16[256,768]{1,0:T(8,128)(2,1)} %shard_map.92), channel_id=1, source_target_pairs={{0,4},{1,5},{2,6},{3,7},{4,8},{5,9},{6,10},{7,11},{8,12},{9,13},{1... | collective-permute-start | bytes 1179656 | tf_op jit(solution)/shard_map/ppermute | solution.py:47
  81.2 3.1 %copy-start.2 = (bf16[256,768]{1,0:T(8,128)(2,1)}, bf16[256,768]{1,0:T(8,128)(2,1)S(1)}, u32[]{:S(2)}) copy-start(bf16[256,768]{1,0:T(8,128)(2,1)S(1)} %get-tuple-element.56.refs_1_.refs_6_) | copy-start | bytes 1179652
  81.3 3.1 %copy-start.6 = (bf16[256,768]{1,0:T(8,128)(2,1)}, bf16[256,768]{1,0:T(8,128)(2,1)S(1)}, u32[]{:S(2)}) copy-start(bf16[256,768]{1,0:T(8,128)(2,1)S(1)} %get-tuple-element.55.refs_2_) | copy-start | bytes 1179652
  81.3 1.8 collective-permute-start.10
  81.3 2.3 %collective-permute-start.9 = (bf16[256,768]{1,0:T(8,128)(2,1)S(1)}, bf16[256,768]{1,0:T(8,128)(2,1)S(1)}, u32[]{:S(2)}, u32[]{:S(2)}) collective-permute-start(bf16[256,768]{1,0:T(8,128)(2,1)S(1)} %get-tuple-element.56.refs_1_.refs_6_), channel_id=1, source_target_pairs={{0,1},{1,0},{2,3},{3,2},{4,5},{5,4},{6,7},{7,6},{8,9},{9,8},{10,11... | collective-permute-start | bytes 1179656 | tf_op jit(solution)/shard_map/ppermute | solution.py:40
  96.9 8.6 %collective-permute-start.11 = (bf16[256,512]{1,0:T(8,128)(2,1)}, bf16[256,512]{1,0:T(8,128)(2,1)S(1)}, u32[]{:S(2)}, u32[]{:S(2)}) collective-permute-start(bf16[256,512]{1,0:T(8,128)(2,1)} %get-tuple-element.32.refs_1_), channel_id=1, source_target_pairs={{0,2},{1,3},{2,0},{3,1},{4,6},{5,7},{6,4},{7,5},{8,10},{9,11},{10,... | collective-permute-start | bytes 786440 | tf_op jit(solution)/shard_map/ppermute | solution.py:22
  98.7 6.8 %collective-permute-start.12 = (bf16[256,512]{1,0:T(8,128)(2,1)}, bf16[256,512]{1,0:T(8,128)(2,1)S(1)}, u32[]{:S(2)}, u32[]{:S(2)}) collective-permute-start(bf16[256,512]{1,0:T(8,128)(2,1)} %get-tuple-element.32.refs_1_), channel_id=1, source_target_pairs={{0,1},{1,0},{2,3},{3,2},{4,5},{5,4},{6,7},{7,6},{8,9},{9,8},{10,11... | collective-permute-start | bytes 786440 | tf_op jit(solution)/shard_map/ppermute | solution.py:40
  105.5 1.5 copy-start.22
  105.5 1.5 collective-permute-start.13
  111.8 16.2 %collective-permute-start.15 = (bf16[256,768]{1,0:T(8,128)(2,1)}, bf16[256,768]{1,0:T(8,128)(2,1)S(1)}, u32[]{:S(2)}, u32[]{:S(2)}) collective-permute-start(bf16[256,768]{1,0:T(8,128)(2,1)} %shard_map.94), channel_id=1, source_target_pairs={{0,6},{1,7},{2,4},{3,5},{4,10},{5,11},{6,8},{7,9},{8,14},{9,15},{1... | collective-permute-start | bytes 1179656 | tf_op jit(solution)/shard_map/ppermute | solution.py:47
  118.3 17.4 %collective-permute-start.14 = (bf16[256,768]{1,0:T(8,128)(2,1)}, bf16[256,768]{1,0:T(8,128)(2,1)}, u32[]{:S(2)}, u32[]{:S(2)}) collective-permute-start(bf16[256,768]{1,0:T(8,128)(2,1)} %shard_map.94), channel_id=1, source_target_pairs={{0,4},{1,5},{2,6},{3,7},{4,8},{5,9},{6,10},{7,11},{8,12},{9,13},{1... | collective-permute-start | bytes 1179656 | tf_op jit(solution)/shard_map/ppermute | solution.py:47
  136.3 3.1 %copy-start.3 = (bf16[256,768]{1,0:T(8,128)(2,1)}, bf16[256,768]{1,0:T(8,128)(2,1)S(1)}, u32[]{:S(2)}) copy-start(bf16[256,768]{1,0:T(8,128)(2,1)S(1)} %get-tuple-element.54.refs_1_.refs_6_) | copy-start | bytes 1179652
  136.3 3.1 %copy-start.7 = (bf16[256,768]{1,0:T(8,128)(2,1)}, bf16[256,768]{1,0:T(8,128)(2,1)S(1)}, u32[]{:S(2)}) copy-start(bf16[256,768]{1,0:T(8,128)(2,1)S(1)} %get-tuple-element.53.refs_2_) | copy-start | bytes 1179652
  136.3 1.8 collective-permute-start.17
  136.4 2.3 %collective-permute-start.16 = (bf16[256,768]{1,0:T(8,128)(2,1)S(1)}, bf16[256,768]{1,0:T(8,128)(2,1)S(1)}, u32[]{:S(2)}, u32[]{:S(2)}) collective-permute-start(bf16[256,768]{1,0:T(8,128)(2,1)S(1)} %get-tuple-element.54.refs_1_.refs_6_), channel_id=1, source_target_pairs={{0,1},{1,0},{2,3},{3,2},{4,5},{5,4},{6,7},{7,6},{8,9},{9,8},{10,11... | collective-permute-start | bytes 1179656 | tf_op jit(solution)/shard_map/ppermute | solution.py:40
  151.9 8.6 %collective-permute-start.18 = (bf16[256,512]{1,0:T(8,128)(2,1)}, bf16[256,512]{1,0:T(8,128)(2,1)S(1)}, u32[]{:S(2)}, u32[]{:S(2)}) collective-permute-start(bf16[256,512]{1,0:T(8,128)(2,1)} %get-tuple-element.35.refs_1_), channel_id=1, source_target_pairs={{0,2},{1,3},{2,0},{3,1},{4,6},{5,7},{6,4},{7,5},{8,10},{9,11},{10,... | collective-permute-start | bytes 786440 | tf_op jit(solution)/shard_map/ppermute | solution.py:22
  152.2 8.3 %collective-permute-start.19 = (bf16[256,512]{1,0:T(8,128)(2,1)}, bf16[256,512]{1,0:T(8,128)(2,1)S(1)}, u32[]{:S(2)}, u32[]{:S(2)}) collective-permute-start(bf16[256,512]{1,0:T(8,128)(2,1)} %get-tuple-element.35.refs_1_), channel_id=1, source_target_pairs={{0,1},{1,0},{2,3},{3,2},{4,5},{5,4},{6,7},{7,6},{8,9},{9,8},{10,11... | collective-permute-start | bytes 786440 | tf_op jit(solution)/shard_map/ppermute | solution.py:40
  160.5 1.5 copy-start.23
  160.5 1.5 collective-permute-start.20
  166.8 14.9 %collective-permute-start.22 = (bf16[256,768]{1,0:T(8,128)(2,1)}, bf16[256,768]{1,0:T(8,128)(2,1)S(1)}, u32[]{:S(2)}, u32[]{:S(2)}) collective-permute-start(bf16[256,768]{1,0:T(8,128)(2,1)} %shard_map.96), channel_id=1, source_target_pairs={{0,6},{1,7},{2,4},{3,5},{4,10},{5,11},{6,8},{7,9},{8,14},{9,15},{1... | collective-permute-start | bytes 1179656 | tf_op jit(solution)/shard_map/ppermute | solution.py:47
  172.0 17.4 %collective-permute-start.21 = (bf16[256,768]{1,0:T(8,128)(2,1)}, bf16[256,768]{1,0:T(8,128)(2,1)}, u32[]{:S(2)}, u32[]{:S(2)}) collective-permute-start(bf16[256,768]{1,0:T(8,128)(2,1)} %shard_map.96), channel_id=1, source_target_pairs={{0,4},{1,5},{2,6},{3,7},{4,8},{5,9},{6,10},{7,11},{8,12},{9,13},{1... | collective-permute-start | bytes 1179656 | tf_op jit(solution)/shard_map/ppermute | solution.py:47
  189.9 2.4 %copy-start.1 = (bf16[256,768]{1,0:T(8,128)(2,1)}, bf16[256,768]{1,0:T(8,128)(2,1)S(1)}, u32[]{:S(2)}) copy-start(bf16[256,768]{1,0:T(8,128)(2,1)S(1)} %get-tuple-element.46.refs_1_.refs_6_) | copy-start | bytes 1179652
  189.9 2.4 %copy-start.5 = (bf16[256,768]{1,0:T(8,128)(2,1)}, bf16[256,768]{1,0:T(8,128)(2,1)S(1)}, u32[]{:S(2)}) copy-start(bf16[256,768]{1,0:T(8,128)(2,1)S(1)} %get-tuple-element.45.refs_2_) | copy-start | bytes 1179652
  189.9 1.8 collective-permute-start.24
  190.0 2.3 %collective-permute-start.23 = (bf16[256,768]{1,0:T(8,128)(2,1)S(1)}, bf16[256,768]{1,0:T(8,128)(2,1)S(1)}, u32[]{:S(2)}, u32[]{:S(2)}) collective-permute-start(bf16[256,768]{1,0:T(8,128)(2,1)S(1)} %get-tuple-element.46.refs_1_.refs_6_), channel_id=1, source_target_pairs={{0,1},{1,0},{2,3},{3,2},{4,5},{5,4},{6,7},{7,6},{8,9},{9,8},{10,11... | collective-permute-start | bytes 1179656 | tf_op jit(solution)/shard_map/ppermute | solution.py:40
  205.6 15.0 %copy-start.8 = (bf16[256,768]{1,0:T(8,128)(2,1)S(1)}, bf16[256,768]{1,0:T(8,128)(2,1)}, u32[]{:S(2)}) copy-start(bf16[256,768]{1,0:T(8,128)(2,1)} %shard_map.92) | copy-start | bytes 1179652
  205.6 15.0 %copy-start.9 = (bf16[256,768]{1,0:T(8,128)(2,1)S(1)}, bf16[256,768]{1,0:T(8,128)(2,1)}, u32[]{:S(2)}) copy-start(bf16[256,768]{1,0:T(8,128)(2,1)} %shard_map.94) | copy-start | bytes 1179652
  205.6 15.0 %copy-start.10 = (bf16[256,768]{1,0:T(8,128)(2,1)S(1)}, bf16[256,768]{1,0:T(8,128)(2,1)}, u32[]{:S(2)}) copy-start(bf16[256,768]{1,0:T(8,128)(2,1)} %shard_map.96) | copy-start | bytes 1179652
  205.6 8.6 %collective-permute-start.25 = (bf16[256,512]{1,0:T(8,128)(2,1)}, bf16[256,512]{1,0:T(8,128)(2,1)S(1)}, u32[]{:S(2)}, u32[]{:S(2)}) collective-permute-start(bf16[256,512]{1,0:T(8,128)(2,1)} %get-tuple-element.38.refs_1_), channel_id=1, source_target_pairs={{0,2},{1,3},{2,0},{3,1},{4,6},{5,7},{6,4},{7,5},{8,10},{9,11},{10,... | collective-permute-start | bytes 786440 | tf_op jit(solution)/shard_map/ppermute | solution.py:22
  207.4 6.8 %collective-permute-start.26 = (bf16[256,512]{1,0:T(8,128)(2,1)}, bf16[256,512]{1,0:T(8,128)(2,1)S(1)}, u32[]{:S(2)}, u32[]{:S(2)}) collective-permute-start(bf16[256,512]{1,0:T(8,128)(2,1)} %get-tuple-element.38.refs_1_), channel_id=1, source_target_pairs={{0,1},{1,0},{2,3},{3,2},{4,5},{5,4},{6,7},{7,6},{8,9},{9,8},{10,11... | collective-permute-start | bytes 786440 | tf_op jit(solution)/shard_map/ppermute | solution.py:40
  214.2 1.5 copy-start.24
  214.2 1.5 collective-permute-start.27
  (14 other events, 13.9 us)

commit v18 on v16

--- a/solution.py
+++ b/solution.py
@@ -79,11 +79,11 @@
 
 def block_kernel(*refs):
     where_ref = refs[0]
-    count = len(refs) - 9
+    count = len(refs) - 10
     part_refs = refs[1 : 1 + count]
     scale_ref, weights_ref, keys_ref, values_ref = refs[1 + count : 5 + count]
     heads_ref, keys_out, values_out = refs[5 + count : 8 + count]
-    shaped_ref = refs[8 + count]
+    shaped_ref, staging_ref = refs[8 + count :]
     start = where_ref[0]
     patch_count = where_ref[1]
     head_dim = keys_ref.shape[2]
@@ -116,15 +116,15 @@
     queries = rms_norm(mixed[:, :head_dim]).astype(jnp.bfloat16)
     fresh_keys = rms_norm(mixed[:, head_dim : 2 * head_dim]).astype(jnp.bfloat16)
     fresh_values = mixed[:, 2 * head_dim :].astype(jnp.bfloat16)
-    rows = lax.broadcasted_iota(jnp.int32, (seq_len, span), 0)
-    picks = lax.broadcasted_iota(jnp.int32, (seq_len, span), 1)
-    placing = ((rows == picks + start) & (picks < patch_count)).astype(jnp.bfloat16)
-    row_ids = lax.broadcasted_iota(jnp.int32, (seq_len, 1), 0)
-    inside = (row_ids >= start) & (row_ids < start + patch_count)
-    placed_keys = jnp.dot(placing, fresh_keys, preferred_element_type=jnp.float32)
-    placed_values = jnp.dot(placing, fresh_values, preferred_element_type=jnp.float32)
-    keys = jnp.where(inside, placed_keys.astype(jnp.bfloat16), keys_ref[0])
-    values = jnp.where(inside, placed_values.astype(jnp.bfloat16), values_ref[0])
+    live = lax.broadcasted_iota(jnp.int32, (span, 1), 0) < patch_count
+    staging_ref[:seq_len] = keys_ref[0].astype(jnp.float32)
+    window = staging_ref[pl.ds(start, span)]
+    staging_ref[pl.ds(start, span)] = jnp.where(live, fresh_keys.astype(jnp.float32), window)
+    keys = staging_ref[:seq_len].astype(jnp.bfloat16)
+    staging_ref[:seq_len] = values_ref[0].astype(jnp.float32)
+    window = staging_ref[pl.ds(start, span)]
+    staging_ref[pl.ds(start, span)] = jnp.where(live, fresh_values.astype(jnp.float32), window)
+    values = staging_ref[:seq_len].astype(jnp.bfloat16)
     keys_out[0] = keys
     values_out[0] = values
     scores = lax.dot_general(
@@ -160,7 +160,10 @@
             cache_spec,
             cache_spec,
         ],
-        scratch_shapes=[pltpu.VMEM((count, span, width), jnp.bfloat16)],
+        scratch_shapes=[
+            pltpu.VMEM((count, span, width), jnp.bfloat16),
+            pltpu.VMEM((seq_len + span, head_dim), jnp.float32),
+        ],
     )
     return pl.pallas_call(
         block_kernel,

time: 212 us -> 209 us (0.986)
  Pallas kernels: 66.6 us -> 63.8 us
    pallas_call x4, Pallas kernels: 50.1 us -> 47.3 us  [attend_block(): pl.pallas_call(block_kernel, grid_spec=grid_spec, out_shape=[jax.ShapeDty...]
where the time goes in v18:
time: 209 us; the launch traced here: 208 us
  waiting for transfers between devices  82.6 us (40%)
  Pallas kernels  63.8 us (31%)
  starting transfers between devices  37.8 us (18%)
  other arithmetic  9.93 us (5%)
  local copies, waits for them, and re-layouts  7.81 us (4%)
  between operations  6.34 us (3%)
    pallas_call x4, Pallas kernels, attend_block(): pl.pallas_call(block_kernel, grid_spec=grid_spec, out_shape=[jax.ShapeDty...  47.3 us
    ppermute x5, waiting for transfers between devices, across_chips(): lax.ppermute(block, 'seq', [(source, (source + step) % count) for source...  36.2 us
    ppermute x6, waiting for transfers between devices, to_next_section(): lax.ppermute(block, ('section', 'seq'), [(section * count + source, (sect...  21.3 us
    ppermute x6, starting transfers between devices, to_next_section(): lax.ppermute(block, ('section', 'seq'), [(section * count + source, (sect...  16.7 us
    pallas_call x4, Pallas kernels, leave_block(): pl.pallas_call(exit_kernel, in_specs=[smem] + [vmem] * (count + 3), out_s...  16.5 us
    ppermute x3, waiting for transfers between devices, across_chips_first_section(): lax.ppermute(block, ('section', 'seq'), [(source, (source + step) % count...  12.8 us
    ppermute x16, waiting for transfers between devices, with_partner(): return parts + [lax.ppermute(part, 'seq', to_partner) for part in parts]  12.3 us
    ppermute x3, starting transfers between devices, across_chips_first_section(): lax.ppermute(block, ('section', 'seq'), [(source, (source + step) % count...  10.9 us
  transfers between devices with their start and end apart: 30, of which 23 were waited for; matrix products, arithmetic and copies ran while one was open for 3% of the time, Pallas kernels for 0%

profile of v18, /device:TPU:0, one launch (start us, length us, event | category | flops | bytes accessed | tf_op | source)
XLA Modules:
  0.0 208.3 jit_solution(5884772190086527559)
XLA Ops:
  0.0 0.8 reduce-window.9
  0.8 1.3 bitcast_subtract_fusion
  2.8 1.2 fusion.3.refs_1_.refs_6_
  4.0 3.0 %collective-permute-start = (bf16[256,768]{1,0:T(8,128)(2,1)S(1)}, bf16[256,768]{1,0:T(8,128)(2,1)S(1)}, u32[]{:S(2)}, u32[]{:S(2)}) collective-permute-start(bf16[256,768]{1,0:T(8,128)(2,1)S(1)} %fusion.3.refs_1_.refs_6_), channel_id=1, source_target_pairs={{0,2},{1,3},{2,0},{3,1},{4,6},{5,7},{6,4},{7,5},{8,10},{9,11},{10,... | collective-permute-start | bytes 1179656 | tf_op jit(solution)/shard_map/ppermute | solution.py:22
  7.9 8.2 %collective-permute-done.refs_2_ = bf16[256,768]{1,0:T(8,128)(2,1)S(1)} collective-permute-done((bf16[256,768]{1,0:T(8,128)(2,1)S(1)}, bf16[256,768]{1,0:T(8,128)(2,1)S(1)}, u32[]{:S(2)}, u32[]{:S(2)}) %collective-permute-start) | collective-permute-done | bytes 393248 | tf_op jit(solution)/shard_map/ppermute | solution.py:22
  19.2 11.8 %shard_map.91 = (bf16[256,512]{1,0:T(8,128)(2,1)}, bf16[4,768,128]{2,1,0:T(8,128)(2,1)}, bf16[4,768,128]{2,1,0:T(8,128)(2,1)}) custom-call(s32[6]{0:T(128)} %get-tuple-element.39.refs_0_, bf16[256,768]{1,0:T(8,128)(2,1)} %copy-done.4, bf16[256,768]{1,0:T(8,128)(2,1)} %copy-done.11, bf16[256,768]{1,0:T(8,128)(2,1)} %copy-done.16, ...), custom_call_target="tpu_custom_call" | custom-call | tf_op jit(solution)/shard_map/pallas_call | solution.py:168
  31.0 1.7 collective-permute-start.3
  32.7 6.8 %collective-permute-done.3.refs_2_ = bf16[256,512]{1,0:T(8,128)(2,1)S(1)} collective-permute-done((bf16[256,512]{1,0:T(8,128)(2,1)}, bf16[256,512]{1,0:T(8,128)(2,1)S(1)}, u32[]{:S(2)}, u32[]{:S(2)}) %collective-permute-start.3) | collective-permute-done | bytes 262176 | tf_op jit(solution)/shard_map/ppermute | solution.py:22
  39.6 1.5 collective-permute-done.5.refs_4_
  41.8 4.2 %shard_map.92 = bf16[256,768]{1,0:T(8,128)(2,1)} custom-call(s32[6]{0:T(128)} %get-tuple-element.39.refs_0_, bf16[256,512]{1,0:T(8,128)(2,1)} %get-tuple-element.21.refs_1_, bf16[256,512]{1,0:T(8,128)(2,1)} %copy-done.20, bf16[256,512]{1,0:T(8,128)(2,1)} %copy-done.24, bf16[256,512]{1,0:T(8,128)(2,1)} %copy-done.28, bf16[4,512,768]{2,1,0:T(8,128)(2,1)} %bitcast.40, ...), custom_call_target="tpu_custom_call" | custom-call | tf_op jit(solution)/shard_map/pallas_call | solution.py:206
  46.0 3.7 %collective-permute-start.6 = (bf16[256,768]{1,0:T(8,128)(2,1)}, bf16[256,768]{1,0:T(8,128)(2,1)S(1)}, u32[]{:S(2)}, u32[]{:S(2)}) collective-permute-start(bf16[256,768]{1,0:T(8,128)(2,1)} %shard_map.92), channel_id=1, source_target_pairs={{0,4},{1,5},{2,6},{3,7},{4,8},{5,9},{6,10},{7,11},{8,12},{9,13},{1... | collective-permute-start | bytes 1179656 | tf_op jit(solution)/shard_map/ppermute | solution.py:47
  53.7 4.4 %collective-permute-start.8 = (bf16[256,768]{1,0:T(8,128)(2,1)}, bf16[256,768]{1,0:T(8,128)(2,1)S(1)}, u32[]{:S(2)}, u32[]{:S(2)}) collective-permute-start(bf16[256,768]{1,0:T(8,128)(2,1)} %shard_map.92), channel_id=1, source_target_pairs={{0,6},{1,7},{2,4},{3,5},{4,10},{5,11},{6,8},{7,9},{8,14},{9,15},{1... | collective-permute-start | bytes 1179656 | tf_op jit(solution)/shard_map/ppermute | solution.py:47
  58.1 0.8 collective-permute-done.6
  59.2 3.9 %collective-permute-start.7 = (bf16[256,768]{1,0:T(8,128)(2,1)S(1)}, bf16[256,768]{1,0:T(8,128)(2,1)S(1)}, u32[]{:S(2)}, u32[]{:S(2)}) collective-permute-start(bf16[256,768]{1,0:T(8,128)(2,1)S(1)} %get-tuple-element.38), channel_id=1, source_target_pairs={{0,2},{1,3},{2,0},{3,1},{16,18},{17,19},{18,16},{19,17}} | collective-permute-start | bytes 1179656 | tf_op jit(solution)/shard_map/ppermute | solution.py:30
  63.2 3.9 %collective-permute-done.8 = bf16[256,768]{1,0:T(8,128)(2,1)S(1)} collective-permute-done((bf16[256,768]{1,0:T(8,128)(2,1)}, bf16[256,768]{1,0:T(8,128)(2,1)S(1)}, u32[]{:S(2)}, u32[]{:S(2)}) %collective-permute-start.8) | collective-permute-done | bytes 393248 | tf_op jit(solution)/shard_map/ppermute | solution.py:47
  67.1 4.1 %collective-permute-done.7 = bf16[256,768]{1,0:T(8,128)(2,1)S(1)} collective-permute-done((bf16[256,768]{1,0:T(8,128)(2,1)S(1)}, bf16[256,768]{1,0:T(8,128)(2,1)S(1)}, u32[]{:S(2)}, u32[]{:S(2)}) %collective-permute-start.7) | collective-permute-done | bytes 393248 | tf_op jit(solution)/shard_map/ppermute | solution.py:30
  71.3 1.7 collective-permute-done.10.refs_4_
  73.0 0.8 copy-done.18
  73.8 11.8 %shard_map.93 = (bf16[256,512]{1,0:T(8,128)(2,1)}, bf16[4,768,128]{2,1,0:T(8,128)(2,1)}, bf16[4,768,128]{2,1,0:T(8,128)(2,1)}) custom-call(s32[6]{0:T(128)} %get-tuple-element.42.refs_0_, bf16[256,768]{1,0:T(8,128)(2,1)} %copy-done.2, bf16[256,768]{1,0:T(8,128)(2,1)} %copy-done.6, ...), custom_call_target="tpu_custom_call", output_to_operand_aliasing={{1}: (7, {}), {2}: (8, {})} | custom-call | tf_op jit(solution)/shard_map/pallas_call | solution.py:168
  85.6 1.5 collective-permute-start.11
  87.1 7.1 %collective-permute-done.11.refs_2_ = bf16[256,512]{1,0:T(8,128)(2,1)S(1)} collective-permute-done((bf16[256,512]{1,0:T(8,128)(2,1)}, bf16[256,512]{1,0:T(8,128)(2,1)S(1)}, u32[]{:S(2)}, u32[]{:S(2)}) %collective-permute-start.11) | collective-permute-done | bytes 262176 | tf_op jit(solution)/shard_map/ppermute | solution.py:22
  94.2 1.5 collective-permute-done.13.refs_4_
  96.4 4.1 %shard_map.94 = bf16[256,768]{1,0:T(8,128)(2,1)} custom-call(s32[6]{0:T(128)} %get-tuple-element.42.refs_0_, bf16[256,512]{1,0:T(8,128)(2,1)} %get-tuple-element.24.refs_1_, bf16[256,512]{1,0:T(8,128)(2,1)} %copy-done.21, bf16[256,512]{1,0:T(8,128)(2,1)} %copy-done.25, bf16[256,512]{1,0:T(8,128)(2,1)} %copy-done.29, bf16[4,512,768]{2,1,0:T(8,128)(2,1)} %bitcast.41, ...), custom_call_target="tpu_custom_call" | custom-call | tf_op jit(solution)/shard_map/pallas_call | solution.py:206
  100.5 1.3 collective-permute-start.14
  104.5 3.3 %collective-permute-start.16 = (bf16[256,768]{1,0:T(8,128)(2,1)}, bf16[256,768]{1,0:T(8,128)(2,1)S(1)}, u32[]{:S(2)}, u32[]{:S(2)}) collective-permute-start(bf16[256,768]{1,0:T(8,128)(2,1)} %shard_map.94), channel_id=1, source_target_pairs={{0,6},{1,7},{2,4},{3,5},{4,10},{5,11},{6,8},{7,9},{8,14},{9,15},{1... | collective-permute-start | bytes 1179656 | tf_op jit(solution)/shard_map/ppermute | solution.py:47
  107.8 3.7 %collective-permute-done.14 = bf16[256,768]{1,0:T(8,128)(2,1)S(1)} collective-permute-done((bf16[256,768]{1,0:T(8,128)(2,1)}, bf16[256,768]{1,0:T(8,128)(2,1)S(1)}, u32[]{:S(2)}, u32[]{:S(2)}) %collective-permute-start.14) | collective-permute-done | bytes 393248 | tf_op jit(solution)/shard_map/ppermute | solution.py:47
  111.8 3.6 %collective-permute-start.15 = (bf16[256,768]{1,0:T(8,128)(2,1)S(1)}, bf16[256,768]{1,0:T(8,128)(2,1)S(1)}, u32[]{:S(2)}, u32[]{:S(2)}) collective-permute-start(bf16[256,768]{1,0:T(8,128)(2,1)S(1)} %get-tuple-element.36), channel_id=1, source_target_pairs={{0,2},{1,3},{2,0},{3,1},{16,18},{17,19},{18,16},{19,17}} | collective-permute-start | bytes 1179656 | tf_op jit(solution)/shard_map/ppermute | solution.py:30
  115.5 4.0 %collective-permute-done.16 = bf16[256,768]{1,0:T(8,128)(2,1)S(1)} collective-permute-done((bf16[256,768]{1,0:T(8,128)(2,1)}, bf16[256,768]{1,0:T(8,128)(2,1)S(1)}, u32[]{:S(2)}, u32[]{:S(2)}) %collective-permute-start.16) | collective-permute-done | bytes 393248 | tf_op jit(solution)/shard_map/ppermute | solution.py:47
  119.5 4.4 %collective-permute-done.15 = bf16[256,768]{1,0:T(8,128)(2,1)S(1)} collective-permute-done((bf16[256,768]{1,0:T(8,128)(2,1)S(1)}, bf16[256,768]{1,0:T(8,128)(2,1)S(1)}, u32[]{:S(2)}, u32[]{:S(2)}) %collective-permute-start.15) | collective-permute-done | bytes 393248 | tf_op jit(solution)/shard_map/ppermute | solution.py:30
  124.0 1.7 collective-permute-done.18.refs_4_
  126.5 11.8 %shard_map.95 = (bf16[256,512]{1,0:T(8,128)(2,1)}, bf16[4,768,128]{2,1,0:T(8,128)(2,1)}, bf16[4,768,128]{2,1,0:T(8,128)(2,1)}) custom-call(s32[6]{0:T(128)} %get-tuple-element.41.refs_0_, bf16[256,768]{1,0:T(8,128)(2,1)} %copy-done.3, bf16[256,768]{1,0:T(8,128)(2,1)} %copy-done.7, ...), custom_call_target="tpu_custom_call", output_to_operand_aliasing={{1}: (7, {}), {2}: (8, {})} | custom-call | tf_op jit(solution)/shard_map/pallas_call | solution.py:168
  138.3 1.5 collective-permute-start.19
  139.8 7.1 %collective-permute-done.19.refs_2_ = bf16[256,512]{1,0:T(8,128)(2,1)S(1)} collective-permute-done((bf16[256,512]{1,0:T(8,128)(2,1)}, bf16[256,512]{1,0:T(8,128)(2,1)S(1)}, u32[]{:S(2)}, u32[]{:S(2)}) %collective-permute-start.19) | collective-permute-done | bytes 262176 | tf_op jit(solution)/shard_map/ppermute | solution.py:22
  146.9 1.5 collective-permute-done.21.refs_4_
  149.1 4.1 %shard_map.96 = bf16[256,768]{1,0:T(8,128)(2,1)} custom-call(s32[6]{0:T(128)} %get-tuple-element.41.refs_0_, bf16[256,512]{1,0:T(8,128)(2,1)} %get-tuple-element.27.refs_1_, bf16[256,512]{1,0:T(8,128)(2,1)} %copy-done.22, bf16[256,512]{1,0:T(8,128)(2,1)} %copy-done.26, bf16[256,512]{1,0:T(8,128)(2,1)} %copy-done.30, bf16[4,512,768]{2,1,0:T(8,128)(2,1)} %bitcast.42, ...), custom_call_target="tpu_custom_call" | custom-call | tf_op jit(solution)/shard_map/pallas_call | solution.py:206
  153.2 1.3 collective-permute-start.22
  157.1 2.6 %collective-permute-start.24 = (bf16[256,768]{1,0:T(8,128)(2,1)}, bf16[256,768]{1,0:T(8,128)(2,1)S(1)}, u32[]{:S(2)}, u32[]{:S(2)}) collective-permute-start(bf16[256,768]{1,0:T(8,128)(2,1)} %shard_map.96), channel_id=1, source_target_pairs={{0,6},{1,7},{2,4},{3,5},{4,10},{5,11},{6,8},{7,9},{8,14},{9,15},{1... | collective-permute-start | bytes 1179656 | tf_op jit(solution)/shard_map/ppermute | solution.py:47
  159.7 4.6 %collective-permute-done.22 = bf16[256,768]{1,0:T(8,128)(2,1)S(1)} collective-permute-done((bf16[256,768]{1,0:T(8,128)(2,1)}, bf16[256,768]{1,0:T(8,128)(2,1)S(1)}, u32[]{:S(2)}, u32[]{:S(2)}) %collective-permute-start.22) | collective-permute-done | bytes 393248 | tf_op jit(solution)/shard_map/ppermute | solution.py:47
  164.5 3.4 %collective-permute-start.23 = (bf16[256,768]{1,0:T(8,128)(2,1)S(1)}, bf16[256,768]{1,0:T(8,128)(2,1)S(1)}, u32[]{:S(2)}, u32[]{:S(2)}) collective-permute-start(bf16[256,768]{1,0:T(8,128)(2,1)S(1)} %get-tuple-element.34), channel_id=1, source_target_pairs={{0,2},{1,3},{2,0},{3,1},{16,18},{17,19},{18,16},{19,17}} | collective-permute-start | bytes 1179656 | tf_op jit(solution)/shard_map/ppermute | solution.py:30
  168.0 4.2 %collective-permute-done.24 = bf16[256,768]{1,0:T(8,128)(2,1)S(1)} collective-permute-done((bf16[256,768]{1,0:T(8,128)(2,1)}, bf16[256,768]{1,0:T(8,128)(2,1)S(1)}, u32[]{:S(2)}, u32[]{:S(2)}) %collective-permute-start.24) | collective-permute-done | bytes 393248 | tf_op jit(solution)/shard_map/ppermute | solution.py:47
  172.2 4.4 %collective-permute-done.23 = bf16[256,768]{1,0:T(8,128)(2,1)S(1)} collective-permute-done((bf16[256,768]{1,0:T(8,128)(2,1)S(1)}, bf16[256,768]{1,0:T(8,128)(2,1)S(1)}, u32[]{:S(2)}, u32[]{:S(2)}) %collective-permute-start.23) | collective-permute-done | bytes 393248 | tf_op jit(solution)/shard_map/ppermute | solution.py:30
  176.7 1.7 collective-permute-done.26.refs_4_
  179.2 11.8 %shard_map.97 = (bf16[256,512]{1,0:T(8,128)(2,1)}, bf16[4,768,128]{2,1,0:T(8,128)(2,1)}, bf16[4,768,128]{2,1,0:T(8,128)(2,1)}) custom-call(s32[6]{0:T(128)} %get-tuple-element.40.refs_0_, bf16[256,768]{1,0:T(8,128)(2,1)} %copy-done.1, bf16[256,768]{1,0:T(8,128)(2,1)} %copy-done.5, ...), custom_call_target="tpu_custom_call", output_to_operand_aliasing={{1}: (7, {}), {2}: (8, {})} | custom-call | tf_op jit(solution)/shard_map/pallas_call | solution.py:168
  191.0 1.6 collective-permute-start.27
  192.6 7.1 %collective-permute-done.27.refs_2_ = bf16[256,512]{1,0:T(8,128)(2,1)S(1)} collective-permute-done((bf16[256,512]{1,0:T(8,128)(2,1)}, bf16[256,512]{1,0:T(8,128)(2,1)S(1)}, u32[]{:S(2)}, u32[]{:S(2)}) %collective-permute-start.27) | collective-permute-done | bytes 262176 | tf_op jit(solution)/shard_map/ppermute | solution.py:22
  199.6 1.5 collective-permute-done.29.refs_4_
  201.9 4.1 %shard_map.98 = bf16[256,768]{1,0:T(8,128)(2,1)} custom-call(s32[6]{0:T(128)} %get-tuple-element.40.refs_0_, bf16[256,512]{1,0:T(8,128)(2,1)} %get-tuple-element.30.refs_1_, bf16[256,512]{1,0:T(8,128)(2,1)} %copy-done.23, bf16[256,512]{1,0:T(8,128)(2,1)} %copy-done.27, bf16[256,512]{1,0:T(8,128)(2,1)} %copy-done.31, bf16[4,512,768]{2,1,0:T(8,128)(2,1)} %bitcast.43, ...), custom_call_target="tpu_custom_call" | custom-call | tf_op jit(solution)/shard_map/pallas_call | solution.py:206
  206.0 2.3 %maximum_bitcast_fusion = bf16[4,1,256,768]{3,2,1,0:T(8,128)(2,1)} fusion(bf16[1,256,768]{2,1,0:T(8,128)(2,1)} %bitcast.47, bf16[1,256,768]{2,1,0:T(8,128)(2,1)S(1)} %bitcast.46, bf16[1,256,768]{2,1,0:T(8,128)(2,1)S(1)} %bitcast.45, bf16[1,256,768]{2,1,0:T(8,128)(2,1)S(1)} %bitcast.44), kind=kLoop, calls=%fused_computation.3 | loop fusion | flops 2359296 | bytes 3145728 | tf_op jit(solution)/shard_map/broadcast_in_dim | solution.py:290
  (112 shorter events, 13.5 us)
Async XLA Ops:
  4.0 14.4 %copy-start.4 = (bf16[256,768]{1,0:T(8,128)(2,1)}, bf16[256,768]{1,0:T(8,128)(2,1)S(1)}, u32[]{:S(2)}) copy-start(bf16[256,768]{1,0:T(8,128)(2,1)S(1)} %fusion.3.refs_1_.refs_6_) | copy-start | bytes 1179652
  4.0 12.1 %collective-permute-start = (bf16[256,768]{1,0:T(8,128)(2,1)S(1)}, bf16[256,768]{1,0:T(8,128)(2,1)S(1)}, u32[]{:S(2)}, u32[]{:S(2)}) collective-permute-start(bf16[256,768]{1,0:T(8,128)(2,1)S(1)} %fusion.3.refs_1_.refs_6_), channel_id=1, source_target_pairs={{0,2},{1,3},{2,0},{3,1},{4,6},{5,7},{6,4},{7,5},{8,10},{9,11},{10,... | collective-permute-start | bytes 1179656 | tf_op jit(solution)/shard_map/ppermute | solution.py:22
  16.1 2.3 %copy-start.11 = (bf16[256,768]{1,0:T(8,128)(2,1)}, bf16[256,768]{1,0:T(8,128)(2,1)S(1)}, u32[]{:S(2)}) copy-start(bf16[256,768]{1,0:T(8,128)(2,1)S(1)} %collective-permute-done.refs_2_) | copy-start | bytes 1179652
  16.1 1.7 collective-permute-start.2
  16.1 2.3 %collective-permute-start.1 = (bf16[256,768]{1,0:T(8,128)(2,1)S(1)}, bf16[256,768]{1,0:T(8,128)(2,1)S(1)}, u32[]{:S(2)}, u32[]{:S(2)}) collective-permute-start(bf16[256,768]{1,0:T(8,128)(2,1)S(1)} %fusion.3.refs_1_.refs_6_), channel_id=1, source_target_pairs={{0,1},{1,0},{2,3},{3,2},{4,5},{5,4},{6,7},{7,6},{8,9},{9,8},{10,11... | collective-permute-start | bytes 1179656 | tf_op jit(solution)/shard_map/ppermute | solution.py:40
  31.0 8.6 %collective-permute-start.3 = (bf16[256,512]{1,0:T(8,128)(2,1)}, bf16[256,512]{1,0:T(8,128)(2,1)S(1)}, u32[]{:S(2)}, u32[]{:S(2)}) collective-permute-start(bf16[256,512]{1,0:T(8,128)(2,1)} %get-tuple-element.21.refs_1_), channel_id=1, source_target_pairs={{0,2},{1,3},{2,0},{3,1},{4,6},{5,7},{6,4},{7,5},{8,10},{9,11},{10,... | collective-permute-start | bytes 786440 | tf_op jit(solution)/shard_map/ppermute | solution.py:22
  32.7 6.8 %collective-permute-start.4 = (bf16[256,512]{1,0:T(8,128)(2,1)}, bf16[256,512]{1,0:T(8,128)(2,1)S(1)}, u32[]{:S(2)}, u32[]{:S(2)}) collective-permute-start(bf16[256,512]{1,0:T(8,128)(2,1)} %get-tuple-element.21.refs_1_), channel_id=1, source_target_pairs={{0,1},{1,0},{2,3},{3,2},{4,5},{5,4},{6,7},{7,6},{8,9},{9,8},{10,11... | collective-permute-start | bytes 786440 | tf_op jit(solution)/shard_map/ppermute | solution.py:40
  39.5 1.5 copy-start.20
  39.5 1.5 collective-permute-start.5
  41.8 10.5 %copy-start.32 = (s32[4]{0:T(128)S(1)}, s32[4]{0:T(128)}, u32[]{:S(2)}) copy-start(s32[4]{0:T(128)} %param.11) | copy-start | bytes 52
  41.8 17.2 %copy-start = (bf16[768,768]{1,0:T(8,128)(2,1)S(1)}, bf16[768,768]{1,0:T(8,128)(2,1)}, u32[]{:S(2)}) copy-start(bf16[768,768]{1,0:T(8,128)(2,1)} %param.9) | copy-start | bytes 3538948
  46.0 13.0 %collective-permute-start.6 = (bf16[256,768]{1,0:T(8,128)(2,1)}, bf16[256,768]{1,0:T(8,128)(2,1)S(1)}, u32[]{:S(2)}, u32[]{:S(2)}) collective-permute-start(bf16[256,768]{1,0:T(8,128)(2,1)} %shard_map.92), channel_id=1, source_target_pairs={{0,4},{1,5},{2,6},{3,7},{4,8},{5,9},{6,10},{7,11},{8,12},{9,13},{1... | collective-permute-start | bytes 1179656 | tf_op jit(solution)/shard_map/ppermute | solution.py:47
  53.7 13.4 %collective-permute-start.8 = (bf16[256,768]{1,0:T(8,128)(2,1)}, bf16[256,768]{1,0:T(8,128)(2,1)S(1)}, u32[]{:S(2)}, u32[]{:S(2)}) collective-permute-start(bf16[256,768]{1,0:T(8,128)(2,1)} %shard_map.92), channel_id=1, source_target_pairs={{0,6},{1,7},{2,4},{3,5},{4,10},{5,11},{6,8},{7,9},{8,14},{9,15},{1... | collective-permute-start | bytes 1179656 | tf_op jit(solution)/shard_map/ppermute | solution.py:47
  59.2 13.8 %copy-start.2 = (bf16[256,768]{1,0:T(8,128)(2,1)}, bf16[256,768]{1,0:T(8,128)(2,1)S(1)}, u32[]{:S(2)}) copy-start(bf16[256,768]{1,0:T(8,128)(2,1)S(1)} %get-tuple-element.37.refs_1_.refs_6_) | copy-start | bytes 1179652
  59.2 12.0 %collective-permute-start.7 = (bf16[256,768]{1,0:T(8,128)(2,1)S(1)}, bf16[256,768]{1,0:T(8,128)(2,1)S(1)}, u32[]{:S(2)}, u32[]{:S(2)}) collective-permute-start(bf16[256,768]{1,0:T(8,128)(2,1)S(1)} %get-tuple-element.38), channel_id=1, source_target_pairs={{0,2},{1,3},{2,0},{3,1},{16,18},{17,19},{18,16},{19,17}} | collective-permute-start | bytes 1179656 | tf_op jit(solution)/shard_map/ppermute | solution.py:30
  63.1 8.2 %collective-permute-start.9 = (bf16[256,768]{1,0:T(8,128)(2,1)S(1)}, bf16[256,768]{1,0:T(8,128)(2,1)S(1)}, u32[]{:S(2)}, u32[]{:S(2)}) collective-permute-start(bf16[256,768]{1,0:T(8,128)(2,1)S(1)} %get-tuple-element.37.refs_1_.refs_6_), channel_id=1, source_target_pairs={{0,1},{1,0},{2,3},{3,2},{4,5},{5,4},{6,7},{7,6},{8,9},{9,8},{10,11... | collective-permute-start | bytes 1179656 | tf_op jit(solution)/shard_map/ppermute | solution.py:40
  71.2 1.8 copy-start.6
  71.2 1.8 collective-permute-start.10
  71.3 1.7 copy-start.13
  85.6 8.6 %collective-permute-start.11 = (bf16[256,512]{1,0:T(8,128)(2,1)}, bf16[256,512]{1,0:T(8,128)(2,1)S(1)}, u32[]{:S(2)}, u32[]{:S(2)}) collective-permute-start(bf16[256,512]{1,0:T(8,128)(2,1)} %get-tuple-element.24.refs_1_), channel_id=1, source_target_pairs={{0,2},{1,3},{2,0},{3,1},{4,6},{5,7},{6,4},{7,5},{8,10},{9,11},{10,... | collective-permute-start | bytes 786440 | tf_op jit(solution)/shard_map/ppermute | solution.py:22
  87.1 7.1 %collective-permute-start.12 = (bf16[256,512]{1,0:T(8,128)(2,1)}, bf16[256,512]{1,0:T(8,128)(2,1)S(1)}, u32[]{:S(2)}, u32[]{:S(2)}) collective-permute-start(bf16[256,512]{1,0:T(8,128)(2,1)} %get-tuple-element.24.refs_1_), channel_id=1, source_target_pairs={{0,1},{1,0},{2,3},{3,2},{4,5},{5,4},{6,7},{7,6},{8,9},{9,8},{10,11... | collective-permute-start | bytes 786440 | tf_op jit(solution)/shard_map/ppermute | solution.py:40
  94.2 1.5 copy-start.21
  94.2 1.5 collective-permute-start.13
  100.5 11.0 %collective-permute-start.14 = (bf16[256,768]{1,0:T(8,128)(2,1)}, bf16[256,768]{1,0:T(8,128)(2,1)S(1)}, u32[]{:S(2)}, u32[]{:S(2)}) collective-permute-start(bf16[256,768]{1,0:T(8,128)(2,1)} %shard_map.94), channel_id=1, source_target_pairs={{0,4},{1,5},{2,6},{3,7},{4,8},{5,9},{6,10},{7,11},{8,12},{9,13},{1... | collective-permute-start | bytes 1179656 | tf_op jit(solution)/shard_map/ppermute | solution.py:47
  104.5 15.0 %collective-permute-start.16 = (bf16[256,768]{1,0:T(8,128)(2,1)}, bf16[256,768]{1,0:T(8,128)(2,1)S(1)}, u32[]{:S(2)}, u32[]{:S(2)}) collective-permute-start(bf16[256,768]{1,0:T(8,128)(2,1)} %shard_map.94), channel_id=1, source_target_pairs={{0,6},{1,7},{2,4},{3,5},{4,10},{5,11},{6,8},{7,9},{8,14},{9,15},{1... | collective-permute-start | bytes 1179656 | tf_op jit(solution)/shard_map/ppermute | solution.py:47
  111.8 13.9 %copy-start.3 = (bf16[256,768]{1,0:T(8,128)(2,1)}, bf16[256,768]{1,0:T(8,128)(2,1)S(1)}, u32[]{:S(2)}) copy-start(bf16[256,768]{1,0:T(8,128)(2,1)S(1)} %get-tuple-element.35.refs_1_.refs_6_) | copy-start | bytes 1179652
  111.8 12.1 %collective-permute-start.15 = (bf16[256,768]{1,0:T(8,128)(2,1)S(1)}, bf16[256,768]{1,0:T(8,128)(2,1)S(1)}, u32[]{:S(2)}, u32[]{:S(2)}) collective-permute-start(bf16[256,768]{1,0:T(8,128)(2,1)S(1)} %get-tuple-element.36), channel_id=1, source_target_pairs={{0,2},{1,3},{2,0},{3,1},{16,18},{17,19},{18,16},{19,17}} | collective-permute-start | bytes 1179656 | tf_op jit(solution)/shard_map/ppermute | solution.py:30
  115.4 8.6 %collective-permute-start.17 = (bf16[256,768]{1,0:T(8,128)(2,1)S(1)}, bf16[256,768]{1,0:T(8,128)(2,1)S(1)}, u32[]{:S(2)}, u32[]{:S(2)}) collective-permute-start(bf16[256,768]{1,0:T(8,128)(2,1)S(1)} %get-tuple-element.35.refs_1_.refs_6_), channel_id=1, source_target_pairs={{0,1},{1,0},{2,3},{3,2},{4,5},{5,4},{6,7},{7,6},{8,9},{9,8},{10,11... | collective-permute-start | bytes 1179656 | tf_op jit(solution)/shard_map/ppermute | solution.py:40
  123.9 1.8 copy-start.7
  123.9 1.8 collective-permute-start.18
  124.0 1.7 copy-start.14
  138.3 8.6 %collective-permute-start.19 = (bf16[256,512]{1,0:T(8,128)(2,1)}, bf16[256,512]{1,0:T(8,128)(2,1)S(1)}, u32[]{:S(2)}, u32[]{:S(2)}) collective-permute-start(bf16[256,512]{1,0:T(8,128)(2,1)} %get-tuple-element.27.refs_1_), channel_id=1, source_target_pairs={{0,2},{1,3},{2,0},{3,1},{4,6},{5,7},{6,4},{7,5},{8,10},{9,11},{10,... | collective-permute-start | bytes 786440 | tf_op jit(solution)/shard_map/ppermute | solution.py:22
  139.8 7.1 %collective-permute-start.20 = (bf16[256,512]{1,0:T(8,128)(2,1)}, bf16[256,512]{1,0:T(8,128)(2,1)S(1)}, u32[]{:S(2)}, u32[]{:S(2)}) collective-permute-start(bf16[256,512]{1,0:T(8,128)(2,1)} %get-tuple-element.27.refs_1_), channel_id=1, source_target_pairs={{0,1},{1,0},{2,3},{3,2},{4,5},{5,4},{6,7},{7,6},{8,9},{9,8},{10,11... | collective-permute-start | bytes 786440 | tf_op jit(solution)/shard_map/ppermute | solution.py:40
  146.9 1.5 collective-permute-start.21
  153.2 11.0 %collective-permute-start.22 = (bf16[256,768]{1,0:T(8,128)(2,1)}, bf16[256,768]{1,0:T(8,128)(2,1)S(1)}, u32[]{:S(2)}, u32[]{:S(2)}) collective-permute-start(bf16[256,768]{1,0:T(8,128)(2,1)} %shard_map.96), channel_id=1, source_target_pairs={{0,4},{1,5},{2,6},{3,7},{4,8},{5,9},{6,10},{7,11},{8,12},{9,13},{1... | collective-permute-start | bytes 1179656 | tf_op jit(solution)/shard_map/ppermute | solution.py:47
  157.1 15.1 %collective-permute-start.24 = (bf16[256,768]{1,0:T(8,128)(2,1)}, bf16[256,768]{1,0:T(8,128)(2,1)S(1)}, u32[]{:S(2)}, u32[]{:S(2)}) collective-permute-start(bf16[256,768]{1,0:T(8,128)(2,1)} %shard_map.96), channel_id=1, source_target_pairs={{0,6},{1,7},{2,4},{3,5},{4,10},{5,11},{6,8},{7,9},{8,14},{9,15},{1... | collective-permute-start | bytes 1179656 | tf_op jit(solution)/shard_map/ppermute | solution.py:47
  164.5 13.9 %copy-start.1 = (bf16[256,768]{1,0:T(8,128)(2,1)}, bf16[256,768]{1,0:T(8,128)(2,1)S(1)}, u32[]{:S(2)}) copy-start(bf16[256,768]{1,0:T(8,128)(2,1)S(1)} %get-tuple-element.33.refs_1_.refs_6_) | copy-start | bytes 1179652
  164.5 12.1 %collective-permute-start.23 = (bf16[256,768]{1,0:T(8,128)(2,1)S(1)}, bf16[256,768]{1,0:T(8,128)(2,1)S(1)}, u32[]{:S(2)}, u32[]{:S(2)}) collective-permute-start(bf16[256,768]{1,0:T(8,128)(2,1)S(1)} %get-tuple-element.34), channel_id=1, source_target_pairs={{0,2},{1,3},{2,0},{3,1},{16,18},{17,19},{18,16},{19,17}} | collective-permute-start | bytes 1179656 | tf_op jit(solution)/shard_map/ppermute | solution.py:30
  167.9 8.8 %collective-permute-start.25 = (bf16[256,768]{1,0:T(8,128)(2,1)S(1)}, bf16[256,768]{1,0:T(8,128)(2,1)S(1)}, u32[]{:S(2)}, u32[]{:S(2)}) collective-permute-start(bf16[256,768]{1,0:T(8,128)(2,1)S(1)} %get-tuple-element.33.refs_1_.refs_6_), channel_id=1, source_target_pairs={{0,1},{1,0},{2,3},{3,2},{4,5},{5,4},{6,7},{7,6},{8,9},{9,8},{10,11... | collective-permute-start | bytes 1179656 | tf_op jit(solution)/shard_map/ppermute | solution.py:40
  176.6 1.8 copy-start.5
  176.6 1.8 collective-permute-start.26
  176.7 1.7 copy-start.12
  191.0 15.0 %copy-start.8 = (bf16[256,768]{1,0:T(8,128)(2,1)S(1)}, bf16[256,768]{1,0:T(8,128)(2,1)}, u32[]{:S(2)}) copy-start(bf16[256,768]{1,0:T(8,128)(2,1)} %shard_map.92) | copy-start | bytes 1179652
  191.0 15.0 %copy-start.9 = (bf16[256,768]{1,0:T(8,128)(2,1)S(1)}, bf16[256,768]{1,0:T(8,128)(2,1)}, u32[]{:S(2)}) copy-start(bf16[256,768]{1,0:T(8,128)(2,1)} %shard_map.94) | copy-start | bytes 1179652
  191.0 15.0 %copy-start.10 = (bf16[256,768]{1,0:T(8,128)(2,1)S(1)}, bf16[256,768]{1,0:T(8,128)(2,1)}, u32[]{:S(2)}) copy-start(bf16[256,768]{1,0:T(8,128)(2,1)} %shard_map.96) | copy-start | bytes 1179652
  191.0 8.6 %collective-permute-start.27 = (bf16[256,512]{1,0:T(8,128)(2,1)}, bf16[256,512]{1,0:T(8,128)(2,1)S(1)}, u32[]{:S(2)}, u32[]{:S(2)}) collective-permute-start(bf16[256,512]{1,0:T(8,128)(2,1)} %get-tuple-element.30.refs_1_), channel_id=1, source_target_pairs={{0,2},{1,3},{2,0},{3,1},{4,6},{5,7},{6,4},{7,5},{8,10},{9,11},{10,... | collective-permute-start | bytes 786440 | tf_op jit(solution)/shard_map/ppermute | solution.py:22
  192.5 7.1 %collective-permute-start.28 = (bf16[256,512]{1,0:T(8,128)(2,1)}, bf16[256,512]{1,0:T(8,128)(2,1)S(1)}, u32[]{:S(2)}, u32[]{:S(2)}) collective-permute-start(bf16[256,512]{1,0:T(8,128)(2,1)} %get-tuple-element.30.refs_1_), channel_id=1, source_target_pairs={{0,1},{1,0},{2,3},{3,2},{4,5},{5,4},{6,7},{7,6},{8,9},{9,8},{10,11... | collective-permute-start | bytes 786440 | tf_op jit(solution)/shard_map/ppermute | solution.py:40
  199.6 1.5 collective-permute-start.29
  (15 other events, 15.8 us)

commit v19 on v18

--- a/solution.py
+++ b/solution.py
@@ -79,11 +79,11 @@
 
 def block_kernel(*refs):
     where_ref = refs[0]
-    count = len(refs) - 10
+    count = len(refs) - 11
     part_refs = refs[1 : 1 + count]
     scale_ref, weights_ref, keys_ref, values_ref = refs[1 + count : 5 + count]
     heads_ref, keys_out, values_out = refs[5 + count : 8 + count]
-    shaped_ref, staging_ref = refs[8 + count :]
+    shaped_ref, staging_ref, value_staging_ref = refs[8 + count :]
     start = where_ref[0]
     patch_count = where_ref[1]
     head_dim = keys_ref.shape[2]
@@ -121,10 +121,12 @@
     window = staging_ref[pl.ds(start, span)]
     staging_ref[pl.ds(start, span)] = jnp.where(live, fresh_keys.astype(jnp.float32), window)
     keys = staging_ref[:seq_len].astype(jnp.bfloat16)
-    staging_ref[:seq_len] = values_ref[0].astype(jnp.float32)
-    window = staging_ref[pl.ds(start, span)]
-    staging_ref[pl.ds(start, span)] = jnp.where(live, fresh_values.astype(jnp.float32), window)
-    values = staging_ref[:seq_len].astype(jnp.bfloat16)
+    value_staging_ref[:seq_len] = values_ref[0].astype(jnp.float32)
+    window = value_staging_ref[pl.ds(start, span)]
+    value_staging_ref[pl.ds(start, span)] = jnp.where(
+        live, fresh_values.astype(jnp.float32), window
+    )
+    values = value_staging_ref[:seq_len].astype(jnp.bfloat16)
     keys_out[0] = keys
     values_out[0] = values
     scores = lax.dot_general(
@@ -163,6 +165,7 @@
         scratch_shapes=[
             pltpu.VMEM((count, span, width), jnp.bfloat16),
             pltpu.VMEM((seq_len + span, head_dim), jnp.float32),
+            pltpu.VMEM((seq_len + span, head_dim), jnp.float32),
         ],
     )
     return pl.pallas_call(

time: 209 us -> 209 us (level)
  no operation moved by 1% of the time
where the time goes in v19:
time: 209 us; the launch traced here: 208 us
  waiting for transfers between devices  82.5 us (39%)
  Pallas kernels  63.6 us (30%)
  starting transfers between devices  37.9 us (18%)
  other arithmetic  9.93 us (5%)
  local copies, waits for them, and re-layouts  7.81 us (4%)
  between operations  6.34 us (3%)
    pallas_call x4, Pallas kernels, attend_block(): pl.pallas_call(block_kernel, grid_spec=grid_spec, out_shape=[jax.ShapeDty...  47.1 us
    ppermute x5, waiting for transfers between devices, across_chips(): lax.ppermute(block, 'seq', [(source, (source + step) % count) for source...  36.2 us
    ppermute x6, waiting for transfers between devices, to_next_section(): lax.ppermute(block, ('section', 'seq'), [(section * count + source, (sect...  21.2 us
    ppermute x6, starting transfers between devices, to_next_section(): lax.ppermute(block, ('section', 'seq'), [(section * count + source, (sect...  16.7 us
    pallas_call x4, Pallas kernels, leave_block(): pl.pallas_call(exit_kernel, in_specs=[smem] + [vmem] * (count + 3), out_s...  16.5 us
    ppermute x3, waiting for transfers between devices, across_chips_first_section(): lax.ppermute(block, ('section', 'seq'), [(source, (source + step) % count...  12.8 us
    ppermute x16, waiting for transfers between devices, with_partner(): return parts + [lax.ppermute(part, 'seq', to_partner) for part in parts]  12.3 us
    ppermute x3, starting transfers between devices, across_chips_first_section(): lax.ppermute(block, ('section', 'seq'), [(source, (source + step) % count...  10.9 us
  transfers between devices with their start and end apart: 30, of which 23 were waited for; matrix products, arithmetic and copies ran while one was open for 3% of the time, Pallas kernels for 0%

profile of v19, /device:TPU:0, one launch (start us, length us, event | category | flops | bytes accessed | tf_op | source)
XLA Modules:
  0.0 208.1 jit_solution(171800093150705273)
XLA Ops:
  0.0 0.8 reduce-window.9
  0.8 1.3 bitcast_subtract_fusion
  2.8 1.2 fusion.3.refs_1_.refs_6_
  4.0 3.0 %collective-permute-start = (bf16[256,768]{1,0:T(8,128)(2,1)S(1)}, bf16[256,768]{1,0:T(8,128)(2,1)S(1)}, u32[]{:S(2)}, u32[]{:S(2)}) collective-permute-start(bf16[256,768]{1,0:T(8,128)(2,1)S(1)} %fusion.3.refs_1_.refs_6_), channel_id=1, source_target_pairs={{0,2},{1,3},{2,0},{3,1},{4,6},{5,7},{6,4},{7,5},{8,10},{9,11},{10,... | collective-permute-start | bytes 1179656 | tf_op jit(solution)/shard_map/ppermute | solution.py:22
  7.9 8.2 %collective-permute-done.refs_2_ = bf16[256,768]{1,0:T(8,128)(2,1)S(1)} collective-permute-done((bf16[256,768]{1,0:T(8,128)(2,1)S(1)}, bf16[256,768]{1,0:T(8,128)(2,1)S(1)}, u32[]{:S(2)}, u32[]{:S(2)}) %collective-permute-start) | collective-permute-done | bytes 393248 | tf_op jit(solution)/shard_map/ppermute | solution.py:22
  19.2 11.8 %shard_map.91 = (bf16[256,512]{1,0:T(8,128)(2,1)}, bf16[4,768,128]{2,1,0:T(8,128)(2,1)}, bf16[4,768,128]{2,1,0:T(8,128)(2,1)}) custom-call(s32[6]{0:T(128)} %get-tuple-element.39.refs_0_, bf16[256,768]{1,0:T(8,128)(2,1)} %copy-done.4, bf16[256,768]{1,0:T(8,128)(2,1)} %copy-done.11, bf16[256,768]{1,0:T(8,128)(2,1)} %copy-done.16, ...), custom_call_target="tpu_custom_call" | custom-call | tf_op jit(solution)/shard_map/pallas_call | solution.py:171
  30.9 1.7 collective-permute-start.3
  32.7 6.8 %collective-permute-done.3.refs_2_ = bf16[256,512]{1,0:T(8,128)(2,1)S(1)} collective-permute-done((bf16[256,512]{1,0:T(8,128)(2,1)}, bf16[256,512]{1,0:T(8,128)(2,1)S(1)}, u32[]{:S(2)}, u32[]{:S(2)}) %collective-permute-start.3) | collective-permute-done | bytes 262176 | tf_op jit(solution)/shard_map/ppermute | solution.py:22
  39.5 1.5 collective-permute-done.5.refs_4_
  41.7 4.2 %shard_map.92 = bf16[256,768]{1,0:T(8,128)(2,1)} custom-call(s32[6]{0:T(128)} %get-tuple-element.39.refs_0_, bf16[256,512]{1,0:T(8,128)(2,1)} %get-tuple-element.21.refs_1_, bf16[256,512]{1,0:T(8,128)(2,1)} %copy-done.20, bf16[256,512]{1,0:T(8,128)(2,1)} %copy-done.24, bf16[256,512]{1,0:T(8,128)(2,1)} %copy-done.28, bf16[4,512,768]{2,1,0:T(8,128)(2,1)} %bitcast.40, ...), custom_call_target="tpu_custom_call" | custom-call | tf_op jit(solution)/shard_map/pallas_call | solution.py:209
  45.9 3.7 %collective-permute-start.6 = (bf16[256,768]{1,0:T(8,128)(2,1)}, bf16[256,768]{1,0:T(8,128)(2,1)S(1)}, u32[]{:S(2)}, u32[]{:S(2)}) collective-permute-start(bf16[256,768]{1,0:T(8,128)(2,1)} %shard_map.92), channel_id=1, source_target_pairs={{0,4},{1,5},{2,6},{3,7},{4,8},{5,9},{6,10},{7,11},{8,12},{9,13},{1... | collective-permute-start | bytes 1179656 | tf_op jit(solution)/shard_map/ppermute | solution.py:47
  53.6 4.4 %collective-permute-start.8 = (bf16[256,768]{1,0:T(8,128)(2,1)}, bf16[256,768]{1,0:T(8,128)(2,1)S(1)}, u32[]{:S(2)}, u32[]{:S(2)}) collective-permute-start(bf16[256,768]{1,0:T(8,128)(2,1)} %shard_map.92), channel_id=1, source_target_pairs={{0,6},{1,7},{2,4},{3,5},{4,10},{5,11},{6,8},{7,9},{8,14},{9,15},{1... | collective-permute-start | bytes 1179656 | tf_op jit(solution)/shard_map/ppermute | solution.py:47
  58.0 0.9 collective-permute-done.6
  59.2 3.9 %collective-permute-start.7 = (bf16[256,768]{1,0:T(8,128)(2,1)S(1)}, bf16[256,768]{1,0:T(8,128)(2,1)S(1)}, u32[]{:S(2)}, u32[]{:S(2)}) collective-permute-start(bf16[256,768]{1,0:T(8,128)(2,1)S(1)} %get-tuple-element.38), channel_id=1, source_target_pairs={{0,2},{1,3},{2,0},{3,1},{16,18},{17,19},{18,16},{19,17}} | collective-permute-start | bytes 1179656 | tf_op jit(solution)/shard_map/ppermute | solution.py:30
  63.2 3.9 %collective-permute-done.8 = bf16[256,768]{1,0:T(8,128)(2,1)S(1)} collective-permute-done((bf16[256,768]{1,0:T(8,128)(2,1)}, bf16[256,768]{1,0:T(8,128)(2,1)S(1)}, u32[]{:S(2)}, u32[]{:S(2)}) %collective-permute-start.8) | collective-permute-done | bytes 393248 | tf_op jit(solution)/shard_map/ppermute | solution.py:47
  67.1 4.1 %collective-permute-done.7 = bf16[256,768]{1,0:T(8,128)(2,1)S(1)} collective-permute-done((bf16[256,768]{1,0:T(8,128)(2,1)S(1)}, bf16[256,768]{1,0:T(8,128)(2,1)S(1)}, u32[]{:S(2)}, u32[]{:S(2)}) %collective-permute-start.7) | collective-permute-done | bytes 393248 | tf_op jit(solution)/shard_map/ppermute | solution.py:30
  71.3 1.7 collective-permute-done.10.refs_4_
  73.0 0.8 copy-done.18
  73.7 11.8 %shard_map.93 = (bf16[256,512]{1,0:T(8,128)(2,1)}, bf16[4,768,128]{2,1,0:T(8,128)(2,1)}, bf16[4,768,128]{2,1,0:T(8,128)(2,1)}) custom-call(s32[6]{0:T(128)} %get-tuple-element.42.refs_0_, bf16[256,768]{1,0:T(8,128)(2,1)} %copy-done.2, bf16[256,768]{1,0:T(8,128)(2,1)} %copy-done.6, ...), custom_call_target="tpu_custom_call", output_to_operand_aliasing={{1}: (7, {}), {2}: (8, {})} | custom-call | tf_op jit(solution)/shard_map/pallas_call | solution.py:171
  85.5 1.5 collective-permute-start.11
  87.0 7.1 %collective-permute-done.11.refs_2_ = bf16[256,512]{1,0:T(8,128)(2,1)S(1)} collective-permute-done((bf16[256,512]{1,0:T(8,128)(2,1)}, bf16[256,512]{1,0:T(8,128)(2,1)S(1)}, u32[]{:S(2)}, u32[]{:S(2)}) %collective-permute-start.11) | collective-permute-done | bytes 262176 | tf_op jit(solution)/shard_map/ppermute | solution.py:22
  94.1 1.5 collective-permute-done.13.refs_4_
  96.3 4.1 %shard_map.94 = bf16[256,768]{1,0:T(8,128)(2,1)} custom-call(s32[6]{0:T(128)} %get-tuple-element.42.refs_0_, bf16[256,512]{1,0:T(8,128)(2,1)} %get-tuple-element.24.refs_1_, bf16[256,512]{1,0:T(8,128)(2,1)} %copy-done.21, bf16[256,512]{1,0:T(8,128)(2,1)} %copy-done.25, bf16[256,512]{1,0:T(8,128)(2,1)} %copy-done.29, bf16[4,512,768]{2,1,0:T(8,128)(2,1)} %bitcast.41, ...), custom_call_target="tpu_custom_call" | custom-call | tf_op jit(solution)/shard_map/pallas_call | solution.py:209
  100.4 1.3 collective-permute-start.14
  104.4 3.3 %collective-permute-start.16 = (bf16[256,768]{1,0:T(8,128)(2,1)}, bf16[256,768]{1,0:T(8,128)(2,1)S(1)}, u32[]{:S(2)}, u32[]{:S(2)}) collective-permute-start(bf16[256,768]{1,0:T(8,128)(2,1)} %shard_map.94), channel_id=1, source_target_pairs={{0,6},{1,7},{2,4},{3,5},{4,10},{5,11},{6,8},{7,9},{8,14},{9,15},{1... | collective-permute-start | bytes 1179656 | tf_op jit(solution)/shard_map/ppermute | solution.py:47
  107.7 3.7 %collective-permute-done.14 = bf16[256,768]{1,0:T(8,128)(2,1)S(1)} collective-permute-done((bf16[256,768]{1,0:T(8,128)(2,1)}, bf16[256,768]{1,0:T(8,128)(2,1)S(1)}, u32[]{:S(2)}, u32[]{:S(2)}) %collective-permute-start.14) | collective-permute-done | bytes 393248 | tf_op jit(solution)/shard_map/ppermute | solution.py:47
  111.7 3.6 %collective-permute-start.15 = (bf16[256,768]{1,0:T(8,128)(2,1)S(1)}, bf16[256,768]{1,0:T(8,128)(2,1)S(1)}, u32[]{:S(2)}, u32[]{:S(2)}) collective-permute-start(bf16[256,768]{1,0:T(8,128)(2,1)S(1)} %get-tuple-element.36), channel_id=1, source_target_pairs={{0,2},{1,3},{2,0},{3,1},{16,18},{17,19},{18,16},{19,17}} | collective-permute-start | bytes 1179656 | tf_op jit(solution)/shard_map/ppermute | solution.py:30
  115.4 4.0 %collective-permute-done.16 = bf16[256,768]{1,0:T(8,128)(2,1)S(1)} collective-permute-done((bf16[256,768]{1,0:T(8,128)(2,1)}, bf16[256,768]{1,0:T(8,128)(2,1)S(1)}, u32[]{:S(2)}, u32[]{:S(2)}) %collective-permute-start.16) | collective-permute-done | bytes 393248 | tf_op jit(solution)/shard_map/ppermute | solution.py:47
  119.4 4.4 %collective-permute-done.15 = bf16[256,768]{1,0:T(8,128)(2,1)S(1)} collective-permute-done((bf16[256,768]{1,0:T(8,128)(2,1)S(1)}, bf16[256,768]{1,0:T(8,128)(2,1)S(1)}, u32[]{:S(2)}, u32[]{:S(2)}) %collective-permute-start.15) | collective-permute-done | bytes 393248 | tf_op jit(solution)/shard_map/ppermute | solution.py:30
  123.9 1.7 collective-permute-done.18.refs_4_
  126.4 11.8 %shard_map.95 = (bf16[256,512]{1,0:T(8,128)(2,1)}, bf16[4,768,128]{2,1,0:T(8,128)(2,1)}, bf16[4,768,128]{2,1,0:T(8,128)(2,1)}) custom-call(s32[6]{0:T(128)} %get-tuple-element.41.refs_0_, bf16[256,768]{1,0:T(8,128)(2,1)} %copy-done.3, bf16[256,768]{1,0:T(8,128)(2,1)} %copy-done.7, ...), custom_call_target="tpu_custom_call", output_to_operand_aliasing={{1}: (7, {}), {2}: (8, {})} | custom-call | tf_op jit(solution)/shard_map/pallas_call | solution.py:171
  138.1 1.5 collective-permute-start.19
  139.7 7.0 %collective-permute-done.19.refs_2_ = bf16[256,512]{1,0:T(8,128)(2,1)S(1)} collective-permute-done((bf16[256,512]{1,0:T(8,128)(2,1)}, bf16[256,512]{1,0:T(8,128)(2,1)S(1)}, u32[]{:S(2)}, u32[]{:S(2)}) %collective-permute-start.19) | collective-permute-done | bytes 262176 | tf_op jit(solution)/shard_map/ppermute | solution.py:22
  146.7 1.5 collective-permute-done.21.refs_4_
  149.0 4.1 %shard_map.96 = bf16[256,768]{1,0:T(8,128)(2,1)} custom-call(s32[6]{0:T(128)} %get-tuple-element.41.refs_0_, bf16[256,512]{1,0:T(8,128)(2,1)} %get-tuple-element.27.refs_1_, bf16[256,512]{1,0:T(8,128)(2,1)} %copy-done.22, bf16[256,512]{1,0:T(8,128)(2,1)} %copy-done.26, bf16[256,512]{1,0:T(8,128)(2,1)} %copy-done.30, bf16[4,512,768]{2,1,0:T(8,128)(2,1)} %bitcast.42, ...), custom_call_target="tpu_custom_call" | custom-call | tf_op jit(solution)/shard_map/pallas_call | solution.py:209
  153.1 1.3 collective-permute-start.22
  156.9 2.6 %collective-permute-start.24 = (bf16[256,768]{1,0:T(8,128)(2,1)}, bf16[256,768]{1,0:T(8,128)(2,1)S(1)}, u32[]{:S(2)}, u32[]{:S(2)}) collective-permute-start(bf16[256,768]{1,0:T(8,128)(2,1)} %shard_map.96), channel_id=1, source_target_pairs={{0,6},{1,7},{2,4},{3,5},{4,10},{5,11},{6,8},{7,9},{8,14},{9,15},{1... | collective-permute-start | bytes 1179656 | tf_op jit(solution)/shard_map/ppermute | solution.py:47
  159.5 4.5 %collective-permute-done.22 = bf16[256,768]{1,0:T(8,128)(2,1)S(1)} collective-permute-done((bf16[256,768]{1,0:T(8,128)(2,1)}, bf16[256,768]{1,0:T(8,128)(2,1)S(1)}, u32[]{:S(2)}, u32[]{:S(2)}) %collective-permute-start.22) | collective-permute-done | bytes 393248 | tf_op jit(solution)/shard_map/ppermute | solution.py:47
  164.3 3.4 %collective-permute-start.23 = (bf16[256,768]{1,0:T(8,128)(2,1)S(1)}, bf16[256,768]{1,0:T(8,128)(2,1)S(1)}, u32[]{:S(2)}, u32[]{:S(2)}) collective-permute-start(bf16[256,768]{1,0:T(8,128)(2,1)S(1)} %get-tuple-element.34), channel_id=1, source_target_pairs={{0,2},{1,3},{2,0},{3,1},{16,18},{17,19},{18,16},{19,17}} | collective-permute-start | bytes 1179656 | tf_op jit(solution)/shard_map/ppermute | solution.py:30
  167.8 4.2 %collective-permute-done.24 = bf16[256,768]{1,0:T(8,128)(2,1)S(1)} collective-permute-done((bf16[256,768]{1,0:T(8,128)(2,1)}, bf16[256,768]{1,0:T(8,128)(2,1)S(1)}, u32[]{:S(2)}, u32[]{:S(2)}) %collective-permute-start.24) | collective-permute-done | bytes 393248 | tf_op jit(solution)/shard_map/ppermute | solution.py:47
  172.0 4.4 %collective-permute-done.23 = bf16[256,768]{1,0:T(8,128)(2,1)S(1)} collective-permute-done((bf16[256,768]{1,0:T(8,128)(2,1)S(1)}, bf16[256,768]{1,0:T(8,128)(2,1)S(1)}, u32[]{:S(2)}, u32[]{:S(2)}) %collective-permute-start.23) | collective-permute-done | bytes 393248 | tf_op jit(solution)/shard_map/ppermute | solution.py:30
  176.6 1.7 collective-permute-done.26.refs_4_
  179.0 11.8 %shard_map.97 = (bf16[256,512]{1,0:T(8,128)(2,1)}, bf16[4,768,128]{2,1,0:T(8,128)(2,1)}, bf16[4,768,128]{2,1,0:T(8,128)(2,1)}) custom-call(s32[6]{0:T(128)} %get-tuple-element.40.refs_0_, bf16[256,768]{1,0:T(8,128)(2,1)} %copy-done.1, bf16[256,768]{1,0:T(8,128)(2,1)} %copy-done.5, ...), custom_call_target="tpu_custom_call", output_to_operand_aliasing={{1}: (7, {}), {2}: (8, {})} | custom-call | tf_op jit(solution)/shard_map/pallas_call | solution.py:171
  190.8 1.6 collective-permute-start.27
  192.4 7.0 %collective-permute-done.27.refs_2_ = bf16[256,512]{1,0:T(8,128)(2,1)S(1)} collective-permute-done((bf16[256,512]{1,0:T(8,128)(2,1)}, bf16[256,512]{1,0:T(8,128)(2,1)S(1)}, u32[]{:S(2)}, u32[]{:S(2)}) %collective-permute-start.27) | collective-permute-done | bytes 262176 | tf_op jit(solution)/shard_map/ppermute | solution.py:22
  199.4 1.5 collective-permute-done.29.refs_4_
  201.7 4.1 %shard_map.98 = bf16[256,768]{1,0:T(8,128)(2,1)} custom-call(s32[6]{0:T(128)} %get-tuple-element.40.refs_0_, bf16[256,512]{1,0:T(8,128)(2,1)} %get-tuple-element.30.refs_1_, bf16[256,512]{1,0:T(8,128)(2,1)} %copy-done.23, bf16[256,512]{1,0:T(8,128)(2,1)} %copy-done.27, bf16[256,512]{1,0:T(8,128)(2,1)} %copy-done.31, bf16[4,512,768]{2,1,0:T(8,128)(2,1)} %bitcast.43, ...), custom_call_target="tpu_custom_call" | custom-call | tf_op jit(solution)/shard_map/pallas_call | solution.py:209
  205.8 2.3 %maximum_bitcast_fusion = bf16[4,1,256,768]{3,2,1,0:T(8,128)(2,1)} fusion(bf16[1,256,768]{2,1,0:T(8,128)(2,1)} %bitcast.47, bf16[1,256,768]{2,1,0:T(8,128)(2,1)S(1)} %bitcast.46, bf16[1,256,768]{2,1,0:T(8,128)(2,1)S(1)} %bitcast.45, bf16[1,256,768]{2,1,0:T(8,128)(2,1)S(1)} %bitcast.44), kind=kLoop, calls=%fused_computation.3 | loop fusion | flops 2359296 | bytes 3145728 | tf_op jit(solution)/shard_map/broadcast_in_dim | solution.py:293
  (112 shorter events, 13.5 us)
Async XLA Ops:
  4.0 14.4 %copy-start.4 = (bf16[256,768]{1,0:T(8,128)(2,1)}, bf16[256,768]{1,0:T(8,128)(2,1)S(1)}, u32[]{:S(2)}) copy-start(bf16[256,768]{1,0:T(8,128)(2,1)S(1)} %fusion.3.refs_1_.refs_6_) | copy-start | bytes 1179652
  4.0 12.1 %collective-permute-start = (bf16[256,768]{1,0:T(8,128)(2,1)S(1)}, bf16[256,768]{1,0:T(8,128)(2,1)S(1)}, u32[]{:S(2)}, u32[]{:S(2)}) collective-permute-start(bf16[256,768]{1,0:T(8,128)(2,1)S(1)} %fusion.3.refs_1_.refs_6_), channel_id=1, source_target_pairs={{0,2},{1,3},{2,0},{3,1},{4,6},{5,7},{6,4},{7,5},{8,10},{9,11},{10,... | collective-permute-start | bytes 1179656 | tf_op jit(solution)/shard_map/ppermute | solution.py:22
  16.1 2.3 %copy-start.11 = (bf16[256,768]{1,0:T(8,128)(2,1)}, bf16[256,768]{1,0:T(8,128)(2,1)S(1)}, u32[]{:S(2)}) copy-start(bf16[256,768]{1,0:T(8,128)(2,1)S(1)} %collective-permute-done.refs_2_) | copy-start | bytes 1179652
  16.1 1.7 collective-permute-start.2
  16.1 2.3 %collective-permute-start.1 = (bf16[256,768]{1,0:T(8,128)(2,1)S(1)}, bf16[256,768]{1,0:T(8,128)(2,1)S(1)}, u32[]{:S(2)}, u32[]{:S(2)}) collective-permute-start(bf16[256,768]{1,0:T(8,128)(2,1)S(1)} %fusion.3.refs_1_.refs_6_), channel_id=1, source_target_pairs={{0,1},{1,0},{2,3},{3,2},{4,5},{5,4},{6,7},{7,6},{8,9},{9,8},{10,11... | collective-permute-start | bytes 1179656 | tf_op jit(solution)/shard_map/ppermute | solution.py:40
  30.9 8.6 %collective-permute-start.3 = (bf16[256,512]{1,0:T(8,128)(2,1)}, bf16[256,512]{1,0:T(8,128)(2,1)S(1)}, u32[]{:S(2)}, u32[]{:S(2)}) collective-permute-start(bf16[256,512]{1,0:T(8,128)(2,1)} %get-tuple-element.21.refs_1_), channel_id=1, source_target_pairs={{0,2},{1,3},{2,0},{3,1},{4,6},{5,7},{6,4},{7,5},{8,10},{9,11},{10,... | collective-permute-start | bytes 786440 | tf_op jit(solution)/shard_map/ppermute | solution.py:22
  32.7 6.8 %collective-permute-start.4 = (bf16[256,512]{1,0:T(8,128)(2,1)}, bf16[256,512]{1,0:T(8,128)(2,1)S(1)}, u32[]{:S(2)}, u32[]{:S(2)}) collective-permute-start(bf16[256,512]{1,0:T(8,128)(2,1)} %get-tuple-element.21.refs_1_), channel_id=1, source_target_pairs={{0,1},{1,0},{2,3},{3,2},{4,5},{5,4},{6,7},{7,6},{8,9},{9,8},{10,11... | collective-permute-start | bytes 786440 | tf_op jit(solution)/shard_map/ppermute | solution.py:40
  39.5 1.5 copy-start.20
  39.5 1.5 collective-permute-start.5
  41.7 10.5 %copy-start.32 = (s32[4]{0:T(128)S(1)}, s32[4]{0:T(128)}, u32[]{:S(2)}) copy-start(s32[4]{0:T(128)} %param.11) | copy-start | bytes 52
  41.7 17.2 %copy-start = (bf16[768,768]{1,0:T(8,128)(2,1)S(1)}, bf16[768,768]{1,0:T(8,128)(2,1)}, u32[]{:S(2)}) copy-start(bf16[768,768]{1,0:T(8,128)(2,1)} %param.9) | copy-start | bytes 3538948
  45.9 13.0 %collective-permute-start.6 = (bf16[256,768]{1,0:T(8,128)(2,1)}, bf16[256,768]{1,0:T(8,128)(2,1)S(1)}, u32[]{:S(2)}, u32[]{:S(2)}) collective-permute-start(bf16[256,768]{1,0:T(8,128)(2,1)} %shard_map.92), channel_id=1, source_target_pairs={{0,4},{1,5},{2,6},{3,7},{4,8},{5,9},{6,10},{7,11},{8,12},{9,13},{1... | collective-permute-start | bytes 1179656 | tf_op jit(solution)/shard_map/ppermute | solution.py:47
  53.6 13.4 %collective-permute-start.8 = (bf16[256,768]{1,0:T(8,128)(2,1)}, bf16[256,768]{1,0:T(8,128)(2,1)S(1)}, u32[]{:S(2)}, u32[]{:S(2)}) collective-permute-start(bf16[256,768]{1,0:T(8,128)(2,1)} %shard_map.92), channel_id=1, source_target_pairs={{0,6},{1,7},{2,4},{3,5},{4,10},{5,11},{6,8},{7,9},{8,14},{9,15},{1... | collective-permute-start | bytes 1179656 | tf_op jit(solution)/shard_map/ppermute | solution.py:47
  59.2 13.8 %copy-start.2 = (bf16[256,768]{1,0:T(8,128)(2,1)}, bf16[256,768]{1,0:T(8,128)(2,1)S(1)}, u32[]{:S(2)}) copy-start(bf16[256,768]{1,0:T(8,128)(2,1)S(1)} %get-tuple-element.37.refs_1_.refs_6_) | copy-start | bytes 1179652
  59.2 11.9 %collective-permute-start.7 = (bf16[256,768]{1,0:T(8,128)(2,1)S(1)}, bf16[256,768]{1,0:T(8,128)(2,1)S(1)}, u32[]{:S(2)}, u32[]{:S(2)}) collective-permute-start(bf16[256,768]{1,0:T(8,128)(2,1)S(1)} %get-tuple-element.38), channel_id=1, source_target_pairs={{0,2},{1,3},{2,0},{3,1},{16,18},{17,19},{18,16},{19,17}} | collective-permute-start | bytes 1179656 | tf_op jit(solution)/shard_map/ppermute | solution.py:30
  63.1 8.1 %collective-permute-start.9 = (bf16[256,768]{1,0:T(8,128)(2,1)S(1)}, bf16[256,768]{1,0:T(8,128)(2,1)S(1)}, u32[]{:S(2)}, u32[]{:S(2)}) collective-permute-start(bf16[256,768]{1,0:T(8,128)(2,1)S(1)} %get-tuple-element.37.refs_1_.refs_6_), channel_id=1, source_target_pairs={{0,1},{1,0},{2,3},{3,2},{4,5},{5,4},{6,7},{7,6},{8,9},{9,8},{10,11... | collective-permute-start | bytes 1179656 | tf_op jit(solution)/shard_map/ppermute | solution.py:40
  71.2 1.8 copy-start.6
  71.2 1.8 collective-permute-start.10
  71.3 1.7 copy-start.13
  85.5 8.6 %collective-permute-start.11 = (bf16[256,512]{1,0:T(8,128)(2,1)}, bf16[256,512]{1,0:T(8,128)(2,1)S(1)}, u32[]{:S(2)}, u32[]{:S(2)}) collective-permute-start(bf16[256,512]{1,0:T(8,128)(2,1)} %get-tuple-element.24.refs_1_), channel_id=1, source_target_pairs={{0,2},{1,3},{2,0},{3,1},{4,6},{5,7},{6,4},{7,5},{8,10},{9,11},{10,... | collective-permute-start | bytes 786440 | tf_op jit(solution)/shard_map/ppermute | solution.py:22
  87.0 7.1 %collective-permute-start.12 = (bf16[256,512]{1,0:T(8,128)(2,1)}, bf16[256,512]{1,0:T(8,128)(2,1)S(1)}, u32[]{:S(2)}, u32[]{:S(2)}) collective-permute-start(bf16[256,512]{1,0:T(8,128)(2,1)} %get-tuple-element.24.refs_1_), channel_id=1, source_target_pairs={{0,1},{1,0},{2,3},{3,2},{4,5},{5,4},{6,7},{7,6},{8,9},{9,8},{10,11... | collective-permute-start | bytes 786440 | tf_op jit(solution)/shard_map/ppermute | solution.py:40
  94.1 1.5 collective-permute-start.13
  100.4 11.0 %collective-permute-start.14 = (bf16[256,768]{1,0:T(8,128)(2,1)}, bf16[256,768]{1,0:T(8,128)(2,1)S(1)}, u32[]{:S(2)}, u32[]{:S(2)}) collective-permute-start(bf16[256,768]{1,0:T(8,128)(2,1)} %shard_map.94), channel_id=1, source_target_pairs={{0,4},{1,5},{2,6},{3,7},{4,8},{5,9},{6,10},{7,11},{8,12},{9,13},{1... | collective-permute-start | bytes 1179656 | tf_op jit(solution)/shard_map/ppermute | solution.py:47
  104.4 15.0 %collective-permute-start.16 = (bf16[256,768]{1,0:T(8,128)(2,1)}, bf16[256,768]{1,0:T(8,128)(2,1)S(1)}, u32[]{:S(2)}, u32[]{:S(2)}) collective-permute-start(bf16[256,768]{1,0:T(8,128)(2,1)} %shard_map.94), channel_id=1, source_target_pairs={{0,6},{1,7},{2,4},{3,5},{4,10},{5,11},{6,8},{7,9},{8,14},{9,15},{1... | collective-permute-start | bytes 1179656 | tf_op jit(solution)/shard_map/ppermute | solution.py:47
  111.7 13.9 %copy-start.3 = (bf16[256,768]{1,0:T(8,128)(2,1)}, bf16[256,768]{1,0:T(8,128)(2,1)S(1)}, u32[]{:S(2)}) copy-start(bf16[256,768]{1,0:T(8,128)(2,1)S(1)} %get-tuple-element.35.refs_1_.refs_6_) | copy-start | bytes 1179652
  111.7 12.0 %collective-permute-start.15 = (bf16[256,768]{1,0:T(8,128)(2,1)S(1)}, bf16[256,768]{1,0:T(8,128)(2,1)S(1)}, u32[]{:S(2)}, u32[]{:S(2)}) collective-permute-start(bf16[256,768]{1,0:T(8,128)(2,1)S(1)} %get-tuple-element.36), channel_id=1, source_target_pairs={{0,2},{1,3},{2,0},{3,1},{16,18},{17,19},{18,16},{19,17}} | collective-permute-start | bytes 1179656 | tf_op jit(solution)/shard_map/ppermute | solution.py:30
  115.3 8.6 %collective-permute-start.17 = (bf16[256,768]{1,0:T(8,128)(2,1)S(1)}, bf16[256,768]{1,0:T(8,128)(2,1)S(1)}, u32[]{:S(2)}, u32[]{:S(2)}) collective-permute-start(bf16[256,768]{1,0:T(8,128)(2,1)S(1)} %get-tuple-element.35.refs_1_.refs_6_), channel_id=1, source_target_pairs={{0,1},{1,0},{2,3},{3,2},{4,5},{5,4},{6,7},{7,6},{8,9},{9,8},{10,11... | collective-permute-start | bytes 1179656 | tf_op jit(solution)/shard_map/ppermute | solution.py:40
  123.8 1.8 copy-start.7
  123.8 1.8 collective-permute-start.18
  123.9 1.7 copy-start.14
  138.1 8.6 %collective-permute-start.19 = (bf16[256,512]{1,0:T(8,128)(2,1)}, bf16[256,512]{1,0:T(8,128)(2,1)S(1)}, u32[]{:S(2)}, u32[]{:S(2)}) collective-permute-start(bf16[256,512]{1,0:T(8,128)(2,1)} %get-tuple-element.27.refs_1_), channel_id=1, source_target_pairs={{0,2},{1,3},{2,0},{3,1},{4,6},{5,7},{6,4},{7,5},{8,10},{9,11},{10,... | collective-permute-start | bytes 786440 | tf_op jit(solution)/shard_map/ppermute | solution.py:22
  139.6 7.1 %collective-permute-start.20 = (bf16[256,512]{1,0:T(8,128)(2,1)}, bf16[256,512]{1,0:T(8,128)(2,1)S(1)}, u32[]{:S(2)}, u32[]{:S(2)}) collective-permute-start(bf16[256,512]{1,0:T(8,128)(2,1)} %get-tuple-element.27.refs_1_), channel_id=1, source_target_pairs={{0,1},{1,0},{2,3},{3,2},{4,5},{5,4},{6,7},{7,6},{8,9},{9,8},{10,11... | collective-permute-start | bytes 786440 | tf_op jit(solution)/shard_map/ppermute | solution.py:40
  146.7 1.5 collective-permute-start.21
  153.1 11.0 %collective-permute-start.22 = (bf16[256,768]{1,0:T(8,128)(2,1)}, bf16[256,768]{1,0:T(8,128)(2,1)S(1)}, u32[]{:S(2)}, u32[]{:S(2)}) collective-permute-start(bf16[256,768]{1,0:T(8,128)(2,1)} %shard_map.96), channel_id=1, source_target_pairs={{0,4},{1,5},{2,6},{3,7},{4,8},{5,9},{6,10},{7,11},{8,12},{9,13},{1... | collective-permute-start | bytes 1179656 | tf_op jit(solution)/shard_map/ppermute | solution.py:47
  156.9 15.1 %collective-permute-start.24 = (bf16[256,768]{1,0:T(8,128)(2,1)}, bf16[256,768]{1,0:T(8,128)(2,1)S(1)}, u32[]{:S(2)}, u32[]{:S(2)}) collective-permute-start(bf16[256,768]{1,0:T(8,128)(2,1)} %shard_map.96), channel_id=1, source_target_pairs={{0,6},{1,7},{2,4},{3,5},{4,10},{5,11},{6,8},{7,9},{8,14},{9,15},{1... | collective-permute-start | bytes 1179656 | tf_op jit(solution)/shard_map/ppermute | solution.py:47
  164.3 13.9 %copy-start.1 = (bf16[256,768]{1,0:T(8,128)(2,1)}, bf16[256,768]{1,0:T(8,128)(2,1)S(1)}, u32[]{:S(2)}) copy-start(bf16[256,768]{1,0:T(8,128)(2,1)S(1)} %get-tuple-element.33.refs_1_.refs_6_) | copy-start | bytes 1179652
  164.3 12.1 %collective-permute-start.23 = (bf16[256,768]{1,0:T(8,128)(2,1)S(1)}, bf16[256,768]{1,0:T(8,128)(2,1)S(1)}, u32[]{:S(2)}, u32[]{:S(2)}) collective-permute-start(bf16[256,768]{1,0:T(8,128)(2,1)S(1)} %get-tuple-element.34), channel_id=1, source_target_pairs={{0,2},{1,3},{2,0},{3,1},{16,18},{17,19},{18,16},{19,17}} | collective-permute-start | bytes 1179656 | tf_op jit(solution)/shard_map/ppermute | solution.py:30
  167.8 8.8 %collective-permute-start.25 = (bf16[256,768]{1,0:T(8,128)(2,1)S(1)}, bf16[256,768]{1,0:T(8,128)(2,1)S(1)}, u32[]{:S(2)}, u32[]{:S(2)}) collective-permute-start(bf16[256,768]{1,0:T(8,128)(2,1)S(1)} %get-tuple-element.33.refs_1_.refs_6_), channel_id=1, source_target_pairs={{0,1},{1,0},{2,3},{3,2},{4,5},{5,4},{6,7},{7,6},{8,9},{9,8},{10,11... | collective-permute-start | bytes 1179656 | tf_op jit(solution)/shard_map/ppermute | solution.py:40
  176.4 1.8 copy-start.5
  176.5 1.8 collective-permute-start.26
  176.5 1.7 copy-start.12
  190.8 15.0 %copy-start.8 = (bf16[256,768]{1,0:T(8,128)(2,1)S(1)}, bf16[256,768]{1,0:T(8,128)(2,1)}, u32[]{:S(2)}) copy-start(bf16[256,768]{1,0:T(8,128)(2,1)} %shard_map.92) | copy-start | bytes 1179652
  190.8 15.0 %copy-start.9 = (bf16[256,768]{1,0:T(8,128)(2,1)S(1)}, bf16[256,768]{1,0:T(8,128)(2,1)}, u32[]{:S(2)}) copy-start(bf16[256,768]{1,0:T(8,128)(2,1)} %shard_map.94) | copy-start | bytes 1179652
  190.8 15.0 %copy-start.10 = (bf16[256,768]{1,0:T(8,128)(2,1)S(1)}, bf16[256,768]{1,0:T(8,128)(2,1)}, u32[]{:S(2)}) copy-start(bf16[256,768]{1,0:T(8,128)(2,1)} %shard_map.96) | copy-start | bytes 1179652
  190.8 8.6 %collective-permute-start.27 = (bf16[256,512]{1,0:T(8,128)(2,1)}, bf16[256,512]{1,0:T(8,128)(2,1)S(1)}, u32[]{:S(2)}, u32[]{:S(2)}) collective-permute-start(bf16[256,512]{1,0:T(8,128)(2,1)} %get-tuple-element.30.refs_1_), channel_id=1, source_target_pairs={{0,2},{1,3},{2,0},{3,1},{4,6},{5,7},{6,4},{7,5},{8,10},{9,11},{10,... | collective-permute-start | bytes 786440 | tf_op jit(solution)/shard_map/ppermute | solution.py:22
  192.4 7.1 %collective-permute-start.28 = (bf16[256,512]{1,0:T(8,128)(2,1)}, bf16[256,512]{1,0:T(8,128)(2,1)S(1)}, u32[]{:S(2)}, u32[]{:S(2)}) collective-permute-start(bf16[256,512]{1,0:T(8,128)(2,1)} %get-tuple-element.30.refs_1_), channel_id=1, source_target_pairs={{0,1},{1,0},{2,3},{3,2},{4,5},{5,4},{6,7},{7,6},{8,9},{9,8},{10,11... | collective-permute-start | bytes 786440 | tf_op jit(solution)/shard_map/ppermute | solution.py:40
  199.4 1.5 copy-start.23
  199.4 1.5 collective-permute-start.29
  (15 other events, 15.8 us)

commit v20 on v18

--- a/solution.py
+++ b/solution.py
@@ -201,17 +201,29 @@
 def leave_block(parts, out_weights, own_rows, gating_here, where):
     count = len(parts)
     span, head_width = parts[0].shape
-    vmem = pl.BlockSpec(memory_space=pltpu.VMEM)
-    smem = pl.BlockSpec(memory_space=pltpu.SMEM)
+    width = out_weights.shape[1]
+    half = width // 2 if width % 256 == 0 else width
+    whole = lambda shape: pl.BlockSpec(shape, lambda j, where: (0,) * len(shape))
+    grid_spec = pltpu.PrefetchScalarGridSpec(
+        num_scalar_prefetch=1,
+        grid=(width // half,),
+        in_specs=[whole((span, head_width)) for _ in parts]
+        + [
+            pl.BlockSpec((count, head_width, half), lambda j, where: (0, 0, j)),
+            pl.BlockSpec((span, half), lambda j, where: (0, j)),
+            pl.BlockSpec((1, half), lambda j, where: (0, j)),
+        ],
+        out_specs=pl.BlockSpec((span, half), lambda j, where: (0, j)),
+    )
     return pl.pallas_call(
         exit_kernel,
-        in_specs=[smem] + [vmem] * (count + 3),
-        out_specs=vmem,
+        grid_spec=grid_spec,
         out_shape=jax.ShapeDtypeStruct(own_rows.shape, own_rows.dtype),
+        compiler_params=pltpu.CompilerParams(dimension_semantics=("arbitrary",)),
     )(
         where,
         *parts,
-        out_weights.reshape(count, head_width, out_weights.shape[1]),
+        out_weights.reshape(count, head_width, width),
         own_rows,
         gating_here.reshape(1, -1),
     )

time: 209 us -> 212 us (1.014)
  Pallas kernels: 63.8 us -> 66.3 us
    pallas_call x4, Pallas kernels: 16.5 us -> 19 us  [leave_block(): pl.pallas_call(exit_kernel, grid_spec=grid_spec, out_shape=jax.ShapeDtype...]
where the time goes in v20:
time: 212 us; the launch traced here: 211 us
  waiting for transfers between devices  82.6 us (39%)
  Pallas kernels  66.3 us (31%)
  starting transfers between devices  37.8 us (18%)
  other arithmetic  9.93 us (5%)
  local copies, waits for them, and re-layouts  7.81 us (4%)
  between operations  6.34 us (3%)
    pallas_call x4, Pallas kernels, attend_block(): pl.pallas_call(block_kernel, grid_spec=grid_spec, out_shape=[jax.ShapeDty...  47.3 us
    ppermute x5, waiting for transfers between devices, across_chips(): lax.ppermute(block, 'seq', [(source, (source + step) % count) for source...  36.2 us
    ppermute x6, waiting for transfers between devices, to_next_section(): lax.ppermute(block, ('section', 'seq'), [(section * count + source, (sect...  21.3 us
    pallas_call x4, Pallas kernels, leave_block(): pl.pallas_call(exit_kernel, grid_spec=grid_spec, out_shape=jax.ShapeDtype...  19 us
    ppermute x6, starting transfers between devices, to_next_section(): lax.ppermute(block, ('section', 'seq'), [(section * count + source, (sect...  16.7 us
    ppermute x3, waiting for transfers between devices, across_chips_first_section(): lax.ppermute(block, ('section', 'seq'), [(source, (source + step) % count...  12.8 us
    ppermute x16, waiting for transfers between devices, with_partner(): return parts + [lax.ppermute(part, 'seq', to_partner) for part in parts]  12.3 us
    ppermute x3, starting transfers between devices, across_chips_first_section(): lax.ppermute(block, ('section', 'seq'), [(source, (source + step) % count...  10.9 us
  transfers between devices with their start and end apart: 30, of which 23 were waited for; matrix products, arithmetic and copies ran while one was open for 3% of the time, Pallas kernels for 0%

profile of v20, /device:TPU:0, one launch (start us, length us, event | category | flops | bytes accessed | tf_op | source)
XLA Modules:
  0.0 210.8 jit_solution(4680847528080945427)
XLA Ops:
  0.0 0.8 reduce-window.9
  0.8 1.3 bitcast_subtract_fusion
  2.8 1.2 fusion.3.refs_1_.refs_6_
  4.0 3.0 %collective-permute-start = (bf16[256,768]{1,0:T(8,128)(2,1)S(1)}, bf16[256,768]{1,0:T(8,128)(2,1)S(1)}, u32[]{:S(2)}, u32[]{:S(2)}) collective-permute-start(bf16[256,768]{1,0:T(8,128)(2,1)S(1)} %fusion.3.refs_1_.refs_6_), channel_id=1, source_target_pairs={{0,2},{1,3},{2,0},{3,1},{4,6},{5,7},{6,4},{7,5},{8,10},{9,11},{10,... | collective-permute-start | bytes 1179656 | tf_op jit(solution)/shard_map/ppermute | solution.py:22
  7.9 8.2 %collective-permute-done.refs_2_ = bf16[256,768]{1,0:T(8,128)(2,1)S(1)} collective-permute-done((bf16[256,768]{1,0:T(8,128)(2,1)S(1)}, bf16[256,768]{1,0:T(8,128)(2,1)S(1)}, u32[]{:S(2)}, u32[]{:S(2)}) %collective-permute-start) | collective-permute-done | bytes 393248 | tf_op jit(solution)/shard_map/ppermute | solution.py:22
  19.2 11.8 %shard_map.91 = (bf16[256,512]{1,0:T(8,128)(2,1)}, bf16[4,768,128]{2,1,0:T(8,128)(2,1)}, bf16[4,768,128]{2,1,0:T(8,128)(2,1)}) custom-call(s32[6]{0:T(128)} %get-tuple-element.39.refs_0_, bf16[256,768]{1,0:T(8,128)(2,1)} %copy-done.4, bf16[256,768]{1,0:T(8,128)(2,1)} %copy-done.11, bf16[256,768]{1,0:T(8,128)(2,1)} %copy-done.16, ...), custom_call_target="tpu_custom_call" | custom-call | tf_op jit(solution)/shard_map/pallas_call | solution.py:168
  31.0 1.7 collective-permute-start.3
  32.7 6.8 %collective-permute-done.3.refs_2_ = bf16[256,512]{1,0:T(8,128)(2,1)S(1)} collective-permute-done((bf16[256,512]{1,0:T(8,128)(2,1)}, bf16[256,512]{1,0:T(8,128)(2,1)S(1)}, u32[]{:S(2)}, u32[]{:S(2)}) %collective-permute-start.3) | collective-permute-done | bytes 262176 | tf_op jit(solution)/shard_map/ppermute | solution.py:22
  39.6 1.5 collective-permute-done.5.refs_4_
  41.8 4.8 %shard_map.92 = bf16[256,768]{1,0:T(8,128)(2,1)} custom-call(s32[6]{0:T(128)} %get-tuple-element.39.refs_0_, bf16[256,512]{1,0:T(8,128)(2,1)} %get-tuple-element.21.refs_1_, bf16[256,512]{1,0:T(8,128)(2,1)} %copy-done.20, bf16[256,512]{1,0:T(8,128)(2,1)} %copy-done.24, bf16[256,512]{1,0:T(8,128)(2,1)} %copy-done.28, bf16[4,512,768]{2,1,0:T(8,128)(2,1)} %bitcast.40, ...), custom_call_target="tpu_custom_call" | custom-call | tf_op jit(solution)/shard_map/pallas_call | solution.py:218
  46.6 3.8 %collective-permute-start.6 = (bf16[256,768]{1,0:T(8,128)(2,1)}, bf16[256,768]{1,0:T(8,128)(2,1)S(1)}, u32[]{:S(2)}, u32[]{:S(2)}) collective-permute-start(bf16[256,768]{1,0:T(8,128)(2,1)} %shard_map.92), channel_id=1, source_target_pairs={{0,4},{1,5},{2,6},{3,7},{4,8},{5,9},{6,10},{7,11},{8,12},{9,13},{1... | collective-permute-start | bytes 1179656 | tf_op jit(solution)/shard_map/ppermute | solution.py:47
  54.3 4.4 %collective-permute-start.8 = (bf16[256,768]{1,0:T(8,128)(2,1)}, bf16[256,768]{1,0:T(8,128)(2,1)S(1)}, u32[]{:S(2)}, u32[]{:S(2)}) collective-permute-start(bf16[256,768]{1,0:T(8,128)(2,1)} %shard_map.92), channel_id=1, source_target_pairs={{0,6},{1,7},{2,4},{3,5},{4,10},{5,11},{6,8},{7,9},{8,14},{9,15},{1... | collective-permute-start | bytes 1179656 | tf_op jit(solution)/shard_map/ppermute | solution.py:47
  58.7 0.9 collective-permute-done.6
  59.9 3.9 %collective-permute-start.7 = (bf16[256,768]{1,0:T(8,128)(2,1)S(1)}, bf16[256,768]{1,0:T(8,128)(2,1)S(1)}, u32[]{:S(2)}, u32[]{:S(2)}) collective-permute-start(bf16[256,768]{1,0:T(8,128)(2,1)S(1)} %get-tuple-element.38), channel_id=1, source_target_pairs={{0,2},{1,3},{2,0},{3,1},{16,18},{17,19},{18,16},{19,17}} | collective-permute-start | bytes 1179656 | tf_op jit(solution)/shard_map/ppermute | solution.py:30
  63.9 3.9 %collective-permute-done.8 = bf16[256,768]{1,0:T(8,128)(2,1)S(1)} collective-permute-done((bf16[256,768]{1,0:T(8,128)(2,1)}, bf16[256,768]{1,0:T(8,128)(2,1)S(1)}, u32[]{:S(2)}, u32[]{:S(2)}) %collective-permute-start.8) | collective-permute-done | bytes 393248 | tf_op jit(solution)/shard_map/ppermute | solution.py:47
  67.8 4.1 %collective-permute-done.7 = bf16[256,768]{1,0:T(8,128)(2,1)S(1)} collective-permute-done((bf16[256,768]{1,0:T(8,128)(2,1)S(1)}, bf16[256,768]{1,0:T(8,128)(2,1)S(1)}, u32[]{:S(2)}, u32[]{:S(2)}) %collective-permute-start.7) | collective-permute-done | bytes 393248 | tf_op jit(solution)/shard_map/ppermute | solution.py:30
  72.0 1.7 collective-permute-done.10.refs_4_
  73.7 0.8 copy-done.18
  74.4 11.8 %shard_map.93 = (bf16[256,512]{1,0:T(8,128)(2,1)}, bf16[4,768,128]{2,1,0:T(8,128)(2,1)}, bf16[4,768,128]{2,1,0:T(8,128)(2,1)}) custom-call(s32[6]{0:T(128)} %get-tuple-element.42.refs_0_, bf16[256,768]{1,0:T(8,128)(2,1)} %copy-done.2, bf16[256,768]{1,0:T(8,128)(2,1)} %copy-done.6, ...), custom_call_target="tpu_custom_call", output_to_operand_aliasing={{1}: (7, {}), {2}: (8, {})} | custom-call | tf_op jit(solution)/shard_map/pallas_call | solution.py:168
  86.3 1.5 collective-permute-start.11
  87.7 7.1 %collective-permute-done.11.refs_2_ = bf16[256,512]{1,0:T(8,128)(2,1)S(1)} collective-permute-done((bf16[256,512]{1,0:T(8,128)(2,1)}, bf16[256,512]{1,0:T(8,128)(2,1)S(1)}, u32[]{:S(2)}, u32[]{:S(2)}) %collective-permute-start.11) | collective-permute-done | bytes 262176 | tf_op jit(solution)/shard_map/ppermute | solution.py:22
  94.8 1.5 collective-permute-done.13.refs_4_
  97.1 4.7 %shard_map.94 = bf16[256,768]{1,0:T(8,128)(2,1)} custom-call(s32[6]{0:T(128)} %get-tuple-element.42.refs_0_, bf16[256,512]{1,0:T(8,128)(2,1)} %get-tuple-element.24.refs_1_, bf16[256,512]{1,0:T(8,128)(2,1)} %copy-done.21, bf16[256,512]{1,0:T(8,128)(2,1)} %copy-done.25, bf16[256,512]{1,0:T(8,128)(2,1)} %copy-done.29, bf16[4,512,768]{2,1,0:T(8,128)(2,1)} %bitcast.41, ...), custom_call_target="tpu_custom_call" | custom-call | tf_op jit(solution)/shard_map/pallas_call | solution.py:218
  101.8 1.3 collective-permute-start.14
  105.7 3.3 %collective-permute-start.16 = (bf16[256,768]{1,0:T(8,128)(2,1)}, bf16[256,768]{1,0:T(8,128)(2,1)S(1)}, u32[]{:S(2)}, u32[]{:S(2)}) collective-permute-start(bf16[256,768]{1,0:T(8,128)(2,1)} %shard_map.94), channel_id=1, source_target_pairs={{0,6},{1,7},{2,4},{3,5},{4,10},{5,11},{6,8},{7,9},{8,14},{9,15},{1... | collective-permute-start | bytes 1179656 | tf_op jit(solution)/shard_map/ppermute | solution.py:47
  109.1 3.7 %collective-permute-done.14 = bf16[256,768]{1,0:T(8,128)(2,1)S(1)} collective-permute-done((bf16[256,768]{1,0:T(8,128)(2,1)}, bf16[256,768]{1,0:T(8,128)(2,1)S(1)}, u32[]{:S(2)}, u32[]{:S(2)}) %collective-permute-start.14) | collective-permute-done | bytes 393248 | tf_op jit(solution)/shard_map/ppermute | solution.py:47
  113.1 3.6 %collective-permute-start.15 = (bf16[256,768]{1,0:T(8,128)(2,1)S(1)}, bf16[256,768]{1,0:T(8,128)(2,1)S(1)}, u32[]{:S(2)}, u32[]{:S(2)}) collective-permute-start(bf16[256,768]{1,0:T(8,128)(2,1)S(1)} %get-tuple-element.36), channel_id=1, source_target_pairs={{0,2},{1,3},{2,0},{3,1},{16,18},{17,19},{18,16},{19,17}} | collective-permute-start | bytes 1179656 | tf_op jit(solution)/shard_map/ppermute | solution.py:30
  116.7 4.0 %collective-permute-done.16 = bf16[256,768]{1,0:T(8,128)(2,1)S(1)} collective-permute-done((bf16[256,768]{1,0:T(8,128)(2,1)}, bf16[256,768]{1,0:T(8,128)(2,1)S(1)}, u32[]{:S(2)}, u32[]{:S(2)}) %collective-permute-start.16) | collective-permute-done | bytes 393248 | tf_op jit(solution)/shard_map/ppermute | solution.py:47
  120.7 4.4 %collective-permute-done.15 = bf16[256,768]{1,0:T(8,128)(2,1)S(1)} collective-permute-done((bf16[256,768]{1,0:T(8,128)(2,1)S(1)}, bf16[256,768]{1,0:T(8,128)(2,1)S(1)}, u32[]{:S(2)}, u32[]{:S(2)}) %collective-permute-start.15) | collective-permute-done | bytes 393248 | tf_op jit(solution)/shard_map/ppermute | solution.py:30
  125.3 1.7 collective-permute-done.18.refs_4_
  127.7 11.8 %shard_map.95 = (bf16[256,512]{1,0:T(8,128)(2,1)}, bf16[4,768,128]{2,1,0:T(8,128)(2,1)}, bf16[4,768,128]{2,1,0:T(8,128)(2,1)}) custom-call(s32[6]{0:T(128)} %get-tuple-element.41.refs_0_, bf16[256,768]{1,0:T(8,128)(2,1)} %copy-done.3, bf16[256,768]{1,0:T(8,128)(2,1)} %copy-done.7, ...), custom_call_target="tpu_custom_call", output_to_operand_aliasing={{1}: (7, {}), {2}: (8, {})} | custom-call | tf_op jit(solution)/shard_map/pallas_call | solution.py:168
  139.5 1.5 collective-permute-start.19
  141.0 7.1 %collective-permute-done.19.refs_2_ = bf16[256,512]{1,0:T(8,128)(2,1)S(1)} collective-permute-done((bf16[256,512]{1,0:T(8,128)(2,1)}, bf16[256,512]{1,0:T(8,128)(2,1)S(1)}, u32[]{:S(2)}, u32[]{:S(2)}) %collective-permute-start.19) | collective-permute-done | bytes 262176 | tf_op jit(solution)/shard_map/ppermute | solution.py:22
  148.1 1.5 collective-permute-done.21.refs_4_
  150.3 4.7 %shard_map.96 = bf16[256,768]{1,0:T(8,128)(2,1)} custom-call(s32[6]{0:T(128)} %get-tuple-element.41.refs_0_, bf16[256,512]{1,0:T(8,128)(2,1)} %get-tuple-element.27.refs_1_, bf16[256,512]{1,0:T(8,128)(2,1)} %copy-done.22, bf16[256,512]{1,0:T(8,128)(2,1)} %copy-done.26, bf16[256,512]{1,0:T(8,128)(2,1)} %copy-done.30, bf16[4,512,768]{2,1,0:T(8,128)(2,1)} %bitcast.42, ...), custom_call_target="tpu_custom_call" | custom-call | tf_op jit(solution)/shard_map/pallas_call | solution.py:218
  155.1 1.3 collective-permute-start.22
  158.9 2.6 %collective-permute-start.24 = (bf16[256,768]{1,0:T(8,128)(2,1)}, bf16[256,768]{1,0:T(8,128)(2,1)S(1)}, u32[]{:S(2)}, u32[]{:S(2)}) collective-permute-start(bf16[256,768]{1,0:T(8,128)(2,1)} %shard_map.96), channel_id=1, source_target_pairs={{0,6},{1,7},{2,4},{3,5},{4,10},{5,11},{6,8},{7,9},{8,14},{9,15},{1... | collective-permute-start | bytes 1179656 | tf_op jit(solution)/shard_map/ppermute | solution.py:47
  161.5 4.6 %collective-permute-done.22 = bf16[256,768]{1,0:T(8,128)(2,1)S(1)} collective-permute-done((bf16[256,768]{1,0:T(8,128)(2,1)}, bf16[256,768]{1,0:T(8,128)(2,1)S(1)}, u32[]{:S(2)}, u32[]{:S(2)}) %collective-permute-start.22) | collective-permute-done | bytes 393248 | tf_op jit(solution)/shard_map/ppermute | solution.py:47
  166.4 3.4 %collective-permute-start.23 = (bf16[256,768]{1,0:T(8,128)(2,1)S(1)}, bf16[256,768]{1,0:T(8,128)(2,1)S(1)}, u32[]{:S(2)}, u32[]{:S(2)}) collective-permute-start(bf16[256,768]{1,0:T(8,128)(2,1)S(1)} %get-tuple-element.34), channel_id=1, source_target_pairs={{0,2},{1,3},{2,0},{3,1},{16,18},{17,19},{18,16},{19,17}} | collective-permute-start | bytes 1179656 | tf_op jit(solution)/shard_map/ppermute | solution.py:30
  169.8 4.2 %collective-permute-done.24 = bf16[256,768]{1,0:T(8,128)(2,1)S(1)} collective-permute-done((bf16[256,768]{1,0:T(8,128)(2,1)}, bf16[256,768]{1,0:T(8,128)(2,1)S(1)}, u32[]{:S(2)}, u32[]{:S(2)}) %collective-permute-start.24) | collective-permute-done | bytes 393248 | tf_op jit(solution)/shard_map/ppermute | solution.py:47
  174.0 4.4 %collective-permute-done.23 = bf16[256,768]{1,0:T(8,128)(2,1)S(1)} collective-permute-done((bf16[256,768]{1,0:T(8,128)(2,1)S(1)}, bf16[256,768]{1,0:T(8,128)(2,1)S(1)}, u32[]{:S(2)}, u32[]{:S(2)}) %collective-permute-start.23) | collective-permute-done | bytes 393248 | tf_op jit(solution)/shard_map/ppermute | solution.py:30
  178.6 1.7 collective-permute-done.26.refs_4_
  181.0 11.8 %shard_map.97 = (bf16[256,512]{1,0:T(8,128)(2,1)}, bf16[4,768,128]{2,1,0:T(8,128)(2,1)}, bf16[4,768,128]{2,1,0:T(8,128)(2,1)}) custom-call(s32[6]{0:T(128)} %get-tuple-element.40.refs_0_, bf16[256,768]{1,0:T(8,128)(2,1)} %copy-done.1, bf16[256,768]{1,0:T(8,128)(2,1)} %copy-done.5, ...), custom_call_target="tpu_custom_call", output_to_operand_aliasing={{1}: (7, {}), {2}: (8, {})} | custom-call | tf_op jit(solution)/shard_map/pallas_call | solution.py:168
  192.8 1.6 collective-permute-start.27
  194.4 7.1 %collective-permute-done.27.refs_2_ = bf16[256,512]{1,0:T(8,128)(2,1)S(1)} collective-permute-done((bf16[256,512]{1,0:T(8,128)(2,1)}, bf16[256,512]{1,0:T(8,128)(2,1)S(1)}, u32[]{:S(2)}, u32[]{:S(2)}) %collective-permute-start.27) | collective-permute-done | bytes 262176 | tf_op jit(solution)/shard_map/ppermute | solution.py:22
  201.5 1.5 collective-permute-done.29.refs_4_
  203.7 4.7 %shard_map.98 = bf16[256,768]{1,0:T(8,128)(2,1)} custom-call(s32[6]{0:T(128)} %get-tuple-element.40.refs_0_, bf16[256,512]{1,0:T(8,128)(2,1)} %get-tuple-element.30.refs_1_, bf16[256,512]{1,0:T(8,128)(2,1)} %copy-done.23, bf16[256,512]{1,0:T(8,128)(2,1)} %copy-done.27, bf16[256,512]{1,0:T(8,128)(2,1)} %copy-done.31, bf16[4,512,768]{2,1,0:T(8,128)(2,1)} %bitcast.43, ...), custom_call_target="tpu_custom_call" | custom-call | tf_op jit(solution)/shard_map/pallas_call | solution.py:218
  208.5 2.3 %maximum_bitcast_fusion = bf16[4,1,256,768]{3,2,1,0:T(8,128)(2,1)} fusion(bf16[1,256,768]{2,1,0:T(8,128)(2,1)} %bitcast.47, bf16[1,256,768]{2,1,0:T(8,128)(2,1)S(1)} %bitcast.46, bf16[1,256,768]{2,1,0:T(8,128)(2,1)S(1)} %bitcast.45, bf16[1,256,768]{2,1,0:T(8,128)(2,1)S(1)} %bitcast.44), kind=kLoop, calls=%fused_computation.3 | loop fusion | flops 2359296 | bytes 3145728 | tf_op jit(solution)/shard_map/broadcast_in_dim | solution.py:302
  (112 shorter events, 13.5 us)
Async XLA Ops:
  4.0 14.4 %copy-start.4 = (bf16[256,768]{1,0:T(8,128)(2,1)}, bf16[256,768]{1,0:T(8,128)(2,1)S(1)}, u32[]{:S(2)}) copy-start(bf16[256,768]{1,0:T(8,128)(2,1)S(1)} %fusion.3.refs_1_.refs_6_) | copy-start | bytes 1179652
  4.0 12.1 %collective-permute-start = (bf16[256,768]{1,0:T(8,128)(2,1)S(1)}, bf16[256,768]{1,0:T(8,128)(2,1)S(1)}, u32[]{:S(2)}, u32[]{:S(2)}) collective-permute-start(bf16[256,768]{1,0:T(8,128)(2,1)S(1)} %fusion.3.refs_1_.refs_6_), channel_id=1, source_target_pairs={{0,2},{1,3},{2,0},{3,1},{4,6},{5,7},{6,4},{7,5},{8,10},{9,11},{10,... | collective-permute-start | bytes 1179656 | tf_op jit(solution)/shard_map/ppermute | solution.py:22
  16.1 2.3 %copy-start.11 = (bf16[256,768]{1,0:T(8,128)(2,1)}, bf16[256,768]{1,0:T(8,128)(2,1)S(1)}, u32[]{:S(2)}) copy-start(bf16[256,768]{1,0:T(8,128)(2,1)S(1)} %collective-permute-done.refs_2_) | copy-start | bytes 1179652
  16.1 1.7 collective-permute-start.2
  16.1 2.3 %collective-permute-start.1 = (bf16[256,768]{1,0:T(8,128)(2,1)S(1)}, bf16[256,768]{1,0:T(8,128)(2,1)S(1)}, u32[]{:S(2)}, u32[]{:S(2)}) collective-permute-start(bf16[256,768]{1,0:T(8,128)(2,1)S(1)} %fusion.3.refs_1_.refs_6_), channel_id=1, source_target_pairs={{0,1},{1,0},{2,3},{3,2},{4,5},{5,4},{6,7},{7,6},{8,9},{9,8},{10,11... | collective-permute-start | bytes 1179656 | tf_op jit(solution)/shard_map/ppermute | solution.py:40
  31.0 8.6 %collective-permute-start.3 = (bf16[256,512]{1,0:T(8,128)(2,1)}, bf16[256,512]{1,0:T(8,128)(2,1)S(1)}, u32[]{:S(2)}, u32[]{:S(2)}) collective-permute-start(bf16[256,512]{1,0:T(8,128)(2,1)} %get-tuple-element.21.refs_1_), channel_id=1, source_target_pairs={{0,2},{1,3},{2,0},{3,1},{4,6},{5,7},{6,4},{7,5},{8,10},{9,11},{10,... | collective-permute-start | bytes 786440 | tf_op jit(solution)/shard_map/ppermute | solution.py:22
  32.7 6.8 %collective-permute-start.4 = (bf16[256,512]{1,0:T(8,128)(2,1)}, bf16[256,512]{1,0:T(8,128)(2,1)S(1)}, u32[]{:S(2)}, u32[]{:S(2)}) collective-permute-start(bf16[256,512]{1,0:T(8,128)(2,1)} %get-tuple-element.21.refs_1_), channel_id=1, source_target_pairs={{0,1},{1,0},{2,3},{3,2},{4,5},{5,4},{6,7},{7,6},{8,9},{9,8},{10,11... | collective-permute-start | bytes 786440 | tf_op jit(solution)/shard_map/ppermute | solution.py:40
  39.5 1.5 copy-start.20
  39.5 1.5 collective-permute-start.5
  41.8 11.2 %copy-start.32 = (s32[4]{0:T(128)S(1)}, s32[4]{0:T(128)}, u32[]{:S(2)}) copy-start(s32[4]{0:T(128)} %param.11) | copy-start | bytes 52
  41.8 17.9 %copy-start = (bf16[768,768]{1,0:T(8,128)(2,1)S(1)}, bf16[768,768]{1,0:T(8,128)(2,1)}, u32[]{:S(2)}) copy-start(bf16[768,768]{1,0:T(8,128)(2,1)} %param.9) | copy-start | bytes 3538948
  46.6 13.0 %collective-permute-start.6 = (bf16[256,768]{1,0:T(8,128)(2,1)}, bf16[256,768]{1,0:T(8,128)(2,1)S(1)}, u32[]{:S(2)}, u32[]{:S(2)}) collective-permute-start(bf16[256,768]{1,0:T(8,128)(2,1)} %shard_map.92), channel_id=1, source_target_pairs={{0,4},{1,5},{2,6},{3,7},{4,8},{5,9},{6,10},{7,11},{8,12},{9,13},{1... | collective-permute-start | bytes 1179656 | tf_op jit(solution)/shard_map/ppermute | solution.py:47
  54.3 13.4 %collective-permute-start.8 = (bf16[256,768]{1,0:T(8,128)(2,1)}, bf16[256,768]{1,0:T(8,128)(2,1)S(1)}, u32[]{:S(2)}, u32[]{:S(2)}) collective-permute-start(bf16[256,768]{1,0:T(8,128)(2,1)} %shard_map.92), channel_id=1, source_target_pairs={{0,6},{1,7},{2,4},{3,5},{4,10},{5,11},{6,8},{7,9},{8,14},{9,15},{1... | collective-permute-start | bytes 1179656 | tf_op jit(solution)/shard_map/ppermute | solution.py:47
  59.9 13.8 %copy-start.2 = (bf16[256,768]{1,0:T(8,128)(2,1)}, bf16[256,768]{1,0:T(8,128)(2,1)S(1)}, u32[]{:S(2)}) copy-start(bf16[256,768]{1,0:T(8,128)(2,1)S(1)} %get-tuple-element.37.refs_1_.refs_6_) | copy-start | bytes 1179652
  59.9 11.9 %collective-permute-start.7 = (bf16[256,768]{1,0:T(8,128)(2,1)S(1)}, bf16[256,768]{1,0:T(8,128)(2,1)S(1)}, u32[]{:S(2)}, u32[]{:S(2)}) collective-permute-start(bf16[256,768]{1,0:T(8,128)(2,1)S(1)} %get-tuple-element.38), channel_id=1, source_target_pairs={{0,2},{1,3},{2,0},{3,1},{16,18},{17,19},{18,16},{19,17}} | collective-permute-start | bytes 1179656 | tf_op jit(solution)/shard_map/ppermute | solution.py:30
  63.8 8.1 %collective-permute-start.9 = (bf16[256,768]{1,0:T(8,128)(2,1)S(1)}, bf16[256,768]{1,0:T(8,128)(2,1)S(1)}, u32[]{:S(2)}, u32[]{:S(2)}) collective-permute-start(bf16[256,768]{1,0:T(8,128)(2,1)S(1)} %get-tuple-element.37.refs_1_.refs_6_), channel_id=1, source_target_pairs={{0,1},{1,0},{2,3},{3,2},{4,5},{5,4},{6,7},{7,6},{8,9},{9,8},{10,11... | collective-permute-start | bytes 1179656 | tf_op jit(solution)/shard_map/ppermute | solution.py:40
  71.9 1.8 copy-start.6
  71.9 1.8 collective-permute-start.10
  72.0 1.7 copy-start.13
  86.3 8.6 %collective-permute-start.11 = (bf16[256,512]{1,0:T(8,128)(2,1)}, bf16[256,512]{1,0:T(8,128)(2,1)S(1)}, u32[]{:S(2)}, u32[]{:S(2)}) collective-permute-start(bf16[256,512]{1,0:T(8,128)(2,1)} %get-tuple-element.24.refs_1_), channel_id=1, source_target_pairs={{0,2},{1,3},{2,0},{3,1},{4,6},{5,7},{6,4},{7,5},{8,10},{9,11},{10,... | collective-permute-start | bytes 786440 | tf_op jit(solution)/shard_map/ppermute | solution.py:22
  87.7 7.1 %collective-permute-start.12 = (bf16[256,512]{1,0:T(8,128)(2,1)}, bf16[256,512]{1,0:T(8,128)(2,1)S(1)}, u32[]{:S(2)}, u32[]{:S(2)}) collective-permute-start(bf16[256,512]{1,0:T(8,128)(2,1)} %get-tuple-element.24.refs_1_), channel_id=1, source_target_pairs={{0,1},{1,0},{2,3},{3,2},{4,5},{5,4},{6,7},{7,6},{8,9},{9,8},{10,11... | collective-permute-start | bytes 786440 | tf_op jit(solution)/shard_map/ppermute | solution.py:40
  94.8 1.5 collective-permute-start.13
  101.8 11.0 %collective-permute-start.14 = (bf16[256,768]{1,0:T(8,128)(2,1)}, bf16[256,768]{1,0:T(8,128)(2,1)S(1)}, u32[]{:S(2)}, u32[]{:S(2)}) collective-permute-start(bf16[256,768]{1,0:T(8,128)(2,1)} %shard_map.94), channel_id=1, source_target_pairs={{0,4},{1,5},{2,6},{3,7},{4,8},{5,9},{6,10},{7,11},{8,12},{9,13},{1... | collective-permute-start | bytes 1179656 | tf_op jit(solution)/shard_map/ppermute | solution.py:47
  105.7 15.0 %collective-permute-start.16 = (bf16[256,768]{1,0:T(8,128)(2,1)}, bf16[256,768]{1,0:T(8,128)(2,1)S(1)}, u32[]{:S(2)}, u32[]{:S(2)}) collective-permute-start(bf16[256,768]{1,0:T(8,128)(2,1)} %shard_map.94), channel_id=1, source_target_pairs={{0,6},{1,7},{2,4},{3,5},{4,10},{5,11},{6,8},{7,9},{8,14},{9,15},{1... | collective-permute-start | bytes 1179656 | tf_op jit(solution)/shard_map/ppermute | solution.py:47
  113.0 13.9 %copy-start.3 = (bf16[256,768]{1,0:T(8,128)(2,1)}, bf16[256,768]{1,0:T(8,128)(2,1)S(1)}, u32[]{:S(2)}) copy-start(bf16[256,768]{1,0:T(8,128)(2,1)S(1)} %get-tuple-element.35.refs_1_.refs_6_) | copy-start | bytes 1179652
  113.1 12.0 %collective-permute-start.15 = (bf16[256,768]{1,0:T(8,128)(2,1)S(1)}, bf16[256,768]{1,0:T(8,128)(2,1)S(1)}, u32[]{:S(2)}, u32[]{:S(2)}) collective-permute-start(bf16[256,768]{1,0:T(8,128)(2,1)S(1)} %get-tuple-element.36), channel_id=1, source_target_pairs={{0,2},{1,3},{2,0},{3,1},{16,18},{17,19},{18,16},{19,17}} | collective-permute-start | bytes 1179656 | tf_op jit(solution)/shard_map/ppermute | solution.py:30
  116.6 8.6 %collective-permute-start.17 = (bf16[256,768]{1,0:T(8,128)(2,1)S(1)}, bf16[256,768]{1,0:T(8,128)(2,1)S(1)}, u32[]{:S(2)}, u32[]{:S(2)}) collective-permute-start(bf16[256,768]{1,0:T(8,128)(2,1)S(1)} %get-tuple-element.35.refs_1_.refs_6_), channel_id=1, source_target_pairs={{0,1},{1,0},{2,3},{3,2},{4,5},{5,4},{6,7},{7,6},{8,9},{9,8},{10,11... | collective-permute-start | bytes 1179656 | tf_op jit(solution)/shard_map/ppermute | solution.py:40
  125.2 1.8 copy-start.7
  125.2 1.8 collective-permute-start.18
  125.3 1.7 copy-start.14
  139.5 8.6 %collective-permute-start.19 = (bf16[256,512]{1,0:T(8,128)(2,1)}, bf16[256,512]{1,0:T(8,128)(2,1)S(1)}, u32[]{:S(2)}, u32[]{:S(2)}) collective-permute-start(bf16[256,512]{1,0:T(8,128)(2,1)} %get-tuple-element.27.refs_1_), channel_id=1, source_target_pairs={{0,2},{1,3},{2,0},{3,1},{4,6},{5,7},{6,4},{7,5},{8,10},{9,11},{10,... | collective-permute-start | bytes 786440 | tf_op jit(solution)/shard_map/ppermute | solution.py:22
  141.0 7.1 %collective-permute-start.20 = (bf16[256,512]{1,0:T(8,128)(2,1)}, bf16[256,512]{1,0:T(8,128)(2,1)S(1)}, u32[]{:S(2)}, u32[]{:S(2)}) collective-permute-start(bf16[256,512]{1,0:T(8,128)(2,1)} %get-tuple-element.27.refs_1_), channel_id=1, source_target_pairs={{0,1},{1,0},{2,3},{3,2},{4,5},{5,4},{6,7},{7,6},{8,9},{9,8},{10,11... | collective-permute-start | bytes 786440 | tf_op jit(solution)/shard_map/ppermute | solution.py:40
  148.1 1.5 copy-start.22
  148.1 1.5 collective-permute-start.21
  155.1 11.0 %collective-permute-start.22 = (bf16[256,768]{1,0:T(8,128)(2,1)}, bf16[256,768]{1,0:T(8,128)(2,1)S(1)}, u32[]{:S(2)}, u32[]{:S(2)}) collective-permute-start(bf16[256,768]{1,0:T(8,128)(2,1)} %shard_map.96), channel_id=1, source_target_pairs={{0,4},{1,5},{2,6},{3,7},{4,8},{5,9},{6,10},{7,11},{8,12},{9,13},{1... | collective-permute-start | bytes 1179656 | tf_op jit(solution)/shard_map/ppermute | solution.py:47
  158.9 15.1 %collective-permute-start.24 = (bf16[256,768]{1,0:T(8,128)(2,1)}, bf16[256,768]{1,0:T(8,128)(2,1)S(1)}, u32[]{:S(2)}, u32[]{:S(2)}) collective-permute-start(bf16[256,768]{1,0:T(8,128)(2,1)} %shard_map.96), channel_id=1, source_target_pairs={{0,6},{1,7},{2,4},{3,5},{4,10},{5,11},{6,8},{7,9},{8,14},{9,15},{1... | collective-permute-start | bytes 1179656 | tf_op jit(solution)/shard_map/ppermute | solution.py:47
  166.3 13.9 %copy-start.1 = (bf16[256,768]{1,0:T(8,128)(2,1)}, bf16[256,768]{1,0:T(8,128)(2,1)S(1)}, u32[]{:S(2)}) copy-start(bf16[256,768]{1,0:T(8,128)(2,1)S(1)} %get-tuple-element.33.refs_1_.refs_6_) | copy-start | bytes 1179652
  166.4 12.0 %collective-permute-start.23 = (bf16[256,768]{1,0:T(8,128)(2,1)S(1)}, bf16[256,768]{1,0:T(8,128)(2,1)S(1)}, u32[]{:S(2)}, u32[]{:S(2)}) collective-permute-start(bf16[256,768]{1,0:T(8,128)(2,1)S(1)} %get-tuple-element.34), channel_id=1, source_target_pairs={{0,2},{1,3},{2,0},{3,1},{16,18},{17,19},{18,16},{19,17}} | collective-permute-start | bytes 1179656 | tf_op jit(solution)/shard_map/ppermute | solution.py:30
  169.8 8.8 %collective-permute-start.25 = (bf16[256,768]{1,0:T(8,128)(2,1)S(1)}, bf16[256,768]{1,0:T(8,128)(2,1)S(1)}, u32[]{:S(2)}, u32[]{:S(2)}) collective-permute-start(bf16[256,768]{1,0:T(8,128)(2,1)S(1)} %get-tuple-element.33.refs_1_.refs_6_), channel_id=1, source_target_pairs={{0,1},{1,0},{2,3},{3,2},{4,5},{5,4},{6,7},{7,6},{8,9},{9,8},{10,11... | collective-permute-start | bytes 1179656 | tf_op jit(solution)/shard_map/ppermute | solution.py:40
  178.4 1.8 copy-start.5
  178.5 1.8 collective-permute-start.26
  178.5 1.7 copy-start.12
  192.8 15.6 %copy-start.8 = (bf16[256,768]{1,0:T(8,128)(2,1)S(1)}, bf16[256,768]{1,0:T(8,128)(2,1)}, u32[]{:S(2)}) copy-start(bf16[256,768]{1,0:T(8,128)(2,1)} %shard_map.92) | copy-start | bytes 1179652
  192.8 15.6 %copy-start.9 = (bf16[256,768]{1,0:T(8,128)(2,1)S(1)}, bf16[256,768]{1,0:T(8,128)(2,1)}, u32[]{:S(2)}) copy-start(bf16[256,768]{1,0:T(8,128)(2,1)} %shard_map.94) | copy-start | bytes 1179652
  192.8 15.6 %copy-start.10 = (bf16[256,768]{1,0:T(8,128)(2,1)S(1)}, bf16[256,768]{1,0:T(8,128)(2,1)}, u32[]{:S(2)}) copy-start(bf16[256,768]{1,0:T(8,128)(2,1)} %shard_map.96) | copy-start | bytes 1179652
  192.8 8.6 %collective-permute-start.27 = (bf16[256,512]{1,0:T(8,128)(2,1)}, bf16[256,512]{1,0:T(8,128)(2,1)S(1)}, u32[]{:S(2)}, u32[]{:S(2)}) collective-permute-start(bf16[256,512]{1,0:T(8,128)(2,1)} %get-tuple-element.30.refs_1_), channel_id=1, source_target_pairs={{0,2},{1,3},{2,0},{3,1},{4,6},{5,7},{6,4},{7,5},{8,10},{9,11},{10,... | collective-permute-start | bytes 786440 | tf_op jit(solution)/shard_map/ppermute | solution.py:22
  194.4 7.1 %collective-permute-start.28 = (bf16[256,512]{1,0:T(8,128)(2,1)}, bf16[256,512]{1,0:T(8,128)(2,1)S(1)}, u32[]{:S(2)}, u32[]{:S(2)}) collective-permute-start(bf16[256,512]{1,0:T(8,128)(2,1)} %get-tuple-element.30.refs_1_), channel_id=1, source_target_pairs={{0,1},{1,0},{2,3},{3,2},{4,5},{5,4},{6,7},{7,6},{8,9},{9,8},{10,11... | collective-permute-start | bytes 786440 | tf_op jit(solution)/shard_map/ppermute | solution.py:40
  201.5 1.5 collective-permute-start.29
  (15 other events, 15.8 us)
